TPU v7x, 32 devices: a whole 2x2x4 slice. The times are simulated.
32 devices in a mesh: grp: 2 (over x), ha: 16 (over z, y, core).
Axes of the slice: x: 2, y: 2, z: 4, core: 2. Of those that a mesh axis runs over, the one named last changes fastest.
Arguments:
- features: bfloat16 [4, 16, 128, 384], P('grp', 'ha'), parts along dimension 0, may hold values from -8 to 8
- first_cache: bfloat16 [4, 16, 128, 384], P('grp', 'ha'), parts along dimension 0, may hold values from -6 to 6
- second_cache: bfloat16 [4, 32, 256, 192], P('grp', 'ha'), parts along dimension 0, may hold values from -6 to 6
- w_query: bfloat16 [384, 384], replicated, may hold values from -2 to 2
- w_key: bfloat16 [384, 384], replicated, may hold values from -2 to 2
- w_value: bfloat16 [384, 384], replicated, may hold values from -0.3125 to 0.3125
- w_output: bfloat16 [384, 384], replicated, may hold values from -0.625 to 0.625
- w_first: bfloat16 [3, 3, 3, 384, 384], replicated, may hold values from -0.0625 to 0.0625
- w_upsample: bfloat16 [3, 3, 384, 192], replicated, may hold values from -0.109375 to 0.109375
- w_second: bfloat16 [3, 3, 3, 192, 192], replicated, may hold values from -0.078125 to 0.078125
Outputs:
- decoded: bfloat16 [4, 32, 256, 192], P('grp', 'ha'), parts along dimension 0
There are 2 independent parts, one for each index of `grp`. A program takes and returns all parts, laid end to end along the dimension named above; an argument that names none is the same for every part. Nothing has to cross between parts.
All inputs are finite; a program needn't handle non-finite values.
Results may differ from a plain program's by a relative error of at most 0.015.
Values may be sent and summed in bfloat16 or wider, within the bound.
No kernel may reach another device: no remote copies, remote signals or barrier semaphores. Data moves between devices by JAX's collectives and lax.ppermute only.
A program may use at most 128 MiB of HBM per device.

v0:
```python
import math

import jax
import jax.numpy as jnp
from jax import lax
from jax.sharding import PartitionSpec as P


def extended(x, sides, width):
    for axis, dim in sides:
        count, length = (lax.axis_size(axis), x.shape[dim])
        up = [(i, (i + 1) % count) for i in range(count - 1)]
        down = [(j, i) for i, j in up]
        last = lax.slice_in_dim(x, length - width, length, axis=dim)
        first = lax.slice_in_dim(x, 0, width, axis=dim)
        before = lax.ppermute(last, axis, up)
        after = lax.ppermute(first, axis, down)
        x = jnp.concatenate([before, x, after], axis=dim)
    return x


def rms_scale(tensor):
    widened = tensor.astype(jnp.float32)
    return widened * lax.rsqrt(jnp.mean(widened * widened, axis=-1, keepdims=True) + 1e-06)


def conv_taps(padded, weight, time_taps):
    frames_out = padded.shape[0] - time_taps + 1
    height_out = padded.shape[1] - 2
    width_out = padded.shape[2]
    in_channels = weight.shape[-2]
    out_channels = weight.shape[-1]
    widened = jnp.pad(padded, ((0, 0), (0, 0), (1, 1), (0, 0)))
    result = jnp.zeros((frames_out, height_out, width_out, out_channels), jnp.float32)
    for time_off in range(time_taps):
        for row_off in range(3):
            window = widened[time_off : time_off + frames_out, row_off : row_off + height_out]
            stacked = jnp.concatenate(
                [window[:, :, col_off : col_off + width_out] for col_off in range(3)], axis=-1
            )
            kernel = weight[time_off, row_off].reshape(3 * in_channels, out_channels)
            result = result + jnp.einsum(
                "fhwc,cd->fhwd", stacked, kernel, preferred_element_type=jnp.float32
            )
    return result


def project_rows(tokens, weight):
    return jnp.einsum("ftc,cd->ftd", tokens, weight, preferred_element_type=jnp.float32).astype(
        jnp.bfloat16
    )


def per_device(
    features,
    first_cache,
    second_cache,
    w_query,
    w_key,
    w_value,
    w_output,
    w_first,
    w_upsample,
    w_second,
):
    frame_count, row_count, width_count, channels = features.shape
    normed = rms_scale(features).astype(jnp.bfloat16)
    normed_tokens = normed.reshape(frame_count, row_count * width_count, channels)
    queries = project_rows(normed_tokens, w_query)
    score_scale = 1.0 / math.sqrt(channels)
    token_count = row_count * width_count
    keys_own = project_rows(normed_tokens, w_key)
    values_own = project_rows(normed_tokens, w_value)
    running_max = jnp.full((frame_count, token_count), -jnp.inf, jnp.float32)
    weight_sum = jnp.zeros((frame_count, token_count), jnp.float32)
    weighted = jnp.zeros((frame_count, token_count, channels), jnp.float32)
    scores = (
        jnp.einsum(
            "fqc,fkc->fqk",
            queries,
            lax.all_gather(keys_own, "ha", axis=1, tiled=True),
            preferred_element_type=jnp.float32,
        )
        * score_scale
    )
    newest = jnp.max(scores, axis=-1)
    shrink = jnp.exp(running_max - newest)
    weights = jnp.exp(scores - newest[..., None])
    weight_sum = weight_sum * shrink + jnp.sum(weights, axis=-1)
    weighted = weighted * shrink[..., None] + jnp.einsum(
        "fqk,fkc->fqc",
        weights.astype(jnp.bfloat16),
        lax.all_gather(values_own, "ha", axis=1, tiled=True),
        preferred_element_type=jnp.float32,
    )
    running_max, weight_sum, weighted = (newest, weight_sum, weighted)
    attended = (weighted / weight_sum[..., None]).astype(jnp.bfloat16)
    projected = jnp.einsum("ftc,cd->ftd", attended, w_output, preferred_element_type=jnp.float32)
    mixed = (
        features.astype(jnp.float32)
        + projected.reshape(frame_count, row_count, width_count, channels)
    ).astype(jnp.bfloat16)
    first_in = jax.nn.silu(rms_scale(mixed)).astype(jnp.bfloat16)
    first_stack = jnp.concatenate([first_cache, first_in], axis=0)
    first_padded = extended(first_stack, (("ha", 1),), 1)
    block_out = (mixed.astype(jnp.float32) + conv_taps(first_padded, w_first, 3)).astype(
        jnp.bfloat16
    )
    enlarged = jnp.repeat(jnp.repeat(block_out, 2, axis=1), 2, axis=2)
    up_padded = extended(enlarged, (("ha", 1),), 1)
    upsampled = conv_taps(up_padded, w_upsample[None], 1).astype(jnp.bfloat16)
    second_in = jax.nn.silu(rms_scale(upsampled)).astype(jnp.bfloat16)
    second_stack = jnp.concatenate([second_cache, second_in], axis=0)
    second_padded = extended(second_stack, (("ha", 1),), 1)
    return (upsampled.astype(jnp.float32) + conv_taps(second_padded, w_second, 3)).astype(
        jnp.bfloat16
    )


def solution(mesh):
    placed = (
        P("grp", "ha", None, None),
        P("grp", "ha", None, None),
        P("grp", "ha", None, None),
        P(),
        P(),
        P(),
        P(),
        P(),
        P(),
        P(),
    )
    return jax.shard_map(
        per_device,
        mesh=mesh,
        in_specs=placed,
        out_specs=P("grp", "ha", None, None),
        check_vma=False,
    )
```

profile of v0, /device:TPU:13, one launch (start us, length us, event | category | flops | bytes accessed | tf_op | source)
XLA Modules:
  0.0 175.2 jit_solution(18347833795651068395)
XLA Ops:
  6.5 1.1 fusion.144
  7.7 2.1 %convolution_convert_fusion.1 = bf16[2,128,384]{2,1,0:T(8,128)(2,1)} fusion(bf16[384,384]{1,0:T(8,128)(2,1)} %param.14, bf16[2,1,128,384]{3,2,1,0:T(8,128)(2,1)} %param.10, f32[2,128]{1,0:T(2,128)S(1)} %add_rsqrt_fusion.2), kind=kOutput, calls=%fused_computation.121 | convolution fusion | flops 75890688 | bytes 689152 | tf_op jit(solution)/shard_map/ftc,cd->ftd/dot_general | solution.py:49
  9.8 2.1 %convolution_convert_fusion = bf16[2,128,384]{2,1,0:T(8,128)(2,1)} fusion(bf16[384,384]{1,0:T(8,128)(2,1)} %param.15, bf16[2,1,128,384]{3,2,1,0:T(8,128)(2,1)} %param.10, f32[2,128]{1,0:T(2,128)S(1)} %add_rsqrt_fusion.2), kind=kOutput, calls=%fused_computation.120 | convolution fusion | flops 75890688 | bytes 689152 | tf_op jit(solution)/shard_map/ftc,cd->ftd/dot_general | solution.py:49
  11.9 44.2 %all-gather.3.cloned.1.call-done = bf16[2,2048,384]{2,1,0:T(8,128)(2,1)} async-done(((bf16[2,128,384]{2,1,0:T(8,128)(2,1)}), bf16[2,2048,384]{2,1,0:T(8,128)(2,1)}) %all-gather.3.cloned.1.call-update) | async-done | bytes 3145744 | tf_op jit(solution)/shard_map/all_gather | solution.py:81
  56.2 3.3 %fusion.193 = (f32[2,128]{1,0:T(2,128)S(1)}, f32[2,128,2048]{2,1,0:T(8,128)S(1)}) fusion(bf16[2,2048,384]{2,1,0:T(8,128)(2,1)} %all-gather.3.cloned.1.call-done, bf16[384,384]{1,0:T(8,128)(2,1)S(1)} %copy-done, bf16[2,1,128,384]{3,2,1,0:T(8,128)(2,1)S(1)} %copy-done.3, f32[2,128]{1,0:T(2,128)S(1)} %add_rsqrt_fusion.2), kind=kOutput, calls=%fused_computation.238 | convolution fusion | flops 479592192 | bytes 5736448 | tf_op jit(solution)/shard_map/fqc,fkc->fqk/dot_general | solution.py:78
  59.5 0.4 fusion.23
  59.9 42.6 %all-gather.5.cloned.1.call-done = bf16[2,2048,384]{2,1,0:T(8,128)(2,1)} async-done(((bf16[2,128,384]{2,1,0:T(8,128)(2,1)}), bf16[2,2048,384]{2,1,0:T(8,128)(2,1)}) %all-gather.5.cloned.1.call-update) | async-done | bytes 3145744 | tf_op jit(solution)/shard_map/all_gather | solution.py:93
  102.5 3.0 %multiply_reduce_fusion.1 = (f32[2,128]{1,0:T(2,128)S(1)}, f32[2,1,128,384]{3,2,0,1:T(8,128)S(1)}) fusion(bf16[384,384]{1,0:T(8,128)(2,1)S(1)} %copy-done.9, bf16[2,2048,384]{2,1,0:T(8,128)(2,1)} %all-gather.5.cloned.1.call-done, f32[2,128,2048]{2,1,0:T(8,128)S(1)} %get-tuple-element.87, f32[2,128]{1,0:T(2,128)S(1)} %get-tuple-element.86, ...), kind=kOutput, calls=%fused_computation.193 | convolution fusion | flops 480083712 | bytes 6131712 | tf_op jit(solution)/shard_map/ftc,cd->ftd/dot_general | solution.py:98
  105.8 3.5 %collective-permute-start = (bf16[4,1,128,384]{3,2,0,1:T(8,128)(2,1)S(1)}, bf16[4,1,128,384]{3,2,0,1:T(8,128)(2,1)S(1)}, u32[]{:S(2)}, u32[]{:S(2)}) collective-permute-start(bf16[4,1,128,384]{3,2,0,1:T(8,128)(2,1)S(1)} %pad_maximum_fusion.4), channel_id=1, source_target_pairs={{0,1},{1,2},{2,3},{3,4},{4,5},{5,6},{6,7},{7,8},{8,9},{9,10},{10,1... | collective-permute-start | bytes 1179656 | tf_op jit(solution)/shard_map/ppermute | solution.py:16
  109.3 1.9 %collective-permute-start.1 = (bf16[4,1,128,384]{3,2,0,1:T(8,128)(2,1)S(1)}, bf16[4,1,128,384]{3,2,0,1:T(8,128)(2,1)S(1)}, u32[]{:S(2)}, u32[]{:S(2)}) collective-permute-start(bf16[4,1,128,384]{3,2,0,1:T(8,128)(2,1)S(1)} %pad_maximum_fusion.4), channel_id=1, source_target_pairs={{1,0},{2,1},{3,2},{4,3},{5,4},{6,5},{7,6},{8,7},{9,8},{10,9},{11,1... | collective-permute-start | bytes 1179656 | tf_op jit(solution)/shard_map/ppermute | solution.py:17
  111.2 3.9 %fusion.183 = (bf16[1,1,3,384,384]{4,3,2,1,0:T(8,128)(2,1)S(1)}, bf16[1,1,3,384,384]{4,3,2,1,0:T(8,128)(2,1)S(1)}, bf16[1,1,3,384,384]{4,3,2,1,0:T(8,128)(2,1)S(...) fusion(bf16[3,3,3,384,384]{4,3,2,1,0:T(8,128)(2,1)} %param.17), kind=kLoop, calls=%fused_computation.228 | loop fusion | bytes 15925248 | tf_op jit(solution)/shard_map/slice | solution.py:41
  115.2 4.1 %collective-permute-done.1 = bf16[4,1,128,384]{3,2,0,1:T(8,128)(2,1)S(1)} collective-permute-done((bf16[4,1,128,384]{3,2,0,1:T(8,128)(2,1)S(1)}, bf16[4,1,128,384]{3,2,0,1:T(8,128)(2,1)S(1)}, u32[]{:S(2)}, u32[]{:S(2)}) %collective-permute-start.1) | collective-permute-done | bytes 393248 | tf_op jit(solution)/shard_map/ppermute | solution.py:17
  119.6 0.6 fusion.188
  120.3 0.5 fusion.104
  120.8 0.5 convolution_add_fusion.15
  121.3 0.5 convolution_add_fusion.14
  121.8 0.5 convolution_add_fusion.13
  122.3 0.5 convolution_add_fusion.12
  122.8 0.5 convolution_add_fusion.11
  123.2 0.5 convolution_add_fusion.10
  123.7 0.5 convolution_add_fusion.9
  124.2 0.5 copy-done.8
  124.7 0.5 fusion.99
  125.5 0.9 slice.411
  126.3 1.9 %collective-permute-start.2 = (bf16[2,1,256,384]{3,2,1,0:T(8,128)(2,1)}, bf16[2,1,256,384]{3,2,1,0:T(8,128)(2,1)}, u32[]{:S(2)}, u32[]{:S(2)}) collective-permute-start(bf16[2,1,256,384]{3,2,1,0:T(8,128)(2,1)} %slice.411), channel_id=1, source_target_pairs={{0,1},{1,2},{2,3},{3,4},{4,5},{5,6},{6,7},{7,8},{8,9},{9,10},{10,1... | collective-permute-start | bytes 1179656 | tf_op jit(solution)/shard_map/ppermute | solution.py:16
  128.3 2.6 %collective-permute-start.3 = (bf16[2,1,256,384]{3,2,1,0:T(8,128)(2,1)}, bf16[2,1,256,384]{3,2,1,0:T(8,128)(2,1)}, u32[]{:S(2)}, u32[]{:S(2)}) collective-permute-start(bf16[2,1,256,384]{3,2,1,0:T(8,128)(2,1)} %slice.411), channel_id=1, source_target_pairs={{1,0},{2,1},{3,2},{4,3},{5,4},{6,5},{7,6},{8,7},{9,8},{10,9},{11,1... | collective-permute-start | bytes 1179656 | tf_op jit(solution)/shard_map/ppermute | solution.py:17
  131.0 0.4 copy.30
  133.5 5.2 %collective-permute-done.3 = bf16[2,1,256,384]{3,2,1,0:T(8,128)(2,1)} collective-permute-done((bf16[2,1,256,384]{3,2,1,0:T(8,128)(2,1)}, bf16[2,1,256,384]{3,2,1,0:T(8,128)(2,1)}, u32[]{:S(2)}, u32[]{:S(2)}) %collective-permute-start.3) | collective-permute-done | bytes 393248 | tf_op jit(solution)/shard_map/ppermute | solution.py:17
  138.8 1.6 fusion.26
  140.3 0.8 fusion.186
  141.1 1.1 fusion.10
  142.2 1.9 %fusion.18 = f32[2,2,256,192]{2,3,1,0:T(8,128)S(1)} fusion(bf16[2,1,256,384]{3,2,1,0:T(8,128)(2,1)} %collective-permute-done.3, bf16[2,2,256,384]{3,2,1,0:T(8,128)(2,1)S(1)} %broadcast_in_dim.28, bf16[2,2,256,384]{3,2,1,0:T(8,128)(2,1)S(1)} %get-tuple-element.46, bf16[2,2,256,384]{3,2,1,0:T(8,128)(2,1)S(1)} %get-tuple-element.42, ...), kind=kOutput, calls=%fused_computation.28 | convolution fusion | flops 462422016 | bytes 3981312 | tf_op jit(solution)/shard_map/fhwc,cd->fhwd/dot_general | solution.py:42
  144.2 2.0 %multiply_reduce_fusion = (f32[2,2,256]{2,1,0:T(2,128)S(1)}, f32[2,2,256,192]{2,3,1,0:T(8,128)S(1)}) fusion(f32[2,2,256,192]{2,3,1,0:T(8,128)S(1)} %fusion.18, f32[2,2,256,192]{2,3,1,0:T(8,128)S(1)} %fusion.10, bf16[1152,192,1,1]{0,1,2,3:T(8,128)(2,1)S(1)} %reshape.127, bf16[2,2,256,384]{3,2,1,0:T(8,128)(2,1)S(1)} %broadcast_in_dim.28, ...), kind=kOutput, calls=%fused_computation.133 | convolution fusion | flops 463600640 | bytes 5558272 | tf_op jit(solution)/shard_map/fhwc,cd->fhwd/dot_general | solution.py:42
  146.6 2.1 %collective-permute-start.4 = (bf16[4,1,256,192]{2,3,1,0:T(8,128)(2,1)S(1)}, bf16[4,1,256,192]{2,3,1,0:T(8,128)(2,1)S(1)}, u32[]{:S(2)}, u32[]{:S(2)}) collective-permute-start(bf16[4,1,256,192]{2,3,1,0:T(8,128)(2,1)S(1)} %get-tuple-element.76), channel_id=1, source_target_pairs={{0,1},{1,2},{2,3},{3,4},{4,5},{5,6},{6,7},{7,8},{8,9},{9,10},{10,1... | collective-permute-start | bytes 1179656 | tf_op jit(solution)/shard_map/ppermute | solution.py:16
  148.6 3.6 %collective-permute-start.5 = (bf16[4,1,256,192]{2,3,1,0:T(8,128)(2,1)S(1)}, bf16[4,1,256,192]{2,3,1,0:T(8,128)(2,1)S(1)}, u32[]{:S(2)}, u32[]{:S(2)}) collective-permute-start(bf16[4,1,256,192]{2,3,1,0:T(8,128)(2,1)S(1)} %get-tuple-element.77), channel_id=1, source_target_pairs={{1,0},{2,1},{3,2},{4,3},{5,4},{6,5},{7,6},{8,7},{9,8},{10,9},{11,1... | collective-permute-start | bytes 1179656 | tf_op jit(solution)/shard_map/ppermute | solution.py:17
  152.4 0.9 collective-permute-done.4
  153.3 5.4 %collective-permute-done.5 = bf16[4,1,256,192]{2,3,1,0:T(8,128)(2,1)S(1)} collective-permute-done((bf16[4,1,256,192]{2,3,1,0:T(8,128)(2,1)S(1)}, bf16[4,1,256,192]{2,3,1,0:T(8,128)(2,1)S(1)}, u32[]{:S(2)}, u32[]{:S(2)}) %collective-permute-start.5) | collective-permute-done | bytes 393248 | tf_op jit(solution)/shard_map/ppermute | solution.py:17
  158.7 2.0 %select_maximum_fusion = bf16[4,4,258,192]{2,3,1,0:T(8,128)(2,1)S(1)} fusion(bf16[4,1,256,192]{2,3,1,0:T(8,128)(2,1)S(1)} %collective-permute-done.5, bf16[4,1,256,192]{2,3,1,0:T(8,128)(2,1)S(1)} %collective-permute-done.4, bf16[2,2,256,192]{2,3,1,0:T(8,128)(2,1)S(1)} %multiply_convert_fusion, bf16[2,2,256,192]{2,3,1,0:T(8,128)(2,1)S(1)} %copy-done.2), kind=kLoop, calls=%fused_computation.10 | loop fusion | flops 11888640 | bytes 3158016 | tf_op jit(solution)/shard_map/concatenate | solution.py:18
  160.7 1.7 fusion.185
  162.8 0.5 fusion.57
  163.4 0.5 convolution_add_fusion.7
  163.9 0.5 convolution_add_fusion.6
  164.4 0.5 convolution_add_fusion.5
  164.9 0.5 convolution_add_fusion.4
  165.5 0.5 convolution_add_fusion.3
  166.0 0.5 convolution_add_fusion.2
  166.5 0.5 convolution_add_fusion.1
  167.1 1.3 fusion.43
  (49 shorter events, 4.2 us)
Async XLA Ops:
  6.5 49.6 %copy-start = (bf16[384,384]{1,0:T(8,128)(2,1)S(1)}, bf16[384,384]{1,0:T(8,128)(2,1)}, u32[]{:S(2)}) copy-start(bf16[384,384]{1,0:T(8,128)(2,1)} %param.13) | copy-start | bytes 884740
  6.5 49.6 %copy-start.3 = (bf16[2,1,128,384]{3,2,1,0:T(8,128)(2,1)S(1)}, bf16[2,1,128,384]{3,2,1,0:T(8,128)(2,1)}, u32[]{:S(2)}) copy-start(bf16[2,1,128,384]{3,2,1,0:T(8,128)(2,1)} %param.10) | copy-start | bytes 589828
  6.5 49.6 %all-gather.3.cloned.1.call-start = ((), (), s32[]{:S(2)}) async-start(), calls=%async_computation | async-start | bytes 3342336 | tf_op jit(solution)/shard_map/all_gather | solution.py:81
  9.8 92.7 %all-gather.5.cloned.1.call-start = ((), (), s32[]{:S(2)}) async-start(), calls=%async_computation.1 | async-start | bytes 3342336 | tf_op jit(solution)/shard_map/all_gather | solution.py:93
  59.5 43.0 %copy-start.9 = (bf16[384,384]{1,0:T(8,128)(2,1)S(1)}, bf16[384,384]{1,0:T(8,128)(2,1)}, u32[]{:S(2)}) copy-start(bf16[384,384]{1,0:T(8,128)(2,1)} %param.16) | copy-start | bytes 884740
  102.5 3.2 %copy-start.5 = (bf16[2,1,128,384]{3,2,1,0:T(8,128)(2,1)S(1)}, bf16[2,1,128,384]{3,2,1,0:T(8,128)(2,1)}, u32[]{:S(2)}) copy-start(bf16[2,1,128,384]{3,2,1,0:T(8,128)(2,1)} %param.11) | copy-start | bytes 589828
  105.5 9.6 %copy-start.7 = (f32[2,1,128,384]{3,2,0,1:T(8,128)}, f32[2,1,128,384]{3,2,0,1:T(8,128)S(1)}, u32[]{:S(2)}) copy-start(f32[2,1,128,384]{3,2,0,1:T(8,128)S(1)} %get-tuple-element.89) | copy-start | bytes 1179652
  105.8 9.4 %collective-permute-start = (bf16[4,1,128,384]{3,2,0,1:T(8,128)(2,1)S(1)}, bf16[4,1,128,384]{3,2,0,1:T(8,128)(2,1)S(1)}, u32[]{:S(2)}, u32[]{:S(2)}) collective-permute-start(bf16[4,1,128,384]{3,2,0,1:T(8,128)(2,1)S(1)} %pad_maximum_fusion.4), channel_id=1, source_target_pairs={{0,1},{1,2},{2,3},{3,4},{4,5},{5,6},{6,7},{7,8},{8,9},{9,10},{10,1... | collective-permute-start | bytes 1179656 | tf_op jit(solution)/shard_map/ppermute | solution.py:16
  109.3 10.0 %collective-permute-start.1 = (bf16[4,1,128,384]{3,2,0,1:T(8,128)(2,1)S(1)}, bf16[4,1,128,384]{3,2,0,1:T(8,128)(2,1)S(1)}, u32[]{:S(2)}, u32[]{:S(2)}) collective-permute-start(bf16[4,1,128,384]{3,2,0,1:T(8,128)(2,1)S(1)} %pad_maximum_fusion.4), channel_id=1, source_target_pairs={{1,0},{2,1},{3,2},{4,3},{5,4},{6,5},{7,6},{8,7},{9,8},{10,9},{11,1... | collective-permute-start | bytes 1179656 | tf_op jit(solution)/shard_map/ppermute | solution.py:17
  123.7 1.0 copy-start.8
  124.7 6.1 %copy-start.6 = (bf16[3,3,384,192]{2,3,1,0:T(8,128)(2,1)S(1)}, bf16[3,3,384,192]{2,3,1,0:T(8,128)(2,1)}, u32[]{:S(2)}) copy-start(bf16[3,3,384,192]{2,3,1,0:T(8,128)(2,1)} %param.18) | copy-start | bytes 3981316
  126.3 7.1 %collective-permute-start.2 = (bf16[2,1,256,384]{3,2,1,0:T(8,128)(2,1)}, bf16[2,1,256,384]{3,2,1,0:T(8,128)(2,1)}, u32[]{:S(2)}, u32[]{:S(2)}) collective-permute-start(bf16[2,1,256,384]{3,2,1,0:T(8,128)(2,1)} %slice.411), channel_id=1, source_target_pairs={{0,1},{1,2},{2,3},{3,4},{4,5},{5,6},{6,7},{7,8},{8,9},{9,10},{10,1... | collective-permute-start | bytes 1179656 | tf_op jit(solution)/shard_map/ppermute | solution.py:16
  128.3 10.4 %collective-permute-start.3 = (bf16[2,1,256,384]{3,2,1,0:T(8,128)(2,1)}, bf16[2,1,256,384]{3,2,1,0:T(8,128)(2,1)}, u32[]{:S(2)}, u32[]{:S(2)}) collective-permute-start(bf16[2,1,256,384]{3,2,1,0:T(8,128)(2,1)} %slice.411), channel_id=1, source_target_pairs={{1,0},{2,1},{3,2},{4,3},{5,4},{6,5},{7,6},{8,7},{9,8},{10,9},{11,1... | collective-permute-start | bytes 1179656 | tf_op jit(solution)/shard_map/ppermute | solution.py:17
  144.2 2.3 %copy-start.2 = (bf16[2,2,256,192]{2,3,1,0:T(8,128)(2,1)S(1)}, bf16[2,2,256,192]{2,3,1,0:T(8,128)(2,1)}, u32[]{:S(2)}) copy-start(bf16[2,2,256,192]{2,3,1,0:T(8,128)(2,1)} %param.12) | copy-start | bytes 1179652
  146.2 6.0 %copy-start.4 = (bf16[3,3,3,192,192]{4,3,2,1,0:T(8,128)(2,1)S(1)}, bf16[3,3,3,192,192]{4,3,2,1,0:T(8,128)(2,1)}, u32[]{:S(2)}) copy-start(bf16[3,3,3,192,192]{4,3,2,1,0:T(8,128)(2,1)} %param.19) | copy-start | bytes 5971972
  146.6 6.8 %collective-permute-start.4 = (bf16[4,1,256,192]{2,3,1,0:T(8,128)(2,1)S(1)}, bf16[4,1,256,192]{2,3,1,0:T(8,128)(2,1)S(1)}, u32[]{:S(2)}, u32[]{:S(2)}) collective-permute-start(bf16[4,1,256,192]{2,3,1,0:T(8,128)(2,1)S(1)} %get-tuple-element.76), channel_id=1, source_target_pairs={{0,1},{1,2},{2,3},{3,4},{4,5},{5,6},{6,7},{7,8},{8,9},{9,10},{10,1... | collective-permute-start | bytes 1179656 | tf_op jit(solution)/shard_map/ppermute | solution.py:16
  148.6 10.1 %collective-permute-start.5 = (bf16[4,1,256,192]{2,3,1,0:T(8,128)(2,1)S(1)}, bf16[4,1,256,192]{2,3,1,0:T(8,128)(2,1)S(1)}, u32[]{:S(2)}, u32[]{:S(2)}) collective-permute-start(bf16[4,1,256,192]{2,3,1,0:T(8,128)(2,1)S(1)} %get-tuple-element.77), channel_id=1, source_target_pairs={{1,0},{2,1},{3,2},{4,3},{5,4},{6,5},{7,6},{8,7},{9,8},{10,9},{11,1... | collective-permute-start | bytes 1179656 | tf_op jit(solution)/shard_map/ppermute | solution.py:17
  167.0 1.3 copy-start.1
Sparse Core Ops, SparseCore 0:
  9.9 46.2 all-gather.2
  58.5 44.0 all-gather.4
where the time goes:
time: 178 us; the launch traced here: 175 us
  waiting for transfers between devices  102 us (57%)
  matrix products  25.3 us (14%)
  starting transfers between devices  15.6 us (9%)
  between operations  13.9 us (8%)
  local copies, waits for them, and re-layouts  11.8 us (7%)
  other arithmetic  6.13 us (3%)
    all_gather x1, waiting for transfers between devices, per_device(): lax.all_gather(keys_own, 'ha', axis=1, tiled=True)  44.2 us
    all_gather x1, waiting for transfers between devices, per_device(): lax.all_gather(values_own, 'ha', axis=1, tiled=True)  42.6 us
    dot_general x21, matrix products, conv_taps(): jnp.einsum('fhwc,cd->fhwd', stacked, kernel, preferred_element_type=jnp.f...  14.9 us
    ppermute x3, waiting for transfers between devices, extended(): after = lax.ppermute(first, axis, down)  14.7 us
    ppermute x3, starting transfers between devices, extended(): after = lax.ppermute(first, axis, down)  8.07 us
    ppermute x3, starting transfers between devices, extended(): before = lax.ppermute(last, axis, up)  7.44 us
    slice x6, local copies, waits for them, and re-layouts, conv_taps(): kernel = weight[time_off, row_off].reshape(3 * in_channels, out_channels)  5.42 us
    dot_general x2, matrix products, project_rows(): jnp.einsum('ftc,cd->ftd', tokens, weight, preferred_element_type=jnp.floa...  4.17 us
  transfers between devices with their start and end apart: 8, of which 6 were waited for; matrix products, arithmetic and copies ran while one was open for 7% of the time, Pallas kernels for 0%

commit v1 on v0

--- a/solution.py
+++ b/solution.py
@@ -6,17 +6,35 @@
 from jax.sharding import PartitionSpec as P
 
 
-def extended(x, sides, width):
-    for axis, dim in sides:
-        count, length = (lax.axis_size(axis), x.shape[dim])
-        up = [(i, (i + 1) % count) for i in range(count - 1)]
-        down = [(j, i) for i, j in up]
-        last = lax.slice_in_dim(x, length - width, length, axis=dim)
-        first = lax.slice_in_dim(x, 0, width, axis=dim)
-        before = lax.ppermute(last, axis, up)
-        after = lax.ppermute(first, axis, down)
-        x = jnp.concatenate([before, x, after], axis=dim)
-    return x
+def halo_rows(x, dim, width):
+    count, length = (lax.axis_size("ha"), x.shape[dim])
+    up = [(i, i + 1) for i in range(count - 1)]
+    down = [(j, i) for i, j in up]
+    last = lax.slice_in_dim(x, length - width, length, axis=dim)
+    first = lax.slice_in_dim(x, 0, width, axis=dim)
+    before = lax.ppermute(last, "ha", up)
+    after = lax.ppermute(first, "ha", down)
+    return before, after
+
+
+def extended(x, dim, width):
+    before, after = halo_rows(x, dim, width)
+    return jnp.concatenate([before, x, after], axis=dim)
+
+
+def gather_rows(x):
+    count = lax.axis_size("ha")
+    chips = count // 2
+    pieces = [x]
+    for shift in range(1, chips):
+        pairs = [
+            (2 * c + k, 2 * ((c + shift) % chips) + k) for c in range(chips) for k in range(2)
+        ]
+        pieces.append(lax.ppermute(x, "ha", pairs))
+    own_chip = jnp.concatenate(pieces, axis=1)
+    swap = [(2 * c + k, 2 * c + 1 - k) for c in range(chips) for k in range(2)]
+    other = lax.ppermute(own_chip, "ha", swap)
+    return jnp.concatenate([own_chip, other], axis=1)
 
 
 def rms_scale(tensor):
@@ -64,36 +82,28 @@
     w_second,
 ):
     frame_count, row_count, width_count, channels = features.shape
+    every_row = gather_rows(features)
+    normed_all = rms_scale(every_row).astype(jnp.bfloat16)
+    all_tokens = normed_all.reshape(frame_count, -1, channels)
     normed = rms_scale(features).astype(jnp.bfloat16)
     normed_tokens = normed.reshape(frame_count, row_count * width_count, channels)
     queries = project_rows(normed_tokens, w_query)
+    keys_all = project_rows(all_tokens, w_key)
+    values_all = project_rows(all_tokens, w_value)
     score_scale = 1.0 / math.sqrt(channels)
-    token_count = row_count * width_count
-    keys_own = project_rows(normed_tokens, w_key)
-    values_own = project_rows(normed_tokens, w_value)
-    running_max = jnp.full((frame_count, token_count), -jnp.inf, jnp.float32)
-    weight_sum = jnp.zeros((frame_count, token_count), jnp.float32)
-    weighted = jnp.zeros((frame_count, token_count, channels), jnp.float32)
     scores = (
-        jnp.einsum(
-            "fqc,fkc->fqk",
-            queries,
-            lax.all_gather(keys_own, "ha", axis=1, tiled=True),
-            preferred_element_type=jnp.float32,
-        )
+        jnp.einsum("fqc,fkc->fqk", queries, keys_all, preferred_element_type=jnp.float32)
         * score_scale
     )
-    newest = jnp.max(scores, axis=-1)
-    shrink = jnp.exp(running_max - newest)
-    weights = jnp.exp(scores - newest[..., None])
-    weight_sum = weight_sum * shrink + jnp.sum(weights, axis=-1)
-    weighted = weighted * shrink[..., None] + jnp.einsum(
+    largest = jnp.max(scores, axis=-1)
+    weights = jnp.exp(scores - largest[..., None])
+    weight_sum = jnp.sum(weights, axis=-1)
+    weighted = jnp.einsum(
         "fqk,fkc->fqc",
         weights.astype(jnp.bfloat16),
-        lax.all_gather(values_own, "ha", axis=1, tiled=True),
+        values_all,
         preferred_element_type=jnp.float32,
     )
-    running_max, weight_sum, weighted = (newest, weight_sum, weighted)
     attended = (weighted / weight_sum[..., None]).astype(jnp.bfloat16)
     projected = jnp.einsum("ftc,cd->ftd", attended, w_output, preferred_element_type=jnp.float32)
     mixed = (
@@ -102,16 +112,17 @@
     ).astype(jnp.bfloat16)
     first_in = jax.nn.silu(rms_scale(mixed)).astype(jnp.bfloat16)
     first_stack = jnp.concatenate([first_cache, first_in], axis=0)
-    first_padded = extended(first_stack, (("ha", 1),), 1)
+    first_padded = extended(first_stack, 1, 1)
     block_out = (mixed.astype(jnp.float32) + conv_taps(first_padded, w_first, 3)).astype(
         jnp.bfloat16
     )
-    enlarged = jnp.repeat(jnp.repeat(block_out, 2, axis=1), 2, axis=2)
-    up_padded = extended(enlarged, (("ha", 1),), 1)
+    block_padded = extended(block_out, 1, 1)
+    enlarged = jnp.repeat(jnp.repeat(block_padded, 2, axis=1), 2, axis=2)
+    up_padded = enlarged[:, 1 : enlarged.shape[1] - 1]
     upsampled = conv_taps(up_padded, w_upsample[None], 1).astype(jnp.bfloat16)
     second_in = jax.nn.silu(rms_scale(upsampled)).astype(jnp.bfloat16)
     second_stack = jnp.concatenate([second_cache, second_in], axis=0)
-    second_padded = extended(second_stack, (("ha", 1),), 1)
+    second_padded = extended(second_stack, 1, 1)
     return (upsampled.astype(jnp.float32) + conv_taps(second_padded, w_second, 3)).astype(
         jnp.bfloat16
     )

time: 178 us -> 124 us (0.70)
  waiting for transfers between devices: 102 us -> 43.2 us
  between operations: 13.9 us -> 0.64 us
  local copies, waits for them, and re-layouts: 11.8 us -> 21.4 us
  starting transfers between devices: 15.6 us -> 23.1 us
    all_gather x2 -> x0, waiting for transfers between devices: 86.8 us -> none  [the longest x1 44.2 us: per_device(): lax.all_gather(keys_own, 'ha', axis=1, tiled=True)]
    ppermute x6 -> x14, waiting for transfers between devices: 15.6 us -> 43.2 us  [the longest x7 30 us: gather_rows(): pieces.append(lax.ppermute(x, 'ha', pairs))]
    ppermute x6 -> x14, starting transfers between devices: 15.5 us -> 23.1 us  [the longest x3 9.38 us: halo_rows(): after = lax.ppermute(first, 'ha', down)]
    dot_general x1 -> x2, matrix products: 3.29 us -> 10.2 us  [the longest x1 5.21 us: per_device(): jnp.einsum('fqc,fkc->fqk', queries, keys_all, preferred_element_type=jnp....]
    reshape x0 -> x1, local copies, waits for them, and re-layouts: none -> 5.03 us  [per_device(): enlarged = jnp.repeat(jnp.repeat(block_padded, 2, axis=1), 2, axis=2)]
    dot_general x2 -> x1, matrix products: 4.17 us -> 1.01 us  [project_rows(): jnp.einsum('ftc,cd->ftd', tokens, weight, preferred_element_type=jnp.floa...]
    broadcast_in_dim x3 -> x2, local copies, waits for them, and re-layouts: 0.42 us -> 2.99 us  [per_device(): enlarged = jnp.repeat(jnp.repeat(block_padded, 2, axis=1), 2, axis=2)]
    slice x6 -> x7, local copies, waits for them, and re-layouts: 3.43 us -> 4.03 us  [conv_taps(): window[:, :, col_off:col_off + width_out]]
  transfers between devices with their start and end apart: 8 -> 14, of which waited for: 6 -> 10; matrix products, arithmetic and copies ran while one was open for 7% -> 8% of each run, Pallas kernels for 0% -> 0%
where the time goes in v1:
time: 124 us; the launch traced here: 122 us
  waiting for transfers between devices  43.2 us (35%)
  matrix products  25.8 us (21%)
  starting transfers between devices  23.1 us (19%)
  local copies, waits for them, and re-layouts  21.4 us (17%)
  other arithmetic  7.62 us (6%)
    ppermute x7, waiting for transfers between devices, gather_rows(): pieces.append(lax.ppermute(x, 'ha', pairs))  30 us
    dot_general x21, matrix products, conv_taps(): jnp.einsum('fhwc,cd->fhwd', stacked, kernel, preferred_element_type=jnp.f...  13.2 us
    ppermute x3, waiting for transfers between devices, halo_rows(): after = lax.ppermute(first, 'ha', down)  9.83 us
    ppermute x3, starting transfers between devices, halo_rows(): after = lax.ppermute(first, 'ha', down)  9.38 us
    ppermute x7, starting transfers between devices, gather_rows(): pieces.append(lax.ppermute(x, 'ha', pairs))  7.15 us
    ppermute x3, starting transfers between devices, halo_rows(): before = lax.ppermute(last, 'ha', up)  6.04 us
    slice x6, local copies, waits for them, and re-layouts, conv_taps(): kernel = weight[time_off, row_off].reshape(3 * in_channels, out_channels)  5.41 us
    dot_general x1, matrix products, per_device(): jnp.einsum('fqc,fkc->fqk', queries, keys_all, preferred_element_type=jnp....  5.21 us
  transfers between devices with their start and end apart: 14, of which 10 were waited for; matrix products, arithmetic and copies ran while one was open for 8% of the time, Pallas kernels for 0%

profile of v1, /device:TPU:13, one launch (start us, length us, event | category | flops | bytes accessed | tf_op | source)
XLA Modules:
  0.0 121.8 jit_solution(11245171781005843114)
XLA Ops:
  0.0 1.2 %collective-permute-start = (bf16[2,1,128,384]{3,2,1,0:T(8,128)(2,1)}, bf16[2,1,128,384]{3,2,1,0:T(8,128)(2,1)S(1)}, u32[]{:S(2)}, u32[]{:S(2)}) collective-permute-start(bf16[2,1,128,384]{3,2,1,0:T(8,128)(2,1)} %param.10), channel_id=1, source_target_pairs={{0,2},{1,3},{2,4},{3,5},{4,6},{5,7},{6,8},{7,9},{8,10},{9,11},{10,... | collective-permute-start | bytes 589832 | tf_op jit(solution)/shard_map/ppermute | solution.py:33
  1.2 1.3 %collective-permute-start.1 = (bf16[2,1,128,384]{3,2,1,0:T(8,128)(2,1)}, bf16[2,1,128,384]{3,2,1,0:T(8,128)(2,1)S(1)}, u32[]{:S(2)}, u32[]{:S(2)}) collective-permute-start(bf16[2,1,128,384]{3,2,1,0:T(8,128)(2,1)} %param.10), channel_id=1, source_target_pairs={{0,4},{1,5},{2,6},{3,7},{4,8},{5,9},{6,10},{7,11},{8,12},{9,13},{1... | collective-permute-start | bytes 589832 | tf_op jit(solution)/shard_map/ppermute | solution.py:33
  2.5 1.0 collective-permute-start.2
  3.5 1.3 %collective-permute-start.3 = (bf16[2,1,128,384]{3,2,1,0:T(8,128)(2,1)}, bf16[2,1,128,384]{3,2,1,0:T(8,128)(2,1)S(1)}, u32[]{:S(2)}, u32[]{:S(2)}) collective-permute-start(bf16[2,1,128,384]{3,2,1,0:T(8,128)(2,1)} %param.10), channel_id=1, source_target_pairs={{0,8},{1,9},{2,10},{3,11},{4,12},{5,13},{6,14},{7,15},{8,0},{9,1},... | collective-permute-start | bytes 589832 | tf_op jit(solution)/shard_map/ppermute | solution.py:33
  4.8 1.0 collective-permute-start.4
  5.9 1.0 constant_dynamic-update-slice_fusion.7
  6.9 1.3 %collective-permute-start.5 = (bf16[2,1,128,384]{3,2,1,0:T(8,128)(2,1)}, bf16[2,1,128,384]{3,2,1,0:T(8,128)(2,1)S(1)}, u32[]{:S(2)}, u32[]{:S(2)}) collective-permute-start(bf16[2,1,128,384]{3,2,1,0:T(8,128)(2,1)} %param.10), channel_id=1, source_target_pairs={{0,12},{1,13},{2,14},{3,15},{4,0},{5,1},{6,2},{7,3},{8,4},{9,5},{1... | collective-permute-start | bytes 589832 | tf_op jit(solution)/shard_map/ppermute | solution.py:33
  8.2 1.9 %collective-permute-done.1 = bf16[2,1,128,384]{3,2,1,0:T(8,128)(2,1)S(1)} collective-permute-done((bf16[2,1,128,384]{3,2,1,0:T(8,128)(2,1)}, bf16[2,1,128,384]{3,2,1,0:T(8,128)(2,1)S(1)}, u32[]{:S(2)}, u32[]{:S(2)}) %collective-permute-start.1) | collective-permute-done | bytes 196640 | tf_op jit(solution)/shard_map/ppermute | solution.py:33
  10.2 20.2 %collective-permute-done.2 = bf16[2,1,128,384]{3,2,1,0:T(8,128)(2,1)S(1)} collective-permute-done((bf16[2,1,128,384]{3,2,1,0:T(8,128)(2,1)}, bf16[2,1,128,384]{3,2,1,0:T(8,128)(2,1)S(1)}, u32[]{:S(2)}, u32[]{:S(2)}) %collective-permute-start.2) | collective-permute-done | bytes 196640 | tf_op jit(solution)/shard_map/ppermute | solution.py:33
  30.5 4.1 %collective-permute-done.3 = bf16[2,1,128,384]{3,2,1,0:T(8,128)(2,1)S(1)} collective-permute-done((bf16[2,1,128,384]{3,2,1,0:T(8,128)(2,1)}, bf16[2,1,128,384]{3,2,1,0:T(8,128)(2,1)S(1)}, u32[]{:S(2)}, u32[]{:S(2)}) %collective-permute-start.3) | collective-permute-done | bytes 196640 | tf_op jit(solution)/shard_map/ppermute | solution.py:33
  34.8 2.7 %collective-permute-done.5 = bf16[2,1,128,384]{3,2,1,0:T(8,128)(2,1)S(1)} collective-permute-done((bf16[2,1,128,384]{3,2,1,0:T(8,128)(2,1)}, bf16[2,1,128,384]{3,2,1,0:T(8,128)(2,1)S(1)}, u32[]{:S(2)}, u32[]{:S(2)}) %collective-permute-start.5) | collective-permute-done | bytes 196640 | tf_op jit(solution)/shard_map/ppermute | solution.py:33
  37.5 1.1 collective-permute-done.6
  38.7 0.6 collective-permute-start.7
  39.4 1.0 convolution_convert_fusion.2
  40.4 1.9 %collective-permute-done.7 = bf16[2,8,128,384]{3,2,1,0:T(8,128)(2,1)S(1)} collective-permute-done((bf16[2,8,128,384]{3,2,1,0:T(8,128)(2,1)S(1)}, bf16[2,8,128,384]{3,2,1,0:T(8,128)(2,1)S(1)}, u32[]{:S(2)}, u32[]{:S(2)}) %collective-permute-start.7) | collective-permute-done | bytes 1572896 | tf_op jit(solution)/shard_map/ppermute | solution.py:36
  42.6 0.7 multiply_reduce_fusion
  43.3 0.7 fusion
  44.1 5.2 %fusion.187 = (f32[2,128]{1,0:T(2,128)S(1)}, f32[2,128,2048]{2,1,0:T(8,128)}) fusion(bf16[2,128,384]{2,1,0:T(8,128)(2,1)} %convolution_convert_fusion.2, bf16[2,2048,384]{2,1,0:T(8,128)(2,1)S(1)} %fusion, bf16[384,384]{1,0:T(8,128)(2,1)S(1)} %copy-done), kind=kOutput, calls=%fused_computation.260 | convolution fusion | flops 1613233920 | bytes 5735424 | tf_op jit(solution)/shard_map/fqc,fkc->fqk/dot_general | solution.py:95
  49.3 2.0 %fusion.24 = f32[2,128]{1,0:T(2,128)S(1)} fusion(f32[2,128,2048]{2,1,0:T(8,128)} %get-tuple-element.104, f32[2,128]{1,0:T(2,128)S(1)} %get-tuple-element.103), kind=kLoop, calls=%fused_computation.36 | loop fusion | flops 1048320 | bytes 2099200 | tf_op jit(solution)/shard_map/reduce_sum | solution.py:100
  51.3 4.9 %fusion.98 = bf16[2,128,384]{2,1,0:T(8,128)(2,1)} fusion(bf16[2,2048,384]{2,1,0:T(8,128)(2,1)S(1)} %fusion, f32[2,128,2048]{2,1,0:T(8,128)} %get-tuple-element.104, f32[2,128]{1,0:T(2,128)S(1)} %get-tuple-element.103, bf16[384,384]{1,0:T(8,128)(2,1)} %param.15, f32[2,128]{1,0:T(2,128)S(1)} %fusion.24), kind=kOutput, calls=%fused_computation.124 | convolution fusion | flops 1613430784 | bytes 5736448 | tf_op jit(solution)/shard_map/fqk,fkc->fqc/dot_general | solution.py:101
  56.2 1.4 %multiply_reduce_fusion.2 = (f32[2,128]{1,0:T(2,128)S(1)}, f32[2,1,128,384]{3,2,0,1:T(8,128)S(1)}) fusion(bf16[2,128,384]{2,1,0:T(8,128)(2,1)} %fusion.98, bf16[384,384]{1,0:T(8,128)(2,1)} %param.16, bf16[2,1,128,384]{3,2,1,0:T(8,128)(2,1)S(1)} %copy-done.4), kind=kOutput, calls=%fused_computation.198 | convolution fusion | flops 76087040 | bytes 1082368 | tf_op jit(solution)/shard_map/ftc,cd->ftd/dot_general | solution.py:108
  57.9 1.0 pad_maximum_fusion.3
  58.9 2.1 %collective-permute-start.8 = (bf16[4,1,128,384]{3,2,0,1:T(8,128)(2,1)S(1)}, bf16[4,1,128,384]{3,2,0,1:T(8,128)(2,1)S(1)}, u32[]{:S(2)}, u32[]{:S(2)}) collective-permute-start(bf16[4,1,128,384]{3,2,0,1:T(8,128)(2,1)S(1)} %pad_maximum_fusion.3), channel_id=1, source_target_pairs={{0,1},{1,2},{2,3},{3,4},{4,5},{5,6},{6,7},{7,8},{8,9},{9,10},{10,1... | collective-permute-start | bytes 1179656 | tf_op jit(solution)/shard_map/ppermute | solution.py:15
  60.9 2.6 %collective-permute-start.9 = (bf16[4,1,128,384]{3,2,0,1:T(8,128)(2,1)S(1)}, bf16[4,1,128,384]{3,2,0,1:T(8,128)(2,1)S(1)}, u32[]{:S(2)}, u32[]{:S(2)}) collective-permute-start(bf16[4,1,128,384]{3,2,0,1:T(8,128)(2,1)S(1)} %pad_maximum_fusion.3), channel_id=1, source_target_pairs={{1,0},{2,1},{3,2},{4,3},{5,4},{6,5},{7,6},{8,7},{9,8},{10,9},{11,1... | collective-permute-start | bytes 1179656 | tf_op jit(solution)/shard_map/ppermute | solution.py:16
  63.5 3.9 %fusion.177 = (bf16[1,1,3,384,384]{4,3,2,1,0:T(8,128)(2,1)S(1)}, bf16[1,1,3,384,384]{4,3,2,1,0:T(8,128)(2,1)S(1)}, bf16[1,1,3,384,384]{4,3,2,1,0:T(8,128)(2,1)S(...) fusion(bf16[3,3,3,384,384]{4,3,2,1,0:T(8,128)(2,1)} %param.17), kind=kLoop, calls=%fused_computation.250 | loop fusion | bytes 15925248 | tf_op jit(solution)/shard_map/slice | solution.py:59
  67.5 3.5 %collective-permute-done.9 = bf16[4,1,128,384]{3,2,0,1:T(8,128)(2,1)S(1)} collective-permute-done((bf16[4,1,128,384]{3,2,0,1:T(8,128)(2,1)S(1)}, bf16[4,1,128,384]{3,2,0,1:T(8,128)(2,1)S(1)}, u32[]{:S(2)}, u32[]{:S(2)}) %collective-permute-start.9) | collective-permute-done | bytes 393248 | tf_op jit(solution)/shard_map/ppermute | solution.py:16
  71.4 0.7 fusion.182
  76.5 1.9 %collective-permute-start.10 = (bf16[2,1,128,384]{3,2,0,1:T(8,128)(2,1)S(1)}, bf16[2,1,128,384]{3,2,0,1:T(8,128)(2,1)S(1)}, u32[]{:S(2)}, u32[]{:S(2)}) collective-permute-start(bf16[2,1,128,384]{3,2,0,1:T(8,128)(2,1)S(1)} %fusion.94), channel_id=1, source_target_pairs={{0,1},{1,2},{2,3},{3,4},{4,5},{5,6},{6,7},{7,8},{8,9},{9,10},{10,1... | collective-permute-start | bytes 589832 | tf_op jit(solution)/shard_map/ppermute | solution.py:15
  78.5 3.8 %collective-permute-start.11 = (bf16[2,1,128,384]{3,2,0,1:T(8,128)(2,1)S(1)}, bf16[2,1,128,384]{3,2,0,1:T(8,128)(2,1)S(1)}, u32[]{:S(2)}, u32[]{:S(2)}) collective-permute-start(bf16[2,1,128,384]{3,2,0,1:T(8,128)(2,1)S(1)} %fusion.94), channel_id=1, source_target_pairs={{1,0},{2,1},{3,2},{4,3},{5,4},{6,5},{7,6},{8,7},{9,8},{10,9},{11,1... | collective-permute-start | bytes 589832 | tf_op jit(solution)/shard_map/ppermute | solution.py:16
  82.8 1.1 reshape.139
  85.5 1.0 collective-permute-done.11
  86.8 2.9 %broadcast_in_dim.7 = bf16[2,6,128,2,384]{4,3,2,1,0:T(2,128)(2,1)} broadcast(bf16[2,6,128,384]{3,2,1,0:T(8,128)(2,1)S(1)} %bitcast.175), dimensions={0,1,2,4} | broadcast | bytes 3538944 | tf_op jit(solution)/shard_map/broadcast_in_dim | solution.py:120
  89.6 5.0 %reshape.124 = bf16[2,6,256,384]{3,2,1,0:T(8,128)(2,1)S(1)} reshape(bf16[2,6,128,2,384]{4,3,2,1,0:T(2,128)(2,1)} %broadcast_in_dim.7) | data formatting | bytes 4718592 | tf_op jit(solution)/shard_map/reshape | solution.py:120
  94.8 1.3 %pad_slice_fusion.5 = (bf16[2,2,256,384]{3,2,1,0:T(8,128)(2,1)S(1)}, bf16[2,2,256,384]{3,2,1,0:T(8,128)(2,1)S(1)}, bf16[2,2,256,384]{3,2,1,0:T(8,128)(2,1)S(1)},...) fusion(bf16[2,4,256,384]{3,2,1,0:T(8,128)(2,1)S(1)} %slice.488,, ...), kind=kLoop, calls=%fused_computation.133 | loop fusion | bytes 11010048 | tf_op jit(solution)/shard_map/slice | solution.py:57
  96.2 1.1 fusion.6
  97.3 1.1 fusion.31
  98.5 1.2 multiply_reduce_fusion.1
  100.0 2.1 %collective-permute-start.12 = (bf16[4,1,256,192]{2,3,1,0:T(8,128)(2,1)S(1)}, bf16[4,1,256,192]{2,3,1,0:T(8,128)(2,1)S(1)}, u32[]{:S(2)}, u32[]{:S(2)}) collective-permute-start(bf16[4,1,256,192]{2,3,1,0:T(8,128)(2,1)S(1)} %get-tuple-element.79), channel_id=1, source_target_pairs={{0,1},{1,2},{2,3},{3,4},{4,5},{5,6},{6,7},{7,8},{8,9},{9,10},{10,1... | collective-permute-start | bytes 1179656 | tf_op jit(solution)/shard_map/ppermute | solution.py:15
  102.1 3.0 %collective-permute-start.13 = (bf16[4,1,256,192]{2,3,1,0:T(8,128)(2,1)S(1)}, bf16[4,1,256,192]{2,3,1,0:T(8,128)(2,1)S(1)}, u32[]{:S(2)}, u32[]{:S(2)}) collective-permute-start(bf16[4,1,256,192]{2,3,1,0:T(8,128)(2,1)S(1)} %get-tuple-element.80), channel_id=1, source_target_pairs={{1,0},{2,1},{3,2},{4,3},{5,4},{6,5},{7,6},{8,7},{9,8},{10,9},{11,1... | collective-permute-start | bytes 1179656 | tf_op jit(solution)/shard_map/ppermute | solution.py:16
  105.3 1.5 %collective-permute-done.12 = bf16[4,1,256,192]{2,3,1,0:T(8,128)(2,1)S(1)} collective-permute-done((bf16[4,1,256,192]{2,3,1,0:T(8,128)(2,1)S(1)}, bf16[4,1,256,192]{2,3,1,0:T(8,128)(2,1)S(1)}, u32[]{:S(2)}, u32[]{:S(2)}) %collective-permute-start.12) | collective-permute-done | bytes 393248 | tf_op jit(solution)/shard_map/ppermute | solution.py:15
  106.8 5.4 %collective-permute-done.13 = bf16[4,1,256,192]{2,3,1,0:T(8,128)(2,1)S(1)} collective-permute-done((bf16[4,1,256,192]{2,3,1,0:T(8,128)(2,1)S(1)}, bf16[4,1,256,192]{2,3,1,0:T(8,128)(2,1)S(1)}, u32[]{:S(2)}, u32[]{:S(2)}) %collective-permute-start.13) | collective-permute-done | bytes 393248 | tf_op jit(solution)/shard_map/ppermute | solution.py:16
  112.5 2.0 %select_maximum_fusion = bf16[4,4,258,192]{2,3,1,0:T(8,128)(2,1)S(1)} fusion(bf16[4,1,256,192]{2,3,1,0:T(8,128)(2,1)S(1)} %collective-permute-done.13, bf16[4,1,256,192]{2,3,1,0:T(8,128)(2,1)S(1)} %collective-permute-done.12, bf16[2,2,256,192]{2,3,1,0:T(8,128)(2,1)S(1)} %multiply_convert_fusion, bf16[2,2,256,192]{2,3,1,0:T(8,128)(2,1)S(1)} %copy-done.2), kind=kLoop, calls=%fused_computation.12 | loop fusion | flops 11888640 | bytes 3158016 | tf_op jit(solution)/shard_map/concatenate | solution.py:22
  114.4 1.7 %fusion.179 = (bf16[2,2,256,192]{2,3,1,0:T(8,128)(2,1)S(1)}, bf16[2,2,256,192]{2,3,1,0:T(8,128)(2,1)S(1)}, bf16[2,2,256,192]{2,3,1,0:T(8,128)(2,1)S(1)}, bf16[2,...) fusion(bf16[4,4,258,192]{2,3,1,0:T(8,128)(2,1)S(1)} %select_max, ...), kind=kLoop, calls=%fused_computation.252 | loop fusion | bytes 14155776 | tf_op jit(solution)/shard_map/slice | solution.py:57
  116.8 0.5 convolution_add_fusion.7
  117.3 0.5 convolution_add_fusion.6
  118.4 0.5 convolution_add_fusion.4
  120.0 0.5 convolution_add_fusion.1
  120.5 1.3 %fusion.43 = bf16[2,2,256,192]{2,3,1,0:T(8,128)(2,1)} fusion(f32[2,2,256,192]{2,3,1,0:T(8,128)S(1)} %get-tuple-element.108, f32[2,2,256,192]{2,3,1,0:T(8,128)S(1)} %convolution_add_fusion.1, bf16[576,192,1,1]{1,0,3,2:T(8,128)(2,1)S(1)} %bitcast.190, bf16[2,2,256,192]{2,3,1,0:T(8,128)(2,1)S(1)} %get-tuple-element.40, ...), kind=kOutput, calls=%fused_computation.57 | convolution fusion | flops 230621184 | bytes 3366912 | tf_op jit(solution)/shard_map/fhwc,cd->fhwd/dot_general | solution.py:60
  (73 shorter events, 11.3 us)
Async XLA Ops:
  0.0 44.0 %copy-start = (bf16[384,384]{1,0:T(8,128)(2,1)S(1)}, bf16[384,384]{1,0:T(8,128)(2,1)}, u32[]{:S(2)}) copy-start(bf16[384,384]{1,0:T(8,128)(2,1)} %param.14) | copy-start | bytes 884740
  0.0 6.9 %collective-permute-start = (bf16[2,1,128,384]{3,2,1,0:T(8,128)(2,1)}, bf16[2,1,128,384]{3,2,1,0:T(8,128)(2,1)S(1)}, u32[]{:S(2)}, u32[]{:S(2)}) collective-permute-start(bf16[2,1,128,384]{3,2,1,0:T(8,128)(2,1)} %param.10), channel_id=1, source_target_pairs={{0,2},{1,3},{2,4},{3,5},{4,6},{5,7},{6,8},{7,9},{8,10},{9,11},{10,... | collective-permute-start | bytes 589832 | tf_op jit(solution)/shard_map/ppermute | solution.py:33
  1.2 8.9 %collective-permute-start.1 = (bf16[2,1,128,384]{3,2,1,0:T(8,128)(2,1)}, bf16[2,1,128,384]{3,2,1,0:T(8,128)(2,1)S(1)}, u32[]{:S(2)}, u32[]{:S(2)}) collective-permute-start(bf16[2,1,128,384]{3,2,1,0:T(8,128)(2,1)} %param.10), channel_id=1, source_target_pairs={{0,4},{1,5},{2,6},{3,7},{4,8},{5,9},{6,10},{7,11},{8,12},{9,13},{1... | collective-permute-start | bytes 589832 | tf_op jit(solution)/shard_map/ppermute | solution.py:33
  2.5 27.9 %collective-permute-start.2 = (bf16[2,1,128,384]{3,2,1,0:T(8,128)(2,1)}, bf16[2,1,128,384]{3,2,1,0:T(8,128)(2,1)S(1)}, u32[]{:S(2)}, u32[]{:S(2)}) collective-permute-start(bf16[2,1,128,384]{3,2,1,0:T(8,128)(2,1)} %param.10), channel_id=1, source_target_pairs={{0,6},{1,7},{2,8},{3,9},{4,10},{5,11},{6,12},{7,13},{8,14},{9,15},... | collective-permute-start | bytes 589832 | tf_op jit(solution)/shard_map/ppermute | solution.py:33
  3.5 31.1 %collective-permute-start.3 = (bf16[2,1,128,384]{3,2,1,0:T(8,128)(2,1)}, bf16[2,1,128,384]{3,2,1,0:T(8,128)(2,1)S(1)}, u32[]{:S(2)}, u32[]{:S(2)}) collective-permute-start(bf16[2,1,128,384]{3,2,1,0:T(8,128)(2,1)} %param.10), channel_id=1, source_target_pairs={{0,8},{1,9},{2,10},{3,11},{4,12},{5,13},{6,14},{7,15},{8,0},{9,1},... | collective-permute-start | bytes 589832 | tf_op jit(solution)/shard_map/ppermute | solution.py:33
  4.8 29.8 %collective-permute-start.4 = (bf16[2,1,128,384]{3,2,1,0:T(8,128)(2,1)}, bf16[2,1,128,384]{3,2,1,0:T(8,128)(2,1)S(1)}, u32[]{:S(2)}, u32[]{:S(2)}) collective-permute-start(bf16[2,1,128,384]{3,2,1,0:T(8,128)(2,1)} %param.10), channel_id=1, source_target_pairs={{0,10},{1,11},{2,12},{3,13},{4,14},{5,15},{6,0},{7,1},{8,2},{9,3},... | collective-permute-start | bytes 589832 | tf_op jit(solution)/shard_map/ppermute | solution.py:33
  6.9 32.4 %copy-start.3 = (bf16[2,1,128,384]{3,2,1,0:T(8,128)(2,1)S(1)}, bf16[2,1,128,384]{3,2,1,0:T(8,128)(2,1)}, u32[]{:S(2)}) copy-start(bf16[2,1,128,384]{3,2,1,0:T(8,128)(2,1)} %param.10) | copy-start | bytes 589828
  6.9 30.6 %collective-permute-start.5 = (bf16[2,1,128,384]{3,2,1,0:T(8,128)(2,1)}, bf16[2,1,128,384]{3,2,1,0:T(8,128)(2,1)S(1)}, u32[]{:S(2)}, u32[]{:S(2)}) collective-permute-start(bf16[2,1,128,384]{3,2,1,0:T(8,128)(2,1)} %param.10), channel_id=1, source_target_pairs={{0,12},{1,13},{2,14},{3,15},{4,0},{5,1},{6,2},{7,3},{8,4},{9,5},{1... | collective-permute-start | bytes 589832 | tf_op jit(solution)/shard_map/ppermute | solution.py:33
  8.2 31.2 %copy-start.9 = (bf16[384,384]{1,0:T(8,128)(2,1)S(1)}, bf16[384,384]{1,0:T(8,128)(2,1)}, u32[]{:S(2)}) copy-start(bf16[384,384]{1,0:T(8,128)(2,1)} %param.13) | copy-start | bytes 884740
  10.1 28.5 %collective-permute-start.6 = (bf16[2,1,128,384]{3,2,1,0:T(8,128)(2,1)}, bf16[2,1,128,384]{3,2,1,0:T(8,128)(2,1)S(1)}, u32[]{:S(2)}, u32[]{:S(2)}) collective-permute-start(bf16[2,1,128,384]{3,2,1,0:T(8,128)(2,1)} %param.10), channel_id=1, source_target_pairs={{0,14},{1,15},{2,0},{3,1},{4,2},{5,3},{6,4},{7,5},{8,6},{9,7},{10,... | collective-permute-start | bytes 589832 | tf_op jit(solution)/shard_map/ppermute | solution.py:33
  38.7 3.6 %collective-permute-start.7 = (bf16[2,8,128,384]{3,2,1,0:T(8,128)(2,1)S(1)}, bf16[2,8,128,384]{3,2,1,0:T(8,128)(2,1)S(1)}, u32[]{:S(2)}, u32[]{:S(2)}) collective-permute-start(bf16[2,8,128,384]{3,2,1,0:T(8,128)(2,1)S(1)} %get-tuple-element.87), channel_id=1, source_target_pairs={{0,1},{1,0},{2,3},{3,2},{4,5},{5,4},{6,7},{7,6},{8,9},{9,8},{10,11... | collective-permute-start | bytes 4718600 | tf_op jit(solution)/shard_map/ppermute | solution.py:36
  51.3 5.0 %copy-start.4 = (bf16[2,1,128,384]{3,2,1,0:T(8,128)(2,1)S(1)}, bf16[2,1,128,384]{3,2,1,0:T(8,128)(2,1)}, u32[]{:S(2)}) copy-start(bf16[2,1,128,384]{3,2,1,0:T(8,128)(2,1)} %param.10) | copy-start | bytes 589828
  58.9 8.6 %copy-start.6 = (bf16[2,1,128,384]{3,2,1,0:T(8,128)(2,1)S(1)}, bf16[2,1,128,384]{3,2,1,0:T(8,128)(2,1)}, u32[]{:S(2)}) copy-start(bf16[2,1,128,384]{3,2,1,0:T(8,128)(2,1)} %param.11) | copy-start | bytes 589828
  58.9 8.7 %collective-permute-start.8 = (bf16[4,1,128,384]{3,2,0,1:T(8,128)(2,1)S(1)}, bf16[4,1,128,384]{3,2,0,1:T(8,128)(2,1)S(1)}, u32[]{:S(2)}, u32[]{:S(2)}) collective-permute-start(bf16[4,1,128,384]{3,2,0,1:T(8,128)(2,1)S(1)} %pad_maximum_fusion.3), channel_id=1, source_target_pairs={{0,1},{1,2},{2,3},{3,4},{4,5},{5,6},{6,7},{7,8},{8,9},{9,10},{10,1... | collective-permute-start | bytes 1179656 | tf_op jit(solution)/shard_map/ppermute | solution.py:15
  60.9 10.1 %collective-permute-start.9 = (bf16[4,1,128,384]{3,2,0,1:T(8,128)(2,1)S(1)}, bf16[4,1,128,384]{3,2,0,1:T(8,128)(2,1)S(1)}, u32[]{:S(2)}, u32[]{:S(2)}) collective-permute-start(bf16[4,1,128,384]{3,2,0,1:T(8,128)(2,1)S(1)} %pad_maximum_fusion.3), channel_id=1, source_target_pairs={{1,0},{2,1},{3,2},{4,3},{5,4},{6,5},{7,6},{8,7},{9,8},{10,9},{11,1... | collective-permute-start | bytes 1179656 | tf_op jit(solution)/shard_map/ppermute | solution.py:16
  76.0 6.2 %copy-start.7 = (bf16[3,3,384,192]{2,3,1,0:T(8,128)(2,1)S(1)}, bf16[3,3,384,192]{2,3,1,0:T(8,128)(2,1)}, u32[]{:S(2)}) copy-start(bf16[3,3,384,192]{2,3,1,0:T(8,128)(2,1)} %param.18) | copy-start | bytes 3981316
  76.5 9.0 %collective-permute-start.10 = (bf16[2,1,128,384]{3,2,0,1:T(8,128)(2,1)S(1)}, bf16[2,1,128,384]{3,2,0,1:T(8,128)(2,1)S(1)}, u32[]{:S(2)}, u32[]{:S(2)}) collective-permute-start(bf16[2,1,128,384]{3,2,0,1:T(8,128)(2,1)S(1)} %fusion.94), channel_id=1, source_target_pairs={{0,1},{1,2},{2,3},{3,4},{4,5},{5,6},{6,7},{7,8},{8,9},{9,10},{10,1... | collective-permute-start | bytes 589832 | tf_op jit(solution)/shard_map/ppermute | solution.py:15
  78.5 8.0 %collective-permute-start.11 = (bf16[2,1,128,384]{3,2,0,1:T(8,128)(2,1)S(1)}, bf16[2,1,128,384]{3,2,0,1:T(8,128)(2,1)S(1)}, u32[]{:S(2)}, u32[]{:S(2)}) collective-permute-start(bf16[2,1,128,384]{3,2,0,1:T(8,128)(2,1)S(1)} %fusion.94), channel_id=1, source_target_pairs={{1,0},{2,1},{3,2},{4,3},{5,4},{6,5},{7,6},{8,7},{9,8},{10,9},{11,1... | collective-permute-start | bytes 589832 | tf_op jit(solution)/shard_map/ppermute | solution.py:16
  94.8 1.3 %copy-start.8 = (bf16[1152,192,1,1]{0,1,2,3:T(8,128)(2,1)S(1)}, bf16[1152,192,1,1]{0,1,2,3:T(8,128)(2,1)}, u32[]{:S(2)}) copy-start(bf16[1152,192,1,1]{0,1,2,3:T(8,128)(2,1)} %reshape.139) | copy-start | bytes 1327108
  98.5 1.4 %copy-start.2 = (bf16[2,2,256,192]{2,3,1,0:T(8,128)(2,1)S(1)}, bf16[2,2,256,192]{2,3,1,0:T(8,128)(2,1)}, u32[]{:S(2)}) copy-start(bf16[2,2,256,192]{2,3,1,0:T(8,128)(2,1)} %param.12) | copy-start | bytes 1179652
  99.7 5.4 %copy-start.5 = (bf16[3,3,3,192,192]{4,3,2,1,0:T(8,128)(2,1)S(1)}, bf16[3,3,3,192,192]{4,3,2,1,0:T(8,128)(2,1)}, u32[]{:S(2)}) copy-start(bf16[3,3,3,192,192]{4,3,2,1,0:T(8,128)(2,1)} %param.19) | copy-start | bytes 5971972
  100.0 6.8 %collective-permute-start.12 = (bf16[4,1,256,192]{2,3,1,0:T(8,128)(2,1)S(1)}, bf16[4,1,256,192]{2,3,1,0:T(8,128)(2,1)S(1)}, u32[]{:S(2)}, u32[]{:S(2)}) collective-permute-start(bf16[4,1,256,192]{2,3,1,0:T(8,128)(2,1)S(1)} %get-tuple-element.79), channel_id=1, source_target_pairs={{0,1},{1,2},{2,3},{3,4},{4,5},{5,6},{6,7},{7,8},{8,9},{9,10},{10,1... | collective-permute-start | bytes 1179656 | tf_op jit(solution)/shard_map/ppermute | solution.py:15
  102.1 10.1 %collective-permute-start.13 = (bf16[4,1,256,192]{2,3,1,0:T(8,128)(2,1)S(1)}, bf16[4,1,256,192]{2,3,1,0:T(8,128)(2,1)S(1)}, u32[]{:S(2)}, u32[]{:S(2)}) collective-permute-start(bf16[4,1,256,192]{2,3,1,0:T(8,128)(2,1)S(1)} %get-tuple-element.80), channel_id=1, source_target_pairs={{1,0},{2,1},{3,2},{4,3},{5,4},{6,5},{7,6},{8,7},{9,8},{10,9},{11,1... | collective-permute-start | bytes 1179656 | tf_op jit(solution)/shard_map/ppermute | solution.py:16
  120.5 1.3 %copy-start.1 = (bf16[384,384]{1,0:T(8,128)(2,1)S(1)}, bf16[384,384]{1,0:T(8,128)(2,1)}, u32[]{:S(2)}) copy-start(bf16[384,384]{1,0:T(8,128)(2,1)} %param.14) | copy-start | bytes 884740

commit v2 on v1

v2 whole, which is shorter than its diff:
```python
import math

import jax
import jax.numpy as jnp
from jax import lax
from jax.sharding import PartitionSpec as P


def halo_rows(x, width):
    count, length = (lax.axis_size("ha"), x.shape[1])
    up = [(i, i + 1) for i in range(count - 1)]
    down = [(j, i) for i, j in up]
    last = lax.slice_in_dim(x, length - width, length, axis=1)
    first = lax.slice_in_dim(x, 0, width, axis=1)
    before = lax.ppermute(last, "ha", up)
    after = lax.ppermute(first, "ha", down)
    return jnp.concatenate([before, x, after], axis=1)


def gather_rows(x):
    count = lax.axis_size("ha")
    chips = count // 2
    pieces = [x]
    for shift in range(1, chips):
        pairs = [
            (2 * c + k, 2 * ((c + shift) % chips) + k) for c in range(chips) for k in range(2)
        ]
        pieces.append(lax.ppermute(x, "ha", pairs))
    own_chip = jnp.concatenate(pieces, axis=1)
    swap = [(2 * c + k, 2 * c + 1 - k) for c in range(chips) for k in range(2)]
    other = lax.ppermute(own_chip, "ha", swap)
    return jnp.concatenate([own_chip, other], axis=1)


def rms_scale(tensor):
    widened = tensor.astype(jnp.float32)
    return widened * lax.rsqrt(jnp.mean(widened * widened, axis=-1, keepdims=True) + 1e-06)


def conv_frames(padded, weight, starts=((0, 1, 2),) * 3, rows=None):
    frames, height, width, channels = padded.shape
    out_rows = height - 2
    cols = jnp.pad(padded, ((0, 0), (0, 0), (1, 1), (0, 0)))
    result = None
    for row_off in range(3):
        if rows is None:
            window = cols[:, row_off : row_off + out_rows]
        else:
            window = jnp.stack([cols[:, r] for r in rows[row_off]], axis=1)
        stacked = jnp.concatenate(
            [window[:, :, s : s + width] for s in starts[row_off]], axis=-1
        )
        kernel = weight[row_off].reshape(3 * channels, weight.shape[-1])
        term = jnp.einsum("fhwc,cd->fhwd", stacked, kernel, preferred_element_type=jnp.float32)
        result = term if result is None else result + term
    return result


def causal_parts(cache_pad, new_pad, weight):
    zero = None
    from_cache = conv_frames(cache_pad, weight[0])
    late = conv_frames(cache_pad[1:2], weight[1])
    zero = jnp.zeros_like(late)
    from_cache = from_cache + jnp.concatenate([late, zero], axis=0)

    def from_new(pad):
        early = conv_frames(pad[0:1], weight[1])
        return conv_frames(pad, weight[2]) + jnp.concatenate([zero, early], axis=0)

    return from_cache, from_new


def project_rows(tokens, weight):
    return jnp.einsum("ftc,cd->ftd", tokens, weight, preferred_element_type=jnp.float32).astype(
        jnp.bfloat16
    )


def upsample_conv(block_pad, weight):
    rows = ((0, 0, 1, 1), (0, 1, 1, 2), (1, 1, 2, 2))
    even = conv_frames(block_pad, weight, starts=((0, 1, 1),) * 3, rows=rows)
    odd = conv_frames(block_pad, weight, starts=((1, 1, 2),) * 3, rows=rows)
    frames, height, width, channels = even.shape
    both = jnp.stack([even, odd], axis=3)
    return both.reshape(frames, height, 2 * width, channels)


def per_device(
    features,
    first_cache,
    second_cache,
    w_query,
    w_key,
    w_value,
    w_output,
    w_first,
    w_upsample,
    w_second,
):
    frame_count, row_count, width_count, channels = features.shape
    me = lax.axis_index("ha")
    count = lax.axis_size("ha")

    first_cache_pad = halo_rows(first_cache, 1)
    second_cache_pad = halo_rows(second_cache, 1)
    first_cached, first_new = causal_parts(first_cache_pad, None, w_first)
    second_cached, second_new = causal_parts(second_cache_pad, None, w_second)

    every_row = gather_rows(features)
    normed_all = rms_scale(every_row).astype(jnp.bfloat16)
    all_tokens = normed_all.reshape(frame_count, -1, channels)
    normed = rms_scale(features).astype(jnp.bfloat16)
    normed_tokens = normed.reshape(frame_count, row_count * width_count, channels)
    queries = project_rows(normed_tokens, w_query)
    keys_all = project_rows(all_tokens, w_key)
    values_all = project_rows(all_tokens, w_value)
    score_scale = 1.0 / math.sqrt(channels)
    scores = (
        jnp.einsum("fqc,fkc->fqk", queries, keys_all, preferred_element_type=jnp.float32)
        * score_scale
    )
    largest = jnp.max(scores, axis=-1)
    weights = jnp.exp(scores - largest[..., None])
    weight_sum = jnp.sum(weights, axis=-1)
    weighted = jnp.einsum(
        "fqk,fkc->fqc",
        weights.astype(jnp.bfloat16),
        values_all,
        preferred_element_type=jnp.float32,
    )
    attended = (weighted / weight_sum[..., None]).astype(jnp.bfloat16)
    projected = jnp.einsum("ftc,cd->ftd", attended, w_output, preferred_element_type=jnp.float32)
    mixed = (
        features.astype(jnp.float32)
        + projected.reshape(frame_count, row_count, width_count, channels)
    ).astype(jnp.bfloat16)
    first_in = jax.nn.silu(rms_scale(mixed)).astype(jnp.bfloat16)
    first_pad = halo_rows(first_in, 1)
    block_out = (mixed.astype(jnp.float32) + first_cached + first_new(first_pad)).astype(
        jnp.bfloat16
    )
    block_pad = halo_rows(block_out, 1)
    upsampled = upsample_conv(block_pad, w_upsample).astype(jnp.bfloat16)
    second_in = jax.nn.silu(rms_scale(upsampled)).astype(jnp.bfloat16)
    row = lax.broadcasted_iota(jnp.int32, (1, second_in.shape[1], 1, 1), 1)
    outside = ((row == 0) & (me == 0)) | ((row == second_in.shape[1] - 1) & (me == count - 1))
    second_in = jnp.where(outside, jnp.zeros_like(second_in), second_in)
    own = upsampled[:, 1 : upsampled.shape[1] - 1]
    return (own.astype(jnp.float32) + second_cached + second_new(second_in)).astype(jnp.bfloat16)


def solution(mesh):
    placed = (
        P("grp", "ha", None, None),
        P("grp", "ha", None, None),
        P("grp", "ha", None, None),
        P(),
        P(),
        P(),
        P(),
        P(),
        P(),
        P(),
    )
    return jax.shard_map(
        per_device,
        mesh=mesh,
        in_specs=placed,
        out_specs=P("grp", "ha", None, None),
        check_vma=False,
    )
```

time: 124 us -> 128 us (1.032)
  waiting for transfers between devices: 43.2 us -> 14.2 us
  local copies, waits for them, and re-layouts: 21.4 us -> 38.2 us
  starting transfers between devices: 23.1 us -> 30.6 us
  matrix products: 25.8 us -> 32.8 us
    ppermute x7, waiting for transfers between devices: 30 us -> 0.02 us  [gather_rows(): pieces.append(lax.ppermute(x, 'ha', pairs))]
    slice x14 -> x38, local copies, waits for them, and re-layouts: 9.6 us -> 22.8 us  [the longest x6 11.4 us: conv_frames(): kernel = weight[row_off].reshape(3 * channels, weight.shape[-1])]
    unnamed x28 -> x114, local copies, waits for them, and re-layouts: 1.43 us -> 9.74 us
    dot_general x21 -> x30, matrix products: 13.2 us -> 20.1 us  [conv_frames(): jnp.einsum('fhwc,cd->fhwd', stacked, kernel, preferred_element_type=jnp.f...]
    ppermute x3 -> x4, starting transfers between devices: 6.04 us -> 12.2 us  [halo_rows(): before = lax.ppermute(last, 'ha', up)]
    reshape x1 -> x0, local copies, waits for them, and re-layouts: 5.03 us -> none  [per_device(): enlarged = jnp.repeat(jnp.repeat(block_padded, 2, axis=1), 2, axis=2)]
    ppermute x3 -> x4, waiting for transfers between devices: 9.83 us -> 13.9 us  [halo_rows(): after = lax.ppermute(first, 'ha', down)]
    broadcast_in_dim x2 -> x0, local copies, waits for them, and re-layouts: 2.99 us -> none  [per_device(): enlarged = jnp.repeat(jnp.repeat(block_padded, 2, axis=1), 2, axis=2)]
  transfers between devices with their start and end apart: 14 -> 16, of which waited for: 10 -> 5; matrix products, arithmetic and copies ran while one was open for 8% -> 30% of each run, Pallas kernels for 0% -> 0%
where the time goes in v2:
time: 128 us; the launch traced here: 126 us
  local copies, waits for them, and re-layouts  38.2 us (30%)
  matrix products  32.8 us (26%)
  starting transfers between devices  30.6 us (24%)
  waiting for transfers between devices  14.2 us (11%)
  other arithmetic  8.54 us (7%)
    dot_general x30, matrix products, conv_frames(): jnp.einsum('fhwc,cd->fhwd', stacked, kernel, preferred_element_type=jnp.f...  20.1 us
    ppermute x4, waiting for transfers between devices, halo_rows(): after = lax.ppermute(first, 'ha', down)  13.9 us
    ppermute x4, starting transfers between devices, halo_rows(): before = lax.ppermute(last, 'ha', up)  12.2 us
    ppermute x4, starting transfers between devices, halo_rows(): after = lax.ppermute(first, 'ha', down)  11.5 us
    slice x6, local copies, waits for them, and re-layouts, conv_frames(): kernel = weight[row_off].reshape(3 * channels, weight.shape[-1])  11.4 us
    unnamed x114, local copies, waits for them, and re-layouts  9.74 us
    slice x24, local copies, waits for them, and re-layouts, conv_frames(): window[:, :, s:s + width]  9.36 us
    ppermute x7, starting transfers between devices, gather_rows(): pieces.append(lax.ppermute(x, 'ha', pairs))  6.85 us
  transfers between devices with their start and end apart: 16, of which 5 were waited for; matrix products, arithmetic and copies ran while one was open for 30% of the time, Pallas kernels for 0%

profile of v2, /device:TPU:13, one launch (start us, length us, event | category | flops | bytes accessed | tf_op | source)
XLA Modules:
  0.0 125.7 jit_solution(9551993226918771999)
XLA Ops:
  0.0 1.2 collective-permute-start
  1.2 1.3 %collective-permute-start.1 = (bf16[2,1,128,384]{3,2,1,0:T(8,128)(2,1)}, bf16[2,1,128,384]{3,2,1,0:T(8,128)(2,1)}, u32[]{:S(2)}, u32[]{:S(2)}) collective-permute-start(bf16[2,1,128,384]{3,2,1,0:T(8,128)(2,1)} %param.10), channel_id=1, source_target_pairs={{0,4},{1,5},{2,6},{3,7},{4,8},{5,9},{6,10},{7,11},{8,12},{9,13},{1... | collective-permute-start | bytes 589832 | tf_op jit(solution)/shard_map/ppermute | solution.py:28
  2.5 1.0 collective-permute-start.2
  3.5 1.3 %collective-permute-start.3 = (bf16[2,1,128,384]{3,2,1,0:T(8,128)(2,1)}, bf16[2,1,128,384]{3,2,1,0:T(8,128)(2,1)}, u32[]{:S(2)}, u32[]{:S(2)}) collective-permute-start(bf16[2,1,128,384]{3,2,1,0:T(8,128)(2,1)} %param.10), channel_id=1, source_target_pairs={{0,8},{1,9},{2,10},{3,11},{4,12},{5,13},{6,14},{7,15},{8,0},{9,1},... | collective-permute-start | bytes 589832 | tf_op jit(solution)/shard_map/ppermute | solution.py:28
  4.8 1.8 %fusion.232 = (bf16[2,1,256,192]{2,3,1,0:T(8,128)(2,1)}, bf16[2,1,256,192]{2,3,1,0:T(8,128)(2,1)}) fusion(bf16[2,2,256,192]{2,3,1,0:T(8,128)(2,1)} %param.12), kind=kLoop, calls=%fused_computation.360 | loop fusion | bytes 786432 | tf_op jit(solution)/shard_map/slice | solution.py:14
  6.6 4.8 %collective-permute-start.14 = (bf16[2,1,256,192]{2,3,1,0:T(8,128)(2,1)}, bf16[2,1,256,192]{2,3,1,0:T(8,128)(2,1)}, u32[]{:S(2)}, u32[]{:S(2)}) collective-permute-start(bf16[2,1,256,192]{2,3,1,0:T(8,128)(2,1)} %get-tuple-element.93), channel_id=1, source_target_pairs={{0,1},{1,2},{2,3},{3,4},{4,5},{5,6},{6,7},{7,8},{8,9},{9,10},{10,1... | collective-permute-start | bytes 589832 | tf_op jit(solution)/shard_map/ppermute | solution.py:15
  11.5 1.0 fusion.162
  12.5 5.8 %fusion.224 = (bf16[1,1,3,384,384]{4,3,2,1,0:T(8,128)(2,1)}, bf16[1,1,3,384,384]{4,3,2,1,0:T(8,128)(2,1)}, bf16[1,1,3,384,384]{4,3,2,1,0:T(8,128)(2,1)}, bf16[1,...) fusion(bf16[3,3,3,384,384]{4,3,2,1,0:T(8,128)(2,1)} %param.17), kind=kLoop, calls=%fused_computation.352 | loop fusion | bytes 15925248 | tf_op jit(solution)/shard_map/slice | solution.py:53
  19.1 1.1 fusion.226
  20.5 1.1 reshape.240
  21.6 1.4 %copy.72 = bf16[1,3,384,192]{2,1,3,0:T(4,128)(2,1)S(1)} copy(bf16[1,3,384,192]{2,3,1,0:T(8,128)(2,1)} %get-tuple-element.26) | data formatting | bytes 884736 | tf_op jit(solution)/shard_map/slice | solution.py:53
  23.0 1.1 reshape.239
  24.2 1.4 %copy.76 = bf16[1,3,384,192]{2,1,3,0:T(4,128)(2,1)S(1)} copy(bf16[1,3,384,192]{2,3,1,0:T(8,128)(2,1)} %get-tuple-element.25) | data formatting | bytes 884736 | tf_op jit(solution)/shard_map/slice | solution.py:53
  25.6 1.1 reshape.241
  26.7 1.3 %fusion.225 = (bf16[1,1,3,192,192]{4,3,2,1,0:T(8,128)(2,1)}, bf16[1,1,3,192,192]{4,3,2,1,0:T(8,128)(2,1)}, bf16[1,1,3,192,192]{4,3,2,1,0:T(8,128)(2,1)}, bf16[1,...) fusion(bf16[3,3,3,192,192]{4,3,2,1,0:T(8,128)(2,1)S(1)} %copy-d, ...), kind=kLoop, calls=%fused_computation.353 | loop fusion | bytes 3981312 | tf_op jit(solution)/shard_map/slice | solution.py:53
  28.1 1.0 convolution_convert_fusion.2
  29.5 1.0 constant_dynamic-update-slice_fusion.21
  30.4 1.9 %collective-permute-start.5 = (bf16[2,1,128,384]{3,2,1,0:T(8,128)(2,1)S(1)}, bf16[2,1,128,384]{3,2,1,0:T(8,128)(2,1)S(1)}, u32[]{:S(2)}, u32[]{:S(2)}) collective-permute-start(bf16[2,1,128,384]{3,2,1,0:T(8,128)(2,1)S(1)} %copy-done.3), channel_id=1, source_target_pairs={{0,12},{1,13},{2,14},{3,15},{4,0},{5,1},{6,2},{7,3},{8,4},{9,5},{1... | collective-permute-start | bytes 589832 | tf_op jit(solution)/shard_map/ppermute | solution.py:28
  32.4 1.0 constant_dynamic-update-slice_fusion.6
  33.4 3.4 %collective-permute-start.8 = (bf16[2,1,128,384]{3,2,0,1:T(8,128)(2,1)S(1)}, bf16[2,1,128,384]{3,2,0,1:T(8,128)(2,1)S(1)}, u32[]{:S(2)}, u32[]{:S(2)}) collective-permute-start(bf16[2,1,128,384]{3,2,0,1:T(8,128)(2,1)S(1)} %bitcast.247), channel_id=1, source_target_pairs={{0,1},{1,2},{2,3},{3,4},{4,5},{5,6},{6,7},{7,8},{8,9},{9,10},{10,1... | collective-permute-start | bytes 589832 | tf_op jit(solution)/shard_map/ppermute | solution.py:15
  36.8 1.0 constant_dynamic-update-slice_fusion.5
  37.8 1.9 %collective-permute-start.9 = (bf16[2,1,128,384]{3,2,0,1:T(8,128)(2,1)S(1)}, bf16[2,1,128,384]{3,2,0,1:T(8,128)(2,1)S(1)}, u32[]{:S(2)}, u32[]{:S(2)}) collective-permute-start(bf16[2,1,128,384]{3,2,0,1:T(8,128)(2,1)S(1)} %bitcast.248), channel_id=1, source_target_pairs={{1,0},{2,1},{3,2},{4,3},{5,4},{6,5},{7,6},{8,7},{9,8},{10,9},{11,1... | collective-permute-start | bytes 589832 | tf_op jit(solution)/shard_map/ppermute | solution.py:16
  39.7 1.0 constant_dynamic-update-slice_fusion.4
  40.8 1.0 constant_dynamic-update-slice_fusion.3
  41.9 4.5 %collective-permute-start.15 = (bf16[2,1,256,192]{2,3,1,0:T(8,128)(2,1)S(1)}, bf16[2,1,256,192]{2,3,1,0:T(8,128)(2,1)S(1)}, u32[]{:S(2)}, u32[]{:S(2)}) collective-permute-start(bf16[2,1,256,192]{2,3,1,0:T(8,128)(2,1)S(1)} %copy-done.46), channel_id=1, source_target_pairs={{1,0},{2,1},{3,2},{4,3},{5,4},{6,5},{7,6},{8,7},{9,8},{10,9},{11,1... | collective-permute-start | bytes 589832 | tf_op jit(solution)/shard_map/ppermute | solution.py:16
  46.4 3.3 %collective-permute-done.9 = bf16[2,1,128,384]{3,2,0,1:T(8,128)(2,1)S(1)} collective-permute-done((bf16[2,1,128,384]{3,2,0,1:T(8,128)(2,1)S(1)}, bf16[2,1,128,384]{3,2,0,1:T(8,128)(2,1)S(1)}, u32[]{:S(2)}, u32[]{:S(2)}) %collective-permute-start.9) | collective-permute-done | bytes 196640 | tf_op jit(solution)/shard_map/ppermute | solution.py:16
  49.9 1.0 pad_slice_fusion.35
  51.1 2.8 %collective-permute-done.15 = bf16[2,1,256,192]{2,3,1,0:T(8,128)(2,1)S(1)} collective-permute-done((bf16[2,1,256,192]{2,3,1,0:T(8,128)(2,1)S(1)}, bf16[2,1,256,192]{2,3,1,0:T(8,128)(2,1)S(1)}, u32[]{:S(2)}, u32[]{:S(2)}) %collective-permute-start.15) | collective-permute-done | bytes 196640 | tf_op jit(solution)/shard_map/ppermute | solution.py:16
  54.0 1.7 %pad_slice_fusion.7 = (bf16[2,2,256,192]{2,3,1,0:T(8,128)(2,1)}, bf16[2,2,256,192]{2,3,1,0:T(8,128)(2,1)S(1)}, bf16[2,2,256,192]{2,3,1,0:T(8,128)(2,1)S(1)}, bf1...) fusion(bf16[2,4,256,192]{2,3,1,0:T(8,128)(2,1)S(1)} %get-tuple-element.125), kind=kLoop, calls=%fused_computation.46 | loop fusion | bytes 3145728 | tf_op jit(solution)/shard_map/slice | solution.py:51
  55.9 1.4 %pad_slice_fusion.23 = (bf16[1,2,256,192]{2,3,1,0:T(8,128)(2,1)}, bf16[1,2,256,192]{2,3,1,0:T(8,128)(2,1)}, bf16[1,2,256,192]{2,3,1,0:T(8,128)(2,1)}, bf16[1,2,2...) fusion(bf16[1,4,256,192]{2,3,1,0:T(8,128)(2,1)S(1)} %slice.689), kind=kLoop, calls=%fused_computation.147 | loop fusion | bytes 1572864 | tf_op jit(solution)/shard_map/slice | solution.py:51
  60.6 1.0 convolution_add_fusion.15
  62.1 1.3 %convolution_add_fusion.7 = f32[2,128,384]{2,1,0:T(8,128)} fusion(f32[2,128,384]{2,1,0:T(8,128)S(1)} %fusion.108, bf16[1152,384,1]{1,0,2:T(8,128)(2,1)S(1)} %bitcast.244, bf16[2,1,128,384]{3,2,0,1:T(8,128)(2,1)S(1)} %get-tuple-element.66, bf16[2,1,128,384]{3,2,0,1:T(8,128)(2,1)S(1)} %copy-done.26, bf16[2,1,128,384]{3,2,0,1:T(8,128)(2,1)S(1)} %get-tuple-element.70), kind=kOutput, calls=%fused_computation.74 | convolution fusion | flops 228360192 | bytes 2260992 | tf_op jit(solution)/shard_map/fhwc,cd->fhwd/dot_general | solution.py:54
  63.4 1.4 %convolution_add_fusion.3 = f32[2,2,256,192]{2,3,1,0:T(8,128)} fusion(f32[2,2,256,192]{2,3,1,0:T(8,128)S(1)} %fusion.60, bf16[576,192,1,1]{1,0,3,2:T(8,128)(2,1)S(1)} %bitcast.261, bf16[2,2,256,192]{2,3,1,0:T(8,128)(2,1)S(1)} %get-tuple-element.55, bf16[2,2,256,192]{2,3,1,0:T(8,128)(2,1)S(1)} %slice.687, bf16[2,2,256,192]{2,3,1,0:T(8,128)(2,1)S(1)} %get-tuple-element.59), kind=kOutput, calls=%fused_computation.65 | convolution fusion | flops 230227968 | bytes 2973696 | tf_op jit(solution)/shard_map/fhwc,cd->fhwd/dot_general | solution.py:54
  66.6 5.2 %fusion.233 = (f32[2,128]{1,0:T(2,128)S(1)}, f32[2,128,2048]{2,1,0:T(8,128)}) fusion(bf16[2,128,384]{2,1,0:T(8,128)(2,1)} %convolution_convert_fusion.2, bf16[2,2048,384]{2,1,0:T(8,128)(2,1)S(1)} %fusion, bf16[384,384]{1,0:T(8,128)(2,1)S(1)} %copy-done), kind=kOutput, calls=%fused_computation.361 | convolution fusion | flops 1613233920 | bytes 5735424 | tf_op jit(solution)/shard_map/fqc,fkc->fqk/dot_general | solution.py:119
  71.8 2.0 %fusion.19 = f32[2,128]{1,0:T(2,128)S(1)} fusion(f32[2,128,2048]{2,1,0:T(8,128)} %get-tuple-element.129, f32[2,128]{1,0:T(2,128)S(1)} %get-tuple-element.128), kind=kLoop, calls=%fused_computation.34 | loop fusion | flops 1048320 | bytes 2099200 | tf_op jit(solution)/shard_map/reduce_sum | solution.py:124
  73.8 4.9 %fusion.91 = bf16[2,128,384]{2,1,0:T(8,128)(2,1)} fusion(bf16[2,2048,384]{2,1,0:T(8,128)(2,1)S(1)} %fusion, f32[2,128,2048]{2,1,0:T(8,128)} %get-tuple-element.129, f32[2,128]{1,0:T(2,128)S(1)} %get-tuple-element.128, bf16[384,384]{1,0:T(8,128)(2,1)} %param.15, f32[2,128]{1,0:T(2,128)S(1)} %fusion.19), kind=kOutput, calls=%fused_computation.123 | convolution fusion | flops 1613430784 | bytes 5736448 | tf_op jit(solution)/shard_map/fqk,fkc->fqc/dot_general | solution.py:125
  78.8 1.5 %multiply_reduce_fusion.2 = (f32[2,128]{1,0:T(2,128)S(1)}, f32[2,1,128,384]{3,2,0,1:T(8,128)S(1)}) fusion(bf16[2,128,384]{2,1,0:T(8,128)(2,1)} %fusion.91, bf16[384,384]{1,0:T(8,128)(2,1)} %param.16, bf16[2,1,128,384]{3,2,1,0:T(8,128)(2,1)S(1)} %copy-done.4), kind=kOutput, calls=%fused_computation.234 | convolution fusion | flops 76087040 | bytes 1082368 | tf_op jit(solution)/shard_map/ftc,cd->ftd/dot_general | solution.py:132
  80.5 1.9 %collective-permute-start.10 = (bf16[2,1,128,384]{3,2,0,1:T(8,128)(2,1)S(1)}, bf16[2,1,128,384]{3,2,0,1:T(8,128)(2,1)S(1)}, u32[]{:S(2)}, u32[]{:S(2)}) collective-permute-start(bf16[2,1,128,384]{3,2,0,1:T(8,128)(2,1)S(1)} %multiply_convert_fusion.1), channel_id=1, source_target_pairs={{0,1},{1,2},{2,3},{3,4},{4,5},{5,6},{6,7},{7,8},{8,9},{9,10},{10,1... | collective-permute-start | bytes 589832 | tf_op jit(solution)/shard_map/ppermute | solution.py:15
  82.4 2.6 %collective-permute-start.11 = (bf16[2,1,128,384]{3,2,0,1:T(8,128)(2,1)S(1)}, bf16[2,1,128,384]{3,2,0,1:T(8,128)(2,1)S(1)}, u32[]{:S(2)}, u32[]{:S(2)}) collective-permute-start(bf16[2,1,128,384]{3,2,0,1:T(8,128)(2,1)S(1)} %multiply_convert_fusion.1), channel_id=1, source_target_pairs={{1,0},{2,1},{3,2},{4,3},{5,4},{6,5},{7,6},{8,7},{9,8},{10,9},{11,1... | collective-permute-start | bytes 589832 | tf_op jit(solution)/shard_map/ppermute | solution.py:16
  85.1 1.6 %fusion.130 = f32[2,256,192]{1,2,0:T(8,128)S(1)} fusion(bf16[576,192,1]{1,0,2:T(8,128)(2,1)} %bitcast.259, bf16[1,2,256,192]{2,3,1,0:T(8,128)(2,1)} %get-tuple-element.84, bf16[1,2,256,192]{2,3,1,0:T(8,128)(2,1)} %slice.690, bf16[1,2,256,192]{2,3,1,0:T(8,128)(2,1)} %get-tuple-element.88), kind=kOutput, calls=%fused_computation.194 | convolution fusion | flops 115015680 | bytes 1204224 | tf_op jit(solution)/shard_map/fhwc,cd->fhwd/dot_general | solution.py:54
  87.1 3.2 %collective-permute-done.11 = bf16[2,1,128,384]{3,2,0,1:T(8,128)(2,1)S(1)} collective-permute-done((bf16[2,1,128,384]{3,2,0,1:T(8,128)(2,1)S(1)}, bf16[2,1,128,384]{3,2,0,1:T(8,128)(2,1)S(1)}, u32[]{:S(2)}, u32[]{:S(2)}) %collective-permute-start.11) | collective-permute-done | bytes 196640 | tf_op jit(solution)/shard_map/ppermute | solution.py:16
  95.2 2.1 %collective-permute-start.12 = (bf16[2,1,128,384]{3,2,0,1:T(8,128)(2,1)S(1)}, bf16[2,1,128,384]{3,2,0,1:T(8,128)(2,1)S(1)}, u32[]{:S(2)}, u32[]{:S(2)}) collective-permute-start(bf16[2,1,128,384]{3,2,0,1:T(8,128)(2,1)S(1)} %fusion.89), channel_id=1, source_target_pairs={{0,1},{1,2},{2,3},{3,4},{4,5},{5,6},{6,7},{7,8},{8,9},{9,10},{10,1... | collective-permute-start | bytes 589832 | tf_op jit(solution)/shard_map/ppermute | solution.py:15
  97.3 2.4 %collective-permute-start.13 = (bf16[2,1,128,384]{3,2,0,1:T(8,128)(2,1)S(1)}, bf16[2,1,128,384]{3,2,0,1:T(8,128)(2,1)S(1)}, u32[]{:S(2)}, u32[]{:S(2)}) collective-permute-start(bf16[2,1,128,384]{3,2,0,1:T(8,128)(2,1)S(1)} %fusion.89), channel_id=1, source_target_pairs={{1,0},{2,1},{3,2},{4,3},{5,4},{6,5},{7,6},{8,7},{9,8},{10,9},{11,1... | collective-permute-start | bytes 589832 | tf_op jit(solution)/shard_map/ppermute | solution.py:16
  100.6 4.6 %collective-permute-done.13 = bf16[2,1,128,384]{3,2,0,1:T(8,128)(2,1)S(1)} collective-permute-done((bf16[2,1,128,384]{3,2,0,1:T(8,128)(2,1)S(1)}, bf16[2,1,128,384]{3,2,0,1:T(8,128)(2,1)S(1)}, u32[]{:S(2)}, u32[]{:S(2)}) %collective-permute-start.13) | collective-permute-done | bytes 196640 | tf_op jit(solution)/shard_map/ppermute | solution.py:16
  109.0 1.0 fusion.227
  114.9 0.9 fusion.37
  116.1 1.0 copy.81
  124.3 1.3 %fusion.45 = bf16[2,2,256,192]{2,3,1,0:T(8,128)(2,1)} fusion(f32[2,2,256,192]{2,3,1,0:T(8,128)S(1)} %fusion.43, f32[2,2,256,192]{2,3,1,0:T(8,128)S(1)} %convolution_add_fusion.1, bf16[576,192,1,1]{1,0,3,2:T(8,128)(2,1)S(1)} %bitcast.251, bf16[2,2,256,192]{2,3,1,0:T(8,128)(2,1)S(1)} %get-tuple-element.43, ...), kind=kOutput, calls=%fused_computation.67 | convolution fusion | flops 230817792 | bytes 3760128 | tf_op jit(solution)/shard_map/fhwc,cd->fhwd/dot_general | solution.py:54
  (200 shorter events, 29.5 us)
Async XLA Ops:
  0.0 66.6 %copy-start = (bf16[384,384]{1,0:T(8,128)(2,1)S(1)}, bf16[384,384]{1,0:T(8,128)(2,1)}, u32[]{:S(2)}) copy-start(bf16[384,384]{1,0:T(8,128)(2,1)} %param.14) | copy-start | bytes 884740
  0.0 30.4 %collective-permute-start = (bf16[2,1,128,384]{3,2,1,0:T(8,128)(2,1)}, bf16[2,1,128,384]{3,2,1,0:T(8,128)(2,1)}, u32[]{:S(2)}, u32[]{:S(2)}) collective-permute-start(bf16[2,1,128,384]{3,2,1,0:T(8,128)(2,1)} %param.10), channel_id=1, source_target_pairs={{0,2},{1,3},{2,4},{3,5},{4,6},{5,7},{6,8},{7,9},{8,10},{9,11},{10,... | collective-permute-start | bytes 589832 | tf_op jit(solution)/shard_map/ppermute | solution.py:28
  1.2 32.1 %collective-permute-start.1 = (bf16[2,1,128,384]{3,2,1,0:T(8,128)(2,1)}, bf16[2,1,128,384]{3,2,1,0:T(8,128)(2,1)}, u32[]{:S(2)}, u32[]{:S(2)}) collective-permute-start(bf16[2,1,128,384]{3,2,1,0:T(8,128)(2,1)} %param.10), channel_id=1, source_target_pairs={{0,4},{1,5},{2,6},{3,7},{4,8},{5,9},{6,10},{7,11},{8,12},{9,13},{1... | collective-permute-start | bytes 589832 | tf_op jit(solution)/shard_map/ppermute | solution.py:28
  2.5 35.3 %collective-permute-start.2 = (bf16[2,1,128,384]{3,2,1,0:T(8,128)(2,1)}, bf16[2,1,128,384]{3,2,1,0:T(8,128)(2,1)}, u32[]{:S(2)}, u32[]{:S(2)}) collective-permute-start(bf16[2,1,128,384]{3,2,1,0:T(8,128)(2,1)} %param.10), channel_id=1, source_target_pairs={{0,6},{1,7},{2,8},{3,9},{4,10},{5,11},{6,12},{7,13},{8,14},{9,15},... | collective-permute-start | bytes 589832 | tf_op jit(solution)/shard_map/ppermute | solution.py:28
  3.5 37.2 %collective-permute-start.3 = (bf16[2,1,128,384]{3,2,1,0:T(8,128)(2,1)}, bf16[2,1,128,384]{3,2,1,0:T(8,128)(2,1)}, u32[]{:S(2)}, u32[]{:S(2)}) collective-permute-start(bf16[2,1,128,384]{3,2,1,0:T(8,128)(2,1)} %param.10), channel_id=1, source_target_pairs={{0,8},{1,9},{2,10},{3,11},{4,12},{5,13},{6,14},{7,15},{8,0},{9,1},... | collective-permute-start | bytes 589832 | tf_op jit(solution)/shard_map/ppermute | solution.py:28
  6.6 22.8 %collective-permute-start.14 = (bf16[2,1,256,192]{2,3,1,0:T(8,128)(2,1)}, bf16[2,1,256,192]{2,3,1,0:T(8,128)(2,1)}, u32[]{:S(2)}, u32[]{:S(2)}) collective-permute-start(bf16[2,1,256,192]{2,3,1,0:T(8,128)(2,1)} %get-tuple-element.93), channel_id=1, source_target_pairs={{0,1},{1,2},{2,3},{3,4},{4,5},{5,6},{6,7},{7,8},{8,9},{9,10},{10,1... | collective-permute-start | bytes 589832 | tf_op jit(solution)/shard_map/ppermute | solution.py:15
  12.5 5.9 %copy-start.21 = (bf16[2,1,128,384]{3,2,1,0:T(8,128)(2,1)S(1)}, bf16[2,1,128,384]{3,2,1,0:T(8,128)(2,1)}, u32[]{:S(2)}) copy-start(bf16[2,1,128,384]{3,2,1,0:T(8,128)(2,1)} %param.11) | copy-start | bytes 589828
  12.5 6.5 %copy-start.9 = (bf16[3,3,384,192]{2,3,1,0:T(8,128)(2,1)S(1)}, bf16[3,3,384,192]{2,3,1,0:T(8,128)(2,1)}, u32[]{:S(2)}) copy-start(bf16[3,3,384,192]{2,3,1,0:T(8,128)(2,1)} %param.18) | copy-start | bytes 3981316
  20.5 6.2 %copy-start.5 = (bf16[3,3,3,192,192]{4,3,2,1,0:T(8,128)(2,1)S(1)}, bf16[3,3,3,192,192]{4,3,2,1,0:T(8,128)(2,1)}, u32[]{:S(2)}) copy-start(bf16[3,3,3,192,192]{4,3,2,1,0:T(8,128)(2,1)} %param.19) | copy-start | bytes 5971972
  28.1 5.2 %copy-start.22 = (bf16[2,1,128,384]{3,2,1,0:T(8,128)(2,1)S(1)}, bf16[2,1,128,384]{3,2,1,0:T(8,128)(2,1)}, u32[]{:S(2)}) copy-start(bf16[2,1,128,384]{3,2,1,0:T(8,128)(2,1)} %param.11) | copy-start | bytes 589828
  28.1 13.8 %copy-start.46 = (bf16[2,1,256,192]{2,3,1,0:T(8,128)(2,1)S(1)}, bf16[2,1,256,192]{2,3,1,0:T(8,128)(2,1)}, u32[]{:S(2)}) copy-start(bf16[2,1,256,192]{2,3,1,0:T(8,128)(2,1)} %get-tuple-element.92) | copy-start | bytes 589828
  29.5 20.4 %collective-permute-start.4 = (bf16[2,1,128,384]{3,2,1,0:T(8,128)(2,1)S(1)}, bf16[2,1,128,384]{3,2,1,0:T(8,128)(2,1)S(1)}, u32[]{:S(2)}, u32[]{:S(2)}) collective-permute-start(bf16[2,1,128,384]{3,2,1,0:T(8,128)(2,1)S(1)} %copy-done.3), channel_id=1, source_target_pairs={{0,10},{1,11},{2,12},{3,13},{4,14},{5,15},{6,0},{7,1},{8,2},{9,3},... | collective-permute-start | bytes 589832 | tf_op jit(solution)/shard_map/ppermute | solution.py:28
  30.4 20.5 %collective-permute-start.5 = (bf16[2,1,128,384]{3,2,1,0:T(8,128)(2,1)S(1)}, bf16[2,1,128,384]{3,2,1,0:T(8,128)(2,1)S(1)}, u32[]{:S(2)}, u32[]{:S(2)}) collective-permute-start(bf16[2,1,128,384]{3,2,1,0:T(8,128)(2,1)S(1)} %copy-done.3), channel_id=1, source_target_pairs={{0,12},{1,13},{2,14},{3,15},{4,0},{5,1},{6,2},{7,3},{8,4},{9,5},{1... | collective-permute-start | bytes 589832 | tf_op jit(solution)/shard_map/ppermute | solution.py:28
  33.4 8.5 %collective-permute-start.8 = (bf16[2,1,128,384]{3,2,0,1:T(8,128)(2,1)S(1)}, bf16[2,1,128,384]{3,2,0,1:T(8,128)(2,1)S(1)}, u32[]{:S(2)}, u32[]{:S(2)}) collective-permute-start(bf16[2,1,128,384]{3,2,0,1:T(8,128)(2,1)S(1)} %bitcast.247), channel_id=1, source_target_pairs={{0,1},{1,2},{2,3},{3,4},{4,5},{5,6},{6,7},{7,8},{8,9},{9,10},{10,1... | collective-permute-start | bytes 589832 | tf_op jit(solution)/shard_map/ppermute | solution.py:15
  37.8 11.9 %collective-permute-start.9 = (bf16[2,1,128,384]{3,2,0,1:T(8,128)(2,1)S(1)}, bf16[2,1,128,384]{3,2,0,1:T(8,128)(2,1)S(1)}, u32[]{:S(2)}, u32[]{:S(2)}) collective-permute-start(bf16[2,1,128,384]{3,2,0,1:T(8,128)(2,1)S(1)} %bitcast.248), channel_id=1, source_target_pairs={{1,0},{2,1},{3,2},{4,3},{5,4},{6,5},{7,6},{8,7},{9,8},{10,9},{11,1... | collective-permute-start | bytes 589832 | tf_op jit(solution)/shard_map/ppermute | solution.py:16
  40.7 15.0 %collective-permute-start.6 = (bf16[2,1,128,384]{3,2,1,0:T(8,128)(2,1)S(1)}, bf16[2,1,128,384]{3,2,1,0:T(8,128)(2,1)S(1)}, u32[]{:S(2)}, u32[]{:S(2)}) collective-permute-start(bf16[2,1,128,384]{3,2,1,0:T(8,128)(2,1)S(1)} %copy-done.3), channel_id=1, source_target_pairs={{0,14},{1,15},{2,0},{3,1},{4,2},{5,3},{6,4},{7,5},{8,6},{9,7},{10,... | collective-permute-start | bytes 589832 | tf_op jit(solution)/shard_map/ppermute | solution.py:28
  40.8 10.2 %copy-start.6 = (bf16[2,2,256,192]{2,3,1,0:T(8,128)(2,1)S(1)}, bf16[2,2,256,192]{2,3,1,0:T(8,128)(2,1)}, u32[]{:S(2)}) copy-start(bf16[2,2,256,192]{2,3,1,0:T(8,128)(2,1)} %param.12) | copy-start | bytes 1179652
  41.9 17.0 %copy-start.25 = (bf16[2,1,128,384]{3,2,0,1:T(8,128)(2,1)}, bf16[2,1,128,384]{3,2,0,1:T(8,128)(2,1)S(1)}, u32[]{:S(2)}) copy-start(bf16[2,1,128,384]{3,2,0,1:T(8,128)(2,1)S(1)} %collective-permute-done.8) | copy-start | bytes 589828
  41.9 12.0 %collective-permute-start.15 = (bf16[2,1,256,192]{2,3,1,0:T(8,128)(2,1)S(1)}, bf16[2,1,256,192]{2,3,1,0:T(8,128)(2,1)S(1)}, u32[]{:S(2)}, u32[]{:S(2)}) collective-permute-start(bf16[2,1,256,192]{2,3,1,0:T(8,128)(2,1)S(1)} %copy-done.46), channel_id=1, source_target_pairs={{1,0},{2,1},{3,2},{4,3},{5,4},{6,5},{7,6},{8,7},{9,8},{10,9},{11,1... | collective-permute-start | bytes 589832 | tf_op jit(solution)/shard_map/ppermute | solution.py:16
  49.8 4.2 %copy-start.2 = (bf16[2,3,128,384]{3,2,0,1:T(8,128)(2,1)}, bf16[2,3,128,384]{3,2,0,1:T(8,128)(2,1)S(1)}, u32[]{:S(2)}) copy-start(bf16[2,3,128,384]{3,2,0,1:T(8,128)(2,1)S(1)} %pad_maximum_fusion.9) | copy-start | bytes 1769476
  54.0 1.8 %copy-start.7 = (bf16[2,3,256,192]{2,3,1,0:T(8,128)(2,1)}, bf16[2,3,256,192]{2,3,1,0:T(8,128)(2,1)S(1)}, u32[]{:S(2)}) copy-start(bf16[2,3,256,192]{2,3,1,0:T(8,128)(2,1)S(1)} %get-tuple-element.124) | copy-start | bytes 1769476
  54.0 3.3 %slice-start = ((bf16[2,3,128,384]{3,2,0,1:T(8,128)(2,1)}), bf16[1,3,128,384]{3,2,0,1:T(8,128)(2,1)S(1)}, s32[]{:S(2)}) async-start(bf16[2,3,128,384]{3,2,0,1:T(8,128)(2,1)} %copy-done.2), calls=%async_computation | async-start | bytes 589824 | tf_op jit(solution)/shard_map/slice | solution.py:62
  55.8 9.0 %collective-permute-start.7 = (bf16[2,8,128,384]{3,2,1,0:T(8,128)(2,1)S(1)}, bf16[2,8,128,384]{3,2,1,0:T(8,128)(2,1)S(1)}, u32[]{:S(2)}, u32[]{:S(2)}) collective-permute-start(bf16[2,8,128,384]{3,2,1,0:T(8,128)(2,1)S(1)} %get-tuple-element.108), channel_id=1, source_target_pairs={{0,1},{1,0},{2,3},{3,2},{4,5},{5,4},{6,7},{7,6},{8,9},{9,8},{10,11... | collective-permute-start | bytes 4718600 | tf_op jit(solution)/shard_map/ppermute | solution.py:31
  58.8 1.7 %copy-start.14 = (bf16[1,1,3,384,384]{4,3,2,1,0:T(8,128)(2,1)S(1)}, bf16[1,1,3,384,384]{4,3,2,1,0:T(8,128)(2,1)}, u32[]{:S(2)}) copy-start(bf16[1,1,3,384,384]{4,3,2,1,0:T(8,128)(2,1)} %get-tuple-element.10) | copy-start | bytes 2654212
  58.9 1.7 %copy-start.48 = (bf16[1,1,128,384]{3,2,0,1:T(8,128)(2,1)S(1)}, bf16[1,1,128,384]{3,2,0,1:T(8,128)(2,1)}, u32[]{:S(2)}) copy-start(bf16[1,1,128,384]{3,2,0,1:T(8,128)(2,1)} %slice.665) | copy-start | bytes 294916
  59.4 2.2 %copy-start.20 = (bf16[1,1,3,384,384]{4,3,2,1,0:T(8,128)(2,1)S(1)}, bf16[1,1,3,384,384]{4,3,2,1,0:T(8,128)(2,1)}, u32[]{:S(2)}) copy-start(bf16[1,1,3,384,384]{4,3,2,1,0:T(8,128)(2,1)} %get-tuple-element.12) | copy-start | bytes 2654212
  60.6 1.5 %copy-start.19 = (bf16[1,1,3,384,384]{4,3,2,1,0:T(8,128)(2,1)S(1)}, bf16[1,1,3,384,384]{4,3,2,1,0:T(8,128)(2,1)}, u32[]{:S(2)}) copy-start(bf16[1,1,3,384,384]{4,3,2,1,0:T(8,128)(2,1)} %get-tuple-element.13) | copy-start | bytes 2654212
  60.6 1.5 %copy-start.26 = (bf16[2,1,128,384]{3,2,0,1:T(8,128)(2,1)S(1)}, bf16[2,1,128,384]{3,2,0,1:T(8,128)(2,1)}, u32[]{:S(2)}) copy-start(bf16[2,1,128,384]{3,2,0,1:T(8,128)(2,1)} %copy-done.25) | copy-start | bytes 589828
  73.8 5.0 %copy-start.4 = (bf16[2,1,128,384]{3,2,1,0:T(8,128)(2,1)S(1)}, bf16[2,1,128,384]{3,2,1,0:T(8,128)(2,1)}, u32[]{:S(2)}) copy-start(bf16[2,1,128,384]{3,2,1,0:T(8,128)(2,1)} %param.10) | copy-start | bytes 589828
  78.7 8.0 %copy-start.13 = (bf16[1,1,3,384,384]{4,3,2,1,0:T(8,128)(2,1)S(1)}, bf16[1,1,3,384,384]{4,3,2,1,0:T(8,128)(2,1)}, u32[]{:S(2)}) copy-start(bf16[1,1,3,384,384]{4,3,2,1,0:T(8,128)(2,1)} %get-tuple-element.9) | copy-start | bytes 2654212
  78.7 8.0 %slice-start.2 = ((bf16[2,1,128,384]{3,2,0,1:T(8,128)(2,1)}), bf16[1,1,128,384]{3,2,0,1:T(8,128)(2,1)S(1)}, s32[]{:S(2)}) async-start(bf16[2,1,128,384]{3,2,0,1:T(8,128)(2,1)} %copy-done.23), calls=%async_computation.2 | async-start | bytes 196608 | tf_op jit(solution)/shard_map/slice | solution.py:51
  78.7 8.0 %copy-start.47 = (bf16[1,1,128,384]{3,2,0,1:T(8,128)(2,1)S(1)}, bf16[1,1,128,384]{3,2,0,1:T(8,128)(2,1)}, u32[]{:S(2)}) copy-start(bf16[1,1,128,384]{3,2,0,1:T(8,128)(2,1)} %get-tuple-element.98) | copy-start | bytes 294916
  78.7 8.0 %copy-start.49 = (f32[128,384]{1,0:T(8,128)S(1)}, f32[128,384]{1,0:T(8,128)}, u32[]{:S(2)}) copy-start(f32[128,384]{1,0:T(8,128)} %convolution_add_fusion.15) | copy-start | bytes 589828
  80.5 6.6 %collective-permute-start.10 = (bf16[2,1,128,384]{3,2,0,1:T(8,128)(2,1)S(1)}, bf16[2,1,128,384]{3,2,0,1:T(8,128)(2,1)S(1)}, u32[]{:S(2)}, u32[]{:S(2)}) collective-permute-start(bf16[2,1,128,384]{3,2,0,1:T(8,128)(2,1)S(1)} %multiply_convert_fusion.1), channel_id=1, source_target_pairs={{0,1},{1,2},{2,3},{3,4},{4,5},{5,6},{6,7},{7,8},{8,9},{9,10},{10,1... | collective-permute-start | bytes 589832 | tf_op jit(solution)/shard_map/ppermute | solution.py:15
  82.4 7.9 %collective-permute-start.11 = (bf16[2,1,128,384]{3,2,0,1:T(8,128)(2,1)S(1)}, bf16[2,1,128,384]{3,2,0,1:T(8,128)(2,1)S(1)}, u32[]{:S(2)}, u32[]{:S(2)}) collective-permute-start(bf16[2,1,128,384]{3,2,0,1:T(8,128)(2,1)S(1)} %multiply_convert_fusion.1), channel_id=1, source_target_pairs={{1,0},{2,1},{3,2},{4,3},{5,4},{6,5},{7,6},{8,7},{9,8},{10,9},{11,1... | collective-permute-start | bytes 589832 | tf_op jit(solution)/shard_map/ppermute | solution.py:16
  87.1 3.8 %copy-start.18 = (bf16[1,1,3,384,384]{4,3,2,1,0:T(8,128)(2,1)S(1)}, bf16[1,1,3,384,384]{4,3,2,1,0:T(8,128)(2,1)}, u32[]{:S(2)}) copy-start(bf16[1,1,3,384,384]{4,3,2,1,0:T(8,128)(2,1)} %get-tuple-element.11) | copy-start | bytes 2654212
  93.2 1.5 %copy-start.50 = (f32[2,128,384]{2,1,0:T(8,128)S(1)}, f32[2,128,384]{2,1,0:T(8,128)}, u32[]{:S(2)}) copy-start(f32[2,128,384]{2,1,0:T(8,128)} %convolution_add_fusion.7) | copy-start | bytes 1179652
  93.7 6.0 %slice-start.1 = ((bf16[2,2,256,192]{2,3,1,0:T(8,128)(2,1)}), bf16[1,2,256,192]{2,3,1,0:T(8,128)(2,1)S(1)}, s32[]{:S(2)}) async-start(bf16[2,2,256,192]{2,3,1,0:T(8,128)(2,1)} %param.12), calls=%async_computation.1 | async-start | bytes 393216 | tf_op jit(solution)/shard_map/slice | solution.py:51
  93.7 6.0 %copy-start.38 = (bf16[1,1,3,192,192]{4,3,2,1,0:T(8,128)(2,1)S(1)}, bf16[1,1,3,192,192]{4,3,2,1,0:T(8,128)(2,1)}, u32[]{:S(2)}) copy-start(bf16[1,1,3,192,192]{4,3,2,1,0:T(8,128)(2,1)} %get-tuple-element.19) | copy-start | bytes 663556
  93.8 6.0 %copy-start.44 = (bf16[1,2,256,192]{2,3,1,0:T(8,128)(2,1)S(1)}, bf16[1,2,256,192]{2,3,1,0:T(8,128)(2,1)}, u32[]{:S(2)}) copy-start(bf16[1,2,256,192]{2,3,1,0:T(8,128)(2,1)} %get-tuple-element.85) | copy-start | bytes 589828
  93.8 6.0 %copy-start.45 = (bf16[1,2,256,192]{2,3,1,0:T(8,128)(2,1)S(1)}, bf16[1,2,256,192]{2,3,1,0:T(8,128)(2,1)}, u32[]{:S(2)}) copy-start(bf16[1,2,256,192]{2,3,1,0:T(8,128)(2,1)} %get-tuple-element.86) | copy-start | bytes 589828
  94.7 5.4 %copy-start.8 = (bf16[2,3,256,192]{2,3,1,0:T(8,128)(2,1)S(1)}, bf16[2,3,256,192]{2,3,1,0:T(8,128)(2,1)}, u32[]{:S(2)}) copy-start(bf16[2,3,256,192]{2,3,1,0:T(8,128)(2,1)} %copy-done.7) | copy-start | bytes 1769476
  95.2 5.0 %copy-start.37 = (bf16[1,1,3,192,192]{4,3,2,1,0:T(8,128)(2,1)S(1)}, bf16[1,1,3,192,192]{4,3,2,1,0:T(8,128)(2,1)}, u32[]{:S(2)}) copy-start(bf16[1,1,3,192,192]{4,3,2,1,0:T(8,128)(2,1)} %get-tuple-element.18) | copy-start | bytes 663556
  95.2 5.0 %copy-start.42 = (bf16[1,2,256,192]{2,3,1,0:T(8,128)(2,1)S(1)}, bf16[1,2,256,192]{2,3,1,0:T(8,128)(2,1)}, u32[]{:S(2)}) copy-start(bf16[1,2,256,192]{2,3,1,0:T(8,128)(2,1)} %get-tuple-element.83) | copy-start | bytes 589828
  95.2 5.0 %copy-start.43 = (bf16[1,2,256,192]{2,3,1,0:T(8,128)(2,1)S(1)}, bf16[1,2,256,192]{2,3,1,0:T(8,128)(2,1)}, u32[]{:S(2)}) copy-start(bf16[1,2,256,192]{2,3,1,0:T(8,128)(2,1)} %get-tuple-element.87) | copy-start | bytes 589828
  95.2 5.4 %collective-permute-start.12 = (bf16[2,1,128,384]{3,2,0,1:T(8,128)(2,1)S(1)}, bf16[2,1,128,384]{3,2,0,1:T(8,128)(2,1)S(1)}, u32[]{:S(2)}, u32[]{:S(2)}) collective-permute-start(bf16[2,1,128,384]{3,2,0,1:T(8,128)(2,1)S(1)} %fusion.89), channel_id=1, source_target_pairs={{0,1},{1,2},{2,3},{3,4},{4,5},{5,6},{6,7},{7,8},{8,9},{9,10},{10,1... | collective-permute-start | bytes 589832 | tf_op jit(solution)/shard_map/ppermute | solution.py:15
  97.3 7.9 %collective-permute-start.13 = (bf16[2,1,128,384]{3,2,0,1:T(8,128)(2,1)S(1)}, bf16[2,1,128,384]{3,2,0,1:T(8,128)(2,1)S(1)}, u32[]{:S(2)}, u32[]{:S(2)}) collective-permute-start(bf16[2,1,128,384]{3,2,0,1:T(8,128)(2,1)S(1)} %fusion.89), channel_id=1, source_target_pairs={{1,0},{2,1},{3,2},{4,3},{5,4},{6,5},{7,6},{8,7},{9,8},{10,9},{11,1... | collective-permute-start | bytes 589832 | tf_op jit(solution)/shard_map/ppermute | solution.py:16
  123.9 1.7 %copy-start.1 = (bf16[384,384]{1,0:T(8,128)(2,1)S(1)}, bf16[384,384]{1,0:T(8,128)(2,1)}, u32[]{:S(2)}) copy-start(bf16[384,384]{1,0:T(8,128)(2,1)} %param.14) | copy-start | bytes 884740
  (24 other events, 28.8 us)

commit v3 on v1

--- a/solution.py
+++ b/solution.py
@@ -20,6 +20,56 @@
 def extended(x, dim, width):
     before, after = halo_rows(x, dim, width)
     return jnp.concatenate([before, x, after], axis=dim)
+
+
+def joint_halo(block, cache):
+    count = lax.axis_size("ha")
+    up = [(i, i + 1) for i in range(count - 1)]
+    down = [(j, i) for i, j in up]
+    frames = block.shape[0]
+
+    def flat(rows):
+        return rows.reshape(frames, -1)
+
+    last = jnp.concatenate([flat(block[:, -1:]), flat(cache[:, -1:])], axis=1)
+    head = jnp.concatenate([flat(block[:, :1]), flat(cache[:, :1])], axis=1)
+    before = lax.ppermute(last, "ha", up)
+    after = lax.ppermute(head, "ha", down)
+    split = block[:, :1].size // frames
+
+    def rows(part, like):
+        return part.reshape((frames, 1) + like.shape[2:])
+
+    block_pad = jnp.concatenate(
+        [rows(before[:, :split], block), block, rows(after[:, :split], block)], axis=1
+    )
+    cache_pad = jnp.concatenate(
+        [rows(before[:, split:], cache), cache, rows(after[:, split:], cache)], axis=1
+    )
+    return block_pad, cache_pad
+
+
+def conv_rows(padded, weight, starts, rows):
+    width = padded.shape[2]
+    channels = padded.shape[3]
+    cols = jnp.pad(padded, ((0, 0), (0, 0), (1, 1), (0, 0)))
+    result = None
+    for row_off in range(3):
+        window = jnp.stack([cols[:, r] for r in rows[row_off]], axis=1)
+        stacked = jnp.concatenate([window[:, :, s : s + width] for s in starts], axis=-1)
+        kernel = weight[row_off].reshape(3 * channels, weight.shape[-1])
+        term = jnp.einsum("fhwc,cd->fhwd", stacked, kernel, preferred_element_type=jnp.float32)
+        result = term if result is None else result + term
+    return result
+
+
+def upsample_conv(block_pad, weight):
+    rows = ((0, 0, 1, 1), (0, 1, 1, 2), (1, 1, 2, 2))
+    even = conv_rows(block_pad, weight, (0, 1, 1), rows)
+    odd = conv_rows(block_pad, weight, (1, 1, 2), rows)
+    frames, height, width, channels = even.shape
+    both = jnp.stack([even, odd], axis=3)
+    return both.reshape(frames, height, 2 * width, channels)
 
 
 def gather_rows(x):
@@ -116,14 +166,17 @@
     block_out = (mixed.astype(jnp.float32) + conv_taps(first_padded, w_first, 3)).astype(
         jnp.bfloat16
     )
-    block_padded = extended(block_out, 1, 1)
-    enlarged = jnp.repeat(jnp.repeat(block_padded, 2, axis=1), 2, axis=2)
-    up_padded = enlarged[:, 1 : enlarged.shape[1] - 1]
-    upsampled = conv_taps(up_padded, w_upsample[None], 1).astype(jnp.bfloat16)
+    block_pad, cache_pad = joint_halo(block_out, second_cache)
+    upsampled = upsample_conv(block_pad, w_upsample).astype(jnp.bfloat16)
     second_in = jax.nn.silu(rms_scale(upsampled)).astype(jnp.bfloat16)
-    second_stack = jnp.concatenate([second_cache, second_in], axis=0)
-    second_padded = extended(second_stack, 1, 1)
-    return (upsampled.astype(jnp.float32) + conv_taps(second_padded, w_second, 3)).astype(
+    me = lax.axis_index("ha")
+    count = lax.axis_size("ha")
+    row = lax.broadcasted_iota(jnp.int32, (1, second_in.shape[1], 1, 1), 1)
+    outside = ((row == 0) & (me == 0)) | ((row == second_in.shape[1] - 1) & (me == count - 1))
+    second_in = jnp.where(outside, jnp.zeros_like(second_in), second_in)
+    second_padded = jnp.concatenate([cache_pad, second_in], axis=0)
+    own = upsampled[:, 1 : upsampled.shape[1] - 1]
+    return (own.astype(jnp.float32) + conv_taps(second_padded, w_second, 3)).astype(
         jnp.bfloat16
     )
 

time: 124 us -> 145 us (1.17)
  local copies, waits for them, and re-layouts: 21.4 us -> 47.2 us
  waiting for transfers between devices: 43.2 us -> 34.9 us
  starting transfers between devices: 23.1 us -> 18.1 us
  matrix products: 25.8 us -> 30.2 us
  other arithmetic: 7.62 us -> 11.9 us
    slice x1 -> x13, local copies, waits for them, and re-layouts: 0.16 us -> 13.9 us  [the longest x4 7.94 us: conv_rows(): kernel = weight[row_off].reshape(3 * channels, weight.shape[-1])]
    unnamed x28 -> x47, local copies, waits for them, and re-layouts: 1.43 us -> 9.11 us
    ppermute x3 -> x1, starting transfers between devices: 9.38 us -> 2.59 us  [halo_rows(): after = lax.ppermute(first, 'ha', down)]
    ppermute x0 -> x2, waiting for transfers between devices: none -> 6.61 us  [the longest x1 6.37 us: joint_halo(): after = lax.ppermute(head, 'ha', down)]
    ppermute x3 -> x1, waiting for transfers between devices: 9.83 us -> 3.5 us  [halo_rows(): after = lax.ppermute(first, 'ha', down)]
    dot_general x0 -> x6, matrix products: none -> 5.64 us  [conv_rows(): jnp.einsum('fhwc,cd->fhwd', stacked, kernel, preferred_element_type=jnp.f...]
    ppermute x7, waiting for transfers between devices: 30 us -> 24.8 us  [gather_rows(): pieces.append(lax.ppermute(x, 'ha', pairs))]
    ppermute x0 -> x2, starting transfers between devices: none -> 5.12 us  [the longest x1 3.2 us: joint_halo(): after = lax.ppermute(head, 'ha', down)]
  transfers between devices with their start and end apart: 14 -> 12, of which waited for: 10 -> 8; matrix products, arithmetic and copies ran while one was open for 8% -> 26% of each run, Pallas kernels for 0% -> 0%
where the time goes in v3:
time: 145 us; the launch traced here: 143 us
  local copies, waits for them, and re-layouts  47.2 us (33%)
  waiting for transfers between devices  34.9 us (24%)
  matrix products  30.2 us (21%)
  starting transfers between devices  18.1 us (12%)
  other arithmetic  11.9 us (8%)
    ppermute x7, waiting for transfers between devices, gather_rows(): pieces.append(lax.ppermute(x, 'ha', pairs))  24.8 us
    dot_general x18, matrix products, conv_taps(): jnp.einsum('fhwc,cd->fhwd', stacked, kernel, preferred_element_type=jnp.f...  9.72 us
    unnamed x47, local copies, waits for them, and re-layouts  9.11 us
    slice x4, local copies, waits for them, and re-layouts, conv_rows(): kernel = weight[row_off].reshape(3 * channels, weight.shape[-1])  7.94 us
    ppermute x7, starting transfers between devices, gather_rows(): pieces.append(lax.ppermute(x, 'ha', pairs))  7.87 us
    dot_general x1, matrix products, per_device(): jnp.einsum('fqc,fkc->fqk', queries, keys_all, preferred_element_type=jnp....  6.43 us
    ppermute x1, waiting for transfers between devices, joint_halo(): after = lax.ppermute(head, 'ha', down)  6.37 us
    another operation x3, local copies, waits for them, and re-layouts, conv_rows(): kernel = weight[row_off].reshape(3 * channels, weight.shape[-1])  6.33 us
  transfers between devices with their start and end apart: 12, of which 8 were waited for; matrix products, arithmetic and copies ran while one was open for 26% of the time, Pallas kernels for 0%

profile of v3, /device:TPU:13, one launch (start us, length us, event | category | flops | bytes accessed | tf_op | source)
XLA Modules:
  0.0 143.1 jit_solution(14972265048331362813)
XLA Ops:
  0.0 1.2 collective-permute-start
  1.2 1.3 collective-permute-start.1
  2.5 1.0 collective-permute-start.2
  3.5 1.3 collective-permute-start.3
  4.9 1.0 collective-permute-start.4
  5.9 1.7 %constant_dynamic-update-slice_fusion.7 = (bf16[2,8,128,384]{3,2,1,0:T(8,128)(2,1)}, bf16[2,16,128,384]{3,2,1,0:T(8,128)(2,1)S(1)}) fusion(bf16[2,1,128,384]{3,2,1,0:T(8,128)(2,1)} %param.10), kind=kLoop, calls=%fused_computation.245 | loop fusion | bytes 589824
  7.5 1.2 collective-permute-start.5
  11.6 18.8 %collective-permute-done.2 = bf16[2,1,128,384]{3,2,1,0:T(8,128)(2,1)S(1)} collective-permute-done((bf16[2,1,128,384]{3,2,1,0:T(8,128)(2,1)}, bf16[2,1,128,384]{3,2,1,0:T(8,128)(2,1)S(1)}, u32[]{:S(2)}, u32[]{:S(2)}) %collective-permute-start.2) | collective-permute-done | bytes 196640 | tf_op jit(solution)/shard_map/ppermute | solution.py:83
  31.1 3.5 %collective-permute-done.3 = bf16[2,1,128,384]{3,2,1,0:T(8,128)(2,1)S(1)} collective-permute-done((bf16[2,1,128,384]{3,2,1,0:T(8,128)(2,1)}, bf16[2,1,128,384]{3,2,1,0:T(8,128)(2,1)S(1)}, u32[]{:S(2)}, u32[]{:S(2)}) %collective-permute-start.3) | collective-permute-done | bytes 196640 | tf_op jit(solution)/shard_map/ppermute | solution.py:83
  36.0 1.4 collective-permute-done.5
  40.6 1.8 %copy.66 = bf16[2,1,256,192]{3,2,0,1:T(8,128)(2,1)} copy(bf16[2,1,256,192]{2,3,1,0:T(8,128)(2,1)} %get-tuple-element.94) | data formatting | bytes 393216 | tf_op jit(solution)/shard_map/slice | solution.py:34
  42.3 2.0 %reshape.166 = bf16[2,49152]{1,0:T(2,128)(2,1)} reshape(bf16[2,1,256,192]{3,2,0,1:T(8,128)(2,1)} %copy.66) | data formatting | bytes 393216 | tf_op jit(solution)/shard_map/reshape | solution.py:32
  44.3 1.8 %copy.67 = bf16[2,1,256,192]{3,2,0,1:T(8,128)(2,1)} copy(bf16[2,1,256,192]{2,3,1,0:T(8,128)(2,1)} %get-tuple-element.93) | data formatting | bytes 393216 | tf_op jit(solution)/shard_map/slice | solution.py:35
  46.0 2.0 %reshape.168 = bf16[2,49152]{1,0:T(2,128)(2,1)} reshape(bf16[2,1,256,192]{3,2,0,1:T(8,128)(2,1)} %copy.67) | data formatting | bytes 393216 | tf_op jit(solution)/shard_map/reshape | solution.py:32
  48.0 2.3 %fusion.190 = (bf16[1,3,384,192]{2,3,1,0:T(8,128)(2,1)}, bf16[1,3,384,192]{2,3,1,0:T(8,128)(2,1)}, bf16[1,3,384,192]{2,3,1,0:T(8,128)(2,1)S(1)}) fusion(bf16[3,3,384,192]{2,3,1,0:T(8,128)(2,1)} %param.18), kind=kLoop, calls=%fused_computation.282 | loop fusion | bytes 2654208 | tf_op jit(solution)/shard_map/slice | solution.py:60
  50.3 1.2 copy.70
  51.5 2.1 %reshape.187 = bf16[1152,192,1,1]{0,1,2,3:T(8,128)(2,1)} reshape(bf16[1,3,384,192]{2,1,3,0:T(4,128)(2,1)} %copy.70) | data formatting | bytes 884736 | tf_op jit(solution)/shard_map/reshape;squeeze | solution.py:60
  53.6 2.2 %copy.68 = bf16[1,3,384,192]{2,1,3,0:T(4,128)(2,1)} copy(bf16[1,3,384,192]{2,3,1,0:T(8,128)(2,1)} %get-tuple-element.47) | data formatting | bytes 884736 | tf_op jit(solution)/shard_map/slice | solution.py:60
  55.8 2.1 %reshape.186 = bf16[1152,192,1,1]{0,1,2,3:T(8,128)(2,1)} reshape(bf16[1,3,384,192]{2,1,3,0:T(4,128)(2,1)} %copy.68) | data formatting | bytes 884736 | tf_op jit(solution)/shard_map/reshape;squeeze | solution.py:60
  57.9 2.2 %copy.72 = bf16[1,3,384,192]{2,1,3,0:T(4,128)(2,1)} copy(bf16[1,3,384,192]{2,3,1,0:T(8,128)(2,1)} %get-tuple-element.46) | data formatting | bytes 884736 | tf_op jit(solution)/shard_map/slice | solution.py:60
  60.2 2.1 %reshape.188 = bf16[1152,192,1,1]{0,1,2,3:T(8,128)(2,1)} reshape(bf16[1,3,384,192]{2,1,3,0:T(4,128)(2,1)} %copy.72) | data formatting | bytes 884736 | tf_op jit(solution)/shard_map/reshape;squeeze | solution.py:60
  62.3 1.0 fusion.156
  63.3 2.1 %convolution_convert_fusion.2 = bf16[2,128,384]{2,1,0:T(8,128)(2,1)} fusion(bf16[384,384]{1,0:T(8,128)(2,1)} %param.13, bf16[2,1,128,384]{3,2,1,0:T(8,128)(2,1)} %param.10, f32[2,128]{1,0:T(2,128)S(1)} %add_rsqrt_fusion.2), kind=kOutput, calls=%fused_computation.145 | convolution fusion | flops 75890688 | bytes 689152 | tf_op jit(solution)/shard_map/ftc,cd->ftd/dot_general | solution.py:117
  65.4 1.8 %constant_dynamic-update-slice_fusion.8 = bf16[2,16,128,384]{3,2,1,0:T(8,128)(2,1)S(1)} fusion(bf16[2,16,128,384]{3,2,1,0:T(8,128)(2,1)S(1)} %get-tuple-element.106, bf16[2,8,128,384]{3,2,1,0:T(8,128)(2,1)} %collective-permute-done.7), kind=kLoop, calls=%fused_computation.246 | loop fusion | bytes 3145728 | tf_op jit(solution)/shard_map/concatenate | solution.py:87
  67.9 2.0 %fusion = bf16[2,2048,384]{2,1,0:T(8,128)(2,1)} fusion(f32[2,2048]{1,0:T(2,128)S(1)} %bitcast.233, bf16[2,16,128,384]{3,2,1,0:T(8,128)(2,1)S(1)} %constant_dynamic-update-slice_fusion.8), kind=kLoop, calls=%fused_computation.1 | loop fusion | flops 4718592 | bytes 6307840 | tf_op jit(solution)/shard_map/convert_element_type | solution.py:136
  69.9 6.4 %fusion.202 = (f32[2,128]{1,0:T(2,128)S(1)}, f32[2,128,2048]{2,1,0:T(8,128)}) fusion(bf16[2,128,384]{2,1,0:T(8,128)(2,1)} %convolution_convert_fusion.2, bf16[2,2048,384]{2,1,0:T(8,128)(2,1)} %fusion, bf16[384,384]{1,0:T(8,128)(2,1)S(1)} %copy-done), kind=kOutput, calls=%fused_computation.294 | convolution fusion | flops 1613233920 | bytes 5735424 | tf_op jit(solution)/shard_map/fqc,fkc->fqk/dot_general | solution.py:145
  76.3 2.0 %fusion.20 = f32[2,128]{1,0:T(2,128)S(1)} fusion(f32[2,128,2048]{2,1,0:T(8,128)} %get-tuple-element.122, f32[2,128]{1,0:T(2,128)S(1)} %get-tuple-element.121), kind=kLoop, calls=%fused_computation.55 | loop fusion | flops 1048320 | bytes 2099200 | tf_op jit(solution)/shard_map/reduce_sum | solution.py:150
  78.4 4.9 %fusion.102 = bf16[2,128,384]{2,1,0:T(8,128)(2,1)} fusion(bf16[2,2048,384]{2,1,0:T(8,128)(2,1)S(1)} %copy-done.2, f32[2,128,2048]{2,1,0:T(8,128)} %get-tuple-element.122, f32[2,128]{1,0:T(2,128)S(1)} %get-tuple-element.121, bf16[384,384]{1,0:T(8,128)(2,1)} %param.15, f32[2,128]{1,0:T(2,128)S(1)} %fusion.20), kind=kOutput, calls=%fused_computation.149 | convolution fusion | flops 1613430784 | bytes 5736448 | tf_op jit(solution)/shard_map/fqk,fkc->fqc/dot_general | solution.py:151
  83.3 1.4 %multiply_reduce_fusion.2 = (f32[2,128]{1,0:T(2,128)S(1)}, f32[2,1,128,384]{3,2,0,1:T(8,128)S(1)}) fusion(bf16[2,128,384]{2,1,0:T(8,128)(2,1)} %fusion.102, bf16[384,384]{1,0:T(8,128)(2,1)} %param.16, bf16[2,1,128,384]{3,2,1,0:T(8,128)(2,1)S(1)} %copy-done.3), kind=kOutput, calls=%fused_computation.227 | convolution fusion | flops 76087040 | bytes 1082368 | tf_op jit(solution)/shard_map/ftc,cd->ftd/dot_general | solution.py:158
  85.0 1.0 pad_maximum_fusion.12
  86.0 2.1 %collective-permute-start.8 = (bf16[4,1,128,384]{3,2,0,1:T(8,128)(2,1)S(1)}, bf16[4,1,128,384]{3,2,0,1:T(8,128)(2,1)S(1)}, u32[]{:S(2)}, u32[]{:S(2)}) collective-permute-start(bf16[4,1,128,384]{3,2,0,1:T(8,128)(2,1)S(1)} %pad_maximum_fusion.12), channel_id=1, source_target_pairs={{0,1},{1,2},{2,3},{3,4},{4,5},{5,6},{6,7},{7,8},{8,9},{9,10},{10,1... | collective-permute-start | bytes 1179656 | tf_op jit(solution)/shard_map/ppermute | solution.py:15
  88.0 2.6 %collective-permute-start.9 = (bf16[4,1,128,384]{3,2,0,1:T(8,128)(2,1)S(1)}, bf16[4,1,128,384]{3,2,0,1:T(8,128)(2,1)S(1)}, u32[]{:S(2)}, u32[]{:S(2)}) collective-permute-start(bf16[4,1,128,384]{3,2,0,1:T(8,128)(2,1)S(1)} %pad_maximum_fusion.12), channel_id=1, source_target_pairs={{1,0},{2,1},{3,2},{4,3},{5,4},{6,5},{7,6},{8,7},{9,8},{10,9},{11,1... | collective-permute-start | bytes 1179656 | tf_op jit(solution)/shard_map/ppermute | solution.py:16
  90.6 3.9 %fusion.187 = (bf16[1,1,3,384,384]{4,3,2,1,0:T(8,128)(2,1)S(1)}, bf16[1,1,3,384,384]{4,3,2,1,0:T(8,128)(2,1)S(1)}, bf16[1,1,3,384,384]{4,3,2,1,0:T(8,128)(2,1)S(...) fusion(bf16[3,3,3,384,384]{4,3,2,1,0:T(8,128)(2,1)} %param.17), kind=kLoop, calls=%fused_computation.279 | loop fusion | bytes 15925248 | tf_op jit(solution)/shard_map/slice | solution.py:109
  94.6 3.5 %collective-permute-done.9 = bf16[4,1,128,384]{3,2,0,1:T(8,128)(2,1)S(1)} collective-permute-done((bf16[4,1,128,384]{3,2,0,1:T(8,128)(2,1)S(1)}, bf16[4,1,128,384]{3,2,0,1:T(8,128)(2,1)S(1)}, u32[]{:S(2)}, u32[]{:S(2)}) %collective-permute-start.9) | collective-permute-done | bytes 393248 | tf_op jit(solution)/shard_map/ppermute | solution.py:16
  104.7 1.9 %collective-permute-start.10 = (bf16[2,98304]{1,0:T(2,128)(2,1)S(1)}, bf16[2,98304]{1,0:T(2,128)(2,1)S(1)}, u32[]{:S(2)}, u32[]{:S(2)}) collective-permute-start(bf16[2,98304]{1,0:T(2,128)(2,1)S(1)} %get-tuple-element.104), channel_id=1, source_target_pairs={{0,1},{1,2},{2,3},{3,4},{4,5},{5,6},{6,7},{7,8},{8,9},{9,10},{10,1... | collective-permute-start | bytes 1179656 | tf_op jit(solution)/shard_map/ppermute | solution.py:36
  106.7 1.2 fusion.188
  107.9 3.2 %collective-permute-start.11 = (bf16[2,98304]{1,0:T(2,128)(2,1)S(1)}, bf16[2,98304]{1,0:T(2,128)(2,1)S(1)}, u32[]{:S(2)}, u32[]{:S(2)}) collective-permute-start(bf16[2,98304]{1,0:T(2,128)(2,1)S(1)} %get-tuple-element.103), channel_id=1, source_target_pairs={{1,0},{2,1},{3,2},{4,3},{5,4},{6,5},{7,6},{8,7},{9,8},{10,9},{11,1... | collective-permute-start | bytes 1179656 | tf_op jit(solution)/shard_map/ppermute | solution.py:37
  111.6 6.4 %collective-permute-done.11 = bf16[2,98304]{1,0:T(2,128)(2,1)S(1)} collective-permute-done((bf16[2,98304]{1,0:T(2,128)(2,1)S(1)}, bf16[2,98304]{1,0:T(2,128)(2,1)S(1)}, u32[]{:S(2)}, u32[]{:S(2)}) %collective-permute-start.11) | collective-permute-done | bytes 393248 | tf_op jit(solution)/shard_map/ppermute | solution.py:37
  120.2 1.0 fusion.4
  121.2 0.9 fusion.16
  122.2 0.9 fusion.10
  124.1 0.9 fusion.23
  125.1 0.9 fusion.32
  127.0 0.9 fusion.29
  128.0 0.9 fusion.38
  129.3 1.0 copy.77
  132.8 2.5 %pad_slice_fusion.1 = (bf16[2,2,256,192]{2,3,1,0:T(8,128)(2,1)S(1)}, bf16[2,2,256,192]{2,3,1,0:T(8,128)(2,1)S(1)}, bf16[2,2,256,192]{2,3,1,0:T(8,128)(2,1)S(1)},...) fusion(bf16[4,4,256,192]{2,3,1,0:T(8,128)(2,1)S(1)} %pad_maximu, ...), kind=kLoop, calls=%fused_computation.4 | loop fusion | bytes 9830400 | tf_op jit(solution)/shard_map/slice | solution.py:107
  141.8 1.3 fusion.46
  (111 shorter events, 29.4 us)
Async XLA Ops:
  0.0 69.9 %copy-start = (bf16[384,384]{1,0:T(8,128)(2,1)S(1)}, bf16[384,384]{1,0:T(8,128)(2,1)}, u32[]{:S(2)}) copy-start(bf16[384,384]{1,0:T(8,128)(2,1)} %param.14) | copy-start | bytes 884740
  0.0 39.8 %copy-start.6 = (bf16[2,2,256,192]{2,3,1,0:T(8,128)(2,1)S(1)}, bf16[2,2,256,192]{2,3,1,0:T(8,128)(2,1)}, u32[]{:S(2)}) copy-start(bf16[2,2,256,192]{2,3,1,0:T(8,128)(2,1)} %param.12) | copy-start | bytes 1179652
  0.0 7.5 %collective-permute-start = (bf16[2,1,128,384]{3,2,1,0:T(8,128)(2,1)}, bf16[2,1,128,384]{3,2,1,0:T(8,128)(2,1)S(1)}, u32[]{:S(2)}, u32[]{:S(2)}) collective-permute-start(bf16[2,1,128,384]{3,2,1,0:T(8,128)(2,1)} %param.10), channel_id=1, source_target_pairs={{0,2},{1,3},{2,4},{3,5},{4,6},{5,7},{6,8},{7,9},{8,10},{9,11},{10,... | collective-permute-start | bytes 589832 | tf_op jit(solution)/shard_map/ppermute | solution.py:83
  1.2 8.9 %collective-permute-start.1 = (bf16[2,1,128,384]{3,2,1,0:T(8,128)(2,1)}, bf16[2,1,128,384]{3,2,1,0:T(8,128)(2,1)S(1)}, u32[]{:S(2)}, u32[]{:S(2)}) collective-permute-start(bf16[2,1,128,384]{3,2,1,0:T(8,128)(2,1)} %param.10), channel_id=1, source_target_pairs={{0,4},{1,5},{2,6},{3,7},{4,8},{5,9},{6,10},{7,11},{8,12},{9,13},{1... | collective-permute-start | bytes 589832 | tf_op jit(solution)/shard_map/ppermute | solution.py:83
  2.5 27.9 %collective-permute-start.2 = (bf16[2,1,128,384]{3,2,1,0:T(8,128)(2,1)}, bf16[2,1,128,384]{3,2,1,0:T(8,128)(2,1)S(1)}, u32[]{:S(2)}, u32[]{:S(2)}) collective-permute-start(bf16[2,1,128,384]{3,2,1,0:T(8,128)(2,1)} %param.10), channel_id=1, source_target_pairs={{0,6},{1,7},{2,8},{3,9},{4,10},{5,11},{6,12},{7,13},{8,14},{9,15},... | collective-permute-start | bytes 589832 | tf_op jit(solution)/shard_map/ppermute | solution.py:83
  3.5 31.1 %collective-permute-start.3 = (bf16[2,1,128,384]{3,2,1,0:T(8,128)(2,1)}, bf16[2,1,128,384]{3,2,1,0:T(8,128)(2,1)S(1)}, u32[]{:S(2)}, u32[]{:S(2)}) collective-permute-start(bf16[2,1,128,384]{3,2,1,0:T(8,128)(2,1)} %param.10), channel_id=1, source_target_pairs={{0,8},{1,9},{2,10},{3,11},{4,12},{5,13},{6,14},{7,15},{8,0},{9,1},... | collective-permute-start | bytes 589832 | tf_op jit(solution)/shard_map/ppermute | solution.py:83
  4.9 30.5 %collective-permute-start.4 = (bf16[2,1,128,384]{3,2,1,0:T(8,128)(2,1)}, bf16[2,1,128,384]{3,2,1,0:T(8,128)(2,1)S(1)}, u32[]{:S(2)}, u32[]{:S(2)}) collective-permute-start(bf16[2,1,128,384]{3,2,1,0:T(8,128)(2,1)} %param.10), channel_id=1, source_target_pairs={{0,10},{1,11},{2,12},{3,13},{4,14},{5,15},{6,0},{7,1},{8,2},{9,3},... | collective-permute-start | bytes 589832 | tf_op jit(solution)/shard_map/ppermute | solution.py:83
  7.5 29.9 %collective-permute-start.5 = (bf16[2,1,128,384]{3,2,1,0:T(8,128)(2,1)}, bf16[2,1,128,384]{3,2,1,0:T(8,128)(2,1)S(1)}, u32[]{:S(2)}, u32[]{:S(2)}) collective-permute-start(bf16[2,1,128,384]{3,2,1,0:T(8,128)(2,1)} %param.10), channel_id=1, source_target_pairs={{0,12},{1,13},{2,14},{3,15},{4,0},{5,1},{6,2},{7,3},{8,4},{9,5},{1... | collective-permute-start | bytes 589832 | tf_op jit(solution)/shard_map/ppermute | solution.py:83
  10.1 28.5 %collective-permute-start.6 = (bf16[2,1,128,384]{3,2,1,0:T(8,128)(2,1)}, bf16[2,1,128,384]{3,2,1,0:T(8,128)(2,1)S(1)}, u32[]{:S(2)}, u32[]{:S(2)}) collective-permute-start(bf16[2,1,128,384]{3,2,1,0:T(8,128)(2,1)} %param.10), channel_id=1, source_target_pairs={{0,14},{1,15},{2,0},{3,1},{4,2},{5,3},{6,4},{7,5},{8,6},{9,7},{10,... | collective-permute-start | bytes 589832 | tf_op jit(solution)/shard_map/ppermute | solution.py:83
  39.3 26.1 %collective-permute-start.7 = (bf16[2,8,128,384]{3,2,1,0:T(8,128)(2,1)}, bf16[2,8,128,384]{3,2,1,0:T(8,128)(2,1)}, u32[]{:S(2)}, u32[]{:S(2)}) collective-permute-start(bf16[2,8,128,384]{3,2,1,0:T(8,128)(2,1)} %get-tuple-element.105), channel_id=1, source_target_pairs={{0,1},{1,0},{2,3},{3,2},{4,5},{5,4},{6,7},{7,6},{8,9},{9,8},{10,11... | collective-permute-start | bytes 4718600 | tf_op jit(solution)/shard_map/ppermute | solution.py:86
  69.9 8.4 %copy-start.2 = (bf16[2,2048,384]{2,1,0:T(8,128)(2,1)S(1)}, bf16[2,2048,384]{2,1,0:T(8,128)(2,1)}, u32[]{:S(2)}) copy-start(bf16[2,2048,384]{2,1,0:T(8,128)(2,1)} %fusion) | copy-start | bytes 9437188
  78.4 5.0 %copy-start.3 = (bf16[2,1,128,384]{3,2,1,0:T(8,128)(2,1)S(1)}, bf16[2,1,128,384]{3,2,1,0:T(8,128)(2,1)}, u32[]{:S(2)}) copy-start(bf16[2,1,128,384]{3,2,1,0:T(8,128)(2,1)} %param.10) | copy-start | bytes 589828
  85.9 8.6 %copy-start.5 = (bf16[2,1,128,384]{3,2,1,0:T(8,128)(2,1)S(1)}, bf16[2,1,128,384]{3,2,1,0:T(8,128)(2,1)}, u32[]{:S(2)}) copy-start(bf16[2,1,128,384]{3,2,1,0:T(8,128)(2,1)} %param.11) | copy-start | bytes 589828
  86.0 8.7 %collective-permute-start.8 = (bf16[4,1,128,384]{3,2,0,1:T(8,128)(2,1)S(1)}, bf16[4,1,128,384]{3,2,0,1:T(8,128)(2,1)S(1)}, u32[]{:S(2)}, u32[]{:S(2)}) collective-permute-start(bf16[4,1,128,384]{3,2,0,1:T(8,128)(2,1)S(1)} %pad_maximum_fusion.12), channel_id=1, source_target_pairs={{0,1},{1,2},{2,3},{3,4},{4,5},{5,6},{6,7},{7,8},{8,9},{9,10},{10,1... | collective-permute-start | bytes 1179656 | tf_op jit(solution)/shard_map/ppermute | solution.py:15
  88.0 10.1 %collective-permute-start.9 = (bf16[4,1,128,384]{3,2,0,1:T(8,128)(2,1)S(1)}, bf16[4,1,128,384]{3,2,0,1:T(8,128)(2,1)S(1)}, u32[]{:S(2)}, u32[]{:S(2)}) collective-permute-start(bf16[4,1,128,384]{3,2,0,1:T(8,128)(2,1)S(1)} %pad_maximum_fusion.12), channel_id=1, source_target_pairs={{1,0},{2,1},{3,2},{4,3},{5,4},{6,5},{7,6},{8,7},{9,8},{10,9},{11,1... | collective-permute-start | bytes 1179656 | tf_op jit(solution)/shard_map/ppermute | solution.py:16
  103.1 0.9 copy-start.8
  103.1 1.0 copy-start.9
  103.1 3.5 %copy-start.4 = (bf16[3,3,3,192,192]{4,3,2,1,0:T(8,128)(2,1)S(1)}, bf16[3,3,3,192,192]{4,3,2,1,0:T(8,128)(2,1)}, u32[]{:S(2)}) copy-start(bf16[3,3,3,192,192]{4,3,2,1,0:T(8,128)(2,1)} %param.19) | copy-start | bytes 5971972
  104.7 6.6 %collective-permute-start.10 = (bf16[2,98304]{1,0:T(2,128)(2,1)S(1)}, bf16[2,98304]{1,0:T(2,128)(2,1)S(1)}, u32[]{:S(2)}, u32[]{:S(2)}) collective-permute-start(bf16[2,98304]{1,0:T(2,128)(2,1)S(1)} %get-tuple-element.104), channel_id=1, source_target_pairs={{0,1},{1,2},{2,3},{3,4},{4,5},{5,6},{6,7},{7,8},{8,9},{9,10},{10,1... | collective-permute-start | bytes 1179656 | tf_op jit(solution)/shard_map/ppermute | solution.py:36
  107.9 10.1 %collective-permute-start.11 = (bf16[2,98304]{1,0:T(2,128)(2,1)S(1)}, bf16[2,98304]{1,0:T(2,128)(2,1)S(1)}, u32[]{:S(2)}, u32[]{:S(2)}) collective-permute-start(bf16[2,98304]{1,0:T(2,128)(2,1)S(1)} %get-tuple-element.103), channel_id=1, source_target_pairs={{1,0},{2,1},{3,2},{4,3},{5,4},{6,5},{7,6},{8,7},{9,8},{10,9},{11,1... | collective-permute-start | bytes 1179656 | tf_op jit(solution)/shard_map/ppermute | solution.py:37
  120.2 1.0 copy-start.12
  123.1 1.0 copy-start.11
  126.0 1.0 copy-start.10
  130.9 1.7 %copy-start.7 = (bf16[2,2,256,192]{2,3,1,0:T(8,128)(2,1)S(1)}, bf16[2,2,256,192]{2,3,1,0:T(8,128)(2,1)}, u32[]{:S(2)}) copy-start(bf16[2,2,256,192]{2,3,1,0:T(8,128)(2,1)} %param.12) | copy-start | bytes 1179652
  135.3 1.0 copy-start.18
  136.3 1.0 copy-start.17
  136.8 1.0 copy-start.16
  137.8 1.0 copy-start.15
  138.3 1.0 copy-start.14
  139.3 1.0 copy-start.13
  141.8 1.3 copy-start.1

commit v4 on v1

--- a/solution.py
+++ b/solution.py
@@ -42,9 +42,9 @@
     return widened * lax.rsqrt(jnp.mean(widened * widened, axis=-1, keepdims=True) + 1e-06)
 
 
-def conv_taps(padded, weight, time_taps):
+def conv_taps(padded, weight, time_taps, rows=None):
     frames_out = padded.shape[0] - time_taps + 1
-    height_out = padded.shape[1] - 2
+    height_out = padded.shape[1] - 2 if rows is None else len(rows[0])
     width_out = padded.shape[2]
     in_channels = weight.shape[-2]
     out_channels = weight.shape[-1]
@@ -52,7 +52,12 @@
     result = jnp.zeros((frames_out, height_out, width_out, out_channels), jnp.float32)
     for time_off in range(time_taps):
         for row_off in range(3):
-            window = widened[time_off : time_off + frames_out, row_off : row_off + height_out]
+            if rows is None:
+                window = widened[time_off : time_off + frames_out, row_off : row_off + height_out]
+            else:
+                window = jnp.stack(
+                    [widened[time_off : time_off + frames_out, r] for r in rows[row_off]], axis=1
+                )
             stacked = jnp.concatenate(
                 [window[:, :, col_off : col_off + width_out] for col_off in range(3)], axis=-1
             )
@@ -113,17 +118,24 @@
     first_in = jax.nn.silu(rms_scale(mixed)).astype(jnp.bfloat16)
     first_stack = jnp.concatenate([first_cache, first_in], axis=0)
     first_padded = extended(first_stack, 1, 1)
+    second_cache_pad = extended(second_cache, 1, 1)
     block_out = (mixed.astype(jnp.float32) + conv_taps(first_padded, w_first, 3)).astype(
         jnp.bfloat16
     )
     block_padded = extended(block_out, 1, 1)
-    enlarged = jnp.repeat(jnp.repeat(block_padded, 2, axis=1), 2, axis=2)
-    up_padded = enlarged[:, 1 : enlarged.shape[1] - 1]
-    upsampled = conv_taps(up_padded, w_upsample[None], 1).astype(jnp.bfloat16)
+    widened = jnp.repeat(block_padded, 2, axis=2)
+    upsampled = conv_taps(
+        widened, w_upsample[None], 1, rows=((0, 0, 1, 1), (0, 1, 1, 2), (1, 1, 2, 2))
+    ).astype(jnp.bfloat16)
     second_in = jax.nn.silu(rms_scale(upsampled)).astype(jnp.bfloat16)
-    second_stack = jnp.concatenate([second_cache, second_in], axis=0)
-    second_padded = extended(second_stack, 1, 1)
-    return (upsampled.astype(jnp.float32) + conv_taps(second_padded, w_second, 3)).astype(
+    me = lax.axis_index("ha")
+    count = lax.axis_size("ha")
+    row = lax.broadcasted_iota(jnp.int32, (1, second_in.shape[1], 1, 1), 1)
+    outside = ((row == 0) & (me == 0)) | ((row == second_in.shape[1] - 1) & (me == count - 1))
+    second_in = jnp.where(outside, jnp.zeros_like(second_in), second_in)
+    second_padded = jnp.concatenate([second_cache_pad, second_in], axis=0)
+    own = upsampled[:, 1 : upsampled.shape[1] - 1]
+    return (own.astype(jnp.float32) + conv_taps(second_padded, w_second, 3)).astype(
         jnp.bfloat16
     )
 

time: 124 us -> 128 us (1.032); the launches traced: 122 us -> 128 us
  local copies, waits for them, and re-layouts: 21.4 us -> 29.6 us
  waiting for transfers between devices: 43.2 us -> 36.9 us
  matrix products: 25.8 us -> 30.6 us
    unnamed x28 -> x64, local copies, waits for them, and re-layouts: 1.43 us -> 8.78 us
    slice x6, local copies, waits for them, and re-layouts: 5.41 us -> 10.2 us  [conv_taps(): kernel = weight[time_off, row_off].reshape(3 * in_channels, out_channels)]
    dot_general x21, matrix products: 13.2 us -> 18 us  [conv_taps(): jnp.einsum('fhwc,cd->fhwd', stacked, kernel, preferred_element_type=jnp.f...]
    reshape x1, local copies, waits for them, and re-layouts: 5.03 us -> 0.71 us  [per_device(): widened = jnp.repeat(block_padded, 2, axis=2)]
    ppermute x3, waiting for transfers between devices: 9.83 us -> 6.87 us  [halo_rows(): after = lax.ppermute(first, 'ha', down)]
    ppermute x3, starting transfers between devices: 9.38 us -> 6.91 us  [halo_rows(): after = lax.ppermute(first, 'ha', down)]
    broadcast_in_dim x2 -> x1, local copies, waits for them, and re-layouts: 2.99 us -> 0.61 us  [per_device(): widened = jnp.repeat(block_padded, 2, axis=2)]
    concatenate x4 -> x2, other arithmetic: 2.54 us -> 0.42 us  [extended(): return jnp.concatenate([before, x, after], axis=dim)]
  transfers between devices with their start and end apart: 14 -> 14, of which waited for: 10 -> 7; matrix products, arithmetic and copies ran while one was open for 8% -> 38% of each run, Pallas kernels for 0% -> 0%
where the time goes in v4:
time: 128 us
  waiting for transfers between devices  36.9 us (29%)
  matrix products  30.6 us (24%)
  local copies, waits for them, and re-layouts  29.6 us (23%)
  starting transfers between devices  22.5 us (18%)
  other arithmetic  7.2 us (6%)
    ppermute x7, waiting for transfers between devices, gather_rows(): pieces.append(lax.ppermute(x, 'ha', pairs))  30 us
    dot_general x21, matrix products, conv_taps(): jnp.einsum('fhwc,cd->fhwd', stacked, kernel, preferred_element_type=jnp.f...  18 us
    slice x6, local copies, waits for them, and re-layouts, conv_taps(): kernel = weight[time_off, row_off].reshape(3 * in_channels, out_channels)  10.2 us
    unnamed x64, local copies, waits for them, and re-layouts  8.78 us
    ppermute x3, starting transfers between devices, halo_rows(): before = lax.ppermute(last, 'ha', up)  7.88 us
    ppermute x7, starting transfers between devices, gather_rows(): pieces.append(lax.ppermute(x, 'ha', pairs))  7.15 us
    ppermute x3, starting transfers between devices, halo_rows(): after = lax.ppermute(first, 'ha', down)  6.91 us
    ppermute x3, waiting for transfers between devices, halo_rows(): after = lax.ppermute(first, 'ha', down)  6.87 us
  transfers between devices with their start and end apart: 14, of which 7 were waited for; matrix products, arithmetic and copies ran while one was open for 38% of the time, Pallas kernels for 0%

profile of v4, /device:TPU:13, one launch (start us, length us, event | category | flops | bytes accessed | tf_op | source)
XLA Modules:
  0.0 127.6 jit_solution(8882333756691225059)
XLA Ops:
  0.0 1.2 collective-permute-start
  1.2 1.3 %collective-permute-start.1 = (bf16[2,1,128,384]{3,2,1,0:T(8,128)(2,1)}, bf16[2,1,128,384]{3,2,1,0:T(8,128)(2,1)S(1)}, u32[]{:S(2)}, u32[]{:S(2)}) collective-permute-start(bf16[2,1,128,384]{3,2,1,0:T(8,128)(2,1)} %param.10), channel_id=1, source_target_pairs={{0,4},{1,5},{2,6},{3,7},{4,8},{5,9},{6,10},{7,11},{8,12},{9,13},{1... | collective-permute-start | bytes 589832 | tf_op jit(solution)/shard_map/ppermute | solution.py:33
  2.5 1.0 collective-permute-start.2
  3.5 1.3 %collective-permute-start.3 = (bf16[2,1,128,384]{3,2,1,0:T(8,128)(2,1)}, bf16[2,1,128,384]{3,2,1,0:T(8,128)(2,1)S(1)}, u32[]{:S(2)}, u32[]{:S(2)}) collective-permute-start(bf16[2,1,128,384]{3,2,1,0:T(8,128)(2,1)} %param.10), channel_id=1, source_target_pairs={{0,8},{1,9},{2,10},{3,11},{4,12},{5,13},{6,14},{7,15},{8,0},{9,1},... | collective-permute-start | bytes 589832 | tf_op jit(solution)/shard_map/ppermute | solution.py:33
  4.8 1.0 collective-permute-start.4
  5.9 1.0 constant_dynamic-update-slice_fusion.7
  6.9 1.3 %collective-permute-start.5 = (bf16[2,1,128,384]{3,2,1,0:T(8,128)(2,1)}, bf16[2,1,128,384]{3,2,1,0:T(8,128)(2,1)S(1)}, u32[]{:S(2)}, u32[]{:S(2)}) collective-permute-start(bf16[2,1,128,384]{3,2,1,0:T(8,128)(2,1)} %param.10), channel_id=1, source_target_pairs={{0,12},{1,13},{2,14},{3,15},{4,0},{5,1},{6,2},{7,3},{8,4},{9,5},{1... | collective-permute-start | bytes 589832 | tf_op jit(solution)/shard_map/ppermute | solution.py:33
  8.2 1.9 %collective-permute-done.1 = bf16[2,1,128,384]{3,2,1,0:T(8,128)(2,1)S(1)} collective-permute-done((bf16[2,1,128,384]{3,2,1,0:T(8,128)(2,1)}, bf16[2,1,128,384]{3,2,1,0:T(8,128)(2,1)S(1)}, u32[]{:S(2)}, u32[]{:S(2)}) %collective-permute-start.1) | collective-permute-done | bytes 196640 | tf_op jit(solution)/shard_map/ppermute | solution.py:33
  10.2 20.2 %collective-permute-done.2 = bf16[2,1,128,384]{3,2,1,0:T(8,128)(2,1)S(1)} collective-permute-done((bf16[2,1,128,384]{3,2,1,0:T(8,128)(2,1)}, bf16[2,1,128,384]{3,2,1,0:T(8,128)(2,1)S(1)}, u32[]{:S(2)}, u32[]{:S(2)}) %collective-permute-start.2) | collective-permute-done | bytes 196640 | tf_op jit(solution)/shard_map/ppermute | solution.py:33
  30.5 4.1 %collective-permute-done.3 = bf16[2,1,128,384]{3,2,1,0:T(8,128)(2,1)S(1)} collective-permute-done((bf16[2,1,128,384]{3,2,1,0:T(8,128)(2,1)}, bf16[2,1,128,384]{3,2,1,0:T(8,128)(2,1)S(1)}, u32[]{:S(2)}, u32[]{:S(2)}) %collective-permute-start.3) | collective-permute-done | bytes 196640 | tf_op jit(solution)/shard_map/ppermute | solution.py:33
  34.8 2.7 %collective-permute-done.5 = bf16[2,1,128,384]{3,2,1,0:T(8,128)(2,1)S(1)} collective-permute-done((bf16[2,1,128,384]{3,2,1,0:T(8,128)(2,1)}, bf16[2,1,128,384]{3,2,1,0:T(8,128)(2,1)S(1)}, u32[]{:S(2)}, u32[]{:S(2)}) %collective-permute-start.5) | collective-permute-done | bytes 196640 | tf_op jit(solution)/shard_map/ppermute | solution.py:33
  37.5 1.1 collective-permute-done.6
  38.7 0.6 collective-permute-start.7
  39.2 0.8 fusion.181
  40.0 1.9 %collective-permute-start.12 = (bf16[2,1,256,192]{2,3,1,0:T(8,128)(2,1)}, bf16[2,1,256,192]{2,3,1,0:T(8,128)(2,1)}, u32[]{:S(2)}, u32[]{:S(2)}) collective-permute-start(bf16[2,1,256,192]{2,3,1,0:T(8,128)(2,1)} %get-tuple-element.83), channel_id=1, source_target_pairs={{0,1},{1,2},{2,3},{3,4},{4,5},{5,6},{6,7},{7,8},{8,9},{9,10},{10,1... | collective-permute-start | bytes 589832 | tf_op jit(solution)/shard_map/ppermute | solution.py:15
  41.9 2.4 %collective-permute-start.13 = (bf16[2,1,256,192]{2,3,1,0:T(8,128)(2,1)}, bf16[2,1,256,192]{2,3,1,0:T(8,128)(2,1)}, u32[]{:S(2)}, u32[]{:S(2)}) collective-permute-start(bf16[2,1,256,192]{2,3,1,0:T(8,128)(2,1)} %get-tuple-element.84), channel_id=1, source_target_pairs={{1,0},{2,1},{3,2},{4,3},{5,4},{6,5},{7,6},{8,7},{9,8},{10,9},{11,1... | collective-permute-start | bytes 589832 | tf_op jit(solution)/shard_map/ppermute | solution.py:16
  44.5 1.0 convolution_convert_fusion.2
  45.5 5.7 %fusion.173 = (bf16[1,1,3,384,384]{4,3,2,1,0:T(8,128)(2,1)}, bf16[1,1,3,384,384]{4,3,2,1,0:T(8,128)(2,1)}, bf16[1,1,3,384,384]{4,3,2,1,0:T(8,128)(2,1)}, bf16[1,...) fusion(bf16[3,3,3,384,384]{4,3,2,1,0:T(8,128)(2,1)} %param.17), kind=kLoop, calls=%fused_computation.268 | loop fusion | bytes 15925248 | tf_op jit(solution)/shard_map/slice | solution.py:64
  51.6 0.7 multiply_reduce_fusion
  52.3 0.7 fusion
  53.1 5.2 %fusion.184 = (f32[2,128]{1,0:T(2,128)S(1)}, f32[2,128,2048]{2,1,0:T(8,128)}) fusion(bf16[2,128,384]{2,1,0:T(8,128)(2,1)} %convolution_convert_fusion.2, bf16[2,2048,384]{2,1,0:T(8,128)(2,1)S(1)} %fusion, bf16[384,384]{1,0:T(8,128)(2,1)S(1)} %copy-done), kind=kOutput, calls=%fused_computation.279 | convolution fusion | flops 1613233920 | bytes 5735424 | tf_op jit(solution)/shard_map/fqc,fkc->fqk/dot_general | solution.py:100
  58.3 2.0 %fusion.23 = f32[2,128]{1,0:T(2,128)S(1)} fusion(f32[2,128,2048]{2,1,0:T(8,128)} %get-tuple-element.108, f32[2,128]{1,0:T(2,128)S(1)} %get-tuple-element.107), kind=kLoop, calls=%fused_computation.51 | loop fusion | flops 1048320 | bytes 2099200 | tf_op jit(solution)/shard_map/reduce_sum | solution.py:105
  60.3 4.9 %fusion.95 = bf16[2,128,384]{2,1,0:T(8,128)(2,1)} fusion(bf16[2,2048,384]{2,1,0:T(8,128)(2,1)S(1)} %fusion, f32[2,128,2048]{2,1,0:T(8,128)} %get-tuple-element.108, f32[2,128]{1,0:T(2,128)S(1)} %get-tuple-element.107, bf16[384,384]{1,0:T(8,128)(2,1)} %param.15, f32[2,128]{1,0:T(2,128)S(1)} %fusion.23), kind=kOutput, calls=%fused_computation.149 | convolution fusion | flops 1613430784 | bytes 5736448 | tf_op jit(solution)/shard_map/fqk,fkc->fqc/dot_general | solution.py:106
  65.2 1.5 %multiply_reduce_fusion.1 = (f32[2,128]{1,0:T(2,128)S(1)}, f32[2,1,128,384]{3,2,0,1:T(8,128)S(1)}) fusion(bf16[2,128,384]{2,1,0:T(8,128)(2,1)} %fusion.95, bf16[384,384]{1,0:T(8,128)(2,1)} %param.16, bf16[2,1,128,384]{3,2,1,0:T(8,128)(2,1)S(1)} %copy-done.3), kind=kOutput, calls=%fused_computation.215 | convolution fusion | flops 76087040 | bytes 1082368 | tf_op jit(solution)/shard_map/ftc,cd->ftd/dot_general | solution.py:113
  67.0 4.1 %collective-permute-start.8 = (bf16[4,1,128,384]{3,2,0,1:T(8,128)(2,1)S(1)}, bf16[4,1,128,384]{3,2,0,1:T(8,128)(2,1)S(1)}, u32[]{:S(2)}, u32[]{:S(2)}) collective-permute-start(bf16[4,1,128,384]{3,2,0,1:T(8,128)(2,1)S(1)} %pad_maximum_fusion.7), channel_id=1, source_target_pairs={{0,1},{1,2},{2,3},{3,4},{4,5},{5,6},{6,7},{7,8},{8,9},{9,10},{10,1... | collective-permute-start | bytes 1179656 | tf_op jit(solution)/shard_map/ppermute | solution.py:15
  71.0 2.1 %collective-permute-start.9 = (bf16[4,1,128,384]{3,2,0,1:T(8,128)(2,1)S(1)}, bf16[4,1,128,384]{3,2,0,1:T(8,128)(2,1)S(1)}, u32[]{:S(2)}, u32[]{:S(2)}) collective-permute-start(bf16[4,1,128,384]{3,2,0,1:T(8,128)(2,1)S(1)} %pad_maximum_fusion.7), channel_id=1, source_target_pairs={{1,0},{2,1},{3,2},{4,3},{5,4},{6,5},{7,6},{8,7},{9,8},{10,9},{11,1... | collective-permute-start | bytes 1179656 | tf_op jit(solution)/shard_map/ppermute | solution.py:16
  73.2 3.2 %fusion.174 = (bf16[1,1,3,192,192]{4,3,2,1,0:T(8,128)(2,1)}, bf16[1,1,3,192,192]{4,3,2,1,0:T(8,128)(2,1)}, bf16[1,1,3,192,192]{4,3,2,1,0:T(8,128)(2,1)}, bf16[1,...) fusion(bf16[3,3,3,192,192]{4,3,2,1,0:T(8,128)(2,1)} %param.19), kind=kLoop, calls=%fused_computation.269 | loop fusion | bytes 3981312 | tf_op jit(solution)/shard_map/slice | solution.py:64
  76.4 4.6 %collective-permute-done.9 = bf16[4,1,128,384]{3,2,0,1:T(8,128)(2,1)S(1)} collective-permute-done((bf16[4,1,128,384]{3,2,0,1:T(8,128)(2,1)S(1)}, bf16[4,1,128,384]{3,2,0,1:T(8,128)(2,1)S(1)}, u32[]{:S(2)}, u32[]{:S(2)}) %collective-permute-start.9) | collective-permute-done | bytes 393248 | tf_op jit(solution)/shard_map/ppermute | solution.py:16
  81.4 0.7 fusion.179
  83.9 0.6 copy-done.14
  85.7 0.6 copy-done.12
  90.1 1.9 %collective-permute-start.10 = (bf16[2,1,128,384]{3,2,0,1:T(8,128)(2,1)S(1)}, bf16[2,1,128,384]{3,2,0,1:T(8,128)(2,1)S(1)}, u32[]{:S(2)}, u32[]{:S(2)}) collective-permute-start(bf16[2,1,128,384]{3,2,0,1:T(8,128)(2,1)S(1)} %fusion.91), channel_id=1, source_target_pairs={{0,1},{1,2},{2,3},{3,4},{4,5},{5,6},{6,7},{7,8},{8,9},{9,10},{10,1... | collective-permute-start | bytes 589832 | tf_op jit(solution)/shard_map/ppermute | solution.py:15
  92.1 2.4 %collective-permute-start.11 = (bf16[2,1,128,384]{3,2,0,1:T(8,128)(2,1)S(1)}, bf16[2,1,128,384]{3,2,0,1:T(8,128)(2,1)S(1)}, u32[]{:S(2)}, u32[]{:S(2)}) collective-permute-start(bf16[2,1,128,384]{3,2,0,1:T(8,128)(2,1)S(1)} %fusion.91), channel_id=1, source_target_pairs={{1,0},{2,1},{3,2},{4,3},{5,4},{6,5},{7,6},{8,7},{9,8},{10,9},{11,1... | collective-permute-start | bytes 589832 | tf_op jit(solution)/shard_map/ppermute | solution.py:16
  95.0 1.1 reshape.151
  97.7 2.2 %collective-permute-done.11 = bf16[2,1,128,384]{3,2,0,1:T(8,128)(2,1)S(1)} collective-permute-done((bf16[2,1,128,384]{3,2,0,1:T(8,128)(2,1)S(1)}, bf16[2,1,128,384]{3,2,0,1:T(8,128)(2,1)S(1)}, u32[]{:S(2)}, u32[]{:S(2)}) %collective-permute-start.11) | collective-permute-done | bytes 196640 | tf_op jit(solution)/shard_map/ppermute | solution.py:16
  100.1 0.6 broadcast_in_dim.11
  100.7 0.7 reshape.135
  102.0 0.7 fusion.26
  103.3 1.9 %fusion.175 = (bf16[2,4,256,384]{3,2,1,0:T(8,128)(2,1)S(1)}, bf16[2,4,256,384]{3,2,1,0:T(8,128)(2,1)S(1)}, bf16[2,4,256,384]{3,2,1,0:T(8,128)(2,1)S(1)}, bf16[2,...) fusion(bf16[2,4,258,384]{3,2,1,0:T(8,128)(2,1)S(1)} %get-tuple-element., ...), kind=kLoop, calls=%fused_computation.270 | loop fusion | bytes 18874368 | tf_op jit(solution)/shard_map/slice | solution.py:62
  105.2 2.0 %fusion.2 = f32[2,4,256,192]{2,3,1,0:T(8,128)S(1)} fusion(bf16[2,2,258,384]{3,2,1,0:T(8,128)(2,1)S(1)} %get-tuple-element.76, bf16[2,2,258,384]{3,2,1,0:T(8,128)(2,1)S(1)} %get-tuple-element.77, bf16[2,4,256,384]{3,2,1,0:T(8,128)(2,1)S(1)} %get-tuple-element.27, bf16[2,4,256,384]{3,2,1,0:T(8,128)(2,1)S(1)} %get-tuple-element.26, ...), kind=kOutput, calls=%fused_computation.5 | convolution fusion | flops 924844032 | bytes 6746112 | tf_op jit(solution)/shard_map/fhwc,cd->fhwd/dot_general | solution.py:65
  107.2 2.3 %fusion.5 = f32[2,4,256,192]{2,3,1,0:T(8,128)S(1)} fusion(bf16[2,4,256,384]{3,2,1,0:T(8,128)(2,1)S(1)} %get-tuple-element.114, bf16[2,4,256,384]{3,2,1,0:T(8,128)(2,1)S(1)} %get-tuple-element.113, bf16[2,4,256,384]{3,2,1,0:T(8,128)(2,1)S(1)} %get-tuple-element.115, bf16[1152,192,1,1]{0,1,2,3:T(8,128)(2,1)S(1)} %reshape.150), kind=kOutput, calls=%fused_computation.7 | convolution fusion | flops 920125440 | bytes 6733824 | tf_op jit(solution)/shard_map/fhwc,cd->fhwd/dot_general | solution.py:65
  109.5 2.0 %fusion.31 = (f32[2,4,256]{2,1,0:T(4,128)S(1)}, bf16[2,4,256,192]{2,3,1,0:T(8,128)(2,1)S(1)}) fusion(bf16[1152,192,1,1]{0,1,2,3:T(8,128)(2,1)S(1)} %reshape.152, bf16[2,4,256,384]{3,2,1,0:T(8,128)(2,1)S(1)} %get-tuple-element.24, bf16[2,4,256,384]{3,2,1,0:T(8,128)(2,1)S(1)} %get-tuple-element.25, bf16[2,4,256,384]{3,2,1,0:T(8,128)(2,1)S(1)} %get-tuple-element.23, ...), kind=kOutput, calls=%fused_computation.65 | convolution fusion | flops 922482688 | bytes 9101312 | tf_op jit(solution)/shard_map/fhwc,cd->fhwd/dot_general | solution.py:65
  112.5 1.2 pad_maximum_fusion.3
  113.7 2.6 %pad_slice_fusion.1 = (bf16[2,2,256,192]{2,3,1,0:T(8,128)(2,1)S(1)}, bf16[2,2,256,192]{2,3,1,0:T(8,128)(2,1)S(1)}, bf16[2,2,256,192]{2,3,1,0:T(8,128)(2,1)S(1)},...) fusion(bf16[4,4,256,192]{2,3,1,0:T(8,128)(2,1)S(1)} %pad_maximu, ...), kind=kLoop, calls=%fused_computation.23 | loop fusion | bytes 9830400 | tf_op jit(solution)/shard_map/slice | solution.py:62
  116.6 0.9 copy-done.27
  118.4 1.5 %convolution_add_fusion.7 = f32[2,2,256,192]{2,3,1,0:T(8,128)S(1)} fusion(f32[2,2,256,192]{2,3,1,0:T(8,128)S(1)} %fusion.53, bf16[576,192,1,1]{1,0,3,2:T(8,128)(2,1)S(1)} %bitcast.195, bf16[2,2,256,192]{2,3,1,0:T(8,128)(2,1)S(1)} %copy-done.6, bf16[2,1,256,192]{2,3,1,0:T(8,128)(2,1)} %collective-permute-done.12, ...), kind=kOutput, calls=%fused_computation.77 | convolution fusion | flops 231407616 | bytes 3170304 | tf_op jit(solution)/shard_map/fhwc,cd->fhwd/dot_general | solution.py:65
  119.9 1.5 %convolution_add_fusion.6 = f32[2,2,256,192]{2,3,1,0:T(8,128)S(1)} fusion(f32[2,2,256,192]{2,3,1,0:T(8,128)S(1)} %convolution_add_fusion.7, bf16[576,192,1,1]{1,0,3,2:T(8,128)(2,1)S(1)} %bitcast.194, bf16[2,1,256,192]{2,3,1,0:T(8,128)(2,1)} %collective-permute-done.13, bf16[2,2,256,192]{2,3,1,0:T(8,128)(2,1)S(1)} %copy-done.6, ...), kind=kOutput, calls=%fused_computation.76 | convolution fusion | flops 231407616 | bytes 3170304 | tf_op jit(solution)/shard_map/fhwc,cd->fhwd/dot_general | solution.py:65
  126.3 1.3 %fusion.39 = bf16[2,2,256,192]{2,3,1,0:T(8,128)(2,1)} fusion(f32[2,2,256,192]{2,3,1,0:T(8,128)S(1)} %convolution_add_fusion.1, bf16[576,192,1,1]{1,0,3,2:T(8,128)(2,1)S(1)} %bitcast.188, bf16[2,2,256,192]{2,3,1,0:T(8,128)(2,1)S(1)} %get-tuple-element.47, bf16[2,2,256,192]{2,3,1,0:T(8,128)(2,1)S(1)} %get-tuple-element.78, ...), kind=kOutput, calls=%fused_computation.83 | convolution fusion | flops 230817792 | bytes 2973696 | tf_op jit(solution)/shard_map/fhwc,cd->fhwd/dot_general | solution.py:65
  (111 shorter events, 18.6 us)
Async XLA Ops:
  0.0 53.1 %copy-start = (bf16[384,384]{1,0:T(8,128)(2,1)S(1)}, bf16[384,384]{1,0:T(8,128)(2,1)}, u32[]{:S(2)}) copy-start(bf16[384,384]{1,0:T(8,128)(2,1)} %param.14) | copy-start | bytes 884740
  0.0 6.9 %collective-permute-start = (bf16[2,1,128,384]{3,2,1,0:T(8,128)(2,1)}, bf16[2,1,128,384]{3,2,1,0:T(8,128)(2,1)S(1)}, u32[]{:S(2)}, u32[]{:S(2)}) collective-permute-start(bf16[2,1,128,384]{3,2,1,0:T(8,128)(2,1)} %param.10), channel_id=1, source_target_pairs={{0,2},{1,3},{2,4},{3,5},{4,6},{5,7},{6,8},{7,9},{8,10},{9,11},{10,... | collective-permute-start | bytes 589832 | tf_op jit(solution)/shard_map/ppermute | solution.py:33
  1.2 8.9 %collective-permute-start.1 = (bf16[2,1,128,384]{3,2,1,0:T(8,128)(2,1)}, bf16[2,1,128,384]{3,2,1,0:T(8,128)(2,1)S(1)}, u32[]{:S(2)}, u32[]{:S(2)}) collective-permute-start(bf16[2,1,128,384]{3,2,1,0:T(8,128)(2,1)} %param.10), channel_id=1, source_target_pairs={{0,4},{1,5},{2,6},{3,7},{4,8},{5,9},{6,10},{7,11},{8,12},{9,13},{1... | collective-permute-start | bytes 589832 | tf_op jit(solution)/shard_map/ppermute | solution.py:33
  2.5 27.9 %collective-permute-start.2 = (bf16[2,1,128,384]{3,2,1,0:T(8,128)(2,1)}, bf16[2,1,128,384]{3,2,1,0:T(8,128)(2,1)S(1)}, u32[]{:S(2)}, u32[]{:S(2)}) collective-permute-start(bf16[2,1,128,384]{3,2,1,0:T(8,128)(2,1)} %param.10), channel_id=1, source_target_pairs={{0,6},{1,7},{2,8},{3,9},{4,10},{5,11},{6,12},{7,13},{8,14},{9,15},... | collective-permute-start | bytes 589832 | tf_op jit(solution)/shard_map/ppermute | solution.py:33
  3.5 31.1 %collective-permute-start.3 = (bf16[2,1,128,384]{3,2,1,0:T(8,128)(2,1)}, bf16[2,1,128,384]{3,2,1,0:T(8,128)(2,1)S(1)}, u32[]{:S(2)}, u32[]{:S(2)}) collective-permute-start(bf16[2,1,128,384]{3,2,1,0:T(8,128)(2,1)} %param.10), channel_id=1, source_target_pairs={{0,8},{1,9},{2,10},{3,11},{4,12},{5,13},{6,14},{7,15},{8,0},{9,1},... | collective-permute-start | bytes 589832 | tf_op jit(solution)/shard_map/ppermute | solution.py:33
  4.8 29.8 %collective-permute-start.4 = (bf16[2,1,128,384]{3,2,1,0:T(8,128)(2,1)}, bf16[2,1,128,384]{3,2,1,0:T(8,128)(2,1)S(1)}, u32[]{:S(2)}, u32[]{:S(2)}) collective-permute-start(bf16[2,1,128,384]{3,2,1,0:T(8,128)(2,1)} %param.10), channel_id=1, source_target_pairs={{0,10},{1,11},{2,12},{3,13},{4,14},{5,15},{6,0},{7,1},{8,2},{9,3},... | collective-permute-start | bytes 589832 | tf_op jit(solution)/shard_map/ppermute | solution.py:33
  6.9 30.6 %collective-permute-start.5 = (bf16[2,1,128,384]{3,2,1,0:T(8,128)(2,1)}, bf16[2,1,128,384]{3,2,1,0:T(8,128)(2,1)S(1)}, u32[]{:S(2)}, u32[]{:S(2)}) collective-permute-start(bf16[2,1,128,384]{3,2,1,0:T(8,128)(2,1)} %param.10), channel_id=1, source_target_pairs={{0,12},{1,13},{2,14},{3,15},{4,0},{5,1},{6,2},{7,3},{8,4},{9,5},{1... | collective-permute-start | bytes 589832 | tf_op jit(solution)/shard_map/ppermute | solution.py:33
  10.1 28.5 %collective-permute-start.6 = (bf16[2,1,128,384]{3,2,1,0:T(8,128)(2,1)}, bf16[2,1,128,384]{3,2,1,0:T(8,128)(2,1)S(1)}, u32[]{:S(2)}, u32[]{:S(2)}) collective-permute-start(bf16[2,1,128,384]{3,2,1,0:T(8,128)(2,1)} %param.10), channel_id=1, source_target_pairs={{0,14},{1,15},{2,0},{3,1},{4,2},{5,3},{6,4},{7,5},{8,6},{9,7},{10,... | collective-permute-start | bytes 589832 | tf_op jit(solution)/shard_map/ppermute | solution.py:33
  10.2 29.0 %copy-start.5 = (bf16[2,2,256,192]{2,3,1,0:T(8,128)(2,1)S(1)}, bf16[2,2,256,192]{2,3,1,0:T(8,128)(2,1)}, u32[]{:S(2)}) copy-start(bf16[2,2,256,192]{2,3,1,0:T(8,128)(2,1)} %param.12) | copy-start | bytes 1179652
  34.6 9.7 %copy-start.2 = (bf16[2,1,128,384]{3,2,1,0:T(8,128)(2,1)S(1)}, bf16[2,1,128,384]{3,2,1,0:T(8,128)(2,1)}, u32[]{:S(2)}) copy-start(bf16[2,1,128,384]{3,2,1,0:T(8,128)(2,1)} %param.10) | copy-start | bytes 589828
  34.6 9.9 %copy-start.18 = (bf16[384,384]{1,0:T(8,128)(2,1)S(1)}, bf16[384,384]{1,0:T(8,128)(2,1)}, u32[]{:S(2)}) copy-start(bf16[384,384]{1,0:T(8,128)(2,1)} %param.13) | copy-start | bytes 884740
  38.7 12.6 %collective-permute-start.7 = (bf16[2,8,128,384]{3,2,1,0:T(8,128)(2,1)S(1)}, bf16[2,8,128,384]{3,2,1,0:T(8,128)(2,1)S(1)}, u32[]{:S(2)}, u32[]{:S(2)}) collective-permute-start(bf16[2,8,128,384]{3,2,1,0:T(8,128)(2,1)S(1)} %get-tuple-element.91), channel_id=1, source_target_pairs={{0,1},{1,0},{2,3},{3,2},{4,5},{5,4},{6,7},{7,6},{8,9},{9,8},{10,11... | collective-permute-start | bytes 4718600 | tf_op jit(solution)/shard_map/ppermute | solution.py:36
  40.0 72.0 %collective-permute-start.12 = (bf16[2,1,256,192]{2,3,1,0:T(8,128)(2,1)}, bf16[2,1,256,192]{2,3,1,0:T(8,128)(2,1)}, u32[]{:S(2)}, u32[]{:S(2)}) collective-permute-start(bf16[2,1,256,192]{2,3,1,0:T(8,128)(2,1)} %get-tuple-element.83), channel_id=1, source_target_pairs={{0,1},{1,2},{2,3},{3,4},{4,5},{5,6},{6,7},{7,8},{8,9},{9,10},{10,1... | collective-permute-start | bytes 589832 | tf_op jit(solution)/shard_map/ppermute | solution.py:15
  41.9 70.1 %collective-permute-start.13 = (bf16[2,1,256,192]{2,3,1,0:T(8,128)(2,1)}, bf16[2,1,256,192]{2,3,1,0:T(8,128)(2,1)}, u32[]{:S(2)}, u32[]{:S(2)}) collective-permute-start(bf16[2,1,256,192]{2,3,1,0:T(8,128)(2,1)} %get-tuple-element.84), channel_id=1, source_target_pairs={{1,0},{2,1},{3,2},{4,3},{5,4},{6,5},{7,6},{8,7},{9,8},{10,9},{11,1... | collective-permute-start | bytes 589832 | tf_op jit(solution)/shard_map/ppermute | solution.py:16
  60.3 5.0 %copy-start.3 = (bf16[2,1,128,384]{3,2,1,0:T(8,128)(2,1)S(1)}, bf16[2,1,128,384]{3,2,1,0:T(8,128)(2,1)}, u32[]{:S(2)}) copy-start(bf16[2,1,128,384]{3,2,1,0:T(8,128)(2,1)} %param.10) | copy-start | bytes 589828
  65.2 1.7 %copy-start.4 = (bf16[2,1,128,384]{3,2,1,0:T(8,128)(2,1)S(1)}, bf16[2,1,128,384]{3,2,1,0:T(8,128)(2,1)}, u32[]{:S(2)}) copy-start(bf16[2,1,128,384]{3,2,1,0:T(8,128)(2,1)} %param.11) | copy-start | bytes 589828
  67.0 9.4 %collective-permute-start.8 = (bf16[4,1,128,384]{3,2,0,1:T(8,128)(2,1)S(1)}, bf16[4,1,128,384]{3,2,0,1:T(8,128)(2,1)S(1)}, u32[]{:S(2)}, u32[]{:S(2)}) collective-permute-start(bf16[4,1,128,384]{3,2,0,1:T(8,128)(2,1)S(1)} %pad_maximum_fusion.7), channel_id=1, source_target_pairs={{0,1},{1,2},{2,3},{3,4},{4,5},{5,6},{6,7},{7,8},{8,9},{9,10},{10,1... | collective-permute-start | bytes 1179656 | tf_op jit(solution)/shard_map/ppermute | solution.py:15
  71.0 10.0 %collective-permute-start.9 = (bf16[4,1,128,384]{3,2,0,1:T(8,128)(2,1)S(1)}, bf16[4,1,128,384]{3,2,0,1:T(8,128)(2,1)S(1)}, u32[]{:S(2)}, u32[]{:S(2)}) collective-permute-start(bf16[4,1,128,384]{3,2,0,1:T(8,128)(2,1)S(1)} %pad_maximum_fusion.7), channel_id=1, source_target_pairs={{1,0},{2,1},{3,2},{4,3},{5,4},{6,5},{7,6},{8,7},{9,8},{10,9},{11,1... | collective-permute-start | bytes 1179656 | tf_op jit(solution)/shard_map/ppermute | solution.py:16
  81.4 1.2 copy-start.16
  82.1 1.2 copy-start.15
  83.4 1.2 copy-start.14
  83.9 1.2 copy-start.13
  85.0 1.2 copy-start.12
  85.6 1.2 copy-start.11
  86.7 1.2 copy-start.10
  87.4 1.2 copy-start.9
  88.4 1.2 copy-start.8
  89.1 5.4 %copy-start.7 = (bf16[3,3,384,192]{2,3,1,0:T(8,128)(2,1)S(1)}, bf16[3,3,384,192]{2,3,1,0:T(8,128)(2,1)}, u32[]{:S(2)}) copy-start(bf16[3,3,384,192]{2,3,1,0:T(8,128)(2,1)} %param.18) | copy-start | bytes 3981316
  90.1 7.6 %collective-permute-start.10 = (bf16[2,1,128,384]{3,2,0,1:T(8,128)(2,1)S(1)}, bf16[2,1,128,384]{3,2,0,1:T(8,128)(2,1)S(1)}, u32[]{:S(2)}, u32[]{:S(2)}) collective-permute-start(bf16[2,1,128,384]{3,2,0,1:T(8,128)(2,1)S(1)} %fusion.91), channel_id=1, source_target_pairs={{0,1},{1,2},{2,3},{3,4},{4,5},{5,6},{6,7},{7,8},{8,9},{9,10},{10,1... | collective-permute-start | bytes 589832 | tf_op jit(solution)/shard_map/ppermute | solution.py:15
  92.1 7.9 %collective-permute-start.11 = (bf16[2,1,128,384]{3,2,0,1:T(8,128)(2,1)S(1)}, bf16[2,1,128,384]{3,2,0,1:T(8,128)(2,1)S(1)}, u32[]{:S(2)}, u32[]{:S(2)}) collective-permute-start(bf16[2,1,128,384]{3,2,0,1:T(8,128)(2,1)S(1)} %fusion.91), channel_id=1, source_target_pairs={{1,0},{2,1},{3,2},{4,3},{5,4},{6,5},{7,6},{8,7},{9,8},{10,9},{11,1... | collective-permute-start | bytes 589832 | tf_op jit(solution)/shard_map/ppermute | solution.py:16
  103.3 2.0 %copy-start.17 = (bf16[1152,192,1,1]{0,1,2,3:T(8,128)(2,1)S(1)}, bf16[1152,192,1,1]{0,1,2,3:T(8,128)(2,1)}, u32[]{:S(2)}) copy-start(bf16[1152,192,1,1]{0,1,2,3:T(8,128)(2,1)} %reshape.151) | copy-start | bytes 1327108
  111.5 1.0 copy-start.6
  116.5 1.0 copy-start.27
  117.5 1.0 copy-start.26
  118.4 1.5 %copy-start.25 = (bf16[1,1,3,192,192]{4,3,2,1,0:T(8,128)(2,1)S(1)}, bf16[1,1,3,192,192]{4,3,2,1,0:T(8,128)(2,1)}, u32[]{:S(2)}) copy-start(bf16[1,1,3,192,192]{4,3,2,1,0:T(8,128)(2,1)} %get-tuple-element.19) | copy-start | bytes 663556
  119.9 1.5 %copy-start.24 = (bf16[1,1,3,192,192]{4,3,2,1,0:T(8,128)(2,1)S(1)}, bf16[1,1,3,192,192]{4,3,2,1,0:T(8,128)(2,1)}, u32[]{:S(2)}) copy-start(bf16[1,1,3,192,192]{4,3,2,1,0:T(8,128)(2,1)} %get-tuple-element.18) | copy-start | bytes 663556
  121.4 1.0 copy-start.23
  122.4 1.0 copy-start.22
  123.4 1.0 copy-start.21
  124.3 1.0 copy-start.20
  125.3 1.0 copy-start.19
  125.8 1.8 %copy-start.1 = (bf16[384,384]{1,0:T(8,128)(2,1)S(1)}, bf16[384,384]{1,0:T(8,128)(2,1)}, u32[]{:S(2)}) copy-start(bf16[384,384]{1,0:T(8,128)(2,1)} %param.14) | copy-start | bytes 884740

commit v5 on v1

--- a/solution.py
+++ b/solution.py
@@ -90,6 +90,7 @@
     queries = project_rows(normed_tokens, w_query)
     keys_all = project_rows(all_tokens, w_key)
     values_all = project_rows(all_tokens, w_value)
+    keys_all, values_all = lax.optimization_barrier((keys_all, values_all))
     score_scale = 1.0 / math.sqrt(channels)
     scores = (
         jnp.einsum("fqc,fkc->fqk", queries, keys_all, preferred_element_type=jnp.float32)

time: 124 us -> 124 us (level)
    dot_general x1 -> x0, matrix products: 4.95 us -> none  [per_device(): jnp.einsum('fqk,fkc->fqc', weights.astype(jnp.bfloat16), values_all, pref...]
    dot_general x1 -> x2, matrix products: 1.01 us -> 5.81 us  [project_rows(): jnp.einsum('ftc,cd->ftd', tokens, weight, preferred_element_type=jnp.floa...]
    dot_general x1, matrix products: 1.44 us -> 3.64 us  [per_device(): jnp.einsum('ftc,cd->ftd', attended, w_output, preferred_element_type=jnp....]
    dot_general x1, matrix products: 5.21 us -> 3.68 us  [per_device(): jnp.einsum('fqc,fkc->fqk', queries, keys_all, preferred_element_type=jnp....]
  transfers between devices with their start and end apart: 14 -> 14, of which waited for: 10 -> 10; matrix products, arithmetic and copies ran while one was open for 8% -> 7% of each run, Pallas kernels for 0% -> 0%
where the time goes in v5:
time: 124 us; the launch traced here: 122 us
  waiting for transfers between devices  44.4 us (36%)
  matrix products  26.3 us (21%)
  starting transfers between devices  22.9 us (18%)
  local copies, waits for them, and re-layouts  21.4 us (17%)
  other arithmetic  6.69 us (5%)
    ppermute x7, waiting for transfers between devices, gather_rows(): pieces.append(lax.ppermute(x, 'ha', pairs))  30 us
    dot_general x21, matrix products, conv_taps(): jnp.einsum('fhwc,cd->fhwd', stacked, kernel, preferred_element_type=jnp.f...  13.2 us
    ppermute x3, waiting for transfers between devices, halo_rows(): after = lax.ppermute(first, 'ha', down)  9.9 us
    ppermute x3, starting transfers between devices, halo_rows(): after = lax.ppermute(first, 'ha', down)  9.27 us
    ppermute x7, starting transfers between devices, gather_rows(): pieces.append(lax.ppermute(x, 'ha', pairs))  7.16 us
    ppermute x3, starting transfers between devices, halo_rows(): before = lax.ppermute(last, 'ha', up)  5.92 us
    dot_general x2, matrix products, project_rows(): jnp.einsum('ftc,cd->ftd', tokens, weight, preferred_element_type=jnp.floa...  5.81 us
    slice x6, local copies, waits for them, and re-layouts, conv_taps(): kernel = weight[time_off, row_off].reshape(3 * in_channels, out_channels)  5.41 us
  transfers between devices with their start and end apart: 14, of which 10 were waited for; matrix products, arithmetic and copies ran while one was open for 7% of the time, Pallas kernels for 0%

profile of v5, /device:TPU:13, one launch (start us, length us, event | category | flops | bytes accessed | tf_op | source)
XLA Modules:
  0.0 122.4 jit_solution(1381273456073024190)
XLA Ops:
  0.0 1.2 %collective-permute-start = (bf16[2,1,128,384]{3,2,1,0:T(8,128)(2,1)}, bf16[2,1,128,384]{3,2,1,0:T(8,128)(2,1)S(1)}, u32[]{:S(2)}, u32[]{:S(2)}) collective-permute-start(bf16[2,1,128,384]{3,2,1,0:T(8,128)(2,1)} %param.10), channel_id=1, source_target_pairs={{0,2},{1,3},{2,4},{3,5},{4,6},{5,7},{6,8},{7,9},{8,10},{9,11},{10,... | collective-permute-start | bytes 589832 | tf_op jit(solution)/shard_map/ppermute | solution.py:33
  1.2 1.3 %collective-permute-start.1 = (bf16[2,1,128,384]{3,2,1,0:T(8,128)(2,1)}, bf16[2,1,128,384]{3,2,1,0:T(8,128)(2,1)S(1)}, u32[]{:S(2)}, u32[]{:S(2)}) collective-permute-start(bf16[2,1,128,384]{3,2,1,0:T(8,128)(2,1)} %param.10), channel_id=1, source_target_pairs={{0,4},{1,5},{2,6},{3,7},{4,8},{5,9},{6,10},{7,11},{8,12},{9,13},{1... | collective-permute-start | bytes 589832 | tf_op jit(solution)/shard_map/ppermute | solution.py:33
  2.5 1.0 collective-permute-start.2
  3.5 1.3 %collective-permute-start.3 = (bf16[2,1,128,384]{3,2,1,0:T(8,128)(2,1)}, bf16[2,1,128,384]{3,2,1,0:T(8,128)(2,1)S(1)}, u32[]{:S(2)}, u32[]{:S(2)}) collective-permute-start(bf16[2,1,128,384]{3,2,1,0:T(8,128)(2,1)} %param.10), channel_id=1, source_target_pairs={{0,8},{1,9},{2,10},{3,11},{4,12},{5,13},{6,14},{7,15},{8,0},{9,1},... | collective-permute-start | bytes 589832 | tf_op jit(solution)/shard_map/ppermute | solution.py:33
  4.9 1.0 collective-permute-start.4
  5.9 1.0 constant_dynamic-update-slice_fusion.7
  6.9 1.3 %collective-permute-start.5 = (bf16[2,1,128,384]{3,2,1,0:T(8,128)(2,1)}, bf16[2,1,128,384]{3,2,1,0:T(8,128)(2,1)S(1)}, u32[]{:S(2)}, u32[]{:S(2)}) collective-permute-start(bf16[2,1,128,384]{3,2,1,0:T(8,128)(2,1)} %param.10), channel_id=1, source_target_pairs={{0,12},{1,13},{2,14},{3,15},{4,0},{5,1},{6,2},{7,3},{8,4},{9,5},{1... | collective-permute-start | bytes 589832 | tf_op jit(solution)/shard_map/ppermute | solution.py:33
  8.2 1.9 %collective-permute-done.1 = bf16[2,1,128,384]{3,2,1,0:T(8,128)(2,1)S(1)} collective-permute-done((bf16[2,1,128,384]{3,2,1,0:T(8,128)(2,1)}, bf16[2,1,128,384]{3,2,1,0:T(8,128)(2,1)S(1)}, u32[]{:S(2)}, u32[]{:S(2)}) %collective-permute-start.1) | collective-permute-done | bytes 196640 | tf_op jit(solution)/shard_map/ppermute | solution.py:33
  10.2 20.2 %collective-permute-done.2 = bf16[2,1,128,384]{3,2,1,0:T(8,128)(2,1)S(1)} collective-permute-done((bf16[2,1,128,384]{3,2,1,0:T(8,128)(2,1)}, bf16[2,1,128,384]{3,2,1,0:T(8,128)(2,1)S(1)}, u32[]{:S(2)}, u32[]{:S(2)}) %collective-permute-start.2) | collective-permute-done | bytes 196640 | tf_op jit(solution)/shard_map/ppermute | solution.py:33
  30.5 4.1 %collective-permute-done.3 = bf16[2,1,128,384]{3,2,1,0:T(8,128)(2,1)S(1)} collective-permute-done((bf16[2,1,128,384]{3,2,1,0:T(8,128)(2,1)}, bf16[2,1,128,384]{3,2,1,0:T(8,128)(2,1)S(1)}, u32[]{:S(2)}, u32[]{:S(2)}) %collective-permute-start.3) | collective-permute-done | bytes 196640 | tf_op jit(solution)/shard_map/ppermute | solution.py:33
  34.8 2.7 %collective-permute-done.5 = bf16[2,1,128,384]{3,2,1,0:T(8,128)(2,1)S(1)} collective-permute-done((bf16[2,1,128,384]{3,2,1,0:T(8,128)(2,1)}, bf16[2,1,128,384]{3,2,1,0:T(8,128)(2,1)S(1)}, u32[]{:S(2)}, u32[]{:S(2)}) %collective-permute-start.5) | collective-permute-done | bytes 196640 | tf_op jit(solution)/shard_map/ppermute | solution.py:33
  37.6 1.0 collective-permute-done.6
  38.7 0.6 collective-permute-start.7
  39.4 2.9 %collective-permute-done.7 = bf16[2,8,128,384]{3,2,1,0:T(8,128)(2,1)S(1)} collective-permute-done((bf16[2,8,128,384]{3,2,1,0:T(8,128)(2,1)S(1)}, bf16[2,8,128,384]{3,2,1,0:T(8,128)(2,1)S(1)}, u32[]{:S(2)}, u32[]{:S(2)}) %collective-permute-start.7) | collective-permute-done | bytes 1572896 | tf_op jit(solution)/shard_map/ppermute | solution.py:36
  42.6 0.7 multiply_reduce_fusion
  43.3 0.7 fusion
  44.1 3.7 %convolution_convert_fusion = bf16[2,2048,384]{2,1,0:T(8,128)(2,1)} fusion(bf16[2,2048,384]{2,1,0:T(8,128)(2,1)S(1)} %fusion, bf16[384,384]{1,0:T(8,128)(2,1)S(1)} %copy-done), kind=kOutput, calls=%fused_computation.8 | convolution fusion | flops 1209532416 | bytes 6586368 | tf_op jit(solution)/shard_map/ftc,cd->ftd/dot_general | solution.py:67
  47.8 2.1 %convolution_convert_fusion.1 = bf16[2,2048,384]{2,1,0:T(8,128)(2,1)S(1)} fusion(bf16[2,2048,384]{2,1,0:T(8,128)(2,1)S(1)} %fusion, bf16[384,384]{1,0:T(8,128)(2,1)S(1)} %copy-done.9), kind=kOutput, calls=%fused_computation.9 | convolution fusion | flops 1209532416 | bytes 6586368 | tf_op jit(solution)/shard_map/ftc,cd->ftd/dot_general | solution.py:67
  49.9 3.7 %fusion.190 = (f32[2,128]{1,0:T(2,128)S(1)}, f32[2,128,2048]{2,1,0:T(8,128)}) fusion(bf16[2,2048,384]{2,1,0:T(8,128)(2,1)S(1)} %convolution_convert_fusion.1, bf16[384,384]{1,0:T(8,128)(2,1)} %param.13, bf16[2,1,128,384]{3,2,1,0:T(8,128)(2,1)S(1)} %copy-done.6, f32[2,128]{1,0:T(2,128)S(1)} %add_rsqrt_fusion.2), kind=kOutput, calls=%fused_computation.260 | convolution fusion | flops 479592192 | bytes 5736448 | tf_op jit(solution)/shard_map/fqc,fkc->fqk/dot_general | solution.py:96
  53.6 2.0 %fusion.24 = f32[2,128]{1,0:T(2,128)S(1)} fusion(f32[2,128,2048]{2,1,0:T(8,128)} %get-tuple-element.108, f32[2,128]{1,0:T(2,128)S(1)} %get-tuple-element.107), kind=kLoop, calls=%fused_computation.36 | loop fusion | flops 1048320 | bytes 2099200 | tf_op jit(solution)/shard_map/reduce_sum | solution.py:101
  55.6 3.6 %multiply_reduce_fusion.2 = (f32[2,128]{1,0:T(2,128)S(1)}, f32[2,1,128,384]{3,2,0,1:T(8,128)S(1)}) fusion(bf16[384,384]{1,0:T(8,128)(2,1)} %param.16, bf16[2,2048,384]{2,1,0:T(8,128)(2,1)} %convolution_convert_fusion, f32[2,128,2048]{2,1,0:T(8,128)} %get-tuple-element.108, f32[2,128]{1,0:T(2,128)S(1)} %get-tuple-element.107, f32[2,128]{1,0:T(2,128)S(1)} %fusion.24, ...), kind=kOutput, calls=%fused_computation.197 | convolution fusion | flops 479985408 | bytes 6130688 | tf_op jit(solution)/shard_map/ftc,cd->ftd/dot_general | solution.py:109
  59.5 1.9 %collective-permute-start.8 = (bf16[4,1,128,384]{3,2,0,1:T(8,128)(2,1)S(1)}, bf16[4,1,128,384]{3,2,0,1:T(8,128)(2,1)S(1)}, u32[]{:S(2)}, u32[]{:S(2)}) collective-permute-start(bf16[4,1,128,384]{3,2,0,1:T(8,128)(2,1)S(1)} %pad_maximum_fusion.3), channel_id=1, source_target_pairs={{0,1},{1,2},{2,3},{3,4},{4,5},{5,6},{6,7},{7,8},{8,9},{9,10},{10,1... | collective-permute-start | bytes 1179656 | tf_op jit(solution)/shard_map/ppermute | solution.py:15
  61.5 2.6 %collective-permute-start.9 = (bf16[4,1,128,384]{3,2,0,1:T(8,128)(2,1)S(1)}, bf16[4,1,128,384]{3,2,0,1:T(8,128)(2,1)S(1)}, u32[]{:S(2)}, u32[]{:S(2)}) collective-permute-start(bf16[4,1,128,384]{3,2,0,1:T(8,128)(2,1)S(1)} %pad_maximum_fusion.3), channel_id=1, source_target_pairs={{1,0},{2,1},{3,2},{4,3},{5,4},{6,5},{7,6},{8,7},{9,8},{10,9},{11,1... | collective-permute-start | bytes 1179656 | tf_op jit(solution)/shard_map/ppermute | solution.py:16
  64.0 3.9 %fusion.180 = (bf16[1,1,3,384,384]{4,3,2,1,0:T(8,128)(2,1)S(1)}, bf16[1,1,3,384,384]{4,3,2,1,0:T(8,128)(2,1)S(1)}, bf16[1,1,3,384,384]{4,3,2,1,0:T(8,128)(2,1)S(...) fusion(bf16[3,3,3,384,384]{4,3,2,1,0:T(8,128)(2,1)} %param.17), kind=kLoop, calls=%fused_computation.250 | loop fusion | bytes 15925248 | tf_op jit(solution)/shard_map/slice | solution.py:59
  68.0 3.5 %collective-permute-done.9 = bf16[4,1,128,384]{3,2,0,1:T(8,128)(2,1)S(1)} collective-permute-done((bf16[4,1,128,384]{3,2,0,1:T(8,128)(2,1)S(1)}, bf16[4,1,128,384]{3,2,0,1:T(8,128)(2,1)S(1)}, u32[]{:S(2)}, u32[]{:S(2)}) %collective-permute-start.9) | collective-permute-done | bytes 393248 | tf_op jit(solution)/shard_map/ppermute | solution.py:16
  71.9 0.7 fusion.185
  77.1 1.9 %collective-permute-start.10 = (bf16[2,1,128,384]{3,2,0,1:T(8,128)(2,1)S(1)}, bf16[2,1,128,384]{3,2,0,1:T(8,128)(2,1)S(1)}, u32[]{:S(2)}, u32[]{:S(2)}) collective-permute-start(bf16[2,1,128,384]{3,2,0,1:T(8,128)(2,1)S(1)} %fusion.93), channel_id=1, source_target_pairs={{0,1},{1,2},{2,3},{3,4},{4,5},{5,6},{6,7},{7,8},{8,9},{9,10},{10,1... | collective-permute-start | bytes 589832 | tf_op jit(solution)/shard_map/ppermute | solution.py:15
  79.0 3.7 %collective-permute-start.11 = (bf16[2,1,128,384]{3,2,0,1:T(8,128)(2,1)S(1)}, bf16[2,1,128,384]{3,2,0,1:T(8,128)(2,1)S(1)}, u32[]{:S(2)}, u32[]{:S(2)}) collective-permute-start(bf16[2,1,128,384]{3,2,0,1:T(8,128)(2,1)S(1)} %fusion.93), channel_id=1, source_target_pairs={{1,0},{2,1},{3,2},{4,3},{5,4},{6,5},{7,6},{8,7},{9,8},{10,9},{11,1... | collective-permute-start | bytes 589832 | tf_op jit(solution)/shard_map/ppermute | solution.py:16
  83.3 1.1 reshape.139
  86.0 1.0 collective-permute-done.11
  87.3 2.9 %broadcast_in_dim.7 = bf16[2,6,128,2,384]{4,3,2,1,0:T(2,128)(2,1)} broadcast(bf16[2,6,128,384]{3,2,1,0:T(8,128)(2,1)S(1)} %bitcast.180), dimensions={0,1,2,4} | broadcast | bytes 3538944 | tf_op jit(solution)/shard_map/broadcast_in_dim | solution.py:121
  90.1 5.0 %reshape.124 = bf16[2,6,256,384]{3,2,1,0:T(8,128)(2,1)S(1)} reshape(bf16[2,6,128,2,384]{4,3,2,1,0:T(2,128)(2,1)} %broadcast_in_dim.7) | data formatting | bytes 4718592 | tf_op jit(solution)/shard_map/reshape | solution.py:121
  95.4 1.3 %pad_slice_fusion.5 = (bf16[2,2,256,384]{3,2,1,0:T(8,128)(2,1)S(1)}, bf16[2,2,256,384]{3,2,1,0:T(8,128)(2,1)S(1)}, bf16[2,2,256,384]{3,2,1,0:T(8,128)(2,1)S(1)},...) fusion(bf16[2,4,256,384]{3,2,1,0:T(8,128)(2,1)S(1)} %slice.488,, ...), kind=kLoop, calls=%fused_computation.132 | loop fusion | bytes 11010048 | tf_op jit(solution)/shard_map/slice | solution.py:57
  96.7 1.1 fusion.6
  97.8 1.1 fusion.30
  99.0 1.2 multiply_reduce_fusion.1
  100.5 2.1 %collective-permute-start.12 = (bf16[4,1,256,192]{2,3,1,0:T(8,128)(2,1)S(1)}, bf16[4,1,256,192]{2,3,1,0:T(8,128)(2,1)S(1)}, u32[]{:S(2)}, u32[]{:S(2)}) collective-permute-start(bf16[4,1,256,192]{2,3,1,0:T(8,128)(2,1)S(1)} %get-tuple-element.83), channel_id=1, source_target_pairs={{0,1},{1,2},{2,3},{3,4},{4,5},{5,6},{6,7},{7,8},{8,9},{9,10},{10,1... | collective-permute-start | bytes 1179656 | tf_op jit(solution)/shard_map/ppermute | solution.py:15
  102.6 2.9 %collective-permute-start.13 = (bf16[4,1,256,192]{2,3,1,0:T(8,128)(2,1)S(1)}, bf16[4,1,256,192]{2,3,1,0:T(8,128)(2,1)S(1)}, u32[]{:S(2)}, u32[]{:S(2)}) collective-permute-start(bf16[4,1,256,192]{2,3,1,0:T(8,128)(2,1)S(1)} %get-tuple-element.84), channel_id=1, source_target_pairs={{1,0},{2,1},{3,2},{4,3},{5,4},{6,5},{7,6},{8,7},{9,8},{10,9},{11,1... | collective-permute-start | bytes 1179656 | tf_op jit(solution)/shard_map/ppermute | solution.py:16
  105.8 1.6 %collective-permute-done.12 = bf16[4,1,256,192]{2,3,1,0:T(8,128)(2,1)S(1)} collective-permute-done((bf16[4,1,256,192]{2,3,1,0:T(8,128)(2,1)S(1)}, bf16[4,1,256,192]{2,3,1,0:T(8,128)(2,1)S(1)}, u32[]{:S(2)}, u32[]{:S(2)}) %collective-permute-start.12) | collective-permute-done | bytes 393248 | tf_op jit(solution)/shard_map/ppermute | solution.py:15
  107.3 5.4 %collective-permute-done.13 = bf16[4,1,256,192]{2,3,1,0:T(8,128)(2,1)S(1)} collective-permute-done((bf16[4,1,256,192]{2,3,1,0:T(8,128)(2,1)S(1)}, bf16[4,1,256,192]{2,3,1,0:T(8,128)(2,1)S(1)}, u32[]{:S(2)}, u32[]{:S(2)}) %collective-permute-start.13) | collective-permute-done | bytes 393248 | tf_op jit(solution)/shard_map/ppermute | solution.py:16
  113.0 2.0 %select_maximum_fusion = bf16[4,4,258,192]{2,3,1,0:T(8,128)(2,1)S(1)} fusion(bf16[4,1,256,192]{2,3,1,0:T(8,128)(2,1)S(1)} %collective-permute-done.13, bf16[4,1,256,192]{2,3,1,0:T(8,128)(2,1)S(1)} %collective-permute-done.12, bf16[2,2,256,192]{2,3,1,0:T(8,128)(2,1)S(1)} %multiply_convert_fusion, bf16[2,2,256,192]{2,3,1,0:T(8,128)(2,1)S(1)} %copy-done.2), kind=kLoop, calls=%fused_computation.12 | loop fusion | flops 11888640 | bytes 3158016 | tf_op jit(solution)/shard_map/concatenate | solution.py:22
  115.0 1.7 %fusion.182 = (bf16[2,2,256,192]{2,3,1,0:T(8,128)(2,1)S(1)}, bf16[2,2,256,192]{2,3,1,0:T(8,128)(2,1)S(1)}, bf16[2,2,256,192]{2,3,1,0:T(8,128)(2,1)S(1)}, bf16[2,...) fusion(bf16[4,4,258,192]{2,3,1,0:T(8,128)(2,1)S(1)} %select_max, ...), kind=kLoop, calls=%fused_computation.252 | loop fusion | bytes 14155776 | tf_op jit(solution)/shard_map/slice | solution.py:57
  117.9 0.5 convolution_add_fusion.6
  118.4 0.5 convolution_add_fusion.5
  119.4 0.5 convolution_add_fusion.3
  120.0 0.5 convolution_add_fusion.2
  120.5 0.5 convolution_add_fusion.1
  121.1 1.3 %fusion.42 = bf16[2,2,256,192]{2,3,1,0:T(8,128)(2,1)} fusion(f32[2,2,256,192]{2,3,1,0:T(8,128)S(1)} %get-tuple-element.112, f32[2,2,256,192]{2,3,1,0:T(8,128)S(1)} %convolution_add_fusion.1, bf16[576,192,1,1]{1,0,3,2:T(8,128)(2,1)S(1)} %bitcast.195, bf16[2,2,256,192]{2,3,1,0:T(8,128)(2,1)S(1)} %get-tuple-element.44, ...), kind=kOutput, calls=%fused_computation.56 | convolution fusion | flops 230621184 | bytes 3366912 | tf_op jit(solution)/shard_map/fhwc,cd->fhwd/dot_general | solution.py:60
  (73 shorter events, 10.9 us)
Async XLA Ops:
  0.0 44.0 %copy-start = (bf16[384,384]{1,0:T(8,128)(2,1)S(1)}, bf16[384,384]{1,0:T(8,128)(2,1)}, u32[]{:S(2)}) copy-start(bf16[384,384]{1,0:T(8,128)(2,1)} %param.15) | copy-start | bytes 884740
  0.0 39.2 %copy-start.5 = (bf16[2,1,128,384]{3,2,1,0:T(8,128)(2,1)S(1)}, bf16[2,1,128,384]{3,2,1,0:T(8,128)(2,1)}, u32[]{:S(2)}) copy-start(bf16[2,1,128,384]{3,2,1,0:T(8,128)(2,1)} %param.10) | copy-start | bytes 589828
  0.0 6.9 %collective-permute-start = (bf16[2,1,128,384]{3,2,1,0:T(8,128)(2,1)}, bf16[2,1,128,384]{3,2,1,0:T(8,128)(2,1)S(1)}, u32[]{:S(2)}, u32[]{:S(2)}) collective-permute-start(bf16[2,1,128,384]{3,2,1,0:T(8,128)(2,1)} %param.10), channel_id=1, source_target_pairs={{0,2},{1,3},{2,4},{3,5},{4,6},{5,7},{6,8},{7,9},{8,10},{9,11},{10,... | collective-permute-start | bytes 589832 | tf_op jit(solution)/shard_map/ppermute | solution.py:33
  1.2 8.9 %collective-permute-start.1 = (bf16[2,1,128,384]{3,2,1,0:T(8,128)(2,1)}, bf16[2,1,128,384]{3,2,1,0:T(8,128)(2,1)S(1)}, u32[]{:S(2)}, u32[]{:S(2)}) collective-permute-start(bf16[2,1,128,384]{3,2,1,0:T(8,128)(2,1)} %param.10), channel_id=1, source_target_pairs={{0,4},{1,5},{2,6},{3,7},{4,8},{5,9},{6,10},{7,11},{8,12},{9,13},{1... | collective-permute-start | bytes 589832 | tf_op jit(solution)/shard_map/ppermute | solution.py:33
  2.5 27.9 %collective-permute-start.2 = (bf16[2,1,128,384]{3,2,1,0:T(8,128)(2,1)}, bf16[2,1,128,384]{3,2,1,0:T(8,128)(2,1)S(1)}, u32[]{:S(2)}, u32[]{:S(2)}) collective-permute-start(bf16[2,1,128,384]{3,2,1,0:T(8,128)(2,1)} %param.10), channel_id=1, source_target_pairs={{0,6},{1,7},{2,8},{3,9},{4,10},{5,11},{6,12},{7,13},{8,14},{9,15},... | collective-permute-start | bytes 589832 | tf_op jit(solution)/shard_map/ppermute | solution.py:33
  3.5 31.1 %collective-permute-start.3 = (bf16[2,1,128,384]{3,2,1,0:T(8,128)(2,1)}, bf16[2,1,128,384]{3,2,1,0:T(8,128)(2,1)S(1)}, u32[]{:S(2)}, u32[]{:S(2)}) collective-permute-start(bf16[2,1,128,384]{3,2,1,0:T(8,128)(2,1)} %param.10), channel_id=1, source_target_pairs={{0,8},{1,9},{2,10},{3,11},{4,12},{5,13},{6,14},{7,15},{8,0},{9,1},... | collective-permute-start | bytes 589832 | tf_op jit(solution)/shard_map/ppermute | solution.py:33
  4.9 29.8 %collective-permute-start.4 = (bf16[2,1,128,384]{3,2,1,0:T(8,128)(2,1)}, bf16[2,1,128,384]{3,2,1,0:T(8,128)(2,1)S(1)}, u32[]{:S(2)}, u32[]{:S(2)}) collective-permute-start(bf16[2,1,128,384]{3,2,1,0:T(8,128)(2,1)} %param.10), channel_id=1, source_target_pairs={{0,10},{1,11},{2,12},{3,13},{4,14},{5,15},{6,0},{7,1},{8,2},{9,3},... | collective-permute-start | bytes 589832 | tf_op jit(solution)/shard_map/ppermute | solution.py:33
  6.9 30.6 %collective-permute-start.5 = (bf16[2,1,128,384]{3,2,1,0:T(8,128)(2,1)}, bf16[2,1,128,384]{3,2,1,0:T(8,128)(2,1)S(1)}, u32[]{:S(2)}, u32[]{:S(2)}) collective-permute-start(bf16[2,1,128,384]{3,2,1,0:T(8,128)(2,1)} %param.10), channel_id=1, source_target_pairs={{0,12},{1,13},{2,14},{3,15},{4,0},{5,1},{6,2},{7,3},{8,4},{9,5},{1... | collective-permute-start | bytes 589832 | tf_op jit(solution)/shard_map/ppermute | solution.py:33
  10.1 28.5 %collective-permute-start.6 = (bf16[2,1,128,384]{3,2,1,0:T(8,128)(2,1)}, bf16[2,1,128,384]{3,2,1,0:T(8,128)(2,1)S(1)}, u32[]{:S(2)}, u32[]{:S(2)}) collective-permute-start(bf16[2,1,128,384]{3,2,1,0:T(8,128)(2,1)} %param.10), channel_id=1, source_target_pairs={{0,14},{1,15},{2,0},{3,1},{4,2},{5,3},{6,4},{7,5},{8,6},{9,7},{10,... | collective-permute-start | bytes 589832 | tf_op jit(solution)/shard_map/ppermute | solution.py:33
  38.7 3.6 %collective-permute-start.7 = (bf16[2,8,128,384]{3,2,1,0:T(8,128)(2,1)S(1)}, bf16[2,8,128,384]{3,2,1,0:T(8,128)(2,1)S(1)}, u32[]{:S(2)}, u32[]{:S(2)}) collective-permute-start(bf16[2,8,128,384]{3,2,1,0:T(8,128)(2,1)S(1)} %get-tuple-element.91), channel_id=1, source_target_pairs={{0,1},{1,0},{2,3},{3,2},{4,5},{5,4},{6,7},{7,6},{8,9},{9,8},{10,11... | collective-permute-start | bytes 4718600 | tf_op jit(solution)/shard_map/ppermute | solution.py:36
  44.1 3.7 %copy-start.9 = (bf16[384,384]{1,0:T(8,128)(2,1)S(1)}, bf16[384,384]{1,0:T(8,128)(2,1)}, u32[]{:S(2)}) copy-start(bf16[384,384]{1,0:T(8,128)(2,1)} %param.14) | copy-start | bytes 884740
  47.8 2.1 %copy-start.6 = (bf16[2,1,128,384]{3,2,1,0:T(8,128)(2,1)S(1)}, bf16[2,1,128,384]{3,2,1,0:T(8,128)(2,1)}, u32[]{:S(2)}) copy-start(bf16[2,1,128,384]{3,2,1,0:T(8,128)(2,1)} %param.10) | copy-start | bytes 589828
  55.6 3.9 %copy-start.4 = (bf16[2,1,128,384]{3,2,1,0:T(8,128)(2,1)S(1)}, bf16[2,1,128,384]{3,2,1,0:T(8,128)(2,1)}, u32[]{:S(2)}) copy-start(bf16[2,1,128,384]{3,2,1,0:T(8,128)(2,1)} %param.11) | copy-start | bytes 589828
  59.5 8.5 %collective-permute-start.8 = (bf16[4,1,128,384]{3,2,0,1:T(8,128)(2,1)S(1)}, bf16[4,1,128,384]{3,2,0,1:T(8,128)(2,1)S(1)}, u32[]{:S(2)}, u32[]{:S(2)}) collective-permute-start(bf16[4,1,128,384]{3,2,0,1:T(8,128)(2,1)S(1)} %pad_maximum_fusion.3), channel_id=1, source_target_pairs={{0,1},{1,2},{2,3},{3,4},{4,5},{5,6},{6,7},{7,8},{8,9},{9,10},{10,1... | collective-permute-start | bytes 1179656 | tf_op jit(solution)/shard_map/ppermute | solution.py:15
  61.5 10.1 %collective-permute-start.9 = (bf16[4,1,128,384]{3,2,0,1:T(8,128)(2,1)S(1)}, bf16[4,1,128,384]{3,2,0,1:T(8,128)(2,1)S(1)}, u32[]{:S(2)}, u32[]{:S(2)}) collective-permute-start(bf16[4,1,128,384]{3,2,0,1:T(8,128)(2,1)S(1)} %pad_maximum_fusion.3), channel_id=1, source_target_pairs={{1,0},{2,1},{3,2},{4,3},{5,4},{6,5},{7,6},{8,7},{9,8},{10,9},{11,1... | collective-permute-start | bytes 1179656 | tf_op jit(solution)/shard_map/ppermute | solution.py:16
  76.1 6.7 %copy-start.7 = (bf16[3,3,384,192]{2,3,1,0:T(8,128)(2,1)S(1)}, bf16[3,3,384,192]{2,3,1,0:T(8,128)(2,1)}, u32[]{:S(2)}) copy-start(bf16[3,3,384,192]{2,3,1,0:T(8,128)(2,1)} %param.18) | copy-start | bytes 3981316
  77.1 8.9 %collective-permute-start.10 = (bf16[2,1,128,384]{3,2,0,1:T(8,128)(2,1)S(1)}, bf16[2,1,128,384]{3,2,0,1:T(8,128)(2,1)S(1)}, u32[]{:S(2)}, u32[]{:S(2)}) collective-permute-start(bf16[2,1,128,384]{3,2,0,1:T(8,128)(2,1)S(1)} %fusion.93), channel_id=1, source_target_pairs={{0,1},{1,2},{2,3},{3,4},{4,5},{5,6},{6,7},{7,8},{8,9},{9,10},{10,1... | collective-permute-start | bytes 589832 | tf_op jit(solution)/shard_map/ppermute | solution.py:15
  79.0 8.0 %collective-permute-start.11 = (bf16[2,1,128,384]{3,2,0,1:T(8,128)(2,1)S(1)}, bf16[2,1,128,384]{3,2,0,1:T(8,128)(2,1)S(1)}, u32[]{:S(2)}, u32[]{:S(2)}) collective-permute-start(bf16[2,1,128,384]{3,2,0,1:T(8,128)(2,1)S(1)} %fusion.93), channel_id=1, source_target_pairs={{1,0},{2,1},{3,2},{4,3},{5,4},{6,5},{7,6},{8,7},{9,8},{10,9},{11,1... | collective-permute-start | bytes 589832 | tf_op jit(solution)/shard_map/ppermute | solution.py:16
  95.3 1.3 %copy-start.8 = (bf16[1152,192,1,1]{0,1,2,3:T(8,128)(2,1)S(1)}, bf16[1152,192,1,1]{0,1,2,3:T(8,128)(2,1)}, u32[]{:S(2)}) copy-start(bf16[1152,192,1,1]{0,1,2,3:T(8,128)(2,1)} %reshape.139) | copy-start | bytes 1327108
  99.0 1.4 %copy-start.2 = (bf16[2,2,256,192]{2,3,1,0:T(8,128)(2,1)S(1)}, bf16[2,2,256,192]{2,3,1,0:T(8,128)(2,1)}, u32[]{:S(2)}) copy-start(bf16[2,2,256,192]{2,3,1,0:T(8,128)(2,1)} %param.12) | copy-start | bytes 1179652
  100.2 5.4 %copy-start.3 = (bf16[3,3,3,192,192]{4,3,2,1,0:T(8,128)(2,1)S(1)}, bf16[3,3,3,192,192]{4,3,2,1,0:T(8,128)(2,1)}, u32[]{:S(2)}) copy-start(bf16[3,3,3,192,192]{4,3,2,1,0:T(8,128)(2,1)} %param.19) | copy-start | bytes 5971972
  100.5 6.8 %collective-permute-start.12 = (bf16[4,1,256,192]{2,3,1,0:T(8,128)(2,1)S(1)}, bf16[4,1,256,192]{2,3,1,0:T(8,128)(2,1)S(1)}, u32[]{:S(2)}, u32[]{:S(2)}) collective-permute-start(bf16[4,1,256,192]{2,3,1,0:T(8,128)(2,1)S(1)} %get-tuple-element.83), channel_id=1, source_target_pairs={{0,1},{1,2},{2,3},{3,4},{4,5},{5,6},{6,7},{7,8},{8,9},{9,10},{10,1... | collective-permute-start | bytes 1179656 | tf_op jit(solution)/shard_map/ppermute | solution.py:15
  102.6 10.1 %collective-permute-start.13 = (bf16[4,1,256,192]{2,3,1,0:T(8,128)(2,1)S(1)}, bf16[4,1,256,192]{2,3,1,0:T(8,128)(2,1)S(1)}, u32[]{:S(2)}, u32[]{:S(2)}) collective-permute-start(bf16[4,1,256,192]{2,3,1,0:T(8,128)(2,1)S(1)} %get-tuple-element.84), channel_id=1, source_target_pairs={{1,0},{2,1},{3,2},{4,3},{5,4},{6,5},{7,6},{8,7},{9,8},{10,9},{11,1... | collective-permute-start | bytes 1179656 | tf_op jit(solution)/shard_map/ppermute | solution.py:16
  120.5 1.9 %copy-start.1 = (bf16[384,384]{1,0:T(8,128)(2,1)S(1)}, bf16[384,384]{1,0:T(8,128)(2,1)}, u32[]{:S(2)}) copy-start(bf16[384,384]{1,0:T(8,128)(2,1)} %param.15) | copy-start | bytes 884740

commit v6 on v4

--- a/solution.py
+++ b/solution.py
@@ -88,6 +88,11 @@
 ):
     frame_count, row_count, width_count, channels = features.shape
     every_row = gather_rows(features)
+    every_row, first_cache, second_cache = lax.optimization_barrier(
+        (every_row, first_cache, second_cache)
+    )
+    first_cache_pad = extended(first_cache, 1, 1)
+    second_cache_pad = extended(second_cache, 1, 1)
     normed_all = rms_scale(every_row).astype(jnp.bfloat16)
     all_tokens = normed_all.reshape(frame_count, -1, channels)
     normed = rms_scale(features).astype(jnp.bfloat16)
@@ -95,6 +100,9 @@
     queries = project_rows(normed_tokens, w_query)
     keys_all = project_rows(all_tokens, w_key)
     values_all = project_rows(all_tokens, w_value)
+    keys_all, values_all, first_cache_pad, second_cache_pad = lax.optimization_barrier(
+        (keys_all, values_all, first_cache_pad, second_cache_pad)
+    )
     score_scale = 1.0 / math.sqrt(channels)
     scores = (
         jnp.einsum("fqc,fkc->fqk", queries, keys_all, preferred_element_type=jnp.float32)
@@ -116,26 +124,18 @@
         + projected.reshape(frame_count, row_count, width_count, channels)
     ).astype(jnp.bfloat16)
     first_in = jax.nn.silu(rms_scale(mixed)).astype(jnp.bfloat16)
-    first_stack = jnp.concatenate([first_cache, first_in], axis=0)
-    first_padded = extended(first_stack, 1, 1)
-    second_cache_pad = extended(second_cache, 1, 1)
+    first_padded = jnp.concatenate([first_cache_pad, extended(first_in, 1, 1)], axis=0)
     block_out = (mixed.astype(jnp.float32) + conv_taps(first_padded, w_first, 3)).astype(
         jnp.bfloat16
     )
     block_padded = extended(block_out, 1, 1)
     widened = jnp.repeat(block_padded, 2, axis=2)
-    upsampled = conv_taps(
-        widened, w_upsample[None], 1, rows=((0, 0, 1, 1), (0, 1, 1, 2), (1, 1, 2, 2))
-    ).astype(jnp.bfloat16)
+    upsampled = conv_taps(widened, w_upsample[None], 1, rows=((0, 1), (1, 1), (1, 2))).astype(
+        jnp.bfloat16
+    )
     second_in = jax.nn.silu(rms_scale(upsampled)).astype(jnp.bfloat16)
-    me = lax.axis_index("ha")
-    count = lax.axis_size("ha")
-    row = lax.broadcasted_iota(jnp.int32, (1, second_in.shape[1], 1, 1), 1)
-    outside = ((row == 0) & (me == 0)) | ((row == second_in.shape[1] - 1) & (me == count - 1))
-    second_in = jnp.where(outside, jnp.zeros_like(second_in), second_in)
-    second_padded = jnp.concatenate([second_cache_pad, second_in], axis=0)
-    own = upsampled[:, 1 : upsampled.shape[1] - 1]
-    return (own.astype(jnp.float32) + conv_taps(second_padded, w_second, 3)).astype(
+    second_padded = jnp.concatenate([second_cache_pad, extended(second_in, 1, 1)], axis=0)
+    return (upsampled.astype(jnp.float32) + conv_taps(second_padded, w_second, 3)).astype(
         jnp.bfloat16
     )
 

time: 128 us -> 150 us (1.17); the launches traced: 128 us -> 148 us
  starting transfers between devices: 22.5 us -> 34.6 us
  local copies, waits for them, and re-layouts: 29.6 us -> 39.5 us
  matrix products: 30.6 us -> 25.7 us
  waiting for transfers between devices: 36.9 us -> 39.8 us
    ppermute x3 -> x5, waiting for transfers between devices: 6.87 us -> 14.7 us  [halo_rows(): after = lax.ppermute(first, 'ha', down)]
    ppermute x3 -> x5, starting transfers between devices: 7.88 us -> 14.5 us  [halo_rows(): before = lax.ppermute(last, 'ha', up)]
    ppermute x7, waiting for transfers between devices: 30 us -> 24.7 us  [gather_rows(): pieces.append(lax.ppermute(x, 'ha', pairs))]
    dot_general x1 -> x0, matrix products: 4.94 us -> none  [per_device(): jnp.einsum('fqk,fkc->fqc', weights.astype(jnp.bfloat16), values_all, pref...]
    ppermute x3 -> x5, starting transfers between devices: 6.91 us -> 11.7 us  [halo_rows(): after = lax.ppermute(first, 'ha', down)]
    dot_general x21, matrix products: 18 us -> 13.2 us  [conv_taps(): jnp.einsum('fhwc,cd->fhwd', stacked, kernel, preferred_element_type=jnp.f...]
    dot_general x1 -> x2, matrix products: 1.01 us -> 5.79 us  [project_rows(): jnp.einsum('ftc,cd->ftd', tokens, weight, preferred_element_type=jnp.floa...]
    another operation x3, local copies, waits for them, and re-layouts: 1.89 us -> 6.32 us  [conv_taps(): kernel = weight[time_off, row_off].reshape(3 * in_channels, out_channels)]
  transfers between devices with their start and end apart: 14 -> 18, of which waited for: 7 -> 9; matrix products, arithmetic and copies ran while one was open for 38% -> 24% of each run, Pallas kernels for 0% -> 0%
where the time goes in v6:
time: 150 us; the launch traced here: 148 us
  waiting for transfers between devices  39.8 us (27%)
  local copies, waits for them, and re-layouts  39.5 us (26%)
  starting transfers between devices  34.6 us (23%)
  matrix products  25.7 us (17%)
  other arithmetic  7.67 us (5%)
    ppermute x7, waiting for transfers between devices, gather_rows(): pieces.append(lax.ppermute(x, 'ha', pairs))  24.7 us
    ppermute x5, waiting for transfers between devices, halo_rows(): after = lax.ppermute(first, 'ha', down)  14.7 us
    ppermute x5, starting transfers between devices, halo_rows(): before = lax.ppermute(last, 'ha', up)  14.5 us
    slice x6, local copies, waits for them, and re-layouts, conv_taps(): kernel = weight[time_off, row_off].reshape(3 * in_channels, out_channels)  13.5 us
    dot_general x21, matrix products, conv_taps(): jnp.einsum('fhwc,cd->fhwd', stacked, kernel, preferred_element_type=jnp.f...  13.2 us
    ppermute x5, starting transfers between devices, halo_rows(): after = lax.ppermute(first, 'ha', down)  11.7 us
    unnamed x63, local copies, waits for them, and re-layouts  11.4 us
    ppermute x7, starting transfers between devices, gather_rows(): pieces.append(lax.ppermute(x, 'ha', pairs))  7.88 us
  transfers between devices with their start and end apart: 18, of which 9 were waited for; matrix products, arithmetic and copies ran while one was open for 24% of the time, Pallas kernels for 0%

profile of v6, /device:TPU:13, one launch (start us, length us, event | category | flops | bytes accessed | tf_op | source)
XLA Modules:
  0.0 148.0 jit_solution(10089881682175853946)
XLA Ops:
  0.0 1.2 collective-permute-start
  1.2 1.3 collective-permute-start.1
  2.5 1.0 collective-permute-start.2
  3.5 1.3 collective-permute-start.3
  4.8 1.0 collective-permute-start.4
  5.9 1.7 %constant_dynamic-update-slice_fusion.7 = (bf16[2,8,128,384]{3,2,1,0:T(8,128)(2,1)}, bf16[2,16,128,384]{3,2,1,0:T(8,128)(2,1)S(1)}) fusion(bf16[2,1,128,384]{3,2,1,0:T(8,128)(2,1)} %param.10), kind=kLoop, calls=%fused_computation.216 | loop fusion | bytes 589824
  7.5 1.2 collective-permute-start.5
  11.6 18.8 %collective-permute-done.2 = bf16[2,1,128,384]{3,2,1,0:T(8,128)(2,1)S(1)} collective-permute-done((bf16[2,1,128,384]{3,2,1,0:T(8,128)(2,1)}, bf16[2,1,128,384]{3,2,1,0:T(8,128)(2,1)S(1)}, u32[]{:S(2)}, u32[]{:S(2)}) %collective-permute-start.2) | collective-permute-done | bytes 196640 | tf_op jit(solution)/shard_map/ppermute | solution.py:33
  31.1 3.5 %collective-permute-done.3 = bf16[2,1,128,384]{3,2,1,0:T(8,128)(2,1)S(1)} collective-permute-done((bf16[2,1,128,384]{3,2,1,0:T(8,128)(2,1)}, bf16[2,1,128,384]{3,2,1,0:T(8,128)(2,1)S(1)}, u32[]{:S(2)}, u32[]{:S(2)}) %collective-permute-start.3) | collective-permute-done | bytes 196640 | tf_op jit(solution)/shard_map/ppermute | solution.py:33
  36.1 1.4 collective-permute-done.5
  39.8 1.1 fusion.177
  40.9 1.2 copy.34
  42.1 2.1 %reshape.127 = bf16[1152,192,1,1]{0,1,2,3:T(8,128)(2,1)} reshape(bf16[1,1,3,384,192]{3,2,4,1,0:T(4,128)(2,1)} %copy.34) | data formatting | bytes 884736 | tf_op jit(solution)/shard_map/reshape;squeeze | solution.py:64
  44.2 2.2 %copy.33 = bf16[1,1,3,384,192]{3,2,4,1,0:T(4,128)(2,1)} copy(bf16[1,1,3,384,192]{3,4,2,1,0:T(8,128)(2,1)} %get-tuple-element.60) | data formatting | bytes 884736 | tf_op jit(solution)/shard_map/slice | solution.py:64
  46.4 2.1 %reshape.126 = bf16[1152,192,1,1]{0,1,2,3:T(8,128)(2,1)} reshape(bf16[1,1,3,384,192]{3,2,4,1,0:T(4,128)(2,1)} %copy.33) | data formatting | bytes 884736 | tf_op jit(solution)/shard_map/reshape;squeeze | solution.py:64
  48.5 2.2 %copy.35 = bf16[1,1,3,384,192]{3,2,4,1,0:T(4,128)(2,1)} copy(bf16[1,1,3,384,192]{3,4,2,1,0:T(8,128)(2,1)} %get-tuple-element.58) | data formatting | bytes 884736 | tf_op jit(solution)/shard_map/slice | solution.py:64
  50.7 2.1 %reshape.128 = bf16[1152,192,1,1]{0,1,2,3:T(8,128)(2,1)} reshape(bf16[1,1,3,384,192]{3,2,4,1,0:T(4,128)(2,1)} %copy.35) | data formatting | bytes 884736 | tf_op jit(solution)/shard_map/reshape;squeeze | solution.py:64
  52.8 1.0 fusion.138
  53.9 5.7 %fusion.174 = (bf16[1,1,3,384,384]{4,3,2,1,0:T(8,128)(2,1)}, bf16[1,1,3,384,384]{4,3,2,1,0:T(8,128)(2,1)}, bf16[1,1,3,384,384]{4,3,2,1,0:T(8,128)(2,1)}, bf16[1,...) fusion(bf16[3,3,3,384,384]{4,3,2,1,0:T(8,128)(2,1)} %param.17), kind=kLoop, calls=%fused_computation.269 | loop fusion | bytes 15925248 | tf_op jit(solution)/shard_map/slice | solution.py:64
  59.6 1.8 %constant_dynamic-update-slice_fusion.8 = bf16[2,16,128,384]{3,2,1,0:T(8,128)(2,1)S(1)} fusion(bf16[2,16,128,384]{3,2,1,0:T(8,128)(2,1)S(1)} %get-tuple-element.100, bf16[2,8,128,384]{3,2,1,0:T(8,128)(2,1)} %collective-permute-done.7), kind=kLoop, calls=%fused_computation.217 | loop fusion | bytes 3145728 | tf_op jit(solution)/shard_map/concatenate | solution.py:37
  61.4 1.9 %collective-permute-start.8 = (bf16[2,1,128,384]{3,2,0,1:T(8,128)(2,1)S(1)}, bf16[2,1,128,384]{3,2,0,1:T(8,128)(2,1)S(1)}, u32[]{:S(2)}, u32[]{:S(2)}) collective-permute-start(bf16[2,1,128,384]{3,2,0,1:T(8,128)(2,1)S(1)} %bitcast.193), channel_id=1, source_target_pairs={{0,1},{1,2},{2,3},{3,4},{4,5},{5,6},{6,7},{7,8},{8,9},{9,10},{10,1... | collective-permute-start | bytes 589832 | tf_op jit(solution)/shard_map/ppermute | solution.py:15
  63.3 2.4 %collective-permute-start.9 = (bf16[2,1,128,384]{3,2,0,1:T(8,128)(2,1)S(1)}, bf16[2,1,128,384]{3,2,0,1:T(8,128)(2,1)S(1)}, u32[]{:S(2)}, u32[]{:S(2)}) collective-permute-start(bf16[2,1,128,384]{3,2,0,1:T(8,128)(2,1)S(1)} %bitcast.194), channel_id=1, source_target_pairs={{1,0},{2,1},{3,2},{4,3},{5,4},{6,5},{7,6},{8,7},{9,8},{10,9},{11,1... | collective-permute-start | bytes 589832 | tf_op jit(solution)/shard_map/ppermute | solution.py:16
  65.8 4.1 %collective-permute-start.10 = (bf16[2,1,256,192]{2,3,1,0:T(8,128)(2,1)S(1)}, bf16[2,1,256,192]{2,3,1,0:T(8,128)(2,1)S(1)}, u32[]{:S(2)}, u32[]{:S(2)}) collective-permute-start(bf16[2,1,256,192]{2,3,1,0:T(8,128)(2,1)S(1)} %get-tuple-element.97), channel_id=1, source_target_pairs={{0,1},{1,2},{2,3},{3,4},{4,5},{5,6},{6,7},{7,8},{8,9},{9,10},{10,1... | collective-permute-start | bytes 589832 | tf_op jit(solution)/shard_map/ppermute | solution.py:15
  69.9 2.1 %collective-permute-start.11 = (bf16[2,1,256,192]{2,3,1,0:T(8,128)(2,1)S(1)}, bf16[2,1,256,192]{2,3,1,0:T(8,128)(2,1)S(1)}, u32[]{:S(2)}, u32[]{:S(2)}) collective-permute-start(bf16[2,1,256,192]{2,3,1,0:T(8,128)(2,1)S(1)} %get-tuple-element.98), channel_id=1, source_target_pairs={{1,0},{2,1},{3,2},{4,3},{5,4},{6,5},{7,6},{8,7},{9,8},{10,9},{11,1... | collective-permute-start | bytes 589832 | tf_op jit(solution)/shard_map/ppermute | solution.py:16
  73.4 3.7 %convolution_convert_fusion = bf16[2,2048,384]{2,1,0:T(8,128)(2,1)} fusion(bf16[2,2048,384]{2,1,0:T(8,128)(2,1)S(1)} %bitcast.172, bf16[384,384]{1,0:T(8,128)(2,1)S(1)} %copy-done), kind=kOutput, calls=%fused_computation.22 | convolution fusion | flops 1209532416 | bytes 6586368 | tf_op jit(solution)/shard_map/ftc,cd->ftd/dot_general | solution.py:72
  77.1 2.1 %convolution_convert_fusion.1 = bf16[2,2048,384]{2,1,0:T(8,128)(2,1)S(1)} fusion(bf16[2,2048,384]{2,1,0:T(8,128)(2,1)S(1)} %bitcast.173, bf16[384,384]{1,0:T(8,128)(2,1)S(1)} %copy-done.21), kind=kOutput, calls=%fused_computation.23 | convolution fusion | flops 1209532416 | bytes 6586368 | tf_op jit(solution)/shard_map/ftc,cd->ftd/dot_general | solution.py:72
  79.3 1.0 pad_maximum_fusion.3
  80.3 0.9 pad_maximum_fusion.4
  81.2 3.6 %fusion.182 = (f32[2,128]{1,0:T(2,128)S(1)}, f32[2,128,2048]{2,1,0:T(8,128)}) fusion(bf16[2,2048,384]{2,1,0:T(8,128)(2,1)S(1)} %convolution_convert_fusion.1, bf16[384,384]{1,0:T(8,128)(2,1)} %param.13, bf16[2,1,128,384]{3,2,1,0:T(8,128)(2,1)S(1)} %copy-done.6, f32[2,128]{1,0:T(2,128)S(1)} %add_rsqrt_fusion.3), kind=kOutput, calls=%fused_computation.277 | convolution fusion | flops 479592192 | bytes 5736448 | tf_op jit(solution)/shard_map/fqc,fkc->fqk/dot_general | solution.py:108
  84.8 2.2 %fusion.21 = f32[2,128]{1,0:T(2,128)S(1)} fusion(f32[2,128,2048]{2,1,0:T(8,128)} %get-tuple-element.116, f32[2,128]{1,0:T(2,128)S(1)} %get-tuple-element.115), kind=kLoop, calls=%fused_computation.45 | loop fusion | flops 1048320 | bytes 2099200 | tf_op jit(solution)/shard_map/reduce_sum | solution.py:113
  87.0 3.0 %multiply_reduce_fusion.1 = (f32[2,128]{1,0:T(2,128)S(1)}, f32[2,1,128,384]{3,2,0,1:T(8,128)S(1)}) fusion(bf16[384,384]{1,0:T(8,128)(2,1)} %param.16, bf16[2,2048,384]{2,1,0:T(8,128)(2,1)} %convolution_convert_fusion, f32[2,128,2048]{2,1,0:T(8,128)S(1)} %copy-done.3, f32[2,128]{1,0:T(2,128)S(1)} %get-tuple-element.115, f32[2,128]{1,0:T(2,128)S(1)} %fusion.21, ...), kind=kOutput, calls=%fused_computation.200 | convolution fusion | flops 479985408 | bytes 6130688 | tf_op jit(solution)/shard_map/ftc,cd->ftd/dot_general | solution.py:121
  90.3 4.5 %collective-permute-start.12 = (bf16[2,1,128,384]{3,2,0,1:T(8,128)(2,1)S(1)}, bf16[2,1,128,384]{3,2,0,1:T(8,128)(2,1)S(1)}, u32[]{:S(2)}, u32[]{:S(2)}) collective-permute-start(bf16[2,1,128,384]{3,2,0,1:T(8,128)(2,1)S(1)} %multiply_convert_fusion.1), channel_id=1, source_target_pairs={{0,1},{1,2},{2,3},{3,4},{4,5},{5,6},{6,7},{7,8},{8,9},{9,10},{10,1... | collective-permute-start | bytes 589832 | tf_op jit(solution)/shard_map/ppermute | solution.py:15
  94.8 2.1 %collective-permute-start.13 = (bf16[2,1,128,384]{3,2,0,1:T(8,128)(2,1)S(1)}, bf16[2,1,128,384]{3,2,0,1:T(8,128)(2,1)S(1)}, u32[]{:S(2)}, u32[]{:S(2)}) collective-permute-start(bf16[2,1,128,384]{3,2,0,1:T(8,128)(2,1)S(1)} %multiply_convert_fusion.1), channel_id=1, source_target_pairs={{1,0},{2,1},{3,2},{4,3},{5,4},{6,5},{7,6},{8,7},{9,8},{10,9},{11,1... | collective-permute-start | bytes 589832 | tf_op jit(solution)/shard_map/ppermute | solution.py:16
  97.4 5.2 %collective-permute-done.13 = bf16[2,1,128,384]{3,2,0,1:T(8,128)(2,1)S(1)} collective-permute-done((bf16[2,1,128,384]{3,2,0,1:T(8,128)(2,1)S(1)}, bf16[2,1,128,384]{3,2,0,1:T(8,128)(2,1)S(1)}, u32[]{:S(2)}, u32[]{:S(2)}) %collective-permute-start.13) | collective-permute-done | bytes 196640 | tf_op jit(solution)/shard_map/ppermute | solution.py:16
  103.7 0.8 copy-done.17
  111.4 2.1 %collective-permute-start.14 = (bf16[2,1,128,384]{3,2,0,1:T(8,128)(2,1)S(1)}, bf16[2,1,128,384]{3,2,0,1:T(8,128)(2,1)S(1)}, u32[]{:S(2)}, u32[]{:S(2)}) collective-permute-start(bf16[2,1,128,384]{3,2,0,1:T(8,128)(2,1)S(1)} %fusion.88), channel_id=1, source_target_pairs={{0,1},{1,2},{2,3},{3,4},{4,5},{5,6},{6,7},{7,8},{8,9},{9,10},{10,1... | collective-permute-start | bytes 589832 | tf_op jit(solution)/shard_map/ppermute | solution.py:15
  113.4 2.4 %collective-permute-start.15 = (bf16[2,1,128,384]{3,2,0,1:T(8,128)(2,1)S(1)}, bf16[2,1,128,384]{3,2,0,1:T(8,128)(2,1)S(1)}, u32[]{:S(2)}, u32[]{:S(2)}) collective-permute-start(bf16[2,1,128,384]{3,2,0,1:T(8,128)(2,1)S(1)} %fusion.88), channel_id=1, source_target_pairs={{1,0},{2,1},{3,2},{4,3},{5,4},{6,5},{7,6},{8,7},{9,8},{10,9},{11,1... | collective-permute-start | bytes 589832 | tf_op jit(solution)/shard_map/ppermute | solution.py:16
  115.9 1.1 fusion.175
  117.0 4.3 %collective-permute-done.15 = bf16[2,1,128,384]{3,2,0,1:T(8,128)(2,1)S(1)} collective-permute-done((bf16[2,1,128,384]{3,2,0,1:T(8,128)(2,1)S(1)}, bf16[2,1,128,384]{3,2,0,1:T(8,128)(2,1)S(1)}, u32[]{:S(2)}, u32[]{:S(2)}) %collective-permute-start.15) | collective-permute-done | bytes 196640 | tf_op jit(solution)/shard_map/ppermute | solution.py:16
  122.7 0.8 pad_slice_fusion.23
  123.8 1.2 fusion.3
  125.0 1.1 fusion.27
  126.2 1.2 multiply_reduce_fusion
  127.7 1.9 %collective-permute-start.16 = (bf16[2,1,256,192]{2,3,1,0:T(8,128)(2,1)S(1)}, bf16[2,1,256,192]{2,3,1,0:T(8,128)(2,1)S(1)}, u32[]{:S(2)}, u32[]{:S(2)}) collective-permute-start(bf16[2,1,256,192]{2,3,1,0:T(8,128)(2,1)S(1)} %get-tuple-element.95), channel_id=1, source_target_pairs={{0,1},{1,2},{2,3},{3,4},{4,5},{5,6},{6,7},{7,8},{8,9},{9,10},{10,1... | collective-permute-start | bytes 589832 | tf_op jit(solution)/shard_map/ppermute | solution.py:15
  129.6 2.7 %collective-permute-start.17 = (bf16[2,1,256,192]{2,3,1,0:T(8,128)(2,1)S(1)}, bf16[2,1,256,192]{2,3,1,0:T(8,128)(2,1)S(1)}, u32[]{:S(2)}, u32[]{:S(2)}) collective-permute-start(bf16[2,1,256,192]{2,3,1,0:T(8,128)(2,1)S(1)} %get-tuple-element.96), channel_id=1, source_target_pairs={{1,0},{2,1},{3,2},{4,3},{5,4},{6,5},{7,6},{8,7},{9,8},{10,9},{11,1... | collective-permute-start | bytes 589832 | tf_op jit(solution)/shard_map/ppermute | solution.py:16
  132.4 5.1 %collective-permute-done.17 = bf16[2,1,256,192]{2,3,1,0:T(8,128)(2,1)S(1)} collective-permute-done((bf16[2,1,256,192]{2,3,1,0:T(8,128)(2,1)S(1)}, bf16[2,1,256,192]{2,3,1,0:T(8,128)(2,1)S(1)}, u32[]{:S(2)}, u32[]{:S(2)}) %collective-permute-start.17) | collective-permute-done | bytes 196640 | tf_op jit(solution)/shard_map/ppermute | solution.py:16
  137.7 2.5 %pad_slice_fusion.1 = (bf16[2,2,256,192]{2,3,1,0:T(8,128)(2,1)S(1)}, bf16[2,2,256,192]{2,3,1,0:T(8,128)(2,1)S(1)}, bf16[2,2,256,192]{2,3,1,0:T(8,128)(2,1)S(1)},...) fusion(bf16[4,4,256,192]{2,3,1,0:T(8,128)(2,1)S(1)} %maximum_ma, ...), kind=kLoop, calls=%fused_computation.5 | loop fusion | bytes 9830400 | tf_op jit(solution)/shard_map/slice | solution.py:62
  146.7 1.3 fusion.36
  (117 shorter events, 25.9 us)
Async XLA Ops:
  0.0 73.4 %copy-start = (bf16[384,384]{1,0:T(8,128)(2,1)S(1)}, bf16[384,384]{1,0:T(8,128)(2,1)}, u32[]{:S(2)}) copy-start(bf16[384,384]{1,0:T(8,128)(2,1)} %param.15) | copy-start | bytes 884740
  0.0 7.5 %collective-permute-start = (bf16[2,1,128,384]{3,2,1,0:T(8,128)(2,1)}, bf16[2,1,128,384]{3,2,1,0:T(8,128)(2,1)S(1)}, u32[]{:S(2)}, u32[]{:S(2)}) collective-permute-start(bf16[2,1,128,384]{3,2,1,0:T(8,128)(2,1)} %param.10), channel_id=1, source_target_pairs={{0,2},{1,3},{2,4},{3,5},{4,6},{5,7},{6,8},{7,9},{8,10},{9,11},{10,... | collective-permute-start | bytes 589832 | tf_op jit(solution)/shard_map/ppermute | solution.py:33
  1.2 8.9 %collective-permute-start.1 = (bf16[2,1,128,384]{3,2,1,0:T(8,128)(2,1)}, bf16[2,1,128,384]{3,2,1,0:T(8,128)(2,1)S(1)}, u32[]{:S(2)}, u32[]{:S(2)}) collective-permute-start(bf16[2,1,128,384]{3,2,1,0:T(8,128)(2,1)} %param.10), channel_id=1, source_target_pairs={{0,4},{1,5},{2,6},{3,7},{4,8},{5,9},{6,10},{7,11},{8,12},{9,13},{1... | collective-permute-start | bytes 589832 | tf_op jit(solution)/shard_map/ppermute | solution.py:33
  2.5 27.9 %collective-permute-start.2 = (bf16[2,1,128,384]{3,2,1,0:T(8,128)(2,1)}, bf16[2,1,128,384]{3,2,1,0:T(8,128)(2,1)S(1)}, u32[]{:S(2)}, u32[]{:S(2)}) collective-permute-start(bf16[2,1,128,384]{3,2,1,0:T(8,128)(2,1)} %param.10), channel_id=1, source_target_pairs={{0,6},{1,7},{2,8},{3,9},{4,10},{5,11},{6,12},{7,13},{8,14},{9,15},... | collective-permute-start | bytes 589832 | tf_op jit(solution)/shard_map/ppermute | solution.py:33
  3.5 31.1 %collective-permute-start.3 = (bf16[2,1,128,384]{3,2,1,0:T(8,128)(2,1)}, bf16[2,1,128,384]{3,2,1,0:T(8,128)(2,1)S(1)}, u32[]{:S(2)}, u32[]{:S(2)}) collective-permute-start(bf16[2,1,128,384]{3,2,1,0:T(8,128)(2,1)} %param.10), channel_id=1, source_target_pairs={{0,8},{1,9},{2,10},{3,11},{4,12},{5,13},{6,14},{7,15},{8,0},{9,1},... | collective-permute-start | bytes 589832 | tf_op jit(solution)/shard_map/ppermute | solution.py:33
  4.8 30.5 %collective-permute-start.4 = (bf16[2,1,128,384]{3,2,1,0:T(8,128)(2,1)}, bf16[2,1,128,384]{3,2,1,0:T(8,128)(2,1)S(1)}, u32[]{:S(2)}, u32[]{:S(2)}) collective-permute-start(bf16[2,1,128,384]{3,2,1,0:T(8,128)(2,1)} %param.10), channel_id=1, source_target_pairs={{0,10},{1,11},{2,12},{3,13},{4,14},{5,15},{6,0},{7,1},{8,2},{9,3},... | collective-permute-start | bytes 589832 | tf_op jit(solution)/shard_map/ppermute | solution.py:33
  7.5 32.3 %copy-start.8 = (bf16[3,3,384,192]{2,3,1,0:T(8,128)(2,1)S(1)}, bf16[3,3,384,192]{2,3,1,0:T(8,128)(2,1)}, u32[]{:S(2)}) copy-start(bf16[3,3,384,192]{2,3,1,0:T(8,128)(2,1)} %param.18) | copy-start | bytes 3981316
  7.5 29.9 %collective-permute-start.5 = (bf16[2,1,128,384]{3,2,1,0:T(8,128)(2,1)}, bf16[2,1,128,384]{3,2,1,0:T(8,128)(2,1)S(1)}, u32[]{:S(2)}, u32[]{:S(2)}) collective-permute-start(bf16[2,1,128,384]{3,2,1,0:T(8,128)(2,1)} %param.10), channel_id=1, source_target_pairs={{0,12},{1,13},{2,14},{3,15},{4,0},{5,1},{6,2},{7,3},{8,4},{9,5},{1... | collective-permute-start | bytes 589832 | tf_op jit(solution)/shard_map/ppermute | solution.py:33
  10.1 28.5 %collective-permute-start.6 = (bf16[2,1,128,384]{3,2,1,0:T(8,128)(2,1)}, bf16[2,1,128,384]{3,2,1,0:T(8,128)(2,1)S(1)}, u32[]{:S(2)}, u32[]{:S(2)}) collective-permute-start(bf16[2,1,128,384]{3,2,1,0:T(8,128)(2,1)} %param.10), channel_id=1, source_target_pairs={{0,14},{1,15},{2,0},{3,1},{4,2},{5,3},{6,4},{7,5},{8,6},{9,7},{10,... | collective-permute-start | bytes 589832 | tf_op jit(solution)/shard_map/ppermute | solution.py:33
  39.3 20.2 %collective-permute-start.7 = (bf16[2,8,128,384]{3,2,1,0:T(8,128)(2,1)}, bf16[2,8,128,384]{3,2,1,0:T(8,128)(2,1)}, u32[]{:S(2)}, u32[]{:S(2)}) collective-permute-start(bf16[2,8,128,384]{3,2,1,0:T(8,128)(2,1)} %get-tuple-element.99), channel_id=1, source_target_pairs={{0,1},{1,0},{2,3},{3,2},{4,5},{5,4},{6,7},{7,6},{8,9},{9,8},{10,11... | collective-permute-start | bytes 4718600 | tf_op jit(solution)/shard_map/ppermute | solution.py:36
  59.5 1.9 %copy-start.27 = (bf16[2,1,128,384]{3,2,1,0:T(8,128)(2,1)S(1)}, bf16[2,1,128,384]{3,2,1,0:T(8,128)(2,1)}, u32[]{:S(2)}) copy-start(bf16[2,1,128,384]{3,2,1,0:T(8,128)(2,1)} %param.11) | copy-start | bytes 589828
  59.5 6.2 %copy-start.7 = (bf16[2,2,256,192]{2,3,1,0:T(8,128)(2,1)S(1)}, bf16[2,2,256,192]{2,3,1,0:T(8,128)(2,1)}, u32[]{:S(2)}) copy-start(bf16[2,2,256,192]{2,3,1,0:T(8,128)(2,1)} %param.12) | copy-start | bytes 1179652
  61.4 18.9 %collective-permute-start.8 = (bf16[2,1,128,384]{3,2,0,1:T(8,128)(2,1)S(1)}, bf16[2,1,128,384]{3,2,0,1:T(8,128)(2,1)S(1)}, u32[]{:S(2)}, u32[]{:S(2)}) collective-permute-start(bf16[2,1,128,384]{3,2,0,1:T(8,128)(2,1)S(1)} %bitcast.193), channel_id=1, source_target_pairs={{0,1},{1,2},{2,3},{3,4},{4,5},{5,6},{6,7},{7,8},{8,9},{9,10},{10,1... | collective-permute-start | bytes 589832 | tf_op jit(solution)/shard_map/ppermute | solution.py:15
  63.3 16.9 %collective-permute-start.9 = (bf16[2,1,128,384]{3,2,0,1:T(8,128)(2,1)S(1)}, bf16[2,1,128,384]{3,2,0,1:T(8,128)(2,1)S(1)}, u32[]{:S(2)}, u32[]{:S(2)}) collective-permute-start(bf16[2,1,128,384]{3,2,0,1:T(8,128)(2,1)S(1)} %bitcast.194), channel_id=1, source_target_pairs={{1,0},{2,1},{3,2},{4,3},{5,4},{6,5},{7,6},{8,7},{9,8},{10,9},{11,1... | collective-permute-start | bytes 589832 | tf_op jit(solution)/shard_map/ppermute | solution.py:16
  65.8 13.5 %collective-permute-start.10 = (bf16[2,1,256,192]{2,3,1,0:T(8,128)(2,1)S(1)}, bf16[2,1,256,192]{2,3,1,0:T(8,128)(2,1)S(1)}, u32[]{:S(2)}, u32[]{:S(2)}) collective-permute-start(bf16[2,1,256,192]{2,3,1,0:T(8,128)(2,1)S(1)} %get-tuple-element.97), channel_id=1, source_target_pairs={{0,1},{1,2},{2,3},{3,4},{4,5},{5,6},{6,7},{7,8},{8,9},{9,10},{10,1... | collective-permute-start | bytes 589832 | tf_op jit(solution)/shard_map/ppermute | solution.py:15
  69.9 9.4 %collective-permute-start.11 = (bf16[2,1,256,192]{2,3,1,0:T(8,128)(2,1)S(1)}, bf16[2,1,256,192]{2,3,1,0:T(8,128)(2,1)S(1)}, u32[]{:S(2)}, u32[]{:S(2)}) collective-permute-start(bf16[2,1,256,192]{2,3,1,0:T(8,128)(2,1)S(1)} %get-tuple-element.98), channel_id=1, source_target_pairs={{1,0},{2,1},{3,2},{4,3},{5,4},{6,5},{7,6},{8,7},{9,8},{10,9},{11,1... | collective-permute-start | bytes 589832 | tf_op jit(solution)/shard_map/ppermute | solution.py:16
  73.4 3.7 %copy-start.21 = (bf16[384,384]{1,0:T(8,128)(2,1)S(1)}, bf16[384,384]{1,0:T(8,128)(2,1)}, u32[]{:S(2)}) copy-start(bf16[384,384]{1,0:T(8,128)(2,1)} %param.14) | copy-start | bytes 884740
  79.2 1.9 %copy-start.6 = (bf16[2,1,128,384]{3,2,1,0:T(8,128)(2,1)S(1)}, bf16[2,1,128,384]{3,2,1,0:T(8,128)(2,1)}, u32[]{:S(2)}) copy-start(bf16[2,1,128,384]{3,2,1,0:T(8,128)(2,1)} %param.10) | copy-start | bytes 589828
  84.8 2.2 %copy-start.3 = (f32[2,128,2048]{2,1,0:T(8,128)S(1)}, f32[2,128,2048]{2,1,0:T(8,128)}, u32[]{:S(2)}) copy-start(f32[2,128,2048]{2,1,0:T(8,128)} %get-tuple-element.116) | copy-start | bytes 6291460
  87.0 9.9 %copy-start.4 = (bf16[2,3,128,384]{3,2,0,1:T(8,128)(2,1)S(1)}, bf16[2,3,128,384]{3,2,0,1:T(8,128)(2,1)}, u32[]{:S(2)}) copy-start(bf16[2,3,128,384]{3,2,0,1:T(8,128)(2,1)} %pad_maximum_fusion.4) | copy-start | bytes 1769476
  90.3 7.2 %collective-permute-start.12 = (bf16[2,1,128,384]{3,2,0,1:T(8,128)(2,1)S(1)}, bf16[2,1,128,384]{3,2,0,1:T(8,128)(2,1)S(1)}, u32[]{:S(2)}, u32[]{:S(2)}) collective-permute-start(bf16[2,1,128,384]{3,2,0,1:T(8,128)(2,1)S(1)} %multiply_convert_fusion.1), channel_id=1, source_target_pairs={{0,1},{1,2},{2,3},{3,4},{4,5},{5,6},{6,7},{7,8},{8,9},{9,10},{10,1... | collective-permute-start | bytes 589832 | tf_op jit(solution)/shard_map/ppermute | solution.py:15
  94.8 7.9 %collective-permute-start.13 = (bf16[2,1,128,384]{3,2,0,1:T(8,128)(2,1)S(1)}, bf16[2,1,128,384]{3,2,0,1:T(8,128)(2,1)S(1)}, u32[]{:S(2)}, u32[]{:S(2)}) collective-permute-start(bf16[2,1,128,384]{3,2,0,1:T(8,128)(2,1)S(1)} %multiply_convert_fusion.1), channel_id=1, source_target_pairs={{1,0},{2,1},{3,2},{4,3},{5,4},{6,5},{7,6},{8,7},{9,8},{10,9},{11,1... | collective-permute-start | bytes 589832 | tf_op jit(solution)/shard_map/ppermute | solution.py:16
  103.3 1.2 copy-start.17
  103.7 1.3 copy-start.16
  104.5 1.2 copy-start.15
  105.5 1.2 copy-start.14
  106.2 1.2 copy-start.13
  107.2 1.2 copy-start.12
  107.9 1.2 copy-start.11
  108.9 1.2 copy-start.10
  109.7 1.2 copy-start.9
  110.6 5.2 %copy-start.5 = (bf16[3,3,3,192,192]{4,3,2,1,0:T(8,128)(2,1)S(1)}, bf16[3,3,3,192,192]{4,3,2,1,0:T(8,128)(2,1)}, u32[]{:S(2)}) copy-start(bf16[3,3,3,192,192]{4,3,2,1,0:T(8,128)(2,1)} %param.19) | copy-start | bytes 5971972
  111.4 5.6 %collective-permute-start.14 = (bf16[2,1,128,384]{3,2,0,1:T(8,128)(2,1)S(1)}, bf16[2,1,128,384]{3,2,0,1:T(8,128)(2,1)S(1)}, u32[]{:S(2)}, u32[]{:S(2)}) collective-permute-start(bf16[2,1,128,384]{3,2,0,1:T(8,128)(2,1)S(1)} %fusion.88), channel_id=1, source_target_pairs={{0,1},{1,2},{2,3},{3,4},{4,5},{5,6},{6,7},{7,8},{8,9},{9,10},{10,1... | collective-permute-start | bytes 589832 | tf_op jit(solution)/shard_map/ppermute | solution.py:15
  113.4 7.9 %collective-permute-start.15 = (bf16[2,1,128,384]{3,2,0,1:T(8,128)(2,1)S(1)}, bf16[2,1,128,384]{3,2,0,1:T(8,128)(2,1)S(1)}, u32[]{:S(2)}, u32[]{:S(2)}) collective-permute-start(bf16[2,1,128,384]{3,2,0,1:T(8,128)(2,1)S(1)} %fusion.88), channel_id=1, source_target_pairs={{1,0},{2,1},{3,2},{4,3},{5,4},{6,5},{7,6},{8,7},{9,8},{10,9},{11,1... | collective-permute-start | bytes 589832 | tf_op jit(solution)/shard_map/ppermute | solution.py:16
  122.7 1.1 copy-start.20
  123.8 1.2 copy-start.19
  125.0 1.2 copy-start.18
  127.4 4.9 %copy-start.2 = (bf16[2,4,256,192]{2,3,1,0:T(8,128)(2,1)S(1)}, bf16[2,4,256,192]{2,3,1,0:T(8,128)(2,1)}, u32[]{:S(2)}) copy-start(bf16[2,4,256,192]{2,3,1,0:T(8,128)(2,1)} %pad_maximum_fusion.3) | copy-start | bytes 2359300
  127.7 4.7 %collective-permute-start.16 = (bf16[2,1,256,192]{2,3,1,0:T(8,128)(2,1)S(1)}, bf16[2,1,256,192]{2,3,1,0:T(8,128)(2,1)S(1)}, u32[]{:S(2)}, u32[]{:S(2)}) collective-permute-start(bf16[2,1,256,192]{2,3,1,0:T(8,128)(2,1)S(1)} %get-tuple-element.95), channel_id=1, source_target_pairs={{0,1},{1,2},{2,3},{3,4},{4,5},{5,6},{6,7},{7,8},{8,9},{9,10},{10,1... | collective-permute-start | bytes 589832 | tf_op jit(solution)/shard_map/ppermute | solution.py:15
  129.6 7.9 %collective-permute-start.17 = (bf16[2,1,256,192]{2,3,1,0:T(8,128)(2,1)S(1)}, bf16[2,1,256,192]{2,3,1,0:T(8,128)(2,1)S(1)}, u32[]{:S(2)}, u32[]{:S(2)}) collective-permute-start(bf16[2,1,256,192]{2,3,1,0:T(8,128)(2,1)S(1)} %get-tuple-element.96), channel_id=1, source_target_pairs={{1,0},{2,1},{3,2},{4,3},{5,4},{6,5},{7,6},{8,7},{9,8},{10,9},{11,1... | collective-permute-start | bytes 589832 | tf_op jit(solution)/shard_map/ppermute | solution.py:16
  140.2 1.0 copy-start.26
  140.4 1.3 copy-start.25
  141.7 1.0 copy-start.24
  142.7 1.0 copy-start.23
  143.6 1.0 copy-start.22
  146.7 1.3 copy-start.1

commit v7 on v6

--- a/solution.py
+++ b/solution.py
@@ -88,11 +88,6 @@
 ):
     frame_count, row_count, width_count, channels = features.shape
     every_row = gather_rows(features)
-    every_row, first_cache, second_cache = lax.optimization_barrier(
-        (every_row, first_cache, second_cache)
-    )
-    first_cache_pad = extended(first_cache, 1, 1)
-    second_cache_pad = extended(second_cache, 1, 1)
     normed_all = rms_scale(every_row).astype(jnp.bfloat16)
     all_tokens = normed_all.reshape(frame_count, -1, channels)
     normed = rms_scale(features).astype(jnp.bfloat16)
@@ -100,9 +95,6 @@
     queries = project_rows(normed_tokens, w_query)
     keys_all = project_rows(all_tokens, w_key)
     values_all = project_rows(all_tokens, w_value)
-    keys_all, values_all, first_cache_pad, second_cache_pad = lax.optimization_barrier(
-        (keys_all, values_all, first_cache_pad, second_cache_pad)
-    )
     score_scale = 1.0 / math.sqrt(channels)
     scores = (
         jnp.einsum("fqc,fkc->fqk", queries, keys_all, preferred_element_type=jnp.float32)
@@ -124,7 +116,8 @@
         + projected.reshape(frame_count, row_count, width_count, channels)
     ).astype(jnp.bfloat16)
     first_in = jax.nn.silu(rms_scale(mixed)).astype(jnp.bfloat16)
-    first_padded = jnp.concatenate([first_cache_pad, extended(first_in, 1, 1)], axis=0)
+    first_stack = jnp.concatenate([first_cache, first_in], axis=0)
+    first_padded = extended(first_stack, 1, 1)
     block_out = (mixed.astype(jnp.float32) + conv_taps(first_padded, w_first, 3)).astype(
         jnp.bfloat16
     )
@@ -134,7 +127,8 @@
         jnp.bfloat16
     )
     second_in = jax.nn.silu(rms_scale(upsampled)).astype(jnp.bfloat16)
-    second_padded = jnp.concatenate([second_cache_pad, extended(second_in, 1, 1)], axis=0)
+    second_stack = jnp.concatenate([second_cache, second_in], axis=0)
+    second_padded = extended(second_stack, 1, 1)
     return (upsampled.astype(jnp.float32) + conv_taps(second_padded, w_second, 3)).astype(
         jnp.bfloat16
     )

time: 150 us -> 117 us (0.78)
  local copies, waits for them, and re-layouts: 39.5 us -> 13.9 us
  starting transfers between devices: 34.6 us -> 22.9 us
  waiting for transfers between devices: 39.8 us -> 43.5 us
    unnamed x63 -> x28, local copies, waits for them, and re-layouts: 11.4 us -> 1.43 us
    ppermute x5 -> x3, starting transfers between devices: 14.5 us -> 6.02 us  [halo_rows(): before = lax.ppermute(last, 'ha', up)]
    slice x6, local copies, waits for them, and re-layouts: 13.5 us -> 5.41 us  [conv_taps(): kernel = weight[time_off, row_off].reshape(3 * in_channels, out_channels)]
    ppermute x7, waiting for transfers between devices: 24.7 us -> 30 us  [gather_rows(): pieces.append(lax.ppermute(x, 'ha', pairs))]
    dot_general x0 -> x1, matrix products: none -> 4.95 us  [per_device(): jnp.einsum('fqk,fkc->fqc', weights.astype(jnp.bfloat16), values_all, pref...]
    dot_general x2 -> x1, matrix products: 5.79 us -> 1.01 us  [project_rows(): jnp.einsum('ftc,cd->ftd', tokens, weight, preferred_element_type=jnp.floa...]
    ppermute x5 -> x3, waiting for transfers between devices: 14.7 us -> 10 us  [halo_rows(): after = lax.ppermute(first, 'ha', down)]
    another operation x3, local copies, waits for them, and re-layouts: 6.32 us -> 1.9 us  [conv_taps(): kernel = weight[time_off, row_off].reshape(3 * in_channels, out_channels)]
  transfers between devices with their start and end apart: 18 -> 14, of which waited for: 9 -> 10; matrix products, arithmetic and copies ran while one was open for 24% -> 9% of each run, Pallas kernels for 0% -> 0%
where the time goes in v7:
time: 117 us; the launch traced here: 115 us
  waiting for transfers between devices  43.5 us (37%)
  matrix products  25.8 us (22%)
  starting transfers between devices  22.9 us (20%)
  local copies, waits for them, and re-layouts  13.9 us (12%)
  other arithmetic  7.92 us (7%)
    ppermute x7, waiting for transfers between devices, gather_rows(): pieces.append(lax.ppermute(x, 'ha', pairs))  30 us
    dot_general x21, matrix products, conv_taps(): jnp.einsum('fhwc,cd->fhwd', stacked, kernel, preferred_element_type=jnp.f...  13.2 us
    ppermute x3, waiting for transfers between devices, halo_rows(): after = lax.ppermute(first, 'ha', down)  10 us
    ppermute x3, starting transfers between devices, halo_rows(): after = lax.ppermute(first, 'ha', down)  9.13 us
    ppermute x7, starting transfers between devices, gather_rows(): pieces.append(lax.ppermute(x, 'ha', pairs))  7.15 us
    ppermute x3, starting transfers between devices, halo_rows(): before = lax.ppermute(last, 'ha', up)  6.02 us
    slice x6, local copies, waits for them, and re-layouts, conv_taps(): kernel = weight[time_off, row_off].reshape(3 * in_channels, out_channels)  5.41 us
    dot_general x1, matrix products, per_device(): jnp.einsum('fqc,fkc->fqk', queries, keys_all, preferred_element_type=jnp....  5.21 us
  transfers between devices with their start and end apart: 14, of which 10 were waited for; matrix products, arithmetic and copies ran while one was open for 9% of the time, Pallas kernels for 0%

profile of v7, /device:TPU:13, one launch (start us, length us, event | category | flops | bytes accessed | tf_op | source)
XLA Modules:
  0.0 114.7 jit_solution(13386830305067955253)
XLA Ops:
  0.0 1.2 %collective-permute-start = (bf16[2,1,128,384]{3,2,1,0:T(8,128)(2,1)}, bf16[2,1,128,384]{3,2,1,0:T(8,128)(2,1)S(1)}, u32[]{:S(2)}, u32[]{:S(2)}) collective-permute-start(bf16[2,1,128,384]{3,2,1,0:T(8,128)(2,1)} %param.10), channel_id=1, source_target_pairs={{0,2},{1,3},{2,4},{3,5},{4,6},{5,7},{6,8},{7,9},{8,10},{9,11},{10,... | collective-permute-start | bytes 589832 | tf_op jit(solution)/shard_map/ppermute | solution.py:33
  1.2 1.3 %collective-permute-start.1 = (bf16[2,1,128,384]{3,2,1,0:T(8,128)(2,1)}, bf16[2,1,128,384]{3,2,1,0:T(8,128)(2,1)S(1)}, u32[]{:S(2)}, u32[]{:S(2)}) collective-permute-start(bf16[2,1,128,384]{3,2,1,0:T(8,128)(2,1)} %param.10), channel_id=1, source_target_pairs={{0,4},{1,5},{2,6},{3,7},{4,8},{5,9},{6,10},{7,11},{8,12},{9,13},{1... | collective-permute-start | bytes 589832 | tf_op jit(solution)/shard_map/ppermute | solution.py:33
  2.5 1.0 collective-permute-start.2
  3.5 1.3 %collective-permute-start.3 = (bf16[2,1,128,384]{3,2,1,0:T(8,128)(2,1)}, bf16[2,1,128,384]{3,2,1,0:T(8,128)(2,1)S(1)}, u32[]{:S(2)}, u32[]{:S(2)}) collective-permute-start(bf16[2,1,128,384]{3,2,1,0:T(8,128)(2,1)} %param.10), channel_id=1, source_target_pairs={{0,8},{1,9},{2,10},{3,11},{4,12},{5,13},{6,14},{7,15},{8,0},{9,1},... | collective-permute-start | bytes 589832 | tf_op jit(solution)/shard_map/ppermute | solution.py:33
  4.8 1.0 collective-permute-start.4
  5.9 1.0 constant_dynamic-update-slice_fusion.7
  6.9 1.3 %collective-permute-start.5 = (bf16[2,1,128,384]{3,2,1,0:T(8,128)(2,1)}, bf16[2,1,128,384]{3,2,1,0:T(8,128)(2,1)S(1)}, u32[]{:S(2)}, u32[]{:S(2)}) collective-permute-start(bf16[2,1,128,384]{3,2,1,0:T(8,128)(2,1)} %param.10), channel_id=1, source_target_pairs={{0,12},{1,13},{2,14},{3,15},{4,0},{5,1},{6,2},{7,3},{8,4},{9,5},{1... | collective-permute-start | bytes 589832 | tf_op jit(solution)/shard_map/ppermute | solution.py:33
  8.2 1.9 %collective-permute-done.1 = bf16[2,1,128,384]{3,2,1,0:T(8,128)(2,1)S(1)} collective-permute-done((bf16[2,1,128,384]{3,2,1,0:T(8,128)(2,1)}, bf16[2,1,128,384]{3,2,1,0:T(8,128)(2,1)S(1)}, u32[]{:S(2)}, u32[]{:S(2)}) %collective-permute-start.1) | collective-permute-done | bytes 196640 | tf_op jit(solution)/shard_map/ppermute | solution.py:33
  10.2 20.2 %collective-permute-done.2 = bf16[2,1,128,384]{3,2,1,0:T(8,128)(2,1)S(1)} collective-permute-done((bf16[2,1,128,384]{3,2,1,0:T(8,128)(2,1)}, bf16[2,1,128,384]{3,2,1,0:T(8,128)(2,1)S(1)}, u32[]{:S(2)}, u32[]{:S(2)}) %collective-permute-start.2) | collective-permute-done | bytes 196640 | tf_op jit(solution)/shard_map/ppermute | solution.py:33
  30.5 4.1 %collective-permute-done.3 = bf16[2,1,128,384]{3,2,1,0:T(8,128)(2,1)S(1)} collective-permute-done((bf16[2,1,128,384]{3,2,1,0:T(8,128)(2,1)}, bf16[2,1,128,384]{3,2,1,0:T(8,128)(2,1)S(1)}, u32[]{:S(2)}, u32[]{:S(2)}) %collective-permute-start.3) | collective-permute-done | bytes 196640 | tf_op jit(solution)/shard_map/ppermute | solution.py:33
  34.8 2.7 %collective-permute-done.5 = bf16[2,1,128,384]{3,2,1,0:T(8,128)(2,1)S(1)} collective-permute-done((bf16[2,1,128,384]{3,2,1,0:T(8,128)(2,1)}, bf16[2,1,128,384]{3,2,1,0:T(8,128)(2,1)S(1)}, u32[]{:S(2)}, u32[]{:S(2)}) %collective-permute-start.5) | collective-permute-done | bytes 196640 | tf_op jit(solution)/shard_map/ppermute | solution.py:33
  37.5 1.1 collective-permute-done.6
  38.7 0.6 collective-permute-start.7
  39.4 1.0 convolution_convert_fusion.2
  40.4 1.9 %collective-permute-done.7 = bf16[2,8,128,384]{3,2,1,0:T(8,128)(2,1)S(1)} collective-permute-done((bf16[2,8,128,384]{3,2,1,0:T(8,128)(2,1)S(1)}, bf16[2,8,128,384]{3,2,1,0:T(8,128)(2,1)S(1)}, u32[]{:S(2)}, u32[]{:S(2)}) %collective-permute-start.7) | collective-permute-done | bytes 1572896 | tf_op jit(solution)/shard_map/ppermute | solution.py:36
  42.6 0.7 multiply_reduce_fusion
  43.3 0.7 fusion
  44.1 5.2 %fusion.189 = (f32[2,128]{1,0:T(2,128)S(1)}, f32[2,128,2048]{2,1,0:T(8,128)}) fusion(bf16[2,128,384]{2,1,0:T(8,128)(2,1)} %convolution_convert_fusion.2, bf16[2,2048,384]{2,1,0:T(8,128)(2,1)S(1)} %fusion, bf16[384,384]{1,0:T(8,128)(2,1)S(1)} %copy-done), kind=kOutput, calls=%fused_computation.265 | convolution fusion | flops 1613233920 | bytes 5735424 | tf_op jit(solution)/shard_map/fqc,fkc->fqk/dot_general | solution.py:100
  49.3 2.0 %fusion.25 = f32[2,128]{1,0:T(2,128)S(1)} fusion(f32[2,128,2048]{2,1,0:T(8,128)} %get-tuple-element.103, f32[2,128]{1,0:T(2,128)S(1)} %get-tuple-element.102), kind=kLoop, calls=%fused_computation.37 | loop fusion | flops 1048320 | bytes 2099200 | tf_op jit(solution)/shard_map/reduce_sum | solution.py:105
  51.3 4.9 %fusion.99 = bf16[2,128,384]{2,1,0:T(8,128)(2,1)} fusion(bf16[2,2048,384]{2,1,0:T(8,128)(2,1)S(1)} %fusion, f32[2,128,2048]{2,1,0:T(8,128)} %get-tuple-element.103, f32[2,128]{1,0:T(2,128)S(1)} %get-tuple-element.102, bf16[384,384]{1,0:T(8,128)(2,1)} %param.15, f32[2,128]{1,0:T(2,128)S(1)} %fusion.25), kind=kOutput, calls=%fused_computation.125 | convolution fusion | flops 1613430784 | bytes 5736448 | tf_op jit(solution)/shard_map/fqk,fkc->fqc/dot_general | solution.py:106
  56.2 1.4 %multiply_reduce_fusion.2 = (f32[2,128]{1,0:T(2,128)S(1)}, f32[2,1,128,384]{3,2,0,1:T(8,128)S(1)}) fusion(bf16[2,128,384]{2,1,0:T(8,128)(2,1)} %fusion.99, bf16[384,384]{1,0:T(8,128)(2,1)} %param.16, bf16[2,1,128,384]{3,2,1,0:T(8,128)(2,1)S(1)} %copy-done.4), kind=kOutput, calls=%fused_computation.204 | convolution fusion | flops 76087040 | bytes 1082368 | tf_op jit(solution)/shard_map/ftc,cd->ftd/dot_general | solution.py:113
  57.9 1.0 pad_maximum_fusion.4
  58.9 2.1 %collective-permute-start.8 = (bf16[4,1,128,384]{3,2,0,1:T(8,128)(2,1)S(1)}, bf16[4,1,128,384]{3,2,0,1:T(8,128)(2,1)S(1)}, u32[]{:S(2)}, u32[]{:S(2)}) collective-permute-start(bf16[4,1,128,384]{3,2,0,1:T(8,128)(2,1)S(1)} %pad_maximum_fusion.4), channel_id=1, source_target_pairs={{0,1},{1,2},{2,3},{3,4},{4,5},{5,6},{6,7},{7,8},{8,9},{9,10},{10,1... | collective-permute-start | bytes 1179656 | tf_op jit(solution)/shard_map/ppermute | solution.py:15
  60.9 2.6 %collective-permute-start.9 = (bf16[4,1,128,384]{3,2,0,1:T(8,128)(2,1)S(1)}, bf16[4,1,128,384]{3,2,0,1:T(8,128)(2,1)S(1)}, u32[]{:S(2)}, u32[]{:S(2)}) collective-permute-start(bf16[4,1,128,384]{3,2,0,1:T(8,128)(2,1)S(1)} %pad_maximum_fusion.4), channel_id=1, source_target_pairs={{1,0},{2,1},{3,2},{4,3},{5,4},{6,5},{7,6},{8,7},{9,8},{10,9},{11,1... | collective-permute-start | bytes 1179656 | tf_op jit(solution)/shard_map/ppermute | solution.py:16
  63.5 3.9 %fusion.180 = (bf16[1,1,3,384,384]{4,3,2,1,0:T(8,128)(2,1)S(1)}, bf16[1,1,3,384,384]{4,3,2,1,0:T(8,128)(2,1)S(1)}, bf16[1,1,3,384,384]{4,3,2,1,0:T(8,128)(2,1)S(...) fusion(bf16[3,3,3,384,384]{4,3,2,1,0:T(8,128)(2,1)} %param.17), kind=kLoop, calls=%fused_computation.256 | loop fusion | bytes 15925248 | tf_op jit(solution)/shard_map/slice | solution.py:64
  67.5 3.5 %collective-permute-done.9 = bf16[4,1,128,384]{3,2,0,1:T(8,128)(2,1)S(1)} collective-permute-done((bf16[4,1,128,384]{3,2,0,1:T(8,128)(2,1)S(1)}, bf16[4,1,128,384]{3,2,0,1:T(8,128)(2,1)S(1)}, u32[]{:S(2)}, u32[]{:S(2)}) %collective-permute-start.9) | collective-permute-done | bytes 393248 | tf_op jit(solution)/shard_map/ppermute | solution.py:16
  71.4 0.7 fusion.184
  76.5 1.9 %collective-permute-start.10 = (bf16[2,1,128,384]{3,2,0,1:T(8,128)(2,1)S(1)}, bf16[2,1,128,384]{3,2,0,1:T(8,128)(2,1)S(1)}, u32[]{:S(2)}, u32[]{:S(2)}) collective-permute-start(bf16[2,1,128,384]{3,2,0,1:T(8,128)(2,1)S(1)} %fusion.95), channel_id=1, source_target_pairs={{0,1},{1,2},{2,3},{3,4},{4,5},{5,6},{6,7},{7,8},{8,9},{9,10},{10,1... | collective-permute-start | bytes 589832 | tf_op jit(solution)/shard_map/ppermute | solution.py:15
  78.5 3.6 %collective-permute-start.11 = (bf16[2,1,128,384]{3,2,0,1:T(8,128)(2,1)S(1)}, bf16[2,1,128,384]{3,2,0,1:T(8,128)(2,1)S(1)}, u32[]{:S(2)}, u32[]{:S(2)}) collective-permute-start(bf16[2,1,128,384]{3,2,0,1:T(8,128)(2,1)S(1)} %fusion.95), channel_id=1, source_target_pairs={{1,0},{2,1},{3,2},{4,3},{5,4},{6,5},{7,6},{8,7},{9,8},{10,9},{11,1... | collective-permute-start | bytes 589832 | tf_op jit(solution)/shard_map/ppermute | solution.py:16
  82.6 1.1 %reshape.136 = bf16[1152,192,1,1]{0,1,2,3:T(8,128)(2,1)} reshape(bf16[1,1,3,384,192]{3,2,4,1,0:T(4,128)(2,1)S(1)} %copy.32) | data formatting | bytes 884736 | tf_op jit(solution)/shard_map/reshape;squeeze | solution.py:64
  85.3 1.2 %collective-permute-done.11 = bf16[2,1,128,384]{3,2,0,1:T(8,128)(2,1)S(1)} collective-permute-done((bf16[2,1,128,384]{3,2,0,1:T(8,128)(2,1)S(1)}, bf16[2,1,128,384]{3,2,0,1:T(8,128)(2,1)S(1)}, u32[]{:S(2)}, u32[]{:S(2)}) %collective-permute-start.11) | collective-permute-done | bytes 196640 | tf_op jit(solution)/shard_map/ppermute | solution.py:16
  86.6 0.6 broadcast_in_dim.4
  87.9 0.8 pad_slice_fusion.9
  89.0 1.2 %fusion.7 = f32[2,2,256,192]{2,3,1,0:T(8,128)S(1)} fusion(bf16[2,1,258,384]{3,2,1,0:T(8,128)(2,1)S(1)} %pad_slice_fusion.10, bf16[2,2,256,384]{3,2,1,0:T(8,128)(2,1)S(1)} %get-tuple-element.79, bf16[2,2,256,384]{3,2,1,0:T(8,128)(2,1)S(1)} %get-tuple-element.78, bf16[1152,192,1,1]{0,1,2,3:T(8,128)(2,1)S(1)} %copy-done.8), kind=kOutput, calls=%fused_computation.19 | convolution fusion | flops 462422016 | bytes 3197952 | tf_op jit(solution)/shard_map/fhwc,cd->fhwd/dot_general | solution.py:65
  90.2 1.1 fusion.32
  91.3 1.2 %multiply_reduce_fusion.1 = (f32[2,2,256]{2,1,0:T(2,128)S(1)}, f32[2,2,256,192]{2,3,1,0:T(8,128)S(1)}) fusion(f32[2,2,256,192]{2,3,1,0:T(8,128)S(1)} %fusion.32, bf16[1152,192,1,1]{0,1,2,3:T(8,128)(2,1)S(1)} %reshape.137, bf16[2,2,256,384]{3,2,1,0:T(8,128)(2,1)S(1)} %get-tuple-element.70, bf16[2,2,256,384]{3,2,1,0:T(8,128)(2,1)S(1)} %get-tuple-element.71, ...), kind=kOutput, calls=%fused_computation.138 | convolution fusion | flops 461044736 | bytes 4378624 | tf_op jit(solution)/shard_map/fhwc,cd->fhwd/dot_general | solution.py:65
  92.8 2.1 %collective-permute-start.12 = (bf16[4,1,256,192]{2,3,1,0:T(8,128)(2,1)S(1)}, bf16[4,1,256,192]{2,3,1,0:T(8,128)(2,1)S(1)}, u32[]{:S(2)}, u32[]{:S(2)}) collective-permute-start(bf16[4,1,256,192]{2,3,1,0:T(8,128)(2,1)S(1)} %get-tuple-element.76), channel_id=1, source_target_pairs={{0,1},{1,2},{2,3},{3,4},{4,5},{5,6},{6,7},{7,8},{8,9},{9,10},{10,1... | collective-permute-start | bytes 1179656 | tf_op jit(solution)/shard_map/ppermute | solution.py:15
  94.9 3.0 %collective-permute-start.13 = (bf16[4,1,256,192]{2,3,1,0:T(8,128)(2,1)S(1)}, bf16[4,1,256,192]{2,3,1,0:T(8,128)(2,1)S(1)}, u32[]{:S(2)}, u32[]{:S(2)}) collective-permute-start(bf16[4,1,256,192]{2,3,1,0:T(8,128)(2,1)S(1)} %get-tuple-element.77), channel_id=1, source_target_pairs={{1,0},{2,1},{3,2},{4,3},{5,4},{6,5},{7,6},{8,7},{9,8},{10,9},{11,1... | collective-permute-start | bytes 1179656 | tf_op jit(solution)/shard_map/ppermute | solution.py:16
  98.1 1.5 %collective-permute-done.12 = bf16[4,1,256,192]{2,3,1,0:T(8,128)(2,1)S(1)} collective-permute-done((bf16[4,1,256,192]{2,3,1,0:T(8,128)(2,1)S(1)}, bf16[4,1,256,192]{2,3,1,0:T(8,128)(2,1)S(1)}, u32[]{:S(2)}, u32[]{:S(2)}) %collective-permute-start.12) | collective-permute-done | bytes 393248 | tf_op jit(solution)/shard_map/ppermute | solution.py:15
  99.6 5.4 %collective-permute-done.13 = bf16[4,1,256,192]{2,3,1,0:T(8,128)(2,1)S(1)} collective-permute-done((bf16[4,1,256,192]{2,3,1,0:T(8,128)(2,1)S(1)}, bf16[4,1,256,192]{2,3,1,0:T(8,128)(2,1)S(1)}, u32[]{:S(2)}, u32[]{:S(2)}) %collective-permute-start.13) | collective-permute-done | bytes 393248 | tf_op jit(solution)/shard_map/ppermute | solution.py:16
  105.0 2.0 %select_maximum_fusion = bf16[4,4,258,192]{2,3,1,0:T(8,128)(2,1)S(1)} fusion(bf16[4,1,256,192]{2,3,1,0:T(8,128)(2,1)S(1)} %collective-permute-done.13, bf16[4,1,256,192]{2,3,1,0:T(8,128)(2,1)S(1)} %collective-permute-done.12, bf16[2,2,256,192]{2,3,1,0:T(8,128)(2,1)S(1)} %multiply_convert_fusion, bf16[2,2,256,192]{2,3,1,0:T(8,128)(2,1)S(1)} %copy-done.2), kind=kLoop, calls=%fused_computation.12 | loop fusion | flops 11888640 | bytes 3158016 | tf_op jit(solution)/shard_map/concatenate | solution.py:22
  107.0 1.7 %fusion.182 = (bf16[2,2,256,192]{2,3,1,0:T(8,128)(2,1)S(1)}, bf16[2,2,256,192]{2,3,1,0:T(8,128)(2,1)S(1)}, bf16[2,2,256,192]{2,3,1,0:T(8,128)(2,1)S(1)}, bf16[2,...) fusion(bf16[4,4,258,192]{2,3,1,0:T(8,128)(2,1)S(1)} %select_max, ...), kind=kLoop, calls=%fused_computation.258 | loop fusion | bytes 14155776 | tf_op jit(solution)/shard_map/slice | solution.py:62
  109.1 0.5 fusion.57
  109.6 0.5 convolution_add_fusion.7
  111.2 0.5 convolution_add_fusion.4
  112.3 0.5 convolution_add_fusion.2
  112.8 0.5 convolution_add_fusion.1
  113.3 1.3 %fusion.44 = bf16[2,2,256,192]{2,3,1,0:T(8,128)(2,1)} fusion(f32[2,2,256,192]{2,3,1,0:T(8,128)S(1)} %get-tuple-element.107, f32[2,2,256,192]{2,3,1,0:T(8,128)S(1)} %convolution_add_fusion.1, bf16[576,192,1,1]{1,0,3,2:T(8,128)(2,1)S(1)} %bitcast.188, bf16[2,2,256,192]{2,3,1,0:T(8,128)(2,1)S(1)} %get-tuple-element.40, ...), kind=kOutput, calls=%fused_computation.58 | convolution fusion | flops 230621184 | bytes 3366912 | tf_op jit(solution)/shard_map/fhwc,cd->fhwd/dot_general | solution.py:65
  (72 shorter events, 11.4 us)
Async XLA Ops:
  0.0 44.0 %copy-start = (bf16[384,384]{1,0:T(8,128)(2,1)S(1)}, bf16[384,384]{1,0:T(8,128)(2,1)}, u32[]{:S(2)}) copy-start(bf16[384,384]{1,0:T(8,128)(2,1)} %param.14) | copy-start | bytes 884740
  0.0 6.9 %collective-permute-start = (bf16[2,1,128,384]{3,2,1,0:T(8,128)(2,1)}, bf16[2,1,128,384]{3,2,1,0:T(8,128)(2,1)S(1)}, u32[]{:S(2)}, u32[]{:S(2)}) collective-permute-start(bf16[2,1,128,384]{3,2,1,0:T(8,128)(2,1)} %param.10), channel_id=1, source_target_pairs={{0,2},{1,3},{2,4},{3,5},{4,6},{5,7},{6,8},{7,9},{8,10},{9,11},{10,... | collective-permute-start | bytes 589832 | tf_op jit(solution)/shard_map/ppermute | solution.py:33
  1.2 8.9 %collective-permute-start.1 = (bf16[2,1,128,384]{3,2,1,0:T(8,128)(2,1)}, bf16[2,1,128,384]{3,2,1,0:T(8,128)(2,1)S(1)}, u32[]{:S(2)}, u32[]{:S(2)}) collective-permute-start(bf16[2,1,128,384]{3,2,1,0:T(8,128)(2,1)} %param.10), channel_id=1, source_target_pairs={{0,4},{1,5},{2,6},{3,7},{4,8},{5,9},{6,10},{7,11},{8,12},{9,13},{1... | collective-permute-start | bytes 589832 | tf_op jit(solution)/shard_map/ppermute | solution.py:33
  2.5 27.9 %collective-permute-start.2 = (bf16[2,1,128,384]{3,2,1,0:T(8,128)(2,1)}, bf16[2,1,128,384]{3,2,1,0:T(8,128)(2,1)S(1)}, u32[]{:S(2)}, u32[]{:S(2)}) collective-permute-start(bf16[2,1,128,384]{3,2,1,0:T(8,128)(2,1)} %param.10), channel_id=1, source_target_pairs={{0,6},{1,7},{2,8},{3,9},{4,10},{5,11},{6,12},{7,13},{8,14},{9,15},... | collective-permute-start | bytes 589832 | tf_op jit(solution)/shard_map/ppermute | solution.py:33
  3.5 31.1 %collective-permute-start.3 = (bf16[2,1,128,384]{3,2,1,0:T(8,128)(2,1)}, bf16[2,1,128,384]{3,2,1,0:T(8,128)(2,1)S(1)}, u32[]{:S(2)}, u32[]{:S(2)}) collective-permute-start(bf16[2,1,128,384]{3,2,1,0:T(8,128)(2,1)} %param.10), channel_id=1, source_target_pairs={{0,8},{1,9},{2,10},{3,11},{4,12},{5,13},{6,14},{7,15},{8,0},{9,1},... | collective-permute-start | bytes 589832 | tf_op jit(solution)/shard_map/ppermute | solution.py:33
  4.8 29.8 %collective-permute-start.4 = (bf16[2,1,128,384]{3,2,1,0:T(8,128)(2,1)}, bf16[2,1,128,384]{3,2,1,0:T(8,128)(2,1)S(1)}, u32[]{:S(2)}, u32[]{:S(2)}) collective-permute-start(bf16[2,1,128,384]{3,2,1,0:T(8,128)(2,1)} %param.10), channel_id=1, source_target_pairs={{0,10},{1,11},{2,12},{3,13},{4,14},{5,15},{6,0},{7,1},{8,2},{9,3},... | collective-permute-start | bytes 589832 | tf_op jit(solution)/shard_map/ppermute | solution.py:33
  6.9 32.4 %copy-start.3 = (bf16[2,1,128,384]{3,2,1,0:T(8,128)(2,1)S(1)}, bf16[2,1,128,384]{3,2,1,0:T(8,128)(2,1)}, u32[]{:S(2)}) copy-start(bf16[2,1,128,384]{3,2,1,0:T(8,128)(2,1)} %param.10) | copy-start | bytes 589828
  6.9 30.6 %collective-permute-start.5 = (bf16[2,1,128,384]{3,2,1,0:T(8,128)(2,1)}, bf16[2,1,128,384]{3,2,1,0:T(8,128)(2,1)S(1)}, u32[]{:S(2)}, u32[]{:S(2)}) collective-permute-start(bf16[2,1,128,384]{3,2,1,0:T(8,128)(2,1)} %param.10), channel_id=1, source_target_pairs={{0,12},{1,13},{2,14},{3,15},{4,0},{5,1},{6,2},{7,3},{8,4},{9,5},{1... | collective-permute-start | bytes 589832 | tf_op jit(solution)/shard_map/ppermute | solution.py:33
  8.2 31.2 %copy-start.9 = (bf16[384,384]{1,0:T(8,128)(2,1)S(1)}, bf16[384,384]{1,0:T(8,128)(2,1)}, u32[]{:S(2)}) copy-start(bf16[384,384]{1,0:T(8,128)(2,1)} %param.13) | copy-start | bytes 884740
  10.1 28.5 %collective-permute-start.6 = (bf16[2,1,128,384]{3,2,1,0:T(8,128)(2,1)}, bf16[2,1,128,384]{3,2,1,0:T(8,128)(2,1)S(1)}, u32[]{:S(2)}, u32[]{:S(2)}) collective-permute-start(bf16[2,1,128,384]{3,2,1,0:T(8,128)(2,1)} %param.10), channel_id=1, source_target_pairs={{0,14},{1,15},{2,0},{3,1},{4,2},{5,3},{6,4},{7,5},{8,6},{9,7},{10,... | collective-permute-start | bytes 589832 | tf_op jit(solution)/shard_map/ppermute | solution.py:33
  38.7 3.6 %collective-permute-start.7 = (bf16[2,8,128,384]{3,2,1,0:T(8,128)(2,1)S(1)}, bf16[2,8,128,384]{3,2,1,0:T(8,128)(2,1)S(1)}, u32[]{:S(2)}, u32[]{:S(2)}) collective-permute-start(bf16[2,8,128,384]{3,2,1,0:T(8,128)(2,1)S(1)} %get-tuple-element.86), channel_id=1, source_target_pairs={{0,1},{1,0},{2,3},{3,2},{4,5},{5,4},{6,7},{7,6},{8,9},{9,8},{10,11... | collective-permute-start | bytes 4718600 | tf_op jit(solution)/shard_map/ppermute | solution.py:36
  51.3 5.0 %copy-start.4 = (bf16[2,1,128,384]{3,2,1,0:T(8,128)(2,1)S(1)}, bf16[2,1,128,384]{3,2,1,0:T(8,128)(2,1)}, u32[]{:S(2)}) copy-start(bf16[2,1,128,384]{3,2,1,0:T(8,128)(2,1)} %param.10) | copy-start | bytes 589828
  58.9 8.6 %copy-start.6 = (bf16[2,1,128,384]{3,2,1,0:T(8,128)(2,1)S(1)}, bf16[2,1,128,384]{3,2,1,0:T(8,128)(2,1)}, u32[]{:S(2)}) copy-start(bf16[2,1,128,384]{3,2,1,0:T(8,128)(2,1)} %param.11) | copy-start | bytes 589828
  58.9 8.7 %collective-permute-start.8 = (bf16[4,1,128,384]{3,2,0,1:T(8,128)(2,1)S(1)}, bf16[4,1,128,384]{3,2,0,1:T(8,128)(2,1)S(1)}, u32[]{:S(2)}, u32[]{:S(2)}) collective-permute-start(bf16[4,1,128,384]{3,2,0,1:T(8,128)(2,1)S(1)} %pad_maximum_fusion.4), channel_id=1, source_target_pairs={{0,1},{1,2},{2,3},{3,4},{4,5},{5,6},{6,7},{7,8},{8,9},{9,10},{10,1... | collective-permute-start | bytes 1179656 | tf_op jit(solution)/shard_map/ppermute | solution.py:15
  60.9 10.1 %collective-permute-start.9 = (bf16[4,1,128,384]{3,2,0,1:T(8,128)(2,1)S(1)}, bf16[4,1,128,384]{3,2,0,1:T(8,128)(2,1)S(1)}, u32[]{:S(2)}, u32[]{:S(2)}) collective-permute-start(bf16[4,1,128,384]{3,2,0,1:T(8,128)(2,1)S(1)} %pad_maximum_fusion.4), channel_id=1, source_target_pairs={{1,0},{2,1},{3,2},{4,3},{5,4},{6,5},{7,6},{8,7},{9,8},{10,9},{11,1... | collective-permute-start | bytes 1179656 | tf_op jit(solution)/shard_map/ppermute | solution.py:16
  76.0 6.0 %copy-start.7 = (bf16[3,3,384,192]{2,3,1,0:T(8,128)(2,1)S(1)}, bf16[3,3,384,192]{2,3,1,0:T(8,128)(2,1)}, u32[]{:S(2)}) copy-start(bf16[3,3,384,192]{2,3,1,0:T(8,128)(2,1)} %param.18) | copy-start | bytes 3981316
  76.5 8.7 %collective-permute-start.10 = (bf16[2,1,128,384]{3,2,0,1:T(8,128)(2,1)S(1)}, bf16[2,1,128,384]{3,2,0,1:T(8,128)(2,1)S(1)}, u32[]{:S(2)}, u32[]{:S(2)}) collective-permute-start(bf16[2,1,128,384]{3,2,0,1:T(8,128)(2,1)S(1)} %fusion.95), channel_id=1, source_target_pairs={{0,1},{1,2},{2,3},{3,4},{4,5},{5,6},{6,7},{7,8},{8,9},{9,10},{10,1... | collective-permute-start | bytes 589832 | tf_op jit(solution)/shard_map/ppermute | solution.py:15
  78.5 8.0 %collective-permute-start.11 = (bf16[2,1,128,384]{3,2,0,1:T(8,128)(2,1)S(1)}, bf16[2,1,128,384]{3,2,0,1:T(8,128)(2,1)S(1)}, u32[]{:S(2)}, u32[]{:S(2)}) collective-permute-start(bf16[2,1,128,384]{3,2,0,1:T(8,128)(2,1)S(1)} %fusion.95), channel_id=1, source_target_pairs={{1,0},{2,1},{3,2},{4,3},{5,4},{6,5},{7,6},{8,7},{9,8},{10,9},{11,1... | collective-permute-start | bytes 589832 | tf_op jit(solution)/shard_map/ppermute | solution.py:16
  87.8 1.1 copy-start.8
  91.3 1.4 %copy-start.2 = (bf16[2,2,256,192]{2,3,1,0:T(8,128)(2,1)S(1)}, bf16[2,2,256,192]{2,3,1,0:T(8,128)(2,1)}, u32[]{:S(2)}) copy-start(bf16[2,2,256,192]{2,3,1,0:T(8,128)(2,1)} %param.12) | copy-start | bytes 1179652
  92.5 5.4 %copy-start.5 = (bf16[3,3,3,192,192]{4,3,2,1,0:T(8,128)(2,1)S(1)}, bf16[3,3,3,192,192]{4,3,2,1,0:T(8,128)(2,1)}, u32[]{:S(2)}) copy-start(bf16[3,3,3,192,192]{4,3,2,1,0:T(8,128)(2,1)} %param.19) | copy-start | bytes 5971972
  92.8 6.8 %collective-permute-start.12 = (bf16[4,1,256,192]{2,3,1,0:T(8,128)(2,1)S(1)}, bf16[4,1,256,192]{2,3,1,0:T(8,128)(2,1)S(1)}, u32[]{:S(2)}, u32[]{:S(2)}) collective-permute-start(bf16[4,1,256,192]{2,3,1,0:T(8,128)(2,1)S(1)} %get-tuple-element.76), channel_id=1, source_target_pairs={{0,1},{1,2},{2,3},{3,4},{4,5},{5,6},{6,7},{7,8},{8,9},{9,10},{10,1... | collective-permute-start | bytes 1179656 | tf_op jit(solution)/shard_map/ppermute | solution.py:15
  94.9 10.1 %collective-permute-start.13 = (bf16[4,1,256,192]{2,3,1,0:T(8,128)(2,1)S(1)}, bf16[4,1,256,192]{2,3,1,0:T(8,128)(2,1)S(1)}, u32[]{:S(2)}, u32[]{:S(2)}) collective-permute-start(bf16[4,1,256,192]{2,3,1,0:T(8,128)(2,1)S(1)} %get-tuple-element.77), channel_id=1, source_target_pairs={{1,0},{2,1},{3,2},{4,3},{5,4},{6,5},{7,6},{8,7},{9,8},{10,9},{11,1... | collective-permute-start | bytes 1179656 | tf_op jit(solution)/shard_map/ppermute | solution.py:16
  113.3 1.3 %copy-start.1 = (bf16[384,384]{1,0:T(8,128)(2,1)S(1)}, bf16[384,384]{1,0:T(8,128)(2,1)}, u32[]{:S(2)}) copy-start(bf16[384,384]{1,0:T(8,128)(2,1)} %param.14) | copy-start | bytes 884740

commit v8 on v7

--- a/solution.py
+++ b/solution.py
@@ -34,7 +34,7 @@
     own_chip = jnp.concatenate(pieces, axis=1)
     swap = [(2 * c + k, 2 * c + 1 - k) for c in range(chips) for k in range(2)]
     other = lax.ppermute(own_chip, "ha", swap)
-    return jnp.concatenate([own_chip, other], axis=1)
+    return pieces + [other]
 
 
 def rms_scale(tensor):
@@ -87,19 +87,21 @@
     w_second,
 ):
     frame_count, row_count, width_count, channels = features.shape
-    every_row = gather_rows(features)
-    normed_all = rms_scale(every_row).astype(jnp.bfloat16)
-    all_tokens = normed_all.reshape(frame_count, -1, channels)
     normed = rms_scale(features).astype(jnp.bfloat16)
     normed_tokens = normed.reshape(frame_count, row_count * width_count, channels)
     queries = project_rows(normed_tokens, w_query)
-    keys_all = project_rows(all_tokens, w_key)
-    values_all = project_rows(all_tokens, w_value)
     score_scale = 1.0 / math.sqrt(channels)
-    scores = (
-        jnp.einsum("fqc,fkc->fqk", queries, keys_all, preferred_element_type=jnp.float32)
-        * score_scale
-    )
+    score_parts, value_parts = [], []
+    for piece in gather_rows(features):
+        piece_tokens = rms_scale(piece).astype(jnp.bfloat16).reshape(frame_count, -1, channels)
+        piece_keys = project_rows(piece_tokens, w_key)
+        value_parts.append(project_rows(piece_tokens, w_value))
+        score_parts.append(
+            jnp.einsum("fqc,fkc->fqk", queries, piece_keys, preferred_element_type=jnp.float32)
+            * score_scale
+        )
+    scores = jnp.concatenate(score_parts, axis=-1)
+    values_all = jnp.concatenate(value_parts, axis=1)
     largest = jnp.max(scores, axis=-1)
     weights = jnp.exp(scores - largest[..., None])
     weight_sum = jnp.sum(weights, axis=-1)

time: 117 us -> 136 us (1.16)
  local copies, waits for them, and re-layouts: 13.9 us -> 34.3 us
  waiting for transfers between devices: 43.5 us -> 26.7 us
  matrix products: 25.8 us -> 40.3 us
  starting transfers between devices: 22.9 us -> 24.3 us
    ppermute x7, waiting for transfers between devices: 30 us -> 14.5 us  [gather_rows(): pieces.append(lax.ppermute(x, 'ha', pairs))]
    unnamed x28 -> x43, local copies, waits for them, and re-layouts: 1.43 us -> 15.9 us
    dot_general x1 -> x10, matrix products: 1.01 us -> 13.3 us  [project_rows(): jnp.einsum('ftc,cd->ftd', tokens, weight, preferred_element_type=jnp.floa...]
    mul x0 -> x8, local copies, waits for them, and re-layouts: none -> 5.61 us  [per_device(): jnp.einsum('fqc,fkc->fqk', queries, piece_keys, preferred_element_type=jn...]
    ppermute x1, waiting for transfers between devices: 1.88 us -> 0.01 us  [gather_rows(): other = lax.ppermute(own_chip, 'ha', swap)]
    reduce_sum x1, other arithmetic: 2.02 us -> 0.43 us  [per_device(): weight_sum = jnp.sum(weights, axis=-1)]
    dot_general x1, matrix products: 1.44 us -> 3 us  [per_device(): jnp.einsum('ftc,cd->ftd', attended, w_output, preferred_element_type=jnp....]
    reduce_sum x2 -> x9, other arithmetic: 0.81 us -> 2.27 us  [rms_scale(): jnp.mean(widened * widened, axis=-1, keepdims=True) + 1e-06]
  transfers between devices with their start and end apart: 14 -> 14, of which waited for: 10 -> 7; matrix products, arithmetic and copies ran while one was open for 9% -> 32% of each run, Pallas kernels for 0% -> 0%
where the time goes in v8:
time: 136 us; the launch traced here: 134 us
  matrix products  40.3 us (30%)
  local copies, waits for them, and re-layouts  34.3 us (25%)
  waiting for transfers between devices  26.7 us (20%)
  starting transfers between devices  24.3 us (18%)
  other arithmetic  7.74 us (6%)
    unnamed x43, local copies, waits for them, and re-layouts  15.9 us
    ppermute x7, waiting for transfers between devices, gather_rows(): pieces.append(lax.ppermute(x, 'ha', pairs))  14.5 us
    dot_general x10, matrix products, project_rows(): jnp.einsum('ftc,cd->ftd', tokens, weight, preferred_element_type=jnp.floa...  13.3 us
    dot_general x21, matrix products, conv_taps(): jnp.einsum('fhwc,cd->fhwd', stacked, kernel, preferred_element_type=jnp.f...  13.2 us
    dot_general x9, matrix products, per_device(): jnp.einsum('fqc,fkc->fqk', queries, piece_keys, preferred_element_type=jn...  10.8 us
    ppermute x3, waiting for transfers between devices, halo_rows(): after = lax.ppermute(first, 'ha', down)  10.4 us
    ppermute x7, starting transfers between devices, gather_rows(): pieces.append(lax.ppermute(x, 'ha', pairs))  8.56 us
    ppermute x3, starting transfers between devices, halo_rows(): after = lax.ppermute(first, 'ha', down)  8.41 us
  transfers between devices with their start and end apart: 14, of which 7 were waited for; matrix products, arithmetic and copies ran while one was open for 32% of the time, Pallas kernels for 0%

profile of v8, /device:TPU:13, one launch (start us, length us, event | category | flops | bytes accessed | tf_op | source)
XLA Modules:
  0.0 134.1 jit_solution(1827393427567054276)
XLA Ops:
  0.0 1.3 collective-permute-start
  1.3 1.3 collective-permute-start.1
  3.6 1.3 %collective-permute-start.3 = (bf16[2,1,128,384]{3,2,1,0:T(8,128)(2,1)}, bf16[2,1,128,384]{3,2,1,0:T(8,128)(2,1)S(1)}, u32[]{:S(2)}, u32[]{:S(2)}) collective-permute-start(bf16[2,1,128,384]{3,2,1,0:T(8,128)(2,1)} %param.10), channel_id=1, source_target_pairs={{0,8},{1,9},{2,10},{3,11},{4,12},{5,13},{6,14},{7,15},{8,0},{9,1},... | collective-permute-start | bytes 589832 | tf_op jit(solution)/shard_map/ppermute | solution.py:33
  4.9 1.0 collective-permute-start.4
  5.9 1.1 fusion.186
  7.0 1.6 %constant_dynamic-update-slice_fusion.7 = bf16[2,8,128,384]{3,2,1,0:T(8,128)(2,1)} fusion(bf16[2,1,128,384]{3,2,1,0:T(8,128)(2,1)} %param.10), kind=kLoop, calls=%fused_computation.312 | loop fusion | bytes 393216
  8.6 1.4 %convolution_convert_fusion.18 = bf16[2,128,384]{2,1,0:T(8,128)(2,1)S(1)} fusion(bf16[384,384]{1,0:T(8,128)(2,1)} %param.13, bf16[2,1,128,384]{3,2,1,0:T(8,128)(2,1)} %param.10, f32[2,128]{1,0:T(2,128)S(1)} %add_rsqrt_fusion.10), kind=kOutput, calls=%fused_computation.148 | convolution fusion | flops 75890688 | bytes 689152 | tf_op jit(solution)/shard_map/ftc,cd->ftd/dot_general | solution.py:72
  10.1 1.6 %fusion.317 = (f32[2,128]{1,0:T(2,128)S(1)}, f32[2,128,128]{1,2,0:T(8,128)S(1)}) fusion(bf16[2,128,384]{2,1,0:T(8,128)(2,1)S(1)} %convolution_convert_fusion.18, bf16[384,384]{1,0:T(8,128)(2,1)} %param.14, bf16[2,1,128,384]{3,2,1,0:T(8,128)(2,1)} %param.10, f32[2,128]{1,0:T(2,128)S(1)} %add_rsqrt_fusion.10), kind=kOutput, calls=%fused_computation.371 | convolution fusion | flops 101121792 | bytes 821248 | tf_op jit(solution)/shard_map/fqc,fkc->fqk/dot_general | solution.py:100
  13.5 1.3 collective-permute-start.5
  16.1 1.4 %collective-permute-start.6 = (bf16[2,1,128,384]{3,2,1,0:T(8,128)(2,1)S(1)}, bf16[2,1,128,384]{3,2,1,0:T(8,128)(2,1)S(1)}, u32[]{:S(2)}, u32[]{:S(2)}) collective-permute-start(bf16[2,1,128,384]{3,2,1,0:T(8,128)(2,1)S(1)} %copy-done.5), channel_id=1, source_target_pairs={{0,14},{1,15},{2,0},{3,1},{4,2},{5,3},{6,4},{7,5},{8,6},{9,7},{10,... | collective-permute-start | bytes 589832 | tf_op jit(solution)/shard_map/ppermute | solution.py:33
  18.9 11.6 %collective-permute-done.2 = bf16[2,1,128,384]{3,2,1,0:T(8,128)(2,1)S(1)} collective-permute-done((bf16[2,1,128,384]{3,2,1,0:T(8,128)(2,1)}, bf16[2,1,128,384]{3,2,1,0:T(8,128)(2,1)S(1)}, u32[]{:S(2)}, u32[]{:S(2)}) %collective-permute-start.2) | collective-permute-done | bytes 196640 | tf_op jit(solution)/shard_map/ppermute | solution.py:33
  31.9 2.8 %collective-permute-done.3 = bf16[2,1,128,384]{3,2,1,0:T(8,128)(2,1)S(1)} collective-permute-done((bf16[2,1,128,384]{3,2,1,0:T(8,128)(2,1)}, bf16[2,1,128,384]{3,2,1,0:T(8,128)(2,1)S(1)}, u32[]{:S(2)}, u32[]{:S(2)}) %collective-permute-start.3) | collective-permute-done | bytes 196640 | tf_op jit(solution)/shard_map/ppermute | solution.py:33
  44.0 1.5 %collective-permute-start.7 = (bf16[2,8,128,384]{3,2,1,0:T(8,128)(2,1)}, bf16[2,8,128,384]{3,2,1,0:T(8,128)(2,1)S(1)}, u32[]{:S(2)}, u32[]{:S(2)}) collective-permute-start(bf16[2,8,128,384]{3,2,1,0:T(8,128)(2,1)} %constant_dynamic-update-slice_fusion), channel_id=1, source_target_pairs={{0,1},{1,0},{2,3},{3,2},{4,5},{5,4},{6,7},{7,6},{8,9},{9,8},{10,11... | collective-permute-start | bytes 4718600 | tf_op jit(solution)/shard_map/ppermute | solution.py:36
  45.5 1.6 %constant_dynamic-update-slice_fusion.15 = f32[2,128,2048]{2,1,0:T(8,128)} fusion(f32[2,128,2048]{2,1,0:T(8,128)} %constant_dynamic-update-slice_fusion.16, f32[2,128,128]{2,1,0:T(8,128)} %copy.37), kind=kLoop, calls=%fused_computation.320 | loop fusion | bytes 262144
  47.0 1.6 %constant_dynamic-update-slice_fusion.14 = f32[2,128,2048]{2,1,0:T(8,128)} fusion(f32[2,128,2048]{2,1,0:T(8,128)} %constant_dynamic-update-slice_fusion.15, f32[2,128,128]{2,1,0:T(8,128)} %copy.38), kind=kLoop, calls=%fused_computation.319 | loop fusion | bytes 262144
  48.6 1.6 %constant_dynamic-update-slice_fusion.13 = f32[2,128,2048]{2,1,0:T(8,128)} fusion(f32[2,128,2048]{2,1,0:T(8,128)} %constant_dynamic-update-slice_fusion.14, f32[2,128,128]{2,1,0:T(8,128)} %copy.39), kind=kLoop, calls=%fused_computation.318 | loop fusion | bytes 262144
  50.2 1.6 %constant_dynamic-update-slice_fusion.12 = f32[2,128,2048]{2,1,0:T(8,128)} fusion(f32[2,128,2048]{2,1,0:T(8,128)} %constant_dynamic-update-slice_fusion.13, f32[2,128,128]{2,1,0:T(8,128)} %copy.40), kind=kLoop, calls=%fused_computation.317 | loop fusion | bytes 262144
  52.5 2.2 %fusion.287 = (f32[2,128]{1,0:T(2,128)S(1)}, f32[2,128,128]{1,2,0:T(8,128)}) fusion(bf16[2,128,384]{2,1,0:T(8,128)(2,1)} %copy-done.10, bf16[384,384]{1,0:T(8,128)(2,1)} %param.14, bf16[2,1,128,384]{3,2,1,0:T(8,128)(2,1)S(1)} %collective-permute-done.6, f32[2,128]{1,0:T(2,128)S(1)} %add_rsqrt_fusion.3), kind=kOutput, calls=%fused_computation.365 | convolution fusion | flops 101121792 | bytes 821248 | tf_op jit(solution)/shard_map/fqc,fkc->fqk/dot_general | solution.py:100
  54.7 1.0 fusion.105
  55.7 1.6 %constant_dynamic-update-slice_fusion.10 = f32[2,128,2048]{2,1,0:T(8,128)} fusion(f32[2,128,2048]{2,1,0:T(8,128)} %constant_dynamic-update-slice_fusion.11, f32[2,128,128]{2,1,0:T(8,128)} %copy.42), kind=kLoop, calls=%fused_computation.315 | loop fusion | bytes 262144
  59.0 1.0 fusion.104
  60.0 1.0 fusion.103
  61.0 1.0 fusion.102
  62.1 1.0 fusion.101
  63.1 1.0 fusion.100
  64.1 1.0 fusion.99
  65.5 1.6 %fusion.2 = bf16[2,8,128,384]{3,2,1,0:T(8,128)(2,1)} fusion(bf16[2,8,128,384]{3,2,1,0:T(8,128)(2,1)S(1)} %collective-permute-done.7, f32[2,8,128]{2,1,0:T(8,128)S(1)} %add_rsqrt_fusion), kind=kLoop, calls=%fused_computation.8 | loop fusion | flops 2359296 | bytes 3153920 | tf_op jit(solution)/shard_map/convert_element_type | solution.py:96
  67.0 3.9 %fusion.282 = (f32[2,128]{1,0:T(2,128)S(1)}, f32[2,128,2048]{2,1,0:T(8,128)}) fusion(f32[2,128,2048]{2,1,0:T(8,128)} %constant_dynamic-update-slice_fusion.9, bf16[2,128,384]{2,1,0:T(8,128)(2,1)S(1)} %copy-done.11, bf16[2,1024,384]{2,1,0:T(8,128)(2,1)} %bitcast.290, bf16[384,384]{1,0:T(8,128)(2,1)S(1)} %copy-done.13), kind=kOutput, calls=%fused_computation.362 | convolution fusion | flops 806616832 | bytes 3113984 | tf_op jit(solution)/shard_map/fqc,fkc->fqk/dot_general | solution.py:100
  71.0 3.8 %fusion.28 = bf16[2,2048,384]{2,1,0:T(8,128)(2,1)} fusion(bf16[2,2048,384]{2,1,0:T(8,128)(2,1)} %fusion.99, bf16[2,1024,384]{2,1,0:T(8,128)(2,1)} %bitcast.291, bf16[384,384]{1,0:T(8,128)(2,1)S(1)} %copy-done), kind=kOutput, calls=%fused_computation.39 | convolution fusion | flops 604766208 | bytes 3440640 | tf_op jit(solution)/shard_map/ftc,cd->ftd/dot_general | solution.py:72
  75.2 3.0 %multiply_reduce_fusion.1 = (f32[2,128]{1,0:T(2,128)S(1)}, f32[2,1,128,384]{3,2,0,1:T(8,128)S(1)}) fusion(bf16[384,384]{1,0:T(8,128)(2,1)} %param.16, bf16[2,2048,384]{2,1,0:T(8,128)(2,1)} %fusion.28, f32[2,128,2048]{2,1,0:T(8,128)S(1)} %copy-done.4, f32[2,128]{1,0:T(2,128)S(1)} %maximum_maximum_fusion.1, f32[2,128]{1,0:T(2,128)S(1)} %fusion.26, ...), kind=kOutput, calls=%fused_computation.274 | convolution fusion | flops 479985408 | bytes 6130688 | tf_op jit(solution)/shard_map/ftc,cd->ftd/dot_general | solution.py:115
  78.5 1.9 %collective-permute-start.8 = (bf16[4,1,128,384]{3,2,0,1:T(8,128)(2,1)S(1)}, bf16[4,1,128,384]{3,2,0,1:T(8,128)(2,1)S(1)}, u32[]{:S(2)}, u32[]{:S(2)}) collective-permute-start(bf16[4,1,128,384]{3,2,0,1:T(8,128)(2,1)S(1)} %pad_maximum_fusion.4), channel_id=1, source_target_pairs={{0,1},{1,2},{2,3},{3,4},{4,5},{5,6},{6,7},{7,8},{8,9},{9,10},{10,1... | collective-permute-start | bytes 1179656 | tf_op jit(solution)/shard_map/ppermute | solution.py:15
  80.4 2.6 %collective-permute-start.9 = (bf16[4,1,128,384]{3,2,0,1:T(8,128)(2,1)S(1)}, bf16[4,1,128,384]{3,2,0,1:T(8,128)(2,1)S(1)}, u32[]{:S(2)}, u32[]{:S(2)}) collective-permute-start(bf16[4,1,128,384]{3,2,0,1:T(8,128)(2,1)S(1)} %pad_maximum_fusion.4), channel_id=1, source_target_pairs={{1,0},{2,1},{3,2},{4,3},{5,4},{6,5},{7,6},{8,7},{9,8},{10,9},{11,1... | collective-permute-start | bytes 1179656 | tf_op jit(solution)/shard_map/ppermute | solution.py:16
  83.0 3.9 %fusion.275 = (bf16[1,1,3,384,384]{4,3,2,1,0:T(8,128)(2,1)S(1)}, bf16[1,1,3,384,384]{4,3,2,1,0:T(8,128)(2,1)S(1)}, bf16[1,1,3,384,384]{4,3,2,1,0:T(8,128)(2,1)S(...) fusion(bf16[3,3,3,384,384]{4,3,2,1,0:T(8,128)(2,1)} %param.17), kind=kLoop, calls=%fused_computation.355 | loop fusion | bytes 15925248 | tf_op jit(solution)/shard_map/slice | solution.py:64
  87.0 3.5 %collective-permute-done.9 = bf16[4,1,128,384]{3,2,0,1:T(8,128)(2,1)S(1)} collective-permute-done((bf16[4,1,128,384]{3,2,0,1:T(8,128)(2,1)S(1)}, bf16[4,1,128,384]{3,2,0,1:T(8,128)(2,1)S(1)}, u32[]{:S(2)}, u32[]{:S(2)}) %collective-permute-start.9) | collective-permute-done | bytes 393248 | tf_op jit(solution)/shard_map/ppermute | solution.py:16
  96.0 1.9 %collective-permute-start.10 = (bf16[2,1,128,384]{3,2,0,1:T(8,128)(2,1)S(1)}, bf16[2,1,128,384]{3,2,0,1:T(8,128)(2,1)S(1)}, u32[]{:S(2)}, u32[]{:S(2)}) collective-permute-start(bf16[2,1,128,384]{3,2,0,1:T(8,128)(2,1)S(1)} %fusion.98), channel_id=1, source_target_pairs={{0,1},{1,2},{2,3},{3,4},{4,5},{5,6},{6,7},{7,8},{8,9},{9,10},{10,1... | collective-permute-start | bytes 589832 | tf_op jit(solution)/shard_map/ppermute | solution.py:15
  98.0 3.2 %collective-permute-start.11 = (bf16[2,1,128,384]{3,2,0,1:T(8,128)(2,1)S(1)}, bf16[2,1,128,384]{3,2,0,1:T(8,128)(2,1)S(1)}, u32[]{:S(2)}, u32[]{:S(2)}) collective-permute-start(bf16[2,1,128,384]{3,2,0,1:T(8,128)(2,1)S(1)} %fusion.98), channel_id=1, source_target_pairs={{1,0},{2,1},{3,2},{4,3},{5,4},{6,5},{7,6},{8,7},{9,8},{10,9},{11,1... | collective-permute-start | bytes 589832 | tf_op jit(solution)/shard_map/ppermute | solution.py:16
  101.7 1.1 reshape.272
  104.4 1.4 %collective-permute-done.11 = bf16[2,1,128,384]{3,2,0,1:T(8,128)(2,1)S(1)} collective-permute-done((bf16[2,1,128,384]{3,2,0,1:T(8,128)(2,1)S(1)}, bf16[2,1,128,384]{3,2,0,1:T(8,128)(2,1)S(1)}, u32[]{:S(2)}, u32[]{:S(2)}) %collective-permute-start.11) | collective-permute-done | bytes 196640 | tf_op jit(solution)/shard_map/ppermute | solution.py:16
  108.4 1.2 fusion.8
  109.6 1.1 fusion.35
  110.7 1.2 multiply_reduce_fusion
  112.2 2.1 %collective-permute-start.12 = (bf16[4,1,256,192]{2,3,1,0:T(8,128)(2,1)S(1)}, bf16[4,1,256,192]{2,3,1,0:T(8,128)(2,1)S(1)}, u32[]{:S(2)}, u32[]{:S(2)}) collective-permute-start(bf16[4,1,256,192]{2,3,1,0:T(8,128)(2,1)S(1)} %get-tuple-element.78), channel_id=1, source_target_pairs={{0,1},{1,2},{2,3},{3,4},{4,5},{5,6},{6,7},{7,8},{8,9},{9,10},{10,1... | collective-permute-start | bytes 1179656 | tf_op jit(solution)/shard_map/ppermute | solution.py:15
  114.3 2.6 %collective-permute-start.13 = (bf16[4,1,256,192]{2,3,1,0:T(8,128)(2,1)S(1)}, bf16[4,1,256,192]{2,3,1,0:T(8,128)(2,1)S(1)}, u32[]{:S(2)}, u32[]{:S(2)}) collective-permute-start(bf16[4,1,256,192]{2,3,1,0:T(8,128)(2,1)S(1)} %get-tuple-element.79), channel_id=1, source_target_pairs={{1,0},{2,1},{3,2},{4,3},{5,4},{6,5},{7,6},{8,7},{9,8},{10,9},{11,1... | collective-permute-start | bytes 1179656 | tf_op jit(solution)/shard_map/ppermute | solution.py:16
  117.1 1.9 %collective-permute-done.12 = bf16[4,1,256,192]{2,3,1,0:T(8,128)(2,1)S(1)} collective-permute-done((bf16[4,1,256,192]{2,3,1,0:T(8,128)(2,1)S(1)}, bf16[4,1,256,192]{2,3,1,0:T(8,128)(2,1)S(1)}, u32[]{:S(2)}, u32[]{:S(2)}) %collective-permute-start.12) | collective-permute-done | bytes 393248 | tf_op jit(solution)/shard_map/ppermute | solution.py:15
  119.0 5.4 %collective-permute-done.13 = bf16[4,1,256,192]{2,3,1,0:T(8,128)(2,1)S(1)} collective-permute-done((bf16[4,1,256,192]{2,3,1,0:T(8,128)(2,1)S(1)}, bf16[4,1,256,192]{2,3,1,0:T(8,128)(2,1)S(1)}, u32[]{:S(2)}, u32[]{:S(2)}) %collective-permute-start.13) | collective-permute-done | bytes 393248 | tf_op jit(solution)/shard_map/ppermute | solution.py:16
  124.4 2.0 %select_maximum_fusion = bf16[4,4,258,192]{2,3,1,0:T(8,128)(2,1)S(1)} fusion(bf16[4,1,256,192]{2,3,1,0:T(8,128)(2,1)S(1)} %collective-permute-done.13, bf16[4,1,256,192]{2,3,1,0:T(8,128)(2,1)S(1)} %collective-permute-done.12, bf16[2,2,256,192]{2,3,1,0:T(8,128)(2,1)S(1)} %multiply_convert_fusion, bf16[2,2,256,192]{2,3,1,0:T(8,128)(2,1)S(1)} %copy-done.2), kind=kLoop, calls=%fused_computation.10 | loop fusion | flops 11888640 | bytes 3158016 | tf_op jit(solution)/shard_map/concatenate | solution.py:22
  126.4 1.7 %fusion.277 = (bf16[2,2,256,192]{2,3,1,0:T(8,128)(2,1)S(1)}, bf16[2,2,256,192]{2,3,1,0:T(8,128)(2,1)S(1)}, bf16[2,2,256,192]{2,3,1,0:T(8,128)(2,1)S(1)}, bf16[2,...) fusion(bf16[4,4,258,192]{2,3,1,0:T(8,128)(2,1)S(1)} %select_max, ...), kind=kLoop, calls=%fused_computation.357 | loop fusion | bytes 14155776 | tf_op jit(solution)/shard_map/slice | solution.py:62
  132.8 1.3 fusion.47
  (125 shorter events, 34.6 us)
Async XLA Ops:
  0.0 12.5 %copy-start = (bf16[384,384]{1,0:T(8,128)(2,1)S(1)}, bf16[384,384]{1,0:T(8,128)(2,1)}, u32[]{:S(2)}) copy-start(bf16[384,384]{1,0:T(8,128)(2,1)} %param.15) | copy-start | bytes 884740
  0.0 12.5 %copy-start.5 = (bf16[2,1,128,384]{3,2,1,0:T(8,128)(2,1)S(1)}, bf16[2,1,128,384]{3,2,1,0:T(8,128)(2,1)}, u32[]{:S(2)}) copy-start(bf16[2,1,128,384]{3,2,1,0:T(8,128)(2,1)} %param.10) | copy-start | bytes 589828
  0.0 14.8 %copy-start.12 = (bf16[384,384]{1,0:T(8,128)(2,1)S(1)}, bf16[384,384]{1,0:T(8,128)(2,1)}, u32[]{:S(2)}) copy-start(bf16[384,384]{1,0:T(8,128)(2,1)} %param.14) | copy-start | bytes 884740
  0.0 13.5 %collective-permute-start = (bf16[2,1,128,384]{3,2,1,0:T(8,128)(2,1)}, bf16[2,1,128,384]{3,2,1,0:T(8,128)(2,1)S(1)}, u32[]{:S(2)}, u32[]{:S(2)}) collective-permute-start(bf16[2,1,128,384]{3,2,1,0:T(8,128)(2,1)} %param.10), channel_id=1, source_target_pairs={{0,2},{1,3},{2,4},{3,5},{4,6},{5,7},{6,8},{7,9},{8,10},{9,11},{10,... | collective-permute-start | bytes 589832 | tf_op jit(solution)/shard_map/ppermute | solution.py:33
  1.3 14.8 %collective-permute-start.1 = (bf16[2,1,128,384]{3,2,1,0:T(8,128)(2,1)}, bf16[2,1,128,384]{3,2,1,0:T(8,128)(2,1)S(1)}, u32[]{:S(2)}, u32[]{:S(2)}) collective-permute-start(bf16[2,1,128,384]{3,2,1,0:T(8,128)(2,1)} %param.10), channel_id=1, source_target_pairs={{0,4},{1,5},{2,6},{3,7},{4,8},{5,9},{6,10},{7,11},{8,12},{9,13},{1... | collective-permute-start | bytes 589832 | tf_op jit(solution)/shard_map/ppermute | solution.py:33
  2.6 27.9 %collective-permute-start.2 = (bf16[2,1,128,384]{3,2,1,0:T(8,128)(2,1)}, bf16[2,1,128,384]{3,2,1,0:T(8,128)(2,1)S(1)}, u32[]{:S(2)}, u32[]{:S(2)}) collective-permute-start(bf16[2,1,128,384]{3,2,1,0:T(8,128)(2,1)} %param.10), channel_id=1, source_target_pairs={{0,6},{1,7},{2,8},{3,9},{4,10},{5,11},{6,12},{7,13},{8,14},{9,15},... | collective-permute-start | bytes 589832 | tf_op jit(solution)/shard_map/ppermute | solution.py:33
  3.6 31.1 %collective-permute-start.3 = (bf16[2,1,128,384]{3,2,1,0:T(8,128)(2,1)}, bf16[2,1,128,384]{3,2,1,0:T(8,128)(2,1)S(1)}, u32[]{:S(2)}, u32[]{:S(2)}) collective-permute-start(bf16[2,1,128,384]{3,2,1,0:T(8,128)(2,1)} %param.10), channel_id=1, source_target_pairs={{0,8},{1,9},{2,10},{3,11},{4,12},{5,13},{6,14},{7,15},{8,0},{9,1},... | collective-permute-start | bytes 589832 | tf_op jit(solution)/shard_map/ppermute | solution.py:33
  4.9 31.2 %collective-permute-start.4 = (bf16[2,1,128,384]{3,2,1,0:T(8,128)(2,1)}, bf16[2,1,128,384]{3,2,1,0:T(8,128)(2,1)S(1)}, u32[]{:S(2)}, u32[]{:S(2)}) collective-permute-start(bf16[2,1,128,384]{3,2,1,0:T(8,128)(2,1)} %param.10), channel_id=1, source_target_pairs={{0,10},{1,11},{2,12},{3,13},{4,14},{5,15},{6,0},{7,1},{8,2},{9,3},... | collective-permute-start | bytes 589832 | tf_op jit(solution)/shard_map/ppermute | solution.py:33
  10.0 27.6 %copy-start.10 = (bf16[2,128,384]{2,1,0:T(8,128)(2,1)}, bf16[2,128,384]{2,1,0:T(8,128)(2,1)S(1)}, u32[]{:S(2)}) copy-start(bf16[2,128,384]{2,1,0:T(8,128)(2,1)S(1)} %convolution_convert_fusion.18) | copy-start | bytes 589828
  13.5 24.1 %collective-permute-start.5 = (bf16[2,1,128,384]{3,2,1,0:T(8,128)(2,1)S(1)}, bf16[2,1,128,384]{3,2,1,0:T(8,128)(2,1)S(1)}, u32[]{:S(2)}, u32[]{:S(2)}) collective-permute-start(bf16[2,1,128,384]{3,2,1,0:T(8,128)(2,1)S(1)} %copy-done.5), channel_id=1, source_target_pairs={{0,12},{1,13},{2,14},{3,15},{4,0},{5,1},{6,2},{7,3},{8,4},{9,5},{1... | collective-permute-start | bytes 589832 | tf_op jit(solution)/shard_map/ppermute | solution.py:33
  16.1 22.8 %collective-permute-start.6 = (bf16[2,1,128,384]{3,2,1,0:T(8,128)(2,1)S(1)}, bf16[2,1,128,384]{3,2,1,0:T(8,128)(2,1)S(1)}, u32[]{:S(2)}, u32[]{:S(2)}) collective-permute-start(bf16[2,1,128,384]{3,2,1,0:T(8,128)(2,1)S(1)} %copy-done.5), channel_id=1, source_target_pairs={{0,14},{1,15},{2,0},{3,1},{4,2},{5,3},{6,4},{7,5},{8,6},{9,7},{10,... | collective-permute-start | bytes 589832 | tf_op jit(solution)/shard_map/ppermute | solution.py:33
  38.9 12.9 %copy-start.8 = (f32[2,128,128]{2,1,0:T(8,128)S(1)}, f32[2,128,128]{2,1,0:T(8,128)}, u32[]{:S(2)}) copy-start(f32[2,128,128]{2,1,0:T(8,128)} %copy.41) | copy-start | bytes 393220
  44.0 21.1 %collective-permute-start.7 = (bf16[2,8,128,384]{3,2,1,0:T(8,128)(2,1)}, bf16[2,8,128,384]{3,2,1,0:T(8,128)(2,1)S(1)}, u32[]{:S(2)}, u32[]{:S(2)}) collective-permute-start(bf16[2,8,128,384]{3,2,1,0:T(8,128)(2,1)} %constant_dynamic-update-slice_fusion), channel_id=1, source_target_pairs={{0,1},{1,0},{2,3},{3,2},{4,5},{5,4},{6,7},{7,6},{8,9},{9,8},{10,11... | collective-permute-start | bytes 4718600 | tf_op jit(solution)/shard_map/ppermute | solution.py:36
  65.1 2.0 %copy-start.11 = (bf16[2,128,384]{2,1,0:T(8,128)(2,1)S(1)}, bf16[2,128,384]{2,1,0:T(8,128)(2,1)}, u32[]{:S(2)}) copy-start(bf16[2,128,384]{2,1,0:T(8,128)(2,1)} %copy-done.10) | copy-start | bytes 589828
  65.1 2.0 %copy-start.13 = (bf16[384,384]{1,0:T(8,128)(2,1)S(1)}, bf16[384,384]{1,0:T(8,128)(2,1)}, u32[]{:S(2)}) copy-start(bf16[384,384]{1,0:T(8,128)(2,1)} %param.14) | copy-start | bytes 884740
  70.9 3.8 %copy-start.4 = (f32[2,128,2048]{2,1,0:T(8,128)S(1)}, f32[2,128,2048]{2,1,0:T(8,128)}, u32[]{:S(2)}) copy-start(f32[2,128,2048]{2,1,0:T(8,128)} %get-tuple-element.75) | copy-start | bytes 6291460
  75.2 3.2 %copy-start.6 = (bf16[2,1,128,384]{3,2,1,0:T(8,128)(2,1)S(1)}, bf16[2,1,128,384]{3,2,1,0:T(8,128)(2,1)}, u32[]{:S(2)}) copy-start(bf16[2,1,128,384]{3,2,1,0:T(8,128)(2,1)} %param.11) | copy-start | bytes 589828
  78.5 8.5 %collective-permute-start.8 = (bf16[4,1,128,384]{3,2,0,1:T(8,128)(2,1)S(1)}, bf16[4,1,128,384]{3,2,0,1:T(8,128)(2,1)S(1)}, u32[]{:S(2)}, u32[]{:S(2)}) collective-permute-start(bf16[4,1,128,384]{3,2,0,1:T(8,128)(2,1)S(1)} %pad_maximum_fusion.4), channel_id=1, source_target_pairs={{0,1},{1,2},{2,3},{3,4},{4,5},{5,6},{6,7},{7,8},{8,9},{9,10},{10,1... | collective-permute-start | bytes 1179656 | tf_op jit(solution)/shard_map/ppermute | solution.py:15
  80.4 10.1 %collective-permute-start.9 = (bf16[4,1,128,384]{3,2,0,1:T(8,128)(2,1)S(1)}, bf16[4,1,128,384]{3,2,0,1:T(8,128)(2,1)S(1)}, u32[]{:S(2)}, u32[]{:S(2)}) collective-permute-start(bf16[4,1,128,384]{3,2,0,1:T(8,128)(2,1)S(1)} %pad_maximum_fusion.4), channel_id=1, source_target_pairs={{1,0},{2,1},{3,2},{4,3},{5,4},{6,5},{7,6},{8,7},{9,8},{10,9},{11,1... | collective-permute-start | bytes 1179656 | tf_op jit(solution)/shard_map/ppermute | solution.py:16
  95.5 5.6 %copy-start.7 = (bf16[3,3,384,192]{2,3,1,0:T(8,128)(2,1)S(1)}, bf16[3,3,384,192]{2,3,1,0:T(8,128)(2,1)}, u32[]{:S(2)}) copy-start(bf16[3,3,384,192]{2,3,1,0:T(8,128)(2,1)} %param.18) | copy-start | bytes 3981316
  96.0 8.4 %collective-permute-start.10 = (bf16[2,1,128,384]{3,2,0,1:T(8,128)(2,1)S(1)}, bf16[2,1,128,384]{3,2,0,1:T(8,128)(2,1)S(1)}, u32[]{:S(2)}, u32[]{:S(2)}) collective-permute-start(bf16[2,1,128,384]{3,2,0,1:T(8,128)(2,1)S(1)} %fusion.98), channel_id=1, source_target_pairs={{0,1},{1,2},{2,3},{3,4},{4,5},{5,6},{6,7},{7,8},{8,9},{9,10},{10,1... | collective-permute-start | bytes 589832 | tf_op jit(solution)/shard_map/ppermute | solution.py:15
  98.0 7.9 %collective-permute-start.11 = (bf16[2,1,128,384]{3,2,0,1:T(8,128)(2,1)S(1)}, bf16[2,1,128,384]{3,2,0,1:T(8,128)(2,1)S(1)}, u32[]{:S(2)}, u32[]{:S(2)}) collective-permute-start(bf16[2,1,128,384]{3,2,0,1:T(8,128)(2,1)S(1)} %fusion.98), channel_id=1, source_target_pairs={{1,0},{2,1},{3,2},{4,3},{5,4},{6,5},{7,6},{8,7},{9,8},{10,9},{11,1... | collective-permute-start | bytes 589832 | tf_op jit(solution)/shard_map/ppermute | solution.py:16
  107.2 1.1 copy-start.9
  110.7 1.4 %copy-start.2 = (bf16[2,2,256,192]{2,3,1,0:T(8,128)(2,1)S(1)}, bf16[2,2,256,192]{2,3,1,0:T(8,128)(2,1)}, u32[]{:S(2)}) copy-start(bf16[2,2,256,192]{2,3,1,0:T(8,128)(2,1)} %param.12) | copy-start | bytes 1179652
  111.9 5.0 %copy-start.3 = (bf16[3,3,3,192,192]{4,3,2,1,0:T(8,128)(2,1)S(1)}, bf16[3,3,3,192,192]{4,3,2,1,0:T(8,128)(2,1)}, u32[]{:S(2)}) copy-start(bf16[3,3,3,192,192]{4,3,2,1,0:T(8,128)(2,1)} %param.19) | copy-start | bytes 5971972
  112.2 6.8 %collective-permute-start.12 = (bf16[4,1,256,192]{2,3,1,0:T(8,128)(2,1)S(1)}, bf16[4,1,256,192]{2,3,1,0:T(8,128)(2,1)S(1)}, u32[]{:S(2)}, u32[]{:S(2)}) collective-permute-start(bf16[4,1,256,192]{2,3,1,0:T(8,128)(2,1)S(1)} %get-tuple-element.78), channel_id=1, source_target_pairs={{0,1},{1,2},{2,3},{3,4},{4,5},{5,6},{6,7},{7,8},{8,9},{9,10},{10,1... | collective-permute-start | bytes 1179656 | tf_op jit(solution)/shard_map/ppermute | solution.py:15
  114.3 10.1 %collective-permute-start.13 = (bf16[4,1,256,192]{2,3,1,0:T(8,128)(2,1)S(1)}, bf16[4,1,256,192]{2,3,1,0:T(8,128)(2,1)S(1)}, u32[]{:S(2)}, u32[]{:S(2)}) collective-permute-start(bf16[4,1,256,192]{2,3,1,0:T(8,128)(2,1)S(1)} %get-tuple-element.79), channel_id=1, source_target_pairs={{1,0},{2,1},{3,2},{4,3},{5,4},{6,5},{7,6},{8,7},{9,8},{10,9},{11,1... | collective-permute-start | bytes 1179656 | tf_op jit(solution)/shard_map/ppermute | solution.py:16
  132.7 1.3 copy-start.1

commit v9 on v7

--- a/solution.py
+++ b/solution.py
@@ -1,8 +1,11 @@
+import functools
 import math
 
 import jax
 import jax.numpy as jnp
 from jax import lax
+from jax.experimental import pallas as pl
+from jax.experimental.pallas import tpu as pltpu
 from jax.sharding import PartitionSpec as P
 
 
@@ -68,6 +71,42 @@
     return result
 
 
+def attention_kernel(scale, q_ref, k_ref, v_ref, o_ref):
+    scores = (
+        lax.dot_general(
+            q_ref[0], k_ref[0], (((1,), (1,)), ((), ())), preferred_element_type=jnp.float32
+        )
+        * scale
+    )
+    largest = jnp.max(scores, axis=-1, keepdims=True)
+    weights = jnp.exp(scores - largest)
+    weight_sum = jnp.sum(weights, axis=-1, keepdims=True)
+    summed = jnp.dot(weights.astype(v_ref.dtype), v_ref[0], preferred_element_type=jnp.float32)
+    o_ref[0] = (summed / weight_sum).astype(o_ref.dtype)
+
+
+def attend(queries, keys_all, values_all, scale):
+    frames, count, channels = queries.shape
+    tokens = keys_all.shape[1]
+    flops = 4 * frames * count * tokens * channels
+    moved = 2 * (queries.size * 2 + keys_all.size + values_all.size)
+    return pl.pallas_call(
+        functools.partial(attention_kernel, scale),
+        grid=(frames,),
+        in_specs=[
+            pl.BlockSpec((1, count, channels), lambda f: (f, 0, 0)),
+            pl.BlockSpec((1, tokens, channels), lambda f: (f, 0, 0)),
+            pl.BlockSpec((1, tokens, channels), lambda f: (f, 0, 0)),
+        ],
+        out_specs=pl.BlockSpec((1, count, channels), lambda f: (f, 0, 0)),
+        out_shape=jax.ShapeDtypeStruct(queries.shape, queries.dtype),
+        compiler_params=pltpu.CompilerParams(vmem_limit_bytes=60 * 1024 * 1024),
+        cost_estimate=pl.CostEstimate(
+            flops=flops, transcendentals=frames * count * tokens, bytes_accessed=moved
+        ),
+    )(queries, keys_all, values_all)
+
+
 def project_rows(tokens, weight):
     return jnp.einsum("ftc,cd->ftd", tokens, weight, preferred_element_type=jnp.float32).astype(
         jnp.bfloat16
@@ -96,20 +135,7 @@
     keys_all = project_rows(all_tokens, w_key)
     values_all = project_rows(all_tokens, w_value)
     score_scale = 1.0 / math.sqrt(channels)
-    scores = (
-        jnp.einsum("fqc,fkc->fqk", queries, keys_all, preferred_element_type=jnp.float32)
-        * score_scale
-    )
-    largest = jnp.max(scores, axis=-1)
-    weights = jnp.exp(scores - largest[..., None])
-    weight_sum = jnp.sum(weights, axis=-1)
-    weighted = jnp.einsum(
-        "fqk,fkc->fqc",
-        weights.astype(jnp.bfloat16),
-        values_all,
-        preferred_element_type=jnp.float32,
-    )
-    attended = (weighted / weight_sum[..., None]).astype(jnp.bfloat16)
+    attended = attend(queries, keys_all, values_all, score_scale)
     projected = jnp.einsum("ftc,cd->ftd", attended, w_output, preferred_element_type=jnp.float32)
     mixed = (
         features.astype(jnp.float32)

time: 117 us -> 116 us (level)
  Pallas kernels: 0 us -> 5.06 us
  other arithmetic: 7.92 us -> 4.97 us
  matrix products: 25.8 us -> 23.1 us
    dot_general x2 -> x0, matrix products: 10.2 us -> none  [the longest x1 5.21 us: per_device(): jnp.einsum('fqc,fkc->fqk', queries, keys_all, preferred_element_type=jnp....]
    dot_general x1 -> x3, matrix products: 1.01 us -> 8.5 us  [project_rows(): jnp.einsum('ftc,cd->ftd', tokens, weight, preferred_element_type=jnp.floa...]
    pallas_call x0 -> x1, Pallas kernels: none -> 5.06 us  [attend(): pl.pallas_call(functools.partial(attention_kernel, scale), grid=(frames,)...]
    reduce_sum x1 -> x0, other arithmetic: 2.02 us -> none  [per_device(): weight_sum = jnp.sum(weights, axis=-1)]
where the time goes in v9:
time: 116 us; the launch traced here: 114 us
  waiting for transfers between devices  43.5 us (38%)
  matrix products  23.1 us (20%)
  starting transfers between devices  22.8 us (20%)
  local copies, waits for them, and re-layouts  13.9 us (12%)
  Pallas kernels  5.06 us (4%)
  other arithmetic  4.97 us (4%)
    ppermute x7, waiting for transfers between devices, gather_rows(): pieces.append(lax.ppermute(x, 'ha', pairs))  30 us
    dot_general x21, matrix products, conv_taps(): jnp.einsum('fhwc,cd->fhwd', stacked, kernel, preferred_element_type=jnp.f...  13.3 us
    ppermute x3, waiting for transfers between devices, halo_rows(): after = lax.ppermute(first, 'ha', down)  10.1 us
    ppermute x3, starting transfers between devices, halo_rows(): after = lax.ppermute(first, 'ha', down)  9.14 us
    dot_general x3, matrix products, project_rows(): jnp.einsum('ftc,cd->ftd', tokens, weight, preferred_element_type=jnp.floa...  8.5 us
    ppermute x7, starting transfers between devices, gather_rows(): pieces.append(lax.ppermute(x, 'ha', pairs))  7.21 us
    ppermute x3, starting transfers between devices, halo_rows(): before = lax.ppermute(last, 'ha', up)  5.89 us
    slice x6, local copies, waits for them, and re-layouts, conv_taps(): kernel = weight[time_off, row_off].reshape(3 * in_channels, out_channels)  5.41 us
  transfers between devices with their start and end apart: 14, of which 10 were waited for; matrix products, arithmetic and copies ran while one was open for 9% of the time, Pallas kernels for 0%

profile of v9, /device:TPU:13, one launch (start us, length us, event | category | flops | bytes accessed | tf_op | source)
XLA Modules:
  0.0 113.9 jit_solution(18088447833060881689)
XLA Ops:
  0.0 1.3 %collective-permute-start = (bf16[2,1,128,384]{3,2,1,0:T(8,128)(2,1)}, bf16[2,1,128,384]{3,2,1,0:T(8,128)(2,1)S(1)}, u32[]{:S(2)}, u32[]{:S(2)}) collective-permute-start(bf16[2,1,128,384]{3,2,1,0:T(8,128)(2,1)} %param.10), channel_id=1, source_target_pairs={{0,2},{1,3},{2,4},{3,5},{4,6},{5,7},{6,8},{7,9},{8,10},{9,11},{10,... | collective-permute-start | bytes 589832 | tf_op jit(solution)/shard_map/ppermute | solution.py:36
  1.3 1.3 %collective-permute-start.1 = (bf16[2,1,128,384]{3,2,1,0:T(8,128)(2,1)}, bf16[2,1,128,384]{3,2,1,0:T(8,128)(2,1)S(1)}, u32[]{:S(2)}, u32[]{:S(2)}) collective-permute-start(bf16[2,1,128,384]{3,2,1,0:T(8,128)(2,1)} %param.10), channel_id=1, source_target_pairs={{0,4},{1,5},{2,6},{3,7},{4,8},{5,9},{6,10},{7,11},{8,12},{9,13},{1... | collective-permute-start | bytes 589832 | tf_op jit(solution)/shard_map/ppermute | solution.py:36
  2.6 1.0 collective-permute-start.2
  3.6 1.3 %collective-permute-start.3 = (bf16[2,1,128,384]{3,2,1,0:T(8,128)(2,1)}, bf16[2,1,128,384]{3,2,1,0:T(8,128)(2,1)S(1)}, u32[]{:S(2)}, u32[]{:S(2)}) collective-permute-start(bf16[2,1,128,384]{3,2,1,0:T(8,128)(2,1)} %param.10), channel_id=1, source_target_pairs={{0,8},{1,9},{2,10},{3,11},{4,12},{5,13},{6,14},{7,15},{8,0},{9,1},... | collective-permute-start | bytes 589832 | tf_op jit(solution)/shard_map/ppermute | solution.py:36
  4.9 1.0 collective-permute-start.4
  5.9 1.0 constant_dynamic-update-slice_fusion.7
  6.9 1.3 %collective-permute-start.5 = (bf16[2,1,128,384]{3,2,1,0:T(8,128)(2,1)}, bf16[2,1,128,384]{3,2,1,0:T(8,128)(2,1)S(1)}, u32[]{:S(2)}, u32[]{:S(2)}) collective-permute-start(bf16[2,1,128,384]{3,2,1,0:T(8,128)(2,1)} %param.10), channel_id=1, source_target_pairs={{0,12},{1,13},{2,14},{3,15},{4,0},{5,1},{6,2},{7,3},{8,4},{9,5},{1... | collective-permute-start | bytes 589832 | tf_op jit(solution)/shard_map/ppermute | solution.py:36
  8.3 1.9 %collective-permute-done.1 = bf16[2,1,128,384]{3,2,1,0:T(8,128)(2,1)S(1)} collective-permute-done((bf16[2,1,128,384]{3,2,1,0:T(8,128)(2,1)}, bf16[2,1,128,384]{3,2,1,0:T(8,128)(2,1)S(1)}, u32[]{:S(2)}, u32[]{:S(2)}) %collective-permute-start.1) | collective-permute-done | bytes 196640 | tf_op jit(solution)/shard_map/ppermute | solution.py:36
  10.3 20.2 %collective-permute-done.2 = bf16[2,1,128,384]{3,2,1,0:T(8,128)(2,1)S(1)} collective-permute-done((bf16[2,1,128,384]{3,2,1,0:T(8,128)(2,1)}, bf16[2,1,128,384]{3,2,1,0:T(8,128)(2,1)S(1)}, u32[]{:S(2)}, u32[]{:S(2)}) %collective-permute-start.2) | collective-permute-done | bytes 196640 | tf_op jit(solution)/shard_map/ppermute | solution.py:36
  30.5 4.1 %collective-permute-done.3 = bf16[2,1,128,384]{3,2,1,0:T(8,128)(2,1)S(1)} collective-permute-done((bf16[2,1,128,384]{3,2,1,0:T(8,128)(2,1)}, bf16[2,1,128,384]{3,2,1,0:T(8,128)(2,1)S(1)}, u32[]{:S(2)}, u32[]{:S(2)}) %collective-permute-start.3) | collective-permute-done | bytes 196640 | tf_op jit(solution)/shard_map/ppermute | solution.py:36
  34.8 2.7 %collective-permute-done.5 = bf16[2,1,128,384]{3,2,1,0:T(8,128)(2,1)S(1)} collective-permute-done((bf16[2,1,128,384]{3,2,1,0:T(8,128)(2,1)}, bf16[2,1,128,384]{3,2,1,0:T(8,128)(2,1)S(1)}, u32[]{:S(2)}, u32[]{:S(2)}) %collective-permute-start.5) | collective-permute-done | bytes 196640 | tf_op jit(solution)/shard_map/ppermute | solution.py:36
  37.6 1.1 collective-permute-done.6
  38.7 0.6 collective-permute-start.7
  39.4 1.0 convolution_convert_fusion.2.q_ref
  40.4 1.9 %collective-permute-done.7 = bf16[2,8,128,384]{3,2,1,0:T(8,128)(2,1)S(1)} collective-permute-done((bf16[2,8,128,384]{3,2,1,0:T(8,128)(2,1)S(1)}, bf16[2,8,128,384]{3,2,1,0:T(8,128)(2,1)S(1)}, u32[]{:S(2)}, u32[]{:S(2)}) %collective-permute-start.7) | collective-permute-done | bytes 1572896 | tf_op jit(solution)/shard_map/ppermute | solution.py:39
  42.6 0.7 multiply_reduce_fusion
  43.4 0.7 fusion
  44.1 3.8 %convolution_convert_fusion.v_ref = bf16[2,2048,384]{2,1,0:T(8,128)(2,1)} fusion(bf16[2,2048,384]{2,1,0:T(8,128)(2,1)S(1)} %fusion, bf16[384,384]{1,0:T(8,128)(2,1)S(1)} %copy-done), kind=kOutput, calls=%fused_computation.8 | convolution fusion | flops 1209532416 | bytes 6586368 | tf_op jit(solution)/shard_map/ftc,cd->ftd/dot_general | solution.py:111
  47.9 3.7 %convolution_convert_fusion.1.k_ref = bf16[2,2048,384]{2,1,0:T(8,128)(2,1)} fusion(bf16[2,2048,384]{2,1,0:T(8,128)(2,1)S(1)} %fusion, bf16[384,384]{1,0:T(8,128)(2,1)S(1)} %copy-done.8), kind=kOutput, calls=%fused_computation.9 | convolution fusion | flops 1209532416 | bytes 6586368 | tf_op jit(solution)/shard_map/ftc,cd->ftd/dot_general | solution.py:111
  51.6 5.1 %shard_map.100 = bf16[2,128,384]{2,1,0:T(8,128)(2,1)} custom-call(bf16[2,128,384]{2,1,0:T(8,128)(2,1)} %convolution_convert_fusion.2.q_ref, bf16[2,2048,384]{2,1,0:T(8,128)(2,1)} %convolution_convert_fusion.1.k_ref, bf16[2,2048,384]{2,1,0:T(8,128)(2,1)} %convolution_convert_fusion.v_ref), custom_call_target="tpu_custom_call" | custom-call | flops 805306368 | bytes 6684672 | tf_op jit(solution)/shard_map/pallas_call | solution.py:93
  56.7 1.3 %multiply_reduce_fusion.2 = (f32[2,128]{1,0:T(2,128)S(1)}, f32[2,1,128,384]{3,2,0,1:T(8,128)S(1)}) fusion(bf16[2,128,384]{2,1,0:T(8,128)(2,1)} %shard_map.100, bf16[384,384]{1,0:T(8,128)(2,1)S(1)} %copy-done.9, bf16[2,1,128,384]{3,2,1,0:T(8,128)(2,1)S(1)} %copy-done.3), kind=kOutput, calls=%fused_computation.196 | convolution fusion | flops 76087040 | bytes 1082368 | tf_op jit(solution)/shard_map/ftc,cd->ftd/dot_general | solution.py:139
  58.3 1.9 %collective-permute-start.8 = (bf16[4,1,128,384]{3,2,0,1:T(8,128)(2,1)S(1)}, bf16[4,1,128,384]{3,2,0,1:T(8,128)(2,1)S(1)}, u32[]{:S(2)}, u32[]{:S(2)}) collective-permute-start(bf16[4,1,128,384]{3,2,0,1:T(8,128)(2,1)S(1)} %pad_maximum_fusion.4), channel_id=1, source_target_pairs={{0,1},{1,2},{2,3},{3,4},{4,5},{5,6},{6,7},{7,8},{8,9},{9,10},{10,1... | collective-permute-start | bytes 1179656 | tf_op jit(solution)/shard_map/ppermute | solution.py:18
  60.2 2.6 %collective-permute-start.9 = (bf16[4,1,128,384]{3,2,0,1:T(8,128)(2,1)S(1)}, bf16[4,1,128,384]{3,2,0,1:T(8,128)(2,1)S(1)}, u32[]{:S(2)}, u32[]{:S(2)}) collective-permute-start(bf16[4,1,128,384]{3,2,0,1:T(8,128)(2,1)S(1)} %pad_maximum_fusion.4), channel_id=1, source_target_pairs={{1,0},{2,1},{3,2},{4,3},{5,4},{6,5},{7,6},{8,7},{9,8},{10,9},{11,1... | collective-permute-start | bytes 1179656 | tf_op jit(solution)/shard_map/ppermute | solution.py:19
  62.8 3.9 %fusion.171 = (bf16[1,1,3,384,384]{4,3,2,1,0:T(8,128)(2,1)S(1)}, bf16[1,1,3,384,384]{4,3,2,1,0:T(8,128)(2,1)S(1)}, bf16[1,1,3,384,384]{4,3,2,1,0:T(8,128)(2,1)S(...) fusion(bf16[3,3,3,384,384]{4,3,2,1,0:T(8,128)(2,1)} %param.17), kind=kLoop, calls=%fused_computation.248 | loop fusion | bytes 15925248 | tf_op jit(solution)/shard_map/slice | solution.py:67
  66.8 3.5 %collective-permute-done.9 = bf16[4,1,128,384]{3,2,0,1:T(8,128)(2,1)S(1)} collective-permute-done((bf16[4,1,128,384]{3,2,0,1:T(8,128)(2,1)S(1)}, bf16[4,1,128,384]{3,2,0,1:T(8,128)(2,1)S(1)}, u32[]{:S(2)}, u32[]{:S(2)}) %collective-permute-start.9) | collective-permute-done | bytes 393248 | tf_op jit(solution)/shard_map/ppermute | solution.py:19
  70.6 0.7 fusion.175
  75.8 1.9 %collective-permute-start.10 = (bf16[2,1,128,384]{3,2,0,1:T(8,128)(2,1)S(1)}, bf16[2,1,128,384]{3,2,0,1:T(8,128)(2,1)S(1)}, u32[]{:S(2)}, u32[]{:S(2)}) collective-permute-start(bf16[2,1,128,384]{3,2,0,1:T(8,128)(2,1)S(1)} %fusion.92), channel_id=1, source_target_pairs={{0,1},{1,2},{2,3},{3,4},{4,5},{5,6},{6,7},{7,8},{8,9},{9,10},{10,1... | collective-permute-start | bytes 589832 | tf_op jit(solution)/shard_map/ppermute | solution.py:18
  77.7 3.6 %collective-permute-start.11 = (bf16[2,1,128,384]{3,2,0,1:T(8,128)(2,1)S(1)}, bf16[2,1,128,384]{3,2,0,1:T(8,128)(2,1)S(1)}, u32[]{:S(2)}, u32[]{:S(2)}) collective-permute-start(bf16[2,1,128,384]{3,2,0,1:T(8,128)(2,1)S(1)} %fusion.92), channel_id=1, source_target_pairs={{1,0},{2,1},{3,2},{4,3},{5,4},{6,5},{7,6},{8,7},{9,8},{10,9},{11,1... | collective-permute-start | bytes 589832 | tf_op jit(solution)/shard_map/ppermute | solution.py:19
  81.8 1.2 %reshape.134 = bf16[1152,192,1,1]{0,1,2,3:T(8,128)(2,1)} reshape(bf16[1,1,3,384,192]{3,2,4,1,0:T(4,128)(2,1)S(1)} %copy.32) | data formatting | bytes 884736 | tf_op jit(solution)/shard_map/reshape;squeeze | solution.py:67
  84.5 1.2 %collective-permute-done.11 = bf16[2,1,128,384]{3,2,0,1:T(8,128)(2,1)S(1)} collective-permute-done((bf16[2,1,128,384]{3,2,0,1:T(8,128)(2,1)S(1)}, bf16[2,1,128,384]{3,2,0,1:T(8,128)(2,1)S(1)}, u32[]{:S(2)}, u32[]{:S(2)}) %collective-permute-start.11) | collective-permute-done | bytes 196640 | tf_op jit(solution)/shard_map/ppermute | solution.py:19
  85.9 0.6 broadcast_in_dim.4
  87.1 0.8 pad_slice_fusion.9
  88.2 1.2 %fusion.7 = f32[2,2,256,192]{2,3,1,0:T(8,128)S(1)} fusion(bf16[2,1,258,384]{3,2,1,0:T(8,128)(2,1)S(1)} %pad_slice_fusion.10, bf16[2,2,256,384]{3,2,1,0:T(8,128)(2,1)S(1)} %get-tuple-element.79, bf16[2,2,256,384]{3,2,1,0:T(8,128)(2,1)S(1)} %get-tuple-element.78, bf16[1152,192,1,1]{0,1,2,3:T(8,128)(2,1)S(1)} %copy-done.7), kind=kOutput, calls=%fused_computation.18 | convolution fusion | flops 462422016 | bytes 3197952 | tf_op jit(solution)/shard_map/fhwc,cd->fhwd/dot_general | solution.py:68
  89.4 1.1 %fusion.29 = f32[2,2,256,192]{2,3,1,0:T(8,128)S(1)} fusion(f32[2,2,256,192]{2,3,1,0:T(8,128)S(1)} %fusion.7, bf16[2,2,256,384]{3,2,1,0:T(8,128)(2,1)S(1)} %get-tuple-element.69, bf16[2,2,256,384]{3,2,1,0:T(8,128)(2,1)S(1)} %get-tuple-element.72, bf16[2,2,256,384]{3,2,1,0:T(8,128)(2,1)S(1)} %get-tuple-element.73, bf16[1152,192,1,1]{0,1,2,3:T(8,128)(2,1)S(1)} %reshape.133), kind=kOutput, calls=%fused_computation.45 | convolution fusion | flops 460259328 | bytes 4374528 | tf_op jit(solution)/shard_map/fhwc,cd->fhwd/dot_general | solution.py:68
  90.6 1.2 %multiply_reduce_fusion.1 = (f32[2,2,256]{2,1,0:T(2,128)S(1)}, f32[2,2,256,192]{2,3,1,0:T(8,128)S(1)}) fusion(f32[2,2,256,192]{2,3,1,0:T(8,128)S(1)} %fusion.29, bf16[1152,192,1,1]{0,1,2,3:T(8,128)(2,1)S(1)} %reshape.135, bf16[2,2,256,384]{3,2,1,0:T(8,128)(2,1)S(1)} %get-tuple-element.70, bf16[2,2,256,384]{3,2,1,0:T(8,128)(2,1)S(1)} %get-tuple-element.71, ...), kind=kOutput, calls=%fused_computation.130 | convolution fusion | flops 461044736 | bytes 4378624 | tf_op jit(solution)/shard_map/fhwc,cd->fhwd/dot_general | solution.py:68
  92.1 2.1 %collective-permute-start.12 = (bf16[4,1,256,192]{2,3,1,0:T(8,128)(2,1)S(1)}, bf16[4,1,256,192]{2,3,1,0:T(8,128)(2,1)S(1)}, u32[]{:S(2)}, u32[]{:S(2)}) collective-permute-start(bf16[4,1,256,192]{2,3,1,0:T(8,128)(2,1)S(1)} %get-tuple-element.76), channel_id=1, source_target_pairs={{0,1},{1,2},{2,3},{3,4},{4,5},{5,6},{6,7},{7,8},{8,9},{9,10},{10,1... | collective-permute-start | bytes 1179656 | tf_op jit(solution)/shard_map/ppermute | solution.py:18
  94.1 3.0 %collective-permute-start.13 = (bf16[4,1,256,192]{2,3,1,0:T(8,128)(2,1)S(1)}, bf16[4,1,256,192]{2,3,1,0:T(8,128)(2,1)S(1)}, u32[]{:S(2)}, u32[]{:S(2)}) collective-permute-start(bf16[4,1,256,192]{2,3,1,0:T(8,128)(2,1)S(1)} %get-tuple-element.77), channel_id=1, source_target_pairs={{1,0},{2,1},{3,2},{4,3},{5,4},{6,5},{7,6},{8,7},{9,8},{10,9},{11,1... | collective-permute-start | bytes 1179656 | tf_op jit(solution)/shard_map/ppermute | solution.py:19
  97.3 1.5 %collective-permute-done.12 = bf16[4,1,256,192]{2,3,1,0:T(8,128)(2,1)S(1)} collective-permute-done((bf16[4,1,256,192]{2,3,1,0:T(8,128)(2,1)S(1)}, bf16[4,1,256,192]{2,3,1,0:T(8,128)(2,1)S(1)}, u32[]{:S(2)}, u32[]{:S(2)}) %collective-permute-start.12) | collective-permute-done | bytes 393248 | tf_op jit(solution)/shard_map/ppermute | solution.py:18
  98.9 5.4 %collective-permute-done.13 = bf16[4,1,256,192]{2,3,1,0:T(8,128)(2,1)S(1)} collective-permute-done((bf16[4,1,256,192]{2,3,1,0:T(8,128)(2,1)S(1)}, bf16[4,1,256,192]{2,3,1,0:T(8,128)(2,1)S(1)}, u32[]{:S(2)}, u32[]{:S(2)}) %collective-permute-start.13) | collective-permute-done | bytes 393248 | tf_op jit(solution)/shard_map/ppermute | solution.py:19
  104.2 2.0 %select_maximum_fusion = bf16[4,4,258,192]{2,3,1,0:T(8,128)(2,1)S(1)} fusion(bf16[4,1,256,192]{2,3,1,0:T(8,128)(2,1)S(1)} %collective-permute-done.13, bf16[4,1,256,192]{2,3,1,0:T(8,128)(2,1)S(1)} %collective-permute-done.12, bf16[2,2,256,192]{2,3,1,0:T(8,128)(2,1)S(1)} %multiply_convert_fusion, bf16[2,2,256,192]{2,3,1,0:T(8,128)(2,1)S(1)} %copy-done.2), kind=kLoop, calls=%fused_computation.11 | loop fusion | flops 11888640 | bytes 3158016 | tf_op jit(solution)/shard_map/concatenate | solution.py:25
  106.2 1.7 %fusion.173 = (bf16[2,2,256,192]{2,3,1,0:T(8,128)(2,1)S(1)}, bf16[2,2,256,192]{2,3,1,0:T(8,128)(2,1)S(1)}, bf16[2,2,256,192]{2,3,1,0:T(8,128)(2,1)S(1)}, bf16[2,...) fusion(bf16[4,4,258,192]{2,3,1,0:T(8,128)(2,1)S(1)} %select_max, ...), kind=kLoop, calls=%fused_computation.250 | loop fusion | bytes 14155776 | tf_op jit(solution)/shard_map/slice | solution.py:65
  108.9 0.5 convolution_add_fusion.7
  109.4 0.5 convolution_add_fusion.6
  109.9 0.5 convolution_add_fusion.5
  111.0 0.5 convolution_add_fusion.3
  111.5 0.5 convolution_add_fusion.2
  112.1 0.5 convolution_add_fusion.1
  112.6 1.3 %fusion.41 = bf16[2,2,256,192]{2,3,1,0:T(8,128)(2,1)} fusion(f32[2,2,256,192]{2,3,1,0:T(8,128)S(1)} %get-tuple-element.105, f32[2,2,256,192]{2,3,1,0:T(8,128)S(1)} %convolution_add_fusion.1, bf16[576,192,1,1]{1,0,3,2:T(8,128)(2,1)S(1)} %bitcast.183, bf16[2,2,256,192]{2,3,1,0:T(8,128)(2,1)S(1)} %get-tuple-element.40, ...), kind=kOutput, calls=%fused_computation.53 | convolution fusion | flops 230621184 | bytes 3366912 | tf_op jit(solution)/shard_map/fhwc,cd->fhwd/dot_general | solution.py:68
  (74 shorter events, 11.0 us)
Async XLA Ops:
  0.0 44.1 %copy-start = (bf16[384,384]{1,0:T(8,128)(2,1)S(1)}, bf16[384,384]{1,0:T(8,128)(2,1)}, u32[]{:S(2)}) copy-start(bf16[384,384]{1,0:T(8,128)(2,1)} %param.15) | copy-start | bytes 884740
  0.0 39.3 %copy-start.3 = (bf16[2,1,128,384]{3,2,1,0:T(8,128)(2,1)S(1)}, bf16[2,1,128,384]{3,2,1,0:T(8,128)(2,1)}, u32[]{:S(2)}) copy-start(bf16[2,1,128,384]{3,2,1,0:T(8,128)(2,1)} %param.10) | copy-start | bytes 589828
  0.0 39.4 %copy-start.10 = (bf16[384,384]{1,0:T(8,128)(2,1)S(1)}, bf16[384,384]{1,0:T(8,128)(2,1)}, u32[]{:S(2)}) copy-start(bf16[384,384]{1,0:T(8,128)(2,1)} %param.13) | copy-start | bytes 884740
  0.0 6.9 %collective-permute-start = (bf16[2,1,128,384]{3,2,1,0:T(8,128)(2,1)}, bf16[2,1,128,384]{3,2,1,0:T(8,128)(2,1)S(1)}, u32[]{:S(2)}, u32[]{:S(2)}) collective-permute-start(bf16[2,1,128,384]{3,2,1,0:T(8,128)(2,1)} %param.10), channel_id=1, source_target_pairs={{0,2},{1,3},{2,4},{3,5},{4,6},{5,7},{6,8},{7,9},{8,10},{9,11},{10,... | collective-permute-start | bytes 589832 | tf_op jit(solution)/shard_map/ppermute | solution.py:36
  1.3 8.9 %collective-permute-start.1 = (bf16[2,1,128,384]{3,2,1,0:T(8,128)(2,1)}, bf16[2,1,128,384]{3,2,1,0:T(8,128)(2,1)S(1)}, u32[]{:S(2)}, u32[]{:S(2)}) collective-permute-start(bf16[2,1,128,384]{3,2,1,0:T(8,128)(2,1)} %param.10), channel_id=1, source_target_pairs={{0,4},{1,5},{2,6},{3,7},{4,8},{5,9},{6,10},{7,11},{8,12},{9,13},{1... | collective-permute-start | bytes 589832 | tf_op jit(solution)/shard_map/ppermute | solution.py:36
  2.6 27.9 %collective-permute-start.2 = (bf16[2,1,128,384]{3,2,1,0:T(8,128)(2,1)}, bf16[2,1,128,384]{3,2,1,0:T(8,128)(2,1)S(1)}, u32[]{:S(2)}, u32[]{:S(2)}) collective-permute-start(bf16[2,1,128,384]{3,2,1,0:T(8,128)(2,1)} %param.10), channel_id=1, source_target_pairs={{0,6},{1,7},{2,8},{3,9},{4,10},{5,11},{6,12},{7,13},{8,14},{9,15},... | collective-permute-start | bytes 589832 | tf_op jit(solution)/shard_map/ppermute | solution.py:36
  3.6 31.1 %collective-permute-start.3 = (bf16[2,1,128,384]{3,2,1,0:T(8,128)(2,1)}, bf16[2,1,128,384]{3,2,1,0:T(8,128)(2,1)S(1)}, u32[]{:S(2)}, u32[]{:S(2)}) collective-permute-start(bf16[2,1,128,384]{3,2,1,0:T(8,128)(2,1)} %param.10), channel_id=1, source_target_pairs={{0,8},{1,9},{2,10},{3,11},{4,12},{5,13},{6,14},{7,15},{8,0},{9,1},... | collective-permute-start | bytes 589832 | tf_op jit(solution)/shard_map/ppermute | solution.py:36
  4.9 29.8 %collective-permute-start.4 = (bf16[2,1,128,384]{3,2,1,0:T(8,128)(2,1)}, bf16[2,1,128,384]{3,2,1,0:T(8,128)(2,1)S(1)}, u32[]{:S(2)}, u32[]{:S(2)}) collective-permute-start(bf16[2,1,128,384]{3,2,1,0:T(8,128)(2,1)} %param.10), channel_id=1, source_target_pairs={{0,10},{1,11},{2,12},{3,13},{4,14},{5,15},{6,0},{7,1},{8,2},{9,3},... | collective-permute-start | bytes 589832 | tf_op jit(solution)/shard_map/ppermute | solution.py:36
  6.9 30.6 %collective-permute-start.5 = (bf16[2,1,128,384]{3,2,1,0:T(8,128)(2,1)}, bf16[2,1,128,384]{3,2,1,0:T(8,128)(2,1)S(1)}, u32[]{:S(2)}, u32[]{:S(2)}) collective-permute-start(bf16[2,1,128,384]{3,2,1,0:T(8,128)(2,1)} %param.10), channel_id=1, source_target_pairs={{0,12},{1,13},{2,14},{3,15},{4,0},{5,1},{6,2},{7,3},{8,4},{9,5},{1... | collective-permute-start | bytes 589832 | tf_op jit(solution)/shard_map/ppermute | solution.py:36
  10.2 28.5 %collective-permute-start.6 = (bf16[2,1,128,384]{3,2,1,0:T(8,128)(2,1)}, bf16[2,1,128,384]{3,2,1,0:T(8,128)(2,1)S(1)}, u32[]{:S(2)}, u32[]{:S(2)}) collective-permute-start(bf16[2,1,128,384]{3,2,1,0:T(8,128)(2,1)} %param.10), channel_id=1, source_target_pairs={{0,14},{1,15},{2,0},{3,1},{4,2},{5,3},{6,4},{7,5},{8,6},{9,7},{10,... | collective-permute-start | bytes 589832 | tf_op jit(solution)/shard_map/ppermute | solution.py:36
  38.7 3.6 %collective-permute-start.7 = (bf16[2,8,128,384]{3,2,1,0:T(8,128)(2,1)S(1)}, bf16[2,8,128,384]{3,2,1,0:T(8,128)(2,1)S(1)}, u32[]{:S(2)}, u32[]{:S(2)}) collective-permute-start(bf16[2,8,128,384]{3,2,1,0:T(8,128)(2,1)S(1)} %get-tuple-element.86), channel_id=1, source_target_pairs={{0,1},{1,0},{2,3},{3,2},{4,5},{5,4},{6,7},{7,6},{8,9},{9,8},{10,11... | collective-permute-start | bytes 4718600 | tf_op jit(solution)/shard_map/ppermute | solution.py:39
  44.1 3.8 %copy-start.8 = (bf16[384,384]{1,0:T(8,128)(2,1)S(1)}, bf16[384,384]{1,0:T(8,128)(2,1)}, u32[]{:S(2)}) copy-start(bf16[384,384]{1,0:T(8,128)(2,1)} %param.14) | copy-start | bytes 884740
  51.6 5.1 %copy-start.9 = (bf16[384,384]{1,0:T(8,128)(2,1)S(1)}, bf16[384,384]{1,0:T(8,128)(2,1)}, u32[]{:S(2)}) copy-start(bf16[384,384]{1,0:T(8,128)(2,1)} %param.16) | copy-start | bytes 884740
  51.6 6.6 %copy-start.5 = (bf16[2,1,128,384]{3,2,1,0:T(8,128)(2,1)S(1)}, bf16[2,1,128,384]{3,2,1,0:T(8,128)(2,1)}, u32[]{:S(2)}) copy-start(bf16[2,1,128,384]{3,2,1,0:T(8,128)(2,1)} %param.11) | copy-start | bytes 589828
  58.3 8.5 %collective-permute-start.8 = (bf16[4,1,128,384]{3,2,0,1:T(8,128)(2,1)S(1)}, bf16[4,1,128,384]{3,2,0,1:T(8,128)(2,1)S(1)}, u32[]{:S(2)}, u32[]{:S(2)}) collective-permute-start(bf16[4,1,128,384]{3,2,0,1:T(8,128)(2,1)S(1)} %pad_maximum_fusion.4), channel_id=1, source_target_pairs={{0,1},{1,2},{2,3},{3,4},{4,5},{5,6},{6,7},{7,8},{8,9},{9,10},{10,1... | collective-permute-start | bytes 1179656 | tf_op jit(solution)/shard_map/ppermute | solution.py:18
  60.2 10.1 %collective-permute-start.9 = (bf16[4,1,128,384]{3,2,0,1:T(8,128)(2,1)S(1)}, bf16[4,1,128,384]{3,2,0,1:T(8,128)(2,1)S(1)}, u32[]{:S(2)}, u32[]{:S(2)}) collective-permute-start(bf16[4,1,128,384]{3,2,0,1:T(8,128)(2,1)S(1)} %pad_maximum_fusion.4), channel_id=1, source_target_pairs={{1,0},{2,1},{3,2},{4,3},{5,4},{6,5},{7,6},{8,7},{9,8},{10,9},{11,1... | collective-permute-start | bytes 1179656 | tf_op jit(solution)/shard_map/ppermute | solution.py:19
  74.8 6.5 %copy-start.6 = (bf16[3,3,384,192]{2,3,1,0:T(8,128)(2,1)S(1)}, bf16[3,3,384,192]{2,3,1,0:T(8,128)(2,1)}, u32[]{:S(2)}) copy-start(bf16[3,3,384,192]{2,3,1,0:T(8,128)(2,1)} %param.18) | copy-start | bytes 3981316
  75.8 8.7 %collective-permute-start.10 = (bf16[2,1,128,384]{3,2,0,1:T(8,128)(2,1)S(1)}, bf16[2,1,128,384]{3,2,0,1:T(8,128)(2,1)S(1)}, u32[]{:S(2)}, u32[]{:S(2)}) collective-permute-start(bf16[2,1,128,384]{3,2,0,1:T(8,128)(2,1)S(1)} %fusion.92), channel_id=1, source_target_pairs={{0,1},{1,2},{2,3},{3,4},{4,5},{5,6},{6,7},{7,8},{8,9},{9,10},{10,1... | collective-permute-start | bytes 589832 | tf_op jit(solution)/shard_map/ppermute | solution.py:18
  77.7 8.0 %collective-permute-start.11 = (bf16[2,1,128,384]{3,2,0,1:T(8,128)(2,1)S(1)}, bf16[2,1,128,384]{3,2,0,1:T(8,128)(2,1)S(1)}, u32[]{:S(2)}, u32[]{:S(2)}) collective-permute-start(bf16[2,1,128,384]{3,2,0,1:T(8,128)(2,1)S(1)} %fusion.92), channel_id=1, source_target_pairs={{1,0},{2,1},{3,2},{4,3},{5,4},{6,5},{7,6},{8,7},{9,8},{10,9},{11,1... | collective-permute-start | bytes 589832 | tf_op jit(solution)/shard_map/ppermute | solution.py:19
  87.1 1.1 copy-start.7
  90.5 1.4 %copy-start.2 = (bf16[2,2,256,192]{2,3,1,0:T(8,128)(2,1)S(1)}, bf16[2,2,256,192]{2,3,1,0:T(8,128)(2,1)}, u32[]{:S(2)}) copy-start(bf16[2,2,256,192]{2,3,1,0:T(8,128)(2,1)} %param.12) | copy-start | bytes 1179652
  91.7 5.4 %copy-start.4 = (bf16[3,3,3,192,192]{4,3,2,1,0:T(8,128)(2,1)S(1)}, bf16[3,3,3,192,192]{4,3,2,1,0:T(8,128)(2,1)}, u32[]{:S(2)}) copy-start(bf16[3,3,3,192,192]{4,3,2,1,0:T(8,128)(2,1)} %param.19) | copy-start | bytes 5971972
  92.1 6.8 %collective-permute-start.12 = (bf16[4,1,256,192]{2,3,1,0:T(8,128)(2,1)S(1)}, bf16[4,1,256,192]{2,3,1,0:T(8,128)(2,1)S(1)}, u32[]{:S(2)}, u32[]{:S(2)}) collective-permute-start(bf16[4,1,256,192]{2,3,1,0:T(8,128)(2,1)S(1)} %get-tuple-element.76), channel_id=1, source_target_pairs={{0,1},{1,2},{2,3},{3,4},{4,5},{5,6},{6,7},{7,8},{8,9},{9,10},{10,1... | collective-permute-start | bytes 1179656 | tf_op jit(solution)/shard_map/ppermute | solution.py:18
  94.1 10.1 %collective-permute-start.13 = (bf16[4,1,256,192]{2,3,1,0:T(8,128)(2,1)S(1)}, bf16[4,1,256,192]{2,3,1,0:T(8,128)(2,1)S(1)}, u32[]{:S(2)}, u32[]{:S(2)}) collective-permute-start(bf16[4,1,256,192]{2,3,1,0:T(8,128)(2,1)S(1)} %get-tuple-element.77), channel_id=1, source_target_pairs={{1,0},{2,1},{3,2},{4,3},{5,4},{6,5},{7,6},{8,7},{9,8},{10,9},{11,1... | collective-permute-start | bytes 1179656 | tf_op jit(solution)/shard_map/ppermute | solution.py:19
  112.1 1.9 %copy-start.1 = (bf16[384,384]{1,0:T(8,128)(2,1)S(1)}, bf16[384,384]{1,0:T(8,128)(2,1)}, u32[]{:S(2)}) copy-start(bf16[384,384]{1,0:T(8,128)(2,1)} %param.15) | copy-start | bytes 884740

commit v10 on v9

--- a/solution.py
+++ b/solution.py
@@ -73,10 +73,7 @@
 
 def attention_kernel(scale, q_ref, k_ref, v_ref, o_ref):
     scores = (
-        lax.dot_general(
-            q_ref[0], k_ref[0], (((1,), (1,)), ((), ())), preferred_element_type=jnp.float32
-        )
-        * scale
+        jnp.dot(q_ref[0], k_ref[0], preferred_element_type=jnp.float32) * scale
     )
     largest = jnp.max(scores, axis=-1, keepdims=True)
     weights = jnp.exp(scores - largest)
@@ -87,7 +84,7 @@
 
 def attend(queries, keys_all, values_all, scale):
     frames, count, channels = queries.shape
-    tokens = keys_all.shape[1]
+    tokens = keys_all.shape[2]
     flops = 4 * frames * count * tokens * channels
     moved = 2 * (queries.size * 2 + keys_all.size + values_all.size)
     return pl.pallas_call(
@@ -95,7 +92,7 @@
         grid=(frames,),
         in_specs=[
             pl.BlockSpec((1, count, channels), lambda f: (f, 0, 0)),
-            pl.BlockSpec((1, tokens, channels), lambda f: (f, 0, 0)),
+            pl.BlockSpec((1, channels, tokens), lambda f: (f, 0, 0)),
             pl.BlockSpec((1, tokens, channels), lambda f: (f, 0, 0)),
         ],
         out_specs=pl.BlockSpec((1, count, channels), lambda f: (f, 0, 0)),
@@ -132,7 +129,9 @@
     normed = rms_scale(features).astype(jnp.bfloat16)
     normed_tokens = normed.reshape(frame_count, row_count * width_count, channels)
     queries = project_rows(normed_tokens, w_query)
-    keys_all = project_rows(all_tokens, w_key)
+    keys_all = jnp.einsum(
+        "ftc,cd->fdt", all_tokens, w_key, preferred_element_type=jnp.float32
+    ).astype(jnp.bfloat16)
     values_all = project_rows(all_tokens, w_value)
     score_scale = 1.0 / math.sqrt(channels)
     attended = attend(queries, keys_all, values_all, score_scale)

time: 116 us -> 115 us (level)
    dot_general x3 -> x2, matrix products: 8.5 us -> 4.79 us  [project_rows(): jnp.einsum('ftc,cd->ftd', tokens, weight, preferred_element_type=jnp.floa...]
    dot_general x0 -> x1, matrix products: none -> 3.49 us  [per_device(): jnp.einsum('ftc,cd->fdt', all_tokens, w_key, preferred_element_type=jnp.f...]
where the time goes in v10:
time: 115 us; the launch traced here: 113 us
  waiting for transfers between devices  43.5 us (38%)
  starting transfers between devices  22.8 us (20%)
  matrix products  22.8 us (20%)
  local copies, waits for them, and re-layouts  13.9 us (12%)
  other arithmetic  4.97 us (4%)
  Pallas kernels  4.74 us (4%)
    ppermute x7, waiting for transfers between devices, gather_rows(): pieces.append(lax.ppermute(x, 'ha', pairs))  30 us
    dot_general x21, matrix products, conv_taps(): jnp.einsum('fhwc,cd->fhwd', stacked, kernel, preferred_element_type=jnp.f...  13.3 us
    ppermute x3, waiting for transfers between devices, halo_rows(): after = lax.ppermute(first, 'ha', down)  10 us
    ppermute x3, starting transfers between devices, halo_rows(): after = lax.ppermute(first, 'ha', down)  9.15 us
    ppermute x7, starting transfers between devices, gather_rows(): pieces.append(lax.ppermute(x, 'ha', pairs))  7.21 us
    ppermute x3, starting transfers between devices, halo_rows(): before = lax.ppermute(last, 'ha', up)  5.89 us
    slice x6, local copies, waits for them, and re-layouts, conv_taps(): kernel = weight[time_off, row_off].reshape(3 * in_channels, out_channels)  5.41 us
    dot_general x2, matrix products, project_rows(): jnp.einsum('ftc,cd->ftd', tokens, weight, preferred_element_type=jnp.floa...  4.79 us
  transfers between devices with their start and end apart: 14, of which 10 were waited for; matrix products, arithmetic and copies ran while one was open for 9% of the time, Pallas kernels for 0%

profile of v10, /device:TPU:13, one launch (start us, length us, event | category | flops | bytes accessed | tf_op | source)
XLA Modules:
  0.0 113.4 jit_solution(17689423311393853595)
XLA Ops:
  0.0 1.3 %collective-permute-start = (bf16[2,1,128,384]{3,2,1,0:T(8,128)(2,1)}, bf16[2,1,128,384]{3,2,1,0:T(8,128)(2,1)S(1)}, u32[]{:S(2)}, u32[]{:S(2)}) collective-permute-start(bf16[2,1,128,384]{3,2,1,0:T(8,128)(2,1)} %param.10), channel_id=1, source_target_pairs={{0,2},{1,3},{2,4},{3,5},{4,6},{5,7},{6,8},{7,9},{8,10},{9,11},{10,... | collective-permute-start | bytes 589832 | tf_op jit(solution)/shard_map/ppermute | solution.py:36
  1.3 1.3 %collective-permute-start.1 = (bf16[2,1,128,384]{3,2,1,0:T(8,128)(2,1)}, bf16[2,1,128,384]{3,2,1,0:T(8,128)(2,1)S(1)}, u32[]{:S(2)}, u32[]{:S(2)}) collective-permute-start(bf16[2,1,128,384]{3,2,1,0:T(8,128)(2,1)} %param.10), channel_id=1, source_target_pairs={{0,4},{1,5},{2,6},{3,7},{4,8},{5,9},{6,10},{7,11},{8,12},{9,13},{1... | collective-permute-start | bytes 589832 | tf_op jit(solution)/shard_map/ppermute | solution.py:36
  2.6 1.0 collective-permute-start.2
  3.6 1.3 %collective-permute-start.3 = (bf16[2,1,128,384]{3,2,1,0:T(8,128)(2,1)}, bf16[2,1,128,384]{3,2,1,0:T(8,128)(2,1)S(1)}, u32[]{:S(2)}, u32[]{:S(2)}) collective-permute-start(bf16[2,1,128,384]{3,2,1,0:T(8,128)(2,1)} %param.10), channel_id=1, source_target_pairs={{0,8},{1,9},{2,10},{3,11},{4,12},{5,13},{6,14},{7,15},{8,0},{9,1},... | collective-permute-start | bytes 589832 | tf_op jit(solution)/shard_map/ppermute | solution.py:36
  4.9 1.0 collective-permute-start.4
  5.9 1.0 constant_dynamic-update-slice_fusion.7
  6.9 1.3 %collective-permute-start.5 = (bf16[2,1,128,384]{3,2,1,0:T(8,128)(2,1)}, bf16[2,1,128,384]{3,2,1,0:T(8,128)(2,1)S(1)}, u32[]{:S(2)}, u32[]{:S(2)}) collective-permute-start(bf16[2,1,128,384]{3,2,1,0:T(8,128)(2,1)} %param.10), channel_id=1, source_target_pairs={{0,12},{1,13},{2,14},{3,15},{4,0},{5,1},{6,2},{7,3},{8,4},{9,5},{1... | collective-permute-start | bytes 589832 | tf_op jit(solution)/shard_map/ppermute | solution.py:36
  8.3 1.9 %collective-permute-done.1 = bf16[2,1,128,384]{3,2,1,0:T(8,128)(2,1)S(1)} collective-permute-done((bf16[2,1,128,384]{3,2,1,0:T(8,128)(2,1)}, bf16[2,1,128,384]{3,2,1,0:T(8,128)(2,1)S(1)}, u32[]{:S(2)}, u32[]{:S(2)}) %collective-permute-start.1) | collective-permute-done | bytes 196640 | tf_op jit(solution)/shard_map/ppermute | solution.py:36
  10.3 20.2 %collective-permute-done.2 = bf16[2,1,128,384]{3,2,1,0:T(8,128)(2,1)S(1)} collective-permute-done((bf16[2,1,128,384]{3,2,1,0:T(8,128)(2,1)}, bf16[2,1,128,384]{3,2,1,0:T(8,128)(2,1)S(1)}, u32[]{:S(2)}, u32[]{:S(2)}) %collective-permute-start.2) | collective-permute-done | bytes 196640 | tf_op jit(solution)/shard_map/ppermute | solution.py:36
  30.5 4.1 %collective-permute-done.3 = bf16[2,1,128,384]{3,2,1,0:T(8,128)(2,1)S(1)} collective-permute-done((bf16[2,1,128,384]{3,2,1,0:T(8,128)(2,1)}, bf16[2,1,128,384]{3,2,1,0:T(8,128)(2,1)S(1)}, u32[]{:S(2)}, u32[]{:S(2)}) %collective-permute-start.3) | collective-permute-done | bytes 196640 | tf_op jit(solution)/shard_map/ppermute | solution.py:36
  34.8 2.7 %collective-permute-done.5 = bf16[2,1,128,384]{3,2,1,0:T(8,128)(2,1)S(1)} collective-permute-done((bf16[2,1,128,384]{3,2,1,0:T(8,128)(2,1)}, bf16[2,1,128,384]{3,2,1,0:T(8,128)(2,1)S(1)}, u32[]{:S(2)}, u32[]{:S(2)}) %collective-permute-start.5) | collective-permute-done | bytes 196640 | tf_op jit(solution)/shard_map/ppermute | solution.py:36
  37.6 1.1 collective-permute-done.6
  38.7 0.6 collective-permute-start.7
  39.4 1.0 convolution_convert_fusion.2.q_ref
  40.4 1.9 %collective-permute-done.7 = bf16[2,8,128,384]{3,2,1,0:T(8,128)(2,1)S(1)} collective-permute-done((bf16[2,8,128,384]{3,2,1,0:T(8,128)(2,1)S(1)}, bf16[2,8,128,384]{3,2,1,0:T(8,128)(2,1)S(1)}, u32[]{:S(2)}, u32[]{:S(2)}) %collective-permute-start.7) | collective-permute-done | bytes 1572896 | tf_op jit(solution)/shard_map/ppermute | solution.py:39
  42.6 0.7 multiply_reduce_fusion
  43.4 0.7 fusion
  44.1 3.8 %convolution_convert_fusion.v_ref = bf16[2,2048,384]{2,1,0:T(8,128)(2,1)} fusion(bf16[2,2048,384]{2,1,0:T(8,128)(2,1)S(1)} %fusion, bf16[384,384]{1,0:T(8,128)(2,1)S(1)} %copy-done), kind=kOutput, calls=%fused_computation.8 | convolution fusion | flops 1209532416 | bytes 6586368 | tf_op jit(solution)/shard_map/ftc,cd->ftd/dot_general | solution.py:108
  47.9 3.5 %fusion.2.k_ref = bf16[2,384,2048]{2,1,0:T(8,128)(2,1)} fusion(bf16[2,2048,384]{2,1,0:T(8,128)(2,1)S(1)} %fusion, bf16[384,384]{1,0:T(8,128)(2,1)S(1)} %copy-done.8), kind=kOutput, calls=%fused_computation.10 | convolution fusion | flops 1209532416 | bytes 6586368 | tf_op jit(solution)/shard_map/ftc,cd->fdt/dot_general | solution.py:132
  51.4 4.7 %shard_map.100 = bf16[2,128,384]{2,1,0:T(8,128)(2,1)} custom-call(bf16[2,128,384]{2,1,0:T(8,128)(2,1)} %convolution_convert_fusion.2.q_ref, bf16[2,384,2048]{2,1,0:T(8,128)(2,1)} %fusion.2.k_ref, bf16[2,2048,384]{2,1,0:T(8,128)(2,1)} %convolution_convert_fusion.v_ref), custom_call_target="tpu_custom_call" | custom-call | flops 805306368 | bytes 6684672 | tf_op jit(solution)/shard_map/pallas_call | solution.py:90
  56.1 1.3 %multiply_reduce_fusion.2 = (f32[2,128]{1,0:T(2,128)S(1)}, f32[2,1,128,384]{3,2,0,1:T(8,128)S(1)}) fusion(bf16[2,128,384]{2,1,0:T(8,128)(2,1)} %shard_map.100, bf16[384,384]{1,0:T(8,128)(2,1)S(1)} %copy-done.9, bf16[2,1,128,384]{3,2,1,0:T(8,128)(2,1)S(1)} %copy-done.3), kind=kOutput, calls=%fused_computation.197 | convolution fusion | flops 76087040 | bytes 1082368 | tf_op jit(solution)/shard_map/ftc,cd->ftd/dot_general | solution.py:138
  57.7 1.9 %collective-permute-start.8 = (bf16[4,1,128,384]{3,2,0,1:T(8,128)(2,1)S(1)}, bf16[4,1,128,384]{3,2,0,1:T(8,128)(2,1)S(1)}, u32[]{:S(2)}, u32[]{:S(2)}) collective-permute-start(bf16[4,1,128,384]{3,2,0,1:T(8,128)(2,1)S(1)} %pad_maximum_fusion.4), channel_id=1, source_target_pairs={{0,1},{1,2},{2,3},{3,4},{4,5},{5,6},{6,7},{7,8},{8,9},{9,10},{10,1... | collective-permute-start | bytes 1179656 | tf_op jit(solution)/shard_map/ppermute | solution.py:18
  59.6 2.6 %collective-permute-start.9 = (bf16[4,1,128,384]{3,2,0,1:T(8,128)(2,1)S(1)}, bf16[4,1,128,384]{3,2,0,1:T(8,128)(2,1)S(1)}, u32[]{:S(2)}, u32[]{:S(2)}) collective-permute-start(bf16[4,1,128,384]{3,2,0,1:T(8,128)(2,1)S(1)} %pad_maximum_fusion.4), channel_id=1, source_target_pairs={{1,0},{2,1},{3,2},{4,3},{5,4},{6,5},{7,6},{8,7},{9,8},{10,9},{11,1... | collective-permute-start | bytes 1179656 | tf_op jit(solution)/shard_map/ppermute | solution.py:19
  62.2 3.9 %fusion.172 = (bf16[1,1,3,384,384]{4,3,2,1,0:T(8,128)(2,1)S(1)}, bf16[1,1,3,384,384]{4,3,2,1,0:T(8,128)(2,1)S(1)}, bf16[1,1,3,384,384]{4,3,2,1,0:T(8,128)(2,1)S(...) fusion(bf16[3,3,3,384,384]{4,3,2,1,0:T(8,128)(2,1)} %param.17), kind=kLoop, calls=%fused_computation.249 | loop fusion | bytes 15925248 | tf_op jit(solution)/shard_map/slice | solution.py:67
  66.2 3.5 %collective-permute-done.9 = bf16[4,1,128,384]{3,2,0,1:T(8,128)(2,1)S(1)} collective-permute-done((bf16[4,1,128,384]{3,2,0,1:T(8,128)(2,1)S(1)}, bf16[4,1,128,384]{3,2,0,1:T(8,128)(2,1)S(1)}, u32[]{:S(2)}, u32[]{:S(2)}) %collective-permute-start.9) | collective-permute-done | bytes 393248 | tf_op jit(solution)/shard_map/ppermute | solution.py:19
  70.1 0.7 fusion.176
  75.2 1.9 %collective-permute-start.10 = (bf16[2,1,128,384]{3,2,0,1:T(8,128)(2,1)S(1)}, bf16[2,1,128,384]{3,2,0,1:T(8,128)(2,1)S(1)}, u32[]{:S(2)}, u32[]{:S(2)}) collective-permute-start(bf16[2,1,128,384]{3,2,0,1:T(8,128)(2,1)S(1)} %fusion.93), channel_id=1, source_target_pairs={{0,1},{1,2},{2,3},{3,4},{4,5},{5,6},{6,7},{7,8},{8,9},{9,10},{10,1... | collective-permute-start | bytes 589832 | tf_op jit(solution)/shard_map/ppermute | solution.py:18
  77.2 3.6 %collective-permute-start.11 = (bf16[2,1,128,384]{3,2,0,1:T(8,128)(2,1)S(1)}, bf16[2,1,128,384]{3,2,0,1:T(8,128)(2,1)S(1)}, u32[]{:S(2)}, u32[]{:S(2)}) collective-permute-start(bf16[2,1,128,384]{3,2,0,1:T(8,128)(2,1)S(1)} %fusion.93), channel_id=1, source_target_pairs={{1,0},{2,1},{3,2},{4,3},{5,4},{6,5},{7,6},{8,7},{9,8},{10,9},{11,1... | collective-permute-start | bytes 589832 | tf_op jit(solution)/shard_map/ppermute | solution.py:19
  81.3 1.2 %reshape.134 = bf16[1152,192,1,1]{0,1,2,3:T(8,128)(2,1)} reshape(bf16[1,1,3,384,192]{3,2,4,1,0:T(4,128)(2,1)S(1)} %copy.32) | data formatting | bytes 884736 | tf_op jit(solution)/shard_map/reshape;squeeze | solution.py:67
  84.0 1.2 %collective-permute-done.11 = bf16[2,1,128,384]{3,2,0,1:T(8,128)(2,1)S(1)} collective-permute-done((bf16[2,1,128,384]{3,2,0,1:T(8,128)(2,1)S(1)}, bf16[2,1,128,384]{3,2,0,1:T(8,128)(2,1)S(1)}, u32[]{:S(2)}, u32[]{:S(2)}) %collective-permute-start.11) | collective-permute-done | bytes 196640 | tf_op jit(solution)/shard_map/ppermute | solution.py:19
  85.3 0.6 broadcast_in_dim.4
  86.6 0.8 pad_slice_fusion.9
  87.7 1.2 %fusion.8 = f32[2,2,256,192]{2,3,1,0:T(8,128)S(1)} fusion(bf16[2,1,258,384]{3,2,1,0:T(8,128)(2,1)S(1)} %pad_slice_fusion.10, bf16[2,2,256,384]{3,2,1,0:T(8,128)(2,1)S(1)} %get-tuple-element.79, bf16[2,2,256,384]{3,2,1,0:T(8,128)(2,1)S(1)} %get-tuple-element.78, bf16[1152,192,1,1]{0,1,2,3:T(8,128)(2,1)S(1)} %copy-done.7), kind=kOutput, calls=%fused_computation.19 | convolution fusion | flops 462422016 | bytes 3197952 | tf_op jit(solution)/shard_map/fhwc,cd->fhwd/dot_general | solution.py:68
  88.9 1.1 %fusion.30 = f32[2,2,256,192]{2,3,1,0:T(8,128)S(1)} fusion(f32[2,2,256,192]{2,3,1,0:T(8,128)S(1)} %fusion.8, bf16[2,2,256,384]{3,2,1,0:T(8,128)(2,1)S(1)} %get-tuple-element.69, bf16[2,2,256,384]{3,2,1,0:T(8,128)(2,1)S(1)} %get-tuple-element.72, bf16[2,2,256,384]{3,2,1,0:T(8,128)(2,1)S(1)} %get-tuple-element.73, bf16[1152,192,1,1]{0,1,2,3:T(8,128)(2,1)S(1)} %reshape.133), kind=kOutput, calls=%fused_computation.46 | convolution fusion | flops 460259328 | bytes 4374528 | tf_op jit(solution)/shard_map/fhwc,cd->fhwd/dot_general | solution.py:68
  90.0 1.2 %multiply_reduce_fusion.1 = (f32[2,2,256]{2,1,0:T(2,128)S(1)}, f32[2,2,256,192]{2,3,1,0:T(8,128)S(1)}) fusion(f32[2,2,256,192]{2,3,1,0:T(8,128)S(1)} %fusion.30, bf16[1152,192,1,1]{0,1,2,3:T(8,128)(2,1)S(1)} %reshape.135, bf16[2,2,256,384]{3,2,1,0:T(8,128)(2,1)S(1)} %get-tuple-element.70, bf16[2,2,256,384]{3,2,1,0:T(8,128)(2,1)S(1)} %get-tuple-element.71, ...), kind=kOutput, calls=%fused_computation.131 | convolution fusion | flops 461044736 | bytes 4378624 | tf_op jit(solution)/shard_map/fhwc,cd->fhwd/dot_general | solution.py:68
  91.5 2.1 %collective-permute-start.12 = (bf16[4,1,256,192]{2,3,1,0:T(8,128)(2,1)S(1)}, bf16[4,1,256,192]{2,3,1,0:T(8,128)(2,1)S(1)}, u32[]{:S(2)}, u32[]{:S(2)}) collective-permute-start(bf16[4,1,256,192]{2,3,1,0:T(8,128)(2,1)S(1)} %get-tuple-element.76), channel_id=1, source_target_pairs={{0,1},{1,2},{2,3},{3,4},{4,5},{5,6},{6,7},{7,8},{8,9},{9,10},{10,1... | collective-permute-start | bytes 1179656 | tf_op jit(solution)/shard_map/ppermute | solution.py:18
  93.6 3.0 %collective-permute-start.13 = (bf16[4,1,256,192]{2,3,1,0:T(8,128)(2,1)S(1)}, bf16[4,1,256,192]{2,3,1,0:T(8,128)(2,1)S(1)}, u32[]{:S(2)}, u32[]{:S(2)}) collective-permute-start(bf16[4,1,256,192]{2,3,1,0:T(8,128)(2,1)S(1)} %get-tuple-element.77), channel_id=1, source_target_pairs={{1,0},{2,1},{3,2},{4,3},{5,4},{6,5},{7,6},{8,7},{9,8},{10,9},{11,1... | collective-permute-start | bytes 1179656 | tf_op jit(solution)/shard_map/ppermute | solution.py:19
  96.8 1.6 %collective-permute-done.12 = bf16[4,1,256,192]{2,3,1,0:T(8,128)(2,1)S(1)} collective-permute-done((bf16[4,1,256,192]{2,3,1,0:T(8,128)(2,1)S(1)}, bf16[4,1,256,192]{2,3,1,0:T(8,128)(2,1)S(1)}, u32[]{:S(2)}, u32[]{:S(2)}) %collective-permute-start.12) | collective-permute-done | bytes 393248 | tf_op jit(solution)/shard_map/ppermute | solution.py:18
  98.3 5.4 %collective-permute-done.13 = bf16[4,1,256,192]{2,3,1,0:T(8,128)(2,1)S(1)} collective-permute-done((bf16[4,1,256,192]{2,3,1,0:T(8,128)(2,1)S(1)}, bf16[4,1,256,192]{2,3,1,0:T(8,128)(2,1)S(1)}, u32[]{:S(2)}, u32[]{:S(2)}) %collective-permute-start.13) | collective-permute-done | bytes 393248 | tf_op jit(solution)/shard_map/ppermute | solution.py:19
  103.7 2.0 %select_maximum_fusion = bf16[4,4,258,192]{2,3,1,0:T(8,128)(2,1)S(1)} fusion(bf16[4,1,256,192]{2,3,1,0:T(8,128)(2,1)S(1)} %collective-permute-done.13, bf16[4,1,256,192]{2,3,1,0:T(8,128)(2,1)S(1)} %collective-permute-done.12, bf16[2,2,256,192]{2,3,1,0:T(8,128)(2,1)S(1)} %multiply_convert_fusion, bf16[2,2,256,192]{2,3,1,0:T(8,128)(2,1)S(1)} %copy-done.2), kind=kLoop, calls=%fused_computation.12 | loop fusion | flops 11888640 | bytes 3158016 | tf_op jit(solution)/shard_map/concatenate | solution.py:25
  105.7 1.7 %fusion.174 = (bf16[2,2,256,192]{2,3,1,0:T(8,128)(2,1)S(1)}, bf16[2,2,256,192]{2,3,1,0:T(8,128)(2,1)S(1)}, bf16[2,2,256,192]{2,3,1,0:T(8,128)(2,1)S(1)}, bf16[2,...) fusion(bf16[4,4,258,192]{2,3,1,0:T(8,128)(2,1)S(1)} %select_max, ...), kind=kLoop, calls=%fused_computation.251 | loop fusion | bytes 14155776 | tf_op jit(solution)/shard_map/slice | solution.py:65
  108.3 0.5 convolution_add_fusion.7
  108.9 0.5 convolution_add_fusion.6
  109.4 0.5 convolution_add_fusion.5
  110.5 0.5 convolution_add_fusion.3
  111.0 0.5 convolution_add_fusion.2
  111.5 0.5 convolution_add_fusion.1
  112.1 1.3 %fusion.42 = bf16[2,2,256,192]{2,3,1,0:T(8,128)(2,1)} fusion(f32[2,2,256,192]{2,3,1,0:T(8,128)S(1)} %get-tuple-element.105, f32[2,2,256,192]{2,3,1,0:T(8,128)S(1)} %convolution_add_fusion.1, bf16[576,192,1,1]{1,0,3,2:T(8,128)(2,1)S(1)} %bitcast.185, bf16[2,2,256,192]{2,3,1,0:T(8,128)(2,1)S(1)} %get-tuple-element.40, ...), kind=kOutput, calls=%fused_computation.54 | convolution fusion | flops 230621184 | bytes 3366912 | tf_op jit(solution)/shard_map/fhwc,cd->fhwd/dot_general | solution.py:68
  (74 shorter events, 11.0 us)
Async XLA Ops:
  0.0 44.1 %copy-start = (bf16[384,384]{1,0:T(8,128)(2,1)S(1)}, bf16[384,384]{1,0:T(8,128)(2,1)}, u32[]{:S(2)}) copy-start(bf16[384,384]{1,0:T(8,128)(2,1)} %param.15) | copy-start | bytes 884740
  0.0 39.3 %copy-start.3 = (bf16[2,1,128,384]{3,2,1,0:T(8,128)(2,1)S(1)}, bf16[2,1,128,384]{3,2,1,0:T(8,128)(2,1)}, u32[]{:S(2)}) copy-start(bf16[2,1,128,384]{3,2,1,0:T(8,128)(2,1)} %param.10) | copy-start | bytes 589828
  0.0 39.4 %copy-start.10 = (bf16[384,384]{1,0:T(8,128)(2,1)S(1)}, bf16[384,384]{1,0:T(8,128)(2,1)}, u32[]{:S(2)}) copy-start(bf16[384,384]{1,0:T(8,128)(2,1)} %param.13) | copy-start | bytes 884740
  0.0 6.9 %collective-permute-start = (bf16[2,1,128,384]{3,2,1,0:T(8,128)(2,1)}, bf16[2,1,128,384]{3,2,1,0:T(8,128)(2,1)S(1)}, u32[]{:S(2)}, u32[]{:S(2)}) collective-permute-start(bf16[2,1,128,384]{3,2,1,0:T(8,128)(2,1)} %param.10), channel_id=1, source_target_pairs={{0,2},{1,3},{2,4},{3,5},{4,6},{5,7},{6,8},{7,9},{8,10},{9,11},{10,... | collective-permute-start | bytes 589832 | tf_op jit(solution)/shard_map/ppermute | solution.py:36
  1.3 8.9 %collective-permute-start.1 = (bf16[2,1,128,384]{3,2,1,0:T(8,128)(2,1)}, bf16[2,1,128,384]{3,2,1,0:T(8,128)(2,1)S(1)}, u32[]{:S(2)}, u32[]{:S(2)}) collective-permute-start(bf16[2,1,128,384]{3,2,1,0:T(8,128)(2,1)} %param.10), channel_id=1, source_target_pairs={{0,4},{1,5},{2,6},{3,7},{4,8},{5,9},{6,10},{7,11},{8,12},{9,13},{1... | collective-permute-start | bytes 589832 | tf_op jit(solution)/shard_map/ppermute | solution.py:36
  2.6 27.9 %collective-permute-start.2 = (bf16[2,1,128,384]{3,2,1,0:T(8,128)(2,1)}, bf16[2,1,128,384]{3,2,1,0:T(8,128)(2,1)S(1)}, u32[]{:S(2)}, u32[]{:S(2)}) collective-permute-start(bf16[2,1,128,384]{3,2,1,0:T(8,128)(2,1)} %param.10), channel_id=1, source_target_pairs={{0,6},{1,7},{2,8},{3,9},{4,10},{5,11},{6,12},{7,13},{8,14},{9,15},... | collective-permute-start | bytes 589832 | tf_op jit(solution)/shard_map/ppermute | solution.py:36
  3.6 31.1 %collective-permute-start.3 = (bf16[2,1,128,384]{3,2,1,0:T(8,128)(2,1)}, bf16[2,1,128,384]{3,2,1,0:T(8,128)(2,1)S(1)}, u32[]{:S(2)}, u32[]{:S(2)}) collective-permute-start(bf16[2,1,128,384]{3,2,1,0:T(8,128)(2,1)} %param.10), channel_id=1, source_target_pairs={{0,8},{1,9},{2,10},{3,11},{4,12},{5,13},{6,14},{7,15},{8,0},{9,1},... | collective-permute-start | bytes 589832 | tf_op jit(solution)/shard_map/ppermute | solution.py:36
  4.9 29.8 %collective-permute-start.4 = (bf16[2,1,128,384]{3,2,1,0:T(8,128)(2,1)}, bf16[2,1,128,384]{3,2,1,0:T(8,128)(2,1)S(1)}, u32[]{:S(2)}, u32[]{:S(2)}) collective-permute-start(bf16[2,1,128,384]{3,2,1,0:T(8,128)(2,1)} %param.10), channel_id=1, source_target_pairs={{0,10},{1,11},{2,12},{3,13},{4,14},{5,15},{6,0},{7,1},{8,2},{9,3},... | collective-permute-start | bytes 589832 | tf_op jit(solution)/shard_map/ppermute | solution.py:36
  6.9 30.6 %collective-permute-start.5 = (bf16[2,1,128,384]{3,2,1,0:T(8,128)(2,1)}, bf16[2,1,128,384]{3,2,1,0:T(8,128)(2,1)S(1)}, u32[]{:S(2)}, u32[]{:S(2)}) collective-permute-start(bf16[2,1,128,384]{3,2,1,0:T(8,128)(2,1)} %param.10), channel_id=1, source_target_pairs={{0,12},{1,13},{2,14},{3,15},{4,0},{5,1},{6,2},{7,3},{8,4},{9,5},{1... | collective-permute-start | bytes 589832 | tf_op jit(solution)/shard_map/ppermute | solution.py:36
  10.2 28.5 %collective-permute-start.6 = (bf16[2,1,128,384]{3,2,1,0:T(8,128)(2,1)}, bf16[2,1,128,384]{3,2,1,0:T(8,128)(2,1)S(1)}, u32[]{:S(2)}, u32[]{:S(2)}) collective-permute-start(bf16[2,1,128,384]{3,2,1,0:T(8,128)(2,1)} %param.10), channel_id=1, source_target_pairs={{0,14},{1,15},{2,0},{3,1},{4,2},{5,3},{6,4},{7,5},{8,6},{9,7},{10,... | collective-permute-start | bytes 589832 | tf_op jit(solution)/shard_map/ppermute | solution.py:36
  38.7 3.6 %collective-permute-start.7 = (bf16[2,8,128,384]{3,2,1,0:T(8,128)(2,1)S(1)}, bf16[2,8,128,384]{3,2,1,0:T(8,128)(2,1)S(1)}, u32[]{:S(2)}, u32[]{:S(2)}) collective-permute-start(bf16[2,8,128,384]{3,2,1,0:T(8,128)(2,1)S(1)} %get-tuple-element.86), channel_id=1, source_target_pairs={{0,1},{1,0},{2,3},{3,2},{4,5},{5,4},{6,7},{7,6},{8,9},{9,8},{10,11... | collective-permute-start | bytes 4718600 | tf_op jit(solution)/shard_map/ppermute | solution.py:39
  44.1 3.8 %copy-start.8 = (bf16[384,384]{1,0:T(8,128)(2,1)S(1)}, bf16[384,384]{1,0:T(8,128)(2,1)}, u32[]{:S(2)}) copy-start(bf16[384,384]{1,0:T(8,128)(2,1)} %param.14) | copy-start | bytes 884740
  51.4 4.7 %copy-start.9 = (bf16[384,384]{1,0:T(8,128)(2,1)S(1)}, bf16[384,384]{1,0:T(8,128)(2,1)}, u32[]{:S(2)}) copy-start(bf16[384,384]{1,0:T(8,128)(2,1)} %param.16) | copy-start | bytes 884740
  51.4 6.3 %copy-start.5 = (bf16[2,1,128,384]{3,2,1,0:T(8,128)(2,1)S(1)}, bf16[2,1,128,384]{3,2,1,0:T(8,128)(2,1)}, u32[]{:S(2)}) copy-start(bf16[2,1,128,384]{3,2,1,0:T(8,128)(2,1)} %param.11) | copy-start | bytes 589828
  57.7 8.5 %collective-permute-start.8 = (bf16[4,1,128,384]{3,2,0,1:T(8,128)(2,1)S(1)}, bf16[4,1,128,384]{3,2,0,1:T(8,128)(2,1)S(1)}, u32[]{:S(2)}, u32[]{:S(2)}) collective-permute-start(bf16[4,1,128,384]{3,2,0,1:T(8,128)(2,1)S(1)} %pad_maximum_fusion.4), channel_id=1, source_target_pairs={{0,1},{1,2},{2,3},{3,4},{4,5},{5,6},{6,7},{7,8},{8,9},{9,10},{10,1... | collective-permute-start | bytes 1179656 | tf_op jit(solution)/shard_map/ppermute | solution.py:18
  59.6 10.1 %collective-permute-start.9 = (bf16[4,1,128,384]{3,2,0,1:T(8,128)(2,1)S(1)}, bf16[4,1,128,384]{3,2,0,1:T(8,128)(2,1)S(1)}, u32[]{:S(2)}, u32[]{:S(2)}) collective-permute-start(bf16[4,1,128,384]{3,2,0,1:T(8,128)(2,1)S(1)} %pad_maximum_fusion.4), channel_id=1, source_target_pairs={{1,0},{2,1},{3,2},{4,3},{5,4},{6,5},{7,6},{8,7},{9,8},{10,9},{11,1... | collective-permute-start | bytes 1179656 | tf_op jit(solution)/shard_map/ppermute | solution.py:19
  74.3 6.5 %copy-start.6 = (bf16[3,3,384,192]{2,3,1,0:T(8,128)(2,1)S(1)}, bf16[3,3,384,192]{2,3,1,0:T(8,128)(2,1)}, u32[]{:S(2)}) copy-start(bf16[3,3,384,192]{2,3,1,0:T(8,128)(2,1)} %param.18) | copy-start | bytes 3981316
  75.2 8.8 %collective-permute-start.10 = (bf16[2,1,128,384]{3,2,0,1:T(8,128)(2,1)S(1)}, bf16[2,1,128,384]{3,2,0,1:T(8,128)(2,1)S(1)}, u32[]{:S(2)}, u32[]{:S(2)}) collective-permute-start(bf16[2,1,128,384]{3,2,0,1:T(8,128)(2,1)S(1)} %fusion.93), channel_id=1, source_target_pairs={{0,1},{1,2},{2,3},{3,4},{4,5},{5,6},{6,7},{7,8},{8,9},{9,10},{10,1... | collective-permute-start | bytes 589832 | tf_op jit(solution)/shard_map/ppermute | solution.py:18
  77.2 8.0 %collective-permute-start.11 = (bf16[2,1,128,384]{3,2,0,1:T(8,128)(2,1)S(1)}, bf16[2,1,128,384]{3,2,0,1:T(8,128)(2,1)S(1)}, u32[]{:S(2)}, u32[]{:S(2)}) collective-permute-start(bf16[2,1,128,384]{3,2,0,1:T(8,128)(2,1)S(1)} %fusion.93), channel_id=1, source_target_pairs={{1,0},{2,1},{3,2},{4,3},{5,4},{6,5},{7,6},{8,7},{9,8},{10,9},{11,1... | collective-permute-start | bytes 589832 | tf_op jit(solution)/shard_map/ppermute | solution.py:19
  86.5 1.1 copy-start.7
  90.0 1.4 %copy-start.2 = (bf16[2,2,256,192]{2,3,1,0:T(8,128)(2,1)S(1)}, bf16[2,2,256,192]{2,3,1,0:T(8,128)(2,1)}, u32[]{:S(2)}) copy-start(bf16[2,2,256,192]{2,3,1,0:T(8,128)(2,1)} %param.12) | copy-start | bytes 1179652
  91.2 5.4 %copy-start.4 = (bf16[3,3,3,192,192]{4,3,2,1,0:T(8,128)(2,1)S(1)}, bf16[3,3,3,192,192]{4,3,2,1,0:T(8,128)(2,1)}, u32[]{:S(2)}) copy-start(bf16[3,3,3,192,192]{4,3,2,1,0:T(8,128)(2,1)} %param.19) | copy-start | bytes 5971972
  91.5 6.8 %collective-permute-start.12 = (bf16[4,1,256,192]{2,3,1,0:T(8,128)(2,1)S(1)}, bf16[4,1,256,192]{2,3,1,0:T(8,128)(2,1)S(1)}, u32[]{:S(2)}, u32[]{:S(2)}) collective-permute-start(bf16[4,1,256,192]{2,3,1,0:T(8,128)(2,1)S(1)} %get-tuple-element.76), channel_id=1, source_target_pairs={{0,1},{1,2},{2,3},{3,4},{4,5},{5,6},{6,7},{7,8},{8,9},{9,10},{10,1... | collective-permute-start | bytes 1179656 | tf_op jit(solution)/shard_map/ppermute | solution.py:18
  93.6 10.1 %collective-permute-start.13 = (bf16[4,1,256,192]{2,3,1,0:T(8,128)(2,1)S(1)}, bf16[4,1,256,192]{2,3,1,0:T(8,128)(2,1)S(1)}, u32[]{:S(2)}, u32[]{:S(2)}) collective-permute-start(bf16[4,1,256,192]{2,3,1,0:T(8,128)(2,1)S(1)} %get-tuple-element.77), channel_id=1, source_target_pairs={{1,0},{2,1},{3,2},{4,3},{5,4},{6,5},{7,6},{8,7},{9,8},{10,9},{11,1... | collective-permute-start | bytes 1179656 | tf_op jit(solution)/shard_map/ppermute | solution.py:19
  111.5 1.9 %copy-start.1 = (bf16[384,384]{1,0:T(8,128)(2,1)S(1)}, bf16[384,384]{1,0:T(8,128)(2,1)}, u32[]{:S(2)}) copy-start(bf16[384,384]{1,0:T(8,128)(2,1)} %param.15) | copy-start | bytes 884740

commit v11 on v10

--- a/solution.py
+++ b/solution.py
@@ -23,6 +23,18 @@
 def extended(x, dim, width):
     before, after = halo_rows(x, dim, width)
     return jnp.concatenate([before, x, after], axis=dim)
+
+
+def gather_chip_rows(x):
+    count = lax.axis_size("ha")
+    chips = count // 2
+    pieces = [x]
+    for shift in range(1, chips):
+        pairs = [
+            (2 * c + k, 2 * ((c + shift) % chips) + k) for c in range(chips) for k in range(2)
+        ]
+        pieces.append(lax.ppermute(x, "ha", pairs))
+    return jnp.concatenate(pieces, axis=1)
 
 
 def gather_rows(x):
@@ -123,11 +135,17 @@
     w_second,
 ):
     frame_count, row_count, width_count, channels = features.shape
-    every_row = gather_rows(features)
+    core = lax.axis_index("ha") % 2
+    count = lax.axis_size("ha")
+    swap = [(i, i ^ 1) for i in range(count)]
+    other = lax.dynamic_slice_in_dim(features, 1 - core, 1, axis=0)
+    mine = lax.dynamic_slice_in_dim(features, core, 1, axis=0)
+    block = jnp.concatenate([mine, lax.ppermute(other, "ha", swap)], axis=1)
+    every_row = gather_chip_rows(block)
     normed_all = rms_scale(every_row).astype(jnp.bfloat16)
-    all_tokens = normed_all.reshape(frame_count, -1, channels)
-    normed = rms_scale(features).astype(jnp.bfloat16)
-    normed_tokens = normed.reshape(frame_count, row_count * width_count, channels)
+    all_tokens = normed_all.reshape(1, -1, channels)
+    normed = rms_scale(block).astype(jnp.bfloat16)
+    normed_tokens = normed.reshape(1, -1, channels)
     queries = project_rows(normed_tokens, w_query)
     keys_all = jnp.einsum(
         "ftc,cd->fdt", all_tokens, w_key, preferred_element_type=jnp.float32
@@ -136,10 +154,16 @@
     score_scale = 1.0 / math.sqrt(channels)
     attended = attend(queries, keys_all, values_all, score_scale)
     projected = jnp.einsum("ftc,cd->ftd", attended, w_output, preferred_element_type=jnp.float32)
-    mixed = (
-        features.astype(jnp.float32)
-        + projected.reshape(frame_count, row_count, width_count, channels)
-    ).astype(jnp.bfloat16)
+    mixed_block = (block.astype(jnp.float32) + projected.reshape(block.shape)).astype(
+        jnp.bfloat16
+    )
+    back = lax.ppermute(mixed_block[:, 1:2], "ha", swap)
+    own = mixed_block[:, 0:1]
+    mixed = jnp.where(
+        core == 0,
+        jnp.concatenate([own, back], axis=0),
+        jnp.concatenate([back, own], axis=0),
+    )
     first_in = jax.nn.silu(rms_scale(mixed)).astype(jnp.bfloat16)
     first_stack = jnp.concatenate([first_cache, first_in], axis=0)
     first_padded = extended(first_stack, 1, 1)

time: 115 us -> 113 us (0.983); the launches traced: 113 us -> 113 us
  starting transfers between devices: 22.8 us -> 27.4 us
  matrix products: 22.8 us -> 19.9 us
  waiting for transfers between devices: 43.5 us -> 41.8 us
    ppermute x3, starting transfers between devices: 5.89 us -> 11.7 us  [halo_rows(): before = lax.ppermute(last, 'ha', up)]
    ppermute x3, waiting for transfers between devices: 10 us -> 7.74 us  [halo_rows(): after = lax.ppermute(first, 'ha', down)]
    ppermute x3, starting transfers between devices: 9.15 us -> 7.15 us  [halo_rows(): after = lax.ppermute(first, 'ha', down)]
    dot_general x2, matrix products: 4.79 us -> 3.22 us  [project_rows(): jnp.einsum('ftc,cd->ftd', tokens, weight, preferred_element_type=jnp.floa...]
    dot_general x1, matrix products: 3.49 us -> 2.21 us  [per_device(): jnp.einsum('ftc,cd->fdt', all_tokens, w_key, preferred_element_type=jnp.f...]
    ppermute x8 -> x9, starting transfers between devices: 7.77 us -> 8.51 us  [the longest x7 7.21 us: gather_chip_rows(): pieces.append(lax.ppermute(x, 'ha', pairs))]
    ppermute x8 -> x9, waiting for transfers between devices: 31.9 us -> 31.6 us  [the longest x7 29.7 us: gather_chip_rows(): pieces.append(lax.ppermute(x, 'ha', pairs))]
  transfers between devices with their start and end apart: 14 -> 15, of which waited for: 10 -> 11; matrix products, arithmetic and copies ran while one was open for 9% -> 8% of each run, Pallas kernels for 0% -> 0%
where the time goes in v11:
time: 113 us
  waiting for transfers between devices  41.8 us (37%)
  starting transfers between devices  27.4 us (24%)
  matrix products  19.9 us (18%)
  local copies, waits for them, and re-layouts  14.1 us (12%)
  other arithmetic  4.56 us (4%)
  Pallas kernels  4.34 us (4%)
    ppermute x7, waiting for transfers between devices, gather_chip_rows(): pieces.append(lax.ppermute(x, 'ha', pairs))  29.7 us
    dot_general x21, matrix products, conv_taps(): jnp.einsum('fhwc,cd->fhwd', stacked, kernel, preferred_element_type=jnp.f...  13.2 us
    ppermute x3, starting transfers between devices, halo_rows(): before = lax.ppermute(last, 'ha', up)  11.7 us
    ppermute x3, waiting for transfers between devices, halo_rows(): after = lax.ppermute(first, 'ha', down)  7.74 us
    ppermute x7, starting transfers between devices, gather_chip_rows(): pieces.append(lax.ppermute(x, 'ha', pairs))  7.21 us
    ppermute x3, starting transfers between devices, halo_rows(): after = lax.ppermute(first, 'ha', down)  7.15 us
    slice x6, local copies, waits for them, and re-layouts, conv_taps(): kernel = weight[time_off, row_off].reshape(3 * in_channels, out_channels)  5.41 us
    pallas_call x1, Pallas kernels, attend(): pl.pallas_call(functools.partial(attention_kernel, scale), grid=(frames,)...  4.34 us
  transfers between devices with their start and end apart: 15, of which 11 were waited for; matrix products, arithmetic and copies ran while one was open for 8% of the time, Pallas kernels for 0%

profile of v11, /device:TPU:13, one launch (start us, length us, event | category | flops | bytes accessed | tf_op | source)
XLA Modules:
  0.0 112.7 jit_solution(11507208906588903687)
XLA Ops:
  0.0 1.0 constant_dynamic-update-slice_fusion.8
  1.0 0.7 collective-permute-start
  1.8 0.9 collective-permute-done
  2.8 1.3 %collective-permute-start.1 = (bf16[1,2,128,384]{3,2,1,0:T(8,128)(2,1)S(1)}, bf16[1,2,128,384]{3,2,1,0:T(8,128)(2,1)S(1)}, u32[]{:S(2)}, u32[]{:S(2)}) collective-permute-start(bf16[1,2,128,384]{3,2,1,0:T(8,128)(2,1)S(1)} %pad_maximum_fusion.5), channel_id=1, source_target_pairs={{0,2},{1,3},{2,4},{3,5},{4,6},{5,7},{6,8},{7,9},{8,10},{9,11},{10,... | collective-permute-start | bytes 589832 | tf_op jit(solution)/shard_map/ppermute | solution.py:36
  4.0 1.3 %collective-permute-start.2 = (bf16[1,2,128,384]{3,2,1,0:T(8,128)(2,1)S(1)}, bf16[1,2,128,384]{3,2,1,0:T(8,128)(2,1)S(1)}, u32[]{:S(2)}, u32[]{:S(2)}) collective-permute-start(bf16[1,2,128,384]{3,2,1,0:T(8,128)(2,1)S(1)} %pad_maximum_fusion.5), channel_id=1, source_target_pairs={{0,4},{1,5},{2,6},{3,7},{4,8},{5,9},{6,10},{7,11},{8,12},{9,13},{1... | collective-permute-start | bytes 589832 | tf_op jit(solution)/shard_map/ppermute | solution.py:36
  5.3 1.0 collective-permute-start.3
  6.3 1.3 %collective-permute-start.4 = (bf16[1,2,128,384]{3,2,1,0:T(8,128)(2,1)S(1)}, bf16[1,2,128,384]{3,2,1,0:T(8,128)(2,1)S(1)}, u32[]{:S(2)}, u32[]{:S(2)}) collective-permute-start(bf16[1,2,128,384]{3,2,1,0:T(8,128)(2,1)S(1)} %pad_maximum_fusion.5), channel_id=1, source_target_pairs={{0,8},{1,9},{2,10},{3,11},{4,12},{5,13},{6,14},{7,15},{8,0},{9,1},... | collective-permute-start | bytes 589832 | tf_op jit(solution)/shard_map/ppermute | solution.py:36
  7.6 1.0 collective-permute-start.5
  8.9 1.0 fusion.91.q_ref
  9.9 1.3 %collective-permute-start.6 = (bf16[1,2,128,384]{3,2,1,0:T(8,128)(2,1)S(1)}, bf16[1,2,128,384]{3,2,1,0:T(8,128)(2,1)S(1)}, u32[]{:S(2)}, u32[]{:S(2)}) collective-permute-start(bf16[1,2,128,384]{3,2,1,0:T(8,128)(2,1)S(1)} %pad_maximum_fusion.5), channel_id=1, source_target_pairs={{0,12},{1,13},{2,14},{3,15},{4,0},{5,1},{6,2},{7,3},{8,4},{9,5},{1... | collective-permute-start | bytes 589832 | tf_op jit(solution)/shard_map/ppermute | solution.py:36
  11.2 1.9 %collective-permute-done.2 = bf16[1,2,128,384]{3,2,1,0:T(8,128)(2,1)S(1)} collective-permute-done((bf16[1,2,128,384]{3,2,1,0:T(8,128)(2,1)S(1)}, bf16[1,2,128,384]{3,2,1,0:T(8,128)(2,1)S(1)}, u32[]{:S(2)}, u32[]{:S(2)}) %collective-permute-start.2) | collective-permute-done | bytes 196640 | tf_op jit(solution)/shard_map/ppermute | solution.py:36
  13.1 20.1 %collective-permute-done.3 = bf16[1,2,128,384]{3,2,1,0:T(8,128)(2,1)S(1)} collective-permute-done((bf16[1,2,128,384]{3,2,1,0:T(8,128)(2,1)S(1)}, bf16[1,2,128,384]{3,2,1,0:T(8,128)(2,1)S(1)}, u32[]{:S(2)}, u32[]{:S(2)}) %collective-permute-start.3) | collective-permute-done | bytes 196640 | tf_op jit(solution)/shard_map/ppermute | solution.py:36
  33.3 4.2 %collective-permute-done.4 = bf16[1,2,128,384]{3,2,1,0:T(8,128)(2,1)S(1)} collective-permute-done((bf16[1,2,128,384]{3,2,1,0:T(8,128)(2,1)S(1)}, bf16[1,2,128,384]{3,2,1,0:T(8,128)(2,1)S(1)}, u32[]{:S(2)}, u32[]{:S(2)}) %collective-permute-start.4) | collective-permute-done | bytes 196640 | tf_op jit(solution)/shard_map/ppermute | solution.py:36
  37.6 2.5 %collective-permute-done.6 = bf16[1,2,128,384]{3,2,1,0:T(8,128)(2,1)S(1)} collective-permute-done((bf16[1,2,128,384]{3,2,1,0:T(8,128)(2,1)S(1)}, bf16[1,2,128,384]{3,2,1,0:T(8,128)(2,1)S(1)}, u32[]{:S(2)}, u32[]{:S(2)}) %collective-permute-start.6) | collective-permute-done | bytes 196640 | tf_op jit(solution)/shard_map/ppermute | solution.py:36
  40.1 1.1 collective-permute-done.7
  42.0 2.2 %fusion.2.k_ref = bf16[1,384,2048]{2,1,0:T(8,128)(2,1)} fusion(bf16[2048,384]{1,0:T(8,128)(2,1)S(1)} %fusion.1, bf16[384,384]{1,0:T(8,128)(2,1)S(1)} %copy-done), kind=kOutput, calls=%fused_computation.10 | convolution fusion | flops 604766208 | bytes 3440640 | tf_op jit(solution)/shard_map/ftc,cd->fdt/dot_general | solution.py:150
  44.2 2.3 %fusion.3.v_ref = bf16[1,2048,384]{2,1,0:T(8,128)(2,1)} fusion(bf16[2048,384]{1,0:T(8,128)(2,1)S(1)} %fusion.1, bf16[384,384]{1,0:T(8,128)(2,1)S(1)} %copy-done.9), kind=kOutput, calls=%fused_computation.11 | convolution fusion | flops 604766208 | bytes 3440640 | tf_op jit(solution)/shard_map/ftc,cd->ftd/dot_general | solution.py:120
  46.4 4.3 %shard_map.100 = bf16[1,256,384]{2,1,0:T(8,128)(2,1)} custom-call(bf16[1,256,384]{2,1,0:T(8,128)(2,1)} %fusion.91.q_ref, bf16[1,384,2048]{2,1,0:T(8,128)(2,1)} %fusion.2.k_ref, bf16[1,2048,384]{2,1,0:T(8,128)(2,1)} %fusion.3.v_ref), custom_call_target="tpu_custom_call" | custom-call | flops 805306368 | bytes 3538944 | tf_op jit(solution)/shard_map/pallas_call | solution.py:102
  50.8 1.2 %fusion.146 = bf16[1,2,128,384]{3,2,1,0:T(8,128)(2,1)S(1)} fusion(bf16[1,128,384]{2,1,0:T(8,128)(2,1)S(1)} %bitcast.161, bf16[1,128,384]{2,1,0:T(8,128)(2,1)S(1)} %bitcast.162, bf16[2,128,384]{2,1,0:T(8,128)(2,1)} %bitcast.173, bf16[384,384]{1,0:T(8,128)(2,1)S(1)} %copy-done.7), kind=kOutput, calls=%fused_computation.203 | convolution fusion | flops 75890688 | bytes 884736 | tf_op jit(solution)/shard_map/ftc,cd->ftd/dot_general | solution.py:156
  52.1 0.6 collective-permute-start.8
  52.6 0.9 collective-permute-done.8
  54.0 2.3 %collective-permute-start.10 = (bf16[4,1,128,384]{3,2,1,0:T(8,128)(2,1)S(1)}, bf16[4,1,128,384]{3,2,1,0:T(8,128)(2,1)S(1)}, u32[]{:S(2)}, u32[]{:S(2)}) collective-permute-start(bf16[4,1,128,384]{3,2,1,0:T(8,128)(2,1)S(1)} %pad_maximum_fusion.4), channel_id=1, source_target_pairs={{1,0},{2,1},{3,2},{4,3},{5,4},{6,5},{7,6},{8,7},{9,8},{10,9},{11,1... | collective-permute-start | bytes 1179656 | tf_op jit(solution)/shard_map/ppermute | solution.py:19
  56.2 4.4 %collective-permute-start.9 = (bf16[4,1,128,384]{3,2,1,0:T(8,128)(2,1)S(1)}, bf16[4,1,128,384]{3,2,1,0:T(8,128)(2,1)S(1)}, u32[]{:S(2)}, u32[]{:S(2)}) collective-permute-start(bf16[4,1,128,384]{3,2,1,0:T(8,128)(2,1)S(1)} %pad_maximum_fusion.4), channel_id=1, source_target_pairs={{0,1},{1,2},{2,3},{3,4},{4,5},{5,6},{6,7},{7,8},{8,9},{9,10},{10,1... | collective-permute-start | bytes 1179656 | tf_op jit(solution)/shard_map/ppermute | solution.py:18
  60.6 3.9 %fusion.170 = (bf16[1,1,3,384,384]{4,3,2,1,0:T(8,128)(2,1)S(1)}, bf16[1,1,3,384,384]{4,3,2,1,0:T(8,128)(2,1)S(1)}, bf16[1,1,3,384,384]{4,3,2,1,0:T(8,128)(2,1)S(...) fusion(bf16[3,3,3,384,384]{4,3,2,1,0:T(8,128)(2,1)} %param.17), kind=kLoop, calls=%fused_computation.246 | loop fusion | bytes 15925248 | tf_op jit(solution)/shard_map/slice | solution.py:79
  64.6 0.5 collective-permute-done.9
  65.5 0.7 fusion.174
  70.7 5.3 %collective-permute-start.11 = (bf16[2,1,128,384]{3,2,0,1:T(8,128)(2,1)S(1)}, bf16[2,1,128,384]{3,2,0,1:T(8,128)(2,1)S(1)}, u32[]{:S(2)}, u32[]{:S(2)}) collective-permute-start(bf16[2,1,128,384]{3,2,0,1:T(8,128)(2,1)S(1)} %fusion.147), channel_id=1, source_target_pairs={{0,1},{1,2},{2,3},{3,4},{4,5},{5,6},{6,7},{7,8},{8,9},{9,10},{10,1... | collective-permute-start | bytes 589832 | tf_op jit(solution)/shard_map/ppermute | solution.py:18
  76.0 2.3 %collective-permute-start.12 = (bf16[2,1,128,384]{3,2,0,1:T(8,128)(2,1)S(1)}, bf16[2,1,128,384]{3,2,0,1:T(8,128)(2,1)S(1)}, u32[]{:S(2)}, u32[]{:S(2)}) collective-permute-start(bf16[2,1,128,384]{3,2,0,1:T(8,128)(2,1)S(1)} %fusion.147), channel_id=1, source_target_pairs={{1,0},{2,1},{3,2},{4,3},{5,4},{6,5},{7,6},{8,7},{9,8},{10,9},{11,1... | collective-permute-start | bytes 589832 | tf_op jit(solution)/shard_map/ppermute | solution.py:19
  78.8 1.2 %reshape.459 = bf16[1152,192,1,1]{0,1,2,3:T(8,128)(2,1)} reshape(bf16[1,1,3,384,192]{3,2,4,1,0:T(4,128)(2,1)S(1)} %copy.28) | data formatting | bytes 884736 | tf_op jit(solution)/shard_map/reshape;squeeze | solution.py:79
  81.5 2.4 %collective-permute-done.12 = bf16[2,1,128,384]{3,2,0,1:T(8,128)(2,1)S(1)} collective-permute-done((bf16[2,1,128,384]{3,2,0,1:T(8,128)(2,1)S(1)}, bf16[2,1,128,384]{3,2,0,1:T(8,128)(2,1)S(1)}, u32[]{:S(2)}, u32[]{:S(2)}) %collective-permute-start.12) | collective-permute-done | bytes 196640 | tf_op jit(solution)/shard_map/ppermute | solution.py:19
  84.0 0.6 broadcast_in_dim.4
  85.2 0.8 pad_slice_fusion.9
  86.4 0.7 copy-done.6
  87.1 1.1 %fusion.9 = f32[2,2,256,192]{2,3,1,0:T(8,128)S(1)} fusion(bf16[2,1,258,384]{3,2,1,0:T(8,128)(2,1)S(1)} %pad_slice_fusion.10, bf16[2,2,256,384]{3,2,1,0:T(8,128)(2,1)S(1)} %get-tuple-element.81, bf16[2,2,256,384]{3,2,1,0:T(8,128)(2,1)S(1)} %get-tuple-element.80, bf16[1152,192,1,1]{0,1,2,3:T(8,128)(2,1)S(1)} %copy-done.6), kind=kOutput, calls=%fused_computation.20 | convolution fusion | flops 462422016 | bytes 3197952 | tf_op jit(solution)/shard_map/fhwc,cd->fhwd/dot_general | solution.py:80
  88.2 1.1 %fusion.31 = f32[2,2,256,192]{2,3,1,0:T(8,128)S(1)} fusion(f32[2,2,256,192]{2,3,1,0:T(8,128)S(1)} %fusion.9, bf16[2,2,256,384]{3,2,1,0:T(8,128)(2,1)S(1)} %get-tuple-element.71, bf16[2,2,256,384]{3,2,1,0:T(8,128)(2,1)S(1)} %get-tuple-element.74, bf16[2,2,256,384]{3,2,1,0:T(8,128)(2,1)S(1)} %get-tuple-element.75, bf16[1152,192,1,1]{0,1,2,3:T(8,128)(2,1)S(1)} %reshape.458), kind=kOutput, calls=%fused_computation.47 | convolution fusion | flops 460259328 | bytes 4374528 | tf_op jit(solution)/shard_map/fhwc,cd->fhwd/dot_general | solution.py:80
  89.4 1.2 %multiply_reduce_fusion.1 = (f32[2,2,256]{2,1,0:T(2,128)S(1)}, f32[2,2,256,192]{2,3,1,0:T(8,128)S(1)}) fusion(f32[2,2,256,192]{2,3,1,0:T(8,128)S(1)} %fusion.31, bf16[1152,192,1,1]{0,1,2,3:T(8,128)(2,1)S(1)} %reshape.460, bf16[2,2,256,384]{3,2,1,0:T(8,128)(2,1)S(1)} %get-tuple-element.72, bf16[2,2,256,384]{3,2,1,0:T(8,128)(2,1)S(1)} %get-tuple-element.73, ...), kind=kOutput, calls=%fused_computation.126 | convolution fusion | flops 461044736 | bytes 4378624 | tf_op jit(solution)/shard_map/fhwc,cd->fhwd/dot_general | solution.py:80
  90.9 2.1 %collective-permute-start.13 = (bf16[4,1,256,192]{2,3,1,0:T(8,128)(2,1)S(1)}, bf16[4,1,256,192]{2,3,1,0:T(8,128)(2,1)S(1)}, u32[]{:S(2)}, u32[]{:S(2)}) collective-permute-start(bf16[4,1,256,192]{2,3,1,0:T(8,128)(2,1)S(1)} %get-tuple-element.78), channel_id=1, source_target_pairs={{0,1},{1,2},{2,3},{3,4},{4,5},{5,6},{6,7},{7,8},{8,9},{9,10},{10,1... | collective-permute-start | bytes 1179656 | tf_op jit(solution)/shard_map/ppermute | solution.py:18
  93.0 2.6 %collective-permute-start.14 = (bf16[4,1,256,192]{2,3,1,0:T(8,128)(2,1)S(1)}, bf16[4,1,256,192]{2,3,1,0:T(8,128)(2,1)S(1)}, u32[]{:S(2)}, u32[]{:S(2)}) collective-permute-start(bf16[4,1,256,192]{2,3,1,0:T(8,128)(2,1)S(1)} %get-tuple-element.79), channel_id=1, source_target_pairs={{1,0},{2,1},{3,2},{4,3},{5,4},{6,5},{7,6},{8,7},{9,8},{10,9},{11,1... | collective-permute-start | bytes 1179656 | tf_op jit(solution)/shard_map/ppermute | solution.py:19
  95.8 1.9 %collective-permute-done.13 = bf16[4,1,256,192]{2,3,1,0:T(8,128)(2,1)S(1)} collective-permute-done((bf16[4,1,256,192]{2,3,1,0:T(8,128)(2,1)S(1)}, bf16[4,1,256,192]{2,3,1,0:T(8,128)(2,1)S(1)}, u32[]{:S(2)}, u32[]{:S(2)}) %collective-permute-start.13) | collective-permute-done | bytes 393248 | tf_op jit(solution)/shard_map/ppermute | solution.py:18
  97.7 5.4 %collective-permute-done.14 = bf16[4,1,256,192]{2,3,1,0:T(8,128)(2,1)S(1)} collective-permute-done((bf16[4,1,256,192]{2,3,1,0:T(8,128)(2,1)S(1)}, bf16[4,1,256,192]{2,3,1,0:T(8,128)(2,1)S(1)}, u32[]{:S(2)}, u32[]{:S(2)}) %collective-permute-start.14) | collective-permute-done | bytes 393248 | tf_op jit(solution)/shard_map/ppermute | solution.py:19
  103.1 2.0 %select_maximum_fusion = bf16[4,4,258,192]{2,3,1,0:T(8,128)(2,1)S(1)} fusion(bf16[4,1,256,192]{2,3,1,0:T(8,128)(2,1)S(1)} %collective-permute-done.14, bf16[4,1,256,192]{2,3,1,0:T(8,128)(2,1)S(1)} %collective-permute-done.13, bf16[2,2,256,192]{2,3,1,0:T(8,128)(2,1)S(1)} %multiply_convert_fusion, bf16[2,2,256,192]{2,3,1,0:T(8,128)(2,1)S(1)} %copy-done.2), kind=kLoop, calls=%fused_computation.13 | loop fusion | flops 11888640 | bytes 3158016 | tf_op jit(solution)/shard_map/concatenate | solution.py:25
  105.0 1.7 %fusion.172 = (bf16[2,2,256,192]{2,3,1,0:T(8,128)(2,1)S(1)}, bf16[2,2,256,192]{2,3,1,0:T(8,128)(2,1)S(1)}, bf16[2,2,256,192]{2,3,1,0:T(8,128)(2,1)S(1)}, bf16[2,...) fusion(bf16[4,4,258,192]{2,3,1,0:T(8,128)(2,1)S(1)} %select_max, ...), kind=kLoop, calls=%fused_computation.248 | loop fusion | bytes 14155776 | tf_op jit(solution)/shard_map/slice | solution.py:77
  107.1 0.5 fusion.53
  109.2 0.5 convolution_add_fusion.4
  109.8 0.5 convolution_add_fusion.3
  110.3 0.5 convolution_add_fusion.2
  110.8 0.5 convolution_add_fusion.1
  111.4 1.3 %fusion.43 = bf16[2,2,256,192]{2,3,1,0:T(8,128)(2,1)} fusion(f32[2,2,256,192]{2,3,1,0:T(8,128)S(1)} %get-tuple-element.93, f32[2,2,256,192]{2,3,1,0:T(8,128)S(1)} %convolution_add_fusion.1, bf16[576,192,1,1]{1,0,3,2:T(8,128)(2,1)S(1)} %bitcast.175, bf16[2,2,256,192]{2,3,1,0:T(8,128)(2,1)S(1)} %get-tuple-element.42, ...), kind=kOutput, calls=%fused_computation.55 | convolution fusion | flops 230621184 | bytes 3366912 | tf_op jit(solution)/shard_map/fhwc,cd->fhwd/dot_general | solution.py:80
  (77 shorter events, 12.0 us)
Async XLA Ops:
  0.0 41.9 %copy-start = (bf16[384,384]{1,0:T(8,128)(2,1)S(1)}, bf16[384,384]{1,0:T(8,128)(2,1)}, u32[]{:S(2)}) copy-start(bf16[384,384]{1,0:T(8,128)(2,1)} %param.14) | copy-start | bytes 884740
  0.0 8.9 %copy-start.8 = (bf16[384,384]{1,0:T(8,128)(2,1)S(1)}, bf16[384,384]{1,0:T(8,128)(2,1)}, u32[]{:S(2)}) copy-start(bf16[384,384]{1,0:T(8,128)(2,1)} %param.13) | copy-start | bytes 884740
  1.0 1.7 %collective-permute-start = (bf16[1,1,128,384]{3,2,1,0:T(8,128)(2,1)S(1)}, bf16[1,1,128,384]{3,2,1,0:T(8,128)(2,1)S(1)}, u32[]{:S(2)}, u32[]{:S(2)}) collective-permute-start(bf16[1,1,128,384]{3,2,1,0:T(8,128)(2,1)S(1)} %get-tuple-element.91), channel_id=1, source_target_pairs={{0,1},{1,0},{2,3},{3,2},{4,5},{5,4},{6,7},{7,6},{8,9},{9,8},{10,11... | collective-permute-start | bytes 294920 | tf_op jit(solution)/shard_map/ppermute | solution.py:143
  2.8 7.1 %collective-permute-start.1 = (bf16[1,2,128,384]{3,2,1,0:T(8,128)(2,1)S(1)}, bf16[1,2,128,384]{3,2,1,0:T(8,128)(2,1)S(1)}, u32[]{:S(2)}, u32[]{:S(2)}) collective-permute-start(bf16[1,2,128,384]{3,2,1,0:T(8,128)(2,1)S(1)} %pad_maximum_fusion.5), channel_id=1, source_target_pairs={{0,2},{1,3},{2,4},{3,5},{4,6},{5,7},{6,8},{7,9},{8,10},{9,11},{10,... | collective-permute-start | bytes 589832 | tf_op jit(solution)/shard_map/ppermute | solution.py:36
  4.0 9.0 %collective-permute-start.2 = (bf16[1,2,128,384]{3,2,1,0:T(8,128)(2,1)S(1)}, bf16[1,2,128,384]{3,2,1,0:T(8,128)(2,1)S(1)}, u32[]{:S(2)}, u32[]{:S(2)}) collective-permute-start(bf16[1,2,128,384]{3,2,1,0:T(8,128)(2,1)S(1)} %pad_maximum_fusion.5), channel_id=1, source_target_pairs={{0,4},{1,5},{2,6},{3,7},{4,8},{5,9},{6,10},{7,11},{8,12},{9,13},{1... | collective-permute-start | bytes 589832 | tf_op jit(solution)/shard_map/ppermute | solution.py:36
  5.3 27.9 %collective-permute-start.3 = (bf16[1,2,128,384]{3,2,1,0:T(8,128)(2,1)S(1)}, bf16[1,2,128,384]{3,2,1,0:T(8,128)(2,1)S(1)}, u32[]{:S(2)}, u32[]{:S(2)}) collective-permute-start(bf16[1,2,128,384]{3,2,1,0:T(8,128)(2,1)S(1)} %pad_maximum_fusion.5), channel_id=1, source_target_pairs={{0,6},{1,7},{2,8},{3,9},{4,10},{5,11},{6,12},{7,13},{8,14},{9,15},... | collective-permute-start | bytes 589832 | tf_op jit(solution)/shard_map/ppermute | solution.py:36
  6.3 31.2 %collective-permute-start.4 = (bf16[1,2,128,384]{3,2,1,0:T(8,128)(2,1)S(1)}, bf16[1,2,128,384]{3,2,1,0:T(8,128)(2,1)S(1)}, u32[]{:S(2)}, u32[]{:S(2)}) collective-permute-start(bf16[1,2,128,384]{3,2,1,0:T(8,128)(2,1)S(1)} %pad_maximum_fusion.5), channel_id=1, source_target_pairs={{0,8},{1,9},{2,10},{3,11},{4,12},{5,13},{6,14},{7,15},{8,0},{9,1},... | collective-permute-start | bytes 589832 | tf_op jit(solution)/shard_map/ppermute | solution.py:36
  7.6 29.9 %collective-permute-start.5 = (bf16[1,2,128,384]{3,2,1,0:T(8,128)(2,1)S(1)}, bf16[1,2,128,384]{3,2,1,0:T(8,128)(2,1)S(1)}, u32[]{:S(2)}, u32[]{:S(2)}) collective-permute-start(bf16[1,2,128,384]{3,2,1,0:T(8,128)(2,1)S(1)} %pad_maximum_fusion.5), channel_id=1, source_target_pairs={{0,10},{1,11},{2,12},{3,13},{4,14},{5,15},{6,0},{7,1},{8,2},{9,3},... | collective-permute-start | bytes 589832 | tf_op jit(solution)/shard_map/ppermute | solution.py:36
  9.9 30.2 %collective-permute-start.6 = (bf16[1,2,128,384]{3,2,1,0:T(8,128)(2,1)S(1)}, bf16[1,2,128,384]{3,2,1,0:T(8,128)(2,1)S(1)}, u32[]{:S(2)}, u32[]{:S(2)}) collective-permute-start(bf16[1,2,128,384]{3,2,1,0:T(8,128)(2,1)S(1)} %pad_maximum_fusion.5), channel_id=1, source_target_pairs={{0,12},{1,13},{2,14},{3,15},{4,0},{5,1},{6,2},{7,3},{8,4},{9,5},{1... | collective-permute-start | bytes 589832 | tf_op jit(solution)/shard_map/ppermute | solution.py:36
  13.1 28.1 %collective-permute-start.7 = (bf16[1,2,128,384]{3,2,1,0:T(8,128)(2,1)S(1)}, bf16[1,2,128,384]{3,2,1,0:T(8,128)(2,1)S(1)}, u32[]{:S(2)}, u32[]{:S(2)}) collective-permute-start(bf16[1,2,128,384]{3,2,1,0:T(8,128)(2,1)S(1)} %pad_maximum_fusion.5), channel_id=1, source_target_pairs={{0,14},{1,15},{2,0},{3,1},{4,2},{5,3},{6,4},{7,5},{8,6},{9,7},{10,... | collective-permute-start | bytes 589832 | tf_op jit(solution)/shard_map/ppermute | solution.py:36
  41.9 2.2 %copy-start.9 = (bf16[384,384]{1,0:T(8,128)(2,1)S(1)}, bf16[384,384]{1,0:T(8,128)(2,1)}, u32[]{:S(2)}) copy-start(bf16[384,384]{1,0:T(8,128)(2,1)} %param.15) | copy-start | bytes 884740
  46.4 4.3 %copy-start.7 = (bf16[384,384]{1,0:T(8,128)(2,1)S(1)}, bf16[384,384]{1,0:T(8,128)(2,1)}, u32[]{:S(2)}) copy-start(bf16[384,384]{1,0:T(8,128)(2,1)} %param.16) | copy-start | bytes 884740
  50.8 3.1 %copy-start.4 = (bf16[2,1,128,384]{3,2,1,0:T(8,128)(2,1)S(1)}, bf16[2,1,128,384]{3,2,1,0:T(8,128)(2,1)}, u32[]{:S(2)}) copy-start(bf16[2,1,128,384]{3,2,1,0:T(8,128)(2,1)} %param.11) | copy-start | bytes 589828
  52.1 1.5 %collective-permute-start.8 = (bf16[1,1,128,384]{3,2,1,0:T(8,128)(2,1)S(1)}, bf16[1,1,128,384]{3,2,1,0:T(8,128)(2,1)S(1)}, u32[]{:S(2)}, u32[]{:S(2)}) collective-permute-start(bf16[1,1,128,384]{3,2,1,0:T(8,128)(2,1)S(1)} %get-tuple-element.90), channel_id=1, source_target_pairs={{0,1},{1,0},{2,3},{3,2},{4,5},{5,4},{6,7},{7,6},{8,9},{9,8},{10,11... | collective-permute-start | bytes 294920 | tf_op jit(solution)/shard_map/ppermute | solution.py:160
  54.0 10.6 %collective-permute-start.10 = (bf16[4,1,128,384]{3,2,1,0:T(8,128)(2,1)S(1)}, bf16[4,1,128,384]{3,2,1,0:T(8,128)(2,1)S(1)}, u32[]{:S(2)}, u32[]{:S(2)}) collective-permute-start(bf16[4,1,128,384]{3,2,1,0:T(8,128)(2,1)S(1)} %pad_maximum_fusion.4), channel_id=1, source_target_pairs={{1,0},{2,1},{3,2},{4,3},{5,4},{6,5},{7,6},{8,7},{9,8},{10,9},{11,1... | collective-permute-start | bytes 1179656 | tf_op jit(solution)/shard_map/ppermute | solution.py:19
  56.2 8.9 %collective-permute-start.9 = (bf16[4,1,128,384]{3,2,1,0:T(8,128)(2,1)S(1)}, bf16[4,1,128,384]{3,2,1,0:T(8,128)(2,1)S(1)}, u32[]{:S(2)}, u32[]{:S(2)}) collective-permute-start(bf16[4,1,128,384]{3,2,1,0:T(8,128)(2,1)S(1)} %pad_maximum_fusion.4), channel_id=1, source_target_pairs={{0,1},{1,2},{2,3},{3,4},{4,5},{5,6},{6,7},{7,8},{8,9},{9,10},{10,1... | collective-permute-start | bytes 1179656 | tf_op jit(solution)/shard_map/ppermute | solution.py:18
  70.2 8.1 %copy-start.5 = (bf16[3,3,384,192]{2,3,1,0:T(8,128)(2,1)S(1)}, bf16[3,3,384,192]{2,3,1,0:T(8,128)(2,1)}, u32[]{:S(2)}) copy-start(bf16[3,3,384,192]{2,3,1,0:T(8,128)(2,1)} %param.18) | copy-start | bytes 3981316
  70.7 10.8 %collective-permute-start.11 = (bf16[2,1,128,384]{3,2,0,1:T(8,128)(2,1)S(1)}, bf16[2,1,128,384]{3,2,0,1:T(8,128)(2,1)S(1)}, u32[]{:S(2)}, u32[]{:S(2)}) collective-permute-start(bf16[2,1,128,384]{3,2,0,1:T(8,128)(2,1)S(1)} %fusion.147), channel_id=1, source_target_pairs={{0,1},{1,2},{2,3},{3,4},{4,5},{5,6},{6,7},{7,8},{8,9},{9,10},{10,1... | collective-permute-start | bytes 589832 | tf_op jit(solution)/shard_map/ppermute | solution.py:18
  76.0 7.9 %collective-permute-start.12 = (bf16[2,1,128,384]{3,2,0,1:T(8,128)(2,1)S(1)}, bf16[2,1,128,384]{3,2,0,1:T(8,128)(2,1)S(1)}, u32[]{:S(2)}, u32[]{:S(2)}) collective-permute-start(bf16[2,1,128,384]{3,2,0,1:T(8,128)(2,1)S(1)} %fusion.147), channel_id=1, source_target_pairs={{1,0},{2,1},{3,2},{4,3},{5,4},{6,5},{7,6},{8,7},{9,8},{10,9},{11,1... | collective-permute-start | bytes 589832 | tf_op jit(solution)/shard_map/ppermute | solution.py:19
  86.0 1.0 copy-start.6
  89.4 1.4 %copy-start.2 = (bf16[2,2,256,192]{2,3,1,0:T(8,128)(2,1)S(1)}, bf16[2,2,256,192]{2,3,1,0:T(8,128)(2,1)}, u32[]{:S(2)}) copy-start(bf16[2,2,256,192]{2,3,1,0:T(8,128)(2,1)} %param.12) | copy-start | bytes 1179652
  90.5 5.0 %copy-start.3 = (bf16[3,3,3,192,192]{4,3,2,1,0:T(8,128)(2,1)S(1)}, bf16[3,3,3,192,192]{4,3,2,1,0:T(8,128)(2,1)}, u32[]{:S(2)}) copy-start(bf16[3,3,3,192,192]{4,3,2,1,0:T(8,128)(2,1)} %param.19) | copy-start | bytes 5971972
  90.9 6.8 %collective-permute-start.13 = (bf16[4,1,256,192]{2,3,1,0:T(8,128)(2,1)S(1)}, bf16[4,1,256,192]{2,3,1,0:T(8,128)(2,1)S(1)}, u32[]{:S(2)}, u32[]{:S(2)}) collective-permute-start(bf16[4,1,256,192]{2,3,1,0:T(8,128)(2,1)S(1)} %get-tuple-element.78), channel_id=1, source_target_pairs={{0,1},{1,2},{2,3},{3,4},{4,5},{5,6},{6,7},{7,8},{8,9},{9,10},{10,1... | collective-permute-start | bytes 1179656 | tf_op jit(solution)/shard_map/ppermute | solution.py:18
  93.0 10.1 %collective-permute-start.14 = (bf16[4,1,256,192]{2,3,1,0:T(8,128)(2,1)S(1)}, bf16[4,1,256,192]{2,3,1,0:T(8,128)(2,1)S(1)}, u32[]{:S(2)}, u32[]{:S(2)}) collective-permute-start(bf16[4,1,256,192]{2,3,1,0:T(8,128)(2,1)S(1)} %get-tuple-element.79), channel_id=1, source_target_pairs={{1,0},{2,1},{3,2},{4,3},{5,4},{6,5},{7,6},{8,7},{9,8},{10,9},{11,1... | collective-permute-start | bytes 1179656 | tf_op jit(solution)/shard_map/ppermute | solution.py:19
  111.3 1.3 %copy-start.1 = (bf16[384,384]{1,0:T(8,128)(2,1)S(1)}, bf16[384,384]{1,0:T(8,128)(2,1)}, u32[]{:S(2)}) copy-start(bf16[384,384]{1,0:T(8,128)(2,1)} %param.14) | copy-start | bytes 884740

commit v12 on v11

--- a/solution.py
+++ b/solution.py
@@ -28,12 +28,27 @@
 def gather_chip_rows(x):
     count = lax.axis_size("ha")
     chips = count // 2
+    ring = list(range(0, chips, 2)) + list(range(chips - 1 - chips % 2, 0, -2))
+    if chips % 2:
+        ring = list(range(chips))
+    place = {c: i for i, c in enumerate(ring)}
+
+    def toward(step):
+        return [
+            (2 * c + k, 2 * ring[(place[c] + step) % chips] + k)
+            for c in range(chips)
+            for k in range(2)
+        ]
+
+    forward, backward = toward(1), toward(-1)
     pieces = [x]
-    for shift in range(1, chips):
-        pairs = [
-            (2 * c + k, 2 * ((c + shift) % chips) + k) for c in range(chips) for k in range(2)
-        ]
-        pieces.append(lax.ppermute(x, "ha", pairs))
+    ahead = behind = x
+    for step in range(1, chips // 2 + 1):
+        ahead = lax.ppermute(ahead, "ha", forward)
+        pieces.append(ahead)
+        if step < chips - step:
+            behind = lax.ppermute(behind, "ha", backward)
+            pieces.append(behind)
     return jnp.concatenate(pieces, axis=1)
 
 

time: 113 us -> 99.5 us (0.88)
  waiting for transfers between devices: 41.8 us -> 26.6 us
  starting transfers between devices: 27.4 us -> 28.6 us
    ppermute x7, waiting for transfers between devices: 29.7 us -> 14.5 us  [the longest x4 14.5 us: gather_chip_rows(): ahead = lax.ppermute(ahead, 'ha', forward)]
    ppermute x1, starting transfers between devices: 0.56 us -> 4.4 us  [per_device(): back = lax.ppermute(mixed_block[:, 1:2], 'ha', swap)]
    ppermute x7, starting transfers between devices: 7.21 us -> 4.62 us  [the longest x3 3.89 us: gather_chip_rows(): behind = lax.ppermute(behind, 'ha', backward)]
  transfers between devices with their start and end apart: 15 -> 15, of which waited for: 11 -> 10; matrix products, arithmetic and copies ran while one was open for 8% -> 9% of each run, Pallas kernels for 0% -> 0%
where the time goes in v12:
time: 99.5 us; the launch traced here: 98.8 us
  starting transfers between devices  28.6 us (29%)
  waiting for transfers between devices  26.6 us (27%)
  matrix products  19.9 us (20%)
  local copies, waits for them, and re-layouts  14.1 us (14%)
  other arithmetic  4.56 us (5%)
  Pallas kernels  4.35 us (4%)
    ppermute x4, waiting for transfers between devices, gather_chip_rows(): ahead = lax.ppermute(ahead, 'ha', forward)  14.5 us
    dot_general x21, matrix products, conv_taps(): jnp.einsum('fhwc,cd->fhwd', stacked, kernel, preferred_element_type=jnp.f...  13.2 us
    ppermute x3, starting transfers between devices, halo_rows(): before = lax.ppermute(last, 'ha', up)  11.8 us
    ppermute x3, waiting for transfers between devices, halo_rows(): after = lax.ppermute(first, 'ha', down)  7.83 us
    ppermute x3, starting transfers between devices, halo_rows(): after = lax.ppermute(first, 'ha', down)  7.04 us
    slice x6, local copies, waits for them, and re-layouts, conv_taps(): kernel = weight[time_off, row_off].reshape(3 * in_channels, out_channels)  5.41 us
    ppermute x1, starting transfers between devices, per_device(): back = lax.ppermute(mixed_block[:, 1:2], 'ha', swap)  4.4 us
    pallas_call x1, Pallas kernels, attend(): pl.pallas_call(functools.partial(attention_kernel, scale), grid=(frames,)...  4.35 us
  transfers between devices with their start and end apart: 15, of which 10 were waited for; matrix products, arithmetic and copies ran while one was open for 9% of the time, Pallas kernels for 0%

profile of v12, /device:TPU:13, one launch (start us, length us, event | category | flops | bytes accessed | tf_op | source)
XLA Modules:
  0.0 98.8 jit_solution(17867286392539770627)
XLA Ops:
  0.0 1.0 %constant_dynamic-update-slice_fusion.8 = (bf16[1,16,128,384]{3,2,1,0:T(8,128)(2,1)S(1)}, bf16[1,1,128,384]{3,2,1,0:T(8,128)(2,1)S(1)}, bf16[1,1,128,384]{3,2,1,0:T(8,128)(2,1)S(1)}) fusion(bf16[2,1,128,384]{3,2,1,0:T(8,128)(2,1)} %param.10, s32[]{:T(128)S(6)} %select_n.39, s32[]{:T(128)S(6)} %select_n.40), kind=kLoop, calls=%fused_computation.217 | loop fusion | bytes 491528
  1.0 0.7 collective-permute-start
  1.8 0.9 collective-permute-done
  3.0 1.3 %collective-permute-start.2 = (bf16[1,2,128,384]{3,2,1,0:T(8,128)(2,1)S(1)}, bf16[1,2,128,384]{3,2,1,0:T(8,128)(2,1)S(1)}, u32[]{:S(2)}, u32[]{:S(2)}) collective-permute-start(bf16[1,2,128,384]{3,2,1,0:T(8,128)(2,1)S(1)} %pad_maximum_fusion.5), channel_id=1, source_target_pairs={{0,2},{1,3},{2,6},{3,7},{4,0},{5,1},{6,10},{7,11},{8,4},{9,5},{10,... | collective-permute-start | bytes 589832 | tf_op jit(solution)/shard_map/ppermute | solution.py:50
  4.5 1.0 fusion.91.q_ref
  5.5 3.4 %collective-permute-done.1 = bf16[1,2,128,384]{3,2,1,0:T(8,128)(2,1)S(1)} collective-permute-done((bf16[1,2,128,384]{3,2,1,0:T(8,128)(2,1)S(1)}, bf16[1,2,128,384]{3,2,1,0:T(8,128)(2,1)S(1)}, u32[]{:S(2)}, u32[]{:S(2)}) %collective-permute-start.1) | collective-permute-done | bytes 196640 | tf_op jit(solution)/shard_map/ppermute | solution.py:47
  9.1 1.3 %collective-permute-start.4 = (bf16[1,2,128,384]{3,2,1,0:T(8,128)(2,1)S(1)}, bf16[1,2,128,384]{3,2,1,0:T(8,128)(2,1)S(1)}, u32[]{:S(2)}, u32[]{:S(2)}) collective-permute-start(bf16[1,2,128,384]{3,2,1,0:T(8,128)(2,1)S(1)} %collective-permute-done.2), channel_id=1, source_target_pairs={{0,2},{1,3},{2,6},{3,7},{4,0},{5,1},{6,10},{7,11},{8,4},{9,5},{10,... | collective-permute-start | bytes 589832 | tf_op jit(solution)/shard_map/ppermute | solution.py:50
  10.5 3.7 %collective-permute-done.3 = bf16[1,2,128,384]{3,2,1,0:T(8,128)(2,1)S(1)} collective-permute-done((bf16[1,2,128,384]{3,2,1,0:T(8,128)(2,1)S(1)}, bf16[1,2,128,384]{3,2,1,0:T(8,128)(2,1)S(1)}, u32[]{:S(2)}, u32[]{:S(2)}) %collective-permute-start.3) | collective-permute-done | bytes 196640 | tf_op jit(solution)/shard_map/ppermute | solution.py:47
  14.3 1.3 %collective-permute-start.6 = (bf16[1,2,128,384]{3,2,1,0:T(8,128)(2,1)S(1)}, bf16[1,2,128,384]{3,2,1,0:T(8,128)(2,1)S(1)}, u32[]{:S(2)}, u32[]{:S(2)}) collective-permute-start(bf16[1,2,128,384]{3,2,1,0:T(8,128)(2,1)S(1)} %collective-permute-done.4), channel_id=1, source_target_pairs={{0,2},{1,3},{2,6},{3,7},{4,0},{5,1},{6,10},{7,11},{8,4},{9,5},{10,... | collective-permute-start | bytes 589832 | tf_op jit(solution)/shard_map/ppermute | solution.py:50
  15.7 3.0 %collective-permute-done.5 = bf16[1,2,128,384]{3,2,1,0:T(8,128)(2,1)S(1)} collective-permute-done((bf16[1,2,128,384]{3,2,1,0:T(8,128)(2,1)S(1)}, bf16[1,2,128,384]{3,2,1,0:T(8,128)(2,1)S(1)}, u32[]{:S(2)}, u32[]{:S(2)}) %collective-permute-start.5) | collective-permute-done | bytes 196640 | tf_op jit(solution)/shard_map/ppermute | solution.py:47
  18.9 4.4 %collective-permute-done.7 = bf16[1,2,128,384]{3,2,1,0:T(8,128)(2,1)S(1)} collective-permute-done((bf16[1,2,128,384]{3,2,1,0:T(8,128)(2,1)S(1)}, bf16[1,2,128,384]{3,2,1,0:T(8,128)(2,1)S(1)}, u32[]{:S(2)}, u32[]{:S(2)}) %collective-permute-start.7) | collective-permute-done | bytes 196640 | tf_op jit(solution)/shard_map/ppermute | solution.py:47
  24.1 2.2 %fusion.2.k_ref = bf16[1,384,2048]{2,1,0:T(8,128)(2,1)} fusion(bf16[2048,384]{1,0:T(8,128)(2,1)S(1)} %fusion.1, bf16[384,384]{1,0:T(8,128)(2,1)S(1)} %copy-done), kind=kOutput, calls=%fused_computation.10 | convolution fusion | flops 604766208 | bytes 3440640 | tf_op jit(solution)/shard_map/ftc,cd->fdt/dot_general | solution.py:165
  26.4 2.3 %fusion.3.v_ref = bf16[1,2048,384]{2,1,0:T(8,128)(2,1)} fusion(bf16[2048,384]{1,0:T(8,128)(2,1)S(1)} %fusion.1, bf16[384,384]{1,0:T(8,128)(2,1)S(1)} %copy-done.9), kind=kOutput, calls=%fused_computation.11 | convolution fusion | flops 604766208 | bytes 3440640 | tf_op jit(solution)/shard_map/ftc,cd->ftd/dot_general | solution.py:135
  28.6 4.3 %shard_map.100 = bf16[1,256,384]{2,1,0:T(8,128)(2,1)} custom-call(bf16[1,256,384]{2,1,0:T(8,128)(2,1)} %fusion.91.q_ref, bf16[1,384,2048]{2,1,0:T(8,128)(2,1)} %fusion.2.k_ref, bf16[1,2048,384]{2,1,0:T(8,128)(2,1)} %fusion.3.v_ref), custom_call_target="tpu_custom_call" | custom-call | flops 805306368 | bytes 3538944 | tf_op jit(solution)/shard_map/pallas_call | solution.py:117
  33.0 1.2 %fusion.146 = bf16[1,2,128,384]{3,2,1,0:T(8,128)(2,1)S(1)} fusion(bf16[1,128,384]{2,1,0:T(8,128)(2,1)S(1)} %bitcast.161, bf16[1,128,384]{2,1,0:T(8,128)(2,1)S(1)} %bitcast.162, bf16[2,128,384]{2,1,0:T(8,128)(2,1)} %bitcast.173, bf16[384,384]{1,0:T(8,128)(2,1)S(1)} %copy-done.7), kind=kOutput, calls=%fused_computation.203 | convolution fusion | flops 75890688 | bytes 884736 | tf_op jit(solution)/shard_map/ftc,cd->ftd/dot_general | solution.py:171
  34.3 4.4 %collective-permute-start.8 = (bf16[1,1,128,384]{3,2,1,0:T(8,128)(2,1)S(1)}, bf16[1,1,128,384]{3,2,1,0:T(8,128)(2,1)S(1)}, u32[]{:S(2)}, u32[]{:S(2)}) collective-permute-start(bf16[1,1,128,384]{3,2,1,0:T(8,128)(2,1)S(1)} %get-tuple-element.90), channel_id=1, source_target_pairs={{0,1},{1,0},{2,3},{3,2},{4,5},{5,4},{6,7},{7,6},{8,9},{9,8},{10,11... | collective-permute-start | bytes 294920 | tf_op jit(solution)/shard_map/ppermute | solution.py:175
  38.7 0.9 collective-permute-done.8
  40.0 2.3 %collective-permute-start.10 = (bf16[4,1,128,384]{3,2,1,0:T(8,128)(2,1)S(1)}, bf16[4,1,128,384]{3,2,1,0:T(8,128)(2,1)S(1)}, u32[]{:S(2)}, u32[]{:S(2)}) collective-permute-start(bf16[4,1,128,384]{3,2,1,0:T(8,128)(2,1)S(1)} %pad_maximum_fusion.4), channel_id=1, source_target_pairs={{1,0},{2,1},{3,2},{4,3},{5,4},{6,5},{7,6},{8,7},{9,8},{10,9},{11,1... | collective-permute-start | bytes 1179656 | tf_op jit(solution)/shard_map/ppermute | solution.py:19
  42.3 4.4 %collective-permute-start.9 = (bf16[4,1,128,384]{3,2,1,0:T(8,128)(2,1)S(1)}, bf16[4,1,128,384]{3,2,1,0:T(8,128)(2,1)S(1)}, u32[]{:S(2)}, u32[]{:S(2)}) collective-permute-start(bf16[4,1,128,384]{3,2,1,0:T(8,128)(2,1)S(1)} %pad_maximum_fusion.4), channel_id=1, source_target_pairs={{0,1},{1,2},{2,3},{3,4},{4,5},{5,6},{6,7},{7,8},{8,9},{9,10},{10,1... | collective-permute-start | bytes 1179656 | tf_op jit(solution)/shard_map/ppermute | solution.py:18
  46.7 3.9 %fusion.170 = (bf16[1,1,3,384,384]{4,3,2,1,0:T(8,128)(2,1)S(1)}, bf16[1,1,3,384,384]{4,3,2,1,0:T(8,128)(2,1)S(1)}, bf16[1,1,3,384,384]{4,3,2,1,0:T(8,128)(2,1)S(...) fusion(bf16[3,3,3,384,384]{4,3,2,1,0:T(8,128)(2,1)} %param.17), kind=kLoop, calls=%fused_computation.246 | loop fusion | bytes 15925248 | tf_op jit(solution)/shard_map/slice | solution.py:94
  50.7 0.6 collective-permute-done.9
  51.6 0.7 fusion.174
  56.3 0.5 fusion.147
  56.8 5.3 %collective-permute-start.11 = (bf16[2,1,128,384]{3,2,0,1:T(8,128)(2,1)S(1)}, bf16[2,1,128,384]{3,2,0,1:T(8,128)(2,1)S(1)}, u32[]{:S(2)}, u32[]{:S(2)}) collective-permute-start(bf16[2,1,128,384]{3,2,0,1:T(8,128)(2,1)S(1)} %fusion.147), channel_id=1, source_target_pairs={{0,1},{1,2},{2,3},{3,4},{4,5},{5,6},{6,7},{7,8},{8,9},{9,10},{10,1... | collective-permute-start | bytes 589832 | tf_op jit(solution)/shard_map/ppermute | solution.py:18
  62.1 2.2 %collective-permute-start.12 = (bf16[2,1,128,384]{3,2,0,1:T(8,128)(2,1)S(1)}, bf16[2,1,128,384]{3,2,0,1:T(8,128)(2,1)S(1)}, u32[]{:S(2)}, u32[]{:S(2)}) collective-permute-start(bf16[2,1,128,384]{3,2,0,1:T(8,128)(2,1)S(1)} %fusion.147), channel_id=1, source_target_pairs={{1,0},{2,1},{3,2},{4,3},{5,4},{6,5},{7,6},{8,7},{9,8},{10,9},{11,1... | collective-permute-start | bytes 589832 | tf_op jit(solution)/shard_map/ppermute | solution.py:19
  64.8 1.2 %reshape.459 = bf16[1152,192,1,1]{0,1,2,3:T(8,128)(2,1)} reshape(bf16[1,1,3,384,192]{3,2,4,1,0:T(4,128)(2,1)S(1)} %copy.28) | data formatting | bytes 884736 | tf_op jit(solution)/shard_map/reshape;squeeze | solution.py:94
  67.5 2.5 %collective-permute-done.12 = bf16[2,1,128,384]{3,2,0,1:T(8,128)(2,1)S(1)} collective-permute-done((bf16[2,1,128,384]{3,2,0,1:T(8,128)(2,1)S(1)}, bf16[2,1,128,384]{3,2,0,1:T(8,128)(2,1)S(1)}, u32[]{:S(2)}, u32[]{:S(2)}) %collective-permute-start.12) | collective-permute-done | bytes 196640 | tf_op jit(solution)/shard_map/ppermute | solution.py:19
  70.2 0.6 broadcast_in_dim.4
  71.4 0.8 pad_slice_fusion.9
  72.5 0.7 copy-done.6
  73.2 1.1 %fusion.9 = f32[2,2,256,192]{2,3,1,0:T(8,128)S(1)} fusion(bf16[2,1,258,384]{3,2,1,0:T(8,128)(2,1)S(1)} %pad_slice_fusion.10, bf16[2,2,256,384]{3,2,1,0:T(8,128)(2,1)S(1)} %get-tuple-element.81, bf16[2,2,256,384]{3,2,1,0:T(8,128)(2,1)S(1)} %get-tuple-element.80, bf16[1152,192,1,1]{0,1,2,3:T(8,128)(2,1)S(1)} %copy-done.6), kind=kOutput, calls=%fused_computation.20 | convolution fusion | flops 462422016 | bytes 3197952 | tf_op jit(solution)/shard_map/fhwc,cd->fhwd/dot_general | solution.py:95
  74.4 1.1 %fusion.31 = f32[2,2,256,192]{2,3,1,0:T(8,128)S(1)} fusion(f32[2,2,256,192]{2,3,1,0:T(8,128)S(1)} %fusion.9, bf16[2,2,256,384]{3,2,1,0:T(8,128)(2,1)S(1)} %get-tuple-element.71, bf16[2,2,256,384]{3,2,1,0:T(8,128)(2,1)S(1)} %get-tuple-element.74, bf16[2,2,256,384]{3,2,1,0:T(8,128)(2,1)S(1)} %get-tuple-element.75, bf16[1152,192,1,1]{0,1,2,3:T(8,128)(2,1)S(1)} %reshape.458), kind=kOutput, calls=%fused_computation.47 | convolution fusion | flops 460259328 | bytes 4374528 | tf_op jit(solution)/shard_map/fhwc,cd->fhwd/dot_general | solution.py:95
  75.5 1.2 %multiply_reduce_fusion.1 = (f32[2,2,256]{2,1,0:T(2,128)S(1)}, f32[2,2,256,192]{2,3,1,0:T(8,128)S(1)}) fusion(f32[2,2,256,192]{2,3,1,0:T(8,128)S(1)} %fusion.31, bf16[1152,192,1,1]{0,1,2,3:T(8,128)(2,1)S(1)} %reshape.460, bf16[2,2,256,384]{3,2,1,0:T(8,128)(2,1)S(1)} %get-tuple-element.72, bf16[2,2,256,384]{3,2,1,0:T(8,128)(2,1)S(1)} %get-tuple-element.73, ...), kind=kOutput, calls=%fused_computation.126 | convolution fusion | flops 461044736 | bytes 4378624 | tf_op jit(solution)/shard_map/fhwc,cd->fhwd/dot_general | solution.py:95
  77.0 2.1 %collective-permute-start.13 = (bf16[4,1,256,192]{2,3,1,0:T(8,128)(2,1)S(1)}, bf16[4,1,256,192]{2,3,1,0:T(8,128)(2,1)S(1)}, u32[]{:S(2)}, u32[]{:S(2)}) collective-permute-start(bf16[4,1,256,192]{2,3,1,0:T(8,128)(2,1)S(1)} %get-tuple-element.78), channel_id=1, source_target_pairs={{0,1},{1,2},{2,3},{3,4},{4,5},{5,6},{6,7},{7,8},{8,9},{9,10},{10,1... | collective-permute-start | bytes 1179656 | tf_op jit(solution)/shard_map/ppermute | solution.py:18
  79.1 2.6 %collective-permute-start.14 = (bf16[4,1,256,192]{2,3,1,0:T(8,128)(2,1)S(1)}, bf16[4,1,256,192]{2,3,1,0:T(8,128)(2,1)S(1)}, u32[]{:S(2)}, u32[]{:S(2)}) collective-permute-start(bf16[4,1,256,192]{2,3,1,0:T(8,128)(2,1)S(1)} %get-tuple-element.79), channel_id=1, source_target_pairs={{1,0},{2,1},{3,2},{4,3},{5,4},{6,5},{7,6},{8,7},{9,8},{10,9},{11,1... | collective-permute-start | bytes 1179656 | tf_op jit(solution)/shard_map/ppermute | solution.py:19
  81.9 1.9 %collective-permute-done.13 = bf16[4,1,256,192]{2,3,1,0:T(8,128)(2,1)S(1)} collective-permute-done((bf16[4,1,256,192]{2,3,1,0:T(8,128)(2,1)S(1)}, bf16[4,1,256,192]{2,3,1,0:T(8,128)(2,1)S(1)}, u32[]{:S(2)}, u32[]{:S(2)}) %collective-permute-start.13) | collective-permute-done | bytes 393248 | tf_op jit(solution)/shard_map/ppermute | solution.py:18
  83.8 5.3 %collective-permute-done.14 = bf16[4,1,256,192]{2,3,1,0:T(8,128)(2,1)S(1)} collective-permute-done((bf16[4,1,256,192]{2,3,1,0:T(8,128)(2,1)S(1)}, bf16[4,1,256,192]{2,3,1,0:T(8,128)(2,1)S(1)}, u32[]{:S(2)}, u32[]{:S(2)}) %collective-permute-start.14) | collective-permute-done | bytes 393248 | tf_op jit(solution)/shard_map/ppermute | solution.py:19
  89.1 2.0 %select_maximum_fusion = bf16[4,4,258,192]{2,3,1,0:T(8,128)(2,1)S(1)} fusion(bf16[4,1,256,192]{2,3,1,0:T(8,128)(2,1)S(1)} %collective-permute-done.14, bf16[4,1,256,192]{2,3,1,0:T(8,128)(2,1)S(1)} %collective-permute-done.13, bf16[2,2,256,192]{2,3,1,0:T(8,128)(2,1)S(1)} %multiply_convert_fusion, bf16[2,2,256,192]{2,3,1,0:T(8,128)(2,1)S(1)} %copy-done.2), kind=kLoop, calls=%fused_computation.13 | loop fusion | flops 11888640 | bytes 3158016 | tf_op jit(solution)/shard_map/concatenate | solution.py:25
  91.1 1.7 %fusion.172 = (bf16[2,2,256,192]{2,3,1,0:T(8,128)(2,1)S(1)}, bf16[2,2,256,192]{2,3,1,0:T(8,128)(2,1)S(1)}, bf16[2,2,256,192]{2,3,1,0:T(8,128)(2,1)S(1)}, bf16[2,...) fusion(bf16[4,4,258,192]{2,3,1,0:T(8,128)(2,1)S(1)} %select_max, ...), kind=kLoop, calls=%fused_computation.248 | loop fusion | bytes 14155776 | tf_op jit(solution)/shard_map/slice | solution.py:92
  93.2 0.5 fusion.53
  93.7 0.5 convolution_add_fusion.7
  94.3 0.5 convolution_add_fusion.6
  94.8 0.5 convolution_add_fusion.5
  95.3 0.5 convolution_add_fusion.4
  95.8 0.5 convolution_add_fusion.3
  96.4 0.5 convolution_add_fusion.2
  96.9 0.5 convolution_add_fusion.1
  97.4 1.3 %fusion.43 = bf16[2,2,256,192]{2,3,1,0:T(8,128)(2,1)} fusion(f32[2,2,256,192]{2,3,1,0:T(8,128)S(1)} %get-tuple-element.93, f32[2,2,256,192]{2,3,1,0:T(8,128)S(1)} %convolution_add_fusion.1, bf16[576,192,1,1]{1,0,3,2:T(8,128)(2,1)S(1)} %bitcast.175, bf16[2,2,256,192]{2,3,1,0:T(8,128)(2,1)S(1)} %get-tuple-element.42, ...), kind=kOutput, calls=%fused_computation.55 | convolution fusion | flops 230621184 | bytes 3366912 | tf_op jit(solution)/shard_map/fhwc,cd->fhwd/dot_general | solution.py:95
  (77 shorter events, 10.7 us)
Async XLA Ops:
  0.0 24.1 %copy-start = (bf16[384,384]{1,0:T(8,128)(2,1)S(1)}, bf16[384,384]{1,0:T(8,128)(2,1)}, u32[]{:S(2)}) copy-start(bf16[384,384]{1,0:T(8,128)(2,1)} %param.14) | copy-start | bytes 884740
  0.0 4.5 %copy-start.8 = (bf16[384,384]{1,0:T(8,128)(2,1)S(1)}, bf16[384,384]{1,0:T(8,128)(2,1)}, u32[]{:S(2)}) copy-start(bf16[384,384]{1,0:T(8,128)(2,1)} %param.13) | copy-start | bytes 884740
  1.0 1.7 %collective-permute-start = (bf16[1,1,128,384]{3,2,1,0:T(8,128)(2,1)S(1)}, bf16[1,1,128,384]{3,2,1,0:T(8,128)(2,1)S(1)}, u32[]{:S(2)}, u32[]{:S(2)}) collective-permute-start(bf16[1,1,128,384]{3,2,1,0:T(8,128)(2,1)S(1)} %get-tuple-element.91), channel_id=1, source_target_pairs={{0,1},{1,0},{2,3},{3,2},{4,5},{5,4},{6,7},{7,6},{8,9},{9,8},{10,11... | collective-permute-start | bytes 294920 | tf_op jit(solution)/shard_map/ppermute | solution.py:158
  2.8 6.2 %collective-permute-start.1 = (bf16[1,2,128,384]{3,2,1,0:T(8,128)(2,1)S(1)}, bf16[1,2,128,384]{3,2,1,0:T(8,128)(2,1)S(1)}, u32[]{:S(2)}, u32[]{:S(2)}) collective-permute-start(bf16[1,2,128,384]{3,2,1,0:T(8,128)(2,1)S(1)} %pad_maximum_fusion.5), channel_id=1, source_target_pairs={{0,4},{1,5},{2,0},{3,1},{4,8},{5,9},{6,2},{7,3},{8,12},{9,13},{10,... | collective-permute-start | bytes 589832 | tf_op jit(solution)/shard_map/ppermute | solution.py:47
  3.0 6.1 %collective-permute-start.2 = (bf16[1,2,128,384]{3,2,1,0:T(8,128)(2,1)S(1)}, bf16[1,2,128,384]{3,2,1,0:T(8,128)(2,1)S(1)}, u32[]{:S(2)}, u32[]{:S(2)}) collective-permute-start(bf16[1,2,128,384]{3,2,1,0:T(8,128)(2,1)S(1)} %pad_maximum_fusion.5), channel_id=1, source_target_pairs={{0,2},{1,3},{2,6},{3,7},{4,0},{5,1},{6,10},{7,11},{8,4},{9,5},{10,... | collective-permute-start | bytes 589832 | tf_op jit(solution)/shard_map/ppermute | solution.py:50
  8.9 5.2 %collective-permute-start.3 = (bf16[1,2,128,384]{3,2,1,0:T(8,128)(2,1)S(1)}, bf16[1,2,128,384]{3,2,1,0:T(8,128)(2,1)S(1)}, u32[]{:S(2)}, u32[]{:S(2)}) collective-permute-start(bf16[1,2,128,384]{3,2,1,0:T(8,128)(2,1)S(1)} %collective-permute-done.1), channel_id=1, source_target_pairs={{0,4},{1,5},{2,0},{3,1},{4,8},{5,9},{6,2},{7,3},{8,12},{9,13},{10,... | collective-permute-start | bytes 589832 | tf_op jit(solution)/shard_map/ppermute | solution.py:47
  9.1 5.2 %collective-permute-start.4 = (bf16[1,2,128,384]{3,2,1,0:T(8,128)(2,1)S(1)}, bf16[1,2,128,384]{3,2,1,0:T(8,128)(2,1)S(1)}, u32[]{:S(2)}, u32[]{:S(2)}) collective-permute-start(bf16[1,2,128,384]{3,2,1,0:T(8,128)(2,1)S(1)} %collective-permute-done.2), channel_id=1, source_target_pairs={{0,2},{1,3},{2,6},{3,7},{4,0},{5,1},{6,10},{7,11},{8,4},{9,5},{10,... | collective-permute-start | bytes 589832 | tf_op jit(solution)/shard_map/ppermute | solution.py:50
  14.1 4.5 %collective-permute-start.5 = (bf16[1,2,128,384]{3,2,1,0:T(8,128)(2,1)S(1)}, bf16[1,2,128,384]{3,2,1,0:T(8,128)(2,1)S(1)}, u32[]{:S(2)}, u32[]{:S(2)}) collective-permute-start(bf16[1,2,128,384]{3,2,1,0:T(8,128)(2,1)S(1)} %collective-permute-done.3), channel_id=1, source_target_pairs={{0,4},{1,5},{2,0},{3,1},{4,8},{5,9},{6,2},{7,3},{8,12},{9,13},{10,... | collective-permute-start | bytes 589832 | tf_op jit(solution)/shard_map/ppermute | solution.py:47
  14.3 4.6 %collective-permute-start.6 = (bf16[1,2,128,384]{3,2,1,0:T(8,128)(2,1)S(1)}, bf16[1,2,128,384]{3,2,1,0:T(8,128)(2,1)S(1)}, u32[]{:S(2)}, u32[]{:S(2)}) collective-permute-start(bf16[1,2,128,384]{3,2,1,0:T(8,128)(2,1)S(1)} %collective-permute-done.4), channel_id=1, source_target_pairs={{0,2},{1,3},{2,6},{3,7},{4,0},{5,1},{6,10},{7,11},{8,4},{9,5},{10,... | collective-permute-start | bytes 589832 | tf_op jit(solution)/shard_map/ppermute | solution.py:50
  18.7 4.7 %collective-permute-start.7 = (bf16[1,2,128,384]{3,2,1,0:T(8,128)(2,1)S(1)}, bf16[1,2,128,384]{3,2,1,0:T(8,128)(2,1)S(1)}, u32[]{:S(2)}, u32[]{:S(2)}) collective-permute-start(bf16[1,2,128,384]{3,2,1,0:T(8,128)(2,1)S(1)} %collective-permute-done.5), channel_id=1, source_target_pairs={{0,4},{1,5},{2,0},{3,1},{4,8},{5,9},{6,2},{7,3},{8,12},{9,13},{10,... | collective-permute-start | bytes 589832 | tf_op jit(solution)/shard_map/ppermute | solution.py:47
  24.1 2.2 %copy-start.9 = (bf16[384,384]{1,0:T(8,128)(2,1)S(1)}, bf16[384,384]{1,0:T(8,128)(2,1)}, u32[]{:S(2)}) copy-start(bf16[384,384]{1,0:T(8,128)(2,1)} %param.15) | copy-start | bytes 884740
  28.6 4.4 %copy-start.7 = (bf16[384,384]{1,0:T(8,128)(2,1)S(1)}, bf16[384,384]{1,0:T(8,128)(2,1)}, u32[]{:S(2)}) copy-start(bf16[384,384]{1,0:T(8,128)(2,1)} %param.16) | copy-start | bytes 884740
  33.0 7.0 %copy-start.4 = (bf16[2,1,128,384]{3,2,1,0:T(8,128)(2,1)S(1)}, bf16[2,1,128,384]{3,2,1,0:T(8,128)(2,1)}, u32[]{:S(2)}) copy-start(bf16[2,1,128,384]{3,2,1,0:T(8,128)(2,1)} %param.11) | copy-start | bytes 589828
  34.3 5.3 %collective-permute-start.8 = (bf16[1,1,128,384]{3,2,1,0:T(8,128)(2,1)S(1)}, bf16[1,1,128,384]{3,2,1,0:T(8,128)(2,1)S(1)}, u32[]{:S(2)}, u32[]{:S(2)}) collective-permute-start(bf16[1,1,128,384]{3,2,1,0:T(8,128)(2,1)S(1)} %get-tuple-element.90), channel_id=1, source_target_pairs={{0,1},{1,0},{2,3},{3,2},{4,5},{5,4},{6,7},{7,6},{8,9},{9,8},{10,11... | collective-permute-start | bytes 294920 | tf_op jit(solution)/shard_map/ppermute | solution.py:175
  40.0 10.6 %collective-permute-start.10 = (bf16[4,1,128,384]{3,2,1,0:T(8,128)(2,1)S(1)}, bf16[4,1,128,384]{3,2,1,0:T(8,128)(2,1)S(1)}, u32[]{:S(2)}, u32[]{:S(2)}) collective-permute-start(bf16[4,1,128,384]{3,2,1,0:T(8,128)(2,1)S(1)} %pad_maximum_fusion.4), channel_id=1, source_target_pairs={{1,0},{2,1},{3,2},{4,3},{5,4},{6,5},{7,6},{8,7},{9,8},{10,9},{11,1... | collective-permute-start | bytes 1179656 | tf_op jit(solution)/shard_map/ppermute | solution.py:19
  42.3 9.0 %collective-permute-start.9 = (bf16[4,1,128,384]{3,2,1,0:T(8,128)(2,1)S(1)}, bf16[4,1,128,384]{3,2,1,0:T(8,128)(2,1)S(1)}, u32[]{:S(2)}, u32[]{:S(2)}) collective-permute-start(bf16[4,1,128,384]{3,2,1,0:T(8,128)(2,1)S(1)} %pad_maximum_fusion.4), channel_id=1, source_target_pairs={{0,1},{1,2},{2,3},{3,4},{4,5},{5,6},{6,7},{7,8},{8,9},{9,10},{10,1... | collective-permute-start | bytes 1179656 | tf_op jit(solution)/shard_map/ppermute | solution.py:18
  56.3 8.0 %copy-start.5 = (bf16[3,3,384,192]{2,3,1,0:T(8,128)(2,1)S(1)}, bf16[3,3,384,192]{2,3,1,0:T(8,128)(2,1)}, u32[]{:S(2)}) copy-start(bf16[3,3,384,192]{2,3,1,0:T(8,128)(2,1)} %param.18) | copy-start | bytes 3981316
  56.8 10.7 %collective-permute-start.11 = (bf16[2,1,128,384]{3,2,0,1:T(8,128)(2,1)S(1)}, bf16[2,1,128,384]{3,2,0,1:T(8,128)(2,1)S(1)}, u32[]{:S(2)}, u32[]{:S(2)}) collective-permute-start(bf16[2,1,128,384]{3,2,0,1:T(8,128)(2,1)S(1)} %fusion.147), channel_id=1, source_target_pairs={{0,1},{1,2},{2,3},{3,4},{4,5},{5,6},{6,7},{7,8},{8,9},{9,10},{10,1... | collective-permute-start | bytes 589832 | tf_op jit(solution)/shard_map/ppermute | solution.py:18
  62.1 7.9 %collective-permute-start.12 = (bf16[2,1,128,384]{3,2,0,1:T(8,128)(2,1)S(1)}, bf16[2,1,128,384]{3,2,0,1:T(8,128)(2,1)S(1)}, u32[]{:S(2)}, u32[]{:S(2)}) collective-permute-start(bf16[2,1,128,384]{3,2,0,1:T(8,128)(2,1)S(1)} %fusion.147), channel_id=1, source_target_pairs={{1,0},{2,1},{3,2},{4,3},{5,4},{6,5},{7,6},{8,7},{9,8},{10,9},{11,1... | collective-permute-start | bytes 589832 | tf_op jit(solution)/shard_map/ppermute | solution.py:19
  72.2 1.0 %copy-start.6 = (bf16[1152,192,1,1]{0,1,2,3:T(8,128)(2,1)S(1)}, bf16[1152,192,1,1]{0,1,2,3:T(8,128)(2,1)}, u32[]{:S(2)}) copy-start(bf16[1152,192,1,1]{0,1,2,3:T(8,128)(2,1)} %reshape.459) | copy-start | bytes 1327108
  75.5 1.4 %copy-start.2 = (bf16[2,2,256,192]{2,3,1,0:T(8,128)(2,1)S(1)}, bf16[2,2,256,192]{2,3,1,0:T(8,128)(2,1)}, u32[]{:S(2)}) copy-start(bf16[2,2,256,192]{2,3,1,0:T(8,128)(2,1)} %param.12) | copy-start | bytes 1179652
  76.7 5.0 %copy-start.3 = (bf16[3,3,3,192,192]{4,3,2,1,0:T(8,128)(2,1)S(1)}, bf16[3,3,3,192,192]{4,3,2,1,0:T(8,128)(2,1)}, u32[]{:S(2)}) copy-start(bf16[3,3,3,192,192]{4,3,2,1,0:T(8,128)(2,1)} %param.19) | copy-start | bytes 5971972
  77.0 6.8 %collective-permute-start.13 = (bf16[4,1,256,192]{2,3,1,0:T(8,128)(2,1)S(1)}, bf16[4,1,256,192]{2,3,1,0:T(8,128)(2,1)S(1)}, u32[]{:S(2)}, u32[]{:S(2)}) collective-permute-start(bf16[4,1,256,192]{2,3,1,0:T(8,128)(2,1)S(1)} %get-tuple-element.78), channel_id=1, source_target_pairs={{0,1},{1,2},{2,3},{3,4},{4,5},{5,6},{6,7},{7,8},{8,9},{9,10},{10,1... | collective-permute-start | bytes 1179656 | tf_op jit(solution)/shard_map/ppermute | solution.py:18
  79.1 10.0 %collective-permute-start.14 = (bf16[4,1,256,192]{2,3,1,0:T(8,128)(2,1)S(1)}, bf16[4,1,256,192]{2,3,1,0:T(8,128)(2,1)S(1)}, u32[]{:S(2)}, u32[]{:S(2)}) collective-permute-start(bf16[4,1,256,192]{2,3,1,0:T(8,128)(2,1)S(1)} %get-tuple-element.79), channel_id=1, source_target_pairs={{1,0},{2,1},{3,2},{4,3},{5,4},{6,5},{7,6},{8,7},{9,8},{10,9},{11,1... | collective-permute-start | bytes 1179656 | tf_op jit(solution)/shard_map/ppermute | solution.py:19
  97.4 1.3 %copy-start.1 = (bf16[384,384]{1,0:T(8,128)(2,1)S(1)}, bf16[384,384]{1,0:T(8,128)(2,1)}, u32[]{:S(2)}) copy-start(bf16[384,384]{1,0:T(8,128)(2,1)} %param.14) | copy-start | bytes 884740

commit v13 on v12

--- a/solution.py
+++ b/solution.py
@@ -49,7 +49,7 @@
         if step < chips - step:
             behind = lax.ppermute(behind, "ha", backward)
             pieces.append(behind)
-    return jnp.concatenate(pieces, axis=1)
+    return pieces
 
 
 def gather_rows(x):
@@ -98,37 +98,49 @@
     return result
 
 
-def attention_kernel(scale, q_ref, k_ref, v_ref, o_ref):
-    scores = (
-        jnp.dot(q_ref[0], k_ref[0], preferred_element_type=jnp.float32) * scale
-    )
-    largest = jnp.max(scores, axis=-1, keepdims=True)
-    weights = jnp.exp(scores - largest)
-    weight_sum = jnp.sum(weights, axis=-1, keepdims=True)
-    summed = jnp.dot(weights.astype(v_ref.dtype), v_ref[0], preferred_element_type=jnp.float32)
+def attention_kernel(scale, parts, q_ref, *refs):
+    o_ref = refs[-1]
+    key_refs, value_refs = refs[:parts], refs[parts : 2 * parts]
+    query = q_ref[0]
+    scores = [
+        jnp.dot(query, k_ref[0], preferred_element_type=jnp.float32) * scale for k_ref in key_refs
+    ]
+    largest = scores[0].max(axis=-1, keepdims=True)
+    for part in scores[1:]:
+        largest = jnp.maximum(largest, part.max(axis=-1, keepdims=True))
+    weight_sum = None
+    summed = None
+    for part, v_ref in zip(scores, value_refs):
+        weights = jnp.exp(part - largest)
+        part_sum = jnp.sum(weights, axis=-1, keepdims=True)
+        product = jnp.dot(
+            weights.astype(v_ref.dtype), v_ref[0], preferred_element_type=jnp.float32
+        )
+        weight_sum = part_sum if weight_sum is None else weight_sum + part_sum
+        summed = product if summed is None else summed + product
     o_ref[0] = (summed / weight_sum).astype(o_ref.dtype)
 
 
-def attend(queries, keys_all, values_all, scale):
+def attend(queries, key_parts, value_parts, scale):
     frames, count, channels = queries.shape
-    tokens = keys_all.shape[2]
+    parts = len(key_parts)
+    tokens = sum(k.shape[2] for k in key_parts)
     flops = 4 * frames * count * tokens * channels
-    moved = 2 * (queries.size * 2 + keys_all.size + values_all.size)
+    moved = 2 * (queries.size * 2 + 2 * tokens * channels * frames)
+    specs = [pl.BlockSpec((1, count, channels), lambda f: (f, 0, 0))]
+    specs += [pl.BlockSpec((1,) + k.shape[1:], lambda f: (f, 0, 0)) for k in key_parts]
+    specs += [pl.BlockSpec((1,) + v.shape[1:], lambda f: (f, 0, 0)) for v in value_parts]
     return pl.pallas_call(
-        functools.partial(attention_kernel, scale),
+        functools.partial(attention_kernel, scale, parts),
         grid=(frames,),
-        in_specs=[
-            pl.BlockSpec((1, count, channels), lambda f: (f, 0, 0)),
-            pl.BlockSpec((1, channels, tokens), lambda f: (f, 0, 0)),
-            pl.BlockSpec((1, tokens, channels), lambda f: (f, 0, 0)),
-        ],
+        in_specs=specs,
         out_specs=pl.BlockSpec((1, count, channels), lambda f: (f, 0, 0)),
         out_shape=jax.ShapeDtypeStruct(queries.shape, queries.dtype),
         compiler_params=pltpu.CompilerParams(vmem_limit_bytes=60 * 1024 * 1024),
         cost_estimate=pl.CostEstimate(
             flops=flops, transcendentals=frames * count * tokens, bytes_accessed=moved
         ),
-    )(queries, keys_all, values_all)
+    )(queries, *key_parts, *value_parts)
 
 
 def project_rows(tokens, weight):
@@ -156,18 +168,20 @@
     other = lax.dynamic_slice_in_dim(features, 1 - core, 1, axis=0)
     mine = lax.dynamic_slice_in_dim(features, core, 1, axis=0)
     block = jnp.concatenate([mine, lax.ppermute(other, "ha", swap)], axis=1)
-    every_row = gather_chip_rows(block)
-    normed_all = rms_scale(every_row).astype(jnp.bfloat16)
-    all_tokens = normed_all.reshape(1, -1, channels)
     normed = rms_scale(block).astype(jnp.bfloat16)
     normed_tokens = normed.reshape(1, -1, channels)
     queries = project_rows(normed_tokens, w_query)
-    keys_all = jnp.einsum(
-        "ftc,cd->fdt", all_tokens, w_key, preferred_element_type=jnp.float32
-    ).astype(jnp.bfloat16)
-    values_all = project_rows(all_tokens, w_value)
+    key_parts, value_parts = [], []
+    for piece in gather_chip_rows(block):
+        piece_tokens = rms_scale(piece).astype(jnp.bfloat16).reshape(1, -1, channels)
+        key_parts.append(
+            jnp.einsum(
+                "ftc,cd->fdt", piece_tokens, w_key, preferred_element_type=jnp.float32
+            ).astype(jnp.bfloat16)
+        )
+        value_parts.append(project_rows(piece_tokens, w_value))
     score_scale = 1.0 / math.sqrt(channels)
-    attended = attend(queries, keys_all, values_all, score_scale)
+    attended = attend(queries, key_parts, value_parts, score_scale)
     projected = jnp.einsum("ftc,cd->ftd", attended, w_output, preferred_element_type=jnp.float32)
     mixed_block = (block.astype(jnp.float32) + projected.reshape(block.shape)).astype(
         jnp.bfloat16

time: 99.5 us -> 105 us (1.055)
  matrix products: 19.9 us -> 31 us
  waiting for transfers between devices: 26.6 us -> 17.6 us
  starting transfers between devices: 28.6 us -> 29.9 us
    ppermute x4, waiting for transfers between devices: 14.5 us -> 4.1 us  [gather_chip_rows(): ahead = lax.ppermute(ahead, 'ha', forward)]
    dot_general x1 -> x8, matrix products: 2.2 us -> 7.98 us  [per_device(): jnp.einsum('ftc,cd->fdt', piece_tokens, w_key, preferred_element_type=jnp...]
    dot_general x2 -> x9, matrix products: 3.22 us -> 8.56 us  [project_rows(): jnp.einsum('ftc,cd->ftd', tokens, weight, preferred_element_type=jnp.floa...]
    ppermute x4, starting transfers between devices: 0.73 us -> 2.19 us  [gather_chip_rows(): ahead = lax.ppermute(ahead, 'ha', forward)]
    ppermute x3, waiting for transfers between devices: 0.01 us -> 1.37 us  [gather_chip_rows(): behind = lax.ppermute(behind, 'ha', backward)]
  transfers between devices with their start and end apart: 15 -> 15, of which waited for: 10 -> 10; matrix products, arithmetic and copies ran while one was open for 9% -> 22% of each run, Pallas kernels for 0% -> 0%
where the time goes in v13:
time: 105 us; the launch traced here: 103 us
  matrix products  31 us (30%)
  starting transfers between devices  29.9 us (28%)
  waiting for transfers between devices  17.6 us (17%)
  local copies, waits for them, and re-layouts  14.6 us (14%)
  other arithmetic  5.4 us (5%)
  Pallas kernels  4.26 us (4%)
    dot_general x21, matrix products, conv_taps(): jnp.einsum('fhwc,cd->fhwd', stacked, kernel, preferred_element_type=jnp.f...  13.2 us
    ppermute x3, starting transfers between devices, halo_rows(): before = lax.ppermute(last, 'ha', up)  12 us
    dot_general x9, matrix products, project_rows(): jnp.einsum('ftc,cd->ftd', tokens, weight, preferred_element_type=jnp.floa...  8.56 us
    dot_general x8, matrix products, per_device(): jnp.einsum('ftc,cd->fdt', piece_tokens, w_key, preferred_element_type=jnp...  7.98 us
    ppermute x3, waiting for transfers between devices, halo_rows(): after = lax.ppermute(first, 'ha', down)  7.85 us
    ppermute x3, starting transfers between devices, halo_rows(): after = lax.ppermute(first, 'ha', down)  7.05 us
    slice x6, local copies, waits for them, and re-layouts, conv_taps(): kernel = weight[time_off, row_off].reshape(3 * in_channels, out_channels)  5.41 us
    ppermute x1, starting transfers between devices, per_device(): back = lax.ppermute(mixed_block[:, 1:2], 'ha', swap)  4.79 us
  transfers between devices with their start and end apart: 15, of which 10 were waited for; matrix products, arithmetic and copies ran while one was open for 22% of the time, Pallas kernels for 0%

profile of v13, /device:TPU:13, one launch (start us, length us, event | category | flops | bytes accessed | tf_op | source)
XLA Modules:
  0.0 103.5 jit_solution(947658325074356666)
XLA Ops:
  0.0 1.0 %constant_dynamic-slice_fusion.1 = (bf16[1,1,128,384]{3,2,1,0:T(8,128)(2,1)S(1)}, bf16[1,1,128,384]{3,2,1,0:T(8,128)(2,1)S(1)}) fusion(bf16[2,1,128,384]{3,2,1,0:T(8,128)(2,1)} %param.10, s32[]{:T(128)S(6)} %select_n.39, s32[]{:T(128)S(6)} %select_n.40), kind=kLoop, calls=%fused_computation.273 | loop fusion | bytes 393224 | tf_op jit(solution)/shard_map/dynamic_slice | solution.py:169
  1.8 0.9 collective-permute-done
  3.0 1.3 %collective-permute-start.2 = (bf16[1,2,128,384]{3,2,1,0:T(8,128)(2,1)S(1)}, bf16[1,2,128,384]{3,2,1,0:T(8,128)(2,1)S(1)}, u32[]{:S(2)}, u32[]{:S(2)}) collective-permute-start(bf16[1,2,128,384]{3,2,1,0:T(8,128)(2,1)S(1)} %pad_maximum_fusion.5), channel_id=1, source_target_pairs={{0,2},{1,3},{2,6},{3,7},{4,0},{5,1},{6,10},{7,11},{8,4},{9,5},{10,... | collective-permute-start | bytes 589832 | tf_op jit(solution)/shard_map/ppermute | solution.py:50
  4.6 1.0 fusion.88.q_ref
  5.5 1.0 fusion.89.refs_0_
  6.5 0.9 fusion.97.refs_8_
  7.5 1.4 %collective-permute-done.2 = bf16[1,2,128,384]{3,2,1,0:T(8,128)(2,1)S(1)} collective-permute-done((bf16[1,2,128,384]{3,2,1,0:T(8,128)(2,1)S(1)}, bf16[1,2,128,384]{3,2,1,0:T(8,128)(2,1)S(1)}, u32[]{:S(2)}, u32[]{:S(2)}) %collective-permute-start.2) | collective-permute-done | bytes 196640 | tf_op jit(solution)/shard_map/ppermute | solution.py:50
  9.1 1.0 fusion.91.refs_2_
  10.1 1.0 fusion.99.refs_10_
  11.7 1.0 fusion.90.refs_1_
  12.7 1.1 %collective-permute-start.4 = (bf16[1,2,128,384]{3,2,1,0:T(8,128)(2,1)S(1)}, bf16[1,2,128,384]{3,2,1,0:T(8,128)(2,1)S(1)}, u32[]{:S(2)}, u32[]{:S(2)}) collective-permute-start(bf16[1,2,128,384]{3,2,1,0:T(8,128)(2,1)S(1)} %collective-permute-done.2), channel_id=1, source_target_pairs={{0,2},{1,3},{2,6},{3,7},{4,0},{5,1},{6,10},{7,11},{8,4},{9,5},{10,... | collective-permute-start | bytes 589832 | tf_op jit(solution)/shard_map/ppermute | solution.py:50
  13.8 0.9 fusion.98.refs_9_
  14.7 1.4 %collective-permute-done.3 = bf16[1,2,128,384]{3,2,1,0:T(8,128)(2,1)S(1)} collective-permute-done((bf16[1,2,128,384]{3,2,1,0:T(8,128)(2,1)S(1)}, bf16[1,2,128,384]{3,2,1,0:T(8,128)(2,1)S(1)}, u32[]{:S(2)}, u32[]{:S(2)}) %collective-permute-start.3) | collective-permute-done | bytes 196640 | tf_op jit(solution)/shard_map/ppermute | solution.py:47
  16.3 0.9 fusion.100.refs_11_
  17.3 1.0 fusion.92.refs_3_
  18.4 0.8 collective-permute-start.5
  19.3 1.0 fusion.101.refs_12_
  21.0 1.0 fusion.93.refs_4_
  22.0 1.0 collective-permute-done.5
  23.2 1.0 fusion.102.refs_13_
  24.2 1.0 fusion.94.refs_5_
  26.2 1.0 fusion.103.refs_14_
  27.1 1.0 fusion.95.refs_6_
  28.1 1.7 %collective-permute-done.7 = bf16[1,2,128,384]{3,2,1,0:T(8,128)(2,1)S(1)} collective-permute-done((bf16[1,2,128,384]{3,2,1,0:T(8,128)(2,1)S(1)}, bf16[1,2,128,384]{3,2,1,0:T(8,128)(2,1)S(1)}, u32[]{:S(2)}, u32[]{:S(2)}) %collective-permute-start.7) | collective-permute-done | bytes 196640 | tf_op jit(solution)/shard_map/ppermute | solution.py:47
  30.1 1.0 fusion.104.refs_15_
  31.1 1.0 fusion.96.refs_7_
  32.1 4.3 %shard_map.100 = bf16[1,256,384]{2,1,0:T(8,128)(2,1)} custom-call(bf16[1,256,384]{2,1,0:T(8,128)(2,1)} %fusion.88.q_ref, bf16[1,384,256]{2,1,0:T(8,128)(2,1)} %fusion.89.refs_0_, bf16[1,384,256]{2,1,0:T(8,128)(2,1)} %fusion.90.refs_1_, bf16[1,384,256]{2,1,0:T(8,128)(2,1)} %fusion.91.refs_2_, bf16[1,384,256]{2,1,0:T(8,128)(2,1)} %fusion.92.refs_3_, ...), custom_call_target="tpu_custom_call" | custom-call | flops 805306368 | bytes 3538944 | tf_op jit(solution)/shard_map/pallas_call | solution.py:133
  36.3 1.2 %fusion.173 = bf16[1,2,128,384]{3,2,1,0:T(8,128)(2,1)S(1)} fusion(bf16[1,128,384]{2,1,0:T(8,128)(2,1)S(1)} %bitcast.247, bf16[1,128,384]{2,1,0:T(8,128)(2,1)S(1)} %bitcast.232, bf16[2,128,384]{2,1,0:T(8,128)(2,1)} %bitcast.258, bf16[384,384]{1,0:T(8,128)(2,1)S(1)} %copy-done.8), kind=kOutput, calls=%fused_computation.256 | convolution fusion | flops 75890688 | bytes 884736 | tf_op jit(solution)/shard_map/ftc,cd->ftd/dot_general | solution.py:185
  37.6 4.8 %collective-permute-start.8 = (bf16[1,1,128,384]{3,2,1,0:T(8,128)(2,1)S(1)}, bf16[1,1,128,384]{3,2,1,0:T(8,128)(2,1)S(1)}, u32[]{:S(2)}, u32[]{:S(2)}) collective-permute-start(bf16[1,1,128,384]{3,2,1,0:T(8,128)(2,1)S(1)} %get-tuple-element.88), channel_id=1, source_target_pairs={{0,1},{1,0},{2,3},{3,2},{4,5},{5,4},{6,7},{7,6},{8,9},{9,8},{10,11... | collective-permute-start | bytes 294920 | tf_op jit(solution)/shard_map/ppermute | solution.py:189
  42.4 0.9 collective-permute-done.8
  43.8 2.3 %collective-permute-start.10 = (bf16[4,1,128,384]{3,2,1,0:T(8,128)(2,1)S(1)}, bf16[4,1,128,384]{3,2,1,0:T(8,128)(2,1)S(1)}, u32[]{:S(2)}, u32[]{:S(2)}) collective-permute-start(bf16[4,1,128,384]{3,2,1,0:T(8,128)(2,1)S(1)} %pad_maximum_fusion.4), channel_id=1, source_target_pairs={{1,0},{2,1},{3,2},{4,3},{5,4},{6,5},{7,6},{8,7},{9,8},{10,9},{11,1... | collective-permute-start | bytes 1179656 | tf_op jit(solution)/shard_map/ppermute | solution.py:19
  46.0 4.7 %collective-permute-start.9 = (bf16[4,1,128,384]{3,2,1,0:T(8,128)(2,1)S(1)}, bf16[4,1,128,384]{3,2,1,0:T(8,128)(2,1)S(1)}, u32[]{:S(2)}, u32[]{:S(2)}) collective-permute-start(bf16[4,1,128,384]{3,2,1,0:T(8,128)(2,1)S(1)} %pad_maximum_fusion.4), channel_id=1, source_target_pairs={{0,1},{1,2},{2,3},{3,4},{4,5},{5,6},{6,7},{7,8},{8,9},{9,10},{10,1... | collective-permute-start | bytes 1179656 | tf_op jit(solution)/shard_map/ppermute | solution.py:18
  50.8 3.9 %fusion.197 = (bf16[1,1,3,384,384]{4,3,2,1,0:T(8,128)(2,1)S(1)}, bf16[1,1,3,384,384]{4,3,2,1,0:T(8,128)(2,1)S(1)}, bf16[1,1,3,384,384]{4,3,2,1,0:T(8,128)(2,1)S(...) fusion(bf16[3,3,3,384,384]{4,3,2,1,0:T(8,128)(2,1)} %param.17), kind=kLoop, calls=%fused_computation.296 | loop fusion | bytes 15925248 | tf_op jit(solution)/shard_map/slice | solution.py:94
  60.9 5.4 %collective-permute-start.11 = (bf16[2,1,128,384]{3,2,0,1:T(8,128)(2,1)S(1)}, bf16[2,1,128,384]{3,2,0,1:T(8,128)(2,1)S(1)}, u32[]{:S(2)}, u32[]{:S(2)}) collective-permute-start(bf16[2,1,128,384]{3,2,0,1:T(8,128)(2,1)S(1)} %fusion.174), channel_id=1, source_target_pairs={{0,1},{1,2},{2,3},{3,4},{4,5},{5,6},{6,7},{7,8},{8,9},{9,10},{10,1... | collective-permute-start | bytes 589832 | tf_op jit(solution)/shard_map/ppermute | solution.py:18
  66.2 2.2 %collective-permute-start.12 = (bf16[2,1,128,384]{3,2,0,1:T(8,128)(2,1)S(1)}, bf16[2,1,128,384]{3,2,0,1:T(8,128)(2,1)S(1)}, u32[]{:S(2)}, u32[]{:S(2)}) collective-permute-start(bf16[2,1,128,384]{3,2,0,1:T(8,128)(2,1)S(1)} %fusion.174), channel_id=1, source_target_pairs={{1,0},{2,1},{3,2},{4,3},{5,4},{6,5},{7,6},{8,7},{9,8},{10,9},{11,1... | collective-permute-start | bytes 589832 | tf_op jit(solution)/shard_map/ppermute | solution.py:19
  68.9 1.1 %reshape.480 = bf16[1152,192,1,1]{0,1,2,3:T(8,128)(2,1)} reshape(bf16[1,1,3,384,192]{3,2,4,1,0:T(4,128)(2,1)S(1)} %copy.42) | data formatting | bytes 884736 | tf_op jit(solution)/shard_map/reshape;squeeze | solution.py:94
  71.6 2.5 %collective-permute-done.12 = bf16[2,1,128,384]{3,2,0,1:T(8,128)(2,1)S(1)} collective-permute-done((bf16[2,1,128,384]{3,2,0,1:T(8,128)(2,1)S(1)}, bf16[2,1,128,384]{3,2,0,1:T(8,128)(2,1)S(1)}, u32[]{:S(2)}, u32[]{:S(2)}) %collective-permute-start.12) | collective-permute-done | bytes 196640 | tf_op jit(solution)/shard_map/ppermute | solution.py:19
  75.5 0.8 pad_slice_fusion.9
  77.3 1.2 %fusion.6 = f32[2,2,256,192]{2,3,1,0:T(8,128)S(1)} fusion(bf16[2,1,258,384]{3,2,1,0:T(8,128)(2,1)S(1)} %pad_slice_fusion.10, bf16[2,2,256,384]{3,2,1,0:T(8,128)(2,1)S(1)} %get-tuple-element.79, bf16[2,2,256,384]{3,2,1,0:T(8,128)(2,1)S(1)} %get-tuple-element.78, bf16[1152,192,1,1]{0,1,2,3:T(8,128)(2,1)S(1)} %copy-done.7), kind=kOutput, calls=%fused_computation.13 | convolution fusion | flops 462422016 | bytes 3197952 | tf_op jit(solution)/shard_map/fhwc,cd->fhwd/dot_general | solution.py:95
  78.5 1.1 %fusion.28 = f32[2,2,256,192]{2,3,1,0:T(8,128)S(1)} fusion(f32[2,2,256,192]{2,3,1,0:T(8,128)S(1)} %fusion.6, bf16[2,2,256,384]{3,2,1,0:T(8,128)(2,1)S(1)} %get-tuple-element.69, bf16[2,2,256,384]{3,2,1,0:T(8,128)(2,1)S(1)} %get-tuple-element.72, bf16[2,2,256,384]{3,2,1,0:T(8,128)(2,1)S(1)} %get-tuple-element.73, bf16[1152,192,1,1]{0,1,2,3:T(8,128)(2,1)S(1)} %reshape.479), kind=kOutput, calls=%fused_computation.40 | convolution fusion | flops 460259328 | bytes 4374528 | tf_op jit(solution)/shard_map/fhwc,cd->fhwd/dot_general | solution.py:95
  79.6 1.2 %multiply_reduce_fusion = (f32[2,2,256]{2,1,0:T(2,128)S(1)}, f32[2,2,256,192]{2,3,1,0:T(8,128)S(1)}) fusion(f32[2,2,256,192]{2,3,1,0:T(8,128)S(1)} %fusion.28, bf16[1152,192,1,1]{0,1,2,3:T(8,128)(2,1)S(1)} %reshape.481, bf16[2,2,256,384]{3,2,1,0:T(8,128)(2,1)S(1)} %get-tuple-element.70, bf16[2,2,256,384]{3,2,1,0:T(8,128)(2,1)S(1)} %get-tuple-element.71, ...), kind=kOutput, calls=%fused_computation.151 | convolution fusion | flops 461044736 | bytes 4378624 | tf_op jit(solution)/shard_map/fhwc,cd->fhwd/dot_general | solution.py:95
  81.9 1.9 %collective-permute-start.13 = (bf16[4,1,256,192]{2,3,1,0:T(8,128)(2,1)S(1)}, bf16[4,1,256,192]{2,3,1,0:T(8,128)(2,1)S(1)}, u32[]{:S(2)}, u32[]{:S(2)}) collective-permute-start(bf16[4,1,256,192]{2,3,1,0:T(8,128)(2,1)S(1)} %get-tuple-element.76), channel_id=1, source_target_pairs={{0,1},{1,2},{2,3},{3,4},{4,5},{5,6},{6,7},{7,8},{8,9},{9,10},{10,1... | collective-permute-start | bytes 1179656 | tf_op jit(solution)/shard_map/ppermute | solution.py:18
  83.8 2.6 %collective-permute-start.14 = (bf16[4,1,256,192]{2,3,1,0:T(8,128)(2,1)S(1)}, bf16[4,1,256,192]{2,3,1,0:T(8,128)(2,1)S(1)}, u32[]{:S(2)}, u32[]{:S(2)}) collective-permute-start(bf16[4,1,256,192]{2,3,1,0:T(8,128)(2,1)S(1)} %get-tuple-element.77), channel_id=1, source_target_pairs={{1,0},{2,1},{3,2},{4,3},{5,4},{6,5},{7,6},{8,7},{9,8},{10,9},{11,1... | collective-permute-start | bytes 1179656 | tf_op jit(solution)/shard_map/ppermute | solution.py:19
  86.7 1.9 %collective-permute-done.13 = bf16[4,1,256,192]{2,3,1,0:T(8,128)(2,1)S(1)} collective-permute-done((bf16[4,1,256,192]{2,3,1,0:T(8,128)(2,1)S(1)}, bf16[4,1,256,192]{2,3,1,0:T(8,128)(2,1)S(1)}, u32[]{:S(2)}, u32[]{:S(2)}) %collective-permute-start.13) | collective-permute-done | bytes 393248 | tf_op jit(solution)/shard_map/ppermute | solution.py:18
  88.5 5.3 %collective-permute-done.14 = bf16[4,1,256,192]{2,3,1,0:T(8,128)(2,1)S(1)} collective-permute-done((bf16[4,1,256,192]{2,3,1,0:T(8,128)(2,1)S(1)}, bf16[4,1,256,192]{2,3,1,0:T(8,128)(2,1)S(1)}, u32[]{:S(2)}, u32[]{:S(2)}) %collective-permute-start.14) | collective-permute-done | bytes 393248 | tf_op jit(solution)/shard_map/ppermute | solution.py:19
  93.9 2.0 %select_maximum_fusion = bf16[4,4,258,192]{2,3,1,0:T(8,128)(2,1)S(1)} fusion(bf16[4,1,256,192]{2,3,1,0:T(8,128)(2,1)S(1)} %collective-permute-done.14, bf16[4,1,256,192]{2,3,1,0:T(8,128)(2,1)S(1)} %collective-permute-done.13, bf16[2,2,256,192]{2,3,1,0:T(8,128)(2,1)S(1)} %multiply_convert_fusion, bf16[2,2,256,192]{2,3,1,0:T(8,128)(2,1)S(1)} %copy-done.3), kind=kLoop, calls=%fused_computation.6 | loop fusion | flops 11888640 | bytes 3158016 | tf_op jit(solution)/shard_map/concatenate | solution.py:25
  95.8 1.7 %fusion.199 = (bf16[2,2,256,192]{2,3,1,0:T(8,128)(2,1)S(1)}, bf16[2,2,256,192]{2,3,1,0:T(8,128)(2,1)S(1)}, bf16[2,2,256,192]{2,3,1,0:T(8,128)(2,1)S(1)}, bf16[2,...) fusion(bf16[4,4,258,192]{2,3,1,0:T(8,128)(2,1)S(1)} %select_max, ...), kind=kLoop, calls=%fused_computation.298 | loop fusion | bytes 14155776 | tf_op jit(solution)/shard_map/slice | solution.py:92
  102.2 1.3 %fusion.40 = bf16[2,2,256,192]{2,3,1,0:T(8,128)(2,1)} fusion(f32[2,2,256,192]{2,3,1,0:T(8,128)S(1)} %get-tuple-element.92, f32[2,2,256,192]{2,3,1,0:T(8,128)S(1)} %convolution_add_fusion.1, bf16[576,192,1,1]{1,0,3,2:T(8,128)(2,1)S(1)} %bitcast.260, bf16[2,2,256,192]{2,3,1,0:T(8,128)(2,1)S(1)} %get-tuple-element.40, ...), kind=kOutput, calls=%fused_computation.48 | convolution fusion | flops 230621184 | bytes 3366912 | tf_op jit(solution)/shard_map/fhwc,cd->fhwd/dot_general | solution.py:95
  (101 shorter events, 21.4 us)
Async XLA Ops:
  0.0 6.5 %copy-start = (bf16[384,384]{1,0:T(8,128)(2,1)S(1)}, bf16[384,384]{1,0:T(8,128)(2,1)}, u32[]{:S(2)}) copy-start(bf16[384,384]{1,0:T(8,128)(2,1)} %param.15) | copy-start | bytes 884740
  0.0 4.5 %copy-start.9 = (bf16[384,384]{1,0:T(8,128)(2,1)S(1)}, bf16[384,384]{1,0:T(8,128)(2,1)}, u32[]{:S(2)}) copy-start(bf16[384,384]{1,0:T(8,128)(2,1)} %param.13) | copy-start | bytes 884740
  0.0 5.5 %copy-start.2 = (bf16[384,384]{1,0:T(8,128)(2,1)S(1)}, bf16[384,384]{1,0:T(8,128)(2,1)}, u32[]{:S(2)}) copy-start(bf16[384,384]{1,0:T(8,128)(2,1)} %param.14) | copy-start | bytes 884740
  1.1 1.7 %collective-permute-start = (bf16[1,1,128,384]{3,2,1,0:T(8,128)(2,1)S(1)}, bf16[1,1,128,384]{3,2,1,0:T(8,128)(2,1)S(1)}, u32[]{:S(2)}, u32[]{:S(2)}) collective-permute-start(bf16[1,1,128,384]{3,2,1,0:T(8,128)(2,1)S(1)} %get-tuple-element.90), channel_id=1, source_target_pairs={{0,1},{1,0},{2,3},{3,2},{4,5},{5,4},{6,7},{7,6},{8,9},{9,8},{10,11... | collective-permute-start | bytes 294920 | tf_op jit(solution)/shard_map/ppermute | solution.py:170
  2.8 8.2 %collective-permute-start.1 = (bf16[1,2,128,384]{3,2,1,0:T(8,128)(2,1)S(1)}, bf16[1,2,128,384]{3,2,1,0:T(8,128)(2,1)S(1)}, u32[]{:S(2)}, u32[]{:S(2)}) collective-permute-start(bf16[1,2,128,384]{3,2,1,0:T(8,128)(2,1)S(1)} %pad_maximum_fusion.5), channel_id=1, source_target_pairs={{0,4},{1,5},{2,0},{3,1},{4,8},{5,9},{6,2},{7,3},{8,12},{9,13},{10,... | collective-permute-start | bytes 589832 | tf_op jit(solution)/shard_map/ppermute | solution.py:47
  3.0 5.8 %collective-permute-start.2 = (bf16[1,2,128,384]{3,2,1,0:T(8,128)(2,1)S(1)}, bf16[1,2,128,384]{3,2,1,0:T(8,128)(2,1)S(1)}, u32[]{:S(2)}, u32[]{:S(2)}) collective-permute-start(bf16[1,2,128,384]{3,2,1,0:T(8,128)(2,1)S(1)} %pad_maximum_fusion.5), channel_id=1, source_target_pairs={{0,2},{1,3},{2,6},{3,7},{4,0},{5,1},{6,10},{7,11},{8,4},{9,5},{10,... | collective-permute-start | bytes 589832 | tf_op jit(solution)/shard_map/ppermute | solution.py:50
  11.2 4.9 %collective-permute-start.3 = (bf16[1,2,128,384]{3,2,1,0:T(8,128)(2,1)S(1)}, bf16[1,2,128,384]{3,2,1,0:T(8,128)(2,1)S(1)}, u32[]{:S(2)}, u32[]{:S(2)}) collective-permute-start(bf16[1,2,128,384]{3,2,1,0:T(8,128)(2,1)S(1)} %collective-permute-done.1), channel_id=1, source_target_pairs={{0,4},{1,5},{2,0},{3,1},{4,8},{5,9},{6,2},{7,3},{8,12},{9,13},{10,... | collective-permute-start | bytes 589832 | tf_op jit(solution)/shard_map/ppermute | solution.py:47
  12.7 5.6 %collective-permute-start.4 = (bf16[1,2,128,384]{3,2,1,0:T(8,128)(2,1)S(1)}, bf16[1,2,128,384]{3,2,1,0:T(8,128)(2,1)S(1)}, u32[]{:S(2)}, u32[]{:S(2)}) collective-permute-start(bf16[1,2,128,384]{3,2,1,0:T(8,128)(2,1)S(1)} %collective-permute-done.2), channel_id=1, source_target_pairs={{0,2},{1,3},{2,6},{3,7},{4,0},{5,1},{6,10},{7,11},{8,4},{9,5},{10,... | collective-permute-start | bytes 589832 | tf_op jit(solution)/shard_map/ppermute | solution.py:50
  18.4 4.6 %collective-permute-start.5 = (bf16[1,2,128,384]{3,2,1,0:T(8,128)(2,1)S(1)}, bf16[1,2,128,384]{3,2,1,0:T(8,128)(2,1)S(1)}, u32[]{:S(2)}, u32[]{:S(2)}) collective-permute-start(bf16[1,2,128,384]{3,2,1,0:T(8,128)(2,1)S(1)} %collective-permute-done.3), channel_id=1, source_target_pairs={{0,4},{1,5},{2,0},{3,1},{4,8},{5,9},{6,2},{7,3},{8,12},{9,13},{10,... | collective-permute-start | bytes 589832 | tf_op jit(solution)/shard_map/ppermute | solution.py:47
  20.2 4.9 %collective-permute-start.6 = (bf16[1,2,128,384]{3,2,1,0:T(8,128)(2,1)S(1)}, bf16[1,2,128,384]{3,2,1,0:T(8,128)(2,1)S(1)}, u32[]{:S(2)}, u32[]{:S(2)}) collective-permute-start(bf16[1,2,128,384]{3,2,1,0:T(8,128)(2,1)S(1)} %collective-permute-done.4), channel_id=1, source_target_pairs={{0,2},{1,3},{2,6},{3,7},{4,0},{5,1},{6,10},{7,11},{8,4},{9,5},{10,... | collective-permute-start | bytes 589832 | tf_op jit(solution)/shard_map/ppermute | solution.py:50
  25.3 4.6 %collective-permute-start.7 = (bf16[1,2,128,384]{3,2,1,0:T(8,128)(2,1)S(1)}, bf16[1,2,128,384]{3,2,1,0:T(8,128)(2,1)S(1)}, u32[]{:S(2)}, u32[]{:S(2)}) collective-permute-start(bf16[1,2,128,384]{3,2,1,0:T(8,128)(2,1)S(1)} %collective-permute-done.5), channel_id=1, source_target_pairs={{0,4},{1,5},{2,0},{3,1},{4,8},{5,9},{6,2},{7,3},{8,12},{9,13},{10,... | collective-permute-start | bytes 589832 | tf_op jit(solution)/shard_map/ppermute | solution.py:47
  32.1 4.3 %copy-start.8 = (bf16[384,384]{1,0:T(8,128)(2,1)S(1)}, bf16[384,384]{1,0:T(8,128)(2,1)}, u32[]{:S(2)}) copy-start(bf16[384,384]{1,0:T(8,128)(2,1)} %param.16) | copy-start | bytes 884740
  36.3 7.4 %copy-start.5 = (bf16[2,1,128,384]{3,2,1,0:T(8,128)(2,1)S(1)}, bf16[2,1,128,384]{3,2,1,0:T(8,128)(2,1)}, u32[]{:S(2)}) copy-start(bf16[2,1,128,384]{3,2,1,0:T(8,128)(2,1)} %param.11) | copy-start | bytes 589828
  37.6 5.7 %collective-permute-start.8 = (bf16[1,1,128,384]{3,2,1,0:T(8,128)(2,1)S(1)}, bf16[1,1,128,384]{3,2,1,0:T(8,128)(2,1)S(1)}, u32[]{:S(2)}, u32[]{:S(2)}) collective-permute-start(bf16[1,1,128,384]{3,2,1,0:T(8,128)(2,1)S(1)} %get-tuple-element.88), channel_id=1, source_target_pairs={{0,1},{1,0},{2,3},{3,2},{4,5},{5,4},{6,7},{7,6},{8,9},{9,8},{10,11... | collective-permute-start | bytes 294920 | tf_op jit(solution)/shard_map/ppermute | solution.py:189
  43.8 11.0 %collective-permute-start.10 = (bf16[4,1,128,384]{3,2,1,0:T(8,128)(2,1)S(1)}, bf16[4,1,128,384]{3,2,1,0:T(8,128)(2,1)S(1)}, u32[]{:S(2)}, u32[]{:S(2)}) collective-permute-start(bf16[4,1,128,384]{3,2,1,0:T(8,128)(2,1)S(1)} %pad_maximum_fusion.4), channel_id=1, source_target_pairs={{1,0},{2,1},{3,2},{4,3},{5,4},{6,5},{7,6},{8,7},{9,8},{10,9},{11,1... | collective-permute-start | bytes 1179656 | tf_op jit(solution)/shard_map/ppermute | solution.py:19
  46.0 9.3 %collective-permute-start.9 = (bf16[4,1,128,384]{3,2,1,0:T(8,128)(2,1)S(1)}, bf16[4,1,128,384]{3,2,1,0:T(8,128)(2,1)S(1)}, u32[]{:S(2)}, u32[]{:S(2)}) collective-permute-start(bf16[4,1,128,384]{3,2,1,0:T(8,128)(2,1)S(1)} %pad_maximum_fusion.4), channel_id=1, source_target_pairs={{0,1},{1,2},{2,3},{3,4},{4,5},{5,6},{6,7},{7,8},{8,9},{9,10},{10,1... | collective-permute-start | bytes 1179656 | tf_op jit(solution)/shard_map/ppermute | solution.py:18
  60.4 8.0 %copy-start.6 = (bf16[3,3,384,192]{2,3,1,0:T(8,128)(2,1)S(1)}, bf16[3,3,384,192]{2,3,1,0:T(8,128)(2,1)}, u32[]{:S(2)}) copy-start(bf16[3,3,384,192]{2,3,1,0:T(8,128)(2,1)} %param.18) | copy-start | bytes 3981316
  60.9 10.7 %collective-permute-start.11 = (bf16[2,1,128,384]{3,2,0,1:T(8,128)(2,1)S(1)}, bf16[2,1,128,384]{3,2,0,1:T(8,128)(2,1)S(1)}, u32[]{:S(2)}, u32[]{:S(2)}) collective-permute-start(bf16[2,1,128,384]{3,2,0,1:T(8,128)(2,1)S(1)} %fusion.174), channel_id=1, source_target_pairs={{0,1},{1,2},{2,3},{3,4},{4,5},{5,6},{6,7},{7,8},{8,9},{9,10},{10,1... | collective-permute-start | bytes 589832 | tf_op jit(solution)/shard_map/ppermute | solution.py:18
  66.2 7.9 %collective-permute-start.12 = (bf16[2,1,128,384]{3,2,0,1:T(8,128)(2,1)S(1)}, bf16[2,1,128,384]{3,2,0,1:T(8,128)(2,1)S(1)}, u32[]{:S(2)}, u32[]{:S(2)}) collective-permute-start(bf16[2,1,128,384]{3,2,0,1:T(8,128)(2,1)S(1)} %fusion.174), channel_id=1, source_target_pairs={{1,0},{2,1},{3,2},{4,3},{5,4},{6,5},{7,6},{8,7},{9,8},{10,9},{11,1... | collective-permute-start | bytes 589832 | tf_op jit(solution)/shard_map/ppermute | solution.py:19
  76.3 1.0 copy-start.7
  79.6 6.8 %copy-start.4 = (bf16[3,3,3,192,192]{4,3,2,1,0:T(8,128)(2,1)S(1)}, bf16[3,3,3,192,192]{4,3,2,1,0:T(8,128)(2,1)}, u32[]{:S(2)}) copy-start(bf16[3,3,3,192,192]{4,3,2,1,0:T(8,128)(2,1)} %param.19) | copy-start | bytes 5971972
  80.8 1.0 copy-start.3
  81.9 6.6 %collective-permute-start.13 = (bf16[4,1,256,192]{2,3,1,0:T(8,128)(2,1)S(1)}, bf16[4,1,256,192]{2,3,1,0:T(8,128)(2,1)S(1)}, u32[]{:S(2)}, u32[]{:S(2)}) collective-permute-start(bf16[4,1,256,192]{2,3,1,0:T(8,128)(2,1)S(1)} %get-tuple-element.76), channel_id=1, source_target_pairs={{0,1},{1,2},{2,3},{3,4},{4,5},{5,6},{6,7},{7,8},{8,9},{9,10},{10,1... | collective-permute-start | bytes 1179656 | tf_op jit(solution)/shard_map/ppermute | solution.py:18
  83.8 10.0 %collective-permute-start.14 = (bf16[4,1,256,192]{2,3,1,0:T(8,128)(2,1)S(1)}, bf16[4,1,256,192]{2,3,1,0:T(8,128)(2,1)S(1)}, u32[]{:S(2)}, u32[]{:S(2)}) collective-permute-start(bf16[4,1,256,192]{2,3,1,0:T(8,128)(2,1)S(1)} %get-tuple-element.77), channel_id=1, source_target_pairs={{1,0},{2,1},{3,2},{4,3},{5,4},{6,5},{7,6},{8,7},{9,8},{10,9},{11,1... | collective-permute-start | bytes 1179656 | tf_op jit(solution)/shard_map/ppermute | solution.py:19
  102.2 1.3 %copy-start.1 = (bf16[384,384]{1,0:T(8,128)(2,1)S(1)}, bf16[384,384]{1,0:T(8,128)(2,1)}, u32[]{:S(2)}) copy-start(bf16[384,384]{1,0:T(8,128)(2,1)} %param.15) | copy-start | bytes 884740

commit v14 on v12

--- a/solution.py
+++ b/solution.py
@@ -98,29 +98,36 @@
     return result
 
 
-def attention_kernel(scale, q_ref, k_ref, v_ref, o_ref):
+def attention_kernel(scale, q_ref, n_ref, wk_ref, wv_ref, o_ref):
+    tokens = n_ref[0]
+    keys = jnp.dot(tokens, wk_ref[...], preferred_element_type=jnp.float32).astype(tokens.dtype)
+    values = jnp.dot(tokens, wv_ref[...], preferred_element_type=jnp.float32).astype(tokens.dtype)
     scores = (
-        jnp.dot(q_ref[0], k_ref[0], preferred_element_type=jnp.float32) * scale
+        lax.dot_general(
+            q_ref[0], keys, (((1,), (1,)), ((), ())), preferred_element_type=jnp.float32
+        )
+        * scale
     )
     largest = jnp.max(scores, axis=-1, keepdims=True)
     weights = jnp.exp(scores - largest)
     weight_sum = jnp.sum(weights, axis=-1, keepdims=True)
-    summed = jnp.dot(weights.astype(v_ref.dtype), v_ref[0], preferred_element_type=jnp.float32)
+    summed = jnp.dot(weights.astype(values.dtype), values, preferred_element_type=jnp.float32)
     o_ref[0] = (summed / weight_sum).astype(o_ref.dtype)
 
 
-def attend(queries, keys_all, values_all, scale):
+def attend(queries, all_tokens, w_key, w_value, scale):
     frames, count, channels = queries.shape
-    tokens = keys_all.shape[2]
-    flops = 4 * frames * count * tokens * channels
-    moved = 2 * (queries.size * 2 + keys_all.size + values_all.size)
+    tokens = all_tokens.shape[1]
+    flops = 4 * frames * count * tokens * channels + 4 * frames * tokens * channels * channels
+    moved = 2 * (queries.size * 2 + all_tokens.size + w_key.size + w_value.size)
     return pl.pallas_call(
         functools.partial(attention_kernel, scale),
         grid=(frames,),
         in_specs=[
             pl.BlockSpec((1, count, channels), lambda f: (f, 0, 0)),
-            pl.BlockSpec((1, channels, tokens), lambda f: (f, 0, 0)),
             pl.BlockSpec((1, tokens, channels), lambda f: (f, 0, 0)),
+            pl.BlockSpec(w_key.shape, lambda f: (0, 0)),
+            pl.BlockSpec(w_value.shape, lambda f: (0, 0)),
         ],
         out_specs=pl.BlockSpec((1, count, channels), lambda f: (f, 0, 0)),
         out_shape=jax.ShapeDtypeStruct(queries.shape, queries.dtype),
@@ -128,7 +135,7 @@
         cost_estimate=pl.CostEstimate(
             flops=flops, transcendentals=frames * count * tokens, bytes_accessed=moved
         ),
-    )(queries, keys_all, values_all)
+    )(queries, all_tokens, w_key, w_value)
 
 
 def project_rows(tokens, weight):
@@ -162,12 +169,8 @@
     normed = rms_scale(block).astype(jnp.bfloat16)
     normed_tokens = normed.reshape(1, -1, channels)
     queries = project_rows(normed_tokens, w_query)
-    keys_all = jnp.einsum(
-        "ftc,cd->fdt", all_tokens, w_key, preferred_element_type=jnp.float32
-    ).astype(jnp.bfloat16)
-    values_all = project_rows(all_tokens, w_value)
     score_scale = 1.0 / math.sqrt(channels)
-    attended = attend(queries, keys_all, values_all, score_scale)
+    attended = attend(queries, all_tokens, w_key, w_value, score_scale)
     projected = jnp.einsum("ftc,cd->ftd", attended, w_output, preferred_element_type=jnp.float32)
     mixed_block = (block.astype(jnp.float32) + projected.reshape(block.shape)).astype(
         jnp.bfloat16

time: 99.5 us -> 98 us (0.985)
  matrix products: 19.9 us -> 15.4 us
  Pallas kernels: 4.35 us -> 5.91 us
  other arithmetic: 4.56 us -> 5.75 us
    dot_general x2 -> x1, matrix products: 3.22 us -> 0.95 us  [project_rows(): jnp.einsum('ftc,cd->ftd', tokens, weight, preferred_element_type=jnp.floa...]
    dot_general x1 -> x0, matrix products: 2.2 us -> none  [per_device(): jnp.einsum('ftc,cd->fdt', all_tokens, w_key, preferred_element_type=jnp.f...]
    pallas_call x1, Pallas kernels: 4.35 us -> 5.91 us  [attend(): pl.pallas_call(functools.partial(attention_kernel, scale), grid=(frames,)...]
    convert_element_type x1, other arithmetic: 0.34 us -> 1.53 us  [per_device(): normed_all = rms_scale(every_row).astype(jnp.bfloat16)]
    unnamed x28 -> x24, local copies, waits for them, and re-layouts: 1.99 us -> 1.96 us
where the time goes in v14:
time: 98 us; the launch traced here: 97.2 us
  starting transfers between devices  28.6 us (29%)
  waiting for transfers between devices  26.8 us (27%)
  matrix products  15.4 us (16%)
  local copies, waits for them, and re-layouts  14.1 us (14%)
  Pallas kernels  5.91 us (6%)
  other arithmetic  5.75 us (6%)
    ppermute x4, waiting for transfers between devices, gather_chip_rows(): ahead = lax.ppermute(ahead, 'ha', forward)  14.5 us
    dot_general x21, matrix products, conv_taps(): jnp.einsum('fhwc,cd->fhwd', stacked, kernel, preferred_element_type=jnp.f...  13.2 us
    ppermute x3, starting transfers between devices, halo_rows(): before = lax.ppermute(last, 'ha', up)  11.8 us
    ppermute x3, waiting for transfers between devices, halo_rows(): after = lax.ppermute(first, 'ha', down)  7.83 us
    ppermute x3, starting transfers between devices, halo_rows(): after = lax.ppermute(first, 'ha', down)  7.04 us
    pallas_call x1, Pallas kernels, attend(): pl.pallas_call(functools.partial(attention_kernel, scale), grid=(frames,)...  5.91 us
    slice x6, local copies, waits for them, and re-layouts, conv_taps(): kernel = weight[time_off, row_off].reshape(3 * in_channels, out_channels)  5.41 us
    ppermute x1, starting transfers between devices, per_device(): back = lax.ppermute(mixed_block[:, 1:2], 'ha', swap)  4.4 us
  transfers between devices with their start and end apart: 15, of which 10 were waited for; matrix products, arithmetic and copies ran while one was open for 9% of the time, Pallas kernels for 0%

profile of v14, /device:TPU:13, one launch (start us, length us, event | category | flops | bytes accessed | tf_op | source)
XLA Modules:
  0.0 97.2 jit_solution(13807140256597052151)
XLA Ops:
  0.0 1.0 %constant_dynamic-update-slice_fusion.8 = (bf16[1,16,128,384]{3,2,1,0:T(8,128)(2,1)S(1)}, bf16[1,1,128,384]{3,2,1,0:T(8,128)(2,1)S(1)}, bf16[1,1,128,384]{3,2,1,0:T(8,128)(2,1)S(1)}) fusion(bf16[2,1,128,384]{3,2,1,0:T(8,128)(2,1)} %param.10, s32[]{:T(128)S(6)} %select_n.39, s32[]{:T(128)S(6)} %select_n.40), kind=kLoop, calls=%fused_computation.213 | loop fusion | bytes 491528
  1.0 0.7 collective-permute-start
  1.8 0.9 collective-permute-done
  3.0 1.3 %collective-permute-start.2 = (bf16[1,2,128,384]{3,2,1,0:T(8,128)(2,1)S(1)}, bf16[1,2,128,384]{3,2,1,0:T(8,128)(2,1)S(1)}, u32[]{:S(2)}, u32[]{:S(2)}) collective-permute-start(bf16[1,2,128,384]{3,2,1,0:T(8,128)(2,1)S(1)} %pad_maximum_fusion.5), channel_id=1, source_target_pairs={{0,2},{1,3},{2,6},{3,7},{4,0},{5,1},{6,10},{7,11},{8,4},{9,5},{10,... | collective-permute-start | bytes 589832 | tf_op jit(solution)/shard_map/ppermute | solution.py:50
  4.5 1.0 fusion.89.q_ref
  5.5 3.4 %collective-permute-done.1 = bf16[1,2,128,384]{3,2,1,0:T(8,128)(2,1)S(1)} collective-permute-done((bf16[1,2,128,384]{3,2,1,0:T(8,128)(2,1)S(1)}, bf16[1,2,128,384]{3,2,1,0:T(8,128)(2,1)S(1)}, u32[]{:S(2)}, u32[]{:S(2)}) %collective-permute-start.1) | collective-permute-done | bytes 196640 | tf_op jit(solution)/shard_map/ppermute | solution.py:47
  9.1 1.3 %collective-permute-start.4 = (bf16[1,2,128,384]{3,2,1,0:T(8,128)(2,1)S(1)}, bf16[1,2,128,384]{3,2,1,0:T(8,128)(2,1)S(1)}, u32[]{:S(2)}, u32[]{:S(2)}) collective-permute-start(bf16[1,2,128,384]{3,2,1,0:T(8,128)(2,1)S(1)} %collective-permute-done.2), channel_id=1, source_target_pairs={{0,2},{1,3},{2,6},{3,7},{4,0},{5,1},{6,10},{7,11},{8,4},{9,5},{10,... | collective-permute-start | bytes 589832 | tf_op jit(solution)/shard_map/ppermute | solution.py:50
  10.5 3.7 %collective-permute-done.3 = bf16[1,2,128,384]{3,2,1,0:T(8,128)(2,1)S(1)} collective-permute-done((bf16[1,2,128,384]{3,2,1,0:T(8,128)(2,1)S(1)}, bf16[1,2,128,384]{3,2,1,0:T(8,128)(2,1)S(1)}, u32[]{:S(2)}, u32[]{:S(2)}) %collective-permute-start.3) | collective-permute-done | bytes 196640 | tf_op jit(solution)/shard_map/ppermute | solution.py:47
  14.3 1.3 %collective-permute-start.6 = (bf16[1,2,128,384]{3,2,1,0:T(8,128)(2,1)S(1)}, bf16[1,2,128,384]{3,2,1,0:T(8,128)(2,1)S(1)}, u32[]{:S(2)}, u32[]{:S(2)}) collective-permute-start(bf16[1,2,128,384]{3,2,1,0:T(8,128)(2,1)S(1)} %collective-permute-done.4), channel_id=1, source_target_pairs={{0,2},{1,3},{2,6},{3,7},{4,0},{5,1},{6,10},{7,11},{8,4},{9,5},{10,... | collective-permute-start | bytes 589832 | tf_op jit(solution)/shard_map/ppermute | solution.py:50
  15.7 3.0 %collective-permute-done.5 = bf16[1,2,128,384]{3,2,1,0:T(8,128)(2,1)S(1)} collective-permute-done((bf16[1,2,128,384]{3,2,1,0:T(8,128)(2,1)S(1)}, bf16[1,2,128,384]{3,2,1,0:T(8,128)(2,1)S(1)}, u32[]{:S(2)}, u32[]{:S(2)}) %collective-permute-start.5) | collective-permute-done | bytes 196640 | tf_op jit(solution)/shard_map/ppermute | solution.py:47
  18.9 4.4 %collective-permute-done.7 = bf16[1,2,128,384]{3,2,1,0:T(8,128)(2,1)S(1)} collective-permute-done((bf16[1,2,128,384]{3,2,1,0:T(8,128)(2,1)S(1)}, bf16[1,2,128,384]{3,2,1,0:T(8,128)(2,1)S(1)}, u32[]{:S(2)}, u32[]{:S(2)}) %collective-permute-start.7) | collective-permute-done | bytes 196640 | tf_op jit(solution)/shard_map/ppermute | solution.py:47
  23.8 1.5 %fusion.1.n_ref = bf16[1,2048,384]{2,1,0:T(8,128)(2,1)} fusion(f32[2048]{0:T(1024)S(1)} %rsqrt_bitcast_fusion, bf16[1,16,128,384]{3,2,1,0:T(8,128)(2,1)S(1)} %constant_dynamic-update-slice_fusion), kind=kLoop, calls=%fused_computation.6 | loop fusion | flops 2359296 | bytes 3153920 | tf_op jit(solution)/shard_map/convert_element_type | solution.py:167
  25.3 5.9 %shard_map.100 = bf16[1,256,384]{2,1,0:T(8,128)(2,1)} custom-call(bf16[1,256,384]{2,1,0:T(8,128)(2,1)} %fusion.89.q_ref, bf16[1,2048,384]{2,1,0:T(8,128)(2,1)} %fusion.1.n_ref, bf16[384,384]{1,0:T(8,128)(2,1)} %wk_ref.1, bf16[384,384]{1,0:T(8,128)(2,1)} %wv_ref.1), custom_call_target="tpu_custom_call" | custom-call | flops 2013265920 | bytes 2555904 | tf_op jit(solution)/shard_map/pallas_call | solution.py:123
  31.2 1.2 %fusion.146 = bf16[1,2,128,384]{3,2,1,0:T(8,128)(2,1)S(1)} fusion(bf16[2,128,384]{2,1,0:T(8,128)(2,1)} %bitcast.175, bf16[384,384]{1,0:T(8,128)(2,1)S(1)} %copy-done.7, bf16[1,128,384]{2,1,0:T(8,128)(2,1)S(1)} %bitcast.153, bf16[1,128,384]{2,1,0:T(8,128)(2,1)S(1)} %bitcast.154), kind=kOutput, calls=%fused_computation.199 | convolution fusion | flops 75890688 | bytes 884736 | tf_op jit(solution)/shard_map/ftc,cd->ftd/dot_general | solution.py:174
  32.5 4.4 %collective-permute-start.8 = (bf16[1,1,128,384]{3,2,1,0:T(8,128)(2,1)S(1)}, bf16[1,1,128,384]{3,2,1,0:T(8,128)(2,1)S(1)}, u32[]{:S(2)}, u32[]{:S(2)}) collective-permute-start(bf16[1,1,128,384]{3,2,1,0:T(8,128)(2,1)S(1)} %get-tuple-element.90), channel_id=1, source_target_pairs={{0,1},{1,0},{2,3},{3,2},{4,5},{5,4},{6,7},{7,6},{8,9},{9,8},{10,11... | collective-permute-start | bytes 294920 | tf_op jit(solution)/shard_map/ppermute | solution.py:178
  36.9 0.9 collective-permute-done.8
  38.2 2.3 %collective-permute-start.10 = (bf16[4,1,128,384]{3,2,1,0:T(8,128)(2,1)S(1)}, bf16[4,1,128,384]{3,2,1,0:T(8,128)(2,1)S(1)}, u32[]{:S(2)}, u32[]{:S(2)}) collective-permute-start(bf16[4,1,128,384]{3,2,1,0:T(8,128)(2,1)S(1)} %pad_maximum_fusion.4), channel_id=1, source_target_pairs={{1,0},{2,1},{3,2},{4,3},{5,4},{6,5},{7,6},{8,7},{9,8},{10,9},{11,1... | collective-permute-start | bytes 1179656 | tf_op jit(solution)/shard_map/ppermute | solution.py:19
  40.5 4.2 %collective-permute-start.9 = (bf16[4,1,128,384]{3,2,1,0:T(8,128)(2,1)S(1)}, bf16[4,1,128,384]{3,2,1,0:T(8,128)(2,1)S(1)}, u32[]{:S(2)}, u32[]{:S(2)}) collective-permute-start(bf16[4,1,128,384]{3,2,1,0:T(8,128)(2,1)S(1)} %pad_maximum_fusion.4), channel_id=1, source_target_pairs={{0,1},{1,2},{2,3},{3,4},{4,5},{5,6},{6,7},{7,8},{8,9},{9,10},{10,1... | collective-permute-start | bytes 1179656 | tf_op jit(solution)/shard_map/ppermute | solution.py:18
  44.7 3.9 %fusion.172 = (bf16[1,1,3,384,384]{4,3,2,1,0:T(8,128)(2,1)S(1)}, bf16[1,1,3,384,384]{4,3,2,1,0:T(8,128)(2,1)S(1)}, bf16[1,1,3,384,384]{4,3,2,1,0:T(8,128)(2,1)S(...) fusion(bf16[3,3,3,384,384]{4,3,2,1,0:T(8,128)(2,1)} %param.17), kind=kLoop, calls=%fused_computation.242 | loop fusion | bytes 15925248 | tf_op jit(solution)/shard_map/slice | solution.py:94
  48.7 0.7 collective-permute-done.9
  49.8 0.7 fusion.176
  54.5 0.5 fusion.149
  55.0 5.5 %collective-permute-start.11 = (bf16[2,1,128,384]{3,2,0,1:T(8,128)(2,1)S(1)}, bf16[2,1,128,384]{3,2,0,1:T(8,128)(2,1)S(1)}, u32[]{:S(2)}, u32[]{:S(2)}) collective-permute-start(bf16[2,1,128,384]{3,2,0,1:T(8,128)(2,1)S(1)} %fusion.149), channel_id=1, source_target_pairs={{0,1},{1,2},{2,3},{3,4},{4,5},{5,6},{6,7},{7,8},{8,9},{9,10},{10,1... | collective-permute-start | bytes 589832 | tf_op jit(solution)/shard_map/ppermute | solution.py:18
  60.5 2.2 %collective-permute-start.12 = (bf16[2,1,128,384]{3,2,0,1:T(8,128)(2,1)S(1)}, bf16[2,1,128,384]{3,2,0,1:T(8,128)(2,1)S(1)}, u32[]{:S(2)}, u32[]{:S(2)}) collective-permute-start(bf16[2,1,128,384]{3,2,0,1:T(8,128)(2,1)S(1)} %fusion.149), channel_id=1, source_target_pairs={{1,0},{2,1},{3,2},{4,3},{5,4},{6,5},{7,6},{8,7},{9,8},{10,9},{11,1... | collective-permute-start | bytes 589832 | tf_op jit(solution)/shard_map/ppermute | solution.py:19
  63.2 1.1 %reshape.477 = bf16[1152,192,1,1]{0,1,2,3:T(8,128)(2,1)} reshape(bf16[1,1,3,384,192]{3,2,4,1,0:T(4,128)(2,1)S(1)} %copy.26) | data formatting | bytes 884736 | tf_op jit(solution)/shard_map/reshape;squeeze | solution.py:94
  65.9 2.5 %collective-permute-done.12 = bf16[2,1,128,384]{3,2,0,1:T(8,128)(2,1)S(1)} collective-permute-done((bf16[2,1,128,384]{3,2,0,1:T(8,128)(2,1)S(1)}, bf16[2,1,128,384]{3,2,0,1:T(8,128)(2,1)S(1)}, u32[]{:S(2)}, u32[]{:S(2)}) %collective-permute-start.12) | collective-permute-done | bytes 196640 | tf_op jit(solution)/shard_map/ppermute | solution.py:19
  68.6 0.6 broadcast_in_dim.4
  69.2 0.5 reshape.463
  69.8 0.8 pad_slice_fusion.9
  70.9 0.7 copy-done.6
  71.6 1.2 %fusion.7 = f32[2,2,256,192]{2,3,1,0:T(8,128)S(1)} fusion(bf16[2,1,258,384]{3,2,1,0:T(8,128)(2,1)S(1)} %pad_slice_fusion.10, bf16[2,2,256,384]{3,2,1,0:T(8,128)(2,1)S(1)} %get-tuple-element.81, bf16[2,2,256,384]{3,2,1,0:T(8,128)(2,1)S(1)} %get-tuple-element.80, bf16[1152,192,1,1]{0,1,2,3:T(8,128)(2,1)S(1)} %copy-done.6), kind=kOutput, calls=%fused_computation.16 | convolution fusion | flops 462422016 | bytes 3197952 | tf_op jit(solution)/shard_map/fhwc,cd->fhwd/dot_general | solution.py:95
  72.8 1.1 %fusion.29 = f32[2,2,256,192]{2,3,1,0:T(8,128)S(1)} fusion(f32[2,2,256,192]{2,3,1,0:T(8,128)S(1)} %fusion.7, bf16[2,2,256,384]{3,2,1,0:T(8,128)(2,1)S(1)} %get-tuple-element.71, bf16[2,2,256,384]{3,2,1,0:T(8,128)(2,1)S(1)} %get-tuple-element.74, bf16[2,2,256,384]{3,2,1,0:T(8,128)(2,1)S(1)} %get-tuple-element.75, bf16[1152,192,1,1]{0,1,2,3:T(8,128)(2,1)S(1)} %reshape.476), kind=kOutput, calls=%fused_computation.43 | convolution fusion | flops 460259328 | bytes 4374528 | tf_op jit(solution)/shard_map/fhwc,cd->fhwd/dot_general | solution.py:95
  73.9 1.2 %multiply_reduce_fusion.1 = (f32[2,2,256]{2,1,0:T(2,128)S(1)}, f32[2,2,256,192]{2,3,1,0:T(8,128)S(1)}) fusion(f32[2,2,256,192]{2,3,1,0:T(8,128)S(1)} %fusion.29, bf16[1152,192,1,1]{0,1,2,3:T(8,128)(2,1)S(1)} %reshape.478, bf16[2,2,256,384]{3,2,1,0:T(8,128)(2,1)S(1)} %get-tuple-element.72, bf16[2,2,256,384]{3,2,1,0:T(8,128)(2,1)S(1)} %get-tuple-element.73, ...), kind=kOutput, calls=%fused_computation.122 | convolution fusion | flops 461044736 | bytes 4378624 | tf_op jit(solution)/shard_map/fhwc,cd->fhwd/dot_general | solution.py:95
  75.4 2.1 %collective-permute-start.13 = (bf16[4,1,256,192]{2,3,1,0:T(8,128)(2,1)S(1)}, bf16[4,1,256,192]{2,3,1,0:T(8,128)(2,1)S(1)}, u32[]{:S(2)}, u32[]{:S(2)}) collective-permute-start(bf16[4,1,256,192]{2,3,1,0:T(8,128)(2,1)S(1)} %get-tuple-element.78), channel_id=1, source_target_pairs={{0,1},{1,2},{2,3},{3,4},{4,5},{5,6},{6,7},{7,8},{8,9},{9,10},{10,1... | collective-permute-start | bytes 1179656 | tf_op jit(solution)/shard_map/ppermute | solution.py:18
  77.5 2.6 %collective-permute-start.14 = (bf16[4,1,256,192]{2,3,1,0:T(8,128)(2,1)S(1)}, bf16[4,1,256,192]{2,3,1,0:T(8,128)(2,1)S(1)}, u32[]{:S(2)}, u32[]{:S(2)}) collective-permute-start(bf16[4,1,256,192]{2,3,1,0:T(8,128)(2,1)S(1)} %get-tuple-element.79), channel_id=1, source_target_pairs={{1,0},{2,1},{3,2},{4,3},{5,4},{6,5},{7,6},{8,7},{9,8},{10,9},{11,1... | collective-permute-start | bytes 1179656 | tf_op jit(solution)/shard_map/ppermute | solution.py:19
  80.3 1.9 %collective-permute-done.13 = bf16[4,1,256,192]{2,3,1,0:T(8,128)(2,1)S(1)} collective-permute-done((bf16[4,1,256,192]{2,3,1,0:T(8,128)(2,1)S(1)}, bf16[4,1,256,192]{2,3,1,0:T(8,128)(2,1)S(1)}, u32[]{:S(2)}, u32[]{:S(2)}) %collective-permute-start.13) | collective-permute-done | bytes 393248 | tf_op jit(solution)/shard_map/ppermute | solution.py:18
  82.2 5.3 %collective-permute-done.14 = bf16[4,1,256,192]{2,3,1,0:T(8,128)(2,1)S(1)} collective-permute-done((bf16[4,1,256,192]{2,3,1,0:T(8,128)(2,1)S(1)}, bf16[4,1,256,192]{2,3,1,0:T(8,128)(2,1)S(1)}, u32[]{:S(2)}, u32[]{:S(2)}) %collective-permute-start.14) | collective-permute-done | bytes 393248 | tf_op jit(solution)/shard_map/ppermute | solution.py:19
  87.5 2.0 %select_maximum_fusion = bf16[4,4,258,192]{2,3,1,0:T(8,128)(2,1)S(1)} fusion(bf16[4,1,256,192]{2,3,1,0:T(8,128)(2,1)S(1)} %collective-permute-done.14, bf16[4,1,256,192]{2,3,1,0:T(8,128)(2,1)S(1)} %collective-permute-done.13, bf16[2,2,256,192]{2,3,1,0:T(8,128)(2,1)S(1)} %multiply_convert_fusion, bf16[2,2,256,192]{2,3,1,0:T(8,128)(2,1)S(1)} %copy-done.2), kind=kLoop, calls=%fused_computation.9 | loop fusion | flops 11888640 | bytes 3158016 | tf_op jit(solution)/shard_map/concatenate | solution.py:25
  89.5 1.7 %fusion.174 = (bf16[2,2,256,192]{2,3,1,0:T(8,128)(2,1)S(1)}, bf16[2,2,256,192]{2,3,1,0:T(8,128)(2,1)S(1)}, bf16[2,2,256,192]{2,3,1,0:T(8,128)(2,1)S(1)}, bf16[2,...) fusion(bf16[4,4,258,192]{2,3,1,0:T(8,128)(2,1)S(1)} %select_max, ...), kind=kLoop, calls=%fused_computation.244 | loop fusion | bytes 14155776 | tf_op jit(solution)/shard_map/slice | solution.py:92
  91.6 0.5 fusion.51
  92.1 0.5 convolution_add_fusion.7
  92.7 0.5 convolution_add_fusion.6
  93.2 0.5 convolution_add_fusion.5
  93.7 0.5 convolution_add_fusion.4
  94.2 0.5 convolution_add_fusion.3
  94.8 0.5 convolution_add_fusion.2
  95.3 0.5 convolution_add_fusion.1
  95.8 1.3 %fusion.41 = bf16[2,2,256,192]{2,3,1,0:T(8,128)(2,1)} fusion(f32[2,2,256,192]{2,3,1,0:T(8,128)S(1)} %get-tuple-element.93, f32[2,2,256,192]{2,3,1,0:T(8,128)S(1)} %convolution_add_fusion.1, bf16[576,192,1,1]{1,0,3,2:T(8,128)(2,1)S(1)} %bitcast.166, bf16[2,2,256,192]{2,3,1,0:T(8,128)(2,1)S(1)} %get-tuple-element.42, ...), kind=kOutput, calls=%fused_computation.51 | convolution fusion | flops 230621184 | bytes 3366912 | tf_op jit(solution)/shard_map/fhwc,cd->fhwd/dot_general | solution.py:95
  (71 shorter events, 9.8 us)
Async XLA Ops:
  0.0 4.5 %copy-start = (bf16[384,384]{1,0:T(8,128)(2,1)S(1)}, bf16[384,384]{1,0:T(8,128)(2,1)}, u32[]{:S(2)}) copy-start(bf16[384,384]{1,0:T(8,128)(2,1)} %param.13) | copy-start | bytes 884740
  1.0 1.7 %collective-permute-start = (bf16[1,1,128,384]{3,2,1,0:T(8,128)(2,1)S(1)}, bf16[1,1,128,384]{3,2,1,0:T(8,128)(2,1)S(1)}, u32[]{:S(2)}, u32[]{:S(2)}) collective-permute-start(bf16[1,1,128,384]{3,2,1,0:T(8,128)(2,1)S(1)} %get-tuple-element.91), channel_id=1, source_target_pairs={{0,1},{1,0},{2,3},{3,2},{4,5},{5,4},{6,7},{7,6},{8,9},{9,8},{10,11... | collective-permute-start | bytes 294920 | tf_op jit(solution)/shard_map/ppermute | solution.py:165
  2.7 6.2 %collective-permute-start.1 = (bf16[1,2,128,384]{3,2,1,0:T(8,128)(2,1)S(1)}, bf16[1,2,128,384]{3,2,1,0:T(8,128)(2,1)S(1)}, u32[]{:S(2)}, u32[]{:S(2)}) collective-permute-start(bf16[1,2,128,384]{3,2,1,0:T(8,128)(2,1)S(1)} %pad_maximum_fusion.5), channel_id=1, source_target_pairs={{0,4},{1,5},{2,0},{3,1},{4,8},{5,9},{6,2},{7,3},{8,12},{9,13},{10,... | collective-permute-start | bytes 589832 | tf_op jit(solution)/shard_map/ppermute | solution.py:47
  3.0 6.1 %collective-permute-start.2 = (bf16[1,2,128,384]{3,2,1,0:T(8,128)(2,1)S(1)}, bf16[1,2,128,384]{3,2,1,0:T(8,128)(2,1)S(1)}, u32[]{:S(2)}, u32[]{:S(2)}) collective-permute-start(bf16[1,2,128,384]{3,2,1,0:T(8,128)(2,1)S(1)} %pad_maximum_fusion.5), channel_id=1, source_target_pairs={{0,2},{1,3},{2,6},{3,7},{4,0},{5,1},{6,10},{7,11},{8,4},{9,5},{10,... | collective-permute-start | bytes 589832 | tf_op jit(solution)/shard_map/ppermute | solution.py:50
  8.9 5.2 %collective-permute-start.3 = (bf16[1,2,128,384]{3,2,1,0:T(8,128)(2,1)S(1)}, bf16[1,2,128,384]{3,2,1,0:T(8,128)(2,1)S(1)}, u32[]{:S(2)}, u32[]{:S(2)}) collective-permute-start(bf16[1,2,128,384]{3,2,1,0:T(8,128)(2,1)S(1)} %collective-permute-done.1), channel_id=1, source_target_pairs={{0,4},{1,5},{2,0},{3,1},{4,8},{5,9},{6,2},{7,3},{8,12},{9,13},{10,... | collective-permute-start | bytes 589832 | tf_op jit(solution)/shard_map/ppermute | solution.py:47
  9.1 5.2 %collective-permute-start.4 = (bf16[1,2,128,384]{3,2,1,0:T(8,128)(2,1)S(1)}, bf16[1,2,128,384]{3,2,1,0:T(8,128)(2,1)S(1)}, u32[]{:S(2)}, u32[]{:S(2)}) collective-permute-start(bf16[1,2,128,384]{3,2,1,0:T(8,128)(2,1)S(1)} %collective-permute-done.2), channel_id=1, source_target_pairs={{0,2},{1,3},{2,6},{3,7},{4,0},{5,1},{6,10},{7,11},{8,4},{9,5},{10,... | collective-permute-start | bytes 589832 | tf_op jit(solution)/shard_map/ppermute | solution.py:50
  14.1 4.5 %collective-permute-start.5 = (bf16[1,2,128,384]{3,2,1,0:T(8,128)(2,1)S(1)}, bf16[1,2,128,384]{3,2,1,0:T(8,128)(2,1)S(1)}, u32[]{:S(2)}, u32[]{:S(2)}) collective-permute-start(bf16[1,2,128,384]{3,2,1,0:T(8,128)(2,1)S(1)} %collective-permute-done.3), channel_id=1, source_target_pairs={{0,4},{1,5},{2,0},{3,1},{4,8},{5,9},{6,2},{7,3},{8,12},{9,13},{10,... | collective-permute-start | bytes 589832 | tf_op jit(solution)/shard_map/ppermute | solution.py:47
  14.3 4.6 %collective-permute-start.6 = (bf16[1,2,128,384]{3,2,1,0:T(8,128)(2,1)S(1)}, bf16[1,2,128,384]{3,2,1,0:T(8,128)(2,1)S(1)}, u32[]{:S(2)}, u32[]{:S(2)}) collective-permute-start(bf16[1,2,128,384]{3,2,1,0:T(8,128)(2,1)S(1)} %collective-permute-done.4), channel_id=1, source_target_pairs={{0,2},{1,3},{2,6},{3,7},{4,0},{5,1},{6,10},{7,11},{8,4},{9,5},{10,... | collective-permute-start | bytes 589832 | tf_op jit(solution)/shard_map/ppermute | solution.py:50
  18.6 4.7 %collective-permute-start.7 = (bf16[1,2,128,384]{3,2,1,0:T(8,128)(2,1)S(1)}, bf16[1,2,128,384]{3,2,1,0:T(8,128)(2,1)S(1)}, u32[]{:S(2)}, u32[]{:S(2)}) collective-permute-start(bf16[1,2,128,384]{3,2,1,0:T(8,128)(2,1)S(1)} %collective-permute-done.5), channel_id=1, source_target_pairs={{0,4},{1,5},{2,0},{3,1},{4,8},{5,9},{6,2},{7,3},{8,12},{9,13},{10,... | collective-permute-start | bytes 589832 | tf_op jit(solution)/shard_map/ppermute | solution.py:47
  25.3 5.9 %copy-start.7 = (bf16[384,384]{1,0:T(8,128)(2,1)S(1)}, bf16[384,384]{1,0:T(8,128)(2,1)}, u32[]{:S(2)}) copy-start(bf16[384,384]{1,0:T(8,128)(2,1)} %param.16) | copy-start | bytes 884740
  31.2 7.0 %copy-start.4 = (bf16[2,1,128,384]{3,2,1,0:T(8,128)(2,1)S(1)}, bf16[2,1,128,384]{3,2,1,0:T(8,128)(2,1)}, u32[]{:S(2)}) copy-start(bf16[2,1,128,384]{3,2,1,0:T(8,128)(2,1)} %param.11) | copy-start | bytes 589828
  32.5 5.3 %collective-permute-start.8 = (bf16[1,1,128,384]{3,2,1,0:T(8,128)(2,1)S(1)}, bf16[1,1,128,384]{3,2,1,0:T(8,128)(2,1)S(1)}, u32[]{:S(2)}, u32[]{:S(2)}) collective-permute-start(bf16[1,1,128,384]{3,2,1,0:T(8,128)(2,1)S(1)} %get-tuple-element.90), channel_id=1, source_target_pairs={{0,1},{1,0},{2,3},{3,2},{4,5},{5,4},{6,7},{7,6},{8,9},{9,8},{10,11... | collective-permute-start | bytes 294920 | tf_op jit(solution)/shard_map/ppermute | solution.py:178
  38.2 10.5 %collective-permute-start.10 = (bf16[4,1,128,384]{3,2,1,0:T(8,128)(2,1)S(1)}, bf16[4,1,128,384]{3,2,1,0:T(8,128)(2,1)S(1)}, u32[]{:S(2)}, u32[]{:S(2)}) collective-permute-start(bf16[4,1,128,384]{3,2,1,0:T(8,128)(2,1)S(1)} %pad_maximum_fusion.4), channel_id=1, source_target_pairs={{1,0},{2,1},{3,2},{4,3},{5,4},{6,5},{7,6},{8,7},{9,8},{10,9},{11,1... | collective-permute-start | bytes 1179656 | tf_op jit(solution)/shard_map/ppermute | solution.py:19
  40.5 8.9 %collective-permute-start.9 = (bf16[4,1,128,384]{3,2,1,0:T(8,128)(2,1)S(1)}, bf16[4,1,128,384]{3,2,1,0:T(8,128)(2,1)S(1)}, u32[]{:S(2)}, u32[]{:S(2)}) collective-permute-start(bf16[4,1,128,384]{3,2,1,0:T(8,128)(2,1)S(1)} %pad_maximum_fusion.4), channel_id=1, source_target_pairs={{0,1},{1,2},{2,3},{3,4},{4,5},{5,6},{6,7},{7,8},{8,9},{9,10},{10,1... | collective-permute-start | bytes 1179656 | tf_op jit(solution)/shard_map/ppermute | solution.py:18
  54.5 8.2 %copy-start.5 = (bf16[3,3,384,192]{2,3,1,0:T(8,128)(2,1)S(1)}, bf16[3,3,384,192]{2,3,1,0:T(8,128)(2,1)}, u32[]{:S(2)}) copy-start(bf16[3,3,384,192]{2,3,1,0:T(8,128)(2,1)} %param.18) | copy-start | bytes 3981316
  55.0 10.9 %collective-permute-start.11 = (bf16[2,1,128,384]{3,2,0,1:T(8,128)(2,1)S(1)}, bf16[2,1,128,384]{3,2,0,1:T(8,128)(2,1)S(1)}, u32[]{:S(2)}, u32[]{:S(2)}) collective-permute-start(bf16[2,1,128,384]{3,2,0,1:T(8,128)(2,1)S(1)} %fusion.149), channel_id=1, source_target_pairs={{0,1},{1,2},{2,3},{3,4},{4,5},{5,6},{6,7},{7,8},{8,9},{9,10},{10,1... | collective-permute-start | bytes 589832 | tf_op jit(solution)/shard_map/ppermute | solution.py:18
  60.5 7.9 %collective-permute-start.12 = (bf16[2,1,128,384]{3,2,0,1:T(8,128)(2,1)S(1)}, bf16[2,1,128,384]{3,2,0,1:T(8,128)(2,1)S(1)}, u32[]{:S(2)}, u32[]{:S(2)}) collective-permute-start(bf16[2,1,128,384]{3,2,0,1:T(8,128)(2,1)S(1)} %fusion.149), channel_id=1, source_target_pairs={{1,0},{2,1},{3,2},{4,3},{5,4},{6,5},{7,6},{8,7},{9,8},{10,9},{11,1... | collective-permute-start | bytes 589832 | tf_op jit(solution)/shard_map/ppermute | solution.py:19
  70.6 1.0 %copy-start.6 = (bf16[1152,192,1,1]{0,1,2,3:T(8,128)(2,1)S(1)}, bf16[1152,192,1,1]{0,1,2,3:T(8,128)(2,1)}, u32[]{:S(2)}) copy-start(bf16[1152,192,1,1]{0,1,2,3:T(8,128)(2,1)} %reshape.477) | copy-start | bytes 1327108
  73.9 1.4 %copy-start.2 = (bf16[2,2,256,192]{2,3,1,0:T(8,128)(2,1)S(1)}, bf16[2,2,256,192]{2,3,1,0:T(8,128)(2,1)}, u32[]{:S(2)}) copy-start(bf16[2,2,256,192]{2,3,1,0:T(8,128)(2,1)} %param.12) | copy-start | bytes 1179652
  75.1 5.0 %copy-start.3 = (bf16[3,3,3,192,192]{4,3,2,1,0:T(8,128)(2,1)S(1)}, bf16[3,3,3,192,192]{4,3,2,1,0:T(8,128)(2,1)}, u32[]{:S(2)}) copy-start(bf16[3,3,3,192,192]{4,3,2,1,0:T(8,128)(2,1)} %param.19) | copy-start | bytes 5971972
  75.4 6.8 %collective-permute-start.13 = (bf16[4,1,256,192]{2,3,1,0:T(8,128)(2,1)S(1)}, bf16[4,1,256,192]{2,3,1,0:T(8,128)(2,1)S(1)}, u32[]{:S(2)}, u32[]{:S(2)}) collective-permute-start(bf16[4,1,256,192]{2,3,1,0:T(8,128)(2,1)S(1)} %get-tuple-element.78), channel_id=1, source_target_pairs={{0,1},{1,2},{2,3},{3,4},{4,5},{5,6},{6,7},{7,8},{8,9},{9,10},{10,1... | collective-permute-start | bytes 1179656 | tf_op jit(solution)/shard_map/ppermute | solution.py:18
  77.5 10.0 %collective-permute-start.14 = (bf16[4,1,256,192]{2,3,1,0:T(8,128)(2,1)S(1)}, bf16[4,1,256,192]{2,3,1,0:T(8,128)(2,1)S(1)}, u32[]{:S(2)}, u32[]{:S(2)}) collective-permute-start(bf16[4,1,256,192]{2,3,1,0:T(8,128)(2,1)S(1)} %get-tuple-element.79), channel_id=1, source_target_pairs={{1,0},{2,1},{3,2},{4,3},{5,4},{6,5},{7,6},{8,7},{9,8},{10,9},{11,1... | collective-permute-start | bytes 1179656 | tf_op jit(solution)/shard_map/ppermute | solution.py:19
  95.8 1.3 %copy-start.1 = (bf16[384,384]{1,0:T(8,128)(2,1)S(1)}, bf16[384,384]{1,0:T(8,128)(2,1)}, u32[]{:S(2)}) copy-start(bf16[384,384]{1,0:T(8,128)(2,1)} %param.13) | copy-start | bytes 884740

commit v15 on v14

--- a/solution.py
+++ b/solution.py
@@ -98,8 +98,11 @@
     return result
 
 
-def attention_kernel(scale, q_ref, n_ref, wk_ref, wv_ref, o_ref):
-    tokens = n_ref[0]
+def attention_kernel(scale, q_ref, x_ref, wk_ref, wv_ref, r_ref, wo_ref, o_ref):
+    raw = x_ref[0].astype(jnp.float32)
+    tokens = (raw * lax.rsqrt(jnp.mean(raw * raw, axis=-1, keepdims=True) + 1e-06)).astype(
+        x_ref.dtype
+    )
     keys = jnp.dot(tokens, wk_ref[...], preferred_element_type=jnp.float32).astype(tokens.dtype)
     values = jnp.dot(tokens, wv_ref[...], preferred_element_type=jnp.float32).astype(tokens.dtype)
     scores = (
@@ -112,14 +115,16 @@
     weights = jnp.exp(scores - largest)
     weight_sum = jnp.sum(weights, axis=-1, keepdims=True)
     summed = jnp.dot(weights.astype(values.dtype), values, preferred_element_type=jnp.float32)
-    o_ref[0] = (summed / weight_sum).astype(o_ref.dtype)
-
-
-def attend(queries, all_tokens, w_key, w_value, scale):
+    attended = (summed / weight_sum).astype(values.dtype)
+    projected = jnp.dot(attended, wo_ref[...], preferred_element_type=jnp.float32)
+    o_ref[0] = (r_ref[0].astype(jnp.float32) + projected).astype(o_ref.dtype)
+
+
+def attend(queries, all_rows, w_key, w_value, residual, w_output, scale):
     frames, count, channels = queries.shape
-    tokens = all_tokens.shape[1]
+    tokens = all_rows.shape[1]
     flops = 4 * frames * count * tokens * channels + 4 * frames * tokens * channels * channels
-    moved = 2 * (queries.size * 2 + all_tokens.size + w_key.size + w_value.size)
+    moved = 2 * (queries.size * 3 + all_rows.size + 3 * w_key.size)
     return pl.pallas_call(
         functools.partial(attention_kernel, scale),
         grid=(frames,),
@@ -128,6 +133,8 @@
             pl.BlockSpec((1, tokens, channels), lambda f: (f, 0, 0)),
             pl.BlockSpec(w_key.shape, lambda f: (0, 0)),
             pl.BlockSpec(w_value.shape, lambda f: (0, 0)),
+            pl.BlockSpec((1, count, channels), lambda f: (f, 0, 0)),
+            pl.BlockSpec(w_output.shape, lambda f: (0, 0)),
         ],
         out_specs=pl.BlockSpec((1, count, channels), lambda f: (f, 0, 0)),
         out_shape=jax.ShapeDtypeStruct(queries.shape, queries.dtype),
@@ -135,7 +142,7 @@
         cost_estimate=pl.CostEstimate(
             flops=flops, transcendentals=frames * count * tokens, bytes_accessed=moved
         ),
-    )(queries, all_tokens, w_key, w_value)
+    )(queries, all_rows, w_key, w_value, residual, w_output)
 
 
 def project_rows(tokens, weight):
@@ -164,17 +171,20 @@
     mine = lax.dynamic_slice_in_dim(features, core, 1, axis=0)
     block = jnp.concatenate([mine, lax.ppermute(other, "ha", swap)], axis=1)
     every_row = gather_chip_rows(block)
-    normed_all = rms_scale(every_row).astype(jnp.bfloat16)
-    all_tokens = normed_all.reshape(1, -1, channels)
+    all_rows = every_row.reshape(1, -1, channels)
     normed = rms_scale(block).astype(jnp.bfloat16)
     normed_tokens = normed.reshape(1, -1, channels)
     queries = project_rows(normed_tokens, w_query)
     score_scale = 1.0 / math.sqrt(channels)
-    attended = attend(queries, all_tokens, w_key, w_value, score_scale)
-    projected = jnp.einsum("ftc,cd->ftd", attended, w_output, preferred_element_type=jnp.float32)
-    mixed_block = (block.astype(jnp.float32) + projected.reshape(block.shape)).astype(
-        jnp.bfloat16
-    )
+    mixed_block = attend(
+        queries,
+        all_rows,
+        w_key,
+        w_value,
+        block.reshape(queries.shape),
+        w_output,
+        score_scale,
+    ).reshape(block.shape)
     back = lax.ppermute(mixed_block[:, 1:2], "ha", swap)
     own = mixed_block[:, 0:1]
     mixed = jnp.where(

time: 98 us -> 97.2 us (level)
  local copies, waits for them, and re-layouts: 14.1 us -> 16.2 us
  other arithmetic: 5.75 us -> 3.8 us
  matrix products: 15.4 us -> 14.2 us
    convert_element_type x1 -> x0, other arithmetic: 1.53 us -> none  [per_device(): normed_all = rms_scale(every_row).astype(jnp.bfloat16)]
    dot_general x1 -> x0, matrix products: 1.23 us -> none  [per_device(): jnp.einsum('ftc,cd->ftd', attended, w_output, preferred_element_type=jnp....]
    unnamed x24 -> x26, local copies, waits for them, and re-layouts: 1.96 us -> 3.16 us
where the time goes in v15:
time: 97.2 us; the launch traced here: 96.4 us
  starting transfers between devices  28.6 us (29%)
  waiting for transfers between devices  26.7 us (27%)
  local copies, waits for them, and re-layouts  16.2 us (17%)
  matrix products  14.2 us (15%)
  Pallas kernels  6.32 us (7%)
  other arithmetic  3.8 us (4%)
    ppermute x4, waiting for transfers between devices, gather_chip_rows(): ahead = lax.ppermute(ahead, 'ha', forward)  14.5 us
    dot_general x21, matrix products, conv_taps(): jnp.einsum('fhwc,cd->fhwd', stacked, kernel, preferred_element_type=jnp.f...  13.2 us
    ppermute x3, starting transfers between devices, halo_rows(): before = lax.ppermute(last, 'ha', up)  11.7 us
    ppermute x3, waiting for transfers between devices, halo_rows(): after = lax.ppermute(first, 'ha', down)  7.65 us
    ppermute x3, starting transfers between devices, halo_rows(): after = lax.ppermute(first, 'ha', down)  7.14 us
    pallas_call x1, Pallas kernels, attend(): pl.pallas_call(functools.partial(attention_kernel, scale), grid=(frames,)...  6.32 us
    slice x6, local copies, waits for them, and re-layouts, conv_taps(): kernel = weight[time_off, row_off].reshape(3 * in_channels, out_channels)  5.41 us
    ppermute x1, starting transfers between devices, per_device(): back = lax.ppermute(mixed_block[:, 1:2], 'ha', swap)  4.39 us
  transfers between devices with their start and end apart: 15, of which 10 were waited for; matrix products, arithmetic and copies ran while one was open for 9% of the time, Pallas kernels for 0%

profile of v15, /device:TPU:13, one launch (start us, length us, event | category | flops | bytes accessed | tf_op | source)
XLA Modules:
  0.0 96.4 jit_solution(8691159624057123643)
XLA Ops:
  0.0 1.0 %constant_dynamic-update-slice_fusion.8 = (bf16[1,16,128,384]{3,2,1,0:T(8,128)(2,1)S(1)}, bf16[1,1,128,384]{3,2,1,0:T(8,128)(2,1)S(1)}, bf16[1,1,128,384]{3,2,1,0:T(8,128)(2,1)S(1)}) fusion(bf16[2,1,128,384]{3,2,1,0:T(8,128)(2,1)} %param.10, s32[]{:T(128)S(6)} %select_n.39, s32[]{:T(128)S(6)} %select_n.40), kind=kLoop, calls=%fused_computation.206 | loop fusion | bytes 491528
  1.0 0.7 collective-permute-start
  1.8 0.9 collective-permute-done
  3.0 1.3 %collective-permute-start.2 = (bf16[1,2,128,384]{3,2,1,0:T(8,128)(2,1)S(1)}, bf16[1,2,128,384]{3,2,1,0:T(8,128)(2,1)S(1)}, u32[]{:S(2)}, u32[]{:S(2)}) collective-permute-start(bf16[1,2,128,384]{3,2,1,0:T(8,128)(2,1)S(1)} %pad_maximum_fusion.5), channel_id=1, source_target_pairs={{0,2},{1,3},{2,6},{3,7},{4,0},{5,1},{6,10},{7,11},{8,4},{9,5},{10,... | collective-permute-start | bytes 589832 | tf_op jit(solution)/shard_map/ppermute | solution.py:50
  4.5 1.0 fusion.88.q_ref
  5.5 3.4 %collective-permute-done.1 = bf16[1,2,128,384]{3,2,1,0:T(8,128)(2,1)S(1)} collective-permute-done((bf16[1,2,128,384]{3,2,1,0:T(8,128)(2,1)S(1)}, bf16[1,2,128,384]{3,2,1,0:T(8,128)(2,1)S(1)}, u32[]{:S(2)}, u32[]{:S(2)}) %collective-permute-start.1) | collective-permute-done | bytes 196640 | tf_op jit(solution)/shard_map/ppermute | solution.py:47
  9.1 1.3 %collective-permute-start.4 = (bf16[1,2,128,384]{3,2,1,0:T(8,128)(2,1)S(1)}, bf16[1,2,128,384]{3,2,1,0:T(8,128)(2,1)S(1)}, u32[]{:S(2)}, u32[]{:S(2)}) collective-permute-start(bf16[1,2,128,384]{3,2,1,0:T(8,128)(2,1)S(1)} %collective-permute-done.2), channel_id=1, source_target_pairs={{0,2},{1,3},{2,6},{3,7},{4,0},{5,1},{6,10},{7,11},{8,4},{9,5},{10,... | collective-permute-start | bytes 589832 | tf_op jit(solution)/shard_map/ppermute | solution.py:50
  10.5 3.7 %collective-permute-done.3 = bf16[1,2,128,384]{3,2,1,0:T(8,128)(2,1)S(1)} collective-permute-done((bf16[1,2,128,384]{3,2,1,0:T(8,128)(2,1)S(1)}, bf16[1,2,128,384]{3,2,1,0:T(8,128)(2,1)S(1)}, u32[]{:S(2)}, u32[]{:S(2)}) %collective-permute-start.3) | collective-permute-done | bytes 196640 | tf_op jit(solution)/shard_map/ppermute | solution.py:47
  14.3 1.3 %collective-permute-start.6 = (bf16[1,2,128,384]{3,2,1,0:T(8,128)(2,1)S(1)}, bf16[1,2,128,384]{3,2,1,0:T(8,128)(2,1)S(1)}, u32[]{:S(2)}, u32[]{:S(2)}) collective-permute-start(bf16[1,2,128,384]{3,2,1,0:T(8,128)(2,1)S(1)} %collective-permute-done.4), channel_id=1, source_target_pairs={{0,2},{1,3},{2,6},{3,7},{4,0},{5,1},{6,10},{7,11},{8,4},{9,5},{10,... | collective-permute-start | bytes 589832 | tf_op jit(solution)/shard_map/ppermute | solution.py:50
  15.7 3.0 %collective-permute-done.5 = bf16[1,2,128,384]{3,2,1,0:T(8,128)(2,1)S(1)} collective-permute-done((bf16[1,2,128,384]{3,2,1,0:T(8,128)(2,1)S(1)}, bf16[1,2,128,384]{3,2,1,0:T(8,128)(2,1)S(1)}, u32[]{:S(2)}, u32[]{:S(2)}) %collective-permute-start.5) | collective-permute-done | bytes 196640 | tf_op jit(solution)/shard_map/ppermute | solution.py:47
  18.9 4.4 %collective-permute-done.7 = bf16[1,2,128,384]{3,2,1,0:T(8,128)(2,1)S(1)} collective-permute-done((bf16[1,2,128,384]{3,2,1,0:T(8,128)(2,1)S(1)}, bf16[1,2,128,384]{3,2,1,0:T(8,128)(2,1)S(1)}, u32[]{:S(2)}, u32[]{:S(2)}) %collective-permute-start.7) | collective-permute-done | bytes 196640 | tf_op jit(solution)/shard_map/ppermute | solution.py:47
  23.4 1.2 %copy-done.8 = bf16[1,16,128,384]{3,2,1,0:T(8,128)(2,1)} copy-done((bf16[1,16,128,384]{3,2,1,0:T(8,128)(2,1)}, bf16[1,16,128,384]{3,2,1,0:T(8,128)(2,1)S(1)}, u32[]{:S(2)}) %copy-start.8) | copy-done | bytes 1572888
  24.6 6.3 %shard_map.100 = bf16[1,256,384]{2,1,0:T(8,128)(2,1)} custom-call(bf16[1,256,384]{2,1,0:T(8,128)(2,1)} %fusion.88.q_ref, bf16[1,2048,384]{2,1,0:T(8,128)(2,1)} %bitcast.168, bf16[384,384]{1,0:T(8,128)(2,1)} %wk_ref.1, bf16[384,384]{1,0:T(8,128)(2,1)} %wv_ref.1, bf16[1,256,384]{2,1,0:T(8,128)(2,1)} %bitcast.166, bf16[384,384]{1,0:T(8,128)(2,1)} %wo_ref.1), custom_call_target="tpu_custom_call" | custom-call | flops 2013265920 | bytes 3047424 | tf_op jit(solution)/shard_map/pallas_call | solution.py:128
  30.9 1.0 %fusion.173 = (bf16[1,1,128,384]{3,2,0,1:T(8,128)(2,1)S(1)}, bf16[1,128,384]{2,1,0:T(8,128)(2,1)S(1)}, bf16[1,1,128,384]{3,2,0,1:T(8,128)(2,1)S(1)}) fusion(bf16[1,2,128,384]{3,2,0,1:T(8,128)(2,1)} %bitcast.167), kind=kLoop, calls=%fused_computation.243 | loop fusion | bytes 491520 | tf_op jit(solution)/shard_map/slice | solution.py:189
  31.9 4.4 %collective-permute-start.8 = (bf16[1,1,128,384]{3,2,0,1:T(8,128)(2,1)S(1)}, bf16[1,1,128,384]{3,2,0,1:T(8,128)(2,1)S(1)}, u32[]{:S(2)}, u32[]{:S(2)}) collective-permute-start(bf16[1,1,128,384]{3,2,0,1:T(8,128)(2,1)S(1)} %get-tuple-element.90), channel_id=1, source_target_pairs={{0,1},{1,0},{2,3},{3,2},{4,5},{5,4},{6,7},{7,6},{8,9},{9,8},{10,11... | collective-permute-start | bytes 294920 | tf_op jit(solution)/shard_map/ppermute | solution.py:188
  36.2 0.9 collective-permute-done.8
  37.6 2.3 %collective-permute-start.10 = (bf16[4,1,128,384]{3,2,0,1:T(8,128)(2,1)S(1)}, bf16[4,1,128,384]{3,2,0,1:T(8,128)(2,1)S(1)}, u32[]{:S(2)}, u32[]{:S(2)}) collective-permute-start(bf16[4,1,128,384]{3,2,0,1:T(8,128)(2,1)S(1)} %pad_maximum_fusion.4), channel_id=1, source_target_pairs={{1,0},{2,1},{3,2},{4,3},{5,4},{6,5},{7,6},{8,7},{9,8},{10,9},{11,1... | collective-permute-start | bytes 1179656 | tf_op jit(solution)/shard_map/ppermute | solution.py:19
  39.9 4.2 %collective-permute-start.9 = (bf16[4,1,128,384]{3,2,0,1:T(8,128)(2,1)S(1)}, bf16[4,1,128,384]{3,2,0,1:T(8,128)(2,1)S(1)}, u32[]{:S(2)}, u32[]{:S(2)}) collective-permute-start(bf16[4,1,128,384]{3,2,0,1:T(8,128)(2,1)S(1)} %pad_maximum_fusion.4), channel_id=1, source_target_pairs={{0,1},{1,2},{2,3},{3,4},{4,5},{5,6},{6,7},{7,8},{8,9},{9,10},{10,1... | collective-permute-start | bytes 1179656 | tf_op jit(solution)/shard_map/ppermute | solution.py:18
  44.1 3.9 %fusion.164 = (bf16[1,1,3,384,384]{4,3,2,1,0:T(8,128)(2,1)S(1)}, bf16[1,1,3,384,384]{4,3,2,1,0:T(8,128)(2,1)S(1)}, bf16[1,1,3,384,384]{4,3,2,1,0:T(8,128)(2,1)S(...) fusion(bf16[3,3,3,384,384]{4,3,2,1,0:T(8,128)(2,1)} %param.17), kind=kLoop, calls=%fused_computation.234 | loop fusion | bytes 15925248 | tf_op jit(solution)/shard_map/slice | solution.py:94
  48.1 0.7 collective-permute-done.9
  49.2 0.7 fusion.168
  53.8 0.5 fusion.141
  54.3 5.3 %collective-permute-start.11 = (bf16[2,1,128,384]{3,2,0,1:T(8,128)(2,1)S(1)}, bf16[2,1,128,384]{3,2,0,1:T(8,128)(2,1)S(1)}, u32[]{:S(2)}, u32[]{:S(2)}) collective-permute-start(bf16[2,1,128,384]{3,2,0,1:T(8,128)(2,1)S(1)} %fusion.141), channel_id=1, source_target_pairs={{0,1},{1,2},{2,3},{3,4},{4,5},{5,6},{6,7},{7,8},{8,9},{9,10},{10,1... | collective-permute-start | bytes 589832 | tf_op jit(solution)/shard_map/ppermute | solution.py:18
  59.7 2.3 %collective-permute-start.12 = (bf16[2,1,128,384]{3,2,0,1:T(8,128)(2,1)S(1)}, bf16[2,1,128,384]{3,2,0,1:T(8,128)(2,1)S(1)}, u32[]{:S(2)}, u32[]{:S(2)}) collective-permute-start(bf16[2,1,128,384]{3,2,0,1:T(8,128)(2,1)S(1)} %fusion.141), channel_id=1, source_target_pairs={{1,0},{2,1},{3,2},{4,3},{5,4},{6,5},{7,6},{8,7},{9,8},{10,9},{11,1... | collective-permute-start | bytes 589832 | tf_op jit(solution)/shard_map/ppermute | solution.py:19
  62.6 1.1 %reshape.290 = bf16[1152,192,1,1]{0,1,2,3:T(8,128)(2,1)} reshape(bf16[1,1,3,384,192]{3,2,4,1,0:T(4,128)(2,1)S(1)} %copy.34) | data formatting | bytes 884736 | tf_op jit(solution)/shard_map/reshape;squeeze | solution.py:94
  65.3 2.3 %collective-permute-done.12 = bf16[2,1,128,384]{3,2,0,1:T(8,128)(2,1)S(1)} collective-permute-done((bf16[2,1,128,384]{3,2,0,1:T(8,128)(2,1)S(1)}, bf16[2,1,128,384]{3,2,0,1:T(8,128)(2,1)S(1)}, u32[]{:S(2)}, u32[]{:S(2)}) %collective-permute-start.12) | collective-permute-done | bytes 196640 | tf_op jit(solution)/shard_map/ppermute | solution.py:19
  67.7 0.6 broadcast_in_dim.4
  68.4 0.5 reshape.278
  69.0 0.8 pad_slice_fusion.9
  70.1 0.7 copy-done.6
  70.8 1.1 %fusion.6 = f32[2,2,256,192]{2,3,1,0:T(8,128)S(1)} fusion(bf16[2,1,258,384]{3,2,1,0:T(8,128)(2,1)S(1)} %pad_slice_fusion.10, bf16[2,2,256,384]{3,2,1,0:T(8,128)(2,1)S(1)} %get-tuple-element.81, bf16[2,2,256,384]{3,2,1,0:T(8,128)(2,1)S(1)} %get-tuple-element.80, bf16[1152,192,1,1]{0,1,2,3:T(8,128)(2,1)S(1)} %copy-done.6), kind=kOutput, calls=%fused_computation.13 | convolution fusion | flops 462422016 | bytes 3197952 | tf_op jit(solution)/shard_map/fhwc,cd->fhwd/dot_general | solution.py:95
  71.9 1.1 %fusion.28 = f32[2,2,256,192]{2,3,1,0:T(8,128)S(1)} fusion(f32[2,2,256,192]{2,3,1,0:T(8,128)S(1)} %fusion.6, bf16[2,2,256,384]{3,2,1,0:T(8,128)(2,1)S(1)} %get-tuple-element.71, bf16[2,2,256,384]{3,2,1,0:T(8,128)(2,1)S(1)} %get-tuple-element.74, bf16[2,2,256,384]{3,2,1,0:T(8,128)(2,1)S(1)} %get-tuple-element.75, bf16[1152,192,1,1]{0,1,2,3:T(8,128)(2,1)S(1)} %reshape.289), kind=kOutput, calls=%fused_computation.40 | convolution fusion | flops 460259328 | bytes 4374528 | tf_op jit(solution)/shard_map/fhwc,cd->fhwd/dot_general | solution.py:95
  73.1 1.2 %multiply_reduce_fusion = (f32[2,2,256]{2,1,0:T(2,128)S(1)}, f32[2,2,256,192]{2,3,1,0:T(8,128)S(1)}) fusion(f32[2,2,256,192]{2,3,1,0:T(8,128)S(1)} %fusion.28, bf16[1152,192,1,1]{0,1,2,3:T(8,128)(2,1)S(1)} %reshape.291, bf16[2,2,256,384]{3,2,1,0:T(8,128)(2,1)S(1)} %get-tuple-element.72, bf16[2,2,256,384]{3,2,1,0:T(8,128)(2,1)S(1)} %get-tuple-element.73, ...), kind=kOutput, calls=%fused_computation.119 | convolution fusion | flops 461044736 | bytes 4378624 | tf_op jit(solution)/shard_map/fhwc,cd->fhwd/dot_general | solution.py:95
  74.6 2.1 %collective-permute-start.13 = (bf16[4,1,256,192]{2,3,1,0:T(8,128)(2,1)S(1)}, bf16[4,1,256,192]{2,3,1,0:T(8,128)(2,1)S(1)}, u32[]{:S(2)}, u32[]{:S(2)}) collective-permute-start(bf16[4,1,256,192]{2,3,1,0:T(8,128)(2,1)S(1)} %get-tuple-element.78), channel_id=1, source_target_pairs={{0,1},{1,2},{2,3},{3,4},{4,5},{5,6},{6,7},{7,8},{8,9},{9,10},{10,1... | collective-permute-start | bytes 1179656 | tf_op jit(solution)/shard_map/ppermute | solution.py:18
  76.8 2.5 %collective-permute-start.14 = (bf16[4,1,256,192]{2,3,1,0:T(8,128)(2,1)S(1)}, bf16[4,1,256,192]{2,3,1,0:T(8,128)(2,1)S(1)}, u32[]{:S(2)}, u32[]{:S(2)}) collective-permute-start(bf16[4,1,256,192]{2,3,1,0:T(8,128)(2,1)S(1)} %get-tuple-element.79), channel_id=1, source_target_pairs={{1,0},{2,1},{3,2},{4,3},{5,4},{6,5},{7,6},{8,7},{9,8},{10,9},{11,1... | collective-permute-start | bytes 1179656 | tf_op jit(solution)/shard_map/ppermute | solution.py:19
  79.5 2.0 %collective-permute-done.13 = bf16[4,1,256,192]{2,3,1,0:T(8,128)(2,1)S(1)} collective-permute-done((bf16[4,1,256,192]{2,3,1,0:T(8,128)(2,1)S(1)}, bf16[4,1,256,192]{2,3,1,0:T(8,128)(2,1)S(1)}, u32[]{:S(2)}, u32[]{:S(2)}) %collective-permute-start.13) | collective-permute-done | bytes 393248 | tf_op jit(solution)/shard_map/ppermute | solution.py:18
  81.5 5.3 %collective-permute-done.14 = bf16[4,1,256,192]{2,3,1,0:T(8,128)(2,1)S(1)} collective-permute-done((bf16[4,1,256,192]{2,3,1,0:T(8,128)(2,1)S(1)}, bf16[4,1,256,192]{2,3,1,0:T(8,128)(2,1)S(1)}, u32[]{:S(2)}, u32[]{:S(2)}) %collective-permute-start.14) | collective-permute-done | bytes 393248 | tf_op jit(solution)/shard_map/ppermute | solution.py:19
  86.8 2.0 %select_maximum_fusion = bf16[4,4,258,192]{2,3,1,0:T(8,128)(2,1)S(1)} fusion(bf16[4,1,256,192]{2,3,1,0:T(8,128)(2,1)S(1)} %collective-permute-done.14, bf16[4,1,256,192]{2,3,1,0:T(8,128)(2,1)S(1)} %collective-permute-done.13, bf16[2,2,256,192]{2,3,1,0:T(8,128)(2,1)S(1)} %multiply_convert_fusion, bf16[2,2,256,192]{2,3,1,0:T(8,128)(2,1)S(1)} %copy-done.2), kind=kLoop, calls=%fused_computation.6 | loop fusion | flops 11888640 | bytes 3158016 | tf_op jit(solution)/shard_map/concatenate | solution.py:25
  88.8 1.7 %fusion.166 = (bf16[2,2,256,192]{2,3,1,0:T(8,128)(2,1)S(1)}, bf16[2,2,256,192]{2,3,1,0:T(8,128)(2,1)S(1)}, bf16[2,2,256,192]{2,3,1,0:T(8,128)(2,1)S(1)}, bf16[2,...) fusion(bf16[4,4,258,192]{2,3,1,0:T(8,128)(2,1)S(1)} %select_max, ...), kind=kLoop, calls=%fused_computation.236 | loop fusion | bytes 14155776 | tf_op jit(solution)/shard_map/slice | solution.py:92
  90.9 0.5 fusion.50
  91.4 0.5 convolution_add_fusion.7
  91.9 0.5 convolution_add_fusion.6
  92.5 0.5 convolution_add_fusion.5
  93.0 0.5 convolution_add_fusion.4
  93.5 0.5 convolution_add_fusion.3
  94.0 0.5 convolution_add_fusion.2
  94.6 0.5 convolution_add_fusion.1
  95.1 1.3 %fusion.40 = bf16[2,2,256,192]{2,3,1,0:T(8,128)(2,1)} fusion(f32[2,2,256,192]{2,3,1,0:T(8,128)S(1)} %get-tuple-element.93, f32[2,2,256,192]{2,3,1,0:T(8,128)S(1)} %convolution_add_fusion.1, bf16[576,192,1,1]{1,0,3,2:T(8,128)(2,1)S(1)} %bitcast.157, bf16[2,2,256,192]{2,3,1,0:T(8,128)(2,1)S(1)} %get-tuple-element.42, ...), kind=kOutput, calls=%fused_computation.48 | convolution fusion | flops 230621184 | bytes 3366912 | tf_op jit(solution)/shard_map/fhwc,cd->fhwd/dot_general | solution.py:95
  (69 shorter events, 9.4 us)
Async XLA Ops:
  0.0 4.5 %copy-start = (bf16[384,384]{1,0:T(8,128)(2,1)S(1)}, bf16[384,384]{1,0:T(8,128)(2,1)}, u32[]{:S(2)}) copy-start(bf16[384,384]{1,0:T(8,128)(2,1)} %param.13) | copy-start | bytes 884740
  1.0 1.7 %collective-permute-start = (bf16[1,1,128,384]{3,2,1,0:T(8,128)(2,1)S(1)}, bf16[1,1,128,384]{3,2,1,0:T(8,128)(2,1)S(1)}, u32[]{:S(2)}, u32[]{:S(2)}) collective-permute-start(bf16[1,1,128,384]{3,2,1,0:T(8,128)(2,1)S(1)} %get-tuple-element.91), channel_id=1, source_target_pairs={{0,1},{1,0},{2,3},{3,2},{4,5},{5,4},{6,7},{7,6},{8,9},{9,8},{10,11... | collective-permute-start | bytes 294920 | tf_op jit(solution)/shard_map/ppermute | solution.py:172
  2.7 16.1 %copy-start.7 = (bf16[1,2,128,384]{3,2,1,0:T(8,128)(2,1)}, bf16[1,2,128,384]{3,2,1,0:T(8,128)(2,1)S(1)}, u32[]{:S(2)}) copy-start(bf16[1,2,128,384]{3,2,1,0:T(8,128)(2,1)S(1)} %pad_maximum_fusion.5) | copy-start | bytes 589828
  2.7 6.2 %collective-permute-start.1 = (bf16[1,2,128,384]{3,2,1,0:T(8,128)(2,1)S(1)}, bf16[1,2,128,384]{3,2,1,0:T(8,128)(2,1)S(1)}, u32[]{:S(2)}, u32[]{:S(2)}) collective-permute-start(bf16[1,2,128,384]{3,2,1,0:T(8,128)(2,1)S(1)} %pad_maximum_fusion.5), channel_id=1, source_target_pairs={{0,4},{1,5},{2,0},{3,1},{4,8},{5,9},{6,2},{7,3},{8,12},{9,13},{10,... | collective-permute-start | bytes 589832 | tf_op jit(solution)/shard_map/ppermute | solution.py:47
  3.0 6.1 %collective-permute-start.2 = (bf16[1,2,128,384]{3,2,1,0:T(8,128)(2,1)S(1)}, bf16[1,2,128,384]{3,2,1,0:T(8,128)(2,1)S(1)}, u32[]{:S(2)}, u32[]{:S(2)}) collective-permute-start(bf16[1,2,128,384]{3,2,1,0:T(8,128)(2,1)S(1)} %pad_maximum_fusion.5), channel_id=1, source_target_pairs={{0,2},{1,3},{2,6},{3,7},{4,0},{5,1},{6,10},{7,11},{8,4},{9,5},{10,... | collective-permute-start | bytes 589832 | tf_op jit(solution)/shard_map/ppermute | solution.py:50
  8.9 5.2 %collective-permute-start.3 = (bf16[1,2,128,384]{3,2,1,0:T(8,128)(2,1)S(1)}, bf16[1,2,128,384]{3,2,1,0:T(8,128)(2,1)S(1)}, u32[]{:S(2)}, u32[]{:S(2)}) collective-permute-start(bf16[1,2,128,384]{3,2,1,0:T(8,128)(2,1)S(1)} %collective-permute-done.1), channel_id=1, source_target_pairs={{0,4},{1,5},{2,0},{3,1},{4,8},{5,9},{6,2},{7,3},{8,12},{9,13},{10,... | collective-permute-start | bytes 589832 | tf_op jit(solution)/shard_map/ppermute | solution.py:47
  9.1 5.2 %collective-permute-start.4 = (bf16[1,2,128,384]{3,2,1,0:T(8,128)(2,1)S(1)}, bf16[1,2,128,384]{3,2,1,0:T(8,128)(2,1)S(1)}, u32[]{:S(2)}, u32[]{:S(2)}) collective-permute-start(bf16[1,2,128,384]{3,2,1,0:T(8,128)(2,1)S(1)} %collective-permute-done.2), channel_id=1, source_target_pairs={{0,2},{1,3},{2,6},{3,7},{4,0},{5,1},{6,10},{7,11},{8,4},{9,5},{10,... | collective-permute-start | bytes 589832 | tf_op jit(solution)/shard_map/ppermute | solution.py:50
  14.1 4.5 %collective-permute-start.5 = (bf16[1,2,128,384]{3,2,1,0:T(8,128)(2,1)S(1)}, bf16[1,2,128,384]{3,2,1,0:T(8,128)(2,1)S(1)}, u32[]{:S(2)}, u32[]{:S(2)}) collective-permute-start(bf16[1,2,128,384]{3,2,1,0:T(8,128)(2,1)S(1)} %collective-permute-done.3), channel_id=1, source_target_pairs={{0,4},{1,5},{2,0},{3,1},{4,8},{5,9},{6,2},{7,3},{8,12},{9,13},{10,... | collective-permute-start | bytes 589832 | tf_op jit(solution)/shard_map/ppermute | solution.py:47
  14.3 4.6 %collective-permute-start.6 = (bf16[1,2,128,384]{3,2,1,0:T(8,128)(2,1)S(1)}, bf16[1,2,128,384]{3,2,1,0:T(8,128)(2,1)S(1)}, u32[]{:S(2)}, u32[]{:S(2)}) collective-permute-start(bf16[1,2,128,384]{3,2,1,0:T(8,128)(2,1)S(1)} %collective-permute-done.4), channel_id=1, source_target_pairs={{0,2},{1,3},{2,6},{3,7},{4,0},{5,1},{6,10},{7,11},{8,4},{9,5},{10,... | collective-permute-start | bytes 589832 | tf_op jit(solution)/shard_map/ppermute | solution.py:50
  18.7 4.7 %collective-permute-start.7 = (bf16[1,2,128,384]{3,2,1,0:T(8,128)(2,1)S(1)}, bf16[1,2,128,384]{3,2,1,0:T(8,128)(2,1)S(1)}, u32[]{:S(2)}, u32[]{:S(2)}) collective-permute-start(bf16[1,2,128,384]{3,2,1,0:T(8,128)(2,1)S(1)} %collective-permute-done.5), channel_id=1, source_target_pairs={{0,4},{1,5},{2,0},{3,1},{4,8},{5,9},{6,2},{7,3},{8,12},{9,13},{10,... | collective-permute-start | bytes 589832 | tf_op jit(solution)/shard_map/ppermute | solution.py:47
  23.4 1.2 %copy-start.8 = (bf16[1,16,128,384]{3,2,1,0:T(8,128)(2,1)}, bf16[1,16,128,384]{3,2,1,0:T(8,128)(2,1)S(1)}, u32[]{:S(2)}) copy-start(bf16[1,16,128,384]{3,2,1,0:T(8,128)(2,1)S(1)} %constant_dynamic-update-slice_fusion) | copy-start | bytes 4718596
  24.6 13.0 %copy-start.4 = (bf16[2,1,128,384]{3,2,1,0:T(8,128)(2,1)S(1)}, bf16[2,1,128,384]{3,2,1,0:T(8,128)(2,1)}, u32[]{:S(2)}) copy-start(bf16[2,1,128,384]{3,2,1,0:T(8,128)(2,1)} %param.11) | copy-start | bytes 589828
  31.9 5.3 %collective-permute-start.8 = (bf16[1,1,128,384]{3,2,0,1:T(8,128)(2,1)S(1)}, bf16[1,1,128,384]{3,2,0,1:T(8,128)(2,1)S(1)}, u32[]{:S(2)}, u32[]{:S(2)}) collective-permute-start(bf16[1,1,128,384]{3,2,0,1:T(8,128)(2,1)S(1)} %get-tuple-element.90), channel_id=1, source_target_pairs={{0,1},{1,0},{2,3},{3,2},{4,5},{5,4},{6,7},{7,6},{8,9},{9,8},{10,11... | collective-permute-start | bytes 294920 | tf_op jit(solution)/shard_map/ppermute | solution.py:188
  37.6 10.5 %collective-permute-start.10 = (bf16[4,1,128,384]{3,2,0,1:T(8,128)(2,1)S(1)}, bf16[4,1,128,384]{3,2,0,1:T(8,128)(2,1)S(1)}, u32[]{:S(2)}, u32[]{:S(2)}) collective-permute-start(bf16[4,1,128,384]{3,2,0,1:T(8,128)(2,1)S(1)} %pad_maximum_fusion.4), channel_id=1, source_target_pairs={{1,0},{2,1},{3,2},{4,3},{5,4},{6,5},{7,6},{8,7},{9,8},{10,9},{11,1... | collective-permute-start | bytes 1179656 | tf_op jit(solution)/shard_map/ppermute | solution.py:19
  39.9 8.9 %collective-permute-start.9 = (bf16[4,1,128,384]{3,2,0,1:T(8,128)(2,1)S(1)}, bf16[4,1,128,384]{3,2,0,1:T(8,128)(2,1)S(1)}, u32[]{:S(2)}, u32[]{:S(2)}) collective-permute-start(bf16[4,1,128,384]{3,2,0,1:T(8,128)(2,1)S(1)} %pad_maximum_fusion.4), channel_id=1, source_target_pairs={{0,1},{1,2},{2,3},{3,4},{4,5},{5,6},{6,7},{7,8},{8,9},{9,10},{10,1... | collective-permute-start | bytes 1179656 | tf_op jit(solution)/shard_map/ppermute | solution.py:18
  53.8 8.2 %copy-start.5 = (bf16[3,3,384,192]{2,3,1,0:T(8,128)(2,1)S(1)}, bf16[3,3,384,192]{2,3,1,0:T(8,128)(2,1)}, u32[]{:S(2)}) copy-start(bf16[3,3,384,192]{2,3,1,0:T(8,128)(2,1)} %param.18) | copy-start | bytes 3981316
  54.3 10.9 %collective-permute-start.11 = (bf16[2,1,128,384]{3,2,0,1:T(8,128)(2,1)S(1)}, bf16[2,1,128,384]{3,2,0,1:T(8,128)(2,1)S(1)}, u32[]{:S(2)}, u32[]{:S(2)}) collective-permute-start(bf16[2,1,128,384]{3,2,0,1:T(8,128)(2,1)S(1)} %fusion.141), channel_id=1, source_target_pairs={{0,1},{1,2},{2,3},{3,4},{4,5},{5,6},{6,7},{7,8},{8,9},{9,10},{10,1... | collective-permute-start | bytes 589832 | tf_op jit(solution)/shard_map/ppermute | solution.py:18
  59.7 7.9 %collective-permute-start.12 = (bf16[2,1,128,384]{3,2,0,1:T(8,128)(2,1)S(1)}, bf16[2,1,128,384]{3,2,0,1:T(8,128)(2,1)S(1)}, u32[]{:S(2)}, u32[]{:S(2)}) collective-permute-start(bf16[2,1,128,384]{3,2,0,1:T(8,128)(2,1)S(1)} %fusion.141), channel_id=1, source_target_pairs={{1,0},{2,1},{3,2},{4,3},{5,4},{6,5},{7,6},{8,7},{9,8},{10,9},{11,1... | collective-permute-start | bytes 589832 | tf_op jit(solution)/shard_map/ppermute | solution.py:19
  69.8 1.0 %copy-start.6 = (bf16[1152,192,1,1]{0,1,2,3:T(8,128)(2,1)S(1)}, bf16[1152,192,1,1]{0,1,2,3:T(8,128)(2,1)}, u32[]{:S(2)}) copy-start(bf16[1152,192,1,1]{0,1,2,3:T(8,128)(2,1)} %reshape.290) | copy-start | bytes 1327108
  73.1 1.4 %copy-start.2 = (bf16[2,2,256,192]{2,3,1,0:T(8,128)(2,1)S(1)}, bf16[2,2,256,192]{2,3,1,0:T(8,128)(2,1)}, u32[]{:S(2)}) copy-start(bf16[2,2,256,192]{2,3,1,0:T(8,128)(2,1)} %param.12) | copy-start | bytes 1179652
  74.3 5.0 %copy-start.3 = (bf16[3,3,3,192,192]{4,3,2,1,0:T(8,128)(2,1)S(1)}, bf16[3,3,3,192,192]{4,3,2,1,0:T(8,128)(2,1)}, u32[]{:S(2)}) copy-start(bf16[3,3,3,192,192]{4,3,2,1,0:T(8,128)(2,1)} %param.19) | copy-start | bytes 5971972
  74.6 6.9 %collective-permute-start.13 = (bf16[4,1,256,192]{2,3,1,0:T(8,128)(2,1)S(1)}, bf16[4,1,256,192]{2,3,1,0:T(8,128)(2,1)S(1)}, u32[]{:S(2)}, u32[]{:S(2)}) collective-permute-start(bf16[4,1,256,192]{2,3,1,0:T(8,128)(2,1)S(1)} %get-tuple-element.78), channel_id=1, source_target_pairs={{0,1},{1,2},{2,3},{3,4},{4,5},{5,6},{6,7},{7,8},{8,9},{9,10},{10,1... | collective-permute-start | bytes 1179656 | tf_op jit(solution)/shard_map/ppermute | solution.py:18
  76.8 10.0 %collective-permute-start.14 = (bf16[4,1,256,192]{2,3,1,0:T(8,128)(2,1)S(1)}, bf16[4,1,256,192]{2,3,1,0:T(8,128)(2,1)S(1)}, u32[]{:S(2)}, u32[]{:S(2)}) collective-permute-start(bf16[4,1,256,192]{2,3,1,0:T(8,128)(2,1)S(1)} %get-tuple-element.79), channel_id=1, source_target_pairs={{1,0},{2,1},{3,2},{4,3},{5,4},{6,5},{7,6},{8,7},{9,8},{10,9},{11,1... | collective-permute-start | bytes 1179656 | tf_op jit(solution)/shard_map/ppermute | solution.py:19
  95.1 1.3 %copy-start.1 = (bf16[384,384]{1,0:T(8,128)(2,1)S(1)}, bf16[384,384]{1,0:T(8,128)(2,1)}, u32[]{:S(2)}) copy-start(bf16[384,384]{1,0:T(8,128)(2,1)} %param.13) | copy-start | bytes 884740

commit v16 on v15

--- a/solution.py
+++ b/solution.py
@@ -145,6 +145,33 @@
     )(queries, all_rows, w_key, w_value, residual, w_output)
 
 
+def conv_frames(padded, weight):
+    frames, height, width, channels = padded.shape
+    cols = jnp.pad(padded, ((0, 0), (0, 0), (1, 1), (0, 0)))
+    result = None
+    for row_off in range(3):
+        window = cols[:, row_off : row_off + height - 2]
+        stacked = jnp.concatenate([window[:, :, c : c + width] for c in range(3)], axis=-1)
+        kernel = weight[row_off].reshape(3 * channels, weight.shape[-1])
+        term = jnp.einsum("fhwc,cd->fhwd", stacked, kernel, preferred_element_type=jnp.float32)
+        result = term if result is None else result + term
+    return result
+
+
+def cached_terms(cache_pad, weight):
+    late = conv_frames(cache_pad[1:2], weight[1])
+    return conv_frames(cache_pad, weight[0]) + jnp.concatenate(
+        [late, jnp.zeros_like(late)], axis=0
+    )
+
+
+def new_terms(new_pad, weight):
+    early = conv_frames(new_pad[0:1], weight[1])
+    return conv_frames(new_pad, weight[2]) + jnp.concatenate(
+        [jnp.zeros_like(early), early], axis=0
+    )
+
+
 def project_rows(tokens, weight):
     return jnp.einsum("ftc,cd->ftd", tokens, weight, preferred_element_type=jnp.float32).astype(
         jnp.bfloat16
@@ -164,6 +191,8 @@
     w_second,
 ):
     frame_count, row_count, width_count, channels = features.shape
+    first_cached = cached_terms(extended(first_cache, 1, 1), w_first)
+    second_cached = cached_terms(extended(second_cache, 1, 1), w_second)
     core = lax.axis_index("ha") % 2
     count = lax.axis_size("ha")
     swap = [(i, i ^ 1) for i in range(count)]
@@ -193,22 +222,16 @@
         jnp.concatenate([back, own], axis=0),
     )
     first_in = jax.nn.silu(rms_scale(mixed)).astype(jnp.bfloat16)
-    first_stack = jnp.concatenate([first_cache, first_in], axis=0)
-    first_padded = extended(first_stack, 1, 1)
-    block_out = (mixed.astype(jnp.float32) + conv_taps(first_padded, w_first, 3)).astype(
-        jnp.bfloat16
-    )
+    first_new = new_terms(extended(first_in, 1, 1), w_first)
+    block_out = (mixed.astype(jnp.float32) + first_cached + first_new).astype(jnp.bfloat16)
     block_padded = extended(block_out, 1, 1)
     widened = jnp.repeat(block_padded, 2, axis=2)
     upsampled = conv_taps(widened, w_upsample[None], 1, rows=((0, 1), (1, 1), (1, 2))).astype(
         jnp.bfloat16
     )
     second_in = jax.nn.silu(rms_scale(upsampled)).astype(jnp.bfloat16)
-    second_stack = jnp.concatenate([second_cache, second_in], axis=0)
-    second_padded = extended(second_stack, 1, 1)
-    return (upsampled.astype(jnp.float32) + conv_taps(second_padded, w_second, 3)).astype(
-        jnp.bfloat16
-    )
+    second_new = new_terms(extended(second_in, 1, 1), w_second)
+    return (upsampled.astype(jnp.float32) + second_cached + second_new).astype(jnp.bfloat16)
 
 
 def solution(mesh):

time: 97.2 us -> 131 us (1.35)
  local copies, waits for them, and re-layouts: 16.2 us -> 39.4 us
  starting transfers between devices: 28.6 us -> 35.5 us
  matrix products: 14.2 us -> 19 us
  waiting for transfers between devices: 26.7 us -> 24.8 us
    slice x1 -> x30, local copies, waits for them, and re-layouts: 0.97 us -> 18.5 us  [the longest x20 8.05 us: conv_frames(): window[:, :, c:c + width]]
    dot_general x0 -> x24, matrix products: none -> 14.5 us  [conv_frames(): jnp.einsum('fhwc,cd->fhwd', stacked, kernel, preferred_element_type=jnp.f...]
    unnamed x26 -> x96, local copies, waits for them, and re-layouts: 3.16 us -> 13.1 us
    dot_general x21 -> x3, matrix products: 13.2 us -> 3.48 us  [conv_taps(): jnp.einsum('fhwc,cd->fhwd', stacked, kernel, preferred_element_type=jnp.f...]
    ppermute x3 -> x5, waiting for transfers between devices: 7.65 us -> 13 us  [halo_rows(): after = lax.ppermute(first, 'ha', down)]
    ppermute x3 -> x5, starting transfers between devices: 7.14 us -> 11.6 us  [halo_rows(): after = lax.ppermute(first, 'ha', down)]
    slice x6 -> x4, local copies, waits for them, and re-layouts: 5.41 us -> 1.28 us  [conv_taps(): kernel = weight[time_off, row_off].reshape(3 * in_channels, out_channels)]
    ppermute x4, waiting for transfers between devices: 14.5 us -> 10.8 us  [gather_chip_rows(): ahead = lax.ppermute(ahead, 'ha', forward)]
  transfers between devices with their start and end apart: 15 -> 19, of which waited for: 10 -> 8; matrix products, arithmetic and copies ran while one was open for 9% -> 27% of each run, Pallas kernels for 0% -> 0%
where the time goes in v16:
time: 131 us; the launch traced here: 129 us
  local copies, waits for them, and re-layouts  39.4 us (30%)
  starting transfers between devices  35.5 us (27%)
  waiting for transfers between devices  24.8 us (19%)
  matrix products  19 us (15%)
  Pallas kernels  6.28 us (5%)
  other arithmetic  3.34 us (3%)
    dot_general x24, matrix products, conv_frames(): jnp.einsum('fhwc,cd->fhwd', stacked, kernel, preferred_element_type=jnp.f...  14.5 us
    ppermute x5, starting transfers between devices, halo_rows(): before = lax.ppermute(last, 'ha', up)  13.5 us
    unnamed x96, local copies, waits for them, and re-layouts  13.1 us
    ppermute x5, waiting for transfers between devices, halo_rows(): after = lax.ppermute(first, 'ha', down)  13 us
    ppermute x5, starting transfers between devices, halo_rows(): after = lax.ppermute(first, 'ha', down)  11.6 us
    ppermute x4, waiting for transfers between devices, gather_chip_rows(): ahead = lax.ppermute(ahead, 'ha', forward)  10.8 us
    slice x20, local copies, waits for them, and re-layouts, conv_frames(): window[:, :, c:c + width]  8.05 us
    slice x2, local copies, waits for them, and re-layouts, conv_frames(): kernel = weight[row_off].reshape(3 * channels, weight.shape[-1])  7.29 us
  transfers between devices with their start and end apart: 19, of which 8 were waited for; matrix products, arithmetic and copies ran while one was open for 27% of the time, Pallas kernels for 0%

profile of v16, /device:TPU:13, one launch (start us, length us, event | category | flops | bytes accessed | tf_op | source)
XLA Modules:
  0.0 129.3 jit_solution(13023948112917270441)
XLA Ops:
  0.0 2.7 %collective-permute-start.10 = (bf16[2,1,128,384]{3,2,0,1:T(8,128)(2,1)}, bf16[2,1,128,384]{3,2,0,1:T(8,128)(2,1)}, u32[]{:S(2)}, u32[]{:S(2)}) collective-permute-start(bf16[2,1,128,384]{3,2,0,1:T(8,128)(2,1)} %bitcast.203), channel_id=1, source_target_pairs={{1,0},{2,1},{3,2},{4,3},{5,4},{6,5},{7,6},{8,7},{9,8},{10,9},{11,1... | collective-permute-start | bytes 589832 | tf_op jit(solution)/shard_map/ppermute | solution.py:19
  2.7 3.9 %collective-permute-start.9 = (bf16[2,1,128,384]{3,2,0,1:T(8,128)(2,1)}, bf16[2,1,128,384]{3,2,0,1:T(8,128)(2,1)}, u32[]{:S(2)}, u32[]{:S(2)}) collective-permute-start(bf16[2,1,128,384]{3,2,0,1:T(8,128)(2,1)} %bitcast.204), channel_id=1, source_target_pairs={{0,1},{1,2},{2,3},{3,4},{4,5},{5,6},{6,7},{7,8},{8,9},{9,10},{10,1... | collective-permute-start | bytes 589832 | tf_op jit(solution)/shard_map/ppermute | solution.py:18
  6.6 1.6 %constant_dynamic-update-slice_fusion.8 = (bf16[1,16,128,384]{3,2,1,0:T(8,128)(2,1)}, bf16[1,1,128,384]{3,2,1,0:T(8,128)(2,1)S(1)}, bf16[1,1,128,384]{3,2,1,0:T(8,128)(2,1)}) fusion(bf16[2,1,128,384]{3,2,1,0:T(8,128)(2,1)} %param.10, s32[]{:T(128)S(6)} %select_n.39, s32[]{:T(128)S(6)} %select_n.40), kind=kLoop, calls=%fused_computation.285 | loop fusion | bytes 491528
  8.3 1.8 %fusion.210 = (bf16[2,1,256,192]{2,3,1,0:T(8,128)(2,1)}, bf16[2,1,256,192]{2,3,1,0:T(8,128)(2,1)}) fusion(bf16[2,2,256,192]{2,3,1,0:T(8,128)(2,1)} %param.12), kind=kLoop, calls=%fused_computation.329 | loop fusion | bytes 786432 | tf_op jit(solution)/shard_map/slice | solution.py:17
  10.1 2.7 %collective-permute-start.15 = (bf16[2,1,256,192]{2,3,1,0:T(8,128)(2,1)}, bf16[2,1,256,192]{2,3,1,0:T(8,128)(2,1)}, u32[]{:S(2)}, u32[]{:S(2)}) collective-permute-start(bf16[2,1,256,192]{2,3,1,0:T(8,128)(2,1)} %get-tuple-element.80), channel_id=1, source_target_pairs={{0,1},{1,2},{2,3},{3,4},{4,5},{5,6},{6,7},{7,8},{8,9},{9,10},{10,1... | collective-permute-start | bytes 589832 | tf_op jit(solution)/shard_map/ppermute | solution.py:18
  12.8 1.9 %collective-permute-start.16 = (bf16[2,1,256,192]{2,3,1,0:T(8,128)(2,1)}, bf16[2,1,256,192]{2,3,1,0:T(8,128)(2,1)}, u32[]{:S(2)}, u32[]{:S(2)}) collective-permute-start(bf16[2,1,256,192]{2,3,1,0:T(8,128)(2,1)} %get-tuple-element.79), channel_id=1, source_target_pairs={{1,0},{2,1},{3,2},{4,3},{5,4},{6,5},{7,6},{8,7},{9,8},{10,9},{11,1... | collective-permute-start | bytes 589832 | tf_op jit(solution)/shard_map/ppermute | solution.py:19
  14.7 5.8 %fusion.206 = (bf16[1,1,3,384,384]{4,3,2,1,0:T(8,128)(2,1)S(1)}, bf16[1,1,3,384,384]{4,3,2,1,0:T(8,128)(2,1)}, bf16[1,1,3,384,384]{4,3,2,1,0:T(8,128)(2,1)}, bf1...) fusion(bf16[3,3,3,384,384]{4,3,2,1,0:T(8,128)(2,1)} %param.17), kind=kLoop, calls=%fused_computation.325 | loop fusion | bytes 15925248 | tf_op jit(solution)/shard_map/slice | solution.py:155
  20.5 1.5 %fusion.207 = (bf16[1,1,3,192,192]{4,3,2,1,0:T(8,128)(2,1)}, bf16[1,1,3,192,192]{4,3,2,1,0:T(8,128)(2,1)}, bf16[1,1,3,192,192]{4,3,2,1,0:T(8,128)(2,1)}, bf16[1,...) fusion(bf16[3,3,3,192,192]{4,3,2,1,0:T(8,128)(2,1)S(1)} %copy-d, ...), kind=kLoop, calls=%fused_computation.326 | loop fusion | bytes 3981312 | tf_op jit(solution)/shard_map/slice | solution.py:155
  24.7 1.2 reshape.402
  26.3 1.2 reshape.401
  27.8 1.1 reshape.403
  30.1 1.0 fusion.77.q_ref
  31.1 1.3 %collective-permute-start.2 = (bf16[1,2,128,384]{3,2,1,0:T(8,128)(2,1)S(1)}, bf16[1,2,128,384]{3,2,1,0:T(8,128)(2,1)S(1)}, u32[]{:S(2)}, u32[]{:S(2)}) collective-permute-start(bf16[1,2,128,384]{3,2,1,0:T(8,128)(2,1)S(1)} %pad_maximum_fusion.7), channel_id=1, source_target_pairs={{0,2},{1,3},{2,6},{3,7},{4,0},{5,1},{6,10},{7,11},{8,4},{9,5},{10,... | collective-permute-start | bytes 589832 | tf_op jit(solution)/shard_map/ppermute | solution.py:50
  32.4 1.1 pad_maximum_fusion.4
  33.5 1.0 pad_slice_fusion.44
  34.5 1.0 constant_dynamic-update-slice_fusion.13
  35.6 1.0 constant_dynamic-update-slice_fusion.14
  36.6 1.7 %pad_slice_fusion.7 = (bf16[2,2,256,192]{2,3,1,0:T(8,128)(2,1)}, bf16[2,2,256,192]{2,3,1,0:T(8,128)(2,1)S(1)}, bf16[2,2,256,192]{2,3,1,0:T(8,128)(2,1)S(1)}, bf1...) fusion(bf16[2,4,256,192]{2,3,1,0:T(8,128)(2,1)S(1)} %get-tuple-element.94), kind=kLoop, calls=%fused_computation.26 | loop fusion | bytes 3145728 | tf_op jit(solution)/shard_map/slice | solution.py:154
  39.3 0.8 pad_slice_fusion.56
  41.6 0.9 slice.644
  42.9 1.4 %convolution_add_fusion.3 = f32[2,2,256,192]{2,3,1,0:T(8,128)} fusion(f32[2,2,256,192]{2,3,1,0:T(8,128)S(1)} %fusion.49, bf16[576,192,1,1]{1,0,3,2:T(8,128)(2,1)S(1)} %bitcast.218, bf16[2,2,256,192]{2,3,1,0:T(8,128)(2,1)S(1)} %get-tuple-element.41, bf16[2,2,256,192]{2,3,1,0:T(8,128)(2,1)S(1)} %slice.660, bf16[2,2,256,192]{2,3,1,0:T(8,128)(2,1)S(1)} %get-tuple-element.45), kind=kOutput, calls=%fused_computation.38 | convolution fusion | flops 230227968 | bytes 2973696 | tf_op jit(solution)/shard_map/fhwc,cd->fhwd/dot_general | solution.py:156
  44.4 2.2 %convolution_add_fusion.7 = f32[2,128,384]{2,1,0:T(8,128)} fusion(f32[2,128,384]{2,1,0:T(8,128)S(1)} %fusion.97, bf16[1152,384,1]{1,0,2:T(8,128)(2,1)S(1)} %bitcast.201, bf16[2,1,128,384]{3,2,0,1:T(8,128)(2,1)S(1)} %get-tuple-element.47, bf16[2,1,128,384]{3,2,0,1:T(8,128)(2,1)} %collective-permute-done.9, bf16[2,1,128,384]{3,2,0,1:T(8,128)(2,1)S(1)} %get-tuple-element.51), kind=kOutput, calls=%fused_computation.49 | convolution fusion | flops 228360192 | bytes 2260992 | tf_op jit(solution)/shard_map/fhwc,cd->fhwd/dot_general | solution.py:156
  47.2 1.3 collective-permute-start.4
  48.5 3.0 %collective-permute-done.3 = bf16[1,2,128,384]{3,2,1,0:T(8,128)(2,1)S(1)} collective-permute-done((bf16[1,2,128,384]{3,2,1,0:T(8,128)(2,1)S(1)}, bf16[1,2,128,384]{3,2,1,0:T(8,128)(2,1)S(1)}, u32[]{:S(2)}, u32[]{:S(2)}) %collective-permute-start.3) | collective-permute-done | bytes 196640 | tf_op jit(solution)/shard_map/ppermute | solution.py:47
  51.7 1.3 collective-permute-start.6
  53.1 3.0 %collective-permute-done.5 = bf16[1,2,128,384]{3,2,1,0:T(8,128)(2,1)S(1)} collective-permute-done((bf16[1,2,128,384]{3,2,1,0:T(8,128)(2,1)S(1)}, bf16[1,2,128,384]{3,2,1,0:T(8,128)(2,1)S(1)}, u32[]{:S(2)}, u32[]{:S(2)}) %collective-permute-start.5) | collective-permute-done | bytes 196640 | tf_op jit(solution)/shard_map/ppermute | solution.py:47
  57.0 4.8 %collective-permute-done.7 = bf16[1,2,128,384]{3,2,1,0:T(8,128)(2,1)S(1)} collective-permute-done((bf16[1,2,128,384]{3,2,1,0:T(8,128)(2,1)S(1)}, bf16[1,2,128,384]{3,2,1,0:T(8,128)(2,1)S(1)}, u32[]{:S(2)}, u32[]{:S(2)}) %collective-permute-start.7) | collective-permute-done | bytes 196640 | tf_op jit(solution)/shard_map/ppermute | solution.py:47
  61.8 1.1 copy-done.40
  63.0 6.3 %shard_map.100 = bf16[1,256,384]{2,1,0:T(8,128)(2,1)} custom-call(bf16[1,256,384]{2,1,0:T(8,128)(2,1)} %fusion.77.q_ref, bf16[1,2048,384]{2,1,0:T(8,128)(2,1)} %bitcast.222, bf16[384,384]{1,0:T(8,128)(2,1)} %wk_ref.1, bf16[384,384]{1,0:T(8,128)(2,1)} %wv_ref.1, bf16[1,256,384]{2,1,0:T(8,128)(2,1)} %bitcast.220, bf16[384,384]{1,0:T(8,128)(2,1)} %wo_ref.1), custom_call_target="tpu_custom_call" | custom-call | flops 2013265920 | bytes 3047424 | tf_op jit(solution)/shard_map/pallas_call | solution.py:128
  69.2 1.0 fusion.211
  70.2 5.5 %collective-permute-start.8 = (bf16[1,1,128,384]{3,2,0,1:T(8,128)(2,1)S(1)}, bf16[1,1,128,384]{3,2,0,1:T(8,128)(2,1)S(1)}, u32[]{:S(2)}, u32[]{:S(2)}) collective-permute-start(bf16[1,1,128,384]{3,2,0,1:T(8,128)(2,1)S(1)} %get-tuple-element.97), channel_id=1, source_target_pairs={{0,1},{1,0},{2,3},{3,2},{4,5},{5,4},{6,7},{7,6},{8,9},{9,8},{10,11... | collective-permute-start | bytes 294920 | tf_op jit(solution)/shard_map/ppermute | solution.py:217
  77.0 3.0 %collective-permute-start.11 = (bf16[2,1,128,384]{3,2,0,1:T(8,128)(2,1)S(1)}, bf16[2,1,128,384]{3,2,0,1:T(8,128)(2,1)S(1)}, u32[]{:S(2)}, u32[]{:S(2)}) collective-permute-start(bf16[2,1,128,384]{3,2,0,1:T(8,128)(2,1)S(1)} %fusion.148), channel_id=1, source_target_pairs={{0,1},{1,2},{2,3},{3,4},{4,5},{5,6},{6,7},{7,8},{8,9},{9,10},{10,1... | collective-permute-start | bytes 589832 | tf_op jit(solution)/shard_map/ppermute | solution.py:18
  80.0 1.9 %collective-permute-start.12 = (bf16[2,1,128,384]{3,2,0,1:T(8,128)(2,1)S(1)}, bf16[2,1,128,384]{3,2,0,1:T(8,128)(2,1)S(1)}, u32[]{:S(2)}, u32[]{:S(2)}) collective-permute-start(bf16[2,1,128,384]{3,2,0,1:T(8,128)(2,1)S(1)} %fusion.148), channel_id=1, source_target_pairs={{1,0},{2,1},{3,2},{4,3},{5,4},{6,5},{7,6},{8,7},{9,8},{10,9},{11,1... | collective-permute-start | bytes 589832 | tf_op jit(solution)/shard_map/ppermute | solution.py:19
  82.3 0.9 slice.646
  83.6 4.3 %collective-permute-done.12 = bf16[2,1,128,384]{3,2,0,1:T(8,128)(2,1)S(1)} collective-permute-done((bf16[2,1,128,384]{3,2,0,1:T(8,128)(2,1)S(1)}, bf16[2,1,128,384]{3,2,0,1:T(8,128)(2,1)S(1)}, u32[]{:S(2)}, u32[]{:S(2)}) %collective-permute-start.12) | collective-permute-done | bytes 196640 | tf_op jit(solution)/shard_map/ppermute | solution.py:19
  90.7 0.8 copy-done.7
  93.9 1.5 %fusion.76 = bf16[2,1,128,384]{3,2,0,1:T(8,128)(2,1)S(1)} fusion(f32[2,1,128,384]{3,2,0,1:T(8,128)S(1)} %fusion.43, f32[2,128,384]{2,1,0:T(8,128)S(1)} %copy-done.42, bf16[1152,384,1]{1,0,2:T(8,128)(2,1)S(1)} %bitcast.191, bf16[2,1,128,384]{3,2,0,1:T(8,128)(2,1)S(1)} %copy-done.33, bf16[2,1,128,384]{3,2,0,1:T(8,128)(2,1)} %collective-permute-done.10, ...), kind=kOutput, calls=%fused_computation.93 | convolution fusion | flops 229146624 | bytes 2850817 | tf_op jit(solution)/shard_map/fhwc,cd->fhwd/dot_general | solution.py:156
  95.4 1.9 %collective-permute-start.13 = (bf16[2,1,128,384]{3,2,0,1:T(8,128)(2,1)S(1)}, bf16[2,1,128,384]{3,2,0,1:T(8,128)(2,1)S(1)}, u32[]{:S(2)}, u32[]{:S(2)}) collective-permute-start(bf16[2,1,128,384]{3,2,0,1:T(8,128)(2,1)S(1)} %fusion.76), channel_id=1, source_target_pairs={{0,1},{1,2},{2,3},{3,4},{4,5},{5,6},{6,7},{7,8},{8,9},{9,10},{10,1... | collective-permute-start | bytes 589832 | tf_op jit(solution)/shard_map/ppermute | solution.py:18
  97.3 2.6 %collective-permute-start.14 = (bf16[2,1,128,384]{3,2,0,1:T(8,128)(2,1)S(1)}, bf16[2,1,128,384]{3,2,0,1:T(8,128)(2,1)S(1)}, u32[]{:S(2)}, u32[]{:S(2)}) collective-permute-start(bf16[2,1,128,384]{3,2,0,1:T(8,128)(2,1)S(1)} %fusion.76), channel_id=1, source_target_pairs={{1,0},{2,1},{3,2},{4,3},{5,4},{6,5},{7,6},{8,7},{9,8},{10,9},{11,1... | collective-permute-start | bytes 589832 | tf_op jit(solution)/shard_map/ppermute | solution.py:19
  101.3 3.9 %collective-permute-done.14 = bf16[2,1,128,384]{3,2,0,1:T(8,128)(2,1)S(1)} collective-permute-done((bf16[2,1,128,384]{3,2,0,1:T(8,128)(2,1)S(1)}, bf16[2,1,128,384]{3,2,0,1:T(8,128)(2,1)S(1)}, u32[]{:S(2)}, u32[]{:S(2)}) %collective-permute-start.14) | collective-permute-done | bytes 196640 | tf_op jit(solution)/shard_map/ppermute | solution.py:19
  108.4 1.2 fusion.1
  109.6 1.1 fusion.26
  110.7 1.2 multiply_reduce_fusion
  112.2 2.1 %collective-permute-start.17 = (bf16[2,1,256,192]{2,3,1,0:T(8,128)(2,1)S(1)}, bf16[2,1,256,192]{2,3,1,0:T(8,128)(2,1)S(1)}, u32[]{:S(2)}, u32[]{:S(2)}) collective-permute-start(bf16[2,1,256,192]{2,3,1,0:T(8,128)(2,1)S(1)} %get-tuple-element.68), channel_id=1, source_target_pairs={{0,1},{1,2},{2,3},{3,4},{4,5},{5,6},{6,7},{7,8},{8,9},{9,10},{10,1... | collective-permute-start | bytes 589832 | tf_op jit(solution)/shard_map/ppermute | solution.py:18
  114.3 2.4 %collective-permute-start.18 = (bf16[2,1,256,192]{2,3,1,0:T(8,128)(2,1)S(1)}, bf16[2,1,256,192]{2,3,1,0:T(8,128)(2,1)S(1)}, u32[]{:S(2)}, u32[]{:S(2)}) collective-permute-start(bf16[2,1,256,192]{2,3,1,0:T(8,128)(2,1)S(1)} %get-tuple-element.69), channel_id=1, source_target_pairs={{1,0},{2,1},{3,2},{4,3},{5,4},{6,5},{7,6},{8,7},{9,8},{10,9},{11,1... | collective-permute-start | bytes 589832 | tf_op jit(solution)/shard_map/ppermute | solution.py:19
  117.3 4.9 %collective-permute-done.18 = bf16[2,1,256,192]{2,3,1,0:T(8,128)(2,1)S(1)} collective-permute-done((bf16[2,1,256,192]{2,3,1,0:T(8,128)(2,1)S(1)}, bf16[2,1,256,192]{2,3,1,0:T(8,128)(2,1)S(1)}, u32[]{:S(2)}, u32[]{:S(2)}) %collective-permute-start.18) | collective-permute-done | bytes 196640 | tf_op jit(solution)/shard_map/ppermute | solution.py:19
  124.6 0.9 pad_slice_fusion.1
  128.0 1.3 %fusion.35 = bf16[2,2,256,192]{2,3,1,0:T(8,128)(2,1)} fusion(f32[2,2,256,192]{2,3,1,0:T(8,128)S(1)} %fusion.22, f32[2,2,256,192]{2,3,1,0:T(8,128)S(1)} %convolution_add_fusion.1, bf16[576,192,1,1]{1,0,3,2:T(8,128)(2,1)S(1)} %bitcast.208, bf16[2,2,256,192]{2,3,1,0:T(8,128)(2,1)S(1)} %get-tuple-element.38, ...), kind=kOutput, calls=%fused_computation.43 | convolution fusion | flops 230817792 | bytes 3760128 | tf_op jit(solution)/shard_map/fhwc,cd->fhwd/dot_general | solution.py:156
  (174 shorter events, 26.4 us)
Async XLA Ops:
  0.0 30.1 %copy-start = (bf16[384,384]{1,0:T(8,128)(2,1)S(1)}, bf16[384,384]{1,0:T(8,128)(2,1)}, u32[]{:S(2)}) copy-start(bf16[384,384]{1,0:T(8,128)(2,1)} %param.13) | copy-start | bytes 884740
  0.0 31.1 %collective-permute-start.10 = (bf16[2,1,128,384]{3,2,0,1:T(8,128)(2,1)}, bf16[2,1,128,384]{3,2,0,1:T(8,128)(2,1)}, u32[]{:S(2)}, u32[]{:S(2)}) collective-permute-start(bf16[2,1,128,384]{3,2,0,1:T(8,128)(2,1)} %bitcast.203), channel_id=1, source_target_pairs={{1,0},{2,1},{3,2},{4,3},{5,4},{6,5},{7,6},{8,7},{9,8},{10,9},{11,1... | collective-permute-start | bytes 589832 | tf_op jit(solution)/shard_map/ppermute | solution.py:19
  2.7 29.6 %collective-permute-start.9 = (bf16[2,1,128,384]{3,2,0,1:T(8,128)(2,1)}, bf16[2,1,128,384]{3,2,0,1:T(8,128)(2,1)}, u32[]{:S(2)}, u32[]{:S(2)}) collective-permute-start(bf16[2,1,128,384]{3,2,0,1:T(8,128)(2,1)} %bitcast.204), channel_id=1, source_target_pairs={{0,1},{1,2},{2,3},{3,4},{4,5},{5,6},{6,7},{7,8},{8,9},{9,10},{10,1... | collective-permute-start | bytes 589832 | tf_op jit(solution)/shard_map/ppermute | solution.py:18
  8.3 20.7 %collective-permute-start = (bf16[1,1,128,384]{3,2,1,0:T(8,128)(2,1)}, bf16[1,1,128,384]{3,2,1,0:T(8,128)(2,1)S(1)}, u32[]{:S(2)}, u32[]{:S(2)}) collective-permute-start(bf16[1,1,128,384]{3,2,1,0:T(8,128)(2,1)} %get-tuple-element.99), channel_id=1, source_target_pairs={{0,1},{1,0},{2,3},{3,2},{4,5},{5,4},{6,7},{7,6},{8,9},{9,8},{10,11... | collective-permute-start | bytes 294920 | tf_op jit(solution)/shard_map/ppermute | solution.py:201
  10.1 24.4 %collective-permute-start.15 = (bf16[2,1,256,192]{2,3,1,0:T(8,128)(2,1)}, bf16[2,1,256,192]{2,3,1,0:T(8,128)(2,1)}, u32[]{:S(2)}, u32[]{:S(2)}) collective-permute-start(bf16[2,1,256,192]{2,3,1,0:T(8,128)(2,1)} %get-tuple-element.80), channel_id=1, source_target_pairs={{0,1},{1,2},{2,3},{3,4},{4,5},{5,6},{6,7},{7,8},{8,9},{9,10},{10,1... | collective-permute-start | bytes 589832 | tf_op jit(solution)/shard_map/ppermute | solution.py:18
  12.8 22.8 %collective-permute-start.16 = (bf16[2,1,256,192]{2,3,1,0:T(8,128)(2,1)}, bf16[2,1,256,192]{2,3,1,0:T(8,128)(2,1)}, u32[]{:S(2)}, u32[]{:S(2)}) collective-permute-start(bf16[2,1,256,192]{2,3,1,0:T(8,128)(2,1)} %get-tuple-element.79), channel_id=1, source_target_pairs={{1,0},{2,1},{3,2},{4,3},{5,4},{6,5},{7,6},{8,7},{9,8},{10,9},{11,1... | collective-permute-start | bytes 589832 | tf_op jit(solution)/shard_map/ppermute | solution.py:19
  14.7 5.8 %copy-start.3 = (bf16[3,3,3,192,192]{4,3,2,1,0:T(8,128)(2,1)S(1)}, bf16[3,3,3,192,192]{4,3,2,1,0:T(8,128)(2,1)}, u32[]{:S(2)}) copy-start(bf16[3,3,3,192,192]{4,3,2,1,0:T(8,128)(2,1)} %param.19) | copy-start | bytes 5971972
  20.5 2.2 %copy-start.5 = (bf16[3,3,384,192]{2,3,1,0:T(8,128)(2,1)S(1)}, bf16[3,3,384,192]{2,3,1,0:T(8,128)(2,1)}, u32[]{:S(2)}) copy-start(bf16[3,3,384,192]{2,3,1,0:T(8,128)(2,1)} %param.18) | copy-start | bytes 3981316
  29.0 4.5 %copy-start.34 = (bf16[1,2,128,384]{3,2,1,0:T(8,128)(2,1)}, bf16[1,2,128,384]{3,2,1,0:T(8,128)(2,1)S(1)}, u32[]{:S(2)}) copy-start(bf16[1,2,128,384]{3,2,1,0:T(8,128)(2,1)S(1)} %pad_maximum_fusion.7) | copy-start | bytes 589828
  29.0 18.0 %collective-permute-start.1 = (bf16[1,2,128,384]{3,2,1,0:T(8,128)(2,1)S(1)}, bf16[1,2,128,384]{3,2,1,0:T(8,128)(2,1)S(1)}, u32[]{:S(2)}, u32[]{:S(2)}) collective-permute-start(bf16[1,2,128,384]{3,2,1,0:T(8,128)(2,1)S(1)} %pad_maximum_fusion.7), channel_id=1, source_target_pairs={{0,4},{1,5},{2,0},{3,1},{4,8},{5,9},{6,2},{7,3},{8,12},{9,13},{10,... | collective-permute-start | bytes 589832 | tf_op jit(solution)/shard_map/ppermute | solution.py:47
  31.1 16.1 %collective-permute-start.2 = (bf16[1,2,128,384]{3,2,1,0:T(8,128)(2,1)S(1)}, bf16[1,2,128,384]{3,2,1,0:T(8,128)(2,1)S(1)}, u32[]{:S(2)}, u32[]{:S(2)}) collective-permute-start(bf16[1,2,128,384]{3,2,1,0:T(8,128)(2,1)S(1)} %pad_maximum_fusion.7), channel_id=1, source_target_pairs={{0,2},{1,3},{2,6},{3,7},{4,0},{5,1},{6,10},{7,11},{8,4},{9,5},{10,... | collective-permute-start | bytes 589832 | tf_op jit(solution)/shard_map/ppermute | solution.py:50
  33.5 2.0 %copy-start.2 = (bf16[2,3,128,384]{3,2,0,1:T(8,128)(2,1)}, bf16[2,3,128,384]{3,2,0,1:T(8,128)(2,1)S(1)}, u32[]{:S(2)}) copy-start(bf16[2,3,128,384]{3,2,0,1:T(8,128)(2,1)S(1)} %pad_maximum_fusion.4) | copy-start | bytes 1769476
  33.5 2.0 %copy-start.4 = (bf16[2,2,256,192]{2,3,1,0:T(8,128)(2,1)S(1)}, bf16[2,2,256,192]{2,3,1,0:T(8,128)(2,1)}, u32[]{:S(2)}) copy-start(bf16[2,2,256,192]{2,3,1,0:T(8,128)(2,1)} %param.12) | copy-start | bytes 1179652
  38.3 1.8 %copy-start.14 = (bf16[1,1,3,384,384]{4,3,2,1,0:T(8,128)(2,1)S(1)}, bf16[1,1,3,384,384]{4,3,2,1,0:T(8,128)(2,1)}, u32[]{:S(2)}) copy-start(bf16[1,1,3,384,384]{4,3,2,1,0:T(8,128)(2,1)} %get-tuple-element.12) | copy-start | bytes 2654212
  41.1 1.5 %copy-start.11 = (bf16[1,1,3,384,384]{4,3,2,1,0:T(8,128)(2,1)S(1)}, bf16[1,1,3,384,384]{4,3,2,1,0:T(8,128)(2,1)}, u32[]{:S(2)}) copy-start(bf16[1,1,3,384,384]{4,3,2,1,0:T(8,128)(2,1)} %get-tuple-element.11) | copy-start | bytes 2654212
  41.6 1.3 %copy-start.30 = (bf16[1,1,3,192,192]{4,3,2,1,0:T(8,128)(2,1)S(1)}, bf16[1,1,3,192,192]{4,3,2,1,0:T(8,128)(2,1)}, u32[]{:S(2)}) copy-start(bf16[1,1,3,192,192]{4,3,2,1,0:T(8,128)(2,1)} %get-tuple-element.23) | copy-start | bytes 663556
  42.9 1.5 %copy-start.13 = (bf16[1,1,3,384,384]{4,3,2,1,0:T(8,128)(2,1)S(1)}, bf16[1,1,3,384,384]{4,3,2,1,0:T(8,128)(2,1)}, u32[]{:S(2)}) copy-start(bf16[1,1,3,384,384]{4,3,2,1,0:T(8,128)(2,1)} %get-tuple-element.13) | copy-start | bytes 2654212
  44.4 2.2 %copy-start.9 = (bf16[1,1,3,384,384]{4,3,2,1,0:T(8,128)(2,1)S(1)}, bf16[1,1,3,384,384]{4,3,2,1,0:T(8,128)(2,1)}, u32[]{:S(2)}) copy-start(bf16[1,1,3,384,384]{4,3,2,1,0:T(8,128)(2,1)} %get-tuple-element.10) | copy-start | bytes 2654212
  44.4 2.2 %copy-start.38 = (bf16[1,1,128,384]{3,2,0,1:T(8,128)(2,1)S(1)}, bf16[1,1,128,384]{3,2,0,1:T(8,128)(2,1)}, u32[]{:S(2)}) copy-start(bf16[1,1,128,384]{3,2,0,1:T(8,128)(2,1)} %slice.645) | copy-start | bytes 294916
  46.6 1.9 %copy-start.39 = (bf16[1,16,128,384]{3,2,1,0:T(8,128)(2,1)S(1)}, bf16[1,16,128,384]{3,2,1,0:T(8,128)(2,1)}, u32[]{:S(2)}) copy-start(bf16[1,16,128,384]{3,2,1,0:T(8,128)(2,1)} %constant_dynamic-update-slice_fusion.7) | copy-start | bytes 4718596
  46.9 4.6 %collective-permute-start.3 = (bf16[1,2,128,384]{3,2,1,0:T(8,128)(2,1)S(1)}, bf16[1,2,128,384]{3,2,1,0:T(8,128)(2,1)S(1)}, u32[]{:S(2)}, u32[]{:S(2)}) collective-permute-start(bf16[1,2,128,384]{3,2,1,0:T(8,128)(2,1)S(1)} %collective-permute-done.1), channel_id=1, source_target_pairs={{0,4},{1,5},{2,0},{3,1},{4,8},{5,9},{6,2},{7,3},{8,12},{9,13},{10,... | collective-permute-start | bytes 589832 | tf_op jit(solution)/shard_map/ppermute | solution.py:47
  47.2 4.5 %collective-permute-start.4 = (bf16[1,2,128,384]{3,2,1,0:T(8,128)(2,1)S(1)}, bf16[1,2,128,384]{3,2,1,0:T(8,128)(2,1)S(1)}, u32[]{:S(2)}, u32[]{:S(2)}) collective-permute-start(bf16[1,2,128,384]{3,2,1,0:T(8,128)(2,1)S(1)} %collective-permute-done.2), channel_id=1, source_target_pairs={{0,2},{1,3},{2,6},{3,7},{4,0},{5,1},{6,10},{7,11},{8,4},{9,5},{10,... | collective-permute-start | bytes 589832 | tf_op jit(solution)/shard_map/ppermute | solution.py:50
  51.5 4.6 %collective-permute-start.5 = (bf16[1,2,128,384]{3,2,1,0:T(8,128)(2,1)S(1)}, bf16[1,2,128,384]{3,2,1,0:T(8,128)(2,1)S(1)}, u32[]{:S(2)}, u32[]{:S(2)}) collective-permute-start(bf16[1,2,128,384]{3,2,1,0:T(8,128)(2,1)S(1)} %collective-permute-done.3), channel_id=1, source_target_pairs={{0,4},{1,5},{2,0},{3,1},{4,8},{5,9},{6,2},{7,3},{8,12},{9,13},{10,... | collective-permute-start | bytes 589832 | tf_op jit(solution)/shard_map/ppermute | solution.py:47
  51.7 5.2 %collective-permute-start.6 = (bf16[1,2,128,384]{3,2,1,0:T(8,128)(2,1)S(1)}, bf16[1,2,128,384]{3,2,1,0:T(8,128)(2,1)S(1)}, u32[]{:S(2)}, u32[]{:S(2)}) collective-permute-start(bf16[1,2,128,384]{3,2,1,0:T(8,128)(2,1)S(1)} %collective-permute-done.4), channel_id=1, source_target_pairs={{0,2},{1,3},{2,6},{3,7},{4,0},{5,1},{6,10},{7,11},{8,4},{9,5},{10,... | collective-permute-start | bytes 589832 | tf_op jit(solution)/shard_map/ppermute | solution.py:50
  56.1 5.7 %collective-permute-start.7 = (bf16[1,2,128,384]{3,2,1,0:T(8,128)(2,1)S(1)}, bf16[1,2,128,384]{3,2,1,0:T(8,128)(2,1)S(1)}, u32[]{:S(2)}, u32[]{:S(2)}) collective-permute-start(bf16[1,2,128,384]{3,2,1,0:T(8,128)(2,1)S(1)} %collective-permute-done.5), channel_id=1, source_target_pairs={{0,4},{1,5},{2,0},{3,1},{4,8},{5,9},{6,2},{7,3},{8,12},{9,13},{10,... | collective-permute-start | bytes 589832 | tf_op jit(solution)/shard_map/ppermute | solution.py:47
  70.2 11.7 %copy-start.27 = (bf16[1,1,3,192,192]{4,3,2,1,0:T(8,128)(2,1)S(1)}, bf16[1,1,3,192,192]{4,3,2,1,0:T(8,128)(2,1)}, u32[]{:S(2)}) copy-start(bf16[1,1,3,192,192]{4,3,2,1,0:T(8,128)(2,1)} %get-tuple-element.20) | copy-start | bytes 663556
  70.2 11.7 %copy-start.35 = (bf16[1,2,256,192]{2,3,1,0:T(8,128)(2,1)S(1)}, bf16[1,2,256,192]{2,3,1,0:T(8,128)(2,1)}, u32[]{:S(2)}) copy-start(bf16[1,2,256,192]{2,3,1,0:T(8,128)(2,1)} %slice.663) | copy-start | bytes 589828
  70.2 6.4 %collective-permute-start.8 = (bf16[1,1,128,384]{3,2,0,1:T(8,128)(2,1)S(1)}, bf16[1,1,128,384]{3,2,0,1:T(8,128)(2,1)S(1)}, u32[]{:S(2)}, u32[]{:S(2)}) collective-permute-start(bf16[1,1,128,384]{3,2,0,1:T(8,128)(2,1)S(1)} %get-tuple-element.97), channel_id=1, source_target_pairs={{0,1},{1,0},{2,3},{3,2},{4,5},{5,4},{6,7},{7,6},{8,9},{9,8},{10,11... | collective-permute-start | bytes 294920 | tf_op jit(solution)/shard_map/ppermute | solution.py:217
  77.0 6.2 %copy-start.8 = (bf16[1,1,3,384,384]{4,3,2,1,0:T(8,128)(2,1)S(1)}, bf16[1,1,3,384,384]{4,3,2,1,0:T(8,128)(2,1)}, u32[]{:S(2)}) copy-start(bf16[1,1,3,384,384]{4,3,2,1,0:T(8,128)(2,1)} %get-tuple-element.9) | copy-start | bytes 2654212
  77.0 6.2 %copy-start.36 = (bf16[1,1,128,384]{3,2,0,1:T(8,128)(2,1)S(1)}, bf16[1,1,128,384]{3,2,0,1:T(8,128)(2,1)}, u32[]{:S(2)}) copy-start(bf16[1,1,128,384]{3,2,0,1:T(8,128)(2,1)} %get-tuple-element.81) | copy-start | bytes 294916
  77.0 6.2 %copy-start.37 = (bf16[1,1,128,384]{3,2,0,1:T(8,128)(2,1)S(1)}, bf16[1,1,128,384]{3,2,0,1:T(8,128)(2,1)}, u32[]{:S(2)}) copy-start(bf16[1,1,128,384]{3,2,0,1:T(8,128)(2,1)} %get-tuple-element.85) | copy-start | bytes 294916
  77.0 6.6 %collective-permute-start.11 = (bf16[2,1,128,384]{3,2,0,1:T(8,128)(2,1)S(1)}, bf16[2,1,128,384]{3,2,0,1:T(8,128)(2,1)S(1)}, u32[]{:S(2)}, u32[]{:S(2)}) collective-permute-start(bf16[2,1,128,384]{3,2,0,1:T(8,128)(2,1)S(1)} %fusion.148), channel_id=1, source_target_pairs={{0,1},{1,2},{2,3},{3,4},{4,5},{5,6},{6,7},{7,8},{8,9},{9,10},{10,1... | collective-permute-start | bytes 589832 | tf_op jit(solution)/shard_map/ppermute | solution.py:18
  80.0 7.9 %collective-permute-start.12 = (bf16[2,1,128,384]{3,2,0,1:T(8,128)(2,1)S(1)}, bf16[2,1,128,384]{3,2,0,1:T(8,128)(2,1)S(1)}, u32[]{:S(2)}, u32[]{:S(2)}) collective-permute-start(bf16[2,1,128,384]{3,2,0,1:T(8,128)(2,1)S(1)} %fusion.148), channel_id=1, source_target_pairs={{1,0},{2,1},{3,2},{4,3},{5,4},{6,5},{7,6},{8,7},{9,8},{10,9},{11,1... | collective-permute-start | bytes 589832 | tf_op jit(solution)/shard_map/ppermute | solution.py:19
  88.0 1.2 copy-start.12
  88.3 1.2 copy-start.10
  92.7 1.2 copy-start.42
  93.9 6.1 %slice-start.1 = ((bf16[2,2,256,192]{2,3,1,0:T(8,128)(2,1)}), bf16[1,2,256,192]{2,3,1,0:T(8,128)(2,1)S(1)}, s32[]{:S(2)}) async-start(bf16[2,2,256,192]{2,3,1,0:T(8,128)(2,1)} %param.12), calls=%async_computation.1 | async-start | bytes 393216 | tf_op jit(solution)/shard_map/slice | solution.py:154
  93.9 6.1 %copy-start.25 = (bf16[1,1,3,192,192]{4,3,2,1,0:T(8,128)(2,1)S(1)}, bf16[1,1,3,192,192]{4,3,2,1,0:T(8,128)(2,1)}, u32[]{:S(2)}) copy-start(bf16[1,1,3,192,192]{4,3,2,1,0:T(8,128)(2,1)} %get-tuple-element.19) | copy-start | bytes 663556
  95.4 5.9 %collective-permute-start.13 = (bf16[2,1,128,384]{3,2,0,1:T(8,128)(2,1)S(1)}, bf16[2,1,128,384]{3,2,0,1:T(8,128)(2,1)S(1)}, u32[]{:S(2)}, u32[]{:S(2)}) collective-permute-start(bf16[2,1,128,384]{3,2,0,1:T(8,128)(2,1)S(1)} %fusion.76), channel_id=1, source_target_pairs={{0,1},{1,2},{2,3},{3,4},{4,5},{5,6},{6,7},{7,8},{8,9},{9,10},{10,1... | collective-permute-start | bytes 589832 | tf_op jit(solution)/shard_map/ppermute | solution.py:18
  97.3 7.9 %collective-permute-start.14 = (bf16[2,1,128,384]{3,2,0,1:T(8,128)(2,1)S(1)}, bf16[2,1,128,384]{3,2,0,1:T(8,128)(2,1)S(1)}, u32[]{:S(2)}, u32[]{:S(2)}) collective-permute-start(bf16[2,1,128,384]{3,2,0,1:T(8,128)(2,1)S(1)} %fusion.76), channel_id=1, source_target_pairs={{1,0},{2,1},{3,2},{4,3},{5,4},{6,5},{7,6},{8,7},{9,8},{10,9},{11,1... | collective-permute-start | bytes 589832 | tf_op jit(solution)/shard_map/ppermute | solution.py:19
  108.4 1.2 copy-start.17
  111.9 4.8 %copy-start.19 = (bf16[2,2,256,192]{2,3,1,0:T(8,128)(2,1)S(1)}, bf16[2,2,256,192]{2,3,1,0:T(8,128)(2,1)}, u32[]{:S(2)}) copy-start(bf16[2,2,256,192]{2,3,1,0:T(8,128)(2,1)} %get-tuple-element.40) | copy-start | bytes 1179652
  111.9 4.8 %copy-start.20 = (bf16[2,2,256,192]{2,3,1,0:T(8,128)(2,1)S(1)}, bf16[2,2,256,192]{2,3,1,0:T(8,128)(2,1)}, u32[]{:S(2)}) copy-start(bf16[2,2,256,192]{2,3,1,0:T(8,128)(2,1)} %get-tuple-element.44) | copy-start | bytes 1179652
  111.9 4.8 %copy-start.29 = (bf16[1,1,3,192,192]{4,3,2,1,0:T(8,128)(2,1)S(1)}, bf16[1,1,3,192,192]{4,3,2,1,0:T(8,128)(2,1)}, u32[]{:S(2)}) copy-start(bf16[1,1,3,192,192]{4,3,2,1,0:T(8,128)(2,1)} %get-tuple-element.21) | copy-start | bytes 663556
  111.9 4.8 %copy-start.41 = (f32[2,2,256,192]{2,3,1,0:T(8,128)S(1)}, f32[2,2,256,192]{2,3,1,0:T(8,128)}, u32[]{:S(2)}) copy-start(f32[2,2,256,192]{2,3,1,0:T(8,128)} %convolution_add_fusion.3) | copy-start | bytes 2359300
  112.2 5.1 %collective-permute-start.17 = (bf16[2,1,256,192]{2,3,1,0:T(8,128)(2,1)S(1)}, bf16[2,1,256,192]{2,3,1,0:T(8,128)(2,1)S(1)}, u32[]{:S(2)}, u32[]{:S(2)}) collective-permute-start(bf16[2,1,256,192]{2,3,1,0:T(8,128)(2,1)S(1)} %get-tuple-element.68), channel_id=1, source_target_pairs={{0,1},{1,2},{2,3},{3,4},{4,5},{5,6},{6,7},{7,8},{8,9},{9,10},{10,1... | collective-permute-start | bytes 589832 | tf_op jit(solution)/shard_map/ppermute | solution.py:18
  114.3 7.9 %collective-permute-start.18 = (bf16[2,1,256,192]{2,3,1,0:T(8,128)(2,1)S(1)}, bf16[2,1,256,192]{2,3,1,0:T(8,128)(2,1)S(1)}, u32[]{:S(2)}, u32[]{:S(2)}) collective-permute-start(bf16[2,1,256,192]{2,3,1,0:T(8,128)(2,1)S(1)} %get-tuple-element.69), channel_id=1, source_target_pairs={{1,0},{2,1},{3,2},{4,3},{5,4},{6,5},{7,6},{8,7},{9,8},{10,9},{11,1... | collective-permute-start | bytes 589832 | tf_op jit(solution)/shard_map/ppermute | solution.py:19
  128.0 1.3 %copy-start.1 = (bf16[384,384]{1,0:T(8,128)(2,1)S(1)}, bf16[384,384]{1,0:T(8,128)(2,1)}, u32[]{:S(2)}) copy-start(bf16[384,384]{1,0:T(8,128)(2,1)} %param.13) | copy-start | bytes 884740
  (16 other events, 16.3 us)

commit v17 on v15

--- a/solution.py
+++ b/solution.py
@@ -44,6 +44,12 @@
     pieces = [x]
     ahead = behind = x
     for step in range(1, chips // 2 + 1):
+        if step == chips - step and x.shape[1] > 1:
+            half = x.shape[1] // 2
+            first = lax.ppermute(ahead[:, :half], "ha", forward)
+            second = lax.ppermute(behind[:, half:], "ha", backward)
+            pieces.append(jnp.concatenate([first, second], axis=1))
+            continue
         ahead = lax.ppermute(ahead, "ha", forward)
         pieces.append(ahead)
         if step < chips - step:

time: 97.2 us -> 96.5 us (level)
  starting transfers between devices: 28.6 us -> 26.8 us
  waiting for transfers between devices: 26.7 us -> 27.7 us
    ppermute x4 -> x3, waiting for transfers between devices: 14.5 us -> 10.1 us  [gather_chip_rows(): ahead = lax.ppermute(ahead, 'ha', forward)]
    ppermute x3, waiting for transfers between devices: 7.65 us -> 11.4 us  [halo_rows(): after = lax.ppermute(first, 'ha', down)]
    ppermute x3, starting transfers between devices: 11.7 us -> 8.43 us  [halo_rows(): before = lax.ppermute(last, 'ha', up)]
    ppermute x0 -> x2, waiting for transfers between devices: none -> 2.36 us  [the longest x1 1.93 us: gather_chip_rows(): first = lax.ppermute(ahead[:, :half], 'ha', forward)]
    ppermute x0 -> x2, starting transfers between devices: none -> 1.57 us  [the longest x1 1.35 us: gather_chip_rows(): second = lax.ppermute(behind[:, half:], 'ha', backward)]
    unnamed x26 -> x27, local copies, waits for them, and re-layouts: 3.16 us -> 3.17 us
  transfers between devices with their start and end apart: 15 -> 16, of which waited for: 10 -> 11; matrix products, arithmetic and copies ran while one was open for 9% -> 9% of each run, Pallas kernels for 0% -> 0%
where the time goes in v17:
time: 96.5 us; the launch traced here: 95.7 us
  waiting for transfers between devices  27.7 us (29%)
  starting transfers between devices  26.8 us (28%)
  local copies, waits for them, and re-layouts  16.2 us (17%)
  matrix products  14.2 us (15%)
  Pallas kernels  6.32 us (7%)
  other arithmetic  3.8 us (4%)
    dot_general x21, matrix products, conv_taps(): jnp.einsum('fhwc,cd->fhwd', stacked, kernel, preferred_element_type=jnp.f...  13.2 us
    ppermute x3, waiting for transfers between devices, halo_rows(): after = lax.ppermute(first, 'ha', down)  11.4 us
    ppermute x3, waiting for transfers between devices, gather_chip_rows(): ahead = lax.ppermute(ahead, 'ha', forward)  10.1 us
    ppermute x3, starting transfers between devices, halo_rows(): before = lax.ppermute(last, 'ha', up)  8.43 us
    ppermute x3, starting transfers between devices, halo_rows(): after = lax.ppermute(first, 'ha', down)  7.06 us
    pallas_call x1, Pallas kernels, attend(): pl.pallas_call(functools.partial(attention_kernel, scale), grid=(frames,)...  6.32 us
    slice x6, local copies, waits for them, and re-layouts, conv_taps(): kernel = weight[time_off, row_off].reshape(3 * in_channels, out_channels)  5.41 us
    ppermute x1, starting transfers between devices, per_device(): back = lax.ppermute(mixed_block[:, 1:2], 'ha', swap)  4.59 us
  transfers between devices with their start and end apart: 16, of which 11 were waited for; matrix products, arithmetic and copies ran while one was open for 9% of the time, Pallas kernels for 0%

profile of v17, /device:TPU:13, one launch (start us, length us, event | category | flops | bytes accessed | tf_op | source)
XLA Modules:
  0.0 95.7 jit_solution(8883461514857523701)
XLA Ops:
  0.0 1.0 %constant_dynamic-update-slice_fusion.9 = (bf16[1,16,128,384]{3,2,1,0:T(8,128)(2,1)S(1)}, bf16[1,1,128,384]{3,2,1,0:T(8,128)(2,1)S(1)}, bf16[1,1,128,384]{3,2,1,0:T(8,128)(2,1)S(1)}) fusion(bf16[2,1,128,384]{3,2,1,0:T(8,128)(2,1)} %param.10, s32[]{:T(128)S(6)} %select_n.39, s32[]{:T(128)S(6)} %select_n.40), kind=kLoop, calls=%fused_computation.207 | loop fusion | bytes 491528
  1.0 0.7 collective-permute-start
  1.8 0.9 collective-permute-done
  3.0 1.3 %collective-permute-start.2 = (bf16[1,2,128,384]{3,2,1,0:T(8,128)(2,1)S(1)}, bf16[1,2,128,384]{3,2,1,0:T(8,128)(2,1)S(1)}, u32[]{:S(2)}, u32[]{:S(2)}) collective-permute-start(bf16[1,2,128,384]{3,2,1,0:T(8,128)(2,1)S(1)} %pad_maximum_fusion.5), channel_id=1, source_target_pairs={{0,2},{1,3},{2,6},{3,7},{4,0},{5,1},{6,10},{7,11},{8,4},{9,5},{10,... | collective-permute-start | bytes 589832 | tf_op jit(solution)/shard_map/ppermute | solution.py:56
  4.5 1.0 fusion.88.q_ref
  5.5 3.4 %collective-permute-done.1 = bf16[1,2,128,384]{3,2,1,0:T(8,128)(2,1)S(1)} collective-permute-done((bf16[1,2,128,384]{3,2,1,0:T(8,128)(2,1)S(1)}, bf16[1,2,128,384]{3,2,1,0:T(8,128)(2,1)S(1)}, u32[]{:S(2)}, u32[]{:S(2)}) %collective-permute-start.1) | collective-permute-done | bytes 196640 | tf_op jit(solution)/shard_map/ppermute | solution.py:53
  9.1 1.3 %collective-permute-start.4 = (bf16[1,2,128,384]{3,2,1,0:T(8,128)(2,1)S(1)}, bf16[1,2,128,384]{3,2,1,0:T(8,128)(2,1)S(1)}, u32[]{:S(2)}, u32[]{:S(2)}) collective-permute-start(bf16[1,2,128,384]{3,2,1,0:T(8,128)(2,1)S(1)} %collective-permute-done.2), channel_id=1, source_target_pairs={{0,2},{1,3},{2,6},{3,7},{4,0},{5,1},{6,10},{7,11},{8,4},{9,5},{10,... | collective-permute-start | bytes 589832 | tf_op jit(solution)/shard_map/ppermute | solution.py:56
  10.5 3.7 %collective-permute-done.3 = bf16[1,2,128,384]{3,2,1,0:T(8,128)(2,1)S(1)} collective-permute-done((bf16[1,2,128,384]{3,2,1,0:T(8,128)(2,1)S(1)}, bf16[1,2,128,384]{3,2,1,0:T(8,128)(2,1)S(1)}, u32[]{:S(2)}, u32[]{:S(2)}) %collective-permute-start.3) | collective-permute-done | bytes 196640 | tf_op jit(solution)/shard_map/ppermute | solution.py:53
  14.3 1.3 %collective-permute-start.6 = (bf16[1,2,128,384]{3,2,1,0:T(8,128)(2,1)S(1)}, bf16[1,2,128,384]{3,2,1,0:T(8,128)(2,1)S(1)}, u32[]{:S(2)}, u32[]{:S(2)}) collective-permute-start(bf16[1,2,128,384]{3,2,1,0:T(8,128)(2,1)S(1)} %collective-permute-done.4), channel_id=1, source_target_pairs={{0,2},{1,3},{2,6},{3,7},{4,0},{5,1},{6,10},{7,11},{8,4},{9,5},{10,... | collective-permute-start | bytes 589832 | tf_op jit(solution)/shard_map/ppermute | solution.py:56
  15.7 3.0 %collective-permute-done.5 = bf16[1,2,128,384]{3,2,1,0:T(8,128)(2,1)S(1)} collective-permute-done((bf16[1,2,128,384]{3,2,1,0:T(8,128)(2,1)S(1)}, bf16[1,2,128,384]{3,2,1,0:T(8,128)(2,1)S(1)}, u32[]{:S(2)}, u32[]{:S(2)}) %collective-permute-start.5) | collective-permute-done | bytes 196640 | tf_op jit(solution)/shard_map/ppermute | solution.py:53
  18.9 1.3 %collective-permute-start.8 = (bf16[1,1,128,384]{3,2,1,0:T(8,128)(2,1)S(1)}, bf16[1,1,128,384]{3,2,1,0:T(8,128)(2,1)S(1)}, u32[]{:S(2)}, u32[]{:S(2)}) collective-permute-start(bf16[1,1,128,384]{3,2,1,0:T(8,128)(2,1)S(1)} %slice.476), channel_id=1, source_target_pairs={{0,2},{1,3},{2,6},{3,7},{4,0},{5,1},{6,10},{7,11},{8,4},{9,5},{10,... | collective-permute-start | bytes 294920 | tf_op jit(solution)/shard_map/ppermute | solution.py:50
  20.3 1.9 %collective-permute-done.7 = bf16[1,1,128,384]{3,2,1,0:T(8,128)(2,1)S(1)} collective-permute-done((bf16[1,1,128,384]{3,2,1,0:T(8,128)(2,1)S(1)}, bf16[1,1,128,384]{3,2,1,0:T(8,128)(2,1)S(1)}, u32[]{:S(2)}, u32[]{:S(2)}) %collective-permute-start.7) | collective-permute-done | bytes 98336 | tf_op jit(solution)/shard_map/ppermute | solution.py:49
  22.8 1.2 %copy-done.8 = bf16[1,16,128,384]{3,2,1,0:T(8,128)(2,1)} copy-done((bf16[1,16,128,384]{3,2,1,0:T(8,128)(2,1)}, bf16[1,16,128,384]{3,2,1,0:T(8,128)(2,1)S(1)}, u32[]{:S(2)}) %copy-start.8) | copy-done | bytes 1572888
  23.9 6.3 %shard_map.100 = bf16[1,256,384]{2,1,0:T(8,128)(2,1)} custom-call(bf16[1,256,384]{2,1,0:T(8,128)(2,1)} %fusion.88.q_ref, bf16[1,2048,384]{2,1,0:T(8,128)(2,1)} %bitcast.168, bf16[384,384]{1,0:T(8,128)(2,1)} %wk_ref.1, bf16[384,384]{1,0:T(8,128)(2,1)} %wv_ref.1, bf16[1,256,384]{2,1,0:T(8,128)(2,1)} %bitcast.166, bf16[384,384]{1,0:T(8,128)(2,1)} %wo_ref.1), custom_call_target="tpu_custom_call" | custom-call | flops 2013265920 | bytes 3047424 | tf_op jit(solution)/shard_map/pallas_call | solution.py:134
  30.3 1.0 %fusion.173 = (bf16[1,1,128,384]{3,2,0,1:T(8,128)(2,1)S(1)}, bf16[1,128,384]{2,1,0:T(8,128)(2,1)S(1)}, bf16[1,1,128,384]{3,2,0,1:T(8,128)(2,1)S(1)}) fusion(bf16[1,2,128,384]{3,2,0,1:T(8,128)(2,1)} %bitcast.167), kind=kLoop, calls=%fused_computation.244 | loop fusion | bytes 491520 | tf_op jit(solution)/shard_map/slice | solution.py:195
  31.2 4.6 %collective-permute-start.9 = (bf16[1,1,128,384]{3,2,0,1:T(8,128)(2,1)S(1)}, bf16[1,1,128,384]{3,2,0,1:T(8,128)(2,1)S(1)}, u32[]{:S(2)}, u32[]{:S(2)}) collective-permute-start(bf16[1,1,128,384]{3,2,0,1:T(8,128)(2,1)S(1)} %get-tuple-element.90), channel_id=1, source_target_pairs={{0,1},{1,0},{2,3},{3,2},{4,5},{5,4},{6,7},{7,6},{8,9},{9,8},{10,11... | collective-permute-start | bytes 294920 | tf_op jit(solution)/shard_map/ppermute | solution.py:194
  35.8 0.9 collective-permute-done.9
  37.2 4.4 %collective-permute-start.10 = (bf16[4,1,128,384]{3,2,0,1:T(8,128)(2,1)S(1)}, bf16[4,1,128,384]{3,2,0,1:T(8,128)(2,1)S(1)}, u32[]{:S(2)}, u32[]{:S(2)}) collective-permute-start(bf16[4,1,128,384]{3,2,0,1:T(8,128)(2,1)S(1)} %pad_maximum_fusion.4), channel_id=1, source_target_pairs={{0,1},{1,2},{2,3},{3,4},{4,5},{5,6},{6,7},{7,8},{8,9},{9,10},{10,1... | collective-permute-start | bytes 1179656 | tf_op jit(solution)/shard_map/ppermute | solution.py:18
  41.6 1.9 %collective-permute-start.11 = (bf16[4,1,128,384]{3,2,0,1:T(8,128)(2,1)S(1)}, bf16[4,1,128,384]{3,2,0,1:T(8,128)(2,1)S(1)}, u32[]{:S(2)}, u32[]{:S(2)}) collective-permute-start(bf16[4,1,128,384]{3,2,0,1:T(8,128)(2,1)S(1)} %pad_maximum_fusion.4), channel_id=1, source_target_pairs={{1,0},{2,1},{3,2},{4,3},{5,4},{6,5},{7,6},{8,7},{9,8},{10,9},{11,1... | collective-permute-start | bytes 1179656 | tf_op jit(solution)/shard_map/ppermute | solution.py:19
  43.5 3.9 %fusion.164 = (bf16[1,1,3,384,384]{4,3,2,1,0:T(8,128)(2,1)S(1)}, bf16[1,1,3,384,384]{4,3,2,1,0:T(8,128)(2,1)S(1)}, bf16[1,1,3,384,384]{4,3,2,1,0:T(8,128)(2,1)S(...) fusion(bf16[3,3,3,384,384]{4,3,2,1,0:T(8,128)(2,1)} %param.17), kind=kLoop, calls=%fused_computation.235 | loop fusion | bytes 15925248 | tf_op jit(solution)/shard_map/slice | solution.py:100
  47.5 4.1 %collective-permute-done.11 = bf16[4,1,128,384]{3,2,0,1:T(8,128)(2,1)S(1)} collective-permute-done((bf16[4,1,128,384]{3,2,0,1:T(8,128)(2,1)S(1)}, bf16[4,1,128,384]{3,2,0,1:T(8,128)(2,1)S(1)}, u32[]{:S(2)}, u32[]{:S(2)}) %collective-permute-start.11) | collective-permute-done | bytes 393248 | tf_op jit(solution)/shard_map/ppermute | solution.py:19
  51.9 0.7 fusion.168
  56.6 0.5 fusion.141
  57.1 1.9 %collective-permute-start.12 = (bf16[2,1,128,384]{3,2,0,1:T(8,128)(2,1)S(1)}, bf16[2,1,128,384]{3,2,0,1:T(8,128)(2,1)S(1)}, u32[]{:S(2)}, u32[]{:S(2)}) collective-permute-start(bf16[2,1,128,384]{3,2,0,1:T(8,128)(2,1)S(1)} %fusion.141), channel_id=1, source_target_pairs={{0,1},{1,2},{2,3},{3,4},{4,5},{5,6},{6,7},{7,8},{8,9},{9,10},{10,1... | collective-permute-start | bytes 589832 | tf_op jit(solution)/shard_map/ppermute | solution.py:18
  59.0 2.6 %collective-permute-start.13 = (bf16[2,1,128,384]{3,2,0,1:T(8,128)(2,1)S(1)}, bf16[2,1,128,384]{3,2,0,1:T(8,128)(2,1)S(1)}, u32[]{:S(2)}, u32[]{:S(2)}) collective-permute-start(bf16[2,1,128,384]{3,2,0,1:T(8,128)(2,1)S(1)} %fusion.141), channel_id=1, source_target_pairs={{1,0},{2,1},{3,2},{4,3},{5,4},{6,5},{7,6},{8,7},{9,8},{10,9},{11,1... | collective-permute-start | bytes 589832 | tf_op jit(solution)/shard_map/ppermute | solution.py:19
  62.1 1.1 %reshape.290 = bf16[1152,192,1,1]{0,1,2,3:T(8,128)(2,1)} reshape(bf16[1,1,3,384,192]{3,2,4,1,0:T(4,128)(2,1)S(1)} %copy.34) | data formatting | bytes 884736 | tf_op jit(solution)/shard_map/reshape;squeeze | solution.py:100
  64.8 2.1 %collective-permute-done.13 = bf16[2,1,128,384]{3,2,0,1:T(8,128)(2,1)S(1)} collective-permute-done((bf16[2,1,128,384]{3,2,0,1:T(8,128)(2,1)S(1)}, bf16[2,1,128,384]{3,2,0,1:T(8,128)(2,1)S(1)}, u32[]{:S(2)}, u32[]{:S(2)}) %collective-permute-start.13) | collective-permute-done | bytes 196640 | tf_op jit(solution)/shard_map/ppermute | solution.py:19
  67.0 0.6 broadcast_in_dim.4
  68.3 0.8 pad_slice_fusion.9
  69.4 0.7 copy-done.6
  70.1 1.2 %fusion.6 = f32[2,2,256,192]{2,3,1,0:T(8,128)S(1)} fusion(bf16[2,1,258,384]{3,2,1,0:T(8,128)(2,1)S(1)} %pad_slice_fusion.10, bf16[2,2,256,384]{3,2,1,0:T(8,128)(2,1)S(1)} %get-tuple-element.81, bf16[2,2,256,384]{3,2,1,0:T(8,128)(2,1)S(1)} %get-tuple-element.80, bf16[1152,192,1,1]{0,1,2,3:T(8,128)(2,1)S(1)} %copy-done.6), kind=kOutput, calls=%fused_computation.13 | convolution fusion | flops 462422016 | bytes 3197952 | tf_op jit(solution)/shard_map/fhwc,cd->fhwd/dot_general | solution.py:101
  71.2 1.1 %fusion.28 = f32[2,2,256,192]{2,3,1,0:T(8,128)S(1)} fusion(f32[2,2,256,192]{2,3,1,0:T(8,128)S(1)} %fusion.6, bf16[2,2,256,384]{3,2,1,0:T(8,128)(2,1)S(1)} %get-tuple-element.71, bf16[2,2,256,384]{3,2,1,0:T(8,128)(2,1)S(1)} %get-tuple-element.74, bf16[2,2,256,384]{3,2,1,0:T(8,128)(2,1)S(1)} %get-tuple-element.75, bf16[1152,192,1,1]{0,1,2,3:T(8,128)(2,1)S(1)} %reshape.289), kind=kOutput, calls=%fused_computation.40 | convolution fusion | flops 460259328 | bytes 4374528 | tf_op jit(solution)/shard_map/fhwc,cd->fhwd/dot_general | solution.py:101
  72.4 1.2 %multiply_reduce_fusion = (f32[2,2,256]{2,1,0:T(2,128)S(1)}, f32[2,2,256,192]{2,3,1,0:T(8,128)S(1)}) fusion(f32[2,2,256,192]{2,3,1,0:T(8,128)S(1)} %fusion.28, bf16[1152,192,1,1]{0,1,2,3:T(8,128)(2,1)S(1)} %reshape.291, bf16[2,2,256,384]{3,2,1,0:T(8,128)(2,1)S(1)} %get-tuple-element.72, bf16[2,2,256,384]{3,2,1,0:T(8,128)(2,1)S(1)} %get-tuple-element.73, ...), kind=kOutput, calls=%fused_computation.119 | convolution fusion | flops 461044736 | bytes 4378624 | tf_op jit(solution)/shard_map/fhwc,cd->fhwd/dot_general | solution.py:101
  73.9 2.1 %collective-permute-start.14 = (bf16[4,1,256,192]{2,3,1,0:T(8,128)(2,1)S(1)}, bf16[4,1,256,192]{2,3,1,0:T(8,128)(2,1)S(1)}, u32[]{:S(2)}, u32[]{:S(2)}) collective-permute-start(bf16[4,1,256,192]{2,3,1,0:T(8,128)(2,1)S(1)} %get-tuple-element.78), channel_id=1, source_target_pairs={{0,1},{1,2},{2,3},{3,4},{4,5},{5,6},{6,7},{7,8},{8,9},{9,10},{10,1... | collective-permute-start | bytes 1179656 | tf_op jit(solution)/shard_map/ppermute | solution.py:18
  76.1 2.5 %collective-permute-start.15 = (bf16[4,1,256,192]{2,3,1,0:T(8,128)(2,1)S(1)}, bf16[4,1,256,192]{2,3,1,0:T(8,128)(2,1)S(1)}, u32[]{:S(2)}, u32[]{:S(2)}) collective-permute-start(bf16[4,1,256,192]{2,3,1,0:T(8,128)(2,1)S(1)} %get-tuple-element.79), channel_id=1, source_target_pairs={{1,0},{2,1},{3,2},{4,3},{5,4},{6,5},{7,6},{8,7},{9,8},{10,9},{11,1... | collective-permute-start | bytes 1179656 | tf_op jit(solution)/shard_map/ppermute | solution.py:19
  78.8 1.9 %collective-permute-done.14 = bf16[4,1,256,192]{2,3,1,0:T(8,128)(2,1)S(1)} collective-permute-done((bf16[4,1,256,192]{2,3,1,0:T(8,128)(2,1)S(1)}, bf16[4,1,256,192]{2,3,1,0:T(8,128)(2,1)S(1)}, u32[]{:S(2)}, u32[]{:S(2)}) %collective-permute-start.14) | collective-permute-done | bytes 393248 | tf_op jit(solution)/shard_map/ppermute | solution.py:18
  80.8 5.3 %collective-permute-done.15 = bf16[4,1,256,192]{2,3,1,0:T(8,128)(2,1)S(1)} collective-permute-done((bf16[4,1,256,192]{2,3,1,0:T(8,128)(2,1)S(1)}, bf16[4,1,256,192]{2,3,1,0:T(8,128)(2,1)S(1)}, u32[]{:S(2)}, u32[]{:S(2)}) %collective-permute-start.15) | collective-permute-done | bytes 393248 | tf_op jit(solution)/shard_map/ppermute | solution.py:19
  86.1 2.0 %select_maximum_fusion = bf16[4,4,258,192]{2,3,1,0:T(8,128)(2,1)S(1)} fusion(bf16[4,1,256,192]{2,3,1,0:T(8,128)(2,1)S(1)} %collective-permute-done.15, bf16[4,1,256,192]{2,3,1,0:T(8,128)(2,1)S(1)} %collective-permute-done.14, bf16[2,2,256,192]{2,3,1,0:T(8,128)(2,1)S(1)} %multiply_convert_fusion, bf16[2,2,256,192]{2,3,1,0:T(8,128)(2,1)S(1)} %copy-done.2), kind=kLoop, calls=%fused_computation.6 | loop fusion | flops 11888640 | bytes 3158016 | tf_op jit(solution)/shard_map/concatenate | solution.py:25
  88.0 1.7 %fusion.166 = (bf16[2,2,256,192]{2,3,1,0:T(8,128)(2,1)S(1)}, bf16[2,2,256,192]{2,3,1,0:T(8,128)(2,1)S(1)}, bf16[2,2,256,192]{2,3,1,0:T(8,128)(2,1)S(1)}, bf16[2,...) fusion(bf16[4,4,258,192]{2,3,1,0:T(8,128)(2,1)S(1)} %select_max, ...), kind=kLoop, calls=%fused_computation.237 | loop fusion | bytes 14155776 | tf_op jit(solution)/shard_map/slice | solution.py:98
  90.1 0.5 fusion.50
  90.7 0.5 convolution_add_fusion.7
  91.2 0.5 convolution_add_fusion.6
  91.7 0.5 convolution_add_fusion.5
  92.2 0.5 convolution_add_fusion.4
  92.8 0.5 convolution_add_fusion.3
  93.3 0.5 convolution_add_fusion.2
  93.8 0.5 convolution_add_fusion.1
  94.4 1.3 %fusion.40 = bf16[2,2,256,192]{2,3,1,0:T(8,128)(2,1)} fusion(f32[2,2,256,192]{2,3,1,0:T(8,128)S(1)} %get-tuple-element.93, f32[2,2,256,192]{2,3,1,0:T(8,128)S(1)} %convolution_add_fusion.1, bf16[576,192,1,1]{1,0,3,2:T(8,128)(2,1)S(1)} %bitcast.157, bf16[2,2,256,192]{2,3,1,0:T(8,128)(2,1)S(1)} %get-tuple-element.42, ...), kind=kOutput, calls=%fused_computation.48 | convolution fusion | flops 230621184 | bytes 3366912 | tf_op jit(solution)/shard_map/fhwc,cd->fhwd/dot_general | solution.py:101
  (74 shorter events, 10.4 us)
Async XLA Ops:
  0.0 4.5 %copy-start = (bf16[384,384]{1,0:T(8,128)(2,1)S(1)}, bf16[384,384]{1,0:T(8,128)(2,1)}, u32[]{:S(2)}) copy-start(bf16[384,384]{1,0:T(8,128)(2,1)} %param.13) | copy-start | bytes 884740
  1.0 1.7 %collective-permute-start = (bf16[1,1,128,384]{3,2,1,0:T(8,128)(2,1)S(1)}, bf16[1,1,128,384]{3,2,1,0:T(8,128)(2,1)S(1)}, u32[]{:S(2)}, u32[]{:S(2)}) collective-permute-start(bf16[1,1,128,384]{3,2,1,0:T(8,128)(2,1)S(1)} %get-tuple-element.91), channel_id=1, source_target_pairs={{0,1},{1,0},{2,3},{3,2},{4,5},{5,4},{6,7},{7,6},{8,9},{9,8},{10,11... | collective-permute-start | bytes 294920 | tf_op jit(solution)/shard_map/ppermute | solution.py:178
  2.7 15.9 %copy-start.7 = (bf16[1,2,128,384]{3,2,1,0:T(8,128)(2,1)}, bf16[1,2,128,384]{3,2,1,0:T(8,128)(2,1)S(1)}, u32[]{:S(2)}) copy-start(bf16[1,2,128,384]{3,2,1,0:T(8,128)(2,1)S(1)} %pad_maximum_fusion.5) | copy-start | bytes 589828
  2.7 6.2 %collective-permute-start.1 = (bf16[1,2,128,384]{3,2,1,0:T(8,128)(2,1)S(1)}, bf16[1,2,128,384]{3,2,1,0:T(8,128)(2,1)S(1)}, u32[]{:S(2)}, u32[]{:S(2)}) collective-permute-start(bf16[1,2,128,384]{3,2,1,0:T(8,128)(2,1)S(1)} %pad_maximum_fusion.5), channel_id=1, source_target_pairs={{0,4},{1,5},{2,0},{3,1},{4,8},{5,9},{6,2},{7,3},{8,12},{9,13},{10,... | collective-permute-start | bytes 589832 | tf_op jit(solution)/shard_map/ppermute | solution.py:53
  3.0 6.1 %collective-permute-start.2 = (bf16[1,2,128,384]{3,2,1,0:T(8,128)(2,1)S(1)}, bf16[1,2,128,384]{3,2,1,0:T(8,128)(2,1)S(1)}, u32[]{:S(2)}, u32[]{:S(2)}) collective-permute-start(bf16[1,2,128,384]{3,2,1,0:T(8,128)(2,1)S(1)} %pad_maximum_fusion.5), channel_id=1, source_target_pairs={{0,2},{1,3},{2,6},{3,7},{4,0},{5,1},{6,10},{7,11},{8,4},{9,5},{10,... | collective-permute-start | bytes 589832 | tf_op jit(solution)/shard_map/ppermute | solution.py:56
  8.9 5.2 %collective-permute-start.3 = (bf16[1,2,128,384]{3,2,1,0:T(8,128)(2,1)S(1)}, bf16[1,2,128,384]{3,2,1,0:T(8,128)(2,1)S(1)}, u32[]{:S(2)}, u32[]{:S(2)}) collective-permute-start(bf16[1,2,128,384]{3,2,1,0:T(8,128)(2,1)S(1)} %collective-permute-done.1), channel_id=1, source_target_pairs={{0,4},{1,5},{2,0},{3,1},{4,8},{5,9},{6,2},{7,3},{8,12},{9,13},{10,... | collective-permute-start | bytes 589832 | tf_op jit(solution)/shard_map/ppermute | solution.py:53
  9.1 5.2 %collective-permute-start.4 = (bf16[1,2,128,384]{3,2,1,0:T(8,128)(2,1)S(1)}, bf16[1,2,128,384]{3,2,1,0:T(8,128)(2,1)S(1)}, u32[]{:S(2)}, u32[]{:S(2)}) collective-permute-start(bf16[1,2,128,384]{3,2,1,0:T(8,128)(2,1)S(1)} %collective-permute-done.2), channel_id=1, source_target_pairs={{0,2},{1,3},{2,6},{3,7},{4,0},{5,1},{6,10},{7,11},{8,4},{9,5},{10,... | collective-permute-start | bytes 589832 | tf_op jit(solution)/shard_map/ppermute | solution.py:56
  14.1 4.5 %collective-permute-start.5 = (bf16[1,2,128,384]{3,2,1,0:T(8,128)(2,1)S(1)}, bf16[1,2,128,384]{3,2,1,0:T(8,128)(2,1)S(1)}, u32[]{:S(2)}, u32[]{:S(2)}) collective-permute-start(bf16[1,2,128,384]{3,2,1,0:T(8,128)(2,1)S(1)} %collective-permute-done.3), channel_id=1, source_target_pairs={{0,4},{1,5},{2,0},{3,1},{4,8},{5,9},{6,2},{7,3},{8,12},{9,13},{10,... | collective-permute-start | bytes 589832 | tf_op jit(solution)/shard_map/ppermute | solution.py:53
  14.3 4.6 %collective-permute-start.6 = (bf16[1,2,128,384]{3,2,1,0:T(8,128)(2,1)S(1)}, bf16[1,2,128,384]{3,2,1,0:T(8,128)(2,1)S(1)}, u32[]{:S(2)}, u32[]{:S(2)}) collective-permute-start(bf16[1,2,128,384]{3,2,1,0:T(8,128)(2,1)S(1)} %collective-permute-done.4), channel_id=1, source_target_pairs={{0,2},{1,3},{2,6},{3,7},{4,0},{5,1},{6,10},{7,11},{8,4},{9,5},{10,... | collective-permute-start | bytes 589832 | tf_op jit(solution)/shard_map/ppermute | solution.py:56
  18.7 3.6 %collective-permute-start.7 = (bf16[1,1,128,384]{3,2,1,0:T(8,128)(2,1)S(1)}, bf16[1,1,128,384]{3,2,1,0:T(8,128)(2,1)S(1)}, u32[]{:S(2)}, u32[]{:S(2)}) collective-permute-start(bf16[1,1,128,384]{3,2,1,0:T(8,128)(2,1)S(1)} %slice.475), channel_id=1, source_target_pairs={{0,4},{1,5},{2,0},{3,1},{4,8},{5,9},{6,2},{7,3},{8,12},{9,13},{10,... | collective-permute-start | bytes 294920 | tf_op jit(solution)/shard_map/ppermute | solution.py:49
  18.9 3.8 %collective-permute-start.8 = (bf16[1,1,128,384]{3,2,1,0:T(8,128)(2,1)S(1)}, bf16[1,1,128,384]{3,2,1,0:T(8,128)(2,1)S(1)}, u32[]{:S(2)}, u32[]{:S(2)}) collective-permute-start(bf16[1,1,128,384]{3,2,1,0:T(8,128)(2,1)S(1)} %slice.476), channel_id=1, source_target_pairs={{0,2},{1,3},{2,6},{3,7},{4,0},{5,1},{6,10},{7,11},{8,4},{9,5},{10,... | collective-permute-start | bytes 294920 | tf_op jit(solution)/shard_map/ppermute | solution.py:50
  22.8 1.2 %copy-start.8 = (bf16[1,16,128,384]{3,2,1,0:T(8,128)(2,1)}, bf16[1,16,128,384]{3,2,1,0:T(8,128)(2,1)S(1)}, u32[]{:S(2)}) copy-start(bf16[1,16,128,384]{3,2,1,0:T(8,128)(2,1)S(1)} %constant_dynamic-update-slice_fusion) | copy-start | bytes 4718596
  23.9 13.2 %copy-start.4 = (bf16[2,1,128,384]{3,2,1,0:T(8,128)(2,1)S(1)}, bf16[2,1,128,384]{3,2,1,0:T(8,128)(2,1)}, u32[]{:S(2)}) copy-start(bf16[2,1,128,384]{3,2,1,0:T(8,128)(2,1)} %param.11) | copy-start | bytes 589828
  31.2 5.5 %collective-permute-start.9 = (bf16[1,1,128,384]{3,2,0,1:T(8,128)(2,1)S(1)}, bf16[1,1,128,384]{3,2,0,1:T(8,128)(2,1)S(1)}, u32[]{:S(2)}, u32[]{:S(2)}) collective-permute-start(bf16[1,1,128,384]{3,2,0,1:T(8,128)(2,1)S(1)} %get-tuple-element.90), channel_id=1, source_target_pairs={{0,1},{1,0},{2,3},{3,2},{4,5},{5,4},{6,7},{7,6},{8,9},{9,8},{10,11... | collective-permute-start | bytes 294920 | tf_op jit(solution)/shard_map/ppermute | solution.py:194
  37.2 10.3 %collective-permute-start.10 = (bf16[4,1,128,384]{3,2,0,1:T(8,128)(2,1)S(1)}, bf16[4,1,128,384]{3,2,0,1:T(8,128)(2,1)S(1)}, u32[]{:S(2)}, u32[]{:S(2)}) collective-permute-start(bf16[4,1,128,384]{3,2,0,1:T(8,128)(2,1)S(1)} %pad_maximum_fusion.4), channel_id=1, source_target_pairs={{0,1},{1,2},{2,3},{3,4},{4,5},{5,6},{6,7},{7,8},{8,9},{9,10},{10,1... | collective-permute-start | bytes 1179656 | tf_op jit(solution)/shard_map/ppermute | solution.py:18
  41.6 10.0 %collective-permute-start.11 = (bf16[4,1,128,384]{3,2,0,1:T(8,128)(2,1)S(1)}, bf16[4,1,128,384]{3,2,0,1:T(8,128)(2,1)S(1)}, u32[]{:S(2)}, u32[]{:S(2)}) collective-permute-start(bf16[4,1,128,384]{3,2,0,1:T(8,128)(2,1)S(1)} %pad_maximum_fusion.4), channel_id=1, source_target_pairs={{1,0},{2,1},{3,2},{4,3},{5,4},{6,5},{7,6},{8,7},{9,8},{10,9},{11,1... | collective-permute-start | bytes 1179656 | tf_op jit(solution)/shard_map/ppermute | solution.py:19
  56.6 5.0 %copy-start.5 = (bf16[3,3,384,192]{2,3,1,0:T(8,128)(2,1)S(1)}, bf16[3,3,384,192]{2,3,1,0:T(8,128)(2,1)}, u32[]{:S(2)}) copy-start(bf16[3,3,384,192]{2,3,1,0:T(8,128)(2,1)} %param.18) | copy-start | bytes 3981316
  57.1 7.7 %collective-permute-start.12 = (bf16[2,1,128,384]{3,2,0,1:T(8,128)(2,1)S(1)}, bf16[2,1,128,384]{3,2,0,1:T(8,128)(2,1)S(1)}, u32[]{:S(2)}, u32[]{:S(2)}) collective-permute-start(bf16[2,1,128,384]{3,2,0,1:T(8,128)(2,1)S(1)} %fusion.141), channel_id=1, source_target_pairs={{0,1},{1,2},{2,3},{3,4},{4,5},{5,6},{6,7},{7,8},{8,9},{9,10},{10,1... | collective-permute-start | bytes 589832 | tf_op jit(solution)/shard_map/ppermute | solution.py:18
  59.0 7.9 %collective-permute-start.13 = (bf16[2,1,128,384]{3,2,0,1:T(8,128)(2,1)S(1)}, bf16[2,1,128,384]{3,2,0,1:T(8,128)(2,1)S(1)}, u32[]{:S(2)}, u32[]{:S(2)}) collective-permute-start(bf16[2,1,128,384]{3,2,0,1:T(8,128)(2,1)S(1)} %fusion.141), channel_id=1, source_target_pairs={{1,0},{2,1},{3,2},{4,3},{5,4},{6,5},{7,6},{8,7},{9,8},{10,9},{11,1... | collective-permute-start | bytes 589832 | tf_op jit(solution)/shard_map/ppermute | solution.py:19
  69.1 1.0 %copy-start.6 = (bf16[1152,192,1,1]{0,1,2,3:T(8,128)(2,1)S(1)}, bf16[1152,192,1,1]{0,1,2,3:T(8,128)(2,1)}, u32[]{:S(2)}) copy-start(bf16[1152,192,1,1]{0,1,2,3:T(8,128)(2,1)} %reshape.290) | copy-start | bytes 1327108
  72.4 1.4 %copy-start.2 = (bf16[2,2,256,192]{2,3,1,0:T(8,128)(2,1)S(1)}, bf16[2,2,256,192]{2,3,1,0:T(8,128)(2,1)}, u32[]{:S(2)}) copy-start(bf16[2,2,256,192]{2,3,1,0:T(8,128)(2,1)} %param.12) | copy-start | bytes 1179652
  73.6 5.0 %copy-start.3 = (bf16[3,3,3,192,192]{4,3,2,1,0:T(8,128)(2,1)S(1)}, bf16[3,3,3,192,192]{4,3,2,1,0:T(8,128)(2,1)}, u32[]{:S(2)}) copy-start(bf16[3,3,3,192,192]{4,3,2,1,0:T(8,128)(2,1)} %param.19) | copy-start | bytes 5971972
  73.9 6.8 %collective-permute-start.14 = (bf16[4,1,256,192]{2,3,1,0:T(8,128)(2,1)S(1)}, bf16[4,1,256,192]{2,3,1,0:T(8,128)(2,1)S(1)}, u32[]{:S(2)}, u32[]{:S(2)}) collective-permute-start(bf16[4,1,256,192]{2,3,1,0:T(8,128)(2,1)S(1)} %get-tuple-element.78), channel_id=1, source_target_pairs={{0,1},{1,2},{2,3},{3,4},{4,5},{5,6},{6,7},{7,8},{8,9},{9,10},{10,1... | collective-permute-start | bytes 1179656 | tf_op jit(solution)/shard_map/ppermute | solution.py:18
  76.1 10.0 %collective-permute-start.15 = (bf16[4,1,256,192]{2,3,1,0:T(8,128)(2,1)S(1)}, bf16[4,1,256,192]{2,3,1,0:T(8,128)(2,1)S(1)}, u32[]{:S(2)}, u32[]{:S(2)}) collective-permute-start(bf16[4,1,256,192]{2,3,1,0:T(8,128)(2,1)S(1)} %get-tuple-element.79), channel_id=1, source_target_pairs={{1,0},{2,1},{3,2},{4,3},{5,4},{6,5},{7,6},{8,7},{9,8},{10,9},{11,1... | collective-permute-start | bytes 1179656 | tf_op jit(solution)/shard_map/ppermute | solution.py:19
  94.4 1.3 %copy-start.1 = (bf16[384,384]{1,0:T(8,128)(2,1)S(1)}, bf16[384,384]{1,0:T(8,128)(2,1)}, u32[]{:S(2)}) copy-start(bf16[384,384]{1,0:T(8,128)(2,1)} %param.13) | copy-start | bytes 884740

commit v18 on v17

--- a/solution.py
+++ b/solution.py
@@ -173,9 +173,10 @@
     core = lax.axis_index("ha") % 2
     count = lax.axis_size("ha")
     swap = [(i, i ^ 1) for i in range(count)]
-    other = lax.dynamic_slice_in_dim(features, 1 - core, 1, axis=0)
+    partner = lax.ppermute(features, "ha", swap)
     mine = lax.dynamic_slice_in_dim(features, core, 1, axis=0)
-    block = jnp.concatenate([mine, lax.ppermute(other, "ha", swap)], axis=1)
+    theirs = lax.dynamic_slice_in_dim(partner, core, 1, axis=0)
+    block = jnp.concatenate([mine, theirs], axis=1)
     every_row = gather_chip_rows(block)
     all_rows = every_row.reshape(1, -1, channels)
     normed = rms_scale(block).astype(jnp.bfloat16)

time: 96.5 us -> 95.9 us (level)
  transfers between devices with their start and end apart: 16 -> 16, of which waited for: 11 -> 11; matrix products, arithmetic and copies ran while one was open for 9% -> 10% of each run, Pallas kernels for 0% -> 0%
where the time goes in v18:
time: 95.9 us; the launch traced here: 95 us
  waiting for transfers between devices  27.1 us (28%)
  starting transfers between devices  26.8 us (28%)
  local copies, waits for them, and re-layouts  16.1 us (17%)
  matrix products  14.2 us (15%)
  Pallas kernels  6.31 us (7%)
  other arithmetic  3.8 us (4%)
    dot_general x21, matrix products, conv_taps(): jnp.einsum('fhwc,cd->fhwd', stacked, kernel, preferred_element_type=jnp.f...  13.2 us
    ppermute x3, waiting for transfers between devices, halo_rows(): after = lax.ppermute(first, 'ha', down)  11.4 us
    ppermute x3, waiting for transfers between devices, gather_chip_rows(): ahead = lax.ppermute(ahead, 'ha', forward)  10.1 us
    ppermute x3, starting transfers between devices, halo_rows(): before = lax.ppermute(last, 'ha', up)  8.45 us
    ppermute x3, starting transfers between devices, halo_rows(): after = lax.ppermute(first, 'ha', down)  7.05 us
    pallas_call x1, Pallas kernels, attend(): pl.pallas_call(functools.partial(attention_kernel, scale), grid=(frames,)...  6.31 us
    slice x6, local copies, waits for them, and re-layouts, conv_taps(): kernel = weight[time_off, row_off].reshape(3 * in_channels, out_channels)  5.41 us
    ppermute x1, starting transfers between devices, per_device(): back = lax.ppermute(mixed_block[:, 1:2], 'ha', swap)  4.63 us
  transfers between devices with their start and end apart: 16, of which 11 were waited for; matrix products, arithmetic and copies ran while one was open for 10% of the time, Pallas kernels for 0%

profile of v18, /device:TPU:13, one launch (start us, length us, event | category | flops | bytes accessed | tf_op | source)
XLA Modules:
  0.0 95.0 jit_solution(4928899764270464879)
XLA Ops:
  0.0 0.7 collective-permute-start
  0.7 0.9 constant_dynamic-update-slice_fusion.9
  2.3 1.3 %collective-permute-start.2 = (bf16[1,2,128,384]{3,2,1,0:T(8,128)(2,1)S(1)}, bf16[1,2,128,384]{3,2,1,0:T(8,128)(2,1)S(1)}, u32[]{:S(2)}, u32[]{:S(2)}) collective-permute-start(bf16[1,2,128,384]{3,2,1,0:T(8,128)(2,1)S(1)} %pad_maximum_fusion.5), channel_id=1, source_target_pairs={{0,2},{1,3},{2,6},{3,7},{4,0},{5,1},{6,10},{7,11},{8,4},{9,5},{10,... | collective-permute-start | bytes 589832 | tf_op jit(solution)/shard_map/ppermute | solution.py:56
  3.8 1.0 %fusion.88.q_ref = bf16[1,256,384]{2,1,0:T(8,128)(2,1)} fusion(bf16[256,384]{1,0:T(8,128)(2,1)S(1)} %fusion.140, bf16[384,384]{1,0:T(8,128)(2,1)S(1)} %copy-done), kind=kOutput, calls=%fused_computation.107 | convolution fusion | flops 75595776 | bytes 688128 | tf_op jit(solution)/shard_map/ftc,cd->ftd/dot_general | solution.py:155
  4.8 3.4 %collective-permute-done.1 = bf16[1,2,128,384]{3,2,1,0:T(8,128)(2,1)S(1)} collective-permute-done((bf16[1,2,128,384]{3,2,1,0:T(8,128)(2,1)S(1)}, bf16[1,2,128,384]{3,2,1,0:T(8,128)(2,1)S(1)}, u32[]{:S(2)}, u32[]{:S(2)}) %collective-permute-start.1) | collective-permute-done | bytes 196640 | tf_op jit(solution)/shard_map/ppermute | solution.py:53
  8.4 1.3 %collective-permute-start.4 = (bf16[1,2,128,384]{3,2,1,0:T(8,128)(2,1)S(1)}, bf16[1,2,128,384]{3,2,1,0:T(8,128)(2,1)S(1)}, u32[]{:S(2)}, u32[]{:S(2)}) collective-permute-start(bf16[1,2,128,384]{3,2,1,0:T(8,128)(2,1)S(1)} %collective-permute-done.2), channel_id=1, source_target_pairs={{0,2},{1,3},{2,6},{3,7},{4,0},{5,1},{6,10},{7,11},{8,4},{9,5},{10,... | collective-permute-start | bytes 589832 | tf_op jit(solution)/shard_map/ppermute | solution.py:56
  9.7 3.6 %collective-permute-done.3 = bf16[1,2,128,384]{3,2,1,0:T(8,128)(2,1)S(1)} collective-permute-done((bf16[1,2,128,384]{3,2,1,0:T(8,128)(2,1)S(1)}, bf16[1,2,128,384]{3,2,1,0:T(8,128)(2,1)S(1)}, u32[]{:S(2)}, u32[]{:S(2)}) %collective-permute-start.3) | collective-permute-done | bytes 196640 | tf_op jit(solution)/shard_map/ppermute | solution.py:53
  13.6 1.3 %collective-permute-start.6 = (bf16[1,2,128,384]{3,2,1,0:T(8,128)(2,1)S(1)}, bf16[1,2,128,384]{3,2,1,0:T(8,128)(2,1)S(1)}, u32[]{:S(2)}, u32[]{:S(2)}) collective-permute-start(bf16[1,2,128,384]{3,2,1,0:T(8,128)(2,1)S(1)} %collective-permute-done.4), channel_id=1, source_target_pairs={{0,2},{1,3},{2,6},{3,7},{4,0},{5,1},{6,10},{7,11},{8,4},{9,5},{10,... | collective-permute-start | bytes 589832 | tf_op jit(solution)/shard_map/ppermute | solution.py:56
  14.9 3.0 %collective-permute-done.5 = bf16[1,2,128,384]{3,2,1,0:T(8,128)(2,1)S(1)} collective-permute-done((bf16[1,2,128,384]{3,2,1,0:T(8,128)(2,1)S(1)}, bf16[1,2,128,384]{3,2,1,0:T(8,128)(2,1)S(1)}, u32[]{:S(2)}, u32[]{:S(2)}) %collective-permute-start.5) | collective-permute-done | bytes 196640 | tf_op jit(solution)/shard_map/ppermute | solution.py:53
  18.2 1.3 %collective-permute-start.8 = (bf16[1,1,128,384]{3,2,1,0:T(8,128)(2,1)S(1)}, bf16[1,1,128,384]{3,2,1,0:T(8,128)(2,1)S(1)}, u32[]{:S(2)}, u32[]{:S(2)}) collective-permute-start(bf16[1,1,128,384]{3,2,1,0:T(8,128)(2,1)S(1)} %slice.476), channel_id=1, source_target_pairs={{0,2},{1,3},{2,6},{3,7},{4,0},{5,1},{6,10},{7,11},{8,4},{9,5},{10,... | collective-permute-start | bytes 294920 | tf_op jit(solution)/shard_map/ppermute | solution.py:50
  19.6 1.9 %collective-permute-done.7 = bf16[1,1,128,384]{3,2,1,0:T(8,128)(2,1)S(1)} collective-permute-done((bf16[1,1,128,384]{3,2,1,0:T(8,128)(2,1)S(1)}, bf16[1,1,128,384]{3,2,1,0:T(8,128)(2,1)S(1)}, u32[]{:S(2)}, u32[]{:S(2)}) %collective-permute-start.7) | collective-permute-done | bytes 98336 | tf_op jit(solution)/shard_map/ppermute | solution.py:49
  22.0 1.2 %copy-done.8 = bf16[1,16,128,384]{3,2,1,0:T(8,128)(2,1)} copy-done((bf16[1,16,128,384]{3,2,1,0:T(8,128)(2,1)}, bf16[1,16,128,384]{3,2,1,0:T(8,128)(2,1)S(1)}, u32[]{:S(2)}) %copy-start.8) | copy-done | bytes 1572888
  23.2 6.3 %shard_map.100 = bf16[1,256,384]{2,1,0:T(8,128)(2,1)} custom-call(bf16[1,256,384]{2,1,0:T(8,128)(2,1)} %fusion.88.q_ref, bf16[1,2048,384]{2,1,0:T(8,128)(2,1)} %bitcast.168, bf16[384,384]{1,0:T(8,128)(2,1)} %wk_ref.1, bf16[384,384]{1,0:T(8,128)(2,1)} %wv_ref.1, bf16[1,256,384]{2,1,0:T(8,128)(2,1)} %bitcast.166, bf16[384,384]{1,0:T(8,128)(2,1)} %wo_ref.1), custom_call_target="tpu_custom_call" | custom-call | flops 2013265920 | bytes 3047424 | tf_op jit(solution)/shard_map/pallas_call | solution.py:134
  29.5 1.0 %fusion.173 = (bf16[1,1,128,384]{3,2,0,1:T(8,128)(2,1)S(1)}, bf16[1,128,384]{2,1,0:T(8,128)(2,1)S(1)}, bf16[1,1,128,384]{3,2,0,1:T(8,128)(2,1)S(1)}) fusion(bf16[1,2,128,384]{3,2,0,1:T(8,128)(2,1)} %bitcast.167), kind=kLoop, calls=%fused_computation.244 | loop fusion | bytes 491520 | tf_op jit(solution)/shard_map/slice | solution.py:196
  30.5 4.6 %collective-permute-start.9 = (bf16[1,1,128,384]{3,2,0,1:T(8,128)(2,1)S(1)}, bf16[1,1,128,384]{3,2,0,1:T(8,128)(2,1)S(1)}, u32[]{:S(2)}, u32[]{:S(2)}) collective-permute-start(bf16[1,1,128,384]{3,2,0,1:T(8,128)(2,1)S(1)} %get-tuple-element.92), channel_id=1, source_target_pairs={{0,1},{1,0},{2,3},{3,2},{4,5},{5,4},{6,7},{7,6},{8,9},{9,8},{10,11... | collective-permute-start | bytes 294920 | tf_op jit(solution)/shard_map/ppermute | solution.py:195
  35.1 0.9 collective-permute-done.9
  36.5 4.4 %collective-permute-start.10 = (bf16[4,1,128,384]{3,2,0,1:T(8,128)(2,1)S(1)}, bf16[4,1,128,384]{3,2,0,1:T(8,128)(2,1)S(1)}, u32[]{:S(2)}, u32[]{:S(2)}) collective-permute-start(bf16[4,1,128,384]{3,2,0,1:T(8,128)(2,1)S(1)} %pad_maximum_fusion.4), channel_id=1, source_target_pairs={{0,1},{1,2},{2,3},{3,4},{4,5},{5,6},{6,7},{7,8},{8,9},{9,10},{10,1... | collective-permute-start | bytes 1179656 | tf_op jit(solution)/shard_map/ppermute | solution.py:18
  40.9 1.9 %collective-permute-start.11 = (bf16[4,1,128,384]{3,2,0,1:T(8,128)(2,1)S(1)}, bf16[4,1,128,384]{3,2,0,1:T(8,128)(2,1)S(1)}, u32[]{:S(2)}, u32[]{:S(2)}) collective-permute-start(bf16[4,1,128,384]{3,2,0,1:T(8,128)(2,1)S(1)} %pad_maximum_fusion.4), channel_id=1, source_target_pairs={{1,0},{2,1},{3,2},{4,3},{5,4},{6,5},{7,6},{8,7},{9,8},{10,9},{11,1... | collective-permute-start | bytes 1179656 | tf_op jit(solution)/shard_map/ppermute | solution.py:19
  42.8 3.9 %fusion.164 = (bf16[1,1,3,384,384]{4,3,2,1,0:T(8,128)(2,1)S(1)}, bf16[1,1,3,384,384]{4,3,2,1,0:T(8,128)(2,1)S(1)}, bf16[1,1,3,384,384]{4,3,2,1,0:T(8,128)(2,1)S(...) fusion(bf16[3,3,3,384,384]{4,3,2,1,0:T(8,128)(2,1)} %param.17), kind=kLoop, calls=%fused_computation.235 | loop fusion | bytes 15925248 | tf_op jit(solution)/shard_map/slice | solution.py:100
  46.8 4.1 %collective-permute-done.11 = bf16[4,1,128,384]{3,2,0,1:T(8,128)(2,1)S(1)} collective-permute-done((bf16[4,1,128,384]{3,2,0,1:T(8,128)(2,1)S(1)}, bf16[4,1,128,384]{3,2,0,1:T(8,128)(2,1)S(1)}, u32[]{:S(2)}, u32[]{:S(2)}) %collective-permute-start.11) | collective-permute-done | bytes 393248 | tf_op jit(solution)/shard_map/ppermute | solution.py:19
  51.2 0.7 fusion.168
  55.9 0.5 fusion.141
  56.4 1.9 %collective-permute-start.12 = (bf16[2,1,128,384]{3,2,0,1:T(8,128)(2,1)S(1)}, bf16[2,1,128,384]{3,2,0,1:T(8,128)(2,1)S(1)}, u32[]{:S(2)}, u32[]{:S(2)}) collective-permute-start(bf16[2,1,128,384]{3,2,0,1:T(8,128)(2,1)S(1)} %fusion.141), channel_id=1, source_target_pairs={{0,1},{1,2},{2,3},{3,4},{4,5},{5,6},{6,7},{7,8},{8,9},{9,10},{10,1... | collective-permute-start | bytes 589832 | tf_op jit(solution)/shard_map/ppermute | solution.py:18
  58.3 2.6 %collective-permute-start.13 = (bf16[2,1,128,384]{3,2,0,1:T(8,128)(2,1)S(1)}, bf16[2,1,128,384]{3,2,0,1:T(8,128)(2,1)S(1)}, u32[]{:S(2)}, u32[]{:S(2)}) collective-permute-start(bf16[2,1,128,384]{3,2,0,1:T(8,128)(2,1)S(1)} %fusion.141), channel_id=1, source_target_pairs={{1,0},{2,1},{3,2},{4,3},{5,4},{6,5},{7,6},{8,7},{9,8},{10,9},{11,1... | collective-permute-start | bytes 589832 | tf_op jit(solution)/shard_map/ppermute | solution.py:19
  61.5 1.1 %reshape.290 = bf16[1152,192,1,1]{0,1,2,3:T(8,128)(2,1)} reshape(bf16[1,1,3,384,192]{3,2,4,1,0:T(4,128)(2,1)S(1)} %copy.34) | data formatting | bytes 884736 | tf_op jit(solution)/shard_map/reshape;squeeze | solution.py:100
  64.1 2.1 %collective-permute-done.13 = bf16[2,1,128,384]{3,2,0,1:T(8,128)(2,1)S(1)} collective-permute-done((bf16[2,1,128,384]{3,2,0,1:T(8,128)(2,1)S(1)}, bf16[2,1,128,384]{3,2,0,1:T(8,128)(2,1)S(1)}, u32[]{:S(2)}, u32[]{:S(2)}) %collective-permute-start.13) | collective-permute-done | bytes 196640 | tf_op jit(solution)/shard_map/ppermute | solution.py:19
  66.4 0.6 broadcast_in_dim.4
  67.0 0.5 reshape.278
  67.6 0.8 pad_slice_fusion.9
  68.7 0.7 copy-done.6
  69.4 1.1 %fusion.6 = f32[2,2,256,192]{2,3,1,0:T(8,128)S(1)} fusion(bf16[2,1,258,384]{3,2,1,0:T(8,128)(2,1)S(1)} %pad_slice_fusion.10, bf16[2,2,256,384]{3,2,1,0:T(8,128)(2,1)S(1)} %get-tuple-element.83, bf16[2,2,256,384]{3,2,1,0:T(8,128)(2,1)S(1)} %get-tuple-element.82, bf16[1152,192,1,1]{0,1,2,3:T(8,128)(2,1)S(1)} %copy-done.6), kind=kOutput, calls=%fused_computation.13 | convolution fusion | flops 462422016 | bytes 3197952 | tf_op jit(solution)/shard_map/fhwc,cd->fhwd/dot_general | solution.py:101
  70.6 1.1 %fusion.28 = f32[2,2,256,192]{2,3,1,0:T(8,128)S(1)} fusion(f32[2,2,256,192]{2,3,1,0:T(8,128)S(1)} %fusion.6, bf16[2,2,256,384]{3,2,1,0:T(8,128)(2,1)S(1)} %get-tuple-element.73, bf16[2,2,256,384]{3,2,1,0:T(8,128)(2,1)S(1)} %get-tuple-element.76, bf16[2,2,256,384]{3,2,1,0:T(8,128)(2,1)S(1)} %get-tuple-element.77, bf16[1152,192,1,1]{0,1,2,3:T(8,128)(2,1)S(1)} %reshape.289), kind=kOutput, calls=%fused_computation.40 | convolution fusion | flops 460259328 | bytes 4374528 | tf_op jit(solution)/shard_map/fhwc,cd->fhwd/dot_general | solution.py:101
  71.7 1.2 %multiply_reduce_fusion = (f32[2,2,256]{2,1,0:T(2,128)S(1)}, f32[2,2,256,192]{2,3,1,0:T(8,128)S(1)}) fusion(f32[2,2,256,192]{2,3,1,0:T(8,128)S(1)} %fusion.28, bf16[1152,192,1,1]{0,1,2,3:T(8,128)(2,1)S(1)} %reshape.291, bf16[2,2,256,384]{3,2,1,0:T(8,128)(2,1)S(1)} %get-tuple-element.74, bf16[2,2,256,384]{3,2,1,0:T(8,128)(2,1)S(1)} %get-tuple-element.75, ...), kind=kOutput, calls=%fused_computation.119 | convolution fusion | flops 461044736 | bytes 4378624 | tf_op jit(solution)/shard_map/fhwc,cd->fhwd/dot_general | solution.py:101
  73.2 2.1 %collective-permute-start.14 = (bf16[4,1,256,192]{2,3,1,0:T(8,128)(2,1)S(1)}, bf16[4,1,256,192]{2,3,1,0:T(8,128)(2,1)S(1)}, u32[]{:S(2)}, u32[]{:S(2)}) collective-permute-start(bf16[4,1,256,192]{2,3,1,0:T(8,128)(2,1)S(1)} %get-tuple-element.80), channel_id=1, source_target_pairs={{0,1},{1,2},{2,3},{3,4},{4,5},{5,6},{6,7},{7,8},{8,9},{9,10},{10,1... | collective-permute-start | bytes 1179656 | tf_op jit(solution)/shard_map/ppermute | solution.py:18
  75.4 2.5 %collective-permute-start.15 = (bf16[4,1,256,192]{2,3,1,0:T(8,128)(2,1)S(1)}, bf16[4,1,256,192]{2,3,1,0:T(8,128)(2,1)S(1)}, u32[]{:S(2)}, u32[]{:S(2)}) collective-permute-start(bf16[4,1,256,192]{2,3,1,0:T(8,128)(2,1)S(1)} %get-tuple-element.81), channel_id=1, source_target_pairs={{1,0},{2,1},{3,2},{4,3},{5,4},{6,5},{7,6},{8,7},{9,8},{10,9},{11,1... | collective-permute-start | bytes 1179656 | tf_op jit(solution)/shard_map/ppermute | solution.py:19
  78.1 1.9 %collective-permute-done.14 = bf16[4,1,256,192]{2,3,1,0:T(8,128)(2,1)S(1)} collective-permute-done((bf16[4,1,256,192]{2,3,1,0:T(8,128)(2,1)S(1)}, bf16[4,1,256,192]{2,3,1,0:T(8,128)(2,1)S(1)}, u32[]{:S(2)}, u32[]{:S(2)}) %collective-permute-start.14) | collective-permute-done | bytes 393248 | tf_op jit(solution)/shard_map/ppermute | solution.py:18
  80.1 5.3 %collective-permute-done.15 = bf16[4,1,256,192]{2,3,1,0:T(8,128)(2,1)S(1)} collective-permute-done((bf16[4,1,256,192]{2,3,1,0:T(8,128)(2,1)S(1)}, bf16[4,1,256,192]{2,3,1,0:T(8,128)(2,1)S(1)}, u32[]{:S(2)}, u32[]{:S(2)}) %collective-permute-start.15) | collective-permute-done | bytes 393248 | tf_op jit(solution)/shard_map/ppermute | solution.py:19
  85.4 2.0 %select_maximum_fusion = bf16[4,4,258,192]{2,3,1,0:T(8,128)(2,1)S(1)} fusion(bf16[4,1,256,192]{2,3,1,0:T(8,128)(2,1)S(1)} %collective-permute-done.15, bf16[4,1,256,192]{2,3,1,0:T(8,128)(2,1)S(1)} %collective-permute-done.14, bf16[2,2,256,192]{2,3,1,0:T(8,128)(2,1)S(1)} %multiply_convert_fusion, bf16[2,2,256,192]{2,3,1,0:T(8,128)(2,1)S(1)} %copy-done.2), kind=kLoop, calls=%fused_computation.6 | loop fusion | flops 11888640 | bytes 3158016 | tf_op jit(solution)/shard_map/concatenate | solution.py:25
  87.3 1.7 %fusion.166 = (bf16[2,2,256,192]{2,3,1,0:T(8,128)(2,1)S(1)}, bf16[2,2,256,192]{2,3,1,0:T(8,128)(2,1)S(1)}, bf16[2,2,256,192]{2,3,1,0:T(8,128)(2,1)S(1)}, bf16[2,...) fusion(bf16[4,4,258,192]{2,3,1,0:T(8,128)(2,1)S(1)} %select_max, ...), kind=kLoop, calls=%fused_computation.237 | loop fusion | bytes 14155776 | tf_op jit(solution)/shard_map/slice | solution.py:98
  89.5 0.5 fusion.50
  90.0 0.5 convolution_add_fusion.7
  90.5 0.5 convolution_add_fusion.6
  91.0 0.5 convolution_add_fusion.5
  91.6 0.5 convolution_add_fusion.4
  92.1 0.5 convolution_add_fusion.3
  92.6 0.5 convolution_add_fusion.2
  93.1 0.5 convolution_add_fusion.1
  93.7 1.3 %fusion.40 = bf16[2,2,256,192]{2,3,1,0:T(8,128)(2,1)} fusion(f32[2,2,256,192]{2,3,1,0:T(8,128)S(1)} %get-tuple-element.94, f32[2,2,256,192]{2,3,1,0:T(8,128)S(1)} %convolution_add_fusion.1, bf16[576,192,1,1]{1,0,3,2:T(8,128)(2,1)S(1)} %bitcast.157, bf16[2,2,256,192]{2,3,1,0:T(8,128)(2,1)S(1)} %get-tuple-element.44, ...), kind=kOutput, calls=%fused_computation.48 | convolution fusion | flops 230621184 | bytes 3366912 | tf_op jit(solution)/shard_map/fhwc,cd->fhwd/dot_general | solution.py:101
  (74 shorter events, 10.3 us)
Async XLA Ops:
  0.0 3.8 %copy-start = (bf16[384,384]{1,0:T(8,128)(2,1)S(1)}, bf16[384,384]{1,0:T(8,128)(2,1)}, u32[]{:S(2)}) copy-start(bf16[384,384]{1,0:T(8,128)(2,1)} %param.13) | copy-start | bytes 884740
  0.0 2.0 %collective-permute-start = (bf16[2,1,128,384]{3,2,1,0:T(8,128)(2,1)}, bf16[2,1,128,384]{3,2,1,0:T(8,128)(2,1)S(1)}, u32[]{:S(2)}, u32[]{:S(2)}) collective-permute-start(bf16[2,1,128,384]{3,2,1,0:T(8,128)(2,1)} %param.10), channel_id=1, source_target_pairs={{0,1},{1,0},{2,3},{3,2},{4,5},{5,4},{6,7},{7,6},{8,9},{9,8},{10,11... | collective-permute-start | bytes 589832 | tf_op jit(solution)/shard_map/ppermute | solution.py:176
  2.0 16.1 %copy-start.7 = (bf16[1,2,128,384]{3,2,1,0:T(8,128)(2,1)}, bf16[1,2,128,384]{3,2,1,0:T(8,128)(2,1)S(1)}, u32[]{:S(2)}) copy-start(bf16[1,2,128,384]{3,2,1,0:T(8,128)(2,1)S(1)} %pad_maximum_fusion.5) | copy-start | bytes 589828
  2.0 6.2 %collective-permute-start.1 = (bf16[1,2,128,384]{3,2,1,0:T(8,128)(2,1)S(1)}, bf16[1,2,128,384]{3,2,1,0:T(8,128)(2,1)S(1)}, u32[]{:S(2)}, u32[]{:S(2)}) collective-permute-start(bf16[1,2,128,384]{3,2,1,0:T(8,128)(2,1)S(1)} %pad_maximum_fusion.5), channel_id=1, source_target_pairs={{0,4},{1,5},{2,0},{3,1},{4,8},{5,9},{6,2},{7,3},{8,12},{9,13},{10,... | collective-permute-start | bytes 589832 | tf_op jit(solution)/shard_map/ppermute | solution.py:53
  2.3 6.1 %collective-permute-start.2 = (bf16[1,2,128,384]{3,2,1,0:T(8,128)(2,1)S(1)}, bf16[1,2,128,384]{3,2,1,0:T(8,128)(2,1)S(1)}, u32[]{:S(2)}, u32[]{:S(2)}) collective-permute-start(bf16[1,2,128,384]{3,2,1,0:T(8,128)(2,1)S(1)} %pad_maximum_fusion.5), channel_id=1, source_target_pairs={{0,2},{1,3},{2,6},{3,7},{4,0},{5,1},{6,10},{7,11},{8,4},{9,5},{10,... | collective-permute-start | bytes 589832 | tf_op jit(solution)/shard_map/ppermute | solution.py:56
  8.2 5.2 %collective-permute-start.3 = (bf16[1,2,128,384]{3,2,1,0:T(8,128)(2,1)S(1)}, bf16[1,2,128,384]{3,2,1,0:T(8,128)(2,1)S(1)}, u32[]{:S(2)}, u32[]{:S(2)}) collective-permute-start(bf16[1,2,128,384]{3,2,1,0:T(8,128)(2,1)S(1)} %collective-permute-done.1), channel_id=1, source_target_pairs={{0,4},{1,5},{2,0},{3,1},{4,8},{5,9},{6,2},{7,3},{8,12},{9,13},{10,... | collective-permute-start | bytes 589832 | tf_op jit(solution)/shard_map/ppermute | solution.py:53
  8.4 5.2 %collective-permute-start.4 = (bf16[1,2,128,384]{3,2,1,0:T(8,128)(2,1)S(1)}, bf16[1,2,128,384]{3,2,1,0:T(8,128)(2,1)S(1)}, u32[]{:S(2)}, u32[]{:S(2)}) collective-permute-start(bf16[1,2,128,384]{3,2,1,0:T(8,128)(2,1)S(1)} %collective-permute-done.2), channel_id=1, source_target_pairs={{0,2},{1,3},{2,6},{3,7},{4,0},{5,1},{6,10},{7,11},{8,4},{9,5},{10,... | collective-permute-start | bytes 589832 | tf_op jit(solution)/shard_map/ppermute | solution.py:56
  13.4 4.5 %collective-permute-start.5 = (bf16[1,2,128,384]{3,2,1,0:T(8,128)(2,1)S(1)}, bf16[1,2,128,384]{3,2,1,0:T(8,128)(2,1)S(1)}, u32[]{:S(2)}, u32[]{:S(2)}) collective-permute-start(bf16[1,2,128,384]{3,2,1,0:T(8,128)(2,1)S(1)} %collective-permute-done.3), channel_id=1, source_target_pairs={{0,4},{1,5},{2,0},{3,1},{4,8},{5,9},{6,2},{7,3},{8,12},{9,13},{10,... | collective-permute-start | bytes 589832 | tf_op jit(solution)/shard_map/ppermute | solution.py:53
  13.6 4.6 %collective-permute-start.6 = (bf16[1,2,128,384]{3,2,1,0:T(8,128)(2,1)S(1)}, bf16[1,2,128,384]{3,2,1,0:T(8,128)(2,1)S(1)}, u32[]{:S(2)}, u32[]{:S(2)}) collective-permute-start(bf16[1,2,128,384]{3,2,1,0:T(8,128)(2,1)S(1)} %collective-permute-done.4), channel_id=1, source_target_pairs={{0,2},{1,3},{2,6},{3,7},{4,0},{5,1},{6,10},{7,11},{8,4},{9,5},{10,... | collective-permute-start | bytes 589832 | tf_op jit(solution)/shard_map/ppermute | solution.py:56
  17.9 3.6 %collective-permute-start.7 = (bf16[1,1,128,384]{3,2,1,0:T(8,128)(2,1)S(1)}, bf16[1,1,128,384]{3,2,1,0:T(8,128)(2,1)S(1)}, u32[]{:S(2)}, u32[]{:S(2)}) collective-permute-start(bf16[1,1,128,384]{3,2,1,0:T(8,128)(2,1)S(1)} %slice.475), channel_id=1, source_target_pairs={{0,4},{1,5},{2,0},{3,1},{4,8},{5,9},{6,2},{7,3},{8,12},{9,13},{10,... | collective-permute-start | bytes 294920 | tf_op jit(solution)/shard_map/ppermute | solution.py:49
  18.2 3.8 %collective-permute-start.8 = (bf16[1,1,128,384]{3,2,1,0:T(8,128)(2,1)S(1)}, bf16[1,1,128,384]{3,2,1,0:T(8,128)(2,1)S(1)}, u32[]{:S(2)}, u32[]{:S(2)}) collective-permute-start(bf16[1,1,128,384]{3,2,1,0:T(8,128)(2,1)S(1)} %slice.476), channel_id=1, source_target_pairs={{0,2},{1,3},{2,6},{3,7},{4,0},{5,1},{6,10},{7,11},{8,4},{9,5},{10,... | collective-permute-start | bytes 294920 | tf_op jit(solution)/shard_map/ppermute | solution.py:50
  22.0 1.2 %copy-start.8 = (bf16[1,16,128,384]{3,2,1,0:T(8,128)(2,1)}, bf16[1,16,128,384]{3,2,1,0:T(8,128)(2,1)S(1)}, u32[]{:S(2)}) copy-start(bf16[1,16,128,384]{3,2,1,0:T(8,128)(2,1)S(1)} %constant_dynamic-update-slice_fusion) | copy-start | bytes 4718596
  23.2 13.2 %copy-start.4 = (bf16[2,1,128,384]{3,2,1,0:T(8,128)(2,1)S(1)}, bf16[2,1,128,384]{3,2,1,0:T(8,128)(2,1)}, u32[]{:S(2)}) copy-start(bf16[2,1,128,384]{3,2,1,0:T(8,128)(2,1)} %param.11) | copy-start | bytes 589828
  30.5 5.6 %collective-permute-start.9 = (bf16[1,1,128,384]{3,2,0,1:T(8,128)(2,1)S(1)}, bf16[1,1,128,384]{3,2,0,1:T(8,128)(2,1)S(1)}, u32[]{:S(2)}, u32[]{:S(2)}) collective-permute-start(bf16[1,1,128,384]{3,2,0,1:T(8,128)(2,1)S(1)} %get-tuple-element.92), channel_id=1, source_target_pairs={{0,1},{1,0},{2,3},{3,2},{4,5},{5,4},{6,7},{7,6},{8,9},{9,8},{10,11... | collective-permute-start | bytes 294920 | tf_op jit(solution)/shard_map/ppermute | solution.py:195
  36.5 10.3 %collective-permute-start.10 = (bf16[4,1,128,384]{3,2,0,1:T(8,128)(2,1)S(1)}, bf16[4,1,128,384]{3,2,0,1:T(8,128)(2,1)S(1)}, u32[]{:S(2)}, u32[]{:S(2)}) collective-permute-start(bf16[4,1,128,384]{3,2,0,1:T(8,128)(2,1)S(1)} %pad_maximum_fusion.4), channel_id=1, source_target_pairs={{0,1},{1,2},{2,3},{3,4},{4,5},{5,6},{6,7},{7,8},{8,9},{9,10},{10,1... | collective-permute-start | bytes 1179656 | tf_op jit(solution)/shard_map/ppermute | solution.py:18
  40.9 10.0 %collective-permute-start.11 = (bf16[4,1,128,384]{3,2,0,1:T(8,128)(2,1)S(1)}, bf16[4,1,128,384]{3,2,0,1:T(8,128)(2,1)S(1)}, u32[]{:S(2)}, u32[]{:S(2)}) collective-permute-start(bf16[4,1,128,384]{3,2,0,1:T(8,128)(2,1)S(1)} %pad_maximum_fusion.4), channel_id=1, source_target_pairs={{1,0},{2,1},{3,2},{4,3},{5,4},{6,5},{7,6},{8,7},{9,8},{10,9},{11,1... | collective-permute-start | bytes 1179656 | tf_op jit(solution)/shard_map/ppermute | solution.py:19
  55.9 5.0 %copy-start.5 = (bf16[3,3,384,192]{2,3,1,0:T(8,128)(2,1)S(1)}, bf16[3,3,384,192]{2,3,1,0:T(8,128)(2,1)}, u32[]{:S(2)}) copy-start(bf16[3,3,384,192]{2,3,1,0:T(8,128)(2,1)} %param.18) | copy-start | bytes 3981316
  56.4 7.8 %collective-permute-start.12 = (bf16[2,1,128,384]{3,2,0,1:T(8,128)(2,1)S(1)}, bf16[2,1,128,384]{3,2,0,1:T(8,128)(2,1)S(1)}, u32[]{:S(2)}, u32[]{:S(2)}) collective-permute-start(bf16[2,1,128,384]{3,2,0,1:T(8,128)(2,1)S(1)} %fusion.141), channel_id=1, source_target_pairs={{0,1},{1,2},{2,3},{3,4},{4,5},{5,6},{6,7},{7,8},{8,9},{9,10},{10,1... | collective-permute-start | bytes 589832 | tf_op jit(solution)/shard_map/ppermute | solution.py:18
  58.3 7.9 %collective-permute-start.13 = (bf16[2,1,128,384]{3,2,0,1:T(8,128)(2,1)S(1)}, bf16[2,1,128,384]{3,2,0,1:T(8,128)(2,1)S(1)}, u32[]{:S(2)}, u32[]{:S(2)}) collective-permute-start(bf16[2,1,128,384]{3,2,0,1:T(8,128)(2,1)S(1)} %fusion.141), channel_id=1, source_target_pairs={{1,0},{2,1},{3,2},{4,3},{5,4},{6,5},{7,6},{8,7},{9,8},{10,9},{11,1... | collective-permute-start | bytes 589832 | tf_op jit(solution)/shard_map/ppermute | solution.py:19
  68.4 1.0 %copy-start.6 = (bf16[1152,192,1,1]{0,1,2,3:T(8,128)(2,1)S(1)}, bf16[1152,192,1,1]{0,1,2,3:T(8,128)(2,1)}, u32[]{:S(2)}) copy-start(bf16[1152,192,1,1]{0,1,2,3:T(8,128)(2,1)} %reshape.290) | copy-start | bytes 1327108
  71.7 1.4 %copy-start.2 = (bf16[2,2,256,192]{2,3,1,0:T(8,128)(2,1)S(1)}, bf16[2,2,256,192]{2,3,1,0:T(8,128)(2,1)}, u32[]{:S(2)}) copy-start(bf16[2,2,256,192]{2,3,1,0:T(8,128)(2,1)} %param.12) | copy-start | bytes 1179652
  72.9 5.0 %copy-start.3 = (bf16[3,3,3,192,192]{4,3,2,1,0:T(8,128)(2,1)S(1)}, bf16[3,3,3,192,192]{4,3,2,1,0:T(8,128)(2,1)}, u32[]{:S(2)}) copy-start(bf16[3,3,3,192,192]{4,3,2,1,0:T(8,128)(2,1)} %param.19) | copy-start | bytes 5971972
  73.2 6.8 %collective-permute-start.14 = (bf16[4,1,256,192]{2,3,1,0:T(8,128)(2,1)S(1)}, bf16[4,1,256,192]{2,3,1,0:T(8,128)(2,1)S(1)}, u32[]{:S(2)}, u32[]{:S(2)}) collective-permute-start(bf16[4,1,256,192]{2,3,1,0:T(8,128)(2,1)S(1)} %get-tuple-element.80), channel_id=1, source_target_pairs={{0,1},{1,2},{2,3},{3,4},{4,5},{5,6},{6,7},{7,8},{8,9},{9,10},{10,1... | collective-permute-start | bytes 1179656 | tf_op jit(solution)/shard_map/ppermute | solution.py:18
  75.4 10.0 %collective-permute-start.15 = (bf16[4,1,256,192]{2,3,1,0:T(8,128)(2,1)S(1)}, bf16[4,1,256,192]{2,3,1,0:T(8,128)(2,1)S(1)}, u32[]{:S(2)}, u32[]{:S(2)}) collective-permute-start(bf16[4,1,256,192]{2,3,1,0:T(8,128)(2,1)S(1)} %get-tuple-element.81), channel_id=1, source_target_pairs={{1,0},{2,1},{3,2},{4,3},{5,4},{6,5},{7,6},{8,7},{9,8},{10,9},{11,1... | collective-permute-start | bytes 1179656 | tf_op jit(solution)/shard_map/ppermute | solution.py:19
  93.7 1.3 %copy-start.1 = (bf16[384,384]{1,0:T(8,128)(2,1)S(1)}, bf16[384,384]{1,0:T(8,128)(2,1)}, u32[]{:S(2)}) copy-start(bf16[384,384]{1,0:T(8,128)(2,1)} %param.13) | copy-start | bytes 884740

commit v19 on v18

--- a/solution.py
+++ b/solution.py
@@ -76,6 +76,30 @@
 def rms_scale(tensor):
     widened = tensor.astype(jnp.float32)
     return widened * lax.rsqrt(jnp.mean(widened * widened, axis=-1, keepdims=True) + 1e-06)
+
+
+def conv_pieces(x, weight, time_taps):
+    before, after = halo_rows(x, 1, 1)
+    pieces = [before] + [x[:, i : i + 1] for i in range(x.shape[1])] + [after]
+    frames_out = x.shape[0] - time_taps + 1
+    height_out = x.shape[1]
+    width_out = x.shape[2]
+    in_channels = weight.shape[-2]
+    result = None
+    for time_off in range(time_taps):
+        for row_off in range(3):
+            window = jnp.concatenate(
+                [p[time_off : time_off + frames_out] for p in pieces[row_off : row_off + height_out]],
+                axis=1,
+            )
+            window = jnp.pad(window, ((0, 0), (0, 0), (1, 1), (0, 0)))
+            stacked = jnp.concatenate(
+                [window[:, :, col_off : col_off + width_out] for col_off in range(3)], axis=-1
+            )
+            kernel = weight[time_off, row_off].reshape(3 * in_channels, weight.shape[-1])
+            term = jnp.einsum("fhwc,cd->fhwd", stacked, kernel, preferred_element_type=jnp.float32)
+            result = term if result is None else result + term
+    return result
 
 
 def conv_taps(padded, weight, time_taps, rows=None):
@@ -201,8 +225,7 @@
     )
     first_in = jax.nn.silu(rms_scale(mixed)).astype(jnp.bfloat16)
     first_stack = jnp.concatenate([first_cache, first_in], axis=0)
-    first_padded = extended(first_stack, 1, 1)
-    block_out = (mixed.astype(jnp.float32) + conv_taps(first_padded, w_first, 3)).astype(
+    block_out = (mixed.astype(jnp.float32) + conv_pieces(first_stack, w_first, 3)).astype(
         jnp.bfloat16
     )
     block_padded = extended(block_out, 1, 1)
@@ -212,8 +235,7 @@
     )
     second_in = jax.nn.silu(rms_scale(upsampled)).astype(jnp.bfloat16)
     second_stack = jnp.concatenate([second_cache, second_in], axis=0)
-    second_padded = extended(second_stack, 1, 1)
-    return (upsampled.astype(jnp.float32) + conv_taps(second_padded, w_second, 3)).astype(
+    return (upsampled.astype(jnp.float32) + conv_pieces(second_stack, w_second, 3)).astype(
         jnp.bfloat16
     )
 

time: 95.9 us -> 118 us (1.23)
  local copies, waits for them, and re-layouts: 16.1 us -> 30.6 us
  starting transfers between devices: 26.8 us -> 31.4 us
  waiting for transfers between devices: 27.1 us -> 28.6 us
    unnamed x27 -> x71, local copies, waits for them, and re-layouts: 3.07 us -> 13.7 us
    dot_general x21 -> x3, matrix products: 13.2 us -> 3.46 us  [conv_taps(): jnp.einsum('fhwc,cd->fhwd', stacked, kernel, preferred_element_type=jnp.f...]
    dot_general x0 -> x18, matrix products: none -> 9.7 us  [conv_pieces(): jnp.einsum('fhwc,cd->fhwd', stacked, kernel, preferred_element_type=jnp.f...]
    slice x0 -> x18, local copies, waits for them, and re-layouts: none -> 9.26 us  [the longest x2 7.11 us: conv_pieces(): weight[time_off, row_off].reshape(3 * in_channels, weight.shape[-1])]
    ppermute x3, starting transfers between devices: 8.45 us -> 13.9 us  [halo_rows(): before = lax.ppermute(last, 'ha', up)]
    slice x6 -> x4, local copies, waits for them, and re-layouts: 5.41 us -> 1.28 us  [conv_taps(): kernel = weight[time_off, row_off].reshape(3 * in_channels, out_channels)]
    slice x6 -> x1, local copies, waits for them, and re-layouts: 3.5 us -> 0.79 us  [conv_taps(): window[:, :, col_off:col_off + width_out]]
    concatenate x4 -> x1, other arithmetic: 2.54 us -> 0.08 us  [extended(): return jnp.concatenate([before, x, after], axis=dim)]
  transfers between devices with their start and end apart: 16 -> 16, of which waited for: 11 -> 11; matrix products, arithmetic and copies ran while one was open for 10% -> 13% of each run, Pallas kernels for 0% -> 0%
where the time goes in v19:
time: 118 us; the launch traced here: 117 us
  starting transfers between devices  31.4 us (27%)
  local copies, waits for them, and re-layouts  30.6 us (26%)
  waiting for transfers between devices  28.6 us (24%)
  matrix products  14.1 us (12%)
  Pallas kernels  6.27 us (5%)
  other arithmetic  4.75 us (4%)
    ppermute x3, starting transfers between devices, halo_rows(): before = lax.ppermute(last, 'ha', up)  13.9 us
    unnamed x71, local copies, waits for them, and re-layouts  13.7 us
    ppermute x3, waiting for transfers between devices, halo_rows(): after = lax.ppermute(first, 'ha', down)  12.4 us
    ppermute x3, waiting for transfers between devices, gather_chip_rows(): ahead = lax.ppermute(ahead, 'ha', forward)  10.2 us
    dot_general x18, matrix products, conv_pieces(): jnp.einsum('fhwc,cd->fhwd', stacked, kernel, preferred_element_type=jnp.f...  9.7 us
    slice x2, local copies, waits for them, and re-layouts, conv_pieces(): weight[time_off, row_off].reshape(3 * in_channels, weight.shape[-1])  7.11 us
    ppermute x3, starting transfers between devices, halo_rows(): after = lax.ppermute(first, 'ha', down)  6.29 us
    pallas_call x1, Pallas kernels, attend(): pl.pallas_call(functools.partial(attention_kernel, scale), grid=(frames,)...  6.27 us
  transfers between devices with their start and end apart: 16, of which 11 were waited for; matrix products, arithmetic and copies ran while one was open for 13% of the time, Pallas kernels for 0%

profile of v19, /device:TPU:13, one launch (start us, length us, event | category | flops | bytes accessed | tf_op | source)
XLA Modules:
  0.0 116.5 jit_solution(5245797941231527767)
XLA Ops:
  0.0 0.7 collective-permute-start
  0.7 0.9 constant_dynamic-update-slice_fusion.9
  2.4 1.3 %collective-permute-start.2 = (bf16[1,2,128,384]{3,2,1,0:T(8,128)(2,1)S(1)}, bf16[1,2,128,384]{3,2,1,0:T(8,128)(2,1)S(1)}, u32[]{:S(2)}, u32[]{:S(2)}) collective-permute-start(bf16[1,2,128,384]{3,2,1,0:T(8,128)(2,1)S(1)} %pad_maximum_fusion.4), channel_id=1, source_target_pairs={{0,2},{1,3},{2,6},{3,7},{4,0},{5,1},{6,10},{7,11},{8,4},{9,5},{10,... | collective-permute-start | bytes 589832 | tf_op jit(solution)/shard_map/ppermute | solution.py:56
  3.8 1.0 fusion.92.q_ref
  4.8 3.6 %collective-permute-done.1 = bf16[1,2,128,384]{3,2,1,0:T(8,128)(2,1)S(1)} collective-permute-done((bf16[1,2,128,384]{3,2,1,0:T(8,128)(2,1)S(1)}, bf16[1,2,128,384]{3,2,1,0:T(8,128)(2,1)S(1)}, u32[]{:S(2)}, u32[]{:S(2)}) %collective-permute-start.1) | collective-permute-done | bytes 196640 | tf_op jit(solution)/shard_map/ppermute | solution.py:53
  8.5 1.3 %collective-permute-start.4 = (bf16[1,2,128,384]{3,2,1,0:T(8,128)(2,1)S(1)}, bf16[1,2,128,384]{3,2,1,0:T(8,128)(2,1)S(1)}, u32[]{:S(2)}, u32[]{:S(2)}) collective-permute-start(bf16[1,2,128,384]{3,2,1,0:T(8,128)(2,1)S(1)} %collective-permute-done.2), channel_id=1, source_target_pairs={{0,2},{1,3},{2,6},{3,7},{4,0},{5,1},{6,10},{7,11},{8,4},{9,5},{10,... | collective-permute-start | bytes 589832 | tf_op jit(solution)/shard_map/ppermute | solution.py:56
  9.9 3.6 %collective-permute-done.3 = bf16[1,2,128,384]{3,2,1,0:T(8,128)(2,1)S(1)} collective-permute-done((bf16[1,2,128,384]{3,2,1,0:T(8,128)(2,1)S(1)}, bf16[1,2,128,384]{3,2,1,0:T(8,128)(2,1)S(1)}, u32[]{:S(2)}, u32[]{:S(2)}) %collective-permute-start.3) | collective-permute-done | bytes 196640 | tf_op jit(solution)/shard_map/ppermute | solution.py:53
  13.7 1.3 %collective-permute-start.6 = (bf16[1,2,128,384]{3,2,1,0:T(8,128)(2,1)S(1)}, bf16[1,2,128,384]{3,2,1,0:T(8,128)(2,1)S(1)}, u32[]{:S(2)}, u32[]{:S(2)}) collective-permute-start(bf16[1,2,128,384]{3,2,1,0:T(8,128)(2,1)S(1)} %collective-permute-done.4), channel_id=1, source_target_pairs={{0,2},{1,3},{2,6},{3,7},{4,0},{5,1},{6,10},{7,11},{8,4},{9,5},{10,... | collective-permute-start | bytes 589832 | tf_op jit(solution)/shard_map/ppermute | solution.py:56
  15.1 3.0 %collective-permute-done.5 = bf16[1,2,128,384]{3,2,1,0:T(8,128)(2,1)S(1)} collective-permute-done((bf16[1,2,128,384]{3,2,1,0:T(8,128)(2,1)S(1)}, bf16[1,2,128,384]{3,2,1,0:T(8,128)(2,1)S(1)}, u32[]{:S(2)}, u32[]{:S(2)}) %collective-permute-start.5) | collective-permute-done | bytes 196640 | tf_op jit(solution)/shard_map/ppermute | solution.py:53
  18.3 1.3 %collective-permute-start.8 = (bf16[1,1,128,384]{3,2,1,0:T(8,128)(2,1)S(1)}, bf16[1,1,128,384]{3,2,1,0:T(8,128)(2,1)S(1)}, u32[]{:S(2)}, u32[]{:S(2)}) collective-permute-start(bf16[1,1,128,384]{3,2,1,0:T(8,128)(2,1)S(1)} %slice.423), channel_id=1, source_target_pairs={{0,2},{1,3},{2,6},{3,7},{4,0},{5,1},{6,10},{7,11},{8,4},{9,5},{10,... | collective-permute-start | bytes 294920 | tf_op jit(solution)/shard_map/ppermute | solution.py:50
  19.7 2.0 %collective-permute-done.7 = bf16[1,1,128,384]{3,2,1,0:T(8,128)(2,1)S(1)} collective-permute-done((bf16[1,1,128,384]{3,2,1,0:T(8,128)(2,1)S(1)}, bf16[1,1,128,384]{3,2,1,0:T(8,128)(2,1)S(1)}, u32[]{:S(2)}, u32[]{:S(2)}) %collective-permute-start.7) | collective-permute-done | bytes 98336 | tf_op jit(solution)/shard_map/ppermute | solution.py:49
  22.2 1.2 %copy-done.30 = bf16[1,16,128,384]{3,2,1,0:T(8,128)(2,1)} copy-done((bf16[1,16,128,384]{3,2,1,0:T(8,128)(2,1)}, bf16[1,16,128,384]{3,2,1,0:T(8,128)(2,1)S(1)}, u32[]{:S(2)}) %copy-start.30) | copy-done | bytes 1572888
  23.3 6.3 %shard_map.100 = bf16[1,256,384]{2,1,0:T(8,128)(2,1)} custom-call(bf16[1,256,384]{2,1,0:T(8,128)(2,1)} %fusion.92.q_ref, bf16[1,2048,384]{2,1,0:T(8,128)(2,1)} %bitcast.168, bf16[384,384]{1,0:T(8,128)(2,1)} %wk_ref.1, bf16[384,384]{1,0:T(8,128)(2,1)} %wv_ref.1, bf16[1,256,384]{2,1,0:T(8,128)(2,1)} %bitcast.166, bf16[384,384]{1,0:T(8,128)(2,1)} %wo_ref.1), custom_call_target="tpu_custom_call" | custom-call | flops 2013265920 | bytes 3047424 | tf_op jit(solution)/shard_map/pallas_call | solution.py:158
  29.6 1.6 %fusion.183 = (bf16[1,1,128,384]{3,2,0,1:T(8,128)(2,1)S(1)}, bf16[1,128,384]{2,1,0:T(8,128)(2,1)}, bf16[1,1,128,384]{3,2,0,1:T(8,128)(2,1)S(1)}) fusion(bf16[1,2,128,384]{3,2,0,1:T(8,128)(2,1)} %bitcast.167), kind=kLoop, calls=%fused_computation.281 | loop fusion | bytes 491520 | tf_op jit(solution)/shard_map/slice | solution.py:220
  31.2 4.6 %collective-permute-start.9 = (bf16[1,1,128,384]{3,2,0,1:T(8,128)(2,1)S(1)}, bf16[1,1,128,384]{3,2,0,1:T(8,128)(2,1)S(1)}, u32[]{:S(2)}, u32[]{:S(2)}) collective-permute-start(bf16[1,1,128,384]{3,2,0,1:T(8,128)(2,1)S(1)} %get-tuple-element.98), channel_id=1, source_target_pairs={{0,1},{1,0},{2,3},{3,2},{4,5},{5,4},{6,7},{7,6},{8,9},{9,8},{10,11... | collective-permute-start | bytes 294920 | tf_op jit(solution)/shard_map/ppermute | solution.py:219
  35.8 5.7 %fusion.170 = (bf16[1,1,3,384,384]{4,3,2,1,0:T(8,128)(2,1)}, bf16[1,1,3,384,384]{4,3,2,1,0:T(8,128)(2,1)}, bf16[1,1,3,384,384]{4,3,2,1,0:T(8,128)(2,1)}, bf16[1,...) fusion(bf16[3,3,3,384,384]{4,3,2,1,0:T(8,128)(2,1)} %param.17), kind=kLoop, calls=%fused_computation.268 | loop fusion | bytes 15925248 | tf_op jit(solution)/shard_map/slice | solution.py:99
  41.8 0.8 pad_maximum_fusion.2
  42.6 4.0 %collective-permute-start.10 = (bf16[4,1,128,384]{3,2,0,1:T(8,128)(2,1)}, bf16[4,1,128,384]{3,2,0,1:T(8,128)(2,1)S(1)}, u32[]{:S(2)}, u32[]{:S(2)}) collective-permute-start(bf16[4,1,128,384]{3,2,0,1:T(8,128)(2,1)} %pad_maximum_fusion.2), channel_id=1, source_target_pairs={{0,1},{1,2},{2,3},{3,4},{4,5},{5,6},{6,7},{7,8},{8,9},{9,10},{10,1... | collective-permute-start | bytes 1179656 | tf_op jit(solution)/shard_map/ppermute | solution.py:18
  47.2 1.2 %reshape.290 = bf16[1152,192,1,1]{0,1,2,3:T(8,128)(2,1)} reshape(bf16[1,1,3,384,192]{3,2,4,1,0:T(4,128)(2,1)S(1)} %copy.36) | data formatting | bytes 884736 | tf_op jit(solution)/shard_map/reshape;squeeze | solution.py:124
  48.8 1.1 reshape.289
  50.7 2.1 %collective-permute-start.11 = (bf16[4,1,128,384]{3,2,0,1:T(8,128)(2,1)}, bf16[4,1,128,384]{3,2,0,1:T(8,128)(2,1)S(1)}, u32[]{:S(2)}, u32[]{:S(2)}) collective-permute-start(bf16[4,1,128,384]{3,2,0,1:T(8,128)(2,1)} %pad_maximum_fusion.2), channel_id=1, source_target_pairs={{1,0},{2,1},{3,2},{4,3},{5,4},{6,5},{7,6},{8,7},{9,8},{10,9},{11,1... | collective-permute-start | bytes 1179656 | tf_op jit(solution)/shard_map/ppermute | solution.py:19
  53.2 7.6 %collective-permute-done.11 = bf16[4,1,128,384]{3,2,0,1:T(8,128)(2,1)S(1)} collective-permute-done((bf16[4,1,128,384]{3,2,0,1:T(8,128)(2,1)}, bf16[4,1,128,384]{3,2,0,1:T(8,128)(2,1)S(1)}, u32[]{:S(2)}, u32[]{:S(2)}) %collective-permute-start.11) | collective-permute-done | bytes 393248 | tf_op jit(solution)/shard_map/ppermute | solution.py:19
  61.4 0.8 copy-done.13
  62.7 0.7 copy-done.12
  63.9 0.7 copy-done.11
  65.0 0.7 copy-done.10
  66.2 0.7 copy-done.9
  67.4 0.7 copy-done.8
  68.5 0.7 copy-done.7
  69.7 0.7 copy-done.6
  70.9 0.7 copy-done.5
  72.1 2.1 %collective-permute-start.13 = (bf16[2,1,128,384]{3,2,0,1:T(8,128)(2,1)S(1)}, bf16[2,1,128,384]{3,2,0,1:T(8,128)(2,1)S(1)}, u32[]{:S(2)}, u32[]{:S(2)}) collective-permute-start(bf16[2,1,128,384]{3,2,0,1:T(8,128)(2,1)S(1)} %fusion.146), channel_id=1, source_target_pairs={{1,0},{2,1},{3,2},{4,3},{5,4},{6,5},{7,6},{8,7},{9,8},{10,9},{11,1... | collective-permute-start | bytes 589832 | tf_op jit(solution)/shard_map/ppermute | solution.py:19
  74.1 4.5 %collective-permute-start.12 = (bf16[2,1,128,384]{3,2,0,1:T(8,128)(2,1)S(1)}, bf16[2,1,128,384]{3,2,0,1:T(8,128)(2,1)S(1)}, u32[]{:S(2)}, u32[]{:S(2)}) collective-permute-start(bf16[2,1,128,384]{3,2,0,1:T(8,128)(2,1)S(1)} %fusion.146), channel_id=1, source_target_pairs={{0,1},{1,2},{2,3},{3,4},{4,5},{5,6},{6,7},{7,8},{8,9},{9,10},{10,1... | collective-permute-start | bytes 589832 | tf_op jit(solution)/shard_map/ppermute | solution.py:18
  78.7 1.4 %fusion.171 = (bf16[1,1,3,192,192]{4,3,2,1,0:T(8,128)(2,1)S(1)}, bf16[1,1,3,192,192]{4,3,2,1,0:T(8,128)(2,1)}, bf16[1,1,3,192,192]{4,3,2,1,0:T(8,128)(2,1)}, bf1...) fusion(bf16[3,3,3,192,192]{4,3,2,1,0:T(8,128)(2,1)S(1)} %copy-d, ...), kind=kLoop, calls=%fused_computation.269 | loop fusion | bytes 3981312 | tf_op jit(solution)/shard_map/slice | solution.py:99
  80.2 1.1 collective-permute-done.12
  81.4 0.6 broadcast_in_dim.4
  82.6 0.8 pad_slice_fusion.13
  83.8 0.7 copy-done.17
  84.5 1.1 fusion.1
  85.6 1.1 fusion.23
  86.8 1.2 multiply_reduce_fusion
  88.2 0.7 copy-done.2
  89.0 0.6 pad_slice_fusion.18
  89.7 5.3 %collective-permute-start.14 = (bf16[4,1,256,192]{2,3,1,0:T(8,128)(2,1)S(1)}, bf16[4,1,256,192]{2,3,1,0:T(8,128)(2,1)S(1)}, u32[]{:S(2)}, u32[]{:S(2)}) collective-permute-start(bf16[4,1,256,192]{2,3,1,0:T(8,128)(2,1)S(1)} %get-tuple-element.39), channel_id=1, source_target_pairs={{0,1},{1,2},{2,3},{3,4},{4,5},{5,6},{6,7},{7,8},{8,9},{9,10},{10,1... | collective-permute-start | bytes 1179656 | tf_op jit(solution)/shard_map/ppermute | solution.py:18
  95.0 2.1 %collective-permute-start.15 = (bf16[4,1,256,192]{2,3,1,0:T(8,128)(2,1)S(1)}, bf16[4,1,256,192]{2,3,1,0:T(8,128)(2,1)S(1)}, u32[]{:S(2)}, u32[]{:S(2)}) collective-permute-start(bf16[4,1,256,192]{2,3,1,0:T(8,128)(2,1)S(1)} %get-tuple-element.38), channel_id=1, source_target_pairs={{1,0},{2,1},{3,2},{4,3},{5,4},{6,5},{7,6},{8,7},{9,8},{10,9},{11,1... | collective-permute-start | bytes 1179656 | tf_op jit(solution)/shard_map/ppermute | solution.py:19
  97.5 2.2 %collective-permute-done.14 = bf16[4,1,256,192]{2,3,1,0:T(8,128)(2,1)S(1)} collective-permute-done((bf16[4,1,256,192]{2,3,1,0:T(8,128)(2,1)S(1)}, bf16[4,1,256,192]{2,3,1,0:T(8,128)(2,1)S(1)}, u32[]{:S(2)}, u32[]{:S(2)}) %collective-permute-start.14) | collective-permute-done | bytes 393248 | tf_op jit(solution)/shard_map/ppermute | solution.py:18
  100.3 4.7 %collective-permute-done.15 = bf16[4,1,256,192]{2,3,1,0:T(8,128)(2,1)S(1)} collective-permute-done((bf16[4,1,256,192]{2,3,1,0:T(8,128)(2,1)S(1)}, bf16[4,1,256,192]{2,3,1,0:T(8,128)(2,1)S(1)}, u32[]{:S(2)}, u32[]{:S(2)}) %collective-permute-start.15) | collective-permute-done | bytes 393248 | tf_op jit(solution)/shard_map/ppermute | solution.py:19
  115.2 1.3 %fusion.32 = bf16[2,2,256,192]{2,3,1,0:T(8,128)(2,1)} fusion(f32[2,2,256,192]{2,3,1,0:T(8,128)S(1)} %get-tuple-element.100, f32[2,2,256,192]{2,3,1,0:T(8,128)S(1)} %convolution_add_fusion.1, bf16[576,192,1,1]{1,0,3,2:T(8,128)(2,1)S(1)} %bitcast.157, bf16[2,2,256,192]{2,3,1,0:T(8,128)(2,1)S(1)} %get-tuple-element.41, ...), kind=kOutput, calls=%fused_computation.34 | convolution fusion | flops 231800832 | bytes 3366912 | tf_op jit(solution)/shard_map/fhwc,cd->fhwd/dot_general | solution.py:100
  (134 shorter events, 21.7 us)
Async XLA Ops:
  0.0 3.8 %copy-start = (bf16[384,384]{1,0:T(8,128)(2,1)S(1)}, bf16[384,384]{1,0:T(8,128)(2,1)}, u32[]{:S(2)}) copy-start(bf16[384,384]{1,0:T(8,128)(2,1)} %param.13) | copy-start | bytes 884740
  0.0 2.0 %collective-permute-start = (bf16[2,1,128,384]{3,2,1,0:T(8,128)(2,1)}, bf16[2,1,128,384]{3,2,1,0:T(8,128)(2,1)S(1)}, u32[]{:S(2)}, u32[]{:S(2)}) collective-permute-start(bf16[2,1,128,384]{3,2,1,0:T(8,128)(2,1)} %param.10), channel_id=1, source_target_pairs={{0,1},{1,0},{2,3},{3,2},{4,5},{5,4},{6,7},{7,6},{8,9},{9,8},{10,11... | collective-permute-start | bytes 589832 | tf_op jit(solution)/shard_map/ppermute | solution.py:200
  2.1 12.9 %copy-start.28 = (bf16[1,2,128,384]{3,2,1,0:T(8,128)(2,1)}, bf16[1,2,128,384]{3,2,1,0:T(8,128)(2,1)S(1)}, u32[]{:S(2)}) copy-start(bf16[1,2,128,384]{3,2,1,0:T(8,128)(2,1)S(1)} %pad_maximum_fusion.4) | copy-start | bytes 589828
  2.1 6.2 %collective-permute-start.1 = (bf16[1,2,128,384]{3,2,1,0:T(8,128)(2,1)S(1)}, bf16[1,2,128,384]{3,2,1,0:T(8,128)(2,1)S(1)}, u32[]{:S(2)}, u32[]{:S(2)}) collective-permute-start(bf16[1,2,128,384]{3,2,1,0:T(8,128)(2,1)S(1)} %pad_maximum_fusion.4), channel_id=1, source_target_pairs={{0,4},{1,5},{2,0},{3,1},{4,8},{5,9},{6,2},{7,3},{8,12},{9,13},{10,... | collective-permute-start | bytes 589832 | tf_op jit(solution)/shard_map/ppermute | solution.py:53
  2.4 6.1 %collective-permute-start.2 = (bf16[1,2,128,384]{3,2,1,0:T(8,128)(2,1)S(1)}, bf16[1,2,128,384]{3,2,1,0:T(8,128)(2,1)S(1)}, u32[]{:S(2)}, u32[]{:S(2)}) collective-permute-start(bf16[1,2,128,384]{3,2,1,0:T(8,128)(2,1)S(1)} %pad_maximum_fusion.4), channel_id=1, source_target_pairs={{0,2},{1,3},{2,6},{3,7},{4,0},{5,1},{6,10},{7,11},{8,4},{9,5},{10,... | collective-permute-start | bytes 589832 | tf_op jit(solution)/shard_map/ppermute | solution.py:56
  8.3 5.2 %collective-permute-start.3 = (bf16[1,2,128,384]{3,2,1,0:T(8,128)(2,1)S(1)}, bf16[1,2,128,384]{3,2,1,0:T(8,128)(2,1)S(1)}, u32[]{:S(2)}, u32[]{:S(2)}) collective-permute-start(bf16[1,2,128,384]{3,2,1,0:T(8,128)(2,1)S(1)} %collective-permute-done.1), channel_id=1, source_target_pairs={{0,4},{1,5},{2,0},{3,1},{4,8},{5,9},{6,2},{7,3},{8,12},{9,13},{10,... | collective-permute-start | bytes 589832 | tf_op jit(solution)/shard_map/ppermute | solution.py:53
  8.5 5.2 %collective-permute-start.4 = (bf16[1,2,128,384]{3,2,1,0:T(8,128)(2,1)S(1)}, bf16[1,2,128,384]{3,2,1,0:T(8,128)(2,1)S(1)}, u32[]{:S(2)}, u32[]{:S(2)}) collective-permute-start(bf16[1,2,128,384]{3,2,1,0:T(8,128)(2,1)S(1)} %collective-permute-done.2), channel_id=1, source_target_pairs={{0,2},{1,3},{2,6},{3,7},{4,0},{5,1},{6,10},{7,11},{8,4},{9,5},{10,... | collective-permute-start | bytes 589832 | tf_op jit(solution)/shard_map/ppermute | solution.py:56
  13.5 4.5 %collective-permute-start.5 = (bf16[1,2,128,384]{3,2,1,0:T(8,128)(2,1)S(1)}, bf16[1,2,128,384]{3,2,1,0:T(8,128)(2,1)S(1)}, u32[]{:S(2)}, u32[]{:S(2)}) collective-permute-start(bf16[1,2,128,384]{3,2,1,0:T(8,128)(2,1)S(1)} %collective-permute-done.3), channel_id=1, source_target_pairs={{0,4},{1,5},{2,0},{3,1},{4,8},{5,9},{6,2},{7,3},{8,12},{9,13},{10,... | collective-permute-start | bytes 589832 | tf_op jit(solution)/shard_map/ppermute | solution.py:53
  13.7 4.6 %collective-permute-start.6 = (bf16[1,2,128,384]{3,2,1,0:T(8,128)(2,1)S(1)}, bf16[1,2,128,384]{3,2,1,0:T(8,128)(2,1)S(1)}, u32[]{:S(2)}, u32[]{:S(2)}) collective-permute-start(bf16[1,2,128,384]{3,2,1,0:T(8,128)(2,1)S(1)} %collective-permute-done.4), channel_id=1, source_target_pairs={{0,2},{1,3},{2,6},{3,7},{4,0},{5,1},{6,10},{7,11},{8,4},{9,5},{10,... | collective-permute-start | bytes 589832 | tf_op jit(solution)/shard_map/ppermute | solution.py:56
  18.0 3.6 %collective-permute-start.7 = (bf16[1,1,128,384]{3,2,1,0:T(8,128)(2,1)S(1)}, bf16[1,1,128,384]{3,2,1,0:T(8,128)(2,1)S(1)}, u32[]{:S(2)}, u32[]{:S(2)}) collective-permute-start(bf16[1,1,128,384]{3,2,1,0:T(8,128)(2,1)S(1)} %slice.422), channel_id=1, source_target_pairs={{0,4},{1,5},{2,0},{3,1},{4,8},{5,9},{6,2},{7,3},{8,12},{9,13},{10,... | collective-permute-start | bytes 294920 | tf_op jit(solution)/shard_map/ppermute | solution.py:49
  18.3 3.8 %collective-permute-start.8 = (bf16[1,1,128,384]{3,2,1,0:T(8,128)(2,1)S(1)}, bf16[1,1,128,384]{3,2,1,0:T(8,128)(2,1)S(1)}, u32[]{:S(2)}, u32[]{:S(2)}) collective-permute-start(bf16[1,1,128,384]{3,2,1,0:T(8,128)(2,1)S(1)} %slice.423), channel_id=1, source_target_pairs={{0,2},{1,3},{2,6},{3,7},{4,0},{5,1},{6,10},{7,11},{8,4},{9,5},{10,... | collective-permute-start | bytes 294920 | tf_op jit(solution)/shard_map/ppermute | solution.py:50
  22.1 1.2 %copy-start.30 = (bf16[1,16,128,384]{3,2,1,0:T(8,128)(2,1)}, bf16[1,16,128,384]{3,2,1,0:T(8,128)(2,1)S(1)}, u32[]{:S(2)}) copy-start(bf16[1,16,128,384]{3,2,1,0:T(8,128)(2,1)S(1)} %constant_dynamic-update-slice_fusion) | copy-start | bytes 4718596
  31.2 10.6 %copy-start.14 = (bf16[2,1,128,384]{3,2,1,0:T(8,128)(2,1)S(1)}, bf16[2,1,128,384]{3,2,1,0:T(8,128)(2,1)}, u32[]{:S(2)}) copy-start(bf16[2,1,128,384]{3,2,1,0:T(8,128)(2,1)} %param.11) | copy-start | bytes 589828
  31.2 10.3 %collective-permute-start.9 = (bf16[1,1,128,384]{3,2,0,1:T(8,128)(2,1)S(1)}, bf16[1,1,128,384]{3,2,0,1:T(8,128)(2,1)S(1)}, u32[]{:S(2)}, u32[]{:S(2)}) collective-permute-start(bf16[1,1,128,384]{3,2,0,1:T(8,128)(2,1)S(1)} %get-tuple-element.98), channel_id=1, source_target_pairs={{0,1},{1,0},{2,3},{3,2},{4,5},{5,4},{6,7},{7,6},{8,9},{9,8},{10,11... | collective-permute-start | bytes 294920 | tf_op jit(solution)/shard_map/ppermute | solution.py:219
  41.4 5.2 %copy-start.4 = (bf16[3,3,384,192]{2,3,1,0:T(8,128)(2,1)S(1)}, bf16[3,3,384,192]{2,3,1,0:T(8,128)(2,1)}, u32[]{:S(2)}) copy-start(bf16[3,3,384,192]{2,3,1,0:T(8,128)(2,1)} %param.18) | copy-start | bytes 3981316
  41.5 5.4 %copy-start.18 = (bf16[1,1,128,384]{3,2,0,1:T(8,128)(2,1)}, bf16[1,1,128,384]{3,2,0,1:T(8,128)(2,1)S(1)}, u32[]{:S(2)}) copy-start(bf16[1,1,128,384]{3,2,0,1:T(8,128)(2,1)S(1)} %collective-permute-done.9) | copy-start | bytes 294916
  42.6 10.5 %collective-permute-start.10 = (bf16[4,1,128,384]{3,2,0,1:T(8,128)(2,1)}, bf16[4,1,128,384]{3,2,0,1:T(8,128)(2,1)S(1)}, u32[]{:S(2)}, u32[]{:S(2)}) collective-permute-start(bf16[4,1,128,384]{3,2,0,1:T(8,128)(2,1)} %pad_maximum_fusion.2), channel_id=1, source_target_pairs={{0,1},{1,2},{2,3},{3,4},{4,5},{5,6},{6,7},{7,8},{8,9},{9,10},{10,1... | collective-permute-start | bytes 1179656 | tf_op jit(solution)/shard_map/ppermute | solution.py:18
  49.9 2.9 %copy-start.15 = (bf16[2,1,128,384]{3,2,1,0:T(8,128)(2,1)S(1)}, bf16[2,1,128,384]{3,2,1,0:T(8,128)(2,1)}, u32[]{:S(2)}) copy-start(bf16[2,1,128,384]{3,2,1,0:T(8,128)(2,1)} %param.11) | copy-start | bytes 589828
  50.7 10.2 %collective-permute-start.11 = (bf16[4,1,128,384]{3,2,0,1:T(8,128)(2,1)}, bf16[4,1,128,384]{3,2,0,1:T(8,128)(2,1)S(1)}, u32[]{:S(2)}, u32[]{:S(2)}) collective-permute-start(bf16[4,1,128,384]{3,2,0,1:T(8,128)(2,1)} %pad_maximum_fusion.2), channel_id=1, source_target_pairs={{1,0},{2,1},{3,2},{4,3},{5,4},{6,5},{7,6},{8,7},{9,8},{10,9},{11,1... | collective-permute-start | bytes 1179656 | tf_op jit(solution)/shard_map/ppermute | solution.py:19
  61.0 1.2 %copy-start.13 = (bf16[1,1,3,384,384]{4,3,2,1,0:T(8,128)(2,1)S(1)}, bf16[1,1,3,384,384]{4,3,2,1,0:T(8,128)(2,1)}, u32[]{:S(2)}) copy-start(bf16[1,1,3,384,384]{4,3,2,1,0:T(8,128)(2,1)} %get-tuple-element.16) | copy-start | bytes 2654212
  62.2 1.2 %copy-start.12 = (bf16[1,1,3,384,384]{4,3,2,1,0:T(8,128)(2,1)S(1)}, bf16[1,1,3,384,384]{4,3,2,1,0:T(8,128)(2,1)}, u32[]{:S(2)}) copy-start(bf16[1,1,3,384,384]{4,3,2,1,0:T(8,128)(2,1)} %get-tuple-element.15) | copy-start | bytes 2654212
  63.4 1.2 %copy-start.11 = (bf16[1,1,3,384,384]{4,3,2,1,0:T(8,128)(2,1)S(1)}, bf16[1,1,3,384,384]{4,3,2,1,0:T(8,128)(2,1)}, u32[]{:S(2)}) copy-start(bf16[1,1,3,384,384]{4,3,2,1,0:T(8,128)(2,1)} %get-tuple-element.14) | copy-start | bytes 2654212
  64.5 1.2 %copy-start.10 = (bf16[1,1,3,384,384]{4,3,2,1,0:T(8,128)(2,1)S(1)}, bf16[1,1,3,384,384]{4,3,2,1,0:T(8,128)(2,1)}, u32[]{:S(2)}) copy-start(bf16[1,1,3,384,384]{4,3,2,1,0:T(8,128)(2,1)} %get-tuple-element.13) | copy-start | bytes 2654212
  65.7 1.2 %copy-start.9 = (bf16[1,1,3,384,384]{4,3,2,1,0:T(8,128)(2,1)S(1)}, bf16[1,1,3,384,384]{4,3,2,1,0:T(8,128)(2,1)}, u32[]{:S(2)}) copy-start(bf16[1,1,3,384,384]{4,3,2,1,0:T(8,128)(2,1)} %get-tuple-element.12) | copy-start | bytes 2654212
  66.9 1.2 %copy-start.8 = (bf16[1,1,3,384,384]{4,3,2,1,0:T(8,128)(2,1)S(1)}, bf16[1,1,3,384,384]{4,3,2,1,0:T(8,128)(2,1)}, u32[]{:S(2)}) copy-start(bf16[1,1,3,384,384]{4,3,2,1,0:T(8,128)(2,1)} %get-tuple-element.11) | copy-start | bytes 2654212
  68.0 1.2 %copy-start.7 = (bf16[1,1,3,384,384]{4,3,2,1,0:T(8,128)(2,1)S(1)}, bf16[1,1,3,384,384]{4,3,2,1,0:T(8,128)(2,1)}, u32[]{:S(2)}) copy-start(bf16[1,1,3,384,384]{4,3,2,1,0:T(8,128)(2,1)} %get-tuple-element.10) | copy-start | bytes 2654212
  69.2 1.2 %copy-start.6 = (bf16[1,1,3,384,384]{4,3,2,1,0:T(8,128)(2,1)S(1)}, bf16[1,1,3,384,384]{4,3,2,1,0:T(8,128)(2,1)}, u32[]{:S(2)}) copy-start(bf16[1,1,3,384,384]{4,3,2,1,0:T(8,128)(2,1)} %get-tuple-element.17) | copy-start | bytes 2654212
  70.4 1.2 %copy-start.5 = (bf16[1,1,3,384,384]{4,3,2,1,0:T(8,128)(2,1)S(1)}, bf16[1,1,3,384,384]{4,3,2,1,0:T(8,128)(2,1)}, u32[]{:S(2)}) copy-start(bf16[1,1,3,384,384]{4,3,2,1,0:T(8,128)(2,1)} %get-tuple-element.9) | copy-start | bytes 2654212
  70.4 1.2 %copy-start.19 = (bf16[1,1,128,384]{3,2,0,1:T(8,128)(2,1)S(1)}, bf16[1,1,128,384]{3,2,0,1:T(8,128)(2,1)}, u32[]{:S(2)}) copy-start(bf16[1,1,128,384]{3,2,0,1:T(8,128)(2,1)} %copy-done.18) | copy-start | bytes 294916
  70.4 1.2 %copy-start.29 = (bf16[1,128,384]{2,1,0:T(8,128)(2,1)S(1)}, bf16[1,128,384]{2,1,0:T(8,128)(2,1)}, u32[]{:S(2)}) copy-start(bf16[1,128,384]{2,1,0:T(8,128)(2,1)} %get-tuple-element.97) | copy-start | bytes 294916
  71.6 7.1 %copy-start.3 = (bf16[3,3,3,192,192]{4,3,2,1,0:T(8,128)(2,1)S(1)}, bf16[3,3,3,192,192]{4,3,2,1,0:T(8,128)(2,1)}, u32[]{:S(2)}) copy-start(bf16[3,3,3,192,192]{4,3,2,1,0:T(8,128)(2,1)} %param.19) | copy-start | bytes 5971972
  72.1 8.1 %collective-permute-start.13 = (bf16[2,1,128,384]{3,2,0,1:T(8,128)(2,1)S(1)}, bf16[2,1,128,384]{3,2,0,1:T(8,128)(2,1)S(1)}, u32[]{:S(2)}, u32[]{:S(2)}) collective-permute-start(bf16[2,1,128,384]{3,2,0,1:T(8,128)(2,1)S(1)} %fusion.146), channel_id=1, source_target_pairs={{1,0},{2,1},{3,2},{4,3},{5,4},{6,5},{7,6},{8,7},{9,8},{10,9},{11,1... | collective-permute-start | bytes 589832 | tf_op jit(solution)/shard_map/ppermute | solution.py:19
  74.1 7.1 %collective-permute-start.12 = (bf16[2,1,128,384]{3,2,0,1:T(8,128)(2,1)S(1)}, bf16[2,1,128,384]{3,2,0,1:T(8,128)(2,1)S(1)}, u32[]{:S(2)}, u32[]{:S(2)}) collective-permute-start(bf16[2,1,128,384]{3,2,0,1:T(8,128)(2,1)S(1)} %fusion.146), channel_id=1, source_target_pairs={{0,1},{1,2},{2,3},{3,4},{4,5},{5,6},{6,7},{7,8},{8,9},{9,10},{10,1... | collective-permute-start | bytes 589832 | tf_op jit(solution)/shard_map/ppermute | solution.py:18
  83.4 1.0 copy-start.17
  84.5 1.2 copy-start.16
  87.9 1.0 copy-start.2
  89.7 10.0 %collective-permute-start.14 = (bf16[4,1,256,192]{2,3,1,0:T(8,128)(2,1)S(1)}, bf16[4,1,256,192]{2,3,1,0:T(8,128)(2,1)S(1)}, u32[]{:S(2)}, u32[]{:S(2)}) collective-permute-start(bf16[4,1,256,192]{2,3,1,0:T(8,128)(2,1)S(1)} %get-tuple-element.39), channel_id=1, source_target_pairs={{0,1},{1,2},{2,3},{3,4},{4,5},{5,6},{6,7},{7,8},{8,9},{9,10},{10,1... | collective-permute-start | bytes 1179656 | tf_op jit(solution)/shard_map/ppermute | solution.py:18
  95.0 10.0 %collective-permute-start.15 = (bf16[4,1,256,192]{2,3,1,0:T(8,128)(2,1)S(1)}, bf16[4,1,256,192]{2,3,1,0:T(8,128)(2,1)S(1)}, u32[]{:S(2)}, u32[]{:S(2)}) collective-permute-start(bf16[4,1,256,192]{2,3,1,0:T(8,128)(2,1)S(1)} %get-tuple-element.38), channel_id=1, source_target_pairs={{1,0},{2,1},{3,2},{4,3},{5,4},{6,5},{7,6},{8,7},{9,8},{10,9},{11,1... | collective-permute-start | bytes 1179656 | tf_op jit(solution)/shard_map/ppermute | solution.py:19
  107.0 1.0 copy-start.27
  107.9 1.0 copy-start.26
  108.9 1.0 copy-start.25
  109.8 1.0 copy-start.24
  110.8 1.0 copy-start.23
  111.8 1.0 copy-start.22
  112.7 1.0 copy-start.21
  113.7 1.0 copy-start.20
  115.2 1.3 %copy-start.1 = (bf16[384,384]{1,0:T(8,128)(2,1)S(1)}, bf16[384,384]{1,0:T(8,128)(2,1)}, u32[]{:S(2)}) copy-start(bf16[384,384]{1,0:T(8,128)(2,1)} %param.13) | copy-start | bytes 884740

commit v20 on v18

--- a/solution.py
+++ b/solution.py
@@ -104,7 +104,7 @@
     return result
 
 
-def attention_kernel(scale, q_ref, x_ref, wk_ref, wv_ref, r_ref, wo_ref, o_ref):
+def attention_kernel(scale, q_ref, x_ref, wk_ref, wv_ref, r_ref, wo_ref, own_ref, other_ref):
     raw = x_ref[0].astype(jnp.float32)
     tokens = (raw * lax.rsqrt(jnp.mean(raw * raw, axis=-1, keepdims=True) + 1e-06)).astype(
         x_ref.dtype
@@ -123,7 +123,10 @@
     summed = jnp.dot(weights.astype(values.dtype), values, preferred_element_type=jnp.float32)
     attended = (summed / weight_sum).astype(values.dtype)
     projected = jnp.dot(attended, wo_ref[...], preferred_element_type=jnp.float32)
-    o_ref[0] = (r_ref[0].astype(jnp.float32) + projected).astype(o_ref.dtype)
+    mixed = (r_ref[0].astype(jnp.float32) + projected).astype(own_ref.dtype)
+    half = own_ref.shape[1]
+    own_ref[0] = mixed[:half]
+    other_ref[0] = mixed[half:]
 
 
 def attend(queries, all_rows, w_key, w_value, residual, w_output, scale):
@@ -142,8 +145,8 @@
             pl.BlockSpec((1, count, channels), lambda f: (f, 0, 0)),
             pl.BlockSpec(w_output.shape, lambda f: (0, 0)),
         ],
-        out_specs=pl.BlockSpec((1, count, channels), lambda f: (f, 0, 0)),
-        out_shape=jax.ShapeDtypeStruct(queries.shape, queries.dtype),
+        out_specs=[pl.BlockSpec((1, count // 2, channels), lambda f: (f, 0, 0))] * 2,
+        out_shape=[jax.ShapeDtypeStruct((frames, count // 2, channels), queries.dtype)] * 2,
         compiler_params=pltpu.CompilerParams(vmem_limit_bytes=60 * 1024 * 1024),
         cost_estimate=pl.CostEstimate(
             flops=flops, transcendentals=frames * count * tokens, bytes_accessed=moved
@@ -183,7 +186,7 @@
     normed_tokens = normed.reshape(1, -1, channels)
     queries = project_rows(normed_tokens, w_query)
     score_scale = 1.0 / math.sqrt(channels)
-    mixed_block = attend(
+    own, theirs = attend(
         queries,
         all_rows,
         w_key,
@@ -191,9 +194,10 @@
         block.reshape(queries.shape),
         w_output,
         score_scale,
-    ).reshape(block.shape)
-    back = lax.ppermute(mixed_block[:, 1:2], "ha", swap)
-    own = mixed_block[:, 0:1]
+    )
+    row_shape = mine.shape
+    back = lax.ppermute(theirs.reshape(row_shape), "ha", swap)
+    own = own.reshape(row_shape)
     mixed = jnp.where(
         core == 0,
         jnp.concatenate([own, back], axis=0),

time: 95.9 us -> 97.4 us (1.016)
  other arithmetic: 3.8 us -> 5.76 us
    unnamed x27 -> x29, local copies, waits for them, and re-layouts: 3.07 us -> 3.47 us
where the time goes in v20:
time: 97.4 us; the launch traced here: 96.5 us
  waiting for transfers between devices  27.4 us (28%)
  starting transfers between devices  26.8 us (28%)
  local copies, waits for them, and re-layouts  15.6 us (16%)
  matrix products  14.2 us (15%)
  Pallas kernels  6.27 us (6%)
  other arithmetic  5.76 us (6%)
    dot_general x21, matrix products, conv_taps(): jnp.einsum('fhwc,cd->fhwd', stacked, kernel, preferred_element_type=jnp.f...  13.2 us
    ppermute x3, waiting for transfers between devices, halo_rows(): after = lax.ppermute(first, 'ha', down)  11.4 us
    ppermute x3, waiting for transfers between devices, gather_chip_rows(): ahead = lax.ppermute(ahead, 'ha', forward)  10.1 us
    ppermute x3, starting transfers between devices, halo_rows(): before = lax.ppermute(last, 'ha', up)  8.44 us
    ppermute x3, starting transfers between devices, halo_rows(): after = lax.ppermute(first, 'ha', down)  7.05 us
    pallas_call x1, Pallas kernels, attend(): pl.pallas_call(functools.partial(attention_kernel, scale), grid=(frames,)...  6.27 us
    slice x6, local copies, waits for them, and re-layouts, conv_taps(): kernel = weight[time_off, row_off].reshape(3 * in_channels, out_channels)  5.41 us
    ppermute x1, starting transfers between devices, per_device(): back = lax.ppermute(theirs.reshape(row_shape), 'ha', swap)  4.57 us
  transfers between devices with their start and end apart: 16, of which 11 were waited for; matrix products, arithmetic and copies ran while one was open for 10% of the time, Pallas kernels for 0%

profile of v20, /device:TPU:13, one launch (start us, length us, event | category | flops | bytes accessed | tf_op | source)
XLA Modules:
  0.0 96.5 jit_solution(10257009055170185974)
XLA Ops:
  0.0 0.7 collective-permute-start
  0.7 0.9 constant_dynamic-update-slice_fusion.9
  2.3 1.3 %collective-permute-start.2 = (bf16[1,2,128,384]{3,2,1,0:T(8,128)(2,1)S(1)}, bf16[1,2,128,384]{3,2,1,0:T(8,128)(2,1)S(1)}, u32[]{:S(2)}, u32[]{:S(2)}) collective-permute-start(bf16[1,2,128,384]{3,2,1,0:T(8,128)(2,1)S(1)} %pad_maximum_fusion.5), channel_id=1, source_target_pairs={{0,2},{1,3},{2,6},{3,7},{4,0},{5,1},{6,10},{7,11},{8,4},{9,5},{10,... | collective-permute-start | bytes 589832 | tf_op jit(solution)/shard_map/ppermute | solution.py:56
  3.8 1.0 fusion.88.q_ref
  4.8 3.4 %collective-permute-done.1 = bf16[1,2,128,384]{3,2,1,0:T(8,128)(2,1)S(1)} collective-permute-done((bf16[1,2,128,384]{3,2,1,0:T(8,128)(2,1)S(1)}, bf16[1,2,128,384]{3,2,1,0:T(8,128)(2,1)S(1)}, u32[]{:S(2)}, u32[]{:S(2)}) %collective-permute-start.1) | collective-permute-done | bytes 196640 | tf_op jit(solution)/shard_map/ppermute | solution.py:53
  8.4 1.3 %collective-permute-start.4 = (bf16[1,2,128,384]{3,2,1,0:T(8,128)(2,1)S(1)}, bf16[1,2,128,384]{3,2,1,0:T(8,128)(2,1)S(1)}, u32[]{:S(2)}, u32[]{:S(2)}) collective-permute-start(bf16[1,2,128,384]{3,2,1,0:T(8,128)(2,1)S(1)} %collective-permute-done.2), channel_id=1, source_target_pairs={{0,2},{1,3},{2,6},{3,7},{4,0},{5,1},{6,10},{7,11},{8,4},{9,5},{10,... | collective-permute-start | bytes 589832 | tf_op jit(solution)/shard_map/ppermute | solution.py:56
  9.7 3.6 %collective-permute-done.3 = bf16[1,2,128,384]{3,2,1,0:T(8,128)(2,1)S(1)} collective-permute-done((bf16[1,2,128,384]{3,2,1,0:T(8,128)(2,1)S(1)}, bf16[1,2,128,384]{3,2,1,0:T(8,128)(2,1)S(1)}, u32[]{:S(2)}, u32[]{:S(2)}) %collective-permute-start.3) | collective-permute-done | bytes 196640 | tf_op jit(solution)/shard_map/ppermute | solution.py:53
  13.6 1.3 %collective-permute-start.6 = (bf16[1,2,128,384]{3,2,1,0:T(8,128)(2,1)S(1)}, bf16[1,2,128,384]{3,2,1,0:T(8,128)(2,1)S(1)}, u32[]{:S(2)}, u32[]{:S(2)}) collective-permute-start(bf16[1,2,128,384]{3,2,1,0:T(8,128)(2,1)S(1)} %collective-permute-done.4), channel_id=1, source_target_pairs={{0,2},{1,3},{2,6},{3,7},{4,0},{5,1},{6,10},{7,11},{8,4},{9,5},{10,... | collective-permute-start | bytes 589832 | tf_op jit(solution)/shard_map/ppermute | solution.py:56
  14.9 3.0 %collective-permute-done.5 = bf16[1,2,128,384]{3,2,1,0:T(8,128)(2,1)S(1)} collective-permute-done((bf16[1,2,128,384]{3,2,1,0:T(8,128)(2,1)S(1)}, bf16[1,2,128,384]{3,2,1,0:T(8,128)(2,1)S(1)}, u32[]{:S(2)}, u32[]{:S(2)}) %collective-permute-start.5) | collective-permute-done | bytes 196640 | tf_op jit(solution)/shard_map/ppermute | solution.py:53
  18.2 1.3 %collective-permute-start.8 = (bf16[1,1,128,384]{3,2,1,0:T(8,128)(2,1)S(1)}, bf16[1,1,128,384]{3,2,1,0:T(8,128)(2,1)S(1)}, u32[]{:S(2)}, u32[]{:S(2)}) collective-permute-start(bf16[1,1,128,384]{3,2,1,0:T(8,128)(2,1)S(1)} %slice.468), channel_id=1, source_target_pairs={{0,2},{1,3},{2,6},{3,7},{4,0},{5,1},{6,10},{7,11},{8,4},{9,5},{10,... | collective-permute-start | bytes 294920 | tf_op jit(solution)/shard_map/ppermute | solution.py:50
  19.6 1.9 %collective-permute-done.7 = bf16[1,1,128,384]{3,2,1,0:T(8,128)(2,1)S(1)} collective-permute-done((bf16[1,1,128,384]{3,2,1,0:T(8,128)(2,1)S(1)}, bf16[1,1,128,384]{3,2,1,0:T(8,128)(2,1)S(1)}, u32[]{:S(2)}, u32[]{:S(2)}) %collective-permute-start.7) | collective-permute-done | bytes 98336 | tf_op jit(solution)/shard_map/ppermute | solution.py:49
  22.0 1.2 %copy-done.9 = bf16[1,16,128,384]{3,2,1,0:T(8,128)(2,1)} copy-done((bf16[1,16,128,384]{3,2,1,0:T(8,128)(2,1)}, bf16[1,16,128,384]{3,2,1,0:T(8,128)(2,1)S(1)}, u32[]{:S(2)}) %copy-start.9) | copy-done | bytes 1572888
  23.2 6.3 %shard_map.100 = (bf16[1,128,384]{2,1,0:T(8,128)(2,1)}, bf16[1,128,384]{2,1,0:T(8,128)(2,1)}) custom-call(bf16[1,256,384]{2,1,0:T(8,128)(2,1)} %fusion.88.q_ref, bf16[1,2048,384]{2,1,0:T(8,128)(2,1)} %bitcast.159, bf16[384,384]{1,0:T(8,128)(2,1)} %wk_ref.1, bf16[384,384]{1,0:T(8,128)(2,1)} %wv_ref.1, bf16[1,256,384]{2,1,0:T(8,128)(2,1)} %bitcast.158, ...), custom_call_target="tpu_custom_call" | custom-call | flops 2013265920 | bytes 3047424 | tf_op jit(solution)/shard_map/pallas_call | solution.py:137
  29.5 4.6 %collective-permute-start.9 = (bf16[1,1,128,384]{3,2,1,0:T(8,128)(2,1)}, bf16[1,1,128,384]{3,2,1,0:T(8,128)(2,1)S(1)}, u32[]{:S(2)}, u32[]{:S(2)}) collective-permute-start(bf16[1,1,128,384]{3,2,1,0:T(8,128)(2,1)} %bitcast.160), channel_id=1, source_target_pairs={{0,1},{1,0},{2,3},{3,2},{4,5},{5,4},{6,7},{7,6},{8,9},{9,8},{10,11... | collective-permute-start | bytes 294920 | tf_op jit(solution)/shard_map/ppermute | solution.py:199
  34.1 1.2 %collective-permute-done.9 = bf16[1,1,128,384]{3,2,1,0:T(8,128)(2,1)S(1)} collective-permute-done((bf16[1,1,128,384]{3,2,1,0:T(8,128)(2,1)}, bf16[1,1,128,384]{3,2,1,0:T(8,128)(2,1)S(1)}, u32[]{:S(2)}, u32[]{:S(2)}) %collective-permute-start.9) | collective-permute-done | bytes 98336 | tf_op jit(solution)/shard_map/ppermute | solution.py:199
  35.2 1.1 %fusion.137 = f32[2,128]{1,0:T(2,128)S(1)} fusion(bf16[1,1,128,384]{3,2,1,0:T(8,128)(2,1)} %bitcast.146, bf16[1,1,128,384]{3,2,1,0:T(8,128)(2,1)S(1)} %collective-permute-done.9, pred[]{:T(512)S(6)} %eq.5), kind=kLoop, calls=%fused_computation.186 | loop fusion | flops 589568 | bytes 197633 | tf_op jit(solution)/shard_map/reduce_sum | solution.py:78
  36.3 1.1 %fusion.136 = bf16[2,1,128,384]{3,2,1,0:T(8,128)(2,1)S(1)} fusion(f32[2,128]{1,0:T(2,128)S(1)} %add_rsqrt_fusion.1, bf16[1,1,128,384]{3,2,1,0:T(8,128)(2,1)} %bitcast.147, bf16[1,1,128,384]{3,2,1,0:T(8,128)(2,1)S(1)} %collective-permute-done.9, pred[]{:T(512)S(6)} %eq.5), kind=kLoop, calls=%fused_computation.185 | loop fusion | flops 983040 | bytes 394241 | tf_op jit(solution)/shard_map/convert_element_type | solution.py:206
  37.6 4.4 %collective-permute-start.10 = (bf16[4,1,128,384]{3,2,1,0:T(8,128)(2,1)S(1)}, bf16[4,1,128,384]{3,2,1,0:T(8,128)(2,1)S(1)}, u32[]{:S(2)}, u32[]{:S(2)}) collective-permute-start(bf16[4,1,128,384]{3,2,1,0:T(8,128)(2,1)S(1)} %pad_maximum_fusion.4), channel_id=1, source_target_pairs={{0,1},{1,2},{2,3},{3,4},{4,5},{5,6},{6,7},{7,8},{8,9},{9,10},{10,1... | collective-permute-start | bytes 1179656 | tf_op jit(solution)/shard_map/ppermute | solution.py:18
  41.9 1.9 %collective-permute-start.11 = (bf16[4,1,128,384]{3,2,1,0:T(8,128)(2,1)S(1)}, bf16[4,1,128,384]{3,2,1,0:T(8,128)(2,1)S(1)}, u32[]{:S(2)}, u32[]{:S(2)}) collective-permute-start(bf16[4,1,128,384]{3,2,1,0:T(8,128)(2,1)S(1)} %pad_maximum_fusion.4), channel_id=1, source_target_pairs={{1,0},{2,1},{3,2},{4,3},{5,4},{6,5},{7,6},{8,7},{9,8},{10,9},{11,1... | collective-permute-start | bytes 1179656 | tf_op jit(solution)/shard_map/ppermute | solution.py:19
  43.9 3.9 %fusion.164 = (bf16[1,1,3,384,384]{4,3,2,1,0:T(8,128)(2,1)S(1)}, bf16[1,1,3,384,384]{4,3,2,1,0:T(8,128)(2,1)S(1)}, bf16[1,1,3,384,384]{4,3,2,1,0:T(8,128)(2,1)S(...) fusion(bf16[3,3,3,384,384]{4,3,2,1,0:T(8,128)(2,1)} %param.17), kind=kLoop, calls=%fused_computation.234 | loop fusion | bytes 15925248 | tf_op jit(solution)/shard_map/slice | solution.py:100
  47.9 4.1 %collective-permute-done.11 = bf16[4,1,128,384]{3,2,1,0:T(8,128)(2,1)S(1)} collective-permute-done((bf16[4,1,128,384]{3,2,1,0:T(8,128)(2,1)S(1)}, bf16[4,1,128,384]{3,2,1,0:T(8,128)(2,1)S(1)}, u32[]{:S(2)}, u32[]{:S(2)}) %collective-permute-start.11) | collective-permute-done | bytes 393248 | tf_op jit(solution)/shard_map/ppermute | solution.py:19
  52.3 0.7 fusion.168
  57.4 0.5 fusion.141
  57.9 1.9 %collective-permute-start.12 = (bf16[2,1,128,384]{3,2,0,1:T(8,128)(2,1)S(1)}, bf16[2,1,128,384]{3,2,0,1:T(8,128)(2,1)S(1)}, u32[]{:S(2)}, u32[]{:S(2)}) collective-permute-start(bf16[2,1,128,384]{3,2,0,1:T(8,128)(2,1)S(1)} %fusion.141), channel_id=1, source_target_pairs={{0,1},{1,2},{2,3},{3,4},{4,5},{5,6},{6,7},{7,8},{8,9},{9,10},{10,1... | collective-permute-start | bytes 589832 | tf_op jit(solution)/shard_map/ppermute | solution.py:18
  59.8 2.6 %collective-permute-start.13 = (bf16[2,1,128,384]{3,2,0,1:T(8,128)(2,1)S(1)}, bf16[2,1,128,384]{3,2,0,1:T(8,128)(2,1)S(1)}, u32[]{:S(2)}, u32[]{:S(2)}) collective-permute-start(bf16[2,1,128,384]{3,2,0,1:T(8,128)(2,1)S(1)} %fusion.141), channel_id=1, source_target_pairs={{1,0},{2,1},{3,2},{4,3},{5,4},{6,5},{7,6},{8,7},{9,8},{10,9},{11,1... | collective-permute-start | bytes 589832 | tf_op jit(solution)/shard_map/ppermute | solution.py:19
  62.9 1.1 %reshape.289 = bf16[1152,192,1,1]{0,1,2,3:T(8,128)(2,1)} reshape(bf16[1,1,3,384,192]{3,2,4,1,0:T(4,128)(2,1)S(1)} %copy.26) | data formatting | bytes 884736 | tf_op jit(solution)/shard_map/reshape;squeeze | solution.py:100
  65.6 2.1 %collective-permute-done.13 = bf16[2,1,128,384]{3,2,0,1:T(8,128)(2,1)S(1)} collective-permute-done((bf16[2,1,128,384]{3,2,0,1:T(8,128)(2,1)S(1)}, bf16[2,1,128,384]{3,2,0,1:T(8,128)(2,1)S(1)}, u32[]{:S(2)}, u32[]{:S(2)}) %collective-permute-start.13) | collective-permute-done | bytes 196640 | tf_op jit(solution)/shard_map/ppermute | solution.py:19
  67.8 0.6 broadcast_in_dim.4
  69.1 0.8 pad_slice_fusion.9
  70.2 0.7 copy-done.6
  70.9 1.1 %fusion.6 = f32[2,2,256,192]{2,3,1,0:T(8,128)S(1)} fusion(bf16[2,1,258,384]{3,2,1,0:T(8,128)(2,1)S(1)} %pad_slice_fusion.10, bf16[2,2,256,384]{3,2,1,0:T(8,128)(2,1)S(1)} %get-tuple-element.87, bf16[2,2,256,384]{3,2,1,0:T(8,128)(2,1)S(1)} %get-tuple-element.86, bf16[1152,192,1,1]{0,1,2,3:T(8,128)(2,1)S(1)} %copy-done.6), kind=kOutput, calls=%fused_computation.13 | convolution fusion | flops 462422016 | bytes 3197952 | tf_op jit(solution)/shard_map/fhwc,cd->fhwd/dot_general | solution.py:101
  72.0 1.1 %fusion.28 = f32[2,2,256,192]{2,3,1,0:T(8,128)S(1)} fusion(f32[2,2,256,192]{2,3,1,0:T(8,128)S(1)} %fusion.6, bf16[2,2,256,384]{3,2,1,0:T(8,128)(2,1)S(1)} %get-tuple-element.77, bf16[2,2,256,384]{3,2,1,0:T(8,128)(2,1)S(1)} %get-tuple-element.80, bf16[2,2,256,384]{3,2,1,0:T(8,128)(2,1)S(1)} %get-tuple-element.81, bf16[1152,192,1,1]{0,1,2,3:T(8,128)(2,1)S(1)} %reshape.288), kind=kOutput, calls=%fused_computation.40 | convolution fusion | flops 460259328 | bytes 4374528 | tf_op jit(solution)/shard_map/fhwc,cd->fhwd/dot_general | solution.py:101
  73.2 1.2 %multiply_reduce_fusion = (f32[2,2,256]{2,1,0:T(2,128)S(1)}, f32[2,2,256,192]{2,3,1,0:T(8,128)S(1)}) fusion(f32[2,2,256,192]{2,3,1,0:T(8,128)S(1)} %fusion.28, bf16[1152,192,1,1]{0,1,2,3:T(8,128)(2,1)S(1)} %reshape.290, bf16[2,2,256,384]{3,2,1,0:T(8,128)(2,1)S(1)} %get-tuple-element.78, bf16[2,2,256,384]{3,2,1,0:T(8,128)(2,1)S(1)} %get-tuple-element.79, ...), kind=kOutput, calls=%fused_computation.119 | convolution fusion | flops 461044736 | bytes 4378624 | tf_op jit(solution)/shard_map/fhwc,cd->fhwd/dot_general | solution.py:101
  74.7 2.1 %collective-permute-start.14 = (bf16[4,1,256,192]{2,3,1,0:T(8,128)(2,1)S(1)}, bf16[4,1,256,192]{2,3,1,0:T(8,128)(2,1)S(1)}, u32[]{:S(2)}, u32[]{:S(2)}) collective-permute-start(bf16[4,1,256,192]{2,3,1,0:T(8,128)(2,1)S(1)} %get-tuple-element.84), channel_id=1, source_target_pairs={{0,1},{1,2},{2,3},{3,4},{4,5},{5,6},{6,7},{7,8},{8,9},{9,10},{10,1... | collective-permute-start | bytes 1179656 | tf_op jit(solution)/shard_map/ppermute | solution.py:18
  76.9 2.5 %collective-permute-start.15 = (bf16[4,1,256,192]{2,3,1,0:T(8,128)(2,1)S(1)}, bf16[4,1,256,192]{2,3,1,0:T(8,128)(2,1)S(1)}, u32[]{:S(2)}, u32[]{:S(2)}) collective-permute-start(bf16[4,1,256,192]{2,3,1,0:T(8,128)(2,1)S(1)} %get-tuple-element.85), channel_id=1, source_target_pairs={{1,0},{2,1},{3,2},{4,3},{5,4},{6,5},{7,6},{8,7},{9,8},{10,9},{11,1... | collective-permute-start | bytes 1179656 | tf_op jit(solution)/shard_map/ppermute | solution.py:19
  79.6 1.9 %collective-permute-done.14 = bf16[4,1,256,192]{2,3,1,0:T(8,128)(2,1)S(1)} collective-permute-done((bf16[4,1,256,192]{2,3,1,0:T(8,128)(2,1)S(1)}, bf16[4,1,256,192]{2,3,1,0:T(8,128)(2,1)S(1)}, u32[]{:S(2)}, u32[]{:S(2)}) %collective-permute-start.14) | collective-permute-done | bytes 393248 | tf_op jit(solution)/shard_map/ppermute | solution.py:18
  81.6 5.3 %collective-permute-done.15 = bf16[4,1,256,192]{2,3,1,0:T(8,128)(2,1)S(1)} collective-permute-done((bf16[4,1,256,192]{2,3,1,0:T(8,128)(2,1)S(1)}, bf16[4,1,256,192]{2,3,1,0:T(8,128)(2,1)S(1)}, u32[]{:S(2)}, u32[]{:S(2)}) %collective-permute-start.15) | collective-permute-done | bytes 393248 | tf_op jit(solution)/shard_map/ppermute | solution.py:19
  86.8 2.0 %select_maximum_fusion = bf16[4,4,258,192]{2,3,1,0:T(8,128)(2,1)S(1)} fusion(bf16[4,1,256,192]{2,3,1,0:T(8,128)(2,1)S(1)} %collective-permute-done.15, bf16[4,1,256,192]{2,3,1,0:T(8,128)(2,1)S(1)} %collective-permute-done.14, bf16[2,2,256,192]{2,3,1,0:T(8,128)(2,1)S(1)} %multiply_convert_fusion, bf16[2,2,256,192]{2,3,1,0:T(8,128)(2,1)S(1)} %copy-done.2), kind=kLoop, calls=%fused_computation.6 | loop fusion | flops 11888640 | bytes 3158016 | tf_op jit(solution)/shard_map/concatenate | solution.py:25
  88.8 1.7 %fusion.166 = (bf16[2,2,256,192]{2,3,1,0:T(8,128)(2,1)S(1)}, bf16[2,2,256,192]{2,3,1,0:T(8,128)(2,1)S(1)}, bf16[2,2,256,192]{2,3,1,0:T(8,128)(2,1)S(1)}, bf16[2,...) fusion(bf16[4,4,258,192]{2,3,1,0:T(8,128)(2,1)S(1)} %select_max, ...), kind=kLoop, calls=%fused_computation.236 | loop fusion | bytes 14155776 | tf_op jit(solution)/shard_map/slice | solution.py:98
  90.9 0.5 fusion.50
  91.5 0.5 convolution_add_fusion.7
  92.0 0.5 convolution_add_fusion.6
  92.5 0.5 convolution_add_fusion.5
  93.0 0.5 convolution_add_fusion.4
  93.6 0.5 convolution_add_fusion.3
  94.1 0.5 convolution_add_fusion.2
  94.6 0.5 convolution_add_fusion.1
  95.2 1.3 %fusion.40 = bf16[2,2,256,192]{2,3,1,0:T(8,128)(2,1)} fusion(f32[2,2,256,192]{2,3,1,0:T(8,128)S(1)} %get-tuple-element.95, f32[2,2,256,192]{2,3,1,0:T(8,128)S(1)} %convolution_add_fusion.1, bf16[576,192,1,1]{1,0,3,2:T(8,128)(2,1)S(1)} %bitcast.149, bf16[2,2,256,192]{2,3,1,0:T(8,128)(2,1)S(1)} %get-tuple-element.48, ...), kind=kOutput, calls=%fused_computation.48 | convolution fusion | flops 230621184 | bytes 3366912 | tf_op jit(solution)/shard_map/fhwc,cd->fhwd/dot_general | solution.py:101
  (75 shorter events, 10.9 us)
Async XLA Ops:
  0.0 3.8 %copy-start = (bf16[384,384]{1,0:T(8,128)(2,1)S(1)}, bf16[384,384]{1,0:T(8,128)(2,1)}, u32[]{:S(2)}) copy-start(bf16[384,384]{1,0:T(8,128)(2,1)} %param.13) | copy-start | bytes 884740
  0.0 2.0 %collective-permute-start = (bf16[2,1,128,384]{3,2,1,0:T(8,128)(2,1)}, bf16[2,1,128,384]{3,2,1,0:T(8,128)(2,1)S(1)}, u32[]{:S(2)}, u32[]{:S(2)}) collective-permute-start(bf16[2,1,128,384]{3,2,1,0:T(8,128)(2,1)} %param.10), channel_id=1, source_target_pairs={{0,1},{1,0},{2,3},{3,2},{4,5},{5,4},{6,7},{7,6},{8,9},{9,8},{10,11... | collective-permute-start | bytes 589832 | tf_op jit(solution)/shard_map/ppermute | solution.py:179
  2.0 16.1 %copy-start.8 = (bf16[1,2,128,384]{3,2,1,0:T(8,128)(2,1)}, bf16[1,2,128,384]{3,2,1,0:T(8,128)(2,1)S(1)}, u32[]{:S(2)}) copy-start(bf16[1,2,128,384]{3,2,1,0:T(8,128)(2,1)S(1)} %pad_maximum_fusion.5) | copy-start | bytes 589828
  2.0 6.2 %collective-permute-start.1 = (bf16[1,2,128,384]{3,2,1,0:T(8,128)(2,1)S(1)}, bf16[1,2,128,384]{3,2,1,0:T(8,128)(2,1)S(1)}, u32[]{:S(2)}, u32[]{:S(2)}) collective-permute-start(bf16[1,2,128,384]{3,2,1,0:T(8,128)(2,1)S(1)} %pad_maximum_fusion.5), channel_id=1, source_target_pairs={{0,4},{1,5},{2,0},{3,1},{4,8},{5,9},{6,2},{7,3},{8,12},{9,13},{10,... | collective-permute-start | bytes 589832 | tf_op jit(solution)/shard_map/ppermute | solution.py:53
  2.3 6.1 %collective-permute-start.2 = (bf16[1,2,128,384]{3,2,1,0:T(8,128)(2,1)S(1)}, bf16[1,2,128,384]{3,2,1,0:T(8,128)(2,1)S(1)}, u32[]{:S(2)}, u32[]{:S(2)}) collective-permute-start(bf16[1,2,128,384]{3,2,1,0:T(8,128)(2,1)S(1)} %pad_maximum_fusion.5), channel_id=1, source_target_pairs={{0,2},{1,3},{2,6},{3,7},{4,0},{5,1},{6,10},{7,11},{8,4},{9,5},{10,... | collective-permute-start | bytes 589832 | tf_op jit(solution)/shard_map/ppermute | solution.py:56
  8.2 5.2 %collective-permute-start.3 = (bf16[1,2,128,384]{3,2,1,0:T(8,128)(2,1)S(1)}, bf16[1,2,128,384]{3,2,1,0:T(8,128)(2,1)S(1)}, u32[]{:S(2)}, u32[]{:S(2)}) collective-permute-start(bf16[1,2,128,384]{3,2,1,0:T(8,128)(2,1)S(1)} %collective-permute-done.1), channel_id=1, source_target_pairs={{0,4},{1,5},{2,0},{3,1},{4,8},{5,9},{6,2},{7,3},{8,12},{9,13},{10,... | collective-permute-start | bytes 589832 | tf_op jit(solution)/shard_map/ppermute | solution.py:53
  8.4 5.2 %collective-permute-start.4 = (bf16[1,2,128,384]{3,2,1,0:T(8,128)(2,1)S(1)}, bf16[1,2,128,384]{3,2,1,0:T(8,128)(2,1)S(1)}, u32[]{:S(2)}, u32[]{:S(2)}) collective-permute-start(bf16[1,2,128,384]{3,2,1,0:T(8,128)(2,1)S(1)} %collective-permute-done.2), channel_id=1, source_target_pairs={{0,2},{1,3},{2,6},{3,7},{4,0},{5,1},{6,10},{7,11},{8,4},{9,5},{10,... | collective-permute-start | bytes 589832 | tf_op jit(solution)/shard_map/ppermute | solution.py:56
  13.4 4.5 %collective-permute-start.5 = (bf16[1,2,128,384]{3,2,1,0:T(8,128)(2,1)S(1)}, bf16[1,2,128,384]{3,2,1,0:T(8,128)(2,1)S(1)}, u32[]{:S(2)}, u32[]{:S(2)}) collective-permute-start(bf16[1,2,128,384]{3,2,1,0:T(8,128)(2,1)S(1)} %collective-permute-done.3), channel_id=1, source_target_pairs={{0,4},{1,5},{2,0},{3,1},{4,8},{5,9},{6,2},{7,3},{8,12},{9,13},{10,... | collective-permute-start | bytes 589832 | tf_op jit(solution)/shard_map/ppermute | solution.py:53
  13.6 4.6 %collective-permute-start.6 = (bf16[1,2,128,384]{3,2,1,0:T(8,128)(2,1)S(1)}, bf16[1,2,128,384]{3,2,1,0:T(8,128)(2,1)S(1)}, u32[]{:S(2)}, u32[]{:S(2)}) collective-permute-start(bf16[1,2,128,384]{3,2,1,0:T(8,128)(2,1)S(1)} %collective-permute-done.4), channel_id=1, source_target_pairs={{0,2},{1,3},{2,6},{3,7},{4,0},{5,1},{6,10},{7,11},{8,4},{9,5},{10,... | collective-permute-start | bytes 589832 | tf_op jit(solution)/shard_map/ppermute | solution.py:56
  17.9 3.6 %collective-permute-start.7 = (bf16[1,1,128,384]{3,2,1,0:T(8,128)(2,1)S(1)}, bf16[1,1,128,384]{3,2,1,0:T(8,128)(2,1)S(1)}, u32[]{:S(2)}, u32[]{:S(2)}) collective-permute-start(bf16[1,1,128,384]{3,2,1,0:T(8,128)(2,1)S(1)} %slice.467), channel_id=1, source_target_pairs={{0,4},{1,5},{2,0},{3,1},{4,8},{5,9},{6,2},{7,3},{8,12},{9,13},{10,... | collective-permute-start | bytes 294920 | tf_op jit(solution)/shard_map/ppermute | solution.py:49
  18.2 3.8 %collective-permute-start.8 = (bf16[1,1,128,384]{3,2,1,0:T(8,128)(2,1)S(1)}, bf16[1,1,128,384]{3,2,1,0:T(8,128)(2,1)S(1)}, u32[]{:S(2)}, u32[]{:S(2)}) collective-permute-start(bf16[1,1,128,384]{3,2,1,0:T(8,128)(2,1)S(1)} %slice.468), channel_id=1, source_target_pairs={{0,2},{1,3},{2,6},{3,7},{4,0},{5,1},{6,10},{7,11},{8,4},{9,5},{10,... | collective-permute-start | bytes 294920 | tf_op jit(solution)/shard_map/ppermute | solution.py:50
  22.0 1.2 %copy-start.9 = (bf16[1,16,128,384]{3,2,1,0:T(8,128)(2,1)}, bf16[1,16,128,384]{3,2,1,0:T(8,128)(2,1)S(1)}, u32[]{:S(2)}) copy-start(bf16[1,16,128,384]{3,2,1,0:T(8,128)(2,1)S(1)} %constant_dynamic-update-slice_fusion) | copy-start | bytes 4718596
  23.2 14.3 %copy-start.4 = (bf16[2,1,128,384]{3,2,1,0:T(8,128)(2,1)S(1)}, bf16[2,1,128,384]{3,2,1,0:T(8,128)(2,1)}, u32[]{:S(2)}) copy-start(bf16[2,1,128,384]{3,2,1,0:T(8,128)(2,1)} %param.11) | copy-start | bytes 589828
  29.5 5.7 %collective-permute-start.9 = (bf16[1,1,128,384]{3,2,1,0:T(8,128)(2,1)}, bf16[1,1,128,384]{3,2,1,0:T(8,128)(2,1)S(1)}, u32[]{:S(2)}, u32[]{:S(2)}) collective-permute-start(bf16[1,1,128,384]{3,2,1,0:T(8,128)(2,1)} %bitcast.160), channel_id=1, source_target_pairs={{0,1},{1,0},{2,3},{3,2},{4,5},{5,4},{6,7},{7,6},{8,9},{9,8},{10,11... | collective-permute-start | bytes 294920 | tf_op jit(solution)/shard_map/ppermute | solution.py:199
  37.6 10.3 %collective-permute-start.10 = (bf16[4,1,128,384]{3,2,1,0:T(8,128)(2,1)S(1)}, bf16[4,1,128,384]{3,2,1,0:T(8,128)(2,1)S(1)}, u32[]{:S(2)}, u32[]{:S(2)}) collective-permute-start(bf16[4,1,128,384]{3,2,1,0:T(8,128)(2,1)S(1)} %pad_maximum_fusion.4), channel_id=1, source_target_pairs={{0,1},{1,2},{2,3},{3,4},{4,5},{5,6},{6,7},{7,8},{8,9},{9,10},{10,1... | collective-permute-start | bytes 1179656 | tf_op jit(solution)/shard_map/ppermute | solution.py:18
  41.9 10.0 %collective-permute-start.11 = (bf16[4,1,128,384]{3,2,1,0:T(8,128)(2,1)S(1)}, bf16[4,1,128,384]{3,2,1,0:T(8,128)(2,1)S(1)}, u32[]{:S(2)}, u32[]{:S(2)}) collective-permute-start(bf16[4,1,128,384]{3,2,1,0:T(8,128)(2,1)S(1)} %pad_maximum_fusion.4), channel_id=1, source_target_pairs={{1,0},{2,1},{3,2},{4,3},{5,4},{6,5},{7,6},{8,7},{9,8},{10,9},{11,1... | collective-permute-start | bytes 1179656 | tf_op jit(solution)/shard_map/ppermute | solution.py:19
  56.5 0.9 copy-start.7
  57.4 5.0 %copy-start.5 = (bf16[3,3,384,192]{2,3,1,0:T(8,128)(2,1)S(1)}, bf16[3,3,384,192]{2,3,1,0:T(8,128)(2,1)}, u32[]{:S(2)}) copy-start(bf16[3,3,384,192]{2,3,1,0:T(8,128)(2,1)} %param.18) | copy-start | bytes 3981316
  57.9 7.7 %collective-permute-start.12 = (bf16[2,1,128,384]{3,2,0,1:T(8,128)(2,1)S(1)}, bf16[2,1,128,384]{3,2,0,1:T(8,128)(2,1)S(1)}, u32[]{:S(2)}, u32[]{:S(2)}) collective-permute-start(bf16[2,1,128,384]{3,2,0,1:T(8,128)(2,1)S(1)} %fusion.141), channel_id=1, source_target_pairs={{0,1},{1,2},{2,3},{3,4},{4,5},{5,6},{6,7},{7,8},{8,9},{9,10},{10,1... | collective-permute-start | bytes 589832 | tf_op jit(solution)/shard_map/ppermute | solution.py:18
  59.8 7.9 %collective-permute-start.13 = (bf16[2,1,128,384]{3,2,0,1:T(8,128)(2,1)S(1)}, bf16[2,1,128,384]{3,2,0,1:T(8,128)(2,1)S(1)}, u32[]{:S(2)}, u32[]{:S(2)}) collective-permute-start(bf16[2,1,128,384]{3,2,0,1:T(8,128)(2,1)S(1)} %fusion.141), channel_id=1, source_target_pairs={{1,0},{2,1},{3,2},{4,3},{5,4},{6,5},{7,6},{8,7},{9,8},{10,9},{11,1... | collective-permute-start | bytes 589832 | tf_op jit(solution)/shard_map/ppermute | solution.py:19
  69.9 1.0 %copy-start.6 = (bf16[1152,192,1,1]{0,1,2,3:T(8,128)(2,1)S(1)}, bf16[1152,192,1,1]{0,1,2,3:T(8,128)(2,1)}, u32[]{:S(2)}) copy-start(bf16[1152,192,1,1]{0,1,2,3:T(8,128)(2,1)} %reshape.289) | copy-start | bytes 1327108
  73.2 1.4 %copy-start.2 = (bf16[2,2,256,192]{2,3,1,0:T(8,128)(2,1)S(1)}, bf16[2,2,256,192]{2,3,1,0:T(8,128)(2,1)}, u32[]{:S(2)}) copy-start(bf16[2,2,256,192]{2,3,1,0:T(8,128)(2,1)} %param.12) | copy-start | bytes 1179652
  74.4 5.0 %copy-start.3 = (bf16[3,3,3,192,192]{4,3,2,1,0:T(8,128)(2,1)S(1)}, bf16[3,3,3,192,192]{4,3,2,1,0:T(8,128)(2,1)}, u32[]{:S(2)}) copy-start(bf16[3,3,3,192,192]{4,3,2,1,0:T(8,128)(2,1)} %param.19) | copy-start | bytes 5971972
  74.7 6.8 %collective-permute-start.14 = (bf16[4,1,256,192]{2,3,1,0:T(8,128)(2,1)S(1)}, bf16[4,1,256,192]{2,3,1,0:T(8,128)(2,1)S(1)}, u32[]{:S(2)}, u32[]{:S(2)}) collective-permute-start(bf16[4,1,256,192]{2,3,1,0:T(8,128)(2,1)S(1)} %get-tuple-element.84), channel_id=1, source_target_pairs={{0,1},{1,2},{2,3},{3,4},{4,5},{5,6},{6,7},{7,8},{8,9},{9,10},{10,1... | collective-permute-start | bytes 1179656 | tf_op jit(solution)/shard_map/ppermute | solution.py:18
  76.9 10.0 %collective-permute-start.15 = (bf16[4,1,256,192]{2,3,1,0:T(8,128)(2,1)S(1)}, bf16[4,1,256,192]{2,3,1,0:T(8,128)(2,1)S(1)}, u32[]{:S(2)}, u32[]{:S(2)}) collective-permute-start(bf16[4,1,256,192]{2,3,1,0:T(8,128)(2,1)S(1)} %get-tuple-element.85), channel_id=1, source_target_pairs={{1,0},{2,1},{3,2},{4,3},{5,4},{6,5},{7,6},{8,7},{9,8},{10,9},{11,1... | collective-permute-start | bytes 1179656 | tf_op jit(solution)/shard_map/ppermute | solution.py:19
  95.1 1.3 %copy-start.1 = (bf16[384,384]{1,0:T(8,128)(2,1)S(1)}, bf16[384,384]{1,0:T(8,128)(2,1)}, u32[]{:S(2)}) copy-start(bf16[384,384]{1,0:T(8,128)(2,1)} %param.13) | copy-start | bytes 884740

commit v21 on v18

--- a/solution.py
+++ b/solution.py
@@ -205,14 +205,15 @@
     block_out = (mixed.astype(jnp.float32) + conv_taps(first_padded, w_first, 3)).astype(
         jnp.bfloat16
     )
+    block_out, later_cache = lax.optimization_barrier((block_out, second_cache))
+    cache_padded = extended(later_cache, 1, 1)
     block_padded = extended(block_out, 1, 1)
     widened = jnp.repeat(block_padded, 2, axis=2)
     upsampled = conv_taps(widened, w_upsample[None], 1, rows=((0, 1), (1, 1), (1, 2))).astype(
         jnp.bfloat16
     )
     second_in = jax.nn.silu(rms_scale(upsampled)).astype(jnp.bfloat16)
-    second_stack = jnp.concatenate([second_cache, second_in], axis=0)
-    second_padded = extended(second_stack, 1, 1)
+    second_padded = jnp.concatenate([cache_padded, extended(second_in, 1, 1)], axis=0)
     return (upsampled.astype(jnp.float32) + conv_taps(second_padded, w_second, 3)).astype(
         jnp.bfloat16
     )

time: 95.9 us -> 102 us (1.064)
  starting transfers between devices: 26.8 us -> 34.4 us
  waiting for transfers between devices: 27.1 us -> 22.2 us
  local copies, waits for them, and re-layouts: 16.1 us -> 19.5 us
  matrix products: 14.2 us -> 16 us
    ppermute x3 -> x4, starting transfers between devices: 8.45 us -> 14.5 us  [halo_rows(): before = lax.ppermute(last, 'ha', up)]
    ppermute x3 -> x4, waiting for transfers between devices: 11.4 us -> 9.19 us  [halo_rows(): after = lax.ppermute(first, 'ha', down)]
    concatenate x4 -> x2, other arithmetic: 2.54 us -> 0.42 us  [extended(): return jnp.concatenate([before, x, after], axis=dim)]
    dot_general x21, matrix products: 13.2 us -> 15.1 us  [conv_taps(): jnp.einsum('fhwc,cd->fhwd', stacked, kernel, preferred_element_type=jnp.f...]
    ppermute x3 -> x4, waiting for transfers between devices: 1.95 us -> 0.24 us  [halo_rows(): before = lax.ppermute(last, 'ha', up)]
    ppermute x3 -> x4, starting transfers between devices: 7.05 us -> 8.57 us  [halo_rows(): after = lax.ppermute(first, 'ha', down)]
    concatenate x1, other arithmetic: 0.07 us -> 1.2 us  [per_device(): jnp.concatenate([cache_padded, extended(second_in, 1, 1)], axis=0)]
    unnamed x27 -> x31, local copies, waits for them, and re-layouts: 3.07 us -> 3.45 us
  transfers between devices with their start and end apart: 16 -> 18, of which waited for: 11 -> 9; matrix products, arithmetic and copies ran while one was open for 10% -> 17% of each run, Pallas kernels for 0% -> 0%
where the time goes in v21:
time: 102 us
  starting transfers between devices  34.4 us (34%)
  waiting for transfers between devices  22.2 us (22%)
  local copies, waits for them, and re-layouts  19.5 us (19%)
  matrix products  16 us (16%)
  Pallas kernels  6.36 us (6%)
  other arithmetic  2.81 us (3%)
    dot_general x21, matrix products, conv_taps(): jnp.einsum('fhwc,cd->fhwd', stacked, kernel, preferred_element_type=jnp.f...  15.1 us
    ppermute x4, starting transfers between devices, halo_rows(): before = lax.ppermute(last, 'ha', up)  14.5 us
    ppermute x3, waiting for transfers between devices, gather_chip_rows(): ahead = lax.ppermute(ahead, 'ha', forward)  10.1 us
    ppermute x4, waiting for transfers between devices, halo_rows(): after = lax.ppermute(first, 'ha', down)  9.19 us
    ppermute x4, starting transfers between devices, halo_rows(): after = lax.ppermute(first, 'ha', down)  8.57 us
    pallas_call x1, Pallas kernels, attend(): pl.pallas_call(functools.partial(attention_kernel, scale), grid=(frames,)...  6.36 us
    slice x6, local copies, waits for them, and re-layouts, conv_taps(): kernel = weight[time_off, row_off].reshape(3 * in_channels, out_channels)  5.4 us
    ppermute x1, starting transfers between devices, per_device(): back = lax.ppermute(mixed_block[:, 1:2], 'ha', swap)  4.57 us
  transfers between devices with their start and end apart: 18, of which 9 were waited for; matrix products, arithmetic and copies ran while one was open for 17% of the time, Pallas kernels for 0%

profile of v21, /device:TPU:13, one launch (start us, length us, event | category | flops | bytes accessed | tf_op | source)
XLA Modules:
  0.0 101.9 jit_solution(8375407351947810744)
XLA Ops:
  0.0 0.7 collective-permute-start
  0.7 0.9 constant_dynamic-update-slice_fusion.9
  2.3 1.3 %collective-permute-start.2 = (bf16[1,2,128,384]{3,2,1,0:T(8,128)(2,1)S(1)}, bf16[1,2,128,384]{3,2,1,0:T(8,128)(2,1)S(1)}, u32[]{:S(2)}, u32[]{:S(2)}) collective-permute-start(bf16[1,2,128,384]{3,2,1,0:T(8,128)(2,1)S(1)} %pad_maximum_fusion.7), channel_id=1, source_target_pairs={{0,2},{1,3},{2,6},{3,7},{4,0},{5,1},{6,10},{7,11},{8,4},{9,5},{10,... | collective-permute-start | bytes 589832 | tf_op jit(solution)/shard_map/ppermute | solution.py:56
  3.8 1.0 fusion.87.q_ref
  4.8 3.4 %collective-permute-done.1 = bf16[1,2,128,384]{3,2,1,0:T(8,128)(2,1)S(1)} collective-permute-done((bf16[1,2,128,384]{3,2,1,0:T(8,128)(2,1)S(1)}, bf16[1,2,128,384]{3,2,1,0:T(8,128)(2,1)S(1)}, u32[]{:S(2)}, u32[]{:S(2)}) %collective-permute-start.1) | collective-permute-done | bytes 196640 | tf_op jit(solution)/shard_map/ppermute | solution.py:53
  8.4 1.3 %collective-permute-start.4 = (bf16[1,2,128,384]{3,2,1,0:T(8,128)(2,1)S(1)}, bf16[1,2,128,384]{3,2,1,0:T(8,128)(2,1)S(1)}, u32[]{:S(2)}, u32[]{:S(2)}) collective-permute-start(bf16[1,2,128,384]{3,2,1,0:T(8,128)(2,1)S(1)} %collective-permute-done.2), channel_id=1, source_target_pairs={{0,2},{1,3},{2,6},{3,7},{4,0},{5,1},{6,10},{7,11},{8,4},{9,5},{10,... | collective-permute-start | bytes 589832 | tf_op jit(solution)/shard_map/ppermute | solution.py:56
  9.7 3.6 %collective-permute-done.3 = bf16[1,2,128,384]{3,2,1,0:T(8,128)(2,1)S(1)} collective-permute-done((bf16[1,2,128,384]{3,2,1,0:T(8,128)(2,1)S(1)}, bf16[1,2,128,384]{3,2,1,0:T(8,128)(2,1)S(1)}, u32[]{:S(2)}, u32[]{:S(2)}) %collective-permute-start.3) | collective-permute-done | bytes 196640 | tf_op jit(solution)/shard_map/ppermute | solution.py:53
  13.6 1.3 %collective-permute-start.6 = (bf16[1,2,128,384]{3,2,1,0:T(8,128)(2,1)S(1)}, bf16[1,2,128,384]{3,2,1,0:T(8,128)(2,1)S(1)}, u32[]{:S(2)}, u32[]{:S(2)}) collective-permute-start(bf16[1,2,128,384]{3,2,1,0:T(8,128)(2,1)S(1)} %collective-permute-done.4), channel_id=1, source_target_pairs={{0,2},{1,3},{2,6},{3,7},{4,0},{5,1},{6,10},{7,11},{8,4},{9,5},{10,... | collective-permute-start | bytes 589832 | tf_op jit(solution)/shard_map/ppermute | solution.py:56
  14.9 3.0 %collective-permute-done.5 = bf16[1,2,128,384]{3,2,1,0:T(8,128)(2,1)S(1)} collective-permute-done((bf16[1,2,128,384]{3,2,1,0:T(8,128)(2,1)S(1)}, bf16[1,2,128,384]{3,2,1,0:T(8,128)(2,1)S(1)}, u32[]{:S(2)}, u32[]{:S(2)}) %collective-permute-start.5) | collective-permute-done | bytes 196640 | tf_op jit(solution)/shard_map/ppermute | solution.py:53
  18.2 1.3 %collective-permute-start.8 = (bf16[1,1,128,384]{3,2,1,0:T(8,128)(2,1)S(1)}, bf16[1,1,128,384]{3,2,1,0:T(8,128)(2,1)S(1)}, u32[]{:S(2)}, u32[]{:S(2)}) collective-permute-start(bf16[1,1,128,384]{3,2,1,0:T(8,128)(2,1)S(1)} %slice.485), channel_id=1, source_target_pairs={{0,2},{1,3},{2,6},{3,7},{4,0},{5,1},{6,10},{7,11},{8,4},{9,5},{10,... | collective-permute-start | bytes 294920 | tf_op jit(solution)/shard_map/ppermute | solution.py:50
  19.6 1.9 %collective-permute-done.7 = bf16[1,1,128,384]{3,2,1,0:T(8,128)(2,1)S(1)} collective-permute-done((bf16[1,1,128,384]{3,2,1,0:T(8,128)(2,1)S(1)}, bf16[1,1,128,384]{3,2,1,0:T(8,128)(2,1)S(1)}, u32[]{:S(2)}, u32[]{:S(2)}) %collective-permute-start.7) | collective-permute-done | bytes 98336 | tf_op jit(solution)/shard_map/ppermute | solution.py:49
  22.0 1.2 %copy-done.10 = bf16[1,16,128,384]{3,2,1,0:T(8,128)(2,1)} copy-done((bf16[1,16,128,384]{3,2,1,0:T(8,128)(2,1)}, bf16[1,16,128,384]{3,2,1,0:T(8,128)(2,1)S(1)}, u32[]{:S(2)}) %copy-start.10) | copy-done | bytes 1572888
  23.2 6.4 %shard_map.100 = bf16[1,256,384]{2,1,0:T(8,128)(2,1)} custom-call(bf16[1,256,384]{2,1,0:T(8,128)(2,1)} %fusion.87.q_ref, bf16[1,2048,384]{2,1,0:T(8,128)(2,1)} %bitcast.168, bf16[384,384]{1,0:T(8,128)(2,1)} %wk_ref.1, bf16[384,384]{1,0:T(8,128)(2,1)} %wv_ref.1, bf16[1,256,384]{2,1,0:T(8,128)(2,1)} %bitcast.166, bf16[384,384]{1,0:T(8,128)(2,1)} %wo_ref.1), custom_call_target="tpu_custom_call" | custom-call | flops 2013265920 | bytes 3047424 | tf_op jit(solution)/shard_map/pallas_call | solution.py:134
  29.6 1.6 %fusion.170 = (bf16[1,1,128,384]{3,2,0,1:T(8,128)(2,1)S(1)}, bf16[1,128,384]{2,1,0:T(8,128)(2,1)}, bf16[1,1,128,384]{3,2,0,1:T(8,128)(2,1)S(1)}) fusion(bf16[1,2,128,384]{3,2,0,1:T(8,128)(2,1)} %bitcast.167), kind=kLoop, calls=%fused_computation.250 | loop fusion | bytes 491520 | tf_op jit(solution)/shard_map/slice | solution.py:196
  31.2 4.6 %collective-permute-start.9 = (bf16[1,1,128,384]{3,2,0,1:T(8,128)(2,1)S(1)}, bf16[1,1,128,384]{3,2,0,1:T(8,128)(2,1)S(1)}, u32[]{:S(2)}, u32[]{:S(2)}) collective-permute-start(bf16[1,1,128,384]{3,2,0,1:T(8,128)(2,1)S(1)} %get-tuple-element.93), channel_id=1, source_target_pairs={{0,1},{1,0},{2,3},{3,2},{4,5},{5,4},{6,7},{7,6},{8,9},{9,8},{10,11... | collective-permute-start | bytes 294920 | tf_op jit(solution)/shard_map/ppermute | solution.py:195
  36.3 1.1 %reshape.290 = bf16[1152,192,1,1]{0,1,2,3:T(8,128)(2,1)} reshape(bf16[1,1,3,384,192]{3,2,4,1,0:T(4,128)(2,1)S(1)} %copy.34) | data formatting | bytes 884736 | tf_op jit(solution)/shard_map/reshape;squeeze | solution.py:100
  37.8 1.2 %reshape.289 = bf16[1152,192,1,1]{0,1,2,3:T(8,128)(2,1)} reshape(bf16[1,1,3,384,192]{3,2,4,1,0:T(4,128)(2,1)S(1)} %copy.33) | data formatting | bytes 884736 | tf_op jit(solution)/shard_map/reshape;squeeze | solution.py:100
  40.2 4.0 %collective-permute-start.10 = (bf16[4,1,128,384]{3,2,0,1:T(8,128)(2,1)S(1)}, bf16[4,1,128,384]{3,2,0,1:T(8,128)(2,1)S(1)}, u32[]{:S(2)}, u32[]{:S(2)}) collective-permute-start(bf16[4,1,128,384]{3,2,0,1:T(8,128)(2,1)S(1)} %pad_maximum_fusion.6), channel_id=1, source_target_pairs={{0,1},{1,2},{2,3},{3,4},{4,5},{5,6},{6,7},{7,8},{8,9},{9,10},{10,1... | collective-permute-start | bytes 1179656 | tf_op jit(solution)/shard_map/ppermute | solution.py:18
  44.2 2.1 %collective-permute-start.11 = (bf16[4,1,128,384]{3,2,0,1:T(8,128)(2,1)S(1)}, bf16[4,1,128,384]{3,2,0,1:T(8,128)(2,1)S(1)}, u32[]{:S(2)}, u32[]{:S(2)}) collective-permute-start(bf16[4,1,128,384]{3,2,0,1:T(8,128)(2,1)S(1)} %pad_maximum_fusion.6), channel_id=1, source_target_pairs={{1,0},{2,1},{3,2},{4,3},{5,4},{6,5},{7,6},{8,7},{9,8},{10,9},{11,1... | collective-permute-start | bytes 1179656 | tf_op jit(solution)/shard_map/ppermute | solution.py:19
  46.3 3.9 %fusion.161 = (bf16[1,1,3,384,384]{4,3,2,1,0:T(8,128)(2,1)S(1)}, bf16[1,1,3,384,384]{4,3,2,1,0:T(8,128)(2,1)S(1)}, bf16[1,1,3,384,384]{4,3,2,1,0:T(8,128)(2,1)S(...) fusion(bf16[3,3,3,384,384]{4,3,2,1,0:T(8,128)(2,1)} %param.17), kind=kLoop, calls=%fused_computation.241 | loop fusion | bytes 15925248 | tf_op jit(solution)/shard_map/slice | solution.py:100
  50.3 3.9 %collective-permute-done.11 = bf16[4,1,128,384]{3,2,0,1:T(8,128)(2,1)S(1)} collective-permute-done((bf16[4,1,128,384]{3,2,0,1:T(8,128)(2,1)S(1)}, bf16[4,1,128,384]{3,2,0,1:T(8,128)(2,1)S(1)}, u32[]{:S(2)}, u32[]{:S(2)}) %collective-permute-start.11) | collective-permute-done | bytes 393248 | tf_op jit(solution)/shard_map/ppermute | solution.py:19
  54.5 0.7 fusion.165
  59.6 0.5 fusion.138
  60.1 1.9 %collective-permute-start.12 = (bf16[2,1,128,384]{3,2,0,1:T(8,128)(2,1)S(1)}, bf16[2,1,128,384]{3,2,0,1:T(8,128)(2,1)S(1)}, u32[]{:S(2)}, u32[]{:S(2)}) collective-permute-start(bf16[2,1,128,384]{3,2,0,1:T(8,128)(2,1)S(1)} %fusion.138), channel_id=1, source_target_pairs={{0,1},{1,2},{2,3},{3,4},{4,5},{5,6},{6,7},{7,8},{8,9},{9,10},{10,1... | collective-permute-start | bytes 589832 | tf_op jit(solution)/shard_map/ppermute | solution.py:18
  62.0 2.4 %collective-permute-start.13 = (bf16[2,1,128,384]{3,2,0,1:T(8,128)(2,1)S(1)}, bf16[2,1,128,384]{3,2,0,1:T(8,128)(2,1)S(1)}, u32[]{:S(2)}, u32[]{:S(2)}) collective-permute-start(bf16[2,1,128,384]{3,2,0,1:T(8,128)(2,1)S(1)} %fusion.138), channel_id=1, source_target_pairs={{1,0},{2,1},{3,2},{4,3},{5,4},{6,5},{7,6},{8,7},{9,8},{10,9},{11,1... | collective-permute-start | bytes 589832 | tf_op jit(solution)/shard_map/ppermute | solution.py:19
  64.4 0.8 fusion.166
  65.2 4.0 %collective-permute-start.14 = (bf16[2,1,256,192]{2,3,1,0:T(8,128)(2,1)}, bf16[2,1,256,192]{2,3,1,0:T(8,128)(2,1)}, u32[]{:S(2)}, u32[]{:S(2)}) collective-permute-start(bf16[2,1,256,192]{2,3,1,0:T(8,128)(2,1)} %get-tuple-element.81), channel_id=1, source_target_pairs={{0,1},{1,2},{2,3},{3,4},{4,5},{5,6},{6,7},{7,8},{8,9},{9,10},{10,1... | collective-permute-start | bytes 589832 | tf_op jit(solution)/shard_map/ppermute | solution.py:18
  69.3 1.9 %collective-permute-start.15 = (bf16[2,1,256,192]{2,3,1,0:T(8,128)(2,1)}, bf16[2,1,256,192]{2,3,1,0:T(8,128)(2,1)}, u32[]{:S(2)}, u32[]{:S(2)}) collective-permute-start(bf16[2,1,256,192]{2,3,1,0:T(8,128)(2,1)} %get-tuple-element.82), channel_id=1, source_target_pairs={{1,0},{2,1},{3,2},{4,3},{5,4},{6,5},{7,6},{8,7},{9,8},{10,9},{11,1... | collective-permute-start | bytes 589832 | tf_op jit(solution)/shard_map/ppermute | solution.py:19
  71.4 0.6 broadcast_in_dim.4
  72.6 0.7 pad_slice_fusion.23
  73.6 0.7 copy-done.7
  74.3 1.1 %fusion.2 = f32[2,2,256,192]{2,3,1,0:T(8,128)S(1)} fusion(bf16[2,1,258,384]{3,2,1,0:T(8,128)(2,1)S(1)} %pad_slice_fusion.24, bf16[2,2,256,384]{3,2,1,0:T(8,128)(2,1)S(1)} %get-tuple-element.80, bf16[2,2,256,384]{3,2,1,0:T(8,128)(2,1)S(1)} %get-tuple-element.79, bf16[1152,192,1,1]{0,1,2,3:T(8,128)(2,1)S(1)} %copy-done.7), kind=kOutput, calls=%fused_computation.23 | convolution fusion | flops 462422016 | bytes 3197952 | tf_op jit(solution)/shard_map/fhwc,cd->fhwd/dot_general | solution.py:101
  75.5 1.1 %fusion.24 = f32[2,2,256,192]{2,3,1,0:T(8,128)S(1)} fusion(f32[2,2,256,192]{2,3,1,0:T(8,128)S(1)} %fusion.2, bf16[2,2,256,384]{3,2,1,0:T(8,128)(2,1)S(1)} %get-tuple-element.74, bf16[2,2,256,384]{3,2,1,0:T(8,128)(2,1)S(1)} %get-tuple-element.77, bf16[2,2,256,384]{3,2,1,0:T(8,128)(2,1)S(1)} %get-tuple-element.78, bf16[1152,192,1,1]{0,1,2,3:T(8,128)(2,1)S(1)} %copy-done.6), kind=kOutput, calls=%fused_computation.51 | convolution fusion | flops 460259328 | bytes 4374528 | tf_op jit(solution)/shard_map/fhwc,cd->fhwd/dot_general | solution.py:101
  76.7 1.2 %multiply_reduce_fusion = (f32[2,2,256]{2,1,0:T(2,128)S(1)}, f32[2,2,256,192]{2,3,1,0:T(8,128)S(1)}) fusion(f32[2,2,256,192]{2,3,1,0:T(8,128)S(1)} %fusion.24, bf16[1152,192,1,1]{0,1,2,3:T(8,128)(2,1)S(1)} %reshape.291, bf16[2,2,256,384]{3,2,1,0:T(8,128)(2,1)S(1)} %get-tuple-element.75, bf16[2,2,256,384]{3,2,1,0:T(8,128)(2,1)S(1)} %get-tuple-element.76, ...), kind=kOutput, calls=%fused_computation.127 | convolution fusion | flops 461044736 | bytes 4378624 | tf_op jit(solution)/shard_map/fhwc,cd->fhwd/dot_general | solution.py:101
  78.1 4.5 %collective-permute-start.16 = (bf16[2,1,256,192]{2,3,1,0:T(8,128)(2,1)S(1)}, bf16[2,1,256,192]{2,3,1,0:T(8,128)(2,1)S(1)}, u32[]{:S(2)}, u32[]{:S(2)}) collective-permute-start(bf16[2,1,256,192]{2,3,1,0:T(8,128)(2,1)S(1)} %get-tuple-element.83), channel_id=1, source_target_pairs={{0,1},{1,2},{2,3},{3,4},{4,5},{5,6},{6,7},{7,8},{8,9},{9,10},{10,1... | collective-permute-start | bytes 589832 | tf_op jit(solution)/shard_map/ppermute | solution.py:18
  82.7 2.1 %collective-permute-start.17 = (bf16[2,1,256,192]{2,3,1,0:T(8,128)(2,1)S(1)}, bf16[2,1,256,192]{2,3,1,0:T(8,128)(2,1)S(1)}, u32[]{:S(2)}, u32[]{:S(2)}) collective-permute-start(bf16[2,1,256,192]{2,3,1,0:T(8,128)(2,1)S(1)} %get-tuple-element.84), channel_id=1, source_target_pairs={{1,0},{2,1},{3,2},{4,3},{5,4},{6,5},{7,6},{8,7},{9,8},{10,9},{11,1... | collective-permute-start | bytes 589832 | tf_op jit(solution)/shard_map/ppermute | solution.py:19
  85.3 5.3 %collective-permute-done.17 = bf16[2,1,256,192]{2,3,1,0:T(8,128)(2,1)S(1)} collective-permute-done((bf16[2,1,256,192]{2,3,1,0:T(8,128)(2,1)S(1)}, bf16[2,1,256,192]{2,3,1,0:T(8,128)(2,1)S(1)}, u32[]{:S(2)}, u32[]{:S(2)}) %collective-permute-start.17) | collective-permute-done | bytes 196640 | tf_op jit(solution)/shard_map/ppermute | solution.py:19
  90.6 1.2 %maximum_maximum_fusion = bf16[4,4,256,192]{2,3,1,0:T(8,128)(2,1)S(1)} fusion(bf16[2,1,256,192]{2,3,1,0:T(8,128)(2,1)S(1)} %collective-permute-done.17, bf16[2,2,256,192]{2,3,1,0:T(8,128)(2,1)S(1)} %multiply_convert_fusion, bf16[2,1,256,192]{2,3,1,0:T(8,128)(2,1)S(1)} %collective-permute-done.16, bf16[2,1,256,192]{2,3,1,0:T(8,128)(2,1)} %collective-permute-done.15, ...), kind=kLoop, calls=%fused_computation.40 | loop fusion | flops 3932160 | bytes 3145728 | tf_op jit(solution)/shard_map/concatenate | solution.py:216
  91.8 2.5 %pad_slice_fusion.1 = (bf16[2,2,256,192]{2,3,1,0:T(8,128)(2,1)S(1)}, bf16[2,2,256,192]{2,3,1,0:T(8,128)(2,1)S(1)}, bf16[2,2,256,192]{2,3,1,0:T(8,128)(2,1)S(1)},...) fusion(bf16[4,4,256,192]{2,3,1,0:T(8,128)(2,1)S(1)} %maximum_ma, ...), kind=kLoop, calls=%fused_computation.1 | loop fusion | bytes 9830400 | tf_op jit(solution)/shard_map/slice | solution.py:98
  94.5 0.5 fusion.55
  95.0 1.5 %convolution_add_fusion.7 = f32[2,2,256,192]{2,3,1,0:T(8,128)S(1)} fusion(f32[2,2,256,192]{2,3,1,0:T(8,128)S(1)} %fusion.55, bf16[576,192,1,1]{1,0,3,2:T(8,128)(2,1)S(1)} %bitcast.164, bf16[2,2,256,192]{2,3,1,0:T(8,128)(2,1)S(1)} %copy-done.4, bf16[2,1,256,192]{2,3,1,0:T(8,128)(2,1)} %collective-permute-done.14, ...), kind=kOutput, calls=%fused_computation.49 | convolution fusion | flops 231407616 | bytes 3170304 | tf_op jit(solution)/shard_map/fhwc,cd->fhwd/dot_general | solution.py:101
  96.5 1.5 %convolution_add_fusion.6 = f32[2,2,256,192]{2,3,1,0:T(8,128)S(1)} fusion(f32[2,2,256,192]{2,3,1,0:T(8,128)S(1)} %convolution_add_fusion.7, bf16[576,192,1,1]{1,0,3,2:T(8,128)(2,1)S(1)} %bitcast.163, bf16[2,1,256,192]{2,3,1,0:T(8,128)(2,1)} %collective-permute-done.15, bf16[2,2,256,192]{2,3,1,0:T(8,128)(2,1)S(1)} %copy-done.4, ...), kind=kOutput, calls=%fused_computation.48 | convolution fusion | flops 231407616 | bytes 3170304 | tf_op jit(solution)/shard_map/fhwc,cd->fhwd/dot_general | solution.py:101
  98.0 0.5 convolution_add_fusion.5
  98.5 0.5 convolution_add_fusion.4
  99.0 0.5 convolution_add_fusion.3
  99.5 0.5 convolution_add_fusion.2
  100.1 0.5 convolution_add_fusion.1
  100.6 1.3 %fusion.36 = bf16[2,2,256,192]{2,3,1,0:T(8,128)(2,1)} fusion(f32[2,2,256,192]{2,3,1,0:T(8,128)S(1)} %get-tuple-element.95, f32[2,2,256,192]{2,3,1,0:T(8,128)S(1)} %convolution_add_fusion.1, bf16[576,192,1,1]{1,0,3,2:T(8,128)(2,1)S(1)} %bitcast.157, bf16[2,1,256,192]{2,3,1,0:T(8,128)(2,1)S(1)} %collective-permute-done.17, ...), kind=kOutput, calls=%fused_computation.59 | convolution fusion | flops 231800832 | bytes 3563520 | tf_op jit(solution)/shard_map/fhwc,cd->fhwd/dot_general | solution.py:101
  (82 shorter events, 10.8 us)
Async XLA Ops:
  0.0 3.8 %copy-start = (bf16[384,384]{1,0:T(8,128)(2,1)S(1)}, bf16[384,384]{1,0:T(8,128)(2,1)}, u32[]{:S(2)}) copy-start(bf16[384,384]{1,0:T(8,128)(2,1)} %param.13) | copy-start | bytes 884740
  0.0 2.0 %collective-permute-start = (bf16[2,1,128,384]{3,2,1,0:T(8,128)(2,1)}, bf16[2,1,128,384]{3,2,1,0:T(8,128)(2,1)S(1)}, u32[]{:S(2)}, u32[]{:S(2)}) collective-permute-start(bf16[2,1,128,384]{3,2,1,0:T(8,128)(2,1)} %param.10), channel_id=1, source_target_pairs={{0,1},{1,0},{2,3},{3,2},{4,5},{5,4},{6,7},{7,6},{8,9},{9,8},{10,11... | collective-permute-start | bytes 589832 | tf_op jit(solution)/shard_map/ppermute | solution.py:176
  2.0 16.1 %copy-start.8 = (bf16[1,2,128,384]{3,2,1,0:T(8,128)(2,1)}, bf16[1,2,128,384]{3,2,1,0:T(8,128)(2,1)S(1)}, u32[]{:S(2)}) copy-start(bf16[1,2,128,384]{3,2,1,0:T(8,128)(2,1)S(1)} %pad_maximum_fusion.7) | copy-start | bytes 589828
  2.0 6.2 %collective-permute-start.1 = (bf16[1,2,128,384]{3,2,1,0:T(8,128)(2,1)S(1)}, bf16[1,2,128,384]{3,2,1,0:T(8,128)(2,1)S(1)}, u32[]{:S(2)}, u32[]{:S(2)}) collective-permute-start(bf16[1,2,128,384]{3,2,1,0:T(8,128)(2,1)S(1)} %pad_maximum_fusion.7), channel_id=1, source_target_pairs={{0,4},{1,5},{2,0},{3,1},{4,8},{5,9},{6,2},{7,3},{8,12},{9,13},{10,... | collective-permute-start | bytes 589832 | tf_op jit(solution)/shard_map/ppermute | solution.py:53
  2.3 6.1 %collective-permute-start.2 = (bf16[1,2,128,384]{3,2,1,0:T(8,128)(2,1)S(1)}, bf16[1,2,128,384]{3,2,1,0:T(8,128)(2,1)S(1)}, u32[]{:S(2)}, u32[]{:S(2)}) collective-permute-start(bf16[1,2,128,384]{3,2,1,0:T(8,128)(2,1)S(1)} %pad_maximum_fusion.7), channel_id=1, source_target_pairs={{0,2},{1,3},{2,6},{3,7},{4,0},{5,1},{6,10},{7,11},{8,4},{9,5},{10,... | collective-permute-start | bytes 589832 | tf_op jit(solution)/shard_map/ppermute | solution.py:56
  8.2 5.2 %collective-permute-start.3 = (bf16[1,2,128,384]{3,2,1,0:T(8,128)(2,1)S(1)}, bf16[1,2,128,384]{3,2,1,0:T(8,128)(2,1)S(1)}, u32[]{:S(2)}, u32[]{:S(2)}) collective-permute-start(bf16[1,2,128,384]{3,2,1,0:T(8,128)(2,1)S(1)} %collective-permute-done.1), channel_id=1, source_target_pairs={{0,4},{1,5},{2,0},{3,1},{4,8},{5,9},{6,2},{7,3},{8,12},{9,13},{10,... | collective-permute-start | bytes 589832 | tf_op jit(solution)/shard_map/ppermute | solution.py:53
  8.4 5.2 %collective-permute-start.4 = (bf16[1,2,128,384]{3,2,1,0:T(8,128)(2,1)S(1)}, bf16[1,2,128,384]{3,2,1,0:T(8,128)(2,1)S(1)}, u32[]{:S(2)}, u32[]{:S(2)}) collective-permute-start(bf16[1,2,128,384]{3,2,1,0:T(8,128)(2,1)S(1)} %collective-permute-done.2), channel_id=1, source_target_pairs={{0,2},{1,3},{2,6},{3,7},{4,0},{5,1},{6,10},{7,11},{8,4},{9,5},{10,... | collective-permute-start | bytes 589832 | tf_op jit(solution)/shard_map/ppermute | solution.py:56
  13.4 4.5 %collective-permute-start.5 = (bf16[1,2,128,384]{3,2,1,0:T(8,128)(2,1)S(1)}, bf16[1,2,128,384]{3,2,1,0:T(8,128)(2,1)S(1)}, u32[]{:S(2)}, u32[]{:S(2)}) collective-permute-start(bf16[1,2,128,384]{3,2,1,0:T(8,128)(2,1)S(1)} %collective-permute-done.3), channel_id=1, source_target_pairs={{0,4},{1,5},{2,0},{3,1},{4,8},{5,9},{6,2},{7,3},{8,12},{9,13},{10,... | collective-permute-start | bytes 589832 | tf_op jit(solution)/shard_map/ppermute | solution.py:53
  13.6 4.6 %collective-permute-start.6 = (bf16[1,2,128,384]{3,2,1,0:T(8,128)(2,1)S(1)}, bf16[1,2,128,384]{3,2,1,0:T(8,128)(2,1)S(1)}, u32[]{:S(2)}, u32[]{:S(2)}) collective-permute-start(bf16[1,2,128,384]{3,2,1,0:T(8,128)(2,1)S(1)} %collective-permute-done.4), channel_id=1, source_target_pairs={{0,2},{1,3},{2,6},{3,7},{4,0},{5,1},{6,10},{7,11},{8,4},{9,5},{10,... | collective-permute-start | bytes 589832 | tf_op jit(solution)/shard_map/ppermute | solution.py:56
  17.9 3.6 %collective-permute-start.7 = (bf16[1,1,128,384]{3,2,1,0:T(8,128)(2,1)S(1)}, bf16[1,1,128,384]{3,2,1,0:T(8,128)(2,1)S(1)}, u32[]{:S(2)}, u32[]{:S(2)}) collective-permute-start(bf16[1,1,128,384]{3,2,1,0:T(8,128)(2,1)S(1)} %slice.484), channel_id=1, source_target_pairs={{0,4},{1,5},{2,0},{3,1},{4,8},{5,9},{6,2},{7,3},{8,12},{9,13},{10,... | collective-permute-start | bytes 294920 | tf_op jit(solution)/shard_map/ppermute | solution.py:49
  18.2 3.8 %collective-permute-start.8 = (bf16[1,1,128,384]{3,2,1,0:T(8,128)(2,1)S(1)}, bf16[1,1,128,384]{3,2,1,0:T(8,128)(2,1)S(1)}, u32[]{:S(2)}, u32[]{:S(2)}) collective-permute-start(bf16[1,1,128,384]{3,2,1,0:T(8,128)(2,1)S(1)} %slice.485), channel_id=1, source_target_pairs={{0,2},{1,3},{2,6},{3,7},{4,0},{5,1},{6,10},{7,11},{8,4},{9,5},{10,... | collective-permute-start | bytes 294920 | tf_op jit(solution)/shard_map/ppermute | solution.py:50
  22.0 1.2 %copy-start.10 = (bf16[1,16,128,384]{3,2,1,0:T(8,128)(2,1)}, bf16[1,16,128,384]{3,2,1,0:T(8,128)(2,1)S(1)}, u32[]{:S(2)}) copy-start(bf16[1,16,128,384]{3,2,1,0:T(8,128)(2,1)S(1)} %constant_dynamic-update-slice_fusion) | copy-start | bytes 4718596
  23.2 12.5 %copy-start.5 = (bf16[3,3,384,192]{2,3,1,0:T(8,128)(2,1)S(1)}, bf16[3,3,384,192]{2,3,1,0:T(8,128)(2,1)}, u32[]{:S(2)}) copy-start(bf16[3,3,384,192]{2,3,1,0:T(8,128)(2,1)} %param.18) | copy-start | bytes 3981316
  31.2 8.6 %collective-permute-start.9 = (bf16[1,1,128,384]{3,2,0,1:T(8,128)(2,1)S(1)}, bf16[1,1,128,384]{3,2,0,1:T(8,128)(2,1)S(1)}, u32[]{:S(2)}, u32[]{:S(2)}) collective-permute-start(bf16[1,1,128,384]{3,2,0,1:T(8,128)(2,1)S(1)} %get-tuple-element.93), channel_id=1, source_target_pairs={{0,1},{1,0},{2,3},{3,2},{4,5},{5,4},{6,7},{7,6},{8,9},{9,8},{10,11... | collective-permute-start | bytes 294920 | tf_op jit(solution)/shard_map/ppermute | solution.py:195
  39.0 1.1 %copy-start.3 = (bf16[2,1,128,384]{3,2,1,0:T(8,128)(2,1)S(1)}, bf16[2,1,128,384]{3,2,1,0:T(8,128)(2,1)}, u32[]{:S(2)}) copy-start(bf16[2,1,128,384]{3,2,1,0:T(8,128)(2,1)} %param.11) | copy-start | bytes 589828
  40.2 10.1 %collective-permute-start.10 = (bf16[4,1,128,384]{3,2,0,1:T(8,128)(2,1)S(1)}, bf16[4,1,128,384]{3,2,0,1:T(8,128)(2,1)S(1)}, u32[]{:S(2)}, u32[]{:S(2)}) collective-permute-start(bf16[4,1,128,384]{3,2,0,1:T(8,128)(2,1)S(1)} %pad_maximum_fusion.6), channel_id=1, source_target_pairs={{0,1},{1,2},{2,3},{3,4},{4,5},{5,6},{6,7},{7,8},{8,9},{9,10},{10,1... | collective-permute-start | bytes 1179656 | tf_op jit(solution)/shard_map/ppermute | solution.py:18
  44.2 10.0 %collective-permute-start.11 = (bf16[4,1,128,384]{3,2,0,1:T(8,128)(2,1)S(1)}, bf16[4,1,128,384]{3,2,0,1:T(8,128)(2,1)S(1)}, u32[]{:S(2)}, u32[]{:S(2)}) collective-permute-start(bf16[4,1,128,384]{3,2,0,1:T(8,128)(2,1)S(1)} %pad_maximum_fusion.6), channel_id=1, source_target_pairs={{1,0},{2,1},{3,2},{4,3},{5,4},{6,5},{7,6},{8,7},{9,8},{10,9},{11,1... | collective-permute-start | bytes 1179656 | tf_op jit(solution)/shard_map/ppermute | solution.py:19
  58.7 0.9 copy-start.9
  59.6 4.9 %copy-start.4 = (bf16[2,2,256,192]{2,3,1,0:T(8,128)(2,1)S(1)}, bf16[2,2,256,192]{2,3,1,0:T(8,128)(2,1)}, u32[]{:S(2)}) copy-start(bf16[2,2,256,192]{2,3,1,0:T(8,128)(2,1)} %param.12) | copy-start | bytes 1179652
  60.1 11.1 %collective-permute-start.12 = (bf16[2,1,128,384]{3,2,0,1:T(8,128)(2,1)S(1)}, bf16[2,1,128,384]{3,2,0,1:T(8,128)(2,1)S(1)}, u32[]{:S(2)}, u32[]{:S(2)}) collective-permute-start(bf16[2,1,128,384]{3,2,0,1:T(8,128)(2,1)S(1)} %fusion.138), channel_id=1, source_target_pairs={{0,1},{1,2},{2,3},{3,4},{4,5},{5,6},{6,7},{7,8},{8,9},{9,10},{10,1... | collective-permute-start | bytes 589832 | tf_op jit(solution)/shard_map/ppermute | solution.py:18
  62.0 9.2 %collective-permute-start.13 = (bf16[2,1,128,384]{3,2,0,1:T(8,128)(2,1)S(1)}, bf16[2,1,128,384]{3,2,0,1:T(8,128)(2,1)S(1)}, u32[]{:S(2)}, u32[]{:S(2)}) collective-permute-start(bf16[2,1,128,384]{3,2,0,1:T(8,128)(2,1)S(1)} %fusion.138), channel_id=1, source_target_pairs={{1,0},{2,1},{3,2},{4,3},{5,4},{6,5},{7,6},{8,7},{9,8},{10,9},{11,1... | collective-permute-start | bytes 589832 | tf_op jit(solution)/shard_map/ppermute | solution.py:19
  65.2 19.8 %collective-permute-start.14 = (bf16[2,1,256,192]{2,3,1,0:T(8,128)(2,1)}, bf16[2,1,256,192]{2,3,1,0:T(8,128)(2,1)}, u32[]{:S(2)}, u32[]{:S(2)}) collective-permute-start(bf16[2,1,256,192]{2,3,1,0:T(8,128)(2,1)} %get-tuple-element.81), channel_id=1, source_target_pairs={{0,1},{1,2},{2,3},{3,4},{4,5},{5,6},{6,7},{7,8},{8,9},{9,10},{10,1... | collective-permute-start | bytes 589832 | tf_op jit(solution)/shard_map/ppermute | solution.py:18
  69.3 15.8 %collective-permute-start.15 = (bf16[2,1,256,192]{2,3,1,0:T(8,128)(2,1)}, bf16[2,1,256,192]{2,3,1,0:T(8,128)(2,1)}, u32[]{:S(2)}, u32[]{:S(2)}) collective-permute-start(bf16[2,1,256,192]{2,3,1,0:T(8,128)(2,1)} %get-tuple-element.82), channel_id=1, source_target_pairs={{1,0},{2,1},{3,2},{4,3},{5,4},{6,5},{7,6},{8,7},{9,8},{10,9},{11,1... | collective-permute-start | bytes 589832 | tf_op jit(solution)/shard_map/ppermute | solution.py:19
  73.3 1.0 copy-start.7
  74.3 1.2 %copy-start.6 = (bf16[1152,192,1,1]{0,1,2,3:T(8,128)(2,1)S(1)}, bf16[1152,192,1,1]{0,1,2,3:T(8,128)(2,1)}, u32[]{:S(2)}) copy-start(bf16[1152,192,1,1]{0,1,2,3:T(8,128)(2,1)} %reshape.289) | copy-start | bytes 1327108
  76.7 8.2 %copy-start.2 = (bf16[3,3,3,192,192]{4,3,2,1,0:T(8,128)(2,1)S(1)}, bf16[3,3,3,192,192]{4,3,2,1,0:T(8,128)(2,1)}, u32[]{:S(2)}) copy-start(bf16[3,3,3,192,192]{4,3,2,1,0:T(8,128)(2,1)} %param.19) | copy-start | bytes 5971972
  78.1 7.1 %collective-permute-start.16 = (bf16[2,1,256,192]{2,3,1,0:T(8,128)(2,1)S(1)}, bf16[2,1,256,192]{2,3,1,0:T(8,128)(2,1)S(1)}, u32[]{:S(2)}, u32[]{:S(2)}) collective-permute-start(bf16[2,1,256,192]{2,3,1,0:T(8,128)(2,1)S(1)} %get-tuple-element.83), channel_id=1, source_target_pairs={{0,1},{1,2},{2,3},{3,4},{4,5},{5,6},{6,7},{7,8},{8,9},{9,10},{10,1... | collective-permute-start | bytes 589832 | tf_op jit(solution)/shard_map/ppermute | solution.py:18
  82.7 7.9 %collective-permute-start.17 = (bf16[2,1,256,192]{2,3,1,0:T(8,128)(2,1)S(1)}, bf16[2,1,256,192]{2,3,1,0:T(8,128)(2,1)S(1)}, u32[]{:S(2)}, u32[]{:S(2)}) collective-permute-start(bf16[2,1,256,192]{2,3,1,0:T(8,128)(2,1)S(1)} %get-tuple-element.84), channel_id=1, source_target_pairs={{1,0},{2,1},{3,2},{4,3},{5,4},{6,5},{7,6},{8,7},{9,8},{10,9},{11,1... | collective-permute-start | bytes 589832 | tf_op jit(solution)/shard_map/ppermute | solution.py:19
  100.6 1.3 %copy-start.1 = (bf16[384,384]{1,0:T(8,128)(2,1)S(1)}, bf16[384,384]{1,0:T(8,128)(2,1)}, u32[]{:S(2)}) copy-start(bf16[384,384]{1,0:T(8,128)(2,1)} %param.13) | copy-start | bytes 884740
